TPU v7x, 32 devices: a whole 2x2x4 slice. The times are simulated.
32 devices in a mesh: groups: 2 (over x), expert: 16 (over z, y, core).
Axes of the slice: x: 2, y: 2, z: 4, core: 2. Of those that a mesh axis runs over, the one named last changes fastest.
Arguments:
- tokens: bfloat16 [4096, 2048], P(('groups', 'expert')), parts along dimension 0, may hold values from -12 to 12
- out_grad: bfloat16 [4096, 2048], P(('groups', 'expert')), parts along dimension 0, may hold values from -6 to 6
- cluster_ids: int32 [4096], P(('groups', 'expert')), parts along dimension 0, may hold values from 0 to 31, as said below
- routes: int32 [1024, 8], P(('groups', 'expert')), parts along dimension 0, may hold values from 0 to 15, all different within a row; in each aligned block of 32 rows (0 to 31, 32 to 63, ...) at most 32 rows name the same one
- route_weights: float32 [1024, 8], P(('groups', 'expert')), parts along dimension 0, may hold values from 0.05 to 0.5
- gate_weight: bfloat16 [16, 2048, 768], P('expert'), may hold values from -0.125 to 0.125
- up_weight: bfloat16 [16, 2048, 768], P('expert'), may hold values from -0.125 to 0.125
- down_weight: bfloat16 [16, 768, 2048], P('expert'), may hold values from -0.21875 to 0.21875
Outputs:
- layer_out: float32 [4096, 2048], P(('groups', 'expert')), parts along dimension 0
- token_grad: float32 [4096, 2048], P(('groups', 'expert')), parts along dimension 0
There are 2 independent parts, one for each index of `groups`. A program takes and returns all parts, laid end to end along the dimension named above; an argument that names none is the same for every part. Nothing has to cross between parts.
Inputs may be any that keep to these rules, and one draw needn't show every extreme that they name: `cluster_ids`: within each block of 128 tokens every one of the 32 cluster numbers occurs at least once. `routes`: each row names 8 different experts. Among the 32 rows of one index of expert no expert is named more than 32 times, and in some such blocks one expert is named exactly 32 times.
All inputs are finite; a program needn't handle non-finite values.
Results may differ from a plain program's by a relative error of at most 0.0027.
Values may be sent and summed in bfloat16 or wider, within the bound.
No kernel may reach another device: no remote copies, remote signals or barrier semaphores. Data moves between devices by JAX's collectives and lax.ppermute only.
A program may use at most 64 MiB of HBM per device.

v0:
```python
import jax
import jax.numpy as jnp
from jax import lax
from jax.sharding import PartitionSpec as P


def expert_forward(inputs, gate_mat, up_mat, down_mat):
    gate_act = jnp.dot(inputs, gate_mat, preferred_element_type=jnp.float32)
    up_act = jnp.dot(inputs, up_mat, preferred_element_type=jnp.float32)
    sigmoid_gate = jax.nn.sigmoid(gate_act)
    hidden = (gate_act * sigmoid_gate * up_act).astype(jnp.bfloat16)
    output = jnp.dot(hidden, down_mat, preferred_element_type=jnp.float32).astype(jnp.bfloat16)
    return (output, gate_act, up_act)


def expert_backward(incoming, gate_act, up_act, gate_mat, up_mat, down_mat):
    against = (((1,), (1,)), ((), ()))
    hidden_grad = lax.dot_general(incoming, down_mat, against, preferred_element_type=jnp.float32)
    sigmoid_gate = jax.nn.sigmoid(gate_act)
    gate_grad = (
        hidden_grad * up_act * sigmoid_gate * (1.0 + gate_act * (1.0 - sigmoid_gate))
    ).astype(jnp.bfloat16)
    up_grad = (hidden_grad * gate_act * sigmoid_gate).astype(jnp.bfloat16)
    summed = lax.dot_general(gate_grad, gate_mat, against, preferred_element_type=jnp.float32)
    summed = summed + lax.dot_general(up_grad, up_mat, against, preferred_element_type=jnp.float32)
    return summed.astype(jnp.bfloat16)


def per_device(
    tokens, out_grad, cluster_ids, routes, route_weights, gate_weight, up_weight, down_weight
):
    model_width = tokens.shape[1]
    cent_rows = routes.shape[0]
    fanout = routes.shape[1]
    experts = lax.axis_size("expert")
    capacity = min(cent_rows, 2 * cent_rows * fanout // experts)
    member = (cluster_ids[:, None] == jnp.arange(cent_rows, dtype=jnp.int32)[None, :]).astype(
        jnp.bfloat16
    )
    counts = jnp.sum(member.astype(jnp.float32), axis=0)
    contract = (((0,), (0,)), ((), ()))
    centroid = (
        lax.dot_general(member, tokens, contract, preferred_element_type=jnp.float32)
        / counts[:, None]
    )
    grad_sum = lax.dot_general(member, out_grad, contract, preferred_element_type=jnp.float32)
    pair_ids = routes.reshape(-1)
    matches = (pair_ids[:, None] == jnp.arange(experts, dtype=jnp.int32)[None, :]).astype(jnp.int32)
    earlier = jnp.cumsum(matches, axis=0) - matches
    position = jnp.sum(earlier * matches, axis=1)
    slot_of = (pair_ids * capacity + position).reshape(cent_rows, fanout)
    slot_range = jnp.arange(experts * capacity, dtype=jnp.int32)
    placing = jnp.any(slot_of[None, :, :] == slot_range[:, None, None], axis=2).astype(jnp.bfloat16)
    send_cent = jnp.dot(placing, centroid.astype(jnp.bfloat16), preferred_element_type=jnp.float32)
    send_cent = send_cent.astype(jnp.bfloat16).reshape(experts, capacity, model_width)
    send_grad = jnp.dot(placing, grad_sum.astype(jnp.bfloat16), preferred_element_type=jnp.float32)
    send_grad = send_grad.astype(jnp.bfloat16).reshape(experts, capacity, model_width)
    gate_mat = gate_weight[0]
    up_mat = up_weight[0]
    down_mat = down_weight[0]
    arrived = lax.all_to_all(send_cent, "expert", split_axis=0, concat_axis=0, tiled=True)
    output, gate_act, up_act = expert_forward(
        arrived.reshape(-1, model_width), gate_mat, up_mat, down_mat
    )
    results = lax.all_to_all(
        output.reshape(experts, capacity, model_width),
        "expert",
        split_axis=0,
        concat_axis=0,
        tiled=True,
    )
    arrived_grad = lax.all_to_all(send_grad, "expert", split_axis=0, concat_axis=0, tiled=True)
    input_grad = expert_backward(
        arrived_grad.reshape(-1, model_width), gate_act, up_act, gate_mat, up_mat, down_mat
    )
    results_grad = lax.all_to_all(
        input_grad.reshape(experts, capacity, model_width),
        "expert",
        split_axis=0,
        concat_axis=0,
        tiled=True,
    )
    returned = results.reshape(-1, model_width)[slot_of]
    returned_grad = results_grad.reshape(-1, model_width)[slot_of]
    combined = jnp.sum(route_weights[:, :, None] * returned.astype(jnp.float32), axis=1)
    centroid_grad = (
        jnp.sum(route_weights[:, :, None] * returned_grad.astype(jnp.float32), axis=1) - grad_sum
    )
    layer_out = tokens.astype(jnp.float32) + jnp.take(combined - centroid, cluster_ids, axis=0)
    token_grad = out_grad.astype(jnp.float32) + jnp.take(
        centroid_grad / counts[:, None], cluster_ids, axis=0
    )
    return (layer_out, token_grad)


def solution(mesh):
    placed = (
        P(("groups", "expert"), None),
        P(("groups", "expert"), None),
        P(("groups", "expert")),
        P(("groups", "expert"), None),
        P(("groups", "expert"), None),
        P("expert", None, None),
        P("expert", None, None),
        P("expert", None, None),
    )
    return jax.shard_map(
        per_device,
        mesh=mesh,
        in_specs=placed,
        out_specs=(P(("groups", "expert"), None), P(("groups", "expert"), None)),
        check_vma=False,
    )
```

profile of v0, /device:TPU:13, one launch (start us, length us, event | category | flops | bytes accessed | tf_op | source)
XLA Modules:
  0.0 248.2 jit_solution(3509352852602041339)
XLA Ops:
  0.6 0.9 copy.18
  1.8 0.6 reduce-window.6
  2.8 0.2 fusion.22
  3.0 0.8 convert_reduce_fusion
  3.8 1.3 convolution_divide_fusion
  5.1 0.7 copy-done.3
  5.7 2.1 convolution_convert_fusion.1
  7.8 6.7 %all-to-all-start = ((bf16[16,32,2048]{2,1,0:T(8,128)(2,1)}), bf16[16,32,2048]{2,1,0:T(8,128)(2,1)}, u32[]{:S(2)}, u32[]{:S(2)}) async-start(bf16[16,32,2048]{2,1,0:T(8,128)(2,1)} %bitcast.60), calls=%async_computation | async-start | bytes 4194304 | tf_op jit(solution)/shard_map/all_to_all | solution.py:61
  14.5 1.2 fusion.28
  15.8 0.7 copy-done.1
  16.5 2.1 convolution_convert_fusion
  18.5 43.5 %all-to-all-done = bf16[16,32,2048]{2,1,0:T(8,128)(2,1)} async-done(((bf16[16,32,2048]{2,1,0:T(8,128)(2,1)}), bf16[16,32,2048]{2,1,0:T(8,128)(2,1)}, u32[]{:S(2)}, u32[]{:S(2)}) %all-to-all-start) | async-done | bytes 2097184 | tf_op jit(solution)/shard_map/all_to_all | solution.py:61
  62.0 4.9 %all-to-all-start.2 = ((bf16[16,32,2048]{2,1,0:T(8,128)(2,1)}), bf16[16,32,2048]{2,1,0:T(8,128)(2,1)}, u32[]{:S(2)}, u32[]{:S(2)}) async-start(bf16[16,32,2048]{2,1,0:T(8,128)(2,1)} %bitcast.59), calls=%async_computation.2 | async-start | bytes 4194304 | tf_op jit(solution)/shard_map/all_to_all | solution.py:72
  67.0 5.5 %fusion.10 = f32[512,768]{1,0:T(8,128)} fusion(bf16[512,2048]{1,0:T(8,128)(2,1)} %bitcast.2, bf16[1,2048,768]{2,1,0:T(8,128)(2,1)} %param.15), kind=kOutput, calls=%fused_computation.15 | convolution fusion | flops 1610612736 | bytes 6815744 | tf_op jit(solution)/shard_map/dot_general | solution.py:8
  72.4 4.6 %fusion.6 = f32[512,768]{1,0:T(8,128)} fusion(bf16[512,2048]{1,0:T(8,128)(2,1)} %bitcast.2, bf16[1,2048,768]{2,1,0:T(8,128)(2,1)S(1)} %copy-done), kind=kOutput, calls=%fused_computation.11 | convolution fusion | flops 1610612736 | bytes 6815744 | tf_op jit(solution)/shard_map/dot_general | solution.py:9
  77.0 37.5 %all-to-all-done.2 = bf16[16,32,2048]{2,1,0:T(8,128)(2,1)} async-done(((bf16[16,32,2048]{2,1,0:T(8,128)(2,1)}), bf16[16,32,2048]{2,1,0:T(8,128)(2,1)}, u32[]{:S(2)}, u32[]{:S(2)}) %all-to-all-start.2) | async-done | bytes 2097184 | tf_op jit(solution)/shard_map/all_to_all | solution.py:72
  114.5 4.5 %fusion = f32[512,768]{1,0:T(8,128)S(1)} fusion(bf16[512,2048]{1,0:T(8,128)(2,1)} %bitcast.10, bf16[1,768,2048]{2,1,0:T(8,128)(2,1)} %param.17), kind=kOutput, calls=%fused_computation.5 | convolution fusion | flops 1610612736 | bytes 6815744 | tf_op jit(solution)/shard_map/dot_general | solution.py:18
  119.0 1.9 fusion.4
  120.9 0.5 copy-done.9
  121.3 3.6 %add_convert_fusion = bf16[512,2048]{1,0:T(8,128)(2,1)} fusion(f32[512,2048]{1,0:T(8,128)S(1)} %fusion.4, bf16[1,2048,768]{2,1,0:T(8,128)(2,1)S(1)} %copy-done.7, f32[512,768]{1,0:T(8,128)S(1)} %copy-done.8, f32[512,768]{1,0:T(8,128)S(1)} %fusion, f32[512,768]{1,0:T(8,128)S(1)} %copy-done.9), kind=kOutput, calls=%fused_computation.4 | convolution fusion | flops 1616642048 | bytes 14155776 | tf_op jit(solution)/shard_map/dot_general | solution.py:24
  124.9 4.9 %all-to-all-start.3 = ((bf16[16,32,2048]{2,1,0:T(8,128)(2,1)}), bf16[16,32,2048]{2,1,0:T(8,128)(2,1)}, u32[]{:S(2)}, u32[]{:S(2)}) async-start(bf16[16,32,2048]{2,1,0:T(8,128)(2,1)} %bitcast.62), calls=%async_computation.3 | async-start | bytes 4194304 | tf_op jit(solution)/shard_map/all_to_all | solution.py:76
  129.8 6.0 %fusion.12 = bf16[512,2048]{1,0:T(8,128)(2,1)} fusion(bf16[1,768,2048]{2,1,0:T(8,128)(2,1)} %param.17, f32[512,768]{1,0:T(8,128)} %fusion.6, f32[512,768]{1,0:T(8,128)} %fusion.10), kind=kOutput, calls=%fused_computation.17 | convolution fusion | flops 1614020608 | bytes 8388608 | tf_op jit(solution)/shard_map/dot_general | solution.py:12
  135.8 41.6 %all-to-all-done.3 = bf16[16,32,2048]{2,1,0:T(8,128)(2,1)} async-done(((bf16[16,32,2048]{2,1,0:T(8,128)(2,1)}), bf16[16,32,2048]{2,1,0:T(8,128)(2,1)}, u32[]{:S(2)}, u32[]{:S(2)}) %all-to-all-start.3) | async-done | bytes 2097184 | tf_op jit(solution)/shard_map/all_to_all | solution.py:76
  177.4 5.0 %all-to-all-start.1 = ((bf16[16,32,2048]{2,1,0:T(8,128)(2,1)}), bf16[16,32,2048]{2,1,0:T(8,128)(2,1)}, u32[]{:S(2)}, u32[]{:S(2)}) async-start(bf16[16,32,2048]{2,1,0:T(8,128)(2,1)} %bitcast.61), calls=%async_computation.1 | async-start | bytes 4194304 | tf_op jit(solution)/shard_map/all_to_all | solution.py:65
  182.6 5.2 %gather_fusion.1 = bf16[256,2048]{1,0:T(8,128)(2,1)} fusion(bf16[512,2048]{1,0:T(8,128)(2,1)} %bitcast.12, s32[1024]{0:T(1024)S(1)} %pad_clamp_fusion.1), kind=kCustom, calls=%fused_computation.3 | custom fusion | bytes 2098176 | tf_op jit(solution)/shard_map/gather | solution.py:84
  187.8 42.1 %all-to-all-done.1 = bf16[16,32,2048]{2,1,0:T(8,128)(2,1)} async-done(((bf16[16,32,2048]{2,1,0:T(8,128)(2,1)}), bf16[16,32,2048]{2,1,0:T(8,128)(2,1)}, u32[]{:S(2)}, u32[]{:S(2)}) %all-to-all-start.1) | async-done | bytes 2097184 | tf_op jit(solution)/shard_map/all_to_all | solution.py:65
  229.9 5.2 %gather_fusion = bf16[256,2048]{1,0:T(8,128)(2,1)} fusion(bf16[512,2048]{1,0:T(8,128)(2,1)} %bitcast.7, s32[1024]{0:T(1024)S(1)} %pad_clamp_fusion.1), kind=kCustom, calls=%fused_computation.2 | custom fusion | bytes 2098176 | tf_op jit(solution)/shard_map/gather | solution.py:83
  235.1 3.4 %fusion.17 = (f32[32,2048]{1,0:T(8,128)S(1)}, f32[32,2048]{1,0:T(8,128)S(1)}) fusion(bf16[256,2048]{1,0:T(8,128)(2,1)} %gather_fusion.1, f32[32,8]{1,0:T(8,128)S(1)} %copy.17, bf16[256,2048]{1,0:T(8,128)(2,1)} %gather_fusion), kind=kLoop, calls=%fused_computation.22 | loop fusion | flops 3014656 | bytes 2622464 | tf_op jit(solution)/shard_map/reduce_sum | solution.py:87
  238.5 0.8 subtract_divide_fusion
  239.3 1.9 gather_fusion.2
  241.3 3.3 %gather_fusion.3 = f32[128,2048]{1,0:T(8,128)} fusion(f32[32,2048]{1,0:T(8,128)} %subtract_divide_fusion, s32[1024]{0:T(1024)S(1)} %pad_clamp_fusion), kind=kCustom, calls=%fused_computation.1.clone | custom fusion | bytes 2097664 | tf_op jit(solution)/shard_map/jit(_take)/gather | solution.py:90
  244.6 3.6 %select_add_fusion = (f32[128,2048]{1,0:T(8,128)}, f32[128,2048]{1,0:T(8,128)}) fusion(f32[128,2048]{1,0:T(8,128)} %gather_fusion.3, bf16[128,2048]{1,0:T(8,128)(2,1)} %param.11, pred[128]{0:T(512)(128)(4,1)S(1)} %compare_and_fusion, f32[128,2048]{1,0:T(8,128)} %gather_fusion.2, bf16[128,2048]{1,0:T(8,128)(2,1)} %param.10), kind=kLoop, calls=%fused_computation.29 | loop fusion | flops 1572864 | bytes 5243008 | tf_op jit(solution)/shard_map/add | solution.py:90
  (33 shorter events, 0.9 us)
Async XLA Ops:
  0.6 71.8 %copy-start = (bf16[1,2048,768]{2,1,0:T(8,128)(2,1)S(1)}, bf16[1,2048,768]{2,1,0:T(8,128)(2,1)}, u32[]{:S(2)}) copy-start(bf16[1,2048,768]{2,1,0:T(8,128)(2,1)} %param.16) | copy-start | bytes 9437188
  5.0 0.7 copy-start.3
  7.8 6.7 %copy-start.6 = (s32[128]{0:T(128)S(1)}, s32[128]{0:T(128)}, u32[]{:S(2)}) copy-start(s32[128]{0:T(128)} %param.12) | copy-start | bytes 1540
  7.8 54.2 %all-to-all-start = ((bf16[16,32,2048]{2,1,0:T(8,128)(2,1)}), bf16[16,32,2048]{2,1,0:T(8,128)(2,1)}, u32[]{:S(2)}, u32[]{:S(2)}) async-start(bf16[16,32,2048]{2,1,0:T(8,128)(2,1)} %bitcast.60), calls=%async_computation | async-start | bytes 4194304 | tf_op jit(solution)/shard_map/all_to_all | solution.py:61
  15.8 0.7 copy-start.1
  62.0 52.4 %all-to-all-start.2 = ((bf16[16,32,2048]{2,1,0:T(8,128)(2,1)}), bf16[16,32,2048]{2,1,0:T(8,128)(2,1)}, u32[]{:S(2)}, u32[]{:S(2)}) async-start(bf16[16,32,2048]{2,1,0:T(8,128)(2,1)} %bitcast.59), calls=%async_computation.2 | async-start | bytes 4194304 | tf_op jit(solution)/shard_map/all_to_all | solution.py:72
  114.5 4.5 %copy-start.8 = (f32[512,768]{1,0:T(8,128)S(1)}, f32[512,768]{1,0:T(8,128)}, u32[]{:S(2)}) copy-start(f32[512,768]{1,0:T(8,128)} %fusion.10) | copy-start | bytes 4718596
  119.0 1.9 copy-start.7
  119.0 2.3 copy-start.9
  124.9 52.4 %all-to-all-start.3 = ((bf16[16,32,2048]{2,1,0:T(8,128)(2,1)}), bf16[16,32,2048]{2,1,0:T(8,128)(2,1)}, u32[]{:S(2)}, u32[]{:S(2)}) async-start(bf16[16,32,2048]{2,1,0:T(8,128)(2,1)} %bitcast.62), calls=%async_computation.3 | async-start | bytes 4194304 | tf_op jit(solution)/shard_map/all_to_all | solution.py:76
  177.4 5.1 %copy-start.5 = (f32[32,8]{0,1:T(8,128)S(1)}, f32[32,8]{0,1:T(8,128)}, u32[]{:S(2)}) copy-start(f32[32,8]{0,1:T(8,128)} %param.14) | copy-start | bytes 3076
  177.4 52.6 %all-to-all-start.1 = ((bf16[16,32,2048]{2,1,0:T(8,128)(2,1)}), bf16[16,32,2048]{2,1,0:T(8,128)(2,1)}, u32[]{:S(2)}, u32[]{:S(2)}) async-start(bf16[16,32,2048]{2,1,0:T(8,128)(2,1)} %bitcast.61), calls=%async_computation.1 | async-start | bytes 4194304 | tf_op jit(solution)/shard_map/all_to_all | solution.py:65
  235.1 3.4 %copy-start.4 = (f32[32,2048]{1,0:T(8,128)S(1)}, f32[32,2048]{1,0:T(8,128)}, u32[]{:S(2)}) copy-start(f32[32,2048]{1,0:T(8,128)} %copy-done.3) | copy-start | bytes 786436
  235.1 3.4 %copy-start.2 = (f32[32,2048]{1,0:T(8,128)S(1)}, f32[32,2048]{1,0:T(8,128)}, u32[]{:S(2)}) copy-start(f32[32,2048]{1,0:T(8,128)} %copy-done.1) | copy-start | bytes 786436
where the time goes:
time: 249 us; the launch traced here: 248 us
  waiting for transfers between devices  165 us (66%)
  matrix products  32.6 us (13%)
  starting transfers between devices  21.6 us (9%)
  local copies, waits for them, and re-layouts  19.1 us (8%)
  other arithmetic  9.52 us (4%)
    all_to_all x1, waiting for transfers between devices, per_device(): lax.all_to_all(send_cent, 'expert', split_axis=0, concat_axis=0, tiled=True)  43.5 us
    all_to_all x1, waiting for transfers between devices, per_device(): lax.all_to_all(output.reshape(experts, capacity, model_width), 'expert',...  42.1 us
    all_to_all x1, waiting for transfers between devices, per_device(): lax.all_to_all(input_grad.reshape(experts, capacity, model_width), 'exper...  41.6 us
    all_to_all x1, waiting for transfers between devices, per_device(): lax.all_to_all(send_grad, 'expert', split_axis=0, concat_axis=0, tiled=True)  37.5 us
    all_to_all x1, starting transfers between devices, per_device(): lax.all_to_all(send_cent, 'expert', split_axis=0, concat_axis=0, tiled=True)  6.69 us
    dot_general x1, matrix products, expert_forward(): jnp.dot(hidden, down_mat, preferred_element_type=jnp.float32)  5.97 us
    dot_general x1, matrix products, expert_forward(): gate_act = jnp.dot(inputs, gate_mat, preferred_element_type=jnp.float32)  5.45 us
    gather x1, local copies, waits for them, and re-layouts, per_device(): returned_grad = results_grad.reshape(-1, model_width)[slot_of]  5.19 us
  transfers between devices with their start and end apart: 4, of which 4 were waited for; matrix products, arithmetic and copies ran while one was open for 10% of the time, Pallas kernels for 0%

commit v1 on v0

--- a/solution.py
+++ b/solution.py
@@ -26,7 +26,7 @@
     return summed.astype(jnp.bfloat16)
 
 
-def per_device(
+def per_device_slots(
     tokens, out_grad, cluster_ids, routes, route_weights, gate_weight, up_weight, down_weight
 ):
     model_width = tokens.shape[1]
@@ -93,6 +93,72 @@
     return (layer_out, token_grad)
 
 
+def expert_dense(cent_in, grad_in, gate_mat, up_mat, down_mat):
+    against = (((1,), (1,)), ((), ()))
+    gate_act = jnp.dot(cent_in, gate_mat, preferred_element_type=jnp.float32)
+    up_act = jnp.dot(cent_in, up_mat, preferred_element_type=jnp.float32)
+    sigmoid_gate = jax.nn.sigmoid(gate_act)
+    hidden = (gate_act * sigmoid_gate * up_act).astype(jnp.bfloat16)
+    output = jnp.dot(hidden, down_mat, preferred_element_type=jnp.float32).astype(jnp.bfloat16)
+    hidden_grad = lax.dot_general(grad_in, down_mat, against, preferred_element_type=jnp.float32)
+    gate_grad = (
+        hidden_grad * up_act * sigmoid_gate * (1.0 + gate_act * (1.0 - sigmoid_gate))
+    ).astype(jnp.bfloat16)
+    up_grad = (hidden_grad * gate_act * sigmoid_gate).astype(jnp.bfloat16)
+    summed = lax.dot_general(gate_grad, gate_mat, against, preferred_element_type=jnp.float32)
+    summed = summed + lax.dot_general(up_grad, up_mat, against, preferred_element_type=jnp.float32)
+    return output, summed.astype(jnp.bfloat16)
+
+
+def per_device_dense(
+    tokens, out_grad, cluster_ids, routes, route_weights, gate_weight, up_weight, down_weight
+):
+    cent_rows = routes.shape[0]
+    me = lax.axis_index("expert")
+    member = (cluster_ids[:, None] == jnp.arange(cent_rows, dtype=jnp.int32)[None, :]).astype(
+        jnp.bfloat16
+    )
+    counts = jnp.sum(member.astype(jnp.float32), axis=0)
+    contract = (((0,), (0,)), ((), ()))
+    centroid = (
+        lax.dot_general(member, tokens, contract, preferred_element_type=jnp.float32)
+        / counts[:, None]
+    )
+    grad_sum = lax.dot_general(member, out_grad, contract, preferred_element_type=jnp.float32)
+    both = jnp.stack([centroid.astype(jnp.bfloat16), grad_sum.astype(jnp.bfloat16)])
+    gathered = lax.all_gather(both, "expert", axis=1, tiled=True)
+    all_routes = lax.all_gather(routes, "expert", axis=0, tiled=True)
+    all_weights = lax.all_gather(route_weights, "expert", axis=0, tiled=True)
+    mine = jnp.sum(jnp.where(all_routes == me, all_weights, 0.0), axis=1)
+    output, input_grad = expert_dense(
+        gathered[0], gathered[1], gate_weight[0], up_weight[0], down_weight[0]
+    )
+    parts = jnp.stack(
+        [
+            (mine[:, None] * output.astype(jnp.float32)).astype(jnp.bfloat16),
+            (mine[:, None] * input_grad.astype(jnp.float32)).astype(jnp.bfloat16),
+        ]
+    )
+    summed = lax.psum_scatter(parts, "expert", scatter_dimension=1, tiled=True)
+    combined = summed[0].astype(jnp.float32)
+    centroid_grad = summed[1].astype(jnp.float32) - grad_sum
+    layer_out = tokens.astype(jnp.float32) + jnp.take(combined - centroid, cluster_ids, axis=0)
+    token_grad = out_grad.astype(jnp.float32) + jnp.take(
+        centroid_grad / counts[:, None], cluster_ids, axis=0
+    )
+    return (layer_out, token_grad)
+
+
+def per_device(*args):
+    routes = args[3]
+    cent_rows, fanout = routes.shape
+    experts = lax.axis_size("expert")
+    capacity = min(cent_rows, 2 * cent_rows * fanout // experts)
+    if capacity == cent_rows:
+        return per_device_dense(*args)
+    return per_device_slots(*args)
+
+
 def solution(mesh):
     placed = (
         P(("groups", "expert"), None),

time: 249 us -> 172 us (0.69)
  the two profiles are of different devices: /device:TPU:13 before, /device:TPU:0 now
where the time goes in v1:
time: 172 us
  waiting for transfers between devices  82.8 us (48%)
  blocking collectives  41.5 us (24%)
  matrix products  16.7 us (10%)
  between operations  14.2 us (8%)
  other arithmetic  9.5 us (6%)
  local copies, waits for them, and re-layouts  6.92 us (4%)
    reduce_scatter x1, waiting for transfers between devices, per_device_dense(): summed = lax.psum_scatter(parts, 'expert', scatter_dimension=1, tiled=True)  70.8 us
    all_gather x1, blocking collectives, per_device_dense(): all_routes = lax.all_gather(routes, 'expert', axis=0, tiled=True)  23.5 us
    all_gather x1, blocking collectives, per_device_dense(): all_weights = lax.all_gather(route_weights, 'expert', axis=0, tiled=True)  18 us
    all_gather x1, waiting for transfers between devices, per_device_dense(): gathered = lax.all_gather(both, 'expert', axis=1, tiled=True)  12 us
    dot_general x1, matrix products, expert_dense(): gate_act = jnp.dot(cent_in, gate_mat, preferred_element_type=jnp.float32)  4.45 us
    add x1, other arithmetic, per_device_dense(): out_grad.astype(jnp.float32)  3.58 us
  transfers between devices with their start and end apart: 2, of which 2 were waited for; matrix products, arithmetic and copies ran while one was open for 0% of the time, Pallas kernels for 0%

profile of v1, /device:TPU:0, one launch (start us, length us, event | category | flops | bytes accessed | tf_op | source)
XLA Modules:
  0.0 171.6 jit_solution(13665000438344344411)
XLA Ops:
  7.2 0.0 copy-start
  7.2 0.0 all-gather.4.cloned.1.call-start
  7.2 0.9 convert_reduce_fusion
  8.2 1.3 fusion.31
  9.4 0.0 copy-start.1
  9.4 1.4 convolution_divide_fusion
  10.9 0.6 copy-done.2
  11.5 0.7 pad_maximum_fusion.1
  12.2 0.0 all-gather.4.cloned.1.call-update
  12.3 0.0 reduce-scatter.2.cloned.1.call-start
  12.3 23.5 %all-gather = s32[16,32,8]{1,2,0:T(8,128)S(1)} all-gather(s32[1,32,8]{1,2,0:T(8,128)S(1)} %bitcast.56), channel_id=1, replica_groups=mesh['groups'=2,'expert'=16] {'expert'}, dimensions={0}, use_global_device_ids=true | all-gather | bytes 17408 | tf_op jit(solution)/shard_map/all_gather | solution.py:130
  35.8 18.0 %all-gather.1 = f32[16,32,8]{1,2,0:T(8,128)S(1)} all-gather(f32[1,32,8]{1,2,0:T(8,128)S(1)} %bitcast.57), channel_id=1, replica_groups=mesh['groups'=2,'expert'=16] {'expert'}, dimensions={0}, use_global_device_ids=true | all-gather | bytes 17408 | tf_op jit(solution)/shard_map/all_gather | solution.py:131
  53.9 0.1 reshape.44
  53.9 12.0 %all-gather.4.cloned.1.call-done = bf16[2,512,2048]{2,1,0:T(8,128)(2,1)} async-done(((bf16[2,32,2048]{2,1,0:T(8,128)(2,1)}), bf16[2,512,2048]{2,1,0:T(8,128)(2,1)}) %all-gather.4.cloned.1.call-update) | async-done | bytes 4194320 | tf_op jit(solution)/shard_map/all_gather | solution.py:129
  65.9 4.5 %fusion.10 = f32[512,768]{1,0:T(8,128)S(1)} fusion(bf16[1,2048,768]{2,1,0:T(8,128)(2,1)} %param.15, bf16[2,512,2048]{2,1,0:T(8,128)(2,1)} %all-gather.4.cloned.1.call-done), kind=kOutput, calls=%fused_computation.16 | convolution fusion | flops 1610612736 | bytes 6815744 | tf_op jit(solution)/shard_map/dot_general | solution.py:98
  70.4 0.0 copy-done.6
  70.4 0.3 copy-done.7
  70.6 1.8 %fusion = f32[512,768]{1,0:T(8,128)S(1)} fusion(bf16[1,768,2048]{2,1,0:T(8,128)(2,1)S(1)} %copy-done.7, bf16[2,512,2048]{2,1,0:T(8,128)(2,1)S(1)} %copy-done.6), kind=kOutput, calls=%fused_computation.6 | convolution fusion | flops 1610612736 | bytes 6815744 | tf_op jit(solution)/shard_map/dot_general | solution.py:103
  72.5 1.9 %fusion.4 = f32[512,2048]{1,0:T(8,128)S(1)} fusion(bf16[1,2048,768]{2,1,0:T(8,128)(2,1)S(1)} %copy-done, f32[512,768]{1,0:T(8,128)S(1)} %fusion, f32[512,768]{1,0:T(8,128)S(1)} %fusion.10), kind=kOutput, calls=%fused_computation.10 | convolution fusion | flops 1612972032 | bytes 10485760 | tf_op jit(solution)/shard_map/dot_general | solution.py:109
  74.3 1.8 %fusion.6 = f32[512,768]{1,0:T(8,128)S(1)} fusion(bf16[1,2048,768]{2,1,0:T(8,128)(2,1)S(1)} %copy-done, bf16[2,512,2048]{2,1,0:T(8,128)(2,1)S(1)} %copy-done.6), kind=kOutput, calls=%fused_computation.12 | convolution fusion | flops 1610612736 | bytes 6815744 | tf_op jit(solution)/shard_map/dot_general | solution.py:99
  76.1 0.0 copy-start.8
  76.1 1.8 %fusion.19 = bf16[1,512,2048]{2,1,0:T(8,128)(2,1)S(1)} fusion(bf16[1,768,2048]{2,1,0:T(8,128)(2,1)S(1)} %copy-done.7, f32[512]{0:T(512)S(1)} %reshape.44, f32[512,768]{1,0:T(8,128)S(1)} %fusion.6, f32[512,768]{1,0:T(8,128)S(1)} %fusion.10), kind=kOutput, calls=%fused_computation.19 | convolution fusion | flops 1617166336 | bytes 8390656 | tf_op jit(solution)/shard_map/dot_general | solution.py:102
  78.0 0.0 copy-done.8
  78.0 2.3 %fusion.24 = bf16[1,512,2048]{2,1,0:T(8,128)(2,1)S(1)} fusion(f32[512,2048]{1,0:T(8,128)S(1)} %fusion.4, bf16[1,2048,768]{2,1,0:T(8,128)(2,1)S(1)} %copy-done.8, f32[512]{0:T(512)S(1)} %reshape.44, f32[512,768]{1,0:T(8,128)S(1)} %fusion.10, f32[512,768]{1,0:T(8,128)S(1)} %fusion, f32[512,768]{1,0:T(8,128)S(1)} %fusion.6), kind=kOutput, calls=%fused_computation.20 | convolution fusion | flops 1619787776 | bytes 14157824 | tf_op jit(solution)/shard_map/dot_general | solution.py:108
  80.3 2.3 %pad_maximum_fusion = bf16[2,512,2048]{2,1,0:T(8,128)(2,1)} fusion(bf16[1,512,2048]{2,1,0:T(8,128)(2,1)S(1)} %fusion.24, bf16[1,512,2048]{2,1,0:T(8,128)(2,1)S(1)} %fusion.19), kind=kLoop, calls=%fused_computation.2 | loop fusion | flops 2097152 | bytes 8388608 | tf_op jit(solution)/shard_map/stack | solution.py:136
  82.6 0.0 reduce-scatter.2.cloned.1.call-update
  82.7 0.6 copy-done.5
  83.3 70.8 %reduce-scatter.2.cloned.1.call-done = bf16[2,32,2048]{2,1,0:T(8,128)(2,1)} async-done(((bf16[2,512,2048]{2,1,0:T(8,128)(2,1)}), bf16[2,32,2048]{2,1,0:T(8,128)(2,1)}) %reduce-scatter.2.cloned.1.call-update) | async-done | bytes 262160 | tf_op jit(solution)/shard_map/reduce_scatter | solution.py:142
  154.1 1.9 %fusion.30 = (f32[32,2048]{1,0:T(8,128)S(1)}, f32[32,2048]{1,0:T(8,128)}) fusion(f32[32,2048]{1,0:T(8,128)} %copy-done.1, bf16[2,32,2048]{2,1,0:T(8,128)(2,1)} %reduce-scatter.2.cloned.1.call-done, f32[32]{0:T(128)S(1)} %convert_reduce_fusion, f32[32,2048]{1,0:T(8,128)} %copy-done.2), kind=kLoop, calls=%fused_computation.35 | loop fusion | flops 327680 | bytes 1310848 | tf_op jit(solution)/shard_map/div | solution.py:147
  156.0 3.3 %gather_fusion = f32[128,2048]{1,0:T(8,128)} fusion(f32[32,2048]{1,0:T(8,128)} %get-tuple-element.4, s32[1024]{0:T(1024)S(1)} %pad_clamp_fusion), kind=kCustom, calls=%fused_computation.clone | custom fusion | bytes 2097664 | tf_op jit(solution)/shard_map/jit(_take)/gather | solution.py:145
  159.3 1.9 %gather_fusion.1 = f32[128,2048]{1,0:T(8,128)} fusion(f32[32,2048]{1,0:T(8,128)S(1)} %get-tuple-element.3, s32[1024]{0:T(1024)S(1)} %pad_clamp_fusion), kind=kCustom, calls=%fused_computation.1.clone | custom fusion | bytes 2097664 | tf_op jit(solution)/shard_map/jit(_take)/gather | solution.py:146
  161.2 3.6 %select_add_fusion = (f32[128,2048]{1,0:T(8,128)}, f32[128,2048]{1,0:T(8,128)}) fusion(f32[128,2048]{1,0:T(8,128)} %gather_fusion.1, bf16[128,2048]{1,0:T(8,128)(2,1)} %param.11, pred[128]{0:T(512)(128)(4,1)S(1)} %compare_and_fusion, f32[128,2048]{1,0:T(8,128)} %gather_fusion, bf16[128,2048]{1,0:T(8,128)(2,1)} %param.10), kind=kLoop, calls=%fused_computation.28 | loop fusion | flops 1572864 | bytes 5243008 | tf_op jit(solution)/shard_map/add | solution.py:146
  (15 shorter events, 0.1 us)
Async XLA Ops:
  7.2 65.3 %copy-start = (bf16[1,2048,768]{2,1,0:T(8,128)(2,1)S(1)}, bf16[1,2048,768]{2,1,0:T(8,128)(2,1)}, u32[]{:S(2)}) copy-start(bf16[1,2048,768]{2,1,0:T(8,128)(2,1)} %param.16) | copy-start | bytes 9437188
  7.2 5.1 %copy-start.3 = (s32[32,8]{0,1:T(8,128)S(1)}, s32[32,8]{0,1:T(8,128)}, u32[]{:S(2)}) copy-start(s32[32,8]{0,1:T(8,128)} %param.13) | copy-start | bytes 3076
  7.2 28.6 %copy-start.4 = (f32[32,8]{0,1:T(8,128)S(1)}, f32[32,8]{0,1:T(8,128)}, u32[]{:S(2)}) copy-start(f32[32,8]{0,1:T(8,128)} %param.14) | copy-start | bytes 3076
  7.2 58.7 %all-gather.4.cloned.1.call-start = ((), (), s32[]{:S(2)}) async-start(), calls=%async_computation.1 | async-start | bytes 4456448 | tf_op jit(solution)/shard_map/all_gather | solution.py:129
  9.4 1.4 copy-start.1
  10.8 0.7 copy-start.2
  12.3 141.8 %reduce-scatter.2.cloned.1.call-start = ((), (), s32[]{:S(2)}) async-start(), calls=%async_computation.2 | async-start | bytes 4456448 | tf_op jit(solution)/shard_map/reduce_scatter | solution.py:142
  65.9 4.5 %copy-start.6 = (bf16[2,512,2048]{2,1,0:T(8,128)(2,1)S(1)}, bf16[2,512,2048]{2,1,0:T(8,128)(2,1)}, u32[]{:S(2)}) copy-start(bf16[2,512,2048]{2,1,0:T(8,128)(2,1)} %all-gather.4.cloned.1.call-done) | copy-start | bytes 12582916
  65.9 4.7 %copy-start.7 = (bf16[1,768,2048]{2,1,0:T(8,128)(2,1)S(1)}, bf16[1,768,2048]{2,1,0:T(8,128)(2,1)}, u32[]{:S(2)}) copy-start(bf16[1,768,2048]{2,1,0:T(8,128)(2,1)} %param.17) | copy-start | bytes 9437188
  76.1 1.9 %copy-start.8 = (bf16[1,2048,768]{2,1,0:T(8,128)(2,1)S(1)}, bf16[1,2048,768]{2,1,0:T(8,128)(2,1)}, u32[]{:S(2)}) copy-start(bf16[1,2048,768]{2,1,0:T(8,128)(2,1)} %param.15) | copy-start | bytes 9437188
  82.6 0.7 copy-start.5
Sparse Core Ops, SparseCore 0:
  12.4 53.4 all-gather.3
  82.8 71.2 reduce-scatter.1

commit v2 on v1

--- a/solution.py
+++ b/solution.py
@@ -125,13 +125,26 @@
         / counts[:, None]
     )
     grad_sum = lax.dot_general(member, out_grad, contract, preferred_element_type=jnp.float32)
-    both = jnp.stack([centroid.astype(jnp.bfloat16), grad_sum.astype(jnp.bfloat16)])
-    gathered = lax.all_gather(both, "expert", axis=1, tiled=True)
-    all_routes = lax.all_gather(routes, "expert", axis=0, tiled=True)
-    all_weights = lax.all_gather(route_weights, "expert", axis=0, tiled=True)
-    mine = jnp.sum(jnp.where(all_routes == me, all_weights, 0.0), axis=1)
+    experts = lax.axis_size("expert")
+    model_width = tokens.shape[1]
+    picked = routes[:, :, None] == jnp.arange(experts, dtype=jnp.int32)[None, None, :]
+    per_expert = jnp.sum(jnp.where(picked, route_weights[:, :, None], 0.0), axis=1)
+    weight_hi = per_expert.astype(jnp.bfloat16)
+    weight_lo = (per_expert - weight_hi.astype(jnp.float32)).astype(jnp.bfloat16)
+    side = jnp.concatenate([weight_hi, weight_lo], axis=1)
+    side_width = -(-side.shape[1] // 128) * 128
+    side = jnp.pad(side, ((0, 0), (0, side_width - side.shape[1])))
+    payload = jnp.concatenate(
+        [centroid.astype(jnp.bfloat16), grad_sum.astype(jnp.bfloat16), side], axis=1
+    )
+    gathered = lax.all_gather(payload, "expert", axis=0, tiled=True)
+    cent_all = gathered[:, :model_width]
+    grad_all = gathered[:, model_width : 2 * model_width]
+    side_all = gathered[:, 2 * model_width : 2 * model_width + 2 * experts].astype(jnp.float32)
+    column = jnp.arange(experts, dtype=jnp.int32)[None, :]
+    mine = jnp.sum(jnp.where(column == me, side_all[:, :experts] + side_all[:, experts:], 0.0), axis=1)
     output, input_grad = expert_dense(
-        gathered[0], gathered[1], gate_weight[0], up_weight[0], down_weight[0]
+        cent_all, grad_all, gate_weight[0], up_weight[0], down_weight[0]
     )
     parts = jnp.stack(
         [

time: 172 us -> 175 us (1.017)
  waiting for transfers between devices: 82.8 us -> 125 us
  blocking collectives: 41.5 us -> 0 us
  other arithmetic: 9.5 us -> 11.4 us
    all_gather x1, waiting for transfers between devices: 12 us -> 54 us  [per_device_dense(): gathered = lax.all_gather(payload, 'expert', axis=0, tiled=True)]
    all_gather x2 -> x0, blocking collectives: 41.5 us -> none  [the longest x1 23.5 us: per_device_dense(): all_routes = lax.all_gather(routes, 'expert', axis=0, tiled=True)]
where the time goes in v2:
time: 175 us; the launch traced here: 174 us
  waiting for transfers between devices  125 us (71%)
  matrix products  18 us (10%)
  between operations  14.2 us (8%)
  other arithmetic  11.4 us (7%)
  local copies, waits for them, and re-layouts  5.99 us (3%)
    reduce_scatter x1, waiting for transfers between devices, per_device_dense(): summed = lax.psum_scatter(parts, 'expert', scatter_dimension=1, tiled=True)  70.5 us
    all_gather x1, waiting for transfers between devices, per_device_dense(): gathered = lax.all_gather(payload, 'expert', axis=0, tiled=True)  54 us
    dot_general x1, matrix products, expert_dense(): gate_act = jnp.dot(cent_in, gate_mat, preferred_element_type=jnp.float32)  4.47 us
    add x1, other arithmetic, per_device_dense(): out_grad.astype(jnp.float32)  3.58 us
  transfers between devices with their start and end apart: 2, of which 2 were waited for; matrix products, arithmetic and copies ran while one was open for 0% of the time, Pallas kernels for 0%

profile of v2, /device:TPU:0, one launch (start us, length us, event | category | flops | bytes accessed | tf_op | source)
XLA Modules:
  0.0 174.3 jit_solution(680471912613489576)
XLA Ops:
  7.2 0.0 copy-start
  7.2 0.0 all-gather.2.cloned.1.call-start
  7.2 0.9 convert_reduce_fusion
  8.1 0.7 select_reduce_fusion
  8.9 0.1 copy.15
  9.0 2.0 %fusion.45 = (bf16[32,2048]{1,0:T(8,128)(2,1)S(1)}, f32[32,2048]{1,0:T(8,128)}) fusion(bf16[128,2048]{1,0:T(8,128)(2,1)} %param.11, s32[128]{0:T(128)} %param.12), kind=kOutput, calls=%fused_computation.63 | convolution fusion | flops 16846848 | bytes 918016 | tf_op jit(solution)/shard_map/dot_general | solution.py:127
  11.0 2.0 %fusion.46 = (bf16[32,2048]{1,0:T(8,128)(2,1)S(1)}, f32[32,2048]{1,0:T(8,128)}) fusion(f32[32]{0:T(128)S(1)} %convert_reduce_fusion, bf16[128,2048]{1,0:T(8,128)(2,1)} %param.10, s32[128]{0:T(128)} %param.12), kind=kOutput, calls=%fused_computation.64 | convolution fusion | flops 16912384 | bytes 918144 | tf_op jit(solution)/shard_map/dot_general | solution.py:124
  12.9 0.7 fusion.34
  13.6 0.0 all-gather.2.cloned.1.call-update
  13.7 0.0 reduce-scatter.2.cloned.1.call-start
  13.7 54.0 %all-gather.2.cloned.1.call-done = bf16[512,4224]{1,0:T(8,128)(2,1)} async-done(((bf16[32,4224]{1,0:T(8,128)(2,1)}), bf16[512,4224]{1,0:T(8,128)(2,1)}) %all-gather.2.cloned.1.call-update) | async-done | bytes 4325392 | tf_op jit(solution)/shard_map/all_gather | solution.py:140
  67.8 0.9 slice_convert_fusion
  68.7 0.0 slice-start
  68.7 0.2 fusion.36
  68.9 0.0 copy-start.2
  69.0 4.5 %fusion.10 = f32[512,768]{1,0:T(8,128)S(1)} fusion(bf16[1,2048,768]{2,1,0:T(8,128)(2,1)} %param.15, bf16[512,4224]{1,0:T(8,128)(2,1)} %all-gather.2.cloned.1.call-done), kind=kOutput, calls=%fused_computation.16 | convolution fusion | flops 1610612736 | bytes 6815744 | tf_op jit(solution)/shard_map/dot_general | solution.py:98
  73.4 0.0 slice-done
  73.5 1.8 %fusion = f32[512,768]{1,0:T(8,128)S(1)} fusion(bf16[1,768,2048]{2,1,0:T(8,128)(2,1)S(1)} %copy-done.2, bf16[512,4224]{1,0:T(8,128)(2,1)S(1)} %bitcast.44), kind=kOutput, calls=%fused_computation.6 | convolution fusion | flops 1610612736 | bytes 6815744 | tf_op jit(solution)/shard_map/dot_general | solution.py:103
  75.3 1.9 %fusion.4 = f32[512,2048]{1,0:T(8,128)S(1)} fusion(bf16[1,2048,768]{2,1,0:T(8,128)(2,1)S(1)} %copy-done, f32[512,768]{1,0:T(8,128)S(1)} %fusion, f32[512,768]{1,0:T(8,128)S(1)} %fusion.10), kind=kOutput, calls=%fused_computation.10 | convolution fusion | flops 1612972032 | bytes 10485760 | tf_op jit(solution)/shard_map/dot_general | solution.py:109
  77.2 1.8 %fusion.6 = f32[512,768]{1,0:T(8,128)S(1)} fusion(bf16[1,2048,768]{2,1,0:T(8,128)(2,1)S(1)} %copy-done, bf16[512,4224]{1,0:T(8,128)(2,1)S(1)} %bitcast.44), kind=kOutput, calls=%fused_computation.12 | convolution fusion | flops 1610612736 | bytes 6815744 | tf_op jit(solution)/shard_map/dot_general | solution.py:99
  79.0 0.0 copy-start.3
  79.0 1.9 %fusion.19 = bf16[1,512,2048]{2,1,0:T(8,128)(2,1)S(1)} fusion(bf16[1,768,2048]{2,1,0:T(8,128)(2,1)S(1)} %copy-done.2, f32[512]{0:T(512)S(1)} %fusion.36, f32[512,768]{1,0:T(8,128)S(1)} %fusion.6, f32[512,768]{1,0:T(8,128)S(1)} %fusion.10), kind=kOutput, calls=%fused_computation.19 | convolution fusion | flops 1617166336 | bytes 8390656 | tf_op jit(solution)/shard_map/dot_general | solution.py:102
  80.9 0.0 copy-done.3
  80.9 2.3 %fusion.24 = bf16[1,512,2048]{2,1,0:T(8,128)(2,1)S(1)} fusion(f32[512,2048]{1,0:T(8,128)S(1)} %fusion.4, bf16[1,2048,768]{2,1,0:T(8,128)(2,1)S(1)} %copy-done.3, f32[512]{0:T(512)S(1)} %fusion.36, f32[512,768]{1,0:T(8,128)S(1)} %fusion.10, f32[512,768]{1,0:T(8,128)S(1)} %fusion, f32[512,768]{1,0:T(8,128)S(1)} %fusion.6), kind=kOutput, calls=%fused_computation.20 | convolution fusion | flops 1619787776 | bytes 14157824 | tf_op jit(solution)/shard_map/dot_general | solution.py:108
  83.2 2.3 %pad_maximum_fusion = bf16[2,512,2048]{2,1,0:T(8,128)(2,1)} fusion(bf16[1,512,2048]{2,1,0:T(8,128)(2,1)S(1)} %fusion.24, bf16[1,512,2048]{2,1,0:T(8,128)(2,1)S(1)} %fusion.19), kind=kLoop, calls=%fused_computation.2 | loop fusion | flops 2097152 | bytes 8388608 | tf_op jit(solution)/shard_map/stack | solution.py:149
  85.5 0.0 reduce-scatter.2.cloned.1.call-update
  85.5 0.6 copy-done.1
  86.2 70.5 %reduce-scatter.2.cloned.1.call-done = bf16[2,32,2048]{2,1,0:T(8,128)(2,1)} async-done(((bf16[2,512,2048]{2,1,0:T(8,128)(2,1)}), bf16[2,32,2048]{2,1,0:T(8,128)(2,1)}) %reduce-scatter.2.cloned.1.call-update) | async-done | bytes 262160 | tf_op jit(solution)/shard_map/reduce_scatter | solution.py:155
  156.7 2.0 %fusion.37 = (f32[32,2048]{1,0:T(8,128)}, f32[32,2048]{1,0:T(8,128)S(1)}) fusion(f32[32,2048]{1,0:T(8,128)} %get-tuple-element.10, bf16[2,32,2048]{2,1,0:T(8,128)(2,1)} %reduce-scatter.2.cloned.1.call-done, f32[32]{0:T(128)S(1)} %convert_reduce_fusion, f32[32,2048]{1,0:T(8,128)} %get-tuple-element.12), kind=kLoop, calls=%fused_computation.41 | loop fusion | flops 327680 | bytes 1310848 | tf_op jit(solution)/shard_map/div | solution.py:160
  158.6 3.3 %gather_fusion.1 = f32[128,2048]{1,0:T(8,128)} fusion(f32[32,2048]{1,0:T(8,128)} %get-tuple-element.5, s32[1024]{0:T(1024)S(1)} %pad_clamp_fusion), kind=kCustom, calls=%fused_computation.1.clone | custom fusion | bytes 2097664 | tf_op jit(solution)/shard_map/jit(_take)/gather | solution.py:159
  161.9 1.9 %gather_fusion = f32[128,2048]{1,0:T(8,128)} fusion(f32[32,2048]{1,0:T(8,128)S(1)} %get-tuple-element.6, s32[1024]{0:T(1024)S(1)} %pad_clamp_fusion), kind=kCustom, calls=%fused_computation.clone | custom fusion | bytes 2097664 | tf_op jit(solution)/shard_map/jit(_take)/gather | solution.py:158
  163.9 3.6 %select_add_fusion = (f32[128,2048]{1,0:T(8,128)}, f32[128,2048]{1,0:T(8,128)}) fusion(f32[128,2048]{1,0:T(8,128)} %gather_fusion.1, bf16[128,2048]{1,0:T(8,128)(2,1)} %param.11, pred[128]{0:T(512)(128)(4,1)S(1)} %compare_and_fusion, f32[128,2048]{1,0:T(8,128)} %gather_fusion, bf16[128,2048]{1,0:T(8,128)(2,1)} %param.10), kind=kLoop, calls=%fused_computation.29 | loop fusion | flops 1572864 | bytes 5243008 | tf_op jit(solution)/shard_map/add | solution.py:159
  (12 shorter events, 0.0 us)
Async XLA Ops:
  7.2 68.1 %copy-start = (bf16[1,2048,768]{2,1,0:T(8,128)(2,1)S(1)}, bf16[1,2048,768]{2,1,0:T(8,128)(2,1)}, u32[]{:S(2)}) copy-start(bf16[1,2048,768]{2,1,0:T(8,128)(2,1)} %param.16) | copy-start | bytes 9437188
  7.2 60.6 %all-gather.2.cloned.1.call-start = ((), (), s32[]{:S(2)}) async-start(), calls=%async_computation.1 | async-start | bytes 4595712 | tf_op jit(solution)/shard_map/all_gather | solution.py:140
  13.7 143.0 %reduce-scatter.2.cloned.1.call-start = ((), (), s32[]{:S(2)}) async-start(), calls=%async_computation.2 | async-start | bytes 4456448 | tf_op jit(solution)/shard_map/reduce_scatter | solution.py:155
  68.7 4.7 %slice-start = ((s8[4325376]{0:T(1024)(128)(4,1)}), s8[4194304]{0:T(1024)(128)(4,1)S(1)}, s32[]{:S(2)}) async-start(s8[4325376]{0:T(1024)(128)(4,1)} %bitcast.43), calls=%async_computation.3 | async-start | bytes 8388608
  68.9 4.5 %slice-start.1 = ((s8[4325376]{0:T(1024)(128)(4,1)}), s8[131072]{0:T(1024)(128)(4,1)S(1)}, s32[]{:S(2)}) async-start(s8[4325376]{0:T(1024)(128)(4,1)} %bitcast.43), calls=%async_computation.4 | async-start | bytes 262144
  68.9 4.5 %copy-start.2 = (bf16[1,768,2048]{2,1,0:T(8,128)(2,1)S(1)}, bf16[1,768,2048]{2,1,0:T(8,128)(2,1)}, u32[]{:S(2)}) copy-start(bf16[1,768,2048]{2,1,0:T(8,128)(2,1)} %param.17) | copy-start | bytes 9437188
  79.0 1.9 %copy-start.3 = (bf16[1,2048,768]{2,1,0:T(8,128)(2,1)S(1)}, bf16[1,2048,768]{2,1,0:T(8,128)(2,1)}, u32[]{:S(2)}) copy-start(bf16[1,2048,768]{2,1,0:T(8,128)(2,1)} %param.15) | copy-start | bytes 9437188
  85.5 0.7 copy-start.1
Sparse Core Ops, SparseCore 0:
  13.8 53.9 all-gather.1
  85.7 70.9 reduce-scatter.1

commit v3 on v2

--- a/solution.py
+++ b/solution.py
@@ -134,27 +134,22 @@
     side = jnp.concatenate([weight_hi, weight_lo], axis=1)
     side_width = -(-side.shape[1] // 128) * 128
     side = jnp.pad(side, ((0, 0), (0, side_width - side.shape[1])))
-    payload = jnp.concatenate(
-        [centroid.astype(jnp.bfloat16), grad_sum.astype(jnp.bfloat16), side], axis=1
-    )
+    payload = jnp.concatenate([centroid.astype(jnp.bfloat16), side], axis=1)
     gathered = lax.all_gather(payload, "expert", axis=0, tiled=True)
+    grad_all = lax.all_gather(grad_sum.astype(jnp.bfloat16), "expert", axis=0, tiled=True)
     cent_all = gathered[:, :model_width]
-    grad_all = gathered[:, model_width : 2 * model_width]
-    side_all = gathered[:, 2 * model_width : 2 * model_width + 2 * experts].astype(jnp.float32)
+    side_all = gathered[:, model_width : model_width + 2 * experts].astype(jnp.float32)
     column = jnp.arange(experts, dtype=jnp.int32)[None, :]
     mine = jnp.sum(jnp.where(column == me, side_all[:, :experts] + side_all[:, experts:], 0.0), axis=1)
     output, input_grad = expert_dense(
         cent_all, grad_all, gate_weight[0], up_weight[0], down_weight[0]
     )
-    parts = jnp.stack(
-        [
-            (mine[:, None] * output.astype(jnp.float32)).astype(jnp.bfloat16),
-            (mine[:, None] * input_grad.astype(jnp.float32)).astype(jnp.bfloat16),
-        ]
-    )
-    summed = lax.psum_scatter(parts, "expert", scatter_dimension=1, tiled=True)
-    combined = summed[0].astype(jnp.float32)
-    centroid_grad = summed[1].astype(jnp.float32) - grad_sum
+    weighted_out = (mine[:, None] * output.astype(jnp.float32)).astype(jnp.bfloat16)
+    weighted_grad = (mine[:, None] * input_grad.astype(jnp.float32)).astype(jnp.bfloat16)
+    summed_out = lax.psum_scatter(weighted_out, "expert", scatter_dimension=0, tiled=True)
+    summed_grad = lax.psum_scatter(weighted_grad, "expert", scatter_dimension=0, tiled=True)
+    combined = summed_out.astype(jnp.float32)
+    centroid_grad = summed_grad.astype(jnp.float32) - grad_sum
     layer_out = tokens.astype(jnp.float32) + jnp.take(combined - centroid, cluster_ids, axis=0)
     token_grad = out_grad.astype(jnp.float32) + jnp.take(
         centroid_grad / counts[:, None], cluster_ids, axis=0

time: 175 us -> 250 us (1.43)
  waiting for transfers between devices: 125 us -> 193 us
  matrix products: 18 us -> 27.4 us
    reduce_scatter x1 -> x2, waiting for transfers between devices: 70.5 us -> 116 us  [the longest x1 61.6 us: per_device_dense(): lax.psum_scatter(weighted_out, 'expert', scatter_dimension=0, tiled=True)]
    all_gather x0 -> x1, waiting for transfers between devices: none -> 40.5 us  [per_device_dense(): lax.all_gather(grad_sum.astype(jnp.bfloat16), 'expert', axis=0, tiled=True)]
    all_gather x1, waiting for transfers between devices: 54 us -> 37.3 us  [per_device_dense(): gathered = lax.all_gather(payload, 'expert', axis=0, tiled=True)]
    dot_general x1, matrix products: 1.87 us -> 5.98 us  [expert_dense(): jnp.dot(hidden, down_mat, preferred_element_type=jnp.float32)]
    dot_general x1, matrix products: 1.82 us -> 5.53 us  [expert_dense(): lax.dot_general(grad_in, down_mat, against, preferred_element_type=jnp.fl...]
  transfers between devices with their start and end apart: 2 -> 4, of which waited for: 2 -> 4; matrix products, arithmetic and copies ran while one was open for 0% -> 8% of each run, Pallas kernels for 0% -> 0%
where the time goes in v3:
time: 250 us
  waiting for transfers between devices  193 us (77%)
  matrix products  27.4 us (11%)
  between operations  13.9 us (6%)
  other arithmetic  9.03 us (4%)
  local copies, waits for them, and re-layouts  6.07 us (2%)
    reduce_scatter x1, waiting for transfers between devices, per_device_dense(): lax.psum_scatter(weighted_out, 'expert', scatter_dimension=0, tiled=True)  61.6 us
    reduce_scatter x1, waiting for transfers between devices, per_device_dense(): lax.psum_scatter(weighted_grad, 'expert', scatter_dimension=0, tiled=True)  53.9 us
    all_gather x1, waiting for transfers between devices, per_device_dense(): lax.all_gather(grad_sum.astype(jnp.bfloat16), 'expert', axis=0, tiled=True)  40.5 us
    all_gather x1, waiting for transfers between devices, per_device_dense(): gathered = lax.all_gather(payload, 'expert', axis=0, tiled=True)  37.3 us
    dot_general x1, matrix products, expert_dense(): jnp.dot(hidden, down_mat, preferred_element_type=jnp.float32)  5.98 us
    dot_general x1, matrix products, expert_dense(): lax.dot_general(grad_in, down_mat, against, preferred_element_type=jnp.fl...  5.53 us
  transfers between devices with their start and end apart: 4, of which 4 were waited for; matrix products, arithmetic and copies ran while one was open for 8% of the time, Pallas kernels for 0%

profile of v3, /device:TPU:0, one launch (start us, length us, event | category | flops | bytes accessed | tf_op | source)
XLA Modules:
  0.0 250.0 jit_solution(16576090353580581532)
XLA Ops:
  7.2 0.0 all-gather.5.cloned.1.call-start
  7.2 2.2 fusion.37
  9.4 0.0 all-gather.5.cloned.1.call-update
  9.4 0.0 all-gather.3.cloned.1.call-start
  9.5 0.7 select_reduce_fusion
  10.2 0.1 copy.15
  10.3 0.8 convert_reduce_fusion
  11.1 2.0 fusion.38
  13.0 0.7 fusion.29
  13.7 0.0 all-gather.3.cloned.1.call-update
  13.7 0.0 reduce-scatter.5.cloned.1.call-start
  13.8 40.5 %all-gather.5.cloned.1.call-done = bf16[512,2048]{1,0:T(8,128)(2,1)} async-done(((bf16[32,2048]{1,0:T(8,128)(2,1)}), bf16[512,2048]{1,0:T(8,128)(2,1)}) %all-gather.5.cloned.1.call-update) | async-done | bytes 2097168 | tf_op jit(solution)/shard_map/all_gather | solution.py:139
  54.3 5.5 %fusion = f32[512,768]{1,0:T(8,128)} fusion(bf16[512,2048]{1,0:T(8,128)(2,1)} %all-gather.5.cloned.1.call-done, bf16[1,768,2048]{2,1,0:T(8,128)(2,1)} %param.17), kind=kOutput, calls=%fused_computation.5 | convolution fusion | flops 1610612736 | bytes 6815744 | tf_op jit(solution)/shard_map/dot_general | solution.py:103
  59.8 37.3 %all-gather.3.cloned.1.call-done = bf16[512,2176]{1,0:T(8,128)(2,1)} async-done(((bf16[32,2176]{1,0:T(8,128)(2,1)}), bf16[512,2176]{1,0:T(8,128)(2,1)}) %all-gather.3.cloned.1.call-update) | async-done | bytes 2228240 | tf_op jit(solution)/shard_map/all_gather | solution.py:138
  97.2 0.9 slice_convert_fusion
  98.1 0.2 fusion.28
  98.4 4.4 %fusion.10 = f32[512,768]{1,0:T(8,128)S(1)} fusion(bf16[1,2048,768]{2,1,0:T(8,128)(2,1)} %param.15, bf16[512,2176]{1,0:T(8,128)(2,1)} %all-gather.3.cloned.1.call-done), kind=kOutput, calls=%fused_computation.15 | convolution fusion | flops 1610612736 | bytes 6815744 | tf_op jit(solution)/shard_map/dot_general | solution.py:98
  102.8 1.9 fusion.4
  104.7 0.3 copy-done.1
  105.0 1.8 fusion.6
  106.8 1.2 copy-done.5
  108.0 3.7 %multiply_convert_fusion = bf16[512,2048]{1,0:T(8,128)(2,1)} fusion(f32[512,2048]{1,0:T(8,128)S(1)} %fusion.4, bf16[1,2048,768]{2,1,0:T(8,128)(2,1)S(1)} %copy-done.3, f32[512]{0:T(512)S(1)} %fusion.28, f32[512,768]{1,0:T(8,128)S(1)} %fusion.10, f32[512,768]{1,0:T(8,128)S(1)} %copy-done.6, f32[512,768]{1,0:T(8,128)S(1)} %fusion.6), kind=kOutput, calls=%fused_computation.2 | convolution fusion | flops 1619787776 | bytes 14157824 | tf_op jit(solution)/shard_map/dot_general | solution.py:108
  111.7 0.0 reduce-scatter.3.cloned.1.call-start
  111.7 6.0 %multiply_convert_fusion.1 = bf16[512,2048]{1,0:T(8,128)(2,1)} fusion(bf16[1,768,2048]{2,1,0:T(8,128)(2,1)} %param.17, f32[512]{0:T(512)S(1)} %fusion.28, f32[512,768]{1,0:T(8,128)} %copy-done.5, f32[512,768]{1,0:T(8,128)} %copy-done.4), kind=kOutput, calls=%fused_computation.4 | convolution fusion | flops 1617166336 | bytes 8390656 | tf_op jit(solution)/shard_map/dot_general | solution.py:102
  117.7 0.6 copy-done.2
  118.4 53.9 %reduce-scatter.5.cloned.1.call-done = bf16[32,2048]{1,0:T(8,128)(2,1)} async-done(((bf16[512,2048]{1,0:T(8,128)(2,1)}), bf16[32,2048]{1,0:T(8,128)(2,1)}) %reduce-scatter.5.cloned.1.call-update) | async-done | bytes 131088 | tf_op jit(solution)/shard_map/reduce_scatter | solution.py:150
  172.3 1.1 subtract_divide_fusion
  173.4 1.9 gather_fusion.1
  175.3 61.6 %reduce-scatter.3.cloned.1.call-done = bf16[32,2048]{1,0:T(8,128)(2,1)} async-done(((bf16[512,2048]{1,0:T(8,128)(2,1)}), bf16[32,2048]{1,0:T(8,128)(2,1)}) %reduce-scatter.3.cloned.1.call-update) | async-done | bytes 131088 | tf_op jit(solution)/shard_map/reduce_scatter | solution.py:149
  236.9 1.0 convert_subtract_fusion
  237.9 1.9 gather_fusion
  239.9 3.6 %select_add_fusion = (f32[128,2048]{1,0:T(8,128)}, f32[128,2048]{1,0:T(8,128)}) fusion(f32[128,2048]{1,0:T(8,128)} %gather_fusion.1, bf16[128,2048]{1,0:T(8,128)(2,1)} %param.11, pred[128]{0:T(512)(128)(4,1)S(1)} %compare_and_fusion, f32[128,2048]{1,0:T(8,128)} %gather_fusion, bf16[128,2048]{1,0:T(8,128)(2,1)} %param.10), kind=kLoop, calls=%fused_computation.25 | loop fusion | flops 1572864 | bytes 5243008 | tf_op jit(solution)/shard_map/add | solution.py:154
  (19 shorter events, 0.1 us)
Async XLA Ops:
  7.2 95.6 %copy-start = (bf16[1,2048,768]{2,1,0:T(8,128)(2,1)S(1)}, bf16[1,2048,768]{2,1,0:T(8,128)(2,1)}, u32[]{:S(2)}) copy-start(bf16[1,2048,768]{2,1,0:T(8,128)(2,1)} %param.16) | copy-start | bytes 9437188
  7.2 47.1 %all-gather.5.cloned.1.call-start = ((), (), s32[]{:S(2)}) async-start(), calls=%async_computation.4 | async-start | bytes 2228224 | tf_op jit(solution)/shard_map/all_gather | solution.py:139
  9.4 87.8 %all-gather.3.cloned.1.call-start = ((), (), s32[]{:S(2)}) async-start(), calls=%async_computation.2 | async-start | bytes 2367488 | tf_op jit(solution)/shard_map/all_gather | solution.py:138
  13.7 158.6 %reduce-scatter.5.cloned.1.call-start = ((), (), s32[]{:S(2)}) async-start(), calls=%async_computation.5 | async-start | bytes 2228224 | tf_op jit(solution)/shard_map/reduce_scatter | solution.py:150
  98.3 4.5 %copy-start.6 = (f32[512,768]{1,0:T(8,128)S(1)}, f32[512,768]{1,0:T(8,128)}, u32[]{:S(2)}) copy-start(f32[512,768]{1,0:T(8,128)} %fusion) | copy-start | bytes 4718596
  102.8 4.0 %copy-start.4 = (f32[512,768]{1,0:T(8,128)}, f32[512,768]{1,0:T(8,128)S(1)}, u32[]{:S(2)}) copy-start(f32[512,768]{1,0:T(8,128)S(1)} %fusion.10) | copy-start | bytes 4718596
  102.8 2.2 copy-start.1
  105.0 3.0 %copy-start.3 = (bf16[1,2048,768]{2,1,0:T(8,128)(2,1)S(1)}, bf16[1,2048,768]{2,1,0:T(8,128)(2,1)}, u32[]{:S(2)}) copy-start(bf16[1,2048,768]{2,1,0:T(8,128)(2,1)} %param.15) | copy-start | bytes 9437188
  106.8 1.2 copy-start.5
  111.7 125.2 %reduce-scatter.3.cloned.1.call-start = ((), (), s32[]{:S(2)}) async-start(), calls=%async_computation.3 | async-start | bytes 2228224 | tf_op jit(solution)/shard_map/reduce_scatter | solution.py:149
  117.7 0.7 copy-start.2
Sparse Core Ops, SparseCore 0:
  10.2 44.0 all-gather.4
  56.6 40.5 all-gather.2
  111.8 60.4 reduce-scatter.4
  176.4 60.5 reduce-scatter.2

commit v4 on v2

--- a/solution.py
+++ b/solution.py
@@ -93,6 +93,88 @@
     return (layer_out, token_grad)
 
 
+def pick(index, options):
+    chosen = options[-1]
+    for position in range(len(options) - 2, -1, -1):
+        chosen = jnp.where(index == position, options[position], chosen)
+    return chosen
+
+
+def line_gather(shard, stride, lines, experts):
+    me = lax.axis_index("expert")
+    line = me // stride
+    here = [(shard, line)]
+    ahead, behind = shard, shard
+    for step in range(1, lines):
+        ahead = lax.ppermute(
+            ahead,
+            "expert",
+            [(j, j + stride) for j in range(experts) if step - 1 <= j // stride < lines - 1],
+        )
+        behind = lax.ppermute(
+            behind,
+            "expert",
+            [(j, j - stride) for j in range(experts) if 1 <= j // stride <= lines - step],
+        )
+        here.append((ahead, line - step))
+        here.append((behind, line + step))
+    slot = lax.broadcasted_iota(jnp.int32, (lines,) + (1,) * shard.ndim, 0)
+    stacked = jnp.zeros((lines,) + shard.shape, shard.dtype)
+    for piece, origin in here:
+        stacked = jnp.where(slot == origin, piece[None], stacked)
+    return stacked
+
+
+def topo_all_gather(shard, experts):
+    lines = experts // 4
+    me = lax.axis_index("expert")
+    column = line_gather(shard, 4, lines, experts)
+    across = lax.ppermute(column, "expert", [(j, j ^ 2) for j in range(experts)])
+    in_row = (me // 2) % 2
+    plane = jnp.stack([pick(in_row, [column, across]), pick(in_row, [across, column])], axis=1)
+    partner = lax.ppermute(plane, "expert", [(j, j ^ 1) for j in range(experts)])
+    on_chip = me % 2
+    full = jnp.stack([pick(on_chip, [plane, partner]), pick(on_chip, [partner, plane])], axis=2)
+    return full.reshape((experts * shard.shape[0],) + shard.shape[1:])
+
+
+def topo_reduce_scatter(blocks, experts):
+    lines = experts // 4
+    me = lax.axis_index("expert")
+    rows = blocks.shape[0] // experts
+    cube = blocks.reshape((lines, 2, 2, rows) + blocks.shape[1:])
+    on_chip = me % 2
+    keep = pick(on_chip, [cube[:, :, 0], cube[:, :, 1]])
+    give = pick(on_chip, [cube[:, :, 1], cube[:, :, 0]])
+    got = lax.ppermute(give.astype(jnp.bfloat16), "expert", [(j, j ^ 1) for j in range(experts)])
+    plane = keep.astype(jnp.float32) + got.astype(jnp.float32)
+    in_row = (me // 2) % 2
+    keep = pick(in_row, [plane[:, 0], plane[:, 1]])
+    give = pick(in_row, [plane[:, 1], plane[:, 0]])
+    got = lax.ppermute(give.astype(jnp.bfloat16), "expert", [(j, j ^ 2) for j in range(experts)])
+    column = keep + got.astype(jnp.float32)
+    line = me // 4
+    total = lax.dynamic_index_in_dim(column, line, 0, keepdims=False)
+    ahead = jnp.zeros_like(total)
+    behind = jnp.zeros_like(total)
+    for step in range(1, lines):
+        target = jnp.clip(line + lines - step, 0, lines - 1)
+        ahead = ahead + lax.dynamic_index_in_dim(column, target, 0, keepdims=False)
+        ahead = lax.ppermute(
+            ahead.astype(jnp.bfloat16),
+            "expert",
+            [(j, j + 4) for j in range(experts) if j // 4 <= step - 1],
+        ).astype(jnp.float32)
+        target = jnp.clip(line - lines + step, 0, lines - 1)
+        behind = behind + lax.dynamic_index_in_dim(column, target, 0, keepdims=False)
+        behind = lax.ppermute(
+            behind.astype(jnp.bfloat16),
+            "expert",
+            [(j, j - 4) for j in range(experts) if j // 4 >= lines - step],
+        ).astype(jnp.float32)
+    return total + ahead + behind
+
+
 def expert_dense(cent_in, grad_in, gate_mat, up_mat, down_mat):
     against = (((1,), (1,)), ((), ()))
     gate_act = jnp.dot(cent_in, gate_mat, preferred_element_type=jnp.float32)
@@ -137,7 +219,7 @@
     payload = jnp.concatenate(
         [centroid.astype(jnp.bfloat16), grad_sum.astype(jnp.bfloat16), side], axis=1
     )
-    gathered = lax.all_gather(payload, "expert", axis=0, tiled=True)
+    gathered = topo_all_gather(payload, experts)
     cent_all = gathered[:, :model_width]
     grad_all = gathered[:, model_width : 2 * model_width]
     side_all = gathered[:, 2 * model_width : 2 * model_width + 2 * experts].astype(jnp.float32)
@@ -146,15 +228,16 @@
     output, input_grad = expert_dense(
         cent_all, grad_all, gate_weight[0], up_weight[0], down_weight[0]
     )
-    parts = jnp.stack(
+    parts = jnp.concatenate(
         [
             (mine[:, None] * output.astype(jnp.float32)).astype(jnp.bfloat16),
             (mine[:, None] * input_grad.astype(jnp.float32)).astype(jnp.bfloat16),
-        ]
-    )
-    summed = lax.psum_scatter(parts, "expert", scatter_dimension=1, tiled=True)
-    combined = summed[0].astype(jnp.float32)
-    centroid_grad = summed[1].astype(jnp.float32) - grad_sum
+        ],
+        axis=1,
+    )
+    summed = topo_reduce_scatter(parts, experts)
+    combined = summed[:, :model_width]
+    centroid_grad = summed[:, model_width:] - grad_sum
     layer_out = tokens.astype(jnp.float32) + jnp.take(combined - centroid, cluster_ids, axis=0)
     token_grad = out_grad.astype(jnp.float32) + jnp.take(
         centroid_grad / counts[:, None], cluster_ids, axis=0
@@ -167,7 +250,7 @@
     cent_rows, fanout = routes.shape
     experts = lax.axis_size("expert")
     capacity = min(cent_rows, 2 * cent_rows * fanout // experts)
-    if capacity == cent_rows:
+    if capacity == cent_rows and experts % 4 == 0:
         return per_device_dense(*args)
     return per_device_slots(*args)
 

time: 175 us -> 178 us (1.017)
  waiting for transfers between devices: 125 us -> 87.4 us
  starting transfers between devices: 0.08 us -> 35 us
  between operations: 14.2 us -> 1.04 us
  other arithmetic: 11.4 us -> 22.7 us
  local copies, waits for them, and re-layouts: 5.99 us -> 10.5 us
  matrix products: 18 us -> 20.3 us
    ppermute x0 -> x16, waiting for transfers between devices: none -> 87.4 us  [the longest x1 24.7 us: topo_reduce_scatter(): lax.ppermute(give.astype(jnp.bfloat16), 'expert', [(j, j ^ 2) for j in ra...]
    reduce_scatter x1 -> x0, waiting for transfers between devices: 70.5 us -> none  [per_device_dense(): summed = lax.psum_scatter(parts, 'expert', scatter_dimension=1, tiled=True)]
    all_gather x1 -> x0, waiting for transfers between devices: 54 us -> none  [per_device_dense(): gathered = lax.all_gather(payload, 'expert', axis=0, tiled=True)]
    ppermute x0 -> x16, starting transfers between devices: none -> 35 us  [the longest x3 16.8 us: topo_reduce_scatter(): lax.ppermute(ahead.astype(jnp.bfloat16), 'expert', [(j, j + 4) for j in r...]
    unnamed x13 -> x30, local copies, waits for them, and re-layouts: 0.75 us -> 5.66 us
    another operation x1 -> x4, other arithmetic: 2.35 us -> 7.04 us  [the longest x2 3.96 us: topo_all_gather(): jnp.stack([pick(in_row, [column, across]), pick(in_row, [across, column])...]
    add x0 -> x3, other arithmetic: none -> 4.58 us  [the longest x1 2.56 us: topo_reduce_scatter(): column = keep + got.astype(jnp.float32)]
    select_n x0 -> x2, other arithmetic: none -> 3.03 us  [the longest x1 2.76 us: line_gather(): stacked = jnp.where(slot == origin, piece[None], stacked)]
  transfers between devices with their start and end apart: 2 -> 16, of which waited for: 2 -> 11; matrix products, arithmetic and copies ran while one was open for 0% -> 0% of each run, Pallas kernels for 0% -> 0%
where the time goes in v4:
time: 178 us; the launch traced here: 177 us
  waiting for transfers between devices  87.4 us (49%)
  starting transfers between devices  35 us (20%)
  other arithmetic  22.7 us (13%)
  matrix products  20.3 us (11%)
  local copies, waits for them, and re-layouts  10.5 us (6%)
    ppermute x1, waiting for transfers between devices, topo_reduce_scatter(): lax.ppermute(give.astype(jnp.bfloat16), 'expert', [(j, j ^ 2) for j in ra...  24.7 us
    ppermute x1, waiting for transfers between devices, topo_all_gather(): lax.ppermute(column, 'expert', [(j, j ^ 2) for j in range(experts)])  22.4 us
    ppermute x3, waiting for transfers between devices, line_gather(): lax.ppermute(behind, 'expert', [(j, j - stride) for j in range(experts) i...  17.4 us
    ppermute x3, starting transfers between devices, topo_reduce_scatter(): lax.ppermute(ahead.astype(jnp.bfloat16), 'expert', [(j, j + 4) for j in r...  16.8 us
    ppermute x3, waiting for transfers between devices, topo_reduce_scatter(): lax.ppermute(ahead.astype(jnp.bfloat16), 'expert', [(j, j + 4) for j in r...  10.1 us
    ppermute x3, starting transfers between devices, line_gather(): lax.ppermute(ahead, 'expert', [(j, j + stride) for j in range(experts) if...  9.04 us
    unnamed x30, local copies, waits for them, and re-layouts  5.66 us
    ppermute x1, waiting for transfers between devices, topo_all_gather(): lax.ppermute(plane, 'expert', [(j, j ^ 1) for j in range(experts)])  4.59 us
  transfers between devices with their start and end apart: 16, of which 11 were waited for; matrix products, arithmetic and copies ran while one was open for 0% of the time, Pallas kernels for 0%

profile of v4, /device:TPU:0, one launch (start us, length us, event | category | flops | bytes accessed | tf_op | source)
XLA Modules:
  0.0 177.0 jit_solution(20669086246101070)
XLA Ops:
  2.4 2.0 %fusion.48 = (bf16[32,2048]{1,0:T(8,128)(2,1)S(1)}, f32[32,2048]{1,0:T(8,128)}) fusion(bf16[128,2048]{1,0:T(8,128)(2,1)} %param.11, s32[128]{0:T(128)} %param.12), kind=kOutput, calls=%fused_computation.92 | convolution fusion | flops 16846848 | bytes 918016 | tf_op jit(solution)/shard_map/dot_general | solution.py:209
  4.4 2.0 %fusion.49 = (bf16[32,2048]{1,0:T(8,128)(2,1)S(1)}, f32[32,2048]{1,0:T(8,128)}) fusion(f32[32]{0:T(128)S(1)} %convert_reduce_fusion, bf16[128,2048]{1,0:T(8,128)(2,1)} %param.10, s32[128]{0:T(128)} %param.12), kind=kOutput, calls=%fused_computation.93 | convolution fusion | flops 16912384 | bytes 918144 | tf_op jit(solution)/shard_map/dot_general | solution.py:206
  7.7 6.3 %collective-permute-start.3 = (bf16[32,4224]{1,0:T(8,128)(2,1)S(1)}, bf16[32,4224]{1,0:T(8,128)(2,1)}, u32[]{:S(2)}, u32[]{:S(2)}) collective-permute-start(bf16[32,4224]{1,0:T(8,128)(2,1)S(1)} %fusion.34), channel_id=1, source_target_pairs={{0,4},{1,5},{2,6},{3,7},{4,8},{5,9},{6,10},{7,11},{8,12},{9,13},{1... | collective-permute-start | bytes 811016 | tf_op jit(solution)/shard_map/ppermute | solution.py:109
  14.0 3.9 %collective-permute-done = bf16[32,4224]{1,0:T(8,128)(2,1)} collective-permute-done((bf16[32,4224]{1,0:T(8,128)(2,1)S(1)}, bf16[32,4224]{1,0:T(8,128)(2,1)}, u32[]{:S(2)}, u32[]{:S(2)}) %collective-permute-start) | collective-permute-done | bytes 270368 | tf_op jit(solution)/shard_map/ppermute | solution.py:114
  20.6 7.2 %collective-permute-done.1 = bf16[32,4224]{1,0:T(8,128)(2,1)} collective-permute-done((bf16[32,4224]{1,0:T(8,128)(2,1)}, bf16[32,4224]{1,0:T(8,128)(2,1)}, u32[]{:S(2)}, u32[]{:S(2)}) %collective-permute-start.1) | collective-permute-done | bytes 270368 | tf_op jit(solution)/shard_map/ppermute | solution.py:114
  30.5 6.2 %collective-permute-done.2 = bf16[32,4224]{1,0:T(8,128)(2,1)} collective-permute-done((bf16[32,4224]{1,0:T(8,128)(2,1)}, bf16[32,4224]{1,0:T(8,128)(2,1)}, u32[]{:S(2)}, u32[]{:S(2)}) %collective-permute-start.2) | collective-permute-done | bytes 270368 | tf_op jit(solution)/shard_map/ppermute | solution.py:114
  36.7 2.8 %select_select_fusion = bf16[4,32,4224]{2,1,0:T(8,128)(2,1)} fusion(pred[4]{0:T(512)(128)(4,1)S(1)} %get-tuple-element.25, pred[4]{0:T(512)(128)(4,1)S(1)} %get-tuple-element.26, pred[4]{0:T(512)(128)(4,1)S(1)} %get-tuple-element.27, pred[4]{0:T(512)(128)(4,1)S(1)} %get-tuple-element.28, pred[4]{0:T(512)(128)(4,1)S(1)} %get-tuple-element.29, ...), kind=kLoop, calls=%fused_computation.37 | loop fusion | flops 3784704 | bytes 2973724 | tf_op jit(solution)/shard_map/jit(_where)/select_n | solution.py:124
  40.5 22.4 %collective-permute-done.6 = bf16[4,32,4224]{2,1,0:T(8,128)(2,1)} collective-permute-done((bf16[4,32,4224]{2,1,0:T(8,128)(2,1)}, bf16[4,32,4224]{2,1,0:T(8,128)(2,1)}, u32[]{:S(2)}, u32[]{:S(2)}) %collective-permute-start.6) | collective-permute-done | bytes 1081376 | tf_op jit(solution)/shard_map/ppermute | solution.py:132
  63.0 2.2 %select_bitcast_fusion.4 = (bf16[4,1,32,4224]{3,2,0,1:T(8,128)(2,1)S(1)}, bf16[4,1,32,4224]{3,2,0,1:T(8,128)(2,1)S(1)}) fusion(bf16[4,32,4224]{2,1,0:T(8,128)(2,1)} %collective-permute-done.6, pred[]{:T(512)S(6)} %eq.131, bf16[32,4224]{1,0:T(8,128)(2,1)S(1)} %fusion.34, pred[4]{0:T(512)(128)(4,1)S(1)} %get-tuple-element.25, ...), kind=kLoop, calls=%fused_computation.36 | loop fusion | flops 4866048 | bytes 5136413 | tf_op jit(solution)/shard_map/stack | solution.py:134
  67.3 4.6 %collective-permute-done.7 = bf16[4,2,32,4224]{3,2,0,1:T(8,128)(2,1)} collective-permute-done((bf16[4,2,32,4224]{3,2,0,1:T(8,128)(2,1)}, bf16[4,2,32,4224]{3,2,0,1:T(8,128)(2,1)}, u32[]{:S(2)}, u32[]{:S(2)}) %collective-permute-start.7) | collective-permute-done | bytes 2162720 | tf_op jit(solution)/shard_map/ppermute | solution.py:135
  71.9 2.6 %select_bitcast_fusion.1 = (bf16[4,2,1,32,4224]{4,3,0,1,2:T(8,128)(2,1)S(1)}, bf16[4,2,1,32,4224]{4,3,0,1,2:T(8,128)(2,1)S(1)}) fusion(bf16[4,2,32,4224]{3,2,0,1:T(8,128)(2,1)} %collective-permute-done.7, pred[]{:T(512)S(6)} %eq.132, bf16[4,1,32,4224]{3,2,0,1:T(8,128)(2,1)} %copy-done.4, bf16[4,1,32,4224]{3,2,0,1:T(8,128)(2,1)} %copy-done.3), kind=kLoop, calls=%fused_computation.24 | loop fusion | flops 3244032 | bytes 8650753 | tf_op jit(solution)/shard_map/stack | solution.py:137
  75.4 2.6 %copy-done.10 = bf16[1,2048,768]{2,1,0:T(8,128)(2,1)S(1)} copy-done((bf16[1,2048,768]{2,1,0:T(8,128)(2,1)S(1)}, bf16[1,2048,768]{2,1,0:T(8,128)(2,1)}, u32[]{:S(2)}) %copy-start.10) | copy-done | bytes 3145752
  78.1 3.0 %fusion.10 = f32[512,768]{1,0:T(8,128)} fusion(bf16[1,2048,768]{2,1,0:T(8,128)(2,1)S(1)} %copy-done.10, bf16[512,4224]{1,0:T(8,128)(2,1)S(1)} %bitcast.70), kind=kOutput, calls=%fused_computation.18 | convolution fusion | flops 1610612736 | bytes 6815744 | tf_op jit(solution)/shard_map/dot_general | solution.py:180
  81.0 3.0 %fusion.6 = f32[512,768]{1,0:T(8,128)} fusion(bf16[1,2048,768]{2,1,0:T(8,128)(2,1)S(1)} %copy-done, bf16[512,4224]{1,0:T(8,128)(2,1)S(1)} %bitcast.71), kind=kOutput, calls=%fused_computation.14 | convolution fusion | flops 1610612736 | bytes 6815744 | tf_op jit(solution)/shard_map/dot_general | solution.py:181
  84.1 4.5 %fusion = f32[512,768]{1,0:T(8,128)S(1)} fusion(bf16[1,768,2048]{2,1,0:T(8,128)(2,1)} %param.17, bf16[512,4224]{1,0:T(8,128)(2,1)} %bitcast.72), kind=kOutput, calls=%fused_computation.8 | convolution fusion | flops 1610612736 | bytes 6815744 | tf_op jit(solution)/shard_map/dot_general | solution.py:185
  88.7 1.8 %fusion.4 = f32[512,2048]{1,0:T(8,128)S(1)} fusion(bf16[1,2048,768]{2,1,0:T(8,128)(2,1)S(1)} %copy-done, f32[512,768]{1,0:T(8,128)S(1)} %fusion, f32[512,768]{1,0:T(8,128)S(1)} %copy-done.12), kind=kOutput, calls=%fused_computation.12 | convolution fusion | flops 1612972032 | bytes 10485760 | tf_op jit(solution)/shard_map/dot_general | solution.py:191
  91.0 1.8 %multiply_convert_fusion.1 = bf16[512,2048]{1,0:T(8,128)(2,1)S(1)} fusion(bf16[1,768,2048]{2,1,0:T(8,128)(2,1)S(1)} %copy-done.9, f32[512]{0:T(512)S(1)} %fusion.39, f32[512,768]{1,0:T(8,128)S(1)} %copy-done.13, f32[512,768]{1,0:T(8,128)S(1)} %copy-done.12), kind=kOutput, calls=%fused_computation.7 | convolution fusion | flops 1617166336 | bytes 8390656 | tf_op jit(solution)/shard_map/dot_general | solution.py:184
  92.9 2.3 %multiply_convert_fusion = bf16[512,2048]{1,0:T(8,128)(2,1)S(1)} fusion(f32[512,2048]{1,0:T(8,128)S(1)} %fusion.4, bf16[1,2048,768]{2,1,0:T(8,128)(2,1)S(1)} %copy-done.11, f32[512]{0:T(512)S(1)} %fusion.39, f32[512,768]{1,0:T(8,128)S(1)} %copy-done.12, f32[512,768]{1,0:T(8,128)S(1)} %fusion, f32[512,768]{1,0:T(8,128)S(1)} %copy-done.13), kind=kOutput, calls=%fused_computation.5 | convolution fusion | flops 1619787776 | bytes 14157824 | tf_op jit(solution)/shard_map/dot_general | solution.py:190
  96.9 4.0 %collective-permute-done.8 = bf16[4,2,32,4096]{3,2,0,1:T(8,128)(2,1)S(1)} collective-permute-done((bf16[4,2,32,4096]{3,2,0,1:T(8,128)(2,1)S(1)}, bf16[4,2,32,4096]{3,2,0,1:T(8,128)(2,1)S(1)}, u32[]{:S(2)}, u32[]{:S(2)}) %collective-permute-start.8) | collective-permute-done | bytes 2097184 | tf_op jit(solution)/shard_map/ppermute | solution.py:149
  102.0 2.0 %copy-done.2 = f32[4,2,32,4096]{3,2,0,1:T(8,128)} copy-done((f32[4,2,32,4096]{3,2,0,1:T(8,128)}, f32[4,2,32,4096]{3,2,0,1:T(8,128)S(1)}, u32[]{:S(2)}) %copy-start.2) | copy-done | bytes 4194328
  104.7 24.7 %collective-permute-done.9 = bf16[4,32,4096]{2,1,0:T(8,128)(2,1)S(1)} collective-permute-done((bf16[4,32,4096]{2,1,0:T(8,128)(2,1)S(1)}, bf16[4,32,4096]{2,1,0:T(8,128)(2,1)S(1)}, u32[]{:S(2)}, u32[]{:S(2)}) %collective-permute-start.9) | collective-permute-done | bytes 1048608 | tf_op jit(solution)/shard_map/ppermute | solution.py:154
  129.4 2.6 %bitcast_add_fusion = f32[4,32,4096]{2,1,0:T(8,128)S(1)} fusion(bf16[4,32,4096]{2,1,0:T(8,128)(2,1)S(1)} %collective-permute-done.9, f32[4,2,32,4096]{3,2,0,1:T(8,128)} %copy-done.2, pred[]{:T(512)S(6)} %eq.131), kind=kLoop, calls=%fused_computation.26 | loop fusion | flops 1572864 | bytes 7340033 | tf_op jit(solution)/shard_map/add | solution.py:155
  134.2 4.4 %collective-permute-done.10 = bf16[32,4096]{1,0:T(8,128)(2,1)S(1)} collective-permute-done((bf16[32,4096]{1,0:T(8,128)(2,1)S(1)}, bf16[32,4096]{1,0:T(8,128)(2,1)S(1)}, u32[]{:S(2)}, u32[]{:S(2)}) %collective-permute-start.10) | collective-permute-done | bytes 262176 | tf_op jit(solution)/shard_map/ppermute | solution.py:163
  138.8 4.5 %collective-permute-start.11 = (bf16[32,4096]{1,0:T(8,128)(2,1)S(1)}, bf16[32,4096]{1,0:T(8,128)(2,1)S(1)}, u32[]{:S(2)}, u32[]{:S(2)}) collective-permute-start(bf16[32,4096]{1,0:T(8,128)(2,1)S(1)} %get-tuple-element.13), channel_id=1, source_target_pairs={{0,4},{1,5},{2,6},{3,7},{4,8},{5,9},{6,10},{7,11},{16,20},{17,21},... | collective-permute-start | bytes 786440 | tf_op jit(solution)/shard_map/ppermute | solution.py:163
  144.7 2.8 %collective-permute-done.11 = bf16[32,4096]{1,0:T(8,128)(2,1)S(1)} collective-permute-done((bf16[32,4096]{1,0:T(8,128)(2,1)S(1)}, bf16[32,4096]{1,0:T(8,128)(2,1)S(1)}, u32[]{:S(2)}, u32[]{:S(2)}) %collective-permute-start.11) | collective-permute-done | bytes 262176 | tf_op jit(solution)/shard_map/ppermute | solution.py:163
  147.5 1.7 fusion.31
  149.2 10.8 %collective-permute-start.12 = (bf16[32,4096]{1,0:T(8,128)(2,1)}, bf16[32,4096]{1,0:T(8,128)(2,1)S(1)}, u32[]{:S(2)}, u32[]{:S(2)}) collective-permute-start(bf16[32,4096]{1,0:T(8,128)(2,1)} %get-tuple-element.11), channel_id=1, source_target_pairs={{0,4},{1,5},{2,6},{3,7},{4,8},{5,9},{6,10},{7,11},{8,12},{9,13},{1... | collective-permute-start | bytes 786440 | tf_op jit(solution)/shard_map/ppermute | solution.py:163
  161.4 2.8 %collective-permute-done.12 = bf16[32,4096]{1,0:T(8,128)(2,1)S(1)} collective-permute-done((bf16[32,4096]{1,0:T(8,128)(2,1)}, bf16[32,4096]{1,0:T(8,128)(2,1)S(1)}, u32[]{:S(2)}, u32[]{:S(2)}) %collective-permute-start.12) | collective-permute-done | bytes 262176 | tf_op jit(solution)/shard_map/ppermute | solution.py:163
  164.2 4.2 %collective-permute-done.15 = bf16[32,4096]{1,0:T(8,128)(2,1)} collective-permute-done((bf16[32,4096]{1,0:T(8,128)(2,1)S(1)}, bf16[32,4096]{1,0:T(8,128)(2,1)}, u32[]{:S(2)}, u32[]{:S(2)}) %collective-permute-start.15) | collective-permute-done | bytes 262176 | tf_op jit(solution)/shard_map/ppermute | solution.py:170
  169.5 1.9 %gather_fusion = f32[128,2048]{1,0:T(8,128)} fusion(f32[32,2048]{1,0:T(8,128)S(1)} %get-tuple-element.18, s32[1024]{0:T(1024)S(1)} %pad_clamp_fusion), kind=kCustom, calls=%fused_computation.clone | custom fusion | bytes 2097664 | tf_op jit(solution)/shard_map/jit(_take)/gather | solution.py:241
  171.5 1.9 %gather_fusion.1 = f32[128,2048]{1,0:T(8,128)} fusion(f32[32,2048]{1,0:T(8,128)S(1)} %get-tuple-element.17, s32[1024]{0:T(1024)S(1)} %pad_clamp_fusion), kind=kCustom, calls=%fused_computation.1.clone | custom fusion | bytes 2097664 | tf_op jit(solution)/shard_map/jit(_take)/gather | solution.py:242
  173.4 3.6 %select_add_fusion = (f32[128,2048]{1,0:T(8,128)}, f32[128,2048]{1,0:T(8,128)}) fusion(f32[128,2048]{1,0:T(8,128)} %gather_fusion.1, bf16[128,2048]{1,0:T(8,128)(2,1)} %param.11, pred[128]{0:T(512)(128)(4,1)S(1)} %compare_and_fusion, f32[128,2048]{1,0:T(8,128)} %gather_fusion, bf16[128,2048]{1,0:T(8,128)(2,1)} %param.10), kind=kLoop, calls=%fused_computation.39 | loop fusion | flops 1572864 | bytes 5243008 | tf_op jit(solution)/shard_map/add | solution.py:242
  (74 shorter events, 22.7 us)
Async XLA Ops:
  0.6 80.4 %copy-start = (bf16[1,2048,768]{2,1,0:T(8,128)(2,1)S(1)}, bf16[1,2048,768]{2,1,0:T(8,128)(2,1)}, u32[]{:S(2)}) copy-start(bf16[1,2048,768]{2,1,0:T(8,128)(2,1)} %param.16) | copy-start | bytes 9437188
  6.4 11.5 %collective-permute-start = (bf16[32,4224]{1,0:T(8,128)(2,1)S(1)}, bf16[32,4224]{1,0:T(8,128)(2,1)}, u32[]{:S(2)}, u32[]{:S(2)}) collective-permute-start(bf16[32,4224]{1,0:T(8,128)(2,1)S(1)} %fusion.34), channel_id=1, source_target_pairs={{4,0},{5,1},{6,2},{7,3},{8,4},{9,5},{10,6},{11,7},{12,8},{13,9},{1... | collective-permute-start | bytes 811016 | tf_op jit(solution)/shard_map/ppermute | solution.py:114
  7.7 11.5 %collective-permute-start.3 = (bf16[32,4224]{1,0:T(8,128)(2,1)S(1)}, bf16[32,4224]{1,0:T(8,128)(2,1)}, u32[]{:S(2)}, u32[]{:S(2)}) collective-permute-start(bf16[32,4224]{1,0:T(8,128)(2,1)S(1)} %fusion.34), channel_id=1, source_target_pairs={{0,4},{1,5},{2,6},{3,7},{4,8},{5,9},{6,10},{7,11},{8,12},{9,13},{1... | collective-permute-start | bytes 811016 | tf_op jit(solution)/shard_map/ppermute | solution.py:109
  17.9 9.9 %collective-permute-start.1 = (bf16[32,4224]{1,0:T(8,128)(2,1)}, bf16[32,4224]{1,0:T(8,128)(2,1)}, u32[]{:S(2)}, u32[]{:S(2)}) collective-permute-start(bf16[32,4224]{1,0:T(8,128)(2,1)} %collective-permute-done), channel_id=1, source_target_pairs={{4,0},{5,1},{6,2},{7,3},{8,4},{9,5},{10,6},{11,7},{20,16},{21,17},... | collective-permute-start | bytes 811016 | tf_op jit(solution)/shard_map/ppermute | solution.py:114
  19.2 9.9 %collective-permute-start.4 = (bf16[32,4224]{1,0:T(8,128)(2,1)}, bf16[32,4224]{1,0:T(8,128)(2,1)}, u32[]{:S(2)}, u32[]{:S(2)}) collective-permute-start(bf16[32,4224]{1,0:T(8,128)(2,1)} %collective-permute-done.3), channel_id=1, source_target_pairs={{4,8},{5,9},{6,10},{7,11},{8,12},{9,13},{10,14},{11,15},{20,24},{2... | collective-permute-start | bytes 811016 | tf_op jit(solution)/shard_map/ppermute | solution.py:109
  27.8 8.9 %collective-permute-start.2 = (bf16[32,4224]{1,0:T(8,128)(2,1)}, bf16[32,4224]{1,0:T(8,128)(2,1)}, u32[]{:S(2)}, u32[]{:S(2)}) collective-permute-start(bf16[32,4224]{1,0:T(8,128)(2,1)} %collective-permute-done.1), channel_id=1, source_target_pairs={{4,0},{5,1},{6,2},{7,3},{20,16},{21,17},{22,18},{23,19}} | collective-permute-start | bytes 811016 | tf_op jit(solution)/shard_map/ppermute | solution.py:114
  29.1 7.6 %collective-permute-start.5 = (bf16[32,4224]{1,0:T(8,128)(2,1)}, bf16[32,4224]{1,0:T(8,128)(2,1)}, u32[]{:S(2)}, u32[]{:S(2)}) collective-permute-start(bf16[32,4224]{1,0:T(8,128)(2,1)} %collective-permute-done.4), channel_id=1, source_target_pairs={{8,12},{9,13},{10,14},{11,15},{24,28},{25,29},{26,30},{27,31}} | collective-permute-start | bytes 811016 | tf_op jit(solution)/shard_map/ppermute | solution.py:109
  39.5 23.5 %collective-permute-start.6 = (bf16[4,32,4224]{2,1,0:T(8,128)(2,1)}, bf16[4,32,4224]{2,1,0:T(8,128)(2,1)}, u32[]{:S(2)}, u32[]{:S(2)}) collective-permute-start(bf16[4,32,4224]{2,1,0:T(8,128)(2,1)} %select_select_fusion), channel_id=1, source_target_pairs={{0,2},{1,3},{2,0},{3,1},{4,6},{5,7},{6,4},{7,5},{8,10},{9,11},{10,... | collective-permute-start | bytes 3244040 | tf_op jit(solution)/shard_map/ppermute | solution.py:132
  65.2 1.7 copy-start.3
  65.2 2.0 %copy-start.4 = (bf16[4,1,32,4224]{3,2,0,1:T(8,128)(2,1)}, bf16[4,1,32,4224]{3,2,0,1:T(8,128)(2,1)S(1)}, u32[]{:S(2)}) copy-start(bf16[4,1,32,4224]{3,2,0,1:T(8,128)(2,1)S(1)} %get-tuple-element.10) | copy-start | bytes 3244036
  67.3 4.6 %collective-permute-start.7 = (bf16[4,2,32,4224]{3,2,0,1:T(8,128)(2,1)}, bf16[4,2,32,4224]{3,2,0,1:T(8,128)(2,1)}, u32[]{:S(2)}, u32[]{:S(2)}) collective-permute-start(bf16[4,2,32,4224]{3,2,0,1:T(8,128)(2,1)} %pad_maximum_fusion.2), channel_id=1, source_target_pairs={{0,1},{1,0},{2,3},{3,2},{4,5},{5,4},{6,7},{7,6},{8,9},{9,8},{10,11... | collective-permute-start | bytes 6488072 | tf_op jit(solution)/shard_map/ppermute | solution.py:135
  75.0 3.1 %copy-start.10 = (bf16[1,2048,768]{2,1,0:T(8,128)(2,1)S(1)}, bf16[1,2048,768]{2,1,0:T(8,128)(2,1)}, u32[]{:S(2)}) copy-start(bf16[1,2048,768]{2,1,0:T(8,128)(2,1)} %param.15) | copy-start | bytes 9437188
  75.4 5.6 %copy-start.5 = (bf16[4,2,2,32,4224]{4,3,2,1,0:T(8,128)(2,1)}, bf16[4,2,2,32,4224]{4,3,2,1,0:T(8,128)(2,1)S(1)}, u32[]{:S(2)}) copy-start(bf16[4,2,2,32,4224]{4,3,2,1,0:T(8,128)(2,1)S(1)} %copy.46) | copy-start | bytes 12976132
  84.1 4.6 %copy-start.12 = (f32[512,768]{1,0:T(8,128)S(1)}, f32[512,768]{1,0:T(8,128)}, u32[]{:S(2)}) copy-start(f32[512,768]{1,0:T(8,128)} %fusion.10) | copy-start | bytes 4718596
  88.7 1.9 %copy-start.9 = (bf16[1,768,2048]{2,1,0:T(8,128)(2,1)S(1)}, bf16[1,768,2048]{2,1,0:T(8,128)(2,1)}, u32[]{:S(2)}) copy-start(bf16[1,768,2048]{2,1,0:T(8,128)(2,1)} %param.17) | copy-start | bytes 9437188
  88.7 2.3 %copy-start.13 = (f32[512,768]{1,0:T(8,128)S(1)}, f32[512,768]{1,0:T(8,128)}, u32[]{:S(2)}) copy-start(f32[512,768]{1,0:T(8,128)} %fusion.6) | copy-start | bytes 4718596
  91.0 1.9 %copy-start.11 = (bf16[1,2048,768]{2,1,0:T(8,128)(2,1)S(1)}, bf16[1,2048,768]{2,1,0:T(8,128)(2,1)}, u32[]{:S(2)}) copy-start(bf16[1,2048,768]{2,1,0:T(8,128)(2,1)} %param.15) | copy-start | bytes 9437188
  96.5 4.4 %collective-permute-start.8 = (bf16[4,2,32,4096]{3,2,0,1:T(8,128)(2,1)S(1)}, bf16[4,2,32,4096]{3,2,0,1:T(8,128)(2,1)S(1)}, u32[]{:S(2)}, u32[]{:S(2)}) collective-permute-start(bf16[4,2,32,4096]{3,2,0,1:T(8,128)(2,1)S(1)} %select_bitcast_fusion.2), channel_id=1, source_target_pairs={{0,1},{1,0},{2,3},{3,2},{4,5},{5,4},{6,7},{7,6},{8,9},{9,8},{10,11... | collective-permute-start | bytes 6291464 | tf_op jit(solution)/shard_map/ppermute | solution.py:149
  102.0 2.0 %copy-start.2 = (f32[4,2,32,4096]{3,2,0,1:T(8,128)}, f32[4,2,32,4096]{3,2,0,1:T(8,128)S(1)}, u32[]{:S(2)}) copy-start(f32[4,2,32,4096]{3,2,0,1:T(8,128)S(1)} %convert_add_fusion) | copy-start | bytes 12582916
  104.1 25.3 %collective-permute-start.9 = (bf16[4,32,4096]{2,1,0:T(8,128)(2,1)S(1)}, bf16[4,32,4096]{2,1,0:T(8,128)(2,1)S(1)}, u32[]{:S(2)}, u32[]{:S(2)}) collective-permute-start(bf16[4,32,4096]{2,1,0:T(8,128)(2,1)S(1)} %fusion.24), channel_id=1, source_target_pairs={{0,2},{1,3},{2,0},{3,1},{4,6},{5,7},{6,4},{7,5},{8,10},{9,11},{10,... | collective-permute-start | bytes 3145736 | tf_op jit(solution)/shard_map/ppermute | solution.py:154
  131.9 12.7 %copy-start.8 = (s32[128]{0:T(128)S(1)}, s32[128]{0:T(128)}, u32[]{:S(2)}) copy-start(s32[128]{0:T(128)} %param.12) | copy-start | bytes 1540
  132.0 6.6 %collective-permute-start.10 = (bf16[32,4096]{1,0:T(8,128)(2,1)S(1)}, bf16[32,4096]{1,0:T(8,128)(2,1)S(1)}, u32[]{:S(2)}, u32[]{:S(2)}) collective-permute-start(bf16[32,4096]{1,0:T(8,128)(2,1)S(1)} %get-tuple-element.15), channel_id=1, source_target_pairs={{0,4},{1,5},{2,6},{3,7},{16,20},{17,21},{18,22},{19,23}} | collective-permute-start | bytes 786440 | tf_op jit(solution)/shard_map/ppermute | solution.py:163
  133.5 5.1 %collective-permute-start.13 = (bf16[32,4096]{1,0:T(8,128)(2,1)S(1)}, bf16[32,4096]{1,0:T(8,128)(2,1)S(1)}, u32[]{:S(2)}, u32[]{:S(2)}) collective-permute-start(bf16[32,4096]{1,0:T(8,128)(2,1)S(1)} %get-tuple-element.16), channel_id=1, source_target_pairs={{12,8},{13,9},{14,10},{15,11},{28,24},{29,25},{30,26},{31,27}} | collective-permute-start | bytes 786440 | tf_op jit(solution)/shard_map/ppermute | solution.py:170
  138.7 30.7 %copy-start.6 = (f32[32,2048]{1,0:T(8,128)S(1)}, f32[32,2048]{1,0:T(8,128)}, u32[]{:S(2)}) copy-start(f32[32,2048]{1,0:T(8,128)} %get-tuple-element.22) | copy-start | bytes 786436
  138.7 30.7 %copy-start.7 = (f32[32,2048]{1,0:T(8,128)S(1)}, f32[32,2048]{1,0:T(8,128)}, u32[]{:S(2)}) copy-start(f32[32,2048]{1,0:T(8,128)} %get-tuple-element.24) | copy-start | bytes 786436
  138.8 8.7 %collective-permute-start.11 = (bf16[32,4096]{1,0:T(8,128)(2,1)S(1)}, bf16[32,4096]{1,0:T(8,128)(2,1)S(1)}, u32[]{:S(2)}, u32[]{:S(2)}) collective-permute-start(bf16[32,4096]{1,0:T(8,128)(2,1)S(1)} %get-tuple-element.13), channel_id=1, source_target_pairs={{0,4},{1,5},{2,6},{3,7},{4,8},{5,9},{6,10},{7,11},{16,20},{17,21},... | collective-permute-start | bytes 786440 | tf_op jit(solution)/shard_map/ppermute | solution.py:163
  143.3 4.2 %collective-permute-start.14 = (bf16[32,4096]{1,0:T(8,128)(2,1)S(1)}, bf16[32,4096]{1,0:T(8,128)(2,1)}, u32[]{:S(2)}, u32[]{:S(2)}) collective-permute-start(bf16[32,4096]{1,0:T(8,128)(2,1)S(1)} %get-tuple-element.14), channel_id=1, source_target_pairs={{8,4},{9,5},{10,6},{11,7},{12,8},{13,9},{14,10},{15,11},{24,20},{2... | collective-permute-start | bytes 786440 | tf_op jit(solution)/shard_map/ppermute | solution.py:170
  149.2 15.0 %collective-permute-start.12 = (bf16[32,4096]{1,0:T(8,128)(2,1)}, bf16[32,4096]{1,0:T(8,128)(2,1)S(1)}, u32[]{:S(2)}, u32[]{:S(2)}) collective-permute-start(bf16[32,4096]{1,0:T(8,128)(2,1)} %get-tuple-element.11), channel_id=1, source_target_pairs={{0,4},{1,5},{2,6},{3,7},{4,8},{5,9},{6,10},{7,11},{8,12},{9,13},{1... | collective-permute-start | bytes 786440 | tf_op jit(solution)/shard_map/ppermute | solution.py:163
  160.0 8.4 %collective-permute-start.15 = (bf16[32,4096]{1,0:T(8,128)(2,1)S(1)}, bf16[32,4096]{1,0:T(8,128)(2,1)}, u32[]{:S(2)}, u32[]{:S(2)}) collective-permute-start(bf16[32,4096]{1,0:T(8,128)(2,1)S(1)} %get-tuple-element.12), channel_id=1, source_target_pairs={{4,0},{5,1},{6,2},{7,3},{8,4},{9,5},{10,6},{11,7},{12,8},{13,9},{1... | collective-permute-start | bytes 786440 | tf_op jit(solution)/shard_map/ppermute | solution.py:170
  171.5 5.5 %copy-start.1 = (bf16[1,2048,768]{2,1,0:T(8,128)(2,1)S(1)}, bf16[1,2048,768]{2,1,0:T(8,128)(2,1)}, u32[]{:S(2)}) copy-start(bf16[1,2048,768]{2,1,0:T(8,128)(2,1)} %param.16) | copy-start | bytes 9437188

commit v5 on v4

--- a/solution.py
+++ b/solution.py
@@ -100,41 +100,51 @@
     return chosen
 
 
-def line_gather(shard, stride, lines, experts):
+def place(pieces, lines, like):
+    slot = lax.broadcasted_iota(jnp.int32, (lines,) + (1,) * like.ndim, 0)
+    stacked = jnp.zeros((lines,) + like.shape, like.dtype)
+    for piece, origin in pieces:
+        stacked = jnp.where(slot == origin, piece[None], stacked)
+    return stacked
+
+
+def topo_all_gather(shard, experts):
+    lines = experts // 4
     me = lax.axis_index("expert")
-    line = me // stride
+    line = me // 4
+    swap_row = [(j, j ^ 2) for j in range(experts)]
     here = [(shard, line)]
+    there = [(lax.ppermute(shard, "expert", swap_row), line)]
     ahead, behind = shard, shard
     for step in range(1, lines):
         ahead = lax.ppermute(
             ahead,
             "expert",
-            [(j, j + stride) for j in range(experts) if step - 1 <= j // stride < lines - 1],
+            [(j, j + 4) for j in range(experts) if step - 1 <= j // 4 < lines - 1],
         )
         behind = lax.ppermute(
             behind,
             "expert",
-            [(j, j - stride) for j in range(experts) if 1 <= j // stride <= lines - step],
+            [(j, j - 4) for j in range(experts) if 1 <= j // 4 <= lines - step],
         )
         here.append((ahead, line - step))
         here.append((behind, line + step))
-    slot = lax.broadcasted_iota(jnp.int32, (lines,) + (1,) * shard.ndim, 0)
-    stacked = jnp.zeros((lines,) + shard.shape, shard.dtype)
-    for piece, origin in here:
-        stacked = jnp.where(slot == origin, piece[None], stacked)
-    return stacked
-
-
-def topo_all_gather(shard, experts):
-    lines = experts // 4
-    me = lax.axis_index("expert")
-    column = line_gather(shard, 4, lines, experts)
-    across = lax.ppermute(column, "expert", [(j, j ^ 2) for j in range(experts)])
+        ahead_row = [(j, j ^ 2) for j in range(experts) if j // 4 >= step]
+        behind_row = [(j, j ^ 2) for j in range(experts) if j // 4 <= lines - 1 - step]
+        there.append((lax.ppermute(ahead, "expert", ahead_row), line - step))
+        there.append((lax.ppermute(behind, "expert", behind_row), line + step))
+    column = place(here, lines, shard)
+    across = place(there, lines, shard)
+    swap_core = [(j, j ^ 1) for j in range(experts)]
+    column_pair = lax.ppermute(column, "expert", swap_core)
+    across_pair = lax.ppermute(across, "expert", swap_core)
     in_row = (me // 2) % 2
-    plane = jnp.stack([pick(in_row, [column, across]), pick(in_row, [across, column])], axis=1)
-    partner = lax.ppermute(plane, "expert", [(j, j ^ 1) for j in range(experts)])
     on_chip = me % 2
-    full = jnp.stack([pick(on_chip, [plane, partner]), pick(on_chip, [partner, plane])], axis=2)
+    mine = jnp.stack([pick(in_row, [column, across]), pick(in_row, [across, column])], axis=1)
+    pair = jnp.stack(
+        [pick(in_row, [column_pair, across_pair]), pick(in_row, [across_pair, column_pair])], axis=1
+    )
+    full = jnp.stack([pick(on_chip, [mine, pair]), pick(on_chip, [pair, mine])], axis=2)
     return full.reshape((experts * shard.shape[0],) + shard.shape[1:])
 
 
@@ -151,28 +161,33 @@
     in_row = (me // 2) % 2
     keep = pick(in_row, [plane[:, 0], plane[:, 1]])
     give = pick(in_row, [plane[:, 1], plane[:, 0]])
-    got = lax.ppermute(give.astype(jnp.bfloat16), "expert", [(j, j ^ 2) for j in range(experts)])
-    column = keep + got.astype(jnp.float32)
     line = me // 4
-    total = lax.dynamic_index_in_dim(column, line, 0, keepdims=False)
-    ahead = jnp.zeros_like(total)
-    behind = jnp.zeros_like(total)
+
+    def row_sum(target, senders):
+        mine = lax.dynamic_index_in_dim(keep, target, 0, keepdims=False)
+        theirs = lax.dynamic_index_in_dim(give, target, 0, keepdims=False)
+        pairs = [(j, j ^ 2) for j in range(experts) if senders(j // 4)]
+        got = lax.ppermute(theirs.astype(jnp.bfloat16), "expert", pairs)
+        return mine + got.astype(jnp.float32)
+
+    ahead = jnp.zeros(keep.shape[1:], jnp.float32)
+    behind = jnp.zeros(keep.shape[1:], jnp.float32)
     for step in range(1, lines):
         target = jnp.clip(line + lines - step, 0, lines - 1)
-        ahead = ahead + lax.dynamic_index_in_dim(column, target, 0, keepdims=False)
+        ahead = ahead + row_sum(target, lambda z, s=step: z <= s - 1)
         ahead = lax.ppermute(
             ahead.astype(jnp.bfloat16),
             "expert",
             [(j, j + 4) for j in range(experts) if j // 4 <= step - 1],
         ).astype(jnp.float32)
         target = jnp.clip(line - lines + step, 0, lines - 1)
-        behind = behind + lax.dynamic_index_in_dim(column, target, 0, keepdims=False)
+        behind = behind + row_sum(target, lambda z, s=step: z >= lines - s)
         behind = lax.ppermute(
             behind.astype(jnp.bfloat16),
             "expert",
             [(j, j - 4) for j in range(experts) if j // 4 >= lines - step],
         ).astype(jnp.float32)
-    return total + ahead + behind
+    return row_sum(line, lambda z: True) + ahead + behind
 
 
 def expert_dense(cent_in, grad_in, gate_mat, up_mat, down_mat):

time: 178 us -> 145 us (0.81)
  waiting for transfers between devices: 87.4 us -> 31.6 us
  starting transfers between devices: 35 us -> 60.1 us
    ppermute x9 -> x22, waiting for transfers between devices: 69.1 us -> 15.2 us  [the longest x3 8.96 us: topo_all_gather(): lax.ppermute(behind, 'expert', [(j, j - 4) for j in range(experts) if 1 <...]
    ppermute x9 -> x22, starting transfers between devices: 14.6 us -> 36.8 us  [the longest x7 11.1 us: row_sum(): got = lax.ppermute(theirs.astype(jnp.bfloat16), 'expert', pairs)]
    add x2 -> x1, other arithmetic: 3.58 us -> 0.11 us  [topo_reduce_scatter(): return row_sum(line, lambda z: True) + ahead + behind]
    ppermute x3, starting transfers between devices: 16.8 us -> 20.1 us  [topo_reduce_scatter(): lax.ppermute(ahead.astype(jnp.bfloat16), 'expert', [(j, j + 4) for j in r...]
    add x1, other arithmetic: 1 us -> 3.93 us  [topo_reduce_scatter(): plane = keep.astype(jnp.float32) + got.astype(jnp.float32)]
    another operation x2, other arithmetic: 3.08 us -> 0.63 us  [the longest x1 0.44 us: topo_all_gather(): jnp.stack([pick(on_chip, [mine, pair]), pick(on_chip, [pair, mine])], axi...]
    ppermute x3, waiting for transfers between devices: 10.1 us -> 8.12 us  [topo_reduce_scatter(): lax.ppermute(ahead.astype(jnp.bfloat16), 'expert', [(j, j + 4) for j in r...]
    unnamed x30 -> x26, local copies, waits for them, and re-layouts: 5.66 us -> 5.12 us
  transfers between devices with their start and end apart: 16 -> 29, of which waited for: 11 -> 10; matrix products, arithmetic and copies ran while one was open for 0% -> 6% of each run, Pallas kernels for 0% -> 0%
where the time goes in v5:
time: 145 us; the launch traced here: 144 us
  starting transfers between devices  60.1 us (41%)
  waiting for transfers between devices  31.6 us (22%)
  other arithmetic  21.1 us (15%)
  matrix products  20.3 us (14%)
  local copies, waits for them, and re-layouts  9.53 us (7%)
    ppermute x3, starting transfers between devices, topo_reduce_scatter(): lax.ppermute(ahead.astype(jnp.bfloat16), 'expert', [(j, j + 4) for j in r...  20.1 us
    ppermute x7, starting transfers between devices, row_sum(): got = lax.ppermute(theirs.astype(jnp.bfloat16), 'expert', pairs)  11.1 us
    ppermute x3, starting transfers between devices, topo_all_gather(): lax.ppermute(ahead, 'expert', [(j, j + 4) for j in range(experts) if step...  9.04 us
    ppermute x3, waiting for transfers between devices, topo_all_gather(): lax.ppermute(behind, 'expert', [(j, j - 4) for j in range(experts) if 1 <...  8.96 us
    ppermute x3, starting transfers between devices, topo_all_gather(): there.append((lax.ppermute(behind, 'expert', behind_row), line + step))  8.94 us
    ppermute x3, waiting for transfers between devices, topo_reduce_scatter(): lax.ppermute(ahead.astype(jnp.bfloat16), 'expert', [(j, j + 4) for j in r...  8.12 us
    another operation x2, other arithmetic, topo_all_gather(): jnp.stack([pick(in_row, [column, across]), pick(in_row, [across, column])...  5.2 us
    unnamed x26, local copies, waits for them, and re-layouts  5.12 us
  transfers between devices with their start and end apart: 29, of which 10 were waited for; matrix products, arithmetic and copies ran while one was open for 6% of the time, Pallas kernels for 0%

profile of v5, /device:TPU:0, one launch (start us, length us, event | category | flops | bytes accessed | tf_op | source)
XLA Modules:
  0.0 143.9 jit_solution(8927961491885831392)
XLA Ops:
  2.4 2.0 %fusion.58 = (bf16[32,2048]{1,0:T(8,128)(2,1)S(1)}, f32[32,2048]{1,0:T(8,128)}) fusion(bf16[128,2048]{1,0:T(8,128)(2,1)} %param.11, s32[128]{0:T(128)} %param.12), kind=kOutput, calls=%fused_computation.117 | convolution fusion | flops 16846848 | bytes 918016 | tf_op jit(solution)/shard_map/dot_general | solution.py:224
  4.4 2.0 %fusion.59 = (bf16[32,2048]{1,0:T(8,128)(2,1)S(1)}, f32[32,2048]{1,0:T(8,128)}) fusion(f32[32]{0:T(128)S(1)} %convert_reduce_fusion, bf16[128,2048]{1,0:T(8,128)(2,1)} %param.10, s32[128]{0:T(128)} %param.12), kind=kOutput, calls=%fused_computation.118 | convolution fusion | flops 16912384 | bytes 918144 | tf_op jit(solution)/shard_map/dot_general | solution.py:221
  7.7 6.3 %collective-permute-start.3 = (bf16[32,4224]{1,0:T(8,128)(2,1)S(1)}, bf16[32,4224]{1,0:T(8,128)(2,1)}, u32[]{:S(2)}, u32[]{:S(2)}) collective-permute-start(bf16[32,4224]{1,0:T(8,128)(2,1)S(1)} %fusion.40), channel_id=1, source_target_pairs={{0,4},{1,5},{2,6},{3,7},{4,8},{5,9},{6,10},{7,11},{8,12},{9,13},{1... | collective-permute-start | bytes 811016 | tf_op jit(solution)/shard_map/ppermute | solution.py:120
  14.0 3.9 %collective-permute-done = bf16[32,4224]{1,0:T(8,128)(2,1)} collective-permute-done((bf16[32,4224]{1,0:T(8,128)(2,1)S(1)}, bf16[32,4224]{1,0:T(8,128)(2,1)}, u32[]{:S(2)}, u32[]{:S(2)}) %collective-permute-start) | collective-permute-done | bytes 270368 | tf_op jit(solution)/shard_map/ppermute | solution.py:125
  22.3 2.3 %collective-permute-start.10 = (bf16[32,4224]{1,0:T(8,128)(2,1)}, bf16[32,4224]{1,0:T(8,128)(2,1)}, u32[]{:S(2)}, u32[]{:S(2)}) collective-permute-start(bf16[32,4224]{1,0:T(8,128)(2,1)} %collective-permute-done), channel_id=1, source_target_pairs={{0,2},{1,3},{2,0},{3,1},{4,6},{5,7},{6,4},{7,5},{8,10},{9,11},{10,... | collective-permute-start | bytes 811016 | tf_op jit(solution)/shard_map/ppermute | solution.py:135
  24.5 3.2 %collective-permute-done.1 = bf16[32,4224]{1,0:T(8,128)(2,1)} collective-permute-done((bf16[32,4224]{1,0:T(8,128)(2,1)}, bf16[32,4224]{1,0:T(8,128)(2,1)}, u32[]{:S(2)}, u32[]{:S(2)}) %collective-permute-start.1) | collective-permute-done | bytes 270368 | tf_op jit(solution)/shard_map/ppermute | solution.py:125
  31.1 3.3 %collective-permute-start.8 = (bf16[32,4224]{1,0:T(8,128)(2,1)}, bf16[32,4224]{1,0:T(8,128)(2,1)S(1)}, u32[]{:S(2)}, u32[]{:S(2)}) collective-permute-start(bf16[32,4224]{1,0:T(8,128)(2,1)} %collective-permute-done.1), channel_id=1, source_target_pairs={{0,2},{1,3},{2,0},{3,1},{4,6},{5,7},{6,4},{7,5},{16,18},{17,19},{1... | collective-permute-start | bytes 811016 | tf_op jit(solution)/shard_map/ppermute | solution.py:135
  36.9 3.4 %collective-permute-start.6 = (bf16[32,4224]{1,0:T(8,128)(2,1)}, bf16[32,4224]{1,0:T(8,128)(2,1)S(1)}, u32[]{:S(2)}, u32[]{:S(2)}) collective-permute-start(bf16[32,4224]{1,0:T(8,128)(2,1)} %collective-permute-done.2), channel_id=1, source_target_pairs={{0,2},{1,3},{2,0},{3,1},{16,18},{17,19},{18,16},{19,17}} | collective-permute-start | bytes 811016 | tf_op jit(solution)/shard_map/ppermute | solution.py:135
  42.9 2.8 %collective-permute-done.6 = bf16[32,4224]{1,0:T(8,128)(2,1)S(1)} collective-permute-done((bf16[32,4224]{1,0:T(8,128)(2,1)}, bf16[32,4224]{1,0:T(8,128)(2,1)S(1)}, u32[]{:S(2)}, u32[]{:S(2)}) %collective-permute-start.6) | collective-permute-done | bytes 270368 | tf_op jit(solution)/shard_map/ppermute | solution.py:135
  47.5 2.6 %select_bitcast_fusion.4 = bf16[4,1,1,32,4224]{4,3,0,2,1:T(8,128)(2,1)S(1)} fusion(pred[]{:T(512)S(6)} %eq.147, bf16[32,4224]{1,0:T(8,128)(2,1)S(1)} %fusion.40, pred[4]{0:T(512)(128)(4,1)S(1)} %get-tuple-element.30, bf16[32,4224]{1,0:T(8,128)(2,1)} %collective-permute-done.3, pred[4]{0:T(512)(128)(4,1)S(1)} %get-tuple-element.31, ...), kind=kLoop, calls=%fused_computation.43 | loop fusion | flops 8110080 | bytes 4866077 | tf_op jit(solution)/shard_map/stack | solution.py:143
  50.1 2.6 %select_bitcast_fusion.3 = bf16[4,1,1,32,4224]{4,3,0,2,1:T(8,128)(2,1)S(1)} fusion(pred[]{:T(512)S(6)} %eq.147, bf16[32,4224]{1,0:T(8,128)(2,1)S(1)} %fusion.40, pred[4]{0:T(512)(128)(4,1)S(1)} %get-tuple-element.30, bf16[32,4224]{1,0:T(8,128)(2,1)} %collective-permute-done.3, pred[4]{0:T(512)(128)(4,1)S(1)} %get-tuple-element.31, ...), kind=kLoop, calls=%fused_computation.42 | loop fusion | flops 8110080 | bytes 4866077 | tf_op jit(solution)/shard_map/stack | solution.py:143
  54.6 2.6 %copy-done.8 = bf16[1,2048,768]{2,1,0:T(8,128)(2,1)S(1)} copy-done((bf16[1,2048,768]{2,1,0:T(8,128)(2,1)S(1)}, bf16[1,2048,768]{2,1,0:T(8,128)(2,1)}, u32[]{:S(2)}) %copy-start.8) | copy-done | bytes 3145752
  57.3 3.0 %fusion.10 = f32[512,768]{1,0:T(8,128)} fusion(bf16[1,2048,768]{2,1,0:T(8,128)(2,1)S(1)} %copy-done.8, bf16[512,4224]{1,0:T(8,128)(2,1)S(1)} %bitcast.107), kind=kOutput, calls=%fused_computation.18 | convolution fusion | flops 1610612736 | bytes 6815744 | tf_op jit(solution)/shard_map/dot_general | solution.py:195
  60.2 3.0 %fusion.6 = f32[512,768]{1,0:T(8,128)} fusion(bf16[1,2048,768]{2,1,0:T(8,128)(2,1)S(1)} %copy-done, bf16[512,4224]{1,0:T(8,128)(2,1)S(1)} %bitcast.108), kind=kOutput, calls=%fused_computation.14 | convolution fusion | flops 1610612736 | bytes 6815744 | tf_op jit(solution)/shard_map/dot_general | solution.py:196
  63.3 4.5 %fusion = f32[512,768]{1,0:T(8,128)S(1)} fusion(bf16[1,768,2048]{2,1,0:T(8,128)(2,1)} %param.17, bf16[512,4224]{1,0:T(8,128)(2,1)} %bitcast.109), kind=kOutput, calls=%fused_computation.8 | convolution fusion | flops 1610612736 | bytes 6815744 | tf_op jit(solution)/shard_map/dot_general | solution.py:200
  72.1 2.3 %multiply_convert_fusion = bf16[512,2048]{1,0:T(8,128)(2,1)S(1)} fusion(f32[512,2048]{1,0:T(8,128)S(1)} %fusion.4, bf16[1,2048,768]{2,1,0:T(8,128)(2,1)S(1)} %copy-done.9, f32[512]{0:T(512)S(1)} %fusion.50, f32[512,768]{1,0:T(8,128)S(1)} %copy-done.10, f32[512,768]{1,0:T(8,128)S(1)} %fusion, f32[512,768]{1,0:T(8,128)S(1)} %copy-done.11), kind=kOutput, calls=%fused_computation.5 | convolution fusion | flops 1619787776 | bytes 14157824 | tf_op jit(solution)/shard_map/dot_general | solution.py:205
  77.4 3.9 %collective-permute-done.15 = bf16[4,2,32,4096]{3,2,1,0:T(8,128)(2,1)} collective-permute-done((bf16[4,2,32,4096]{3,2,1,0:T(8,128)(2,1)S(1)}, bf16[4,2,32,4096]{3,2,1,0:T(8,128)(2,1)}, u32[]{:S(2)}, u32[]{:S(2)}) %collective-permute-start.15) | collective-permute-done | bytes 2097184 | tf_op jit(solution)/shard_map/ppermute | solution.py:159
  81.3 3.9 %convert_add_fusion = f32[4,2,32,4096]{3,2,1,0:T(8,128)S(1)} fusion(bf16[4,2,32,4096]{3,2,1,0:T(8,128)(2,1)} %collective-permute-done.15, pred[]{:T(512)S(6)} %eq.148, bf16[4,2,2,32,4096]{4,3,2,1,0:T(8,128)(2,1)} %bitcast.105), kind=kLoop, calls=%fused_computation.4 | loop fusion | flops 4194304 | bytes 10485761 | tf_op jit(solution)/shard_map/add | solution.py:160
  85.6 3.1 %collective-permute-start.17 = (bf16[32,4096]{1,0:T(8,128)(2,1)S(1)}, bf16[32,4096]{1,0:T(8,128)(2,1)S(1)}, u32[]{:S(2)}, u32[]{:S(2)}) collective-permute-start(bf16[32,4096]{1,0:T(8,128)(2,1)S(1)} %get-tuple-element.21), channel_id=1, source_target_pairs={{0,2},{1,3},{2,0},{3,1},{16,18},{17,19},{18,16},{19,17}} | collective-permute-start | bytes 786440 | tf_op jit(solution)/shard_map/ppermute | solution.py:170
  89.7 3.0 %collective-permute-start.19 = (bf16[32,4096]{1,0:T(8,128)(2,1)S(1)}, bf16[32,4096]{1,0:T(8,128)(2,1)S(1)}, u32[]{:S(2)}, u32[]{:S(2)}) collective-permute-start(bf16[32,4096]{1,0:T(8,128)(2,1)S(1)} %get-tuple-element.20), channel_id=1, source_target_pairs={{0,2},{1,3},{2,0},{3,1},{4,6},{5,7},{6,4},{7,5},{16,18},{17,19},{1... | collective-permute-start | bytes 786440 | tf_op jit(solution)/shard_map/ppermute | solution.py:170
  93.4 3.3 %collective-permute-done.17 = bf16[32,4096]{1,0:T(8,128)(2,1)S(1)} collective-permute-done((bf16[32,4096]{1,0:T(8,128)(2,1)S(1)}, bf16[32,4096]{1,0:T(8,128)(2,1)S(1)}, u32[]{:S(2)}, u32[]{:S(2)}) %collective-permute-start.17) | collective-permute-done | bytes 262176 | tf_op jit(solution)/shard_map/ppermute | solution.py:170
  96.8 2.2 %collective-permute-start.18 = (bf16[32,4096]{1,0:T(8,128)(2,1)S(1)}, bf16[32,4096]{1,0:T(8,128)(2,1)S(1)}, u32[]{:S(2)}, u32[]{:S(2)}) collective-permute-start(bf16[32,4096]{1,0:T(8,128)(2,1)S(1)} %get-tuple-element.13), channel_id=1, source_target_pairs={{0,4},{1,5},{2,6},{3,7},{16,20},{17,21},{18,22},{19,23}} | collective-permute-start | bytes 786440 | tf_op jit(solution)/shard_map/ppermute | solution.py:178
  99.7 2.4 %collective-permute-start.21 = (bf16[32,4096]{1,0:T(8,128)(2,1)S(1)}, bf16[32,4096]{1,0:T(8,128)(2,1)S(1)}, u32[]{:S(2)}, u32[]{:S(2)}) collective-permute-start(bf16[32,4096]{1,0:T(8,128)(2,1)S(1)} %get-tuple-element.19), channel_id=1, source_target_pairs={{0,2},{1,3},{2,0},{3,1},{4,6},{5,7},{6,4},{7,5},{8,10},{9,11},{10,... | collective-permute-start | bytes 786440 | tf_op jit(solution)/shard_map/ppermute | solution.py:170
  102.8 2.0 %collective-permute-done.18 = bf16[32,4096]{1,0:T(8,128)(2,1)S(1)} collective-permute-done((bf16[32,4096]{1,0:T(8,128)(2,1)S(1)}, bf16[32,4096]{1,0:T(8,128)(2,1)S(1)}, u32[]{:S(2)}, u32[]{:S(2)}) %collective-permute-start.18) | collective-permute-done | bytes 262176 | tf_op jit(solution)/shard_map/ppermute | solution.py:178
  104.9 4.4 %collective-permute-start.20 = (bf16[32,4096]{1,0:T(8,128)(2,1)S(1)}, bf16[32,4096]{1,0:T(8,128)(2,1)S(1)}, u32[]{:S(2)}, u32[]{:S(2)}) collective-permute-start(bf16[32,4096]{1,0:T(8,128)(2,1)S(1)} %get-tuple-element.11), channel_id=1, source_target_pairs={{0,4},{1,5},{2,6},{3,7},{4,8},{5,9},{6,10},{7,11},{16,20},{17,21},... | collective-permute-start | bytes 786440 | tf_op jit(solution)/shard_map/ppermute | solution.py:178
  110.6 3.6 %collective-permute-done.20 = bf16[32,4096]{1,0:T(8,128)(2,1)S(1)} collective-permute-done((bf16[32,4096]{1,0:T(8,128)(2,1)S(1)}, bf16[32,4096]{1,0:T(8,128)(2,1)S(1)}, u32[]{:S(2)}, u32[]{:S(2)}) %collective-permute-start.20) | collective-permute-done | bytes 262176 | tf_op jit(solution)/shard_map/ppermute | solution.py:178
  114.4 13.6 %collective-permute-start.22 = (bf16[32,4096]{1,0:T(8,128)(2,1)S(1)}, bf16[32,4096]{1,0:T(8,128)(2,1)S(1)}, u32[]{:S(2)}, u32[]{:S(2)}) collective-permute-start(bf16[32,4096]{1,0:T(8,128)(2,1)S(1)} %get-tuple-element.9), channel_id=1, source_target_pairs={{0,4},{1,5},{2,6},{3,7},{4,8},{5,9},{6,10},{7,11},{8,12},{9,13},{1... | collective-permute-start | bytes 786440 | tf_op jit(solution)/shard_map/ppermute | solution.py:178
  129.4 2.5 %collective-permute-done.22 = bf16[32,4096]{1,0:T(8,128)(2,1)S(1)} collective-permute-done((bf16[32,4096]{1,0:T(8,128)(2,1)S(1)}, bf16[32,4096]{1,0:T(8,128)(2,1)S(1)}, u32[]{:S(2)}, u32[]{:S(2)}) %collective-permute-start.22) | collective-permute-done | bytes 262176 | tf_op jit(solution)/shard_map/ppermute | solution.py:178
  131.9 4.4 %collective-permute-done.28 = bf16[32,4096]{1,0:T(8,128)(2,1)S(1)} collective-permute-done((bf16[32,4096]{1,0:T(8,128)(2,1)S(1)}, bf16[32,4096]{1,0:T(8,128)(2,1)S(1)}, u32[]{:S(2)}, u32[]{:S(2)}) %collective-permute-start.28) | collective-permute-done | bytes 262176 | tf_op jit(solution)/shard_map/ppermute | solution.py:185
  136.5 1.9 %gather_fusion = f32[128,2048]{1,0:T(8,128)} fusion(f32[32,2048]{1,0:T(8,128)S(1)} %get-tuple-element.23, s32[1024]{0:T(1024)S(1)} %pad_clamp_fusion), kind=kCustom, calls=%fused_computation.clone | custom fusion | bytes 2097664 | tf_op jit(solution)/shard_map/jit(_take)/gather | solution.py:256
  138.4 1.9 %gather_fusion.1 = f32[128,2048]{1,0:T(8,128)} fusion(f32[32,2048]{1,0:T(8,128)S(1)} %get-tuple-element.22, s32[1024]{0:T(1024)S(1)} %pad_clamp_fusion), kind=kCustom, calls=%fused_computation.1.clone | custom fusion | bytes 2097664 | tf_op jit(solution)/shard_map/jit(_take)/gather | solution.py:257
  140.4 3.6 %select_add_fusion = (f32[128,2048]{1,0:T(8,128)}, f32[128,2048]{1,0:T(8,128)}) fusion(f32[128,2048]{1,0:T(8,128)} %gather_fusion.1, bf16[128,2048]{1,0:T(8,128)(2,1)} %param.11, pred[128]{0:T(512)(128)(4,1)S(1)} %compare_and_fusion, f32[128,2048]{1,0:T(8,128)} %gather_fusion, bf16[128,2048]{1,0:T(8,128)(2,1)} %param.10), kind=kLoop, calls=%fused_computation.46 | loop fusion | flops 1572864 | bytes 5243008 | tf_op jit(solution)/shard_map/add | solution.py:257
  (98 shorter events, 33.2 us)
Async XLA Ops:
  0.6 59.6 %copy-start = (bf16[1,2048,768]{2,1,0:T(8,128)(2,1)S(1)}, bf16[1,2048,768]{2,1,0:T(8,128)(2,1)}, u32[]{:S(2)}) copy-start(bf16[1,2048,768]{2,1,0:T(8,128)(2,1)} %param.16) | copy-start | bytes 9437188
  6.4 11.5 %collective-permute-start = (bf16[32,4224]{1,0:T(8,128)(2,1)S(1)}, bf16[32,4224]{1,0:T(8,128)(2,1)}, u32[]{:S(2)}, u32[]{:S(2)}) collective-permute-start(bf16[32,4224]{1,0:T(8,128)(2,1)S(1)} %fusion.40), channel_id=1, source_target_pairs={{4,0},{5,1},{6,2},{7,3},{8,4},{9,5},{10,6},{11,7},{12,8},{13,9},{1... | collective-permute-start | bytes 811016 | tf_op jit(solution)/shard_map/ppermute | solution.py:125
  7.7 11.5 %collective-permute-start.3 = (bf16[32,4224]{1,0:T(8,128)(2,1)S(1)}, bf16[32,4224]{1,0:T(8,128)(2,1)}, u32[]{:S(2)}, u32[]{:S(2)}) collective-permute-start(bf16[32,4224]{1,0:T(8,128)(2,1)S(1)} %fusion.40), channel_id=1, source_target_pairs={{0,4},{1,5},{2,6},{3,7},{4,8},{5,9},{6,10},{7,11},{8,12},{9,13},{1... | collective-permute-start | bytes 811016 | tf_op jit(solution)/shard_map/ppermute | solution.py:120
  17.9 9.9 %collective-permute-start.1 = (bf16[32,4224]{1,0:T(8,128)(2,1)}, bf16[32,4224]{1,0:T(8,128)(2,1)}, u32[]{:S(2)}, u32[]{:S(2)}) collective-permute-start(bf16[32,4224]{1,0:T(8,128)(2,1)} %collective-permute-done), channel_id=1, source_target_pairs={{4,0},{5,1},{6,2},{7,3},{8,4},{9,5},{10,6},{11,7},{20,16},{21,17},... | collective-permute-start | bytes 811016 | tf_op jit(solution)/shard_map/ppermute | solution.py:125
  19.2 9.9 %collective-permute-start.4 = (bf16[32,4224]{1,0:T(8,128)(2,1)}, bf16[32,4224]{1,0:T(8,128)(2,1)}, u32[]{:S(2)}, u32[]{:S(2)}) collective-permute-start(bf16[32,4224]{1,0:T(8,128)(2,1)} %collective-permute-done.3), channel_id=1, source_target_pairs={{4,8},{5,9},{6,10},{7,11},{8,12},{9,13},{10,14},{11,15},{20,24},{2... | collective-permute-start | bytes 811016 | tf_op jit(solution)/shard_map/ppermute | solution.py:120
  20.6 10.5 %collective-permute-start.12 = (bf16[32,4224]{1,0:T(8,128)(2,1)S(1)}, bf16[32,4224]{1,0:T(8,128)(2,1)}, u32[]{:S(2)}, u32[]{:S(2)}) collective-permute-start(bf16[32,4224]{1,0:T(8,128)(2,1)S(1)} %fusion.40), channel_id=1, source_target_pairs={{0,2},{1,3},{2,0},{3,1},{4,6},{5,7},{6,4},{7,5},{8,10},{9,11},{10,... | collective-permute-start | bytes 811016 | tf_op jit(solution)/shard_map/ppermute | solution.py:117
  22.3 12.1 %collective-permute-start.10 = (bf16[32,4224]{1,0:T(8,128)(2,1)}, bf16[32,4224]{1,0:T(8,128)(2,1)}, u32[]{:S(2)}, u32[]{:S(2)}) collective-permute-start(bf16[32,4224]{1,0:T(8,128)(2,1)} %collective-permute-done), channel_id=1, source_target_pairs={{0,2},{1,3},{2,0},{3,1},{4,6},{5,7},{6,4},{7,5},{8,10},{9,11},{10,... | collective-permute-start | bytes 811016 | tf_op jit(solution)/shard_map/ppermute | solution.py:135
  27.8 9.2 %collective-permute-start.2 = (bf16[32,4224]{1,0:T(8,128)(2,1)}, bf16[32,4224]{1,0:T(8,128)(2,1)}, u32[]{:S(2)}, u32[]{:S(2)}) collective-permute-start(bf16[32,4224]{1,0:T(8,128)(2,1)} %collective-permute-done.1), channel_id=1, source_target_pairs={{4,0},{5,1},{6,2},{7,3},{20,16},{21,17},{22,18},{23,19}} | collective-permute-start | bytes 811016 | tf_op jit(solution)/shard_map/ppermute | solution.py:125
  29.1 11.3 %collective-permute-start.5 = (bf16[32,4224]{1,0:T(8,128)(2,1)}, bf16[32,4224]{1,0:T(8,128)(2,1)}, u32[]{:S(2)}, u32[]{:S(2)}) collective-permute-start(bf16[32,4224]{1,0:T(8,128)(2,1)} %collective-permute-done.4), channel_id=1, source_target_pairs={{8,12},{9,13},{10,14},{11,15},{24,28},{25,29},{26,30},{27,31}} | collective-permute-start | bytes 811016 | tf_op jit(solution)/shard_map/ppermute | solution.py:120
  30.5 12.4 %collective-permute-start.11 = (bf16[32,4224]{1,0:T(8,128)(2,1)}, bf16[32,4224]{1,0:T(8,128)(2,1)S(1)}, u32[]{:S(2)}, u32[]{:S(2)}) collective-permute-start(bf16[32,4224]{1,0:T(8,128)(2,1)} %collective-permute-done.3), channel_id=1, source_target_pairs={{4,6},{5,7},{6,4},{7,5},{8,10},{9,11},{10,8},{11,9},{12,14},{13,15... | collective-permute-start | bytes 811016 | tf_op jit(solution)/shard_map/ppermute | solution.py:134
  31.1 11.8 %collective-permute-start.8 = (bf16[32,4224]{1,0:T(8,128)(2,1)}, bf16[32,4224]{1,0:T(8,128)(2,1)S(1)}, u32[]{:S(2)}, u32[]{:S(2)}) collective-permute-start(bf16[32,4224]{1,0:T(8,128)(2,1)} %collective-permute-done.1), channel_id=1, source_target_pairs={{0,2},{1,3},{2,0},{3,1},{4,6},{5,7},{6,4},{7,5},{16,18},{17,19},{1... | collective-permute-start | bytes 811016 | tf_op jit(solution)/shard_map/ppermute | solution.py:135
  34.4 8.5 %collective-permute-start.9 = (bf16[32,4224]{1,0:T(8,128)(2,1)}, bf16[32,4224]{1,0:T(8,128)(2,1)S(1)}, u32[]{:S(2)}, u32[]{:S(2)}) collective-permute-start(bf16[32,4224]{1,0:T(8,128)(2,1)} %collective-permute-done.4), channel_id=1, source_target_pairs={{8,10},{9,11},{10,8},{11,9},{12,14},{13,15},{14,12},{15,13},{24,26... | collective-permute-start | bytes 811016 | tf_op jit(solution)/shard_map/ppermute | solution.py:134
  36.9 8.9 %collective-permute-start.6 = (bf16[32,4224]{1,0:T(8,128)(2,1)}, bf16[32,4224]{1,0:T(8,128)(2,1)S(1)}, u32[]{:S(2)}, u32[]{:S(2)}) collective-permute-start(bf16[32,4224]{1,0:T(8,128)(2,1)} %collective-permute-done.2), channel_id=1, source_target_pairs={{0,2},{1,3},{2,0},{3,1},{16,18},{17,19},{18,16},{19,17}} | collective-permute-start | bytes 811016 | tf_op jit(solution)/shard_map/ppermute | solution.py:135
  40.4 5.4 %collective-permute-start.7 = (bf16[32,4224]{1,0:T(8,128)(2,1)}, bf16[32,4224]{1,0:T(8,128)(2,1)S(1)}, u32[]{:S(2)}, u32[]{:S(2)}) collective-permute-start(bf16[32,4224]{1,0:T(8,128)(2,1)} %collective-permute-done.5), channel_id=1, source_target_pairs={{12,14},{13,15},{14,12},{15,13},{28,30},{29,31},{30,28},{31,29}} | collective-permute-start | bytes 811016 | tf_op jit(solution)/shard_map/ppermute | solution.py:134
  42.8 9.9 %collective-permute-start.13 = (bf16[4,32,4224]{2,1,0:T(8,128)(2,1)S(1)}, bf16[4,32,4224]{2,1,0:T(8,128)(2,1)S(1)}, u32[]{:S(2)}, u32[]{:S(2)}) collective-permute-start(bf16[4,32,4224]{2,1,0:T(8,128)(2,1)S(1)} %select_select_fusion.1), channel_id=1, source_target_pairs={{0,1},{1,0},{2,3},{3,2},{4,5},{5,4},{6,7},{7,6},{8,9},{9,8},{10,11... | collective-permute-start | bytes 3244040 | tf_op jit(solution)/shard_map/ppermute | solution.py:139
  47.4 5.3 %collective-permute-start.14 = (bf16[4,32,4224]{2,1,0:T(8,128)(2,1)S(1)}, bf16[4,32,4224]{2,1,0:T(8,128)(2,1)S(1)}, u32[]{:S(2)}, u32[]{:S(2)}) collective-permute-start(bf16[4,32,4224]{2,1,0:T(8,128)(2,1)S(1)} %select_select_fusion), channel_id=1, source_target_pairs={{0,1},{1,0},{2,3},{3,2},{4,5},{5,4},{6,7},{7,6},{8,9},{9,8},{10,11... | collective-permute-start | bytes 3244040 | tf_op jit(solution)/shard_map/ppermute | solution.py:140
  76.9 4.4 %collective-permute-start.15 = (bf16[4,2,32,4096]{3,2,1,0:T(8,128)(2,1)S(1)}, bf16[4,2,32,4096]{3,2,1,0:T(8,128)(2,1)}, u32[]{:S(2)}, u32[]{:S(2)}) collective-permute-start(bf16[4,2,32,4096]{3,2,1,0:T(8,128)(2,1)S(1)} %select_bitcast_fusion), channel_id=1, source_target_pairs={{0,1},{1,0},{2,3},{3,2},{4,5},{5,4},{6,7},{7,6},{8,9},{9,8},{10,11... | collective-permute-start | bytes 6291464 | tf_op jit(solution)/shard_map/ppermute | solution.py:159
  85.6 11.0 %collective-permute-start.17 = (bf16[32,4096]{1,0:T(8,128)(2,1)S(1)}, bf16[32,4096]{1,0:T(8,128)(2,1)S(1)}, u32[]{:S(2)}, u32[]{:S(2)}) collective-permute-start(bf16[32,4096]{1,0:T(8,128)(2,1)S(1)} %get-tuple-element.21), channel_id=1, source_target_pairs={{0,2},{1,3},{2,0},{3,1},{16,18},{17,19},{18,16},{19,17}} | collective-permute-start | bytes 786440 | tf_op jit(solution)/shard_map/ppermute | solution.py:170
  88.8 7.9 %collective-permute-start.23 = (bf16[32,4096]{1,0:T(8,128)(2,1)S(1)}, bf16[32,4096]{1,0:T(8,128)(2,1)S(1)}, u32[]{:S(2)}, u32[]{:S(2)}) collective-permute-start(bf16[32,4096]{1,0:T(8,128)(2,1)S(1)} %get-tuple-element.18), channel_id=1, source_target_pairs={{12,14},{13,15},{14,12},{15,13},{28,30},{29,31},{30,28},{31,29}} | collective-permute-start | bytes 786440 | tf_op jit(solution)/shard_map/ppermute | solution.py:170
  89.7 12.4 %collective-permute-start.19 = (bf16[32,4096]{1,0:T(8,128)(2,1)S(1)}, bf16[32,4096]{1,0:T(8,128)(2,1)S(1)}, u32[]{:S(2)}, u32[]{:S(2)}) collective-permute-start(bf16[32,4096]{1,0:T(8,128)(2,1)S(1)} %get-tuple-element.20), channel_id=1, source_target_pairs={{0,2},{1,3},{2,0},{3,1},{4,6},{5,7},{6,4},{7,5},{16,18},{17,19},{1... | collective-permute-start | bytes 786440 | tf_op jit(solution)/shard_map/ppermute | solution.py:170
  92.7 10.1 %collective-permute-start.25 = (bf16[32,4096]{1,0:T(8,128)(2,1)S(1)}, bf16[32,4096]{1,0:T(8,128)(2,1)S(1)}, u32[]{:S(2)}, u32[]{:S(2)}) collective-permute-start(bf16[32,4096]{1,0:T(8,128)(2,1)S(1)} %get-tuple-element.17), channel_id=1, source_target_pairs={{8,10},{9,11},{10,8},{11,9},{12,14},{13,15},{14,12},{15,13},{24,26... | collective-permute-start | bytes 786440 | tf_op jit(solution)/shard_map/ppermute | solution.py:170
  96.8 7.9 %collective-permute-start.18 = (bf16[32,4096]{1,0:T(8,128)(2,1)S(1)}, bf16[32,4096]{1,0:T(8,128)(2,1)S(1)}, u32[]{:S(2)}, u32[]{:S(2)}) collective-permute-start(bf16[32,4096]{1,0:T(8,128)(2,1)S(1)} %get-tuple-element.13), channel_id=1, source_target_pairs={{0,4},{1,5},{2,6},{3,7},{16,20},{17,21},{18,22},{19,23}} | collective-permute-start | bytes 786440 | tf_op jit(solution)/shard_map/ppermute | solution.py:178
  99.0 5.8 %collective-permute-start.24 = (bf16[32,4096]{1,0:T(8,128)(2,1)S(1)}, bf16[32,4096]{1,0:T(8,128)(2,1)S(1)}, u32[]{:S(2)}, u32[]{:S(2)}) collective-permute-start(bf16[32,4096]{1,0:T(8,128)(2,1)S(1)} %get-tuple-element.14), channel_id=1, source_target_pairs={{12,8},{13,9},{14,10},{15,11},{28,24},{29,25},{30,26},{31,27}} | collective-permute-start | bytes 786440 | tf_op jit(solution)/shard_map/ppermute | solution.py:185
  99.7 11.0 %collective-permute-start.21 = (bf16[32,4096]{1,0:T(8,128)(2,1)S(1)}, bf16[32,4096]{1,0:T(8,128)(2,1)S(1)}, u32[]{:S(2)}, u32[]{:S(2)}) collective-permute-start(bf16[32,4096]{1,0:T(8,128)(2,1)S(1)} %get-tuple-element.19), channel_id=1, source_target_pairs={{0,2},{1,3},{2,0},{3,1},{4,6},{5,7},{6,4},{7,5},{8,10},{9,11},{10,... | collective-permute-start | bytes 786440 | tf_op jit(solution)/shard_map/ppermute | solution.py:170
  102.1 8.5 %collective-permute-start.27 = (bf16[32,4096]{1,0:T(8,128)(2,1)S(1)}, bf16[32,4096]{1,0:T(8,128)(2,1)S(1)}, u32[]{:S(2)}, u32[]{:S(2)}) collective-permute-start(bf16[32,4096]{1,0:T(8,128)(2,1)S(1)} %get-tuple-element.16), channel_id=1, source_target_pairs={{4,6},{5,7},{6,4},{7,5},{8,10},{9,11},{10,8},{11,9},{12,14},{13,15... | collective-permute-start | bytes 786440 | tf_op jit(solution)/shard_map/ppermute | solution.py:170
  104.9 9.3 %collective-permute-start.20 = (bf16[32,4096]{1,0:T(8,128)(2,1)S(1)}, bf16[32,4096]{1,0:T(8,128)(2,1)S(1)}, u32[]{:S(2)}, u32[]{:S(2)}) collective-permute-start(bf16[32,4096]{1,0:T(8,128)(2,1)S(1)} %get-tuple-element.11), channel_id=1, source_target_pairs={{0,4},{1,5},{2,6},{3,7},{4,8},{5,9},{6,10},{7,11},{16,20},{17,21},... | collective-permute-start | bytes 786440 | tf_op jit(solution)/shard_map/ppermute | solution.py:178
  109.3 4.9 %collective-permute-start.26 = (bf16[32,4096]{1,0:T(8,128)(2,1)S(1)}, bf16[32,4096]{1,0:T(8,128)(2,1)S(1)}, u32[]{:S(2)}, u32[]{:S(2)}) collective-permute-start(bf16[32,4096]{1,0:T(8,128)(2,1)S(1)} %get-tuple-element.12), channel_id=1, source_target_pairs={{8,4},{9,5},{10,6},{11,7},{12,8},{13,9},{14,10},{15,11},{24,20},{2... | collective-permute-start | bytes 786440 | tf_op jit(solution)/shard_map/ppermute | solution.py:185
  110.0 19.3 %collective-permute-start.16 = (bf16[32,4096]{1,0:T(8,128)(2,1)S(1)}, bf16[32,4096]{1,0:T(8,128)(2,1)S(1)}, u32[]{:S(2)}, u32[]{:S(2)}) collective-permute-start(bf16[32,4096]{1,0:T(8,128)(2,1)S(1)} %get-tuple-element.15), channel_id=1, source_target_pairs={{0,2},{1,3},{2,0},{3,1},{4,6},{5,7},{6,4},{7,5},{8,10},{9,11},{10,... | collective-permute-start | bytes 786440 | tf_op jit(solution)/shard_map/ppermute | solution.py:170
  114.4 22.0 %copy-start.4 = (f32[32,2048]{1,0:T(8,128)S(1)}, f32[32,2048]{1,0:T(8,128)}, u32[]{:S(2)}) copy-start(f32[32,2048]{1,0:T(8,128)} %get-tuple-element.27) | copy-start | bytes 786436
  114.4 22.0 %copy-start.5 = (f32[32,2048]{1,0:T(8,128)S(1)}, f32[32,2048]{1,0:T(8,128)}, u32[]{:S(2)}) copy-start(f32[32,2048]{1,0:T(8,128)} %get-tuple-element.29) | copy-start | bytes 786436
  114.4 17.4 %collective-permute-start.22 = (bf16[32,4096]{1,0:T(8,128)(2,1)S(1)}, bf16[32,4096]{1,0:T(8,128)(2,1)S(1)}, u32[]{:S(2)}, u32[]{:S(2)}) collective-permute-start(bf16[32,4096]{1,0:T(8,128)(2,1)S(1)} %get-tuple-element.9), channel_id=1, source_target_pairs={{0,4},{1,5},{2,6},{3,7},{4,8},{5,9},{6,10},{7,11},{8,12},{9,13},{1... | collective-permute-start | bytes 786440 | tf_op jit(solution)/shard_map/ppermute | solution.py:178
  128.0 8.3 %collective-permute-start.28 = (bf16[32,4096]{1,0:T(8,128)(2,1)S(1)}, bf16[32,4096]{1,0:T(8,128)(2,1)S(1)}, u32[]{:S(2)}, u32[]{:S(2)}) collective-permute-start(bf16[32,4096]{1,0:T(8,128)(2,1)S(1)} %get-tuple-element.10), channel_id=1, source_target_pairs={{4,0},{5,1},{6,2},{7,3},{8,4},{9,5},{10,6},{11,7},{12,8},{13,9},{1... | collective-permute-start | bytes 786440 | tf_op jit(solution)/shard_map/ppermute | solution.py:185
  (9 other events, 40.1 us)

commit v6 on v5

--- a/solution.py
+++ b/solution.py
@@ -231,28 +231,20 @@
     side = jnp.concatenate([weight_hi, weight_lo], axis=1)
     side_width = -(-side.shape[1] // 128) * 128
     side = jnp.pad(side, ((0, 0), (0, side_width - side.shape[1])))
-    payload = jnp.concatenate(
-        [centroid.astype(jnp.bfloat16), grad_sum.astype(jnp.bfloat16), side], axis=1
-    )
+    payload = jnp.concatenate([centroid.astype(jnp.bfloat16), side], axis=1)
     gathered = topo_all_gather(payload, experts)
+    grad_all = topo_all_gather(grad_sum.astype(jnp.bfloat16), experts)
     cent_all = gathered[:, :model_width]
-    grad_all = gathered[:, model_width : 2 * model_width]
-    side_all = gathered[:, 2 * model_width : 2 * model_width + 2 * experts].astype(jnp.float32)
+    side_all = gathered[:, model_width : model_width + 2 * experts].astype(jnp.float32)
     column = jnp.arange(experts, dtype=jnp.int32)[None, :]
     mine = jnp.sum(jnp.where(column == me, side_all[:, :experts] + side_all[:, experts:], 0.0), axis=1)
     output, input_grad = expert_dense(
         cent_all, grad_all, gate_weight[0], up_weight[0], down_weight[0]
     )
-    parts = jnp.concatenate(
-        [
-            (mine[:, None] * output.astype(jnp.float32)).astype(jnp.bfloat16),
-            (mine[:, None] * input_grad.astype(jnp.float32)).astype(jnp.bfloat16),
-        ],
-        axis=1,
-    )
-    summed = topo_reduce_scatter(parts, experts)
-    combined = summed[:, :model_width]
-    centroid_grad = summed[:, model_width:] - grad_sum
+    weighted_out = (mine[:, None] * output.astype(jnp.float32)).astype(jnp.bfloat16)
+    weighted_grad = (mine[:, None] * input_grad.astype(jnp.float32)).astype(jnp.bfloat16)
+    combined = topo_reduce_scatter(weighted_out, experts)
+    centroid_grad = topo_reduce_scatter(weighted_grad, experts) - grad_sum
     layer_out = tokens.astype(jnp.float32) + jnp.take(combined - centroid, cluster_ids, axis=0)
     token_grad = out_grad.astype(jnp.float32) + jnp.take(
         centroid_grad / counts[:, None], cluster_ids, axis=0

time: 145 us -> 182 us (1.26)
  starting transfers between devices: 60.1 us -> 100 us
  waiting for transfers between devices: 31.6 us -> 21.6 us
  other arithmetic: 21.1 us -> 26.2 us
    ppermute x7 -> x14, starting transfers between devices: 11.1 us -> 22.5 us  [row_sum(): got = lax.ppermute(theirs.astype(jnp.bfloat16), 'expert', pairs)]
    ppermute x3 -> x6, waiting for transfers between devices: 8.12 us -> 0.18 us  [topo_reduce_scatter(): lax.ppermute(ahead.astype(jnp.bfloat16), 'expert', [(j, j + 4) for j in r...]
    ppermute x3 -> x6, starting transfers between devices: 8.94 us -> 16.7 us  [topo_all_gather(): there.append((lax.ppermute(behind, 'expert', behind_row), line + step))]
    ppermute x3 -> x6, starting transfers between devices: 9.04 us -> 14.7 us  [topo_all_gather(): lax.ppermute(ahead, 'expert', [(j, j + 4) for j in range(experts) if step...]
    ppermute x3 -> x6, waiting for transfers between devices: 4.41 us -> 0.02 us  [topo_reduce_scatter(): lax.ppermute(behind.astype(jnp.bfloat16), 'expert', [(j, j - 4) for j in...]
    ppermute x3 -> x6, starting transfers between devices: 20.1 us -> 24.1 us  [topo_reduce_scatter(): lax.ppermute(ahead.astype(jnp.bfloat16), 'expert', [(j, j + 4) for j in r...]
    ppermute x3 -> x6, starting transfers between devices: 3.85 us -> 7.71 us  [topo_all_gather(): lax.ppermute(behind, 'expert', [(j, j - 4) for j in range(experts) if 1 <...]
    ppermute x7 -> x14, waiting for transfers between devices: 3.32 us -> 6.91 us  [row_sum(): got = lax.ppermute(theirs.astype(jnp.bfloat16), 'expert', pairs)]
  transfers between devices with their start and end apart: 29 -> 58, of which waited for: 10 -> 8; matrix products, arithmetic and copies ran while one was open for 6% -> 17% of each run, Pallas kernels for 0% -> 0%
where the time goes in v6:
time: 182 us; the launch traced here: 180 us
  starting transfers between devices  100 us (55%)
  other arithmetic  26.2 us (14%)
  waiting for transfers between devices  21.6 us (12%)
  matrix products  19.6 us (11%)
  local copies, waits for them, and re-layouts  10.5 us (6%)
  between operations  1.85 us (1%)
    ppermute x6, starting transfers between devices, topo_reduce_scatter(): lax.ppermute(ahead.astype(jnp.bfloat16), 'expert', [(j, j + 4) for j in r...  24.1 us
    ppermute x14, starting transfers between devices, row_sum(): got = lax.ppermute(theirs.astype(jnp.bfloat16), 'expert', pairs)  22.5 us
    ppermute x6, starting transfers between devices, topo_all_gather(): there.append((lax.ppermute(behind, 'expert', behind_row), line + step))  16.7 us
    ppermute x6, starting transfers between devices, topo_all_gather(): lax.ppermute(ahead, 'expert', [(j, j + 4) for j in range(experts) if step...  14.7 us
    ppermute x6, waiting for transfers between devices, topo_all_gather(): lax.ppermute(behind, 'expert', [(j, j - 4) for j in range(experts) if 1 <...  10.4 us
    ppermute x6, starting transfers between devices, topo_all_gather(): lax.ppermute(behind, 'expert', [(j, j - 4) for j in range(experts) if 1 <...  7.71 us
    ppermute x14, waiting for transfers between devices, row_sum(): got = lax.ppermute(theirs.astype(jnp.bfloat16), 'expert', pairs)  6.91 us
    another operation x4, other arithmetic, topo_all_gather(): jnp.stack([pick(in_row, [column, across]), pick(in_row, [across, column])...  6.68 us
  transfers between devices with their start and end apart: 58, of which 8 were waited for; matrix products, arithmetic and copies ran while one was open for 17% of the time, Pallas kernels for 0%

profile of v6, /device:TPU:0, one launch (start us, length us, event | category | flops | bytes accessed | tf_op | source)
XLA Modules:
  0.0 179.8 jit_solution(16000077106260658102)
XLA Ops:
  0.6 2.1 %fusion.80 = (bf16[32,2048]{1,0:T(8,128)(2,1)S(1)}, f32[32,2048]{1,0:T(8,128)}) fusion(bf16[128,2048]{1,0:T(8,128)(2,1)} %param.11, s32[128]{0:T(128)} %param.12), kind=kOutput, calls=%fused_computation.169 | convolution fusion | flops 16846848 | bytes 918016 | tf_op jit(solution)/shard_map/dot_general | solution.py:224
  2.8 5.6 %collective-permute-start.32 = (bf16[32,2048]{1,0:T(8,128)(2,1)S(1)}, bf16[32,2048]{1,0:T(8,128)(2,1)}, u32[]{:S(2)}, u32[]{:S(2)}) collective-permute-start(bf16[32,2048]{1,0:T(8,128)(2,1)S(1)} %get-tuple-element.41), channel_id=1, source_target_pairs={{0,4},{1,5},{2,6},{3,7},{4,8},{5,9},{6,10},{7,11},{8,12},{9,13},{1... | collective-permute-start | bytes 393224 | tf_op jit(solution)/shard_map/ppermute | solution.py:120
  14.8 4.6 %collective-permute-start.3 = (bf16[32,2176]{1,0:T(8,128)(2,1)S(1)}, bf16[32,2176]{1,0:T(8,128)(2,1)S(1)}, u32[]{:S(2)}, u32[]{:S(2)}) collective-permute-start(bf16[32,2176]{1,0:T(8,128)(2,1)S(1)} %fusion.56), channel_id=1, source_target_pairs={{0,4},{1,5},{2,6},{3,7},{4,8},{5,9},{6,10},{7,11},{8,12},{9,13},{1... | collective-permute-start | bytes 417800 | tf_op jit(solution)/shard_map/ppermute | solution.py:120
  31.8 3.8 %collective-permute-done.30 = bf16[32,2048]{1,0:T(8,128)(2,1)} collective-permute-done((bf16[32,2048]{1,0:T(8,128)(2,1)}, bf16[32,2048]{1,0:T(8,128)(2,1)}, u32[]{:S(2)}, u32[]{:S(2)}) %collective-permute-start.30) | collective-permute-done | bytes 131104 | tf_op jit(solution)/shard_map/ppermute | solution.py:125
  39.3 5.8 %collective-permute-done.1 = bf16[32,2176]{1,0:T(8,128)(2,1)} collective-permute-done((bf16[32,2176]{1,0:T(8,128)(2,1)}, bf16[32,2176]{1,0:T(8,128)(2,1)}, u32[]{:S(2)}, u32[]{:S(2)}) %collective-permute-start.1) | collective-permute-done | bytes 139296 | tf_op jit(solution)/shard_map/ppermute | solution.py:125
  45.1 2.4 %collective-permute-start.39 = (bf16[32,2048]{1,0:T(8,128)(2,1)}, bf16[32,2048]{1,0:T(8,128)(2,1)S(1)}, u32[]{:S(2)}, u32[]{:S(2)}) collective-permute-start(bf16[32,2048]{1,0:T(8,128)(2,1)} %collective-permute-done.29), channel_id=1, source_target_pairs={{0,2},{1,3},{2,0},{3,1},{4,6},{5,7},{6,4},{7,5},{8,10},{9,11},{10,... | collective-permute-start | bytes 393224 | tf_op jit(solution)/shard_map/ppermute | solution.py:135
  51.8 3.4 %collective-permute-start.37 = (bf16[32,2048]{1,0:T(8,128)(2,1)}, bf16[32,2048]{1,0:T(8,128)(2,1)S(1)}, u32[]{:S(2)}, u32[]{:S(2)}) collective-permute-start(bf16[32,2048]{1,0:T(8,128)(2,1)} %collective-permute-done.30), channel_id=1, source_target_pairs={{0,2},{1,3},{2,0},{3,1},{4,6},{5,7},{6,4},{7,5},{16,18},{17,19},{1... | collective-permute-start | bytes 393224 | tf_op jit(solution)/shard_map/ppermute | solution.py:135
  56.7 2.4 %collective-permute-start.35 = (bf16[32,2048]{1,0:T(8,128)(2,1)}, bf16[32,2048]{1,0:T(8,128)(2,1)S(1)}, u32[]{:S(2)}, u32[]{:S(2)}) collective-permute-start(bf16[32,2048]{1,0:T(8,128)(2,1)} %collective-permute-done.31), channel_id=1, source_target_pairs={{0,2},{1,3},{2,0},{3,1},{16,18},{17,19},{18,16},{19,17}} | collective-permute-start | bytes 393224 | tf_op jit(solution)/shard_map/ppermute | solution.py:135
  62.8 2.4 %collective-permute-start.10 = (bf16[32,2176]{1,0:T(8,128)(2,1)}, bf16[32,2176]{1,0:T(8,128)(2,1)S(1)}, u32[]{:S(2)}, u32[]{:S(2)}) collective-permute-start(bf16[32,2176]{1,0:T(8,128)(2,1)} %collective-permute-done), channel_id=1, source_target_pairs={{0,2},{1,3},{2,0},{3,1},{4,6},{5,7},{6,4},{7,5},{8,10},{9,11},{10,... | collective-permute-start | bytes 417800 | tf_op jit(solution)/shard_map/ppermute | solution.py:135
  65.9 3.4 %collective-permute-start.8 = (bf16[32,2176]{1,0:T(8,128)(2,1)}, bf16[32,2176]{1,0:T(8,128)(2,1)S(1)}, u32[]{:S(2)}, u32[]{:S(2)}) collective-permute-start(bf16[32,2176]{1,0:T(8,128)(2,1)} %collective-permute-done.1), channel_id=1, source_target_pairs={{0,2},{1,3},{2,0},{3,1},{4,6},{5,7},{6,4},{7,5},{16,18},{17,19},{1... | collective-permute-start | bytes 417800 | tf_op jit(solution)/shard_map/ppermute | solution.py:135
  73.6 2.6 %collective-permute-start.6 = (bf16[32,2176]{1,0:T(8,128)(2,1)S(1)}, bf16[32,2176]{1,0:T(8,128)(2,1)S(1)}, u32[]{:S(2)}, u32[]{:S(2)}) collective-permute-start(bf16[32,2176]{1,0:T(8,128)(2,1)S(1)} %collective-permute-done.2), channel_id=1, source_target_pairs={{0,2},{1,3},{2,0},{3,1},{16,18},{17,19},{18,16},{19,17}} | collective-permute-start | bytes 417800 | tf_op jit(solution)/shard_map/ppermute | solution.py:135
  78.0 2.5 %collective-permute-done.6 = bf16[32,2176]{1,0:T(8,128)(2,1)S(1)} collective-permute-done((bf16[32,2176]{1,0:T(8,128)(2,1)S(1)}, bf16[32,2176]{1,0:T(8,128)(2,1)S(1)}, u32[]{:S(2)}, u32[]{:S(2)}) %collective-permute-start.6) | collective-permute-done | bytes 139296 | tf_op jit(solution)/shard_map/ppermute | solution.py:135
  86.6 3.0 %fusion = f32[512,768]{1,0:T(8,128)} fusion(bf16[512,2048]{1,0:T(8,128)(2,1)S(1)} %bitcast.207, bf16[1,768,2048]{2,1,0:T(8,128)(2,1)S(1)} %copy-done.18), kind=kOutput, calls=%fused_computation.5 | convolution fusion | flops 1610612736 | bytes 6815744 | tf_op jit(solution)/shard_map/dot_general | solution.py:200
  92.9 3.0 %fusion.10 = f32[512,768]{1,0:T(8,128)} fusion(bf16[1,2048,768]{2,1,0:T(8,128)(2,1)S(1)} %copy-done.16, bf16[512,2176]{1,0:T(8,128)(2,1)S(1)} %bitcast.205), kind=kOutput, calls=%fused_computation.15 | convolution fusion | flops 1610612736 | bytes 6815744 | tf_op jit(solution)/shard_map/dot_general | solution.py:195
  96.1 3.5 %fusion.6 = f32[512,768]{1,0:T(8,128)S(1)} fusion(bf16[1,2048,768]{2,1,0:T(8,128)(2,1)S(1)} %copy-done, bf16[512,2176]{1,0:T(8,128)(2,1)} %bitcast.206), kind=kOutput, calls=%fused_computation.11 | convolution fusion | flops 1610612736 | bytes 6815744 | tf_op jit(solution)/shard_map/dot_general | solution.py:196
  101.6 2.3 %multiply_convert_fusion = bf16[512,2048]{1,0:T(8,128)(2,1)S(1)} fusion(f32[512,2048]{1,0:T(8,128)S(1)} %fusion.4, bf16[1,2048,768]{2,1,0:T(8,128)(2,1)S(1)} %copy-done.17, f32[512]{0:T(512)S(1)} %fusion.72, f32[512,768]{1,0:T(8,128)S(1)} %copy-done.21, f32[512,768]{1,0:T(8,128)S(1)} %copy-done.20, f32[512,768]{1,0:T(8,128)S(1)} %fusion.6), kind=kOutput, calls=%fused_computation.2 | convolution fusion | flops 1619787776 | bytes 14157824 | tf_op jit(solution)/shard_map/dot_general | solution.py:205
  111.7 2.4 %collective-permute-start.50 = (bf16[32,2048]{1,0:T(8,128)(2,1)S(1)}, bf16[32,2048]{1,0:T(8,128)(2,1)S(1)}, u32[]{:S(2)}, u32[]{:S(2)}) collective-permute-start(bf16[32,2048]{1,0:T(8,128)(2,1)S(1)} %get-tuple-element.29), channel_id=1, source_target_pairs={{0,2},{1,3},{2,0},{3,1},{4,6},{5,7},{6,4},{7,5},{8,10},{9,11},{10,... | collective-permute-start | bytes 393224 | tf_op jit(solution)/shard_map/ppermute | solution.py:170
  114.1 3.4 %collective-permute-start.48 = (bf16[32,2048]{1,0:T(8,128)(2,1)S(1)}, bf16[32,2048]{1,0:T(8,128)(2,1)S(1)}, u32[]{:S(2)}, u32[]{:S(2)}) collective-permute-start(bf16[32,2048]{1,0:T(8,128)(2,1)S(1)} %get-tuple-element.30), channel_id=1, source_target_pairs={{0,2},{1,3},{2,0},{3,1},{4,6},{5,7},{6,4},{7,5},{16,18},{17,19},{1... | collective-permute-start | bytes 393224 | tf_op jit(solution)/shard_map/ppermute | solution.py:170
  117.6 2.4 %collective-permute-start.46 = (bf16[32,2048]{1,0:T(8,128)(2,1)S(1)}, bf16[32,2048]{1,0:T(8,128)(2,1)S(1)}, u32[]{:S(2)}, u32[]{:S(2)}) collective-permute-start(bf16[32,2048]{1,0:T(8,128)(2,1)S(1)} %get-tuple-element.31), channel_id=1, source_target_pairs={{0,2},{1,3},{2,0},{3,1},{16,18},{17,19},{18,16},{19,17}} | collective-permute-start | bytes 393224 | tf_op jit(solution)/shard_map/ppermute | solution.py:170
  121.5 3.5 %collective-permute-done.46 = bf16[32,2048]{1,0:T(8,128)(2,1)S(1)} collective-permute-done((bf16[32,2048]{1,0:T(8,128)(2,1)S(1)}, bf16[32,2048]{1,0:T(8,128)(2,1)S(1)}, u32[]{:S(2)}, u32[]{:S(2)}) %collective-permute-start.46) | collective-permute-done | bytes 131104 | tf_op jit(solution)/shard_map/ppermute | solution.py:170
  125.0 2.8 %collective-permute-start.17 = (bf16[32,2048]{1,0:T(8,128)(2,1)S(1)}, bf16[32,2048]{1,0:T(8,128)(2,1)S(1)}, u32[]{:S(2)}, u32[]{:S(2)}) collective-permute-start(bf16[32,2048]{1,0:T(8,128)(2,1)S(1)} %get-tuple-element.38), channel_id=1, source_target_pairs={{0,2},{1,3},{2,0},{3,1},{16,18},{17,19},{18,16},{19,17}} | collective-permute-start | bytes 393224 | tf_op jit(solution)/shard_map/ppermute | solution.py:170
  128.5 3.3 %collective-permute-done.17 = bf16[32,2048]{1,0:T(8,128)(2,1)S(1)} collective-permute-done((bf16[32,2048]{1,0:T(8,128)(2,1)S(1)}, bf16[32,2048]{1,0:T(8,128)(2,1)S(1)}, u32[]{:S(2)}, u32[]{:S(2)}) %collective-permute-start.17) | collective-permute-done | bytes 131104 | tf_op jit(solution)/shard_map/ppermute | solution.py:170
  133.9 2.8 %collective-permute-start.19 = (bf16[32,2048]{1,0:T(8,128)(2,1)S(1)}, bf16[32,2048]{1,0:T(8,128)(2,1)S(1)}, u32[]{:S(2)}, u32[]{:S(2)}) collective-permute-start(bf16[32,2048]{1,0:T(8,128)(2,1)S(1)} %get-tuple-element.37), channel_id=1, source_target_pairs={{0,2},{1,3},{2,0},{3,1},{4,6},{5,7},{6,4},{7,5},{16,18},{17,19},{1... | collective-permute-start | bytes 393224 | tf_op jit(solution)/shard_map/ppermute | solution.py:170
  137.4 2.6 %collective-permute-start.18 = (bf16[32,2048]{1,0:T(8,128)(2,1)S(1)}, bf16[32,2048]{1,0:T(8,128)(2,1)S(1)}, u32[]{:S(2)}, u32[]{:S(2)}) collective-permute-start(bf16[32,2048]{1,0:T(8,128)(2,1)S(1)} %get-tuple-element.23), channel_id=1, source_target_pairs={{0,4},{1,5},{2,6},{3,7},{16,20},{17,21},{18,22},{19,23}} | collective-permute-start | bytes 393224 | tf_op jit(solution)/shard_map/ppermute | solution.py:178
  142.5 4.3 %collective-permute-start.49 = (bf16[32,2048]{1,0:T(8,128)(2,1)S(1)}, bf16[32,2048]{1,0:T(8,128)(2,1)S(1)}, u32[]{:S(2)}, u32[]{:S(2)}) collective-permute-start(bf16[32,2048]{1,0:T(8,128)(2,1)S(1)} %get-tuple-element.13), channel_id=1, source_target_pairs={{0,4},{1,5},{2,6},{3,7},{4,8},{5,9},{6,10},{7,11},{16,20},{17,21},... | collective-permute-start | bytes 393224 | tf_op jit(solution)/shard_map/ppermute | solution.py:178
  147.6 2.8 %collective-permute-start.21 = (bf16[32,2048]{1,0:T(8,128)(2,1)S(1)}, bf16[32,2048]{1,0:T(8,128)(2,1)S(1)}, u32[]{:S(2)}, u32[]{:S(2)}) collective-permute-start(bf16[32,2048]{1,0:T(8,128)(2,1)S(1)} %get-tuple-element.36), channel_id=1, source_target_pairs={{0,2},{1,3},{2,0},{3,1},{4,6},{5,7},{6,4},{7,5},{8,10},{9,11},{10,... | collective-permute-start | bytes 393224 | tf_op jit(solution)/shard_map/ppermute | solution.py:170
  151.1 5.0 %collective-permute-start.20 = (bf16[32,2048]{1,0:T(8,128)(2,1)S(1)}, bf16[32,2048]{1,0:T(8,128)(2,1)S(1)}, u32[]{:S(2)}, u32[]{:S(2)}) collective-permute-start(bf16[32,2048]{1,0:T(8,128)(2,1)S(1)} %get-tuple-element.21), channel_id=1, source_target_pairs={{0,4},{1,5},{2,6},{3,7},{4,8},{5,9},{6,10},{7,11},{16,20},{17,21},... | collective-permute-start | bytes 393224 | tf_op jit(solution)/shard_map/ppermute | solution.py:178
  159.1 5.8 %collective-permute-start.51 = (bf16[32,2048]{1,0:T(8,128)(2,1)S(1)}, bf16[32,2048]{1,0:T(8,128)(2,1)S(1)}, u32[]{:S(2)}, u32[]{:S(2)}) collective-permute-start(bf16[32,2048]{1,0:T(8,128)(2,1)S(1)} %get-tuple-element.11), channel_id=1, source_target_pairs={{0,4},{1,5},{2,6},{3,7},{4,8},{5,9},{6,10},{7,11},{8,12},{9,13},{1... | collective-permute-start | bytes 393224 | tf_op jit(solution)/shard_map/ppermute | solution.py:178
  166.3 5.2 %collective-permute-start.22 = (bf16[32,2048]{1,0:T(8,128)(2,1)S(1)}, bf16[32,2048]{1,0:T(8,128)(2,1)S(1)}, u32[]{:S(2)}, u32[]{:S(2)}) collective-permute-start(bf16[32,2048]{1,0:T(8,128)(2,1)S(1)} %get-tuple-element.19), channel_id=1, source_target_pairs={{0,4},{1,5},{2,6},{3,7},{4,8},{5,9},{6,10},{7,11},{8,12},{9,13},{1... | collective-permute-start | bytes 393224 | tf_op jit(solution)/shard_map/ppermute | solution.py:178
  171.7 2.2 %gather_fusion.1 = f32[128,2048]{1,0:T(8,128)} fusion(f32[32,2048]{1,0:T(8,128)S(1)} %fusion.42, s32[1024]{0:T(1024)} %pad_clamp_fusion), kind=kCustom, calls=%fused_computation.1.clone | custom fusion | bytes 2097664 | tf_op jit(solution)/shard_map/jit(_take)/gather | solution.py:249
  174.1 2.2 %gather_fusion = f32[128,2048]{1,0:T(8,128)} fusion(f32[32,2048]{1,0:T(8,128)S(1)} %fusion.55, s32[1024]{0:T(1024)} %pad_clamp_fusion), kind=kCustom, calls=%fused_computation.clone | custom fusion | bytes 2097664 | tf_op jit(solution)/shard_map/jit(_take)/gather | solution.py:248
  176.3 3.6 %select_add_fusion = (f32[128,2048]{1,0:T(8,128)}, f32[128,2048]{1,0:T(8,128)}) fusion(f32[128,2048]{1,0:T(8,128)} %gather_fusion.1, bf16[128,2048]{1,0:T(8,128)(2,1)} %param.11, pred[128]{0:T(512)(128)(4,1)S(1)} %copy-done.15, f32[128,2048]{1,0:T(8,128)} %gather_fusion, bf16[128,2048]{1,0:T(8,128)(2,1)} %param.10), kind=kLoop, calls=%fused_computation.39 | loop fusion | flops 1572864 | bytes 5243008 | tf_op jit(solution)/shard_map/add | solution.py:249
  (191 shorter events, 71.0 us)
Async XLA Ops:
  2.8 21.4 %collective-permute-start.32 = (bf16[32,2048]{1,0:T(8,128)(2,1)S(1)}, bf16[32,2048]{1,0:T(8,128)(2,1)}, u32[]{:S(2)}, u32[]{:S(2)}) collective-permute-start(bf16[32,2048]{1,0:T(8,128)(2,1)S(1)} %get-tuple-element.41), channel_id=1, source_target_pairs={{0,4},{1,5},{2,6},{3,7},{4,8},{5,9},{6,10},{7,11},{8,12},{9,13},{1... | collective-permute-start | bytes 393224 | tf_op jit(solution)/shard_map/ppermute | solution.py:120
  8.3 17.1 %collective-permute-start.29 = (bf16[32,2048]{1,0:T(8,128)(2,1)S(1)}, bf16[32,2048]{1,0:T(8,128)(2,1)}, u32[]{:S(2)}, u32[]{:S(2)}) collective-permute-start(bf16[32,2048]{1,0:T(8,128)(2,1)S(1)} %get-tuple-element.41), channel_id=1, source_target_pairs={{4,0},{5,1},{6,2},{7,3},{8,4},{9,5},{10,6},{11,7},{12,8},{13,9},{1... | collective-permute-start | bytes 393224 | tf_op jit(solution)/shard_map/ppermute | solution.py:125
  9.6 41.5 %collective-permute-start.41 = (bf16[32,2048]{1,0:T(8,128)(2,1)S(1)}, bf16[32,2048]{1,0:T(8,128)(2,1)}, u32[]{:S(2)}, u32[]{:S(2)}) collective-permute-start(bf16[32,2048]{1,0:T(8,128)(2,1)S(1)} %get-tuple-element.41), channel_id=1, source_target_pairs={{0,2},{1,3},{2,0},{3,1},{4,6},{5,7},{6,4},{7,5},{8,10},{9,11},{10,... | collective-permute-start | bytes 393224 | tf_op jit(solution)/shard_map/ppermute | solution.py:117
  14.8 13.1 %collective-permute-start.3 = (bf16[32,2176]{1,0:T(8,128)(2,1)S(1)}, bf16[32,2176]{1,0:T(8,128)(2,1)S(1)}, u32[]{:S(2)}, u32[]{:S(2)}) collective-permute-start(bf16[32,2176]{1,0:T(8,128)(2,1)S(1)} %fusion.56), channel_id=1, source_target_pairs={{0,4},{1,5},{2,6},{3,7},{4,8},{5,9},{6,10},{7,11},{8,12},{9,13},{1... | collective-permute-start | bytes 417800 | tf_op jit(solution)/shard_map/ppermute | solution.py:120
  19.4 9.8 %collective-permute-start = (bf16[32,2176]{1,0:T(8,128)(2,1)S(1)}, bf16[32,2176]{1,0:T(8,128)(2,1)}, u32[]{:S(2)}, u32[]{:S(2)}) collective-permute-start(bf16[32,2176]{1,0:T(8,128)(2,1)S(1)} %fusion.56), channel_id=1, source_target_pairs={{4,0},{5,1},{6,2},{7,3},{8,4},{9,5},{10,6},{11,7},{12,8},{13,9},{1... | collective-permute-start | bytes 417800 | tf_op jit(solution)/shard_map/ppermute | solution.py:125
  25.5 10.1 %collective-permute-start.30 = (bf16[32,2048]{1,0:T(8,128)(2,1)}, bf16[32,2048]{1,0:T(8,128)(2,1)}, u32[]{:S(2)}, u32[]{:S(2)}) collective-permute-start(bf16[32,2048]{1,0:T(8,128)(2,1)} %collective-permute-done.29), channel_id=1, source_target_pairs={{4,0},{5,1},{6,2},{7,3},{8,4},{9,5},{10,6},{11,7},{20,16},{21,17},... | collective-permute-start | bytes 393224 | tf_op jit(solution)/shard_map/ppermute | solution.py:125
  27.9 10.8 %collective-permute-start.4 = (bf16[32,2176]{1,0:T(8,128)(2,1)S(1)}, bf16[32,2176]{1,0:T(8,128)(2,1)}, u32[]{:S(2)}, u32[]{:S(2)}) collective-permute-start(bf16[32,2176]{1,0:T(8,128)(2,1)S(1)} %collective-permute-done.3), channel_id=1, source_target_pairs={{4,8},{5,9},{6,10},{7,11},{8,12},{9,13},{10,14},{11,15},{20,24},{2... | collective-permute-start | bytes 417800 | tf_op jit(solution)/shard_map/ppermute | solution.py:120
  29.2 15.9 %collective-permute-start.1 = (bf16[32,2176]{1,0:T(8,128)(2,1)}, bf16[32,2176]{1,0:T(8,128)(2,1)}, u32[]{:S(2)}, u32[]{:S(2)}) collective-permute-start(bf16[32,2176]{1,0:T(8,128)(2,1)} %collective-permute-done), channel_id=1, source_target_pairs={{4,0},{5,1},{6,2},{7,3},{8,4},{9,5},{10,6},{11,7},{20,16},{21,17},... | collective-permute-start | bytes 417800 | tf_op jit(solution)/shard_map/ppermute | solution.py:125
  30.5 17.1 %collective-permute-start.34 = (bf16[32,2048]{1,0:T(8,128)(2,1)}, bf16[32,2048]{1,0:T(8,128)(2,1)}, u32[]{:S(2)}, u32[]{:S(2)}) collective-permute-start(bf16[32,2048]{1,0:T(8,128)(2,1)} %collective-permute-done.33), channel_id=1, source_target_pairs={{8,12},{9,13},{10,14},{11,15},{24,28},{25,29},{26,30},{27,31}} | collective-permute-start | bytes 393224 | tf_op jit(solution)/shard_map/ppermute | solution.py:120
  35.6 12.7 %collective-permute-start.31 = (bf16[32,2048]{1,0:T(8,128)(2,1)}, bf16[32,2048]{1,0:T(8,128)(2,1)}, u32[]{:S(2)}, u32[]{:S(2)}) collective-permute-start(bf16[32,2048]{1,0:T(8,128)(2,1)} %collective-permute-done.30), channel_id=1, source_target_pairs={{4,0},{5,1},{6,2},{7,3},{20,16},{21,17},{22,18},{23,19}} | collective-permute-start | bytes 393224 | tf_op jit(solution)/shard_map/ppermute | solution.py:125
  38.6 13.1 %collective-permute-start.40 = (bf16[32,2048]{1,0:T(8,128)(2,1)}, bf16[32,2048]{1,0:T(8,128)(2,1)S(1)}, u32[]{:S(2)}, u32[]{:S(2)}) collective-permute-start(bf16[32,2048]{1,0:T(8,128)(2,1)} %collective-permute-done.32), channel_id=1, source_target_pairs={{4,6},{5,7},{6,4},{7,5},{8,10},{9,11},{10,8},{11,9},{12,14},{13,15... | collective-permute-start | bytes 393224 | tf_op jit(solution)/shard_map/ppermute | solution.py:134
  45.1 15.4 %collective-permute-start.39 = (bf16[32,2048]{1,0:T(8,128)(2,1)}, bf16[32,2048]{1,0:T(8,128)(2,1)S(1)}, u32[]{:S(2)}, u32[]{:S(2)}) collective-permute-start(bf16[32,2048]{1,0:T(8,128)(2,1)} %collective-permute-done.29), channel_id=1, source_target_pairs={{0,2},{1,3},{2,0},{3,1},{4,6},{5,7},{6,4},{7,5},{8,10},{9,11},{10,... | collective-permute-start | bytes 393224 | tf_op jit(solution)/shard_map/ppermute | solution.py:135
  51.1 11.0 %collective-permute-start.38 = (bf16[32,2048]{1,0:T(8,128)(2,1)}, bf16[32,2048]{1,0:T(8,128)(2,1)S(1)}, u32[]{:S(2)}, u32[]{:S(2)}) collective-permute-start(bf16[32,2048]{1,0:T(8,128)(2,1)} %collective-permute-done.33), channel_id=1, source_target_pairs={{8,10},{9,11},{10,8},{11,9},{12,14},{13,15},{14,12},{15,13},{24,26... | collective-permute-start | bytes 393224 | tf_op jit(solution)/shard_map/ppermute | solution.py:134
  51.8 11.0 %collective-permute-start.37 = (bf16[32,2048]{1,0:T(8,128)(2,1)}, bf16[32,2048]{1,0:T(8,128)(2,1)S(1)}, u32[]{:S(2)}, u32[]{:S(2)}) collective-permute-start(bf16[32,2048]{1,0:T(8,128)(2,1)} %collective-permute-done.30), channel_id=1, source_target_pairs={{0,2},{1,3},{2,0},{3,1},{4,6},{5,7},{6,4},{7,5},{16,18},{17,19},{1... | collective-permute-start | bytes 393224 | tf_op jit(solution)/shard_map/ppermute | solution.py:135
  55.2 10.0 %collective-permute-start.36 = (bf16[32,2048]{1,0:T(8,128)(2,1)}, bf16[32,2048]{1,0:T(8,128)(2,1)S(1)}, u32[]{:S(2)}, u32[]{:S(2)}) collective-permute-start(bf16[32,2048]{1,0:T(8,128)(2,1)} %collective-permute-done.34), channel_id=1, source_target_pairs={{12,14},{13,15},{14,12},{15,13},{28,30},{29,31},{30,28},{31,29}} | collective-permute-start | bytes 393224 | tf_op jit(solution)/shard_map/ppermute | solution.py:134
  56.7 9.2 %collective-permute-start.35 = (bf16[32,2048]{1,0:T(8,128)(2,1)}, bf16[32,2048]{1,0:T(8,128)(2,1)S(1)}, u32[]{:S(2)}, u32[]{:S(2)}) collective-permute-start(bf16[32,2048]{1,0:T(8,128)(2,1)} %collective-permute-done.31), channel_id=1, source_target_pairs={{0,2},{1,3},{2,0},{3,1},{16,18},{17,19},{18,16},{19,17}} | collective-permute-start | bytes 393224 | tf_op jit(solution)/shard_map/ppermute | solution.py:135
  60.5 12.3 %collective-permute-start.12 = (bf16[32,2176]{1,0:T(8,128)(2,1)S(1)}, bf16[32,2176]{1,0:T(8,128)(2,1)S(1)}, u32[]{:S(2)}, u32[]{:S(2)}) collective-permute-start(bf16[32,2176]{1,0:T(8,128)(2,1)S(1)} %fusion.56), channel_id=1, source_target_pairs={{0,2},{1,3},{2,0},{3,1},{4,6},{5,7},{6,4},{7,5},{8,10},{9,11},{10,... | collective-permute-start | bytes 417800 | tf_op jit(solution)/shard_map/ppermute | solution.py:117
  62.1 11.4 %collective-permute-start.11 = (bf16[32,2176]{1,0:T(8,128)(2,1)S(1)}, bf16[32,2176]{1,0:T(8,128)(2,1)S(1)}, u32[]{:S(2)}, u32[]{:S(2)}) collective-permute-start(bf16[32,2176]{1,0:T(8,128)(2,1)S(1)} %collective-permute-done.3), channel_id=1, source_target_pairs={{4,6},{5,7},{6,4},{7,5},{8,10},{9,11},{10,8},{11,9},{12,14},{13,15... | collective-permute-start | bytes 417800 | tf_op jit(solution)/shard_map/ppermute | solution.py:134
  62.8 14.6 %collective-permute-start.10 = (bf16[32,2176]{1,0:T(8,128)(2,1)}, bf16[32,2176]{1,0:T(8,128)(2,1)S(1)}, u32[]{:S(2)}, u32[]{:S(2)}) collective-permute-start(bf16[32,2176]{1,0:T(8,128)(2,1)} %collective-permute-done), channel_id=1, source_target_pairs={{0,2},{1,3},{2,0},{3,1},{4,6},{5,7},{6,4},{7,5},{8,10},{9,11},{10,... | collective-permute-start | bytes 417800 | tf_op jit(solution)/shard_map/ppermute | solution.py:135
  65.2 12.2 %collective-permute-start.9 = (bf16[32,2176]{1,0:T(8,128)(2,1)}, bf16[32,2176]{1,0:T(8,128)(2,1)S(1)}, u32[]{:S(2)}, u32[]{:S(2)}) collective-permute-start(bf16[32,2176]{1,0:T(8,128)(2,1)} %collective-permute-done.4), channel_id=1, source_target_pairs={{8,10},{9,11},{10,8},{11,9},{12,14},{13,15},{14,12},{15,13},{24,26... | collective-permute-start | bytes 417800 | tf_op jit(solution)/shard_map/ppermute | solution.py:134
  65.9 12.0 %collective-permute-start.8 = (bf16[32,2176]{1,0:T(8,128)(2,1)}, bf16[32,2176]{1,0:T(8,128)(2,1)S(1)}, u32[]{:S(2)}, u32[]{:S(2)}) collective-permute-start(bf16[32,2176]{1,0:T(8,128)(2,1)} %collective-permute-done.1), channel_id=1, source_target_pairs={{0,2},{1,3},{2,0},{3,1},{4,6},{5,7},{6,4},{7,5},{16,18},{17,19},{1... | collective-permute-start | bytes 417800 | tf_op jit(solution)/shard_map/ppermute | solution.py:135
  77.5 12.1 %collective-permute-start.13 = (bf16[4,32,2176]{2,1,0:T(8,128)(2,1)S(1)}, bf16[4,32,2176]{2,1,0:T(8,128)(2,1)S(1)}, u32[]{:S(2)}, u32[]{:S(2)}) collective-permute-start(bf16[4,32,2176]{2,1,0:T(8,128)(2,1)S(1)} %select_select_fusion.1), channel_id=1, source_target_pairs={{0,1},{1,0},{2,3},{3,2},{4,5},{5,4},{6,7},{7,6},{8,9},{9,8},{10,11... | collective-permute-start | bytes 1671176 | tf_op jit(solution)/shard_map/ppermute | solution.py:139
  111.7 35.9 %collective-permute-start.50 = (bf16[32,2048]{1,0:T(8,128)(2,1)S(1)}, bf16[32,2048]{1,0:T(8,128)(2,1)S(1)}, u32[]{:S(2)}, u32[]{:S(2)}) collective-permute-start(bf16[32,2048]{1,0:T(8,128)(2,1)S(1)} %get-tuple-element.29), channel_id=1, source_target_pairs={{0,2},{1,3},{2,0},{3,1},{4,6},{5,7},{6,4},{7,5},{8,10},{9,11},{10,... | collective-permute-start | bytes 393224 | tf_op jit(solution)/shard_map/ppermute | solution.py:170
  114.1 19.7 %collective-permute-start.48 = (bf16[32,2048]{1,0:T(8,128)(2,1)S(1)}, bf16[32,2048]{1,0:T(8,128)(2,1)S(1)}, u32[]{:S(2)}, u32[]{:S(2)}) collective-permute-start(bf16[32,2048]{1,0:T(8,128)(2,1)S(1)} %get-tuple-element.30), channel_id=1, source_target_pairs={{0,2},{1,3},{2,0},{3,1},{4,6},{5,7},{6,4},{7,5},{16,18},{17,19},{1... | collective-permute-start | bytes 393224 | tf_op jit(solution)/shard_map/ppermute | solution.py:170
  120.7 16.0 %collective-permute-start.54 = (bf16[32,2048]{1,0:T(8,128)(2,1)S(1)}, bf16[32,2048]{1,0:T(8,128)(2,1)S(1)}, u32[]{:S(2)}, u32[]{:S(2)}) collective-permute-start(bf16[32,2048]{1,0:T(8,128)(2,1)S(1)} %get-tuple-element.27), channel_id=1, source_target_pairs={{8,10},{9,11},{10,8},{11,9},{12,14},{13,15},{14,12},{15,13},{24,26... | collective-permute-start | bytes 393224 | tf_op jit(solution)/shard_map/ppermute | solution.py:170
  140.8 9.6 %collective-permute-start.56 = (bf16[32,2048]{1,0:T(8,128)(2,1)S(1)}, bf16[32,2048]{1,0:T(8,128)(2,1)S(1)}, u32[]{:S(2)}, u32[]{:S(2)}) collective-permute-start(bf16[32,2048]{1,0:T(8,128)(2,1)S(1)} %get-tuple-element.26), channel_id=1, source_target_pairs={{4,6},{5,7},{6,4},{7,5},{8,10},{9,11},{10,8},{11,9},{12,14},{13,15... | collective-permute-start | bytes 393224 | tf_op jit(solution)/shard_map/ppermute | solution.py:170
  141.6 24.7 %collective-permute-start.45 = (bf16[32,2048]{1,0:T(8,128)(2,1)S(1)}, bf16[32,2048]{1,0:T(8,128)(2,1)S(1)}, u32[]{:S(2)}, u32[]{:S(2)}) collective-permute-start(bf16[32,2048]{1,0:T(8,128)(2,1)S(1)} %get-tuple-element.25), channel_id=1, source_target_pairs={{0,2},{1,3},{2,0},{3,1},{4,6},{5,7},{6,4},{7,5},{8,10},{9,11},{10,... | collective-permute-start | bytes 393224 | tf_op jit(solution)/shard_map/ppermute | solution.py:170
  146.9 9.2 %collective-permute-start.55 = (bf16[32,2048]{1,0:T(8,128)(2,1)S(1)}, bf16[32,2048]{1,0:T(8,128)(2,1)S(1)}, u32[]{:S(2)}, u32[]{:S(2)}) collective-permute-start(bf16[32,2048]{1,0:T(8,128)(2,1)S(1)} %get-tuple-element.14), channel_id=1, source_target_pairs={{8,4},{9,5},{10,6},{11,7},{12,8},{13,9},{14,10},{15,11},{24,20},{2... | collective-permute-start | bytes 393224 | tf_op jit(solution)/shard_map/ppermute | solution.py:185
  147.6 9.2 %collective-permute-start.21 = (bf16[32,2048]{1,0:T(8,128)(2,1)S(1)}, bf16[32,2048]{1,0:T(8,128)(2,1)S(1)}, u32[]{:S(2)}, u32[]{:S(2)}) collective-permute-start(bf16[32,2048]{1,0:T(8,128)(2,1)S(1)} %get-tuple-element.36), channel_id=1, source_target_pairs={{0,2},{1,3},{2,0},{3,1},{4,6},{5,7},{6,4},{7,5},{8,10},{9,11},{10,... | collective-permute-start | bytes 393224 | tf_op jit(solution)/shard_map/ppermute | solution.py:170
  156.9 17.0 %collective-permute-start.16 = (bf16[32,2048]{1,0:T(8,128)(2,1)S(1)}, bf16[32,2048]{1,0:T(8,128)(2,1)S(1)}, u32[]{:S(2)}, u32[]{:S(2)}) collective-permute-start(bf16[32,2048]{1,0:T(8,128)(2,1)S(1)} %get-tuple-element.32), channel_id=1, source_target_pairs={{0,2},{1,3},{2,0},{3,1},{4,6},{5,7},{6,4},{7,5},{8,10},{9,11},{10,... | collective-permute-start | bytes 393224 | tf_op jit(solution)/shard_map/ppermute | solution.py:170
  157.8 13.7 %collective-permute-start.57 = (bf16[32,2048]{1,0:T(8,128)(2,1)S(1)}, bf16[32,2048]{1,0:T(8,128)(2,1)S(1)}, u32[]{:S(2)}, u32[]{:S(2)}) collective-permute-start(bf16[32,2048]{1,0:T(8,128)(2,1)S(1)} %get-tuple-element.12), channel_id=1, source_target_pairs={{4,0},{5,1},{6,2},{7,3},{8,4},{9,5},{10,6},{11,7},{12,8},{13,9},{1... | collective-permute-start | bytes 393224 | tf_op jit(solution)/shard_map/ppermute | solution.py:185
  159.1 12.4 %collective-permute-start.51 = (bf16[32,2048]{1,0:T(8,128)(2,1)S(1)}, bf16[32,2048]{1,0:T(8,128)(2,1)S(1)}, u32[]{:S(2)}, u32[]{:S(2)}) collective-permute-start(bf16[32,2048]{1,0:T(8,128)(2,1)S(1)} %get-tuple-element.11), channel_id=1, source_target_pairs={{0,4},{1,5},{2,6},{3,7},{4,8},{5,9},{6,10},{7,11},{8,12},{9,13},{1... | collective-permute-start | bytes 393224 | tf_op jit(solution)/shard_map/ppermute | solution.py:178
  (48 other events, 589.1 us)

commit v7 on v5

--- a/solution.py
+++ b/solution.py
@@ -231,13 +231,11 @@
     side = jnp.concatenate([weight_hi, weight_lo], axis=1)
     side_width = -(-side.shape[1] // 128) * 128
     side = jnp.pad(side, ((0, 0), (0, side_width - side.shape[1])))
-    payload = jnp.concatenate(
-        [centroid.astype(jnp.bfloat16), grad_sum.astype(jnp.bfloat16), side], axis=1
-    )
+    grad_all = lax.all_gather(grad_sum.astype(jnp.bfloat16), "expert", axis=0, tiled=True)
+    payload = jnp.concatenate([centroid.astype(jnp.bfloat16), side], axis=1)
     gathered = topo_all_gather(payload, experts)
     cent_all = gathered[:, :model_width]
-    grad_all = gathered[:, model_width : 2 * model_width]
-    side_all = gathered[:, 2 * model_width : 2 * model_width + 2 * experts].astype(jnp.float32)
+    side_all = gathered[:, model_width : model_width + 2 * experts].astype(jnp.float32)
     column = jnp.arange(experts, dtype=jnp.int32)[None, :]
     mine = jnp.sum(jnp.where(column == me, side_all[:, :experts] + side_all[:, experts:], 0.0), axis=1)
     output, input_grad = expert_dense(

time: 145 us -> 141 us (0.972)
  between operations: 1.26 us -> 14.8 us
  starting transfers between devices: 60.1 us -> 52.3 us
  waiting for transfers between devices: 31.6 us -> 24.5 us
  other arithmetic: 21.1 us -> 18.3 us
    ppermute x3, starting transfers between devices: 20.1 us -> 13.6 us  [topo_reduce_scatter(): lax.ppermute(ahead.astype(jnp.bfloat16), 'expert', [(j, j + 4) for j in r...]
    ppermute x3, waiting for transfers between devices: 8.12 us -> 4.65 us  [topo_reduce_scatter(): lax.ppermute(ahead.astype(jnp.bfloat16), 'expert', [(j, j + 4) for j in r...]
    ppermute x3, waiting for transfers between devices: 8.96 us -> 6.73 us  [topo_all_gather(): lax.ppermute(behind, 'expert', [(j, j - 4) for j in range(experts) if 1 <...]
    ppermute x3, waiting for transfers between devices: 4.41 us -> 2.36 us  [topo_reduce_scatter(): lax.ppermute(behind.astype(jnp.bfloat16), 'expert', [(j, j - 4) for j in...]
    another operation x2, other arithmetic: 5.2 us -> 3.64 us  [topo_all_gather(): jnp.stack([pick(in_row, [column, across]), pick(in_row, [across, column])...]
    dot_general x1, matrix products: 2.98 us -> 4.49 us  [expert_dense(): gate_act = jnp.dot(cent_in, gate_mat, preferred_element_type=jnp.float32)]
    unnamed x26 -> x34, local copies, waits for them, and re-layouts: 5.12 us -> 4.99 us
  transfers between devices with their start and end apart: 29 -> 30, of which waited for: 10 -> 10; matrix products, arithmetic and copies ran while one was open for 6% -> 14% of each run, Pallas kernels for 0% -> 0%
where the time goes in v7:
time: 141 us; the launch traced here: 140 us
  starting transfers between devices  52.3 us (37%)
  waiting for transfers between devices  24.5 us (17%)
  matrix products  21.2 us (15%)
  other arithmetic  18.3 us (13%)
  between operations  14.8 us (10%)
  local copies, waits for them, and re-layouts  9.2 us (7%)
    ppermute x3, starting transfers between devices, topo_reduce_scatter(): lax.ppermute(ahead.astype(jnp.bfloat16), 'expert', [(j, j + 4) for j in r...  13.6 us
    ppermute x7, starting transfers between devices, row_sum(): got = lax.ppermute(theirs.astype(jnp.bfloat16), 'expert', pairs)  11.3 us
    ppermute x3, starting transfers between devices, topo_all_gather(): there.append((lax.ppermute(behind, 'expert', behind_row), line + step))  8.43 us
    ppermute x3, starting transfers between devices, topo_all_gather(): lax.ppermute(ahead, 'expert', [(j, j + 4) for j in range(experts) if step...  7.59 us
    ppermute x3, waiting for transfers between devices, topo_all_gather(): lax.ppermute(behind, 'expert', [(j, j - 4) for j in range(experts) if 1 <...  6.73 us
    unnamed x34, local copies, waits for them, and re-layouts  4.99 us
    ppermute x3, waiting for transfers between devices, topo_reduce_scatter(): lax.ppermute(ahead.astype(jnp.bfloat16), 'expert', [(j, j + 4) for j in r...  4.65 us
    dot_general x1, matrix products, expert_dense(): gate_act = jnp.dot(cent_in, gate_mat, preferred_element_type=jnp.float32)  4.49 us
  transfers between devices with their start and end apart: 30, of which 10 were waited for; matrix products, arithmetic and copies ran while one was open for 14% of the time, Pallas kernels for 0%

profile of v7, /device:TPU:0, one launch (start us, length us, event | category | flops | bytes accessed | tf_op | source)
XLA Modules:
  0.0 140.3 jit_solution(17378916092571799343)
XLA Ops:
  9.0 2.0 %fusion.58 = (bf16[32,2048]{1,0:T(8,128)(2,1)S(1)}, f32[32,2048]{1,0:T(8,128)}) fusion(f32[32]{0:T(128)S(1)} %convert_reduce_fusion, bf16[128,2048]{1,0:T(8,128)(2,1)} %param.10, s32[128]{0:T(128)} %param.12), kind=kOutput, calls=%fused_computation.117 | convolution fusion | flops 16912384 | bytes 918144 | tf_op jit(solution)/shard_map/dot_general | solution.py:221
  11.0 4.9 %collective-permute-start.3 = (bf16[32,2176]{1,0:T(8,128)(2,1)S(1)}, bf16[32,2176]{1,0:T(8,128)(2,1)S(1)}, u32[]{:S(2)}, u32[]{:S(2)}) collective-permute-start(bf16[32,2176]{1,0:T(8,128)(2,1)S(1)} %fusion.47), channel_id=1, source_target_pairs={{0,4},{1,5},{2,6},{3,7},{4,8},{5,9},{6,10},{7,11},{8,12},{9,13},{1... | collective-permute-start | bytes 417800 | tf_op jit(solution)/shard_map/ppermute | solution.py:120
  17.2 1.6 %collective-permute-start.12 = (bf16[32,2176]{1,0:T(8,128)(2,1)S(1)}, bf16[32,2176]{1,0:T(8,128)(2,1)}, u32[]{:S(2)}, u32[]{:S(2)}) collective-permute-start(bf16[32,2176]{1,0:T(8,128)(2,1)S(1)} %fusion.47), channel_id=1, source_target_pairs={{0,2},{1,3},{2,0},{3,1},{4,6},{5,7},{6,4},{7,5},{8,10},{9,11},{10,... | collective-permute-start | bytes 417800 | tf_op jit(solution)/shard_map/ppermute | solution.py:117
  18.8 2.0 %fusion.57 = (bf16[32,2048]{1,0:T(8,128)(2,1)}, f32[32,2048]{1,0:T(8,128)}) fusion(bf16[128,2048]{1,0:T(8,128)(2,1)} %param.11, s32[128]{0:T(128)} %param.12), kind=kOutput, calls=%fused_computation.116 | convolution fusion | flops 16846848 | bytes 918016 | tf_op jit(solution)/shard_map/dot_general | solution.py:224
  27.0 5.9 %collective-permute-done.1 = bf16[32,2176]{1,0:T(8,128)(2,1)} collective-permute-done((bf16[32,2176]{1,0:T(8,128)(2,1)}, bf16[32,2176]{1,0:T(8,128)(2,1)}, u32[]{:S(2)}, u32[]{:S(2)}) %collective-permute-start.1) | collective-permute-done | bytes 139296 | tf_op jit(solution)/shard_map/ppermute | solution.py:125
  34.3 2.4 %collective-permute-start.10 = (bf16[32,2176]{1,0:T(8,128)(2,1)}, bf16[32,2176]{1,0:T(8,128)(2,1)S(1)}, u32[]{:S(2)}, u32[]{:S(2)}) collective-permute-start(bf16[32,2176]{1,0:T(8,128)(2,1)} %collective-permute-done), channel_id=1, source_target_pairs={{0,2},{1,3},{2,0},{3,1},{4,6},{5,7},{6,4},{7,5},{8,10},{9,11},{10,... | collective-permute-start | bytes 417800 | tf_op jit(solution)/shard_map/ppermute | solution.py:135
  37.4 3.4 %collective-permute-start.8 = (bf16[32,2176]{1,0:T(8,128)(2,1)}, bf16[32,2176]{1,0:T(8,128)(2,1)S(1)}, u32[]{:S(2)}, u32[]{:S(2)}) collective-permute-start(bf16[32,2176]{1,0:T(8,128)(2,1)} %collective-permute-done.1), channel_id=1, source_target_pairs={{0,2},{1,3},{2,0},{3,1},{4,6},{5,7},{6,4},{7,5},{16,18},{17,19},{1... | collective-permute-start | bytes 417800 | tf_op jit(solution)/shard_map/ppermute | solution.py:135
  41.5 2.6 %collective-permute-start.6 = (bf16[32,2176]{1,0:T(8,128)(2,1)}, bf16[32,2176]{1,0:T(8,128)(2,1)S(1)}, u32[]{:S(2)}, u32[]{:S(2)}) collective-permute-start(bf16[32,2176]{1,0:T(8,128)(2,1)} %collective-permute-done.2), channel_id=1, source_target_pairs={{0,2},{1,3},{2,0},{3,1},{16,18},{17,19},{18,16},{19,17}} | collective-permute-start | bytes 417800 | tf_op jit(solution)/shard_map/ppermute | solution.py:135
  44.1 1.5 %select_select_fusion.1 = bf16[4,32,2176]{2,1,0:T(8,128)(2,1)S(1)} fusion(pred[4]{0:T(512)(128)(4,1)S(1)} %get-tuple-element.30, pred[4]{0:T(512)(128)(4,1)S(1)} %get-tuple-element.31, pred[4]{0:T(512)(128)(4,1)S(1)} %get-tuple-element.32, pred[4]{0:T(512)(128)(4,1)S(1)} %get-tuple-element.33, pred[4]{0:T(512)(128)(4,1)S(1)} %get-tuple-element.34, ...), kind=kLoop, calls=%fused_computation.45 | loop fusion | flops 1949696 | bytes 1531932 | tf_op jit(solution)/shard_map/jit(_where)/select_n | solution.py:107
  45.7 3.0 %collective-permute-done.6 = bf16[32,2176]{1,0:T(8,128)(2,1)S(1)} collective-permute-done((bf16[32,2176]{1,0:T(8,128)(2,1)}, bf16[32,2176]{1,0:T(8,128)(2,1)S(1)}, u32[]{:S(2)}, u32[]{:S(2)}) %collective-permute-start.6) | collective-permute-done | bytes 139296 | tf_op jit(solution)/shard_map/ppermute | solution.py:135
  50.1 1.8 %select_bitcast_fusion.3 = bf16[4,1,1,32,2176]{4,3,0,2,1:T(8,128)(2,1)S(1)} fusion(pred[]{:T(512)S(6)} %eq.147, bf16[32,2176]{1,0:T(8,128)(2,1)S(1)} %fusion.47, pred[4]{0:T(512)(128)(4,1)S(1)} %get-tuple-element.30, bf16[32,2176]{1,0:T(8,128)(2,1)S(1)} %collective-permute-done.3, pred[4]{0:T(512)(128)(4,1)S(1)} %get-tuple-element.31, ...), kind=kLoop, calls=%fused_computation.46 | loop fusion | flops 4177920 | bytes 2506781 | tf_op jit(solution)/shard_map/stack | solution.py:143
  51.9 1.8 %select_bitcast_fusion.4 = bf16[4,1,1,32,2176]{4,3,0,2,1:T(8,128)(2,1)S(1)} fusion(pred[]{:T(512)S(6)} %eq.147, bf16[32,2176]{1,0:T(8,128)(2,1)S(1)} %fusion.47, pred[4]{0:T(512)(128)(4,1)S(1)} %get-tuple-element.30, bf16[32,2176]{1,0:T(8,128)(2,1)S(1)} %collective-permute-done.3, pred[4]{0:T(512)(128)(4,1)S(1)} %get-tuple-element.31, ...), kind=kLoop, calls=%fused_computation.47 | loop fusion | flops 4177920 | bytes 2506781 | tf_op jit(solution)/shard_map/stack | solution.py:143
  56.2 4.5 %fusion.10 = f32[512,768]{1,0:T(8,128)S(1)} fusion(bf16[1,2048,768]{2,1,0:T(8,128)(2,1)} %param.15, bf16[512,2176]{1,0:T(8,128)(2,1)} %bitcast.108), kind=kOutput, calls=%fused_computation.17 | convolution fusion | flops 1610612736 | bytes 6815744 | tf_op jit(solution)/shard_map/dot_general | solution.py:195
  60.7 1.8 %fusion.6 = f32[512,768]{1,0:T(8,128)S(1)} fusion(bf16[1,2048,768]{2,1,0:T(8,128)(2,1)S(1)} %copy-done.9, bf16[512,2176]{1,0:T(8,128)(2,1)S(1)} %bitcast.109), kind=kOutput, calls=%fused_computation.13 | convolution fusion | flops 1610612736 | bytes 6815744 | tf_op jit(solution)/shard_map/dot_general | solution.py:196
  63.7 3.2 %multiply_convert_fusion.1 = bf16[512,2048]{1,0:T(8,128)(2,1)} fusion(bf16[1,768,2048]{2,1,0:T(8,128)(2,1)S(1)} %copy-done, f32[512]{0:T(512)S(1)} %fusion.49, f32[512,768]{1,0:T(8,128)S(1)} %fusion.6, f32[512,768]{1,0:T(8,128)S(1)} %fusion.10), kind=kOutput, calls=%fused_computation.6 | convolution fusion | flops 1617166336 | bytes 8390656 | tf_op jit(solution)/shard_map/dot_general | solution.py:199
  66.9 3.6 %fusion = f32[512,768]{1,0:T(8,128)S(1)} fusion(bf16[512,2048]{1,0:T(8,128)(2,1)} %all-gather.2.cloned.1.call-done, bf16[1,768,2048]{2,1,0:T(8,128)(2,1)S(1)} %copy-done), kind=kOutput, calls=%fused_computation.7 | convolution fusion | flops 1610612736 | bytes 6815744 | tf_op jit(solution)/shard_map/dot_general | solution.py:200
  70.5 1.8 %fusion.4 = f32[512,2048]{1,0:T(8,128)S(1)} fusion(bf16[1,2048,768]{2,1,0:T(8,128)(2,1)S(1)} %copy-done.10, f32[512,768]{1,0:T(8,128)S(1)} %fusion, f32[512,768]{1,0:T(8,128)S(1)} %copy-done.13), kind=kOutput, calls=%fused_computation.11 | convolution fusion | flops 1612972032 | bytes 10485760 | tf_op jit(solution)/shard_map/dot_general | solution.py:206
  72.9 2.3 %multiply_convert_fusion = bf16[512,2048]{1,0:T(8,128)(2,1)S(1)} fusion(f32[512,2048]{1,0:T(8,128)S(1)} %fusion.4, bf16[1,2048,768]{2,1,0:T(8,128)(2,1)S(1)} %copy-done.11, f32[512]{0:T(512)S(1)} %fusion.49, f32[512,768]{1,0:T(8,128)S(1)} %copy-done.13, f32[512,768]{1,0:T(8,128)S(1)} %fusion, f32[512,768]{1,0:T(8,128)S(1)} %copy-done.15), kind=kOutput, calls=%fused_computation.4 | convolution fusion | flops 1619787776 | bytes 14157824 | tf_op jit(solution)/shard_map/dot_general | solution.py:205
  75.9 1.7 %copy-done.2 = bf16[512,4096]{1,0:T(8,128)(2,1)} copy-done((bf16[512,4096]{1,0:T(8,128)(2,1)}, bf16[512,4096]{1,0:T(8,128)(2,1)S(1)}, u32[]{:S(2)}) %copy-start.2) | copy-done | bytes 4194328
  78.1 3.9 %collective-permute-done.15 = bf16[4,2,32,4096]{3,2,1,0:T(8,128)(2,1)} collective-permute-done((bf16[4,2,32,4096]{3,2,1,0:T(8,128)(2,1)S(1)}, bf16[4,2,32,4096]{3,2,1,0:T(8,128)(2,1)}, u32[]{:S(2)}, u32[]{:S(2)}) %collective-permute-start.15) | collective-permute-done | bytes 2097184 | tf_op jit(solution)/shard_map/ppermute | solution.py:159
  82.1 4.1 %convert_add_fusion = f32[4,2,32,4096]{3,2,1,0:T(8,128)S(1)} fusion(bf16[4,2,32,4096]{3,2,1,0:T(8,128)(2,1)} %collective-permute-done.15, pred[]{:T(512)S(6)} %eq.148, bf16[4,2,2,32,4096]{4,3,2,1,0:T(8,128)(2,1)} %bitcast.106), kind=kLoop, calls=%fused_computation.3 | loop fusion | flops 4194304 | bytes 10485761 | tf_op jit(solution)/shard_map/add | solution.py:160
  86.5 2.6 %collective-permute-start.17 = (bf16[32,4096]{1,0:T(8,128)(2,1)S(1)}, bf16[32,4096]{1,0:T(8,128)(2,1)S(1)}, u32[]{:S(2)}, u32[]{:S(2)}) collective-permute-start(bf16[32,4096]{1,0:T(8,128)(2,1)S(1)} %get-tuple-element.21), channel_id=1, source_target_pairs={{0,2},{1,3},{2,0},{3,1},{16,18},{17,19},{18,16},{19,17}} | collective-permute-start | bytes 786440 | tf_op jit(solution)/shard_map/ppermute | solution.py:170
  90.1 3.2 %collective-permute-start.19 = (bf16[32,4096]{1,0:T(8,128)(2,1)S(1)}, bf16[32,4096]{1,0:T(8,128)(2,1)S(1)}, u32[]{:S(2)}, u32[]{:S(2)}) collective-permute-start(bf16[32,4096]{1,0:T(8,128)(2,1)S(1)} %get-tuple-element.20), channel_id=1, source_target_pairs={{0,2},{1,3},{2,0},{3,1},{4,6},{5,7},{6,4},{7,5},{16,18},{17,19},{1... | collective-permute-start | bytes 786440 | tf_op jit(solution)/shard_map/ppermute | solution.py:170
  94.0 3.5 %collective-permute-done.17 = bf16[32,4096]{1,0:T(8,128)(2,1)S(1)} collective-permute-done((bf16[32,4096]{1,0:T(8,128)(2,1)S(1)}, bf16[32,4096]{1,0:T(8,128)(2,1)S(1)}, u32[]{:S(2)}, u32[]{:S(2)}) %collective-permute-start.17) | collective-permute-done | bytes 262176 | tf_op jit(solution)/shard_map/ppermute | solution.py:170
  99.7 2.6 %collective-permute-start.21 = (bf16[32,4096]{1,0:T(8,128)(2,1)S(1)}, bf16[32,4096]{1,0:T(8,128)(2,1)S(1)}, u32[]{:S(2)}, u32[]{:S(2)}) collective-permute-start(bf16[32,4096]{1,0:T(8,128)(2,1)S(1)} %get-tuple-element.19), channel_id=1, source_target_pairs={{0,2},{1,3},{2,0},{3,1},{4,6},{5,7},{6,4},{7,5},{8,10},{9,11},{10,... | collective-permute-start | bytes 786440 | tf_op jit(solution)/shard_map/ppermute | solution.py:170
  104.1 4.4 %collective-permute-start.20 = (bf16[32,4096]{1,0:T(8,128)(2,1)S(1)}, bf16[32,4096]{1,0:T(8,128)(2,1)S(1)}, u32[]{:S(2)}, u32[]{:S(2)}) collective-permute-start(bf16[32,4096]{1,0:T(8,128)(2,1)S(1)} %get-tuple-element.9), channel_id=1, source_target_pairs={{0,4},{1,5},{2,6},{3,7},{4,8},{5,9},{6,10},{7,11},{16,20},{17,21},... | collective-permute-start | bytes 786440 | tf_op jit(solution)/shard_map/ppermute | solution.py:178
  110.1 2.5 %collective-permute-done.20 = bf16[32,4096]{1,0:T(8,128)(2,1)S(1)} collective-permute-done((bf16[32,4096]{1,0:T(8,128)(2,1)S(1)}, bf16[32,4096]{1,0:T(8,128)(2,1)S(1)}, u32[]{:S(2)}, u32[]{:S(2)}) %collective-permute-start.20) | collective-permute-done | bytes 262176 | tf_op jit(solution)/shard_map/ppermute | solution.py:178
  114.1 7.9 %collective-permute-start.22 = (bf16[32,4096]{1,0:T(8,128)(2,1)S(1)}, bf16[32,4096]{1,0:T(8,128)(2,1)S(1)}, u32[]{:S(2)}, u32[]{:S(2)}) collective-permute-start(bf16[32,4096]{1,0:T(8,128)(2,1)S(1)} %get-tuple-element.7), channel_id=1, source_target_pairs={{0,4},{1,5},{2,6},{3,7},{4,8},{5,9},{6,10},{7,11},{8,12},{9,13},{1... | collective-permute-start | bytes 786440 | tf_op jit(solution)/shard_map/ppermute | solution.py:178
  122.0 2.4 %collective-permute-done.28 = bf16[32,4096]{1,0:T(8,128)(2,1)S(1)} collective-permute-done((bf16[32,4096]{1,0:T(8,128)(2,1)S(1)}, bf16[32,4096]{1,0:T(8,128)(2,1)S(1)}, u32[]{:S(2)}, u32[]{:S(2)}) %collective-permute-start.28) | collective-permute-done | bytes 262176 | tf_op jit(solution)/shard_map/ppermute | solution.py:185
  126.1 1.9 %gather_fusion.1 = f32[128,2048]{1,0:T(8,128)} fusion(f32[32,2048]{1,0:T(8,128)S(1)} %get-tuple-element.22, s32[1024]{0:T(1024)S(1)} %pad_clamp_fusion), kind=kCustom, calls=%fused_computation.1.clone | custom fusion | bytes 2097664 | tf_op jit(solution)/shard_map/jit(_take)/gather | solution.py:255
  128.0 1.9 %gather_fusion = f32[128,2048]{1,0:T(8,128)} fusion(f32[32,2048]{1,0:T(8,128)S(1)} %get-tuple-element.23, s32[1024]{0:T(1024)S(1)} %pad_clamp_fusion), kind=kCustom, calls=%fused_computation.clone | custom fusion | bytes 2097664 | tf_op jit(solution)/shard_map/jit(_take)/gather | solution.py:254
  129.9 3.6 %select_add_fusion = (f32[128,2048]{1,0:T(8,128)}, f32[128,2048]{1,0:T(8,128)}) fusion(f32[128,2048]{1,0:T(8,128)} %gather_fusion.1, bf16[128,2048]{1,0:T(8,128)(2,1)} %param.11, pred[128]{0:T(512)(128)(4,1)S(1)} %compare_and_fusion, f32[128,2048]{1,0:T(8,128)} %gather_fusion, bf16[128,2048]{1,0:T(8,128)(2,1)} %param.10), kind=kLoop, calls=%fused_computation.37 | loop fusion | flops 1572864 | bytes 5243008 | tf_op jit(solution)/shard_map/add | solution.py:255
  (109 shorter events, 29.1 us)
Async XLA Ops:
  7.2 56.5 %copy-start = (bf16[1,768,2048]{2,1,0:T(8,128)(2,1)S(1)}, bf16[1,768,2048]{2,1,0:T(8,128)(2,1)}, u32[]{:S(2)}) copy-start(bf16[1,768,2048]{2,1,0:T(8,128)(2,1)} %param.17) | copy-start | bytes 9437188
  7.2 59.7 %all-gather.2.cloned.1.call-start = ((), (), s32[]{:S(2)}) async-start(), calls=%async_computation | async-start | bytes 2228224 | tf_op jit(solution)/shard_map/all_gather | solution.py:234
  11.0 9.9 %collective-permute-start.3 = (bf16[32,2176]{1,0:T(8,128)(2,1)S(1)}, bf16[32,2176]{1,0:T(8,128)(2,1)S(1)}, u32[]{:S(2)}, u32[]{:S(2)}) collective-permute-start(bf16[32,2176]{1,0:T(8,128)(2,1)S(1)} %fusion.47), channel_id=1, source_target_pairs={{0,4},{1,5},{2,6},{3,7},{4,8},{5,9},{6,10},{7,11},{8,12},{9,13},{1... | collective-permute-start | bytes 417800 | tf_op jit(solution)/shard_map/ppermute | solution.py:120
  15.9 7.1 %collective-permute-start = (bf16[32,2176]{1,0:T(8,128)(2,1)S(1)}, bf16[32,2176]{1,0:T(8,128)(2,1)}, u32[]{:S(2)}, u32[]{:S(2)}) collective-permute-start(bf16[32,2176]{1,0:T(8,128)(2,1)S(1)} %fusion.47), channel_id=1, source_target_pairs={{4,0},{5,1},{6,2},{7,3},{8,4},{9,5},{10,6},{11,7},{12,8},{13,9},{1... | collective-permute-start | bytes 417800 | tf_op jit(solution)/shard_map/ppermute | solution.py:125
  17.2 19.5 %collective-permute-start.12 = (bf16[32,2176]{1,0:T(8,128)(2,1)S(1)}, bf16[32,2176]{1,0:T(8,128)(2,1)}, u32[]{:S(2)}, u32[]{:S(2)}) collective-permute-start(bf16[32,2176]{1,0:T(8,128)(2,1)S(1)} %fusion.47), channel_id=1, source_target_pairs={{0,2},{1,3},{2,0},{3,1},{4,6},{5,7},{6,4},{7,5},{8,10},{9,11},{10,... | collective-permute-start | bytes 417800 | tf_op jit(solution)/shard_map/ppermute | solution.py:117
  20.9 4.8 %collective-permute-start.4 = (bf16[32,2176]{1,0:T(8,128)(2,1)S(1)}, bf16[32,2176]{1,0:T(8,128)(2,1)}, u32[]{:S(2)}, u32[]{:S(2)}) collective-permute-start(bf16[32,2176]{1,0:T(8,128)(2,1)S(1)} %collective-permute-done.3), channel_id=1, source_target_pairs={{4,8},{5,9},{6,10},{7,11},{8,12},{9,13},{10,14},{11,15},{20,24},{2... | collective-permute-start | bytes 417800 | tf_op jit(solution)/shard_map/ppermute | solution.py:120
  23.0 9.9 %collective-permute-start.1 = (bf16[32,2176]{1,0:T(8,128)(2,1)}, bf16[32,2176]{1,0:T(8,128)(2,1)}, u32[]{:S(2)}, u32[]{:S(2)}) collective-permute-start(bf16[32,2176]{1,0:T(8,128)(2,1)} %collective-permute-done), channel_id=1, source_target_pairs={{4,0},{5,1},{6,2},{7,3},{8,4},{9,5},{10,6},{11,7},{20,16},{21,17},... | collective-permute-start | bytes 417800 | tf_op jit(solution)/shard_map/ppermute | solution.py:125
  24.4 13.0 %collective-permute-start.11 = (bf16[32,2176]{1,0:T(8,128)(2,1)S(1)}, bf16[32,2176]{1,0:T(8,128)(2,1)}, u32[]{:S(2)}, u32[]{:S(2)}) collective-permute-start(bf16[32,2176]{1,0:T(8,128)(2,1)S(1)} %collective-permute-done.3), channel_id=1, source_target_pairs={{4,6},{5,7},{6,4},{7,5},{8,10},{9,11},{10,8},{11,9},{12,14},{13,15... | collective-permute-start | bytes 417800 | tf_op jit(solution)/shard_map/ppermute | solution.py:134
  25.7 15.1 %collective-permute-start.5 = (bf16[32,2176]{1,0:T(8,128)(2,1)}, bf16[32,2176]{1,0:T(8,128)(2,1)}, u32[]{:S(2)}, u32[]{:S(2)}) collective-permute-start(bf16[32,2176]{1,0:T(8,128)(2,1)} %collective-permute-done.4), channel_id=1, source_target_pairs={{8,12},{9,13},{10,14},{11,15},{24,28},{25,29},{26,30},{27,31}} | collective-permute-start | bytes 417800 | tf_op jit(solution)/shard_map/ppermute | solution.py:120
  32.9 8.6 %collective-permute-start.2 = (bf16[32,2176]{1,0:T(8,128)(2,1)}, bf16[32,2176]{1,0:T(8,128)(2,1)}, u32[]{:S(2)}, u32[]{:S(2)}) collective-permute-start(bf16[32,2176]{1,0:T(8,128)(2,1)} %collective-permute-done.1), channel_id=1, source_target_pairs={{4,0},{5,1},{6,2},{7,3},{20,16},{21,17},{22,18},{23,19}} | collective-permute-start | bytes 417800 | tf_op jit(solution)/shard_map/ppermute | solution.py:125
  34.3 11.3 %collective-permute-start.10 = (bf16[32,2176]{1,0:T(8,128)(2,1)}, bf16[32,2176]{1,0:T(8,128)(2,1)S(1)}, u32[]{:S(2)}, u32[]{:S(2)}) collective-permute-start(bf16[32,2176]{1,0:T(8,128)(2,1)} %collective-permute-done), channel_id=1, source_target_pairs={{0,2},{1,3},{2,0},{3,1},{4,6},{5,7},{6,4},{7,5},{8,10},{9,11},{10,... | collective-permute-start | bytes 417800 | tf_op jit(solution)/shard_map/ppermute | solution.py:135
  36.7 9.0 %collective-permute-start.9 = (bf16[32,2176]{1,0:T(8,128)(2,1)}, bf16[32,2176]{1,0:T(8,128)(2,1)S(1)}, u32[]{:S(2)}, u32[]{:S(2)}) collective-permute-start(bf16[32,2176]{1,0:T(8,128)(2,1)} %collective-permute-done.4), channel_id=1, source_target_pairs={{8,10},{9,11},{10,8},{11,9},{12,14},{13,15},{14,12},{15,13},{24,26... | collective-permute-start | bytes 417800 | tf_op jit(solution)/shard_map/ppermute | solution.py:134
  37.4 8.3 %collective-permute-start.8 = (bf16[32,2176]{1,0:T(8,128)(2,1)}, bf16[32,2176]{1,0:T(8,128)(2,1)S(1)}, u32[]{:S(2)}, u32[]{:S(2)}) collective-permute-start(bf16[32,2176]{1,0:T(8,128)(2,1)} %collective-permute-done.1), channel_id=1, source_target_pairs={{0,2},{1,3},{2,0},{3,1},{4,6},{5,7},{6,4},{7,5},{16,18},{17,19},{1... | collective-permute-start | bytes 417800 | tf_op jit(solution)/shard_map/ppermute | solution.py:135
  40.8 4.9 %collective-permute-start.7 = (bf16[32,2176]{1,0:T(8,128)(2,1)}, bf16[32,2176]{1,0:T(8,128)(2,1)S(1)}, u32[]{:S(2)}, u32[]{:S(2)}) collective-permute-start(bf16[32,2176]{1,0:T(8,128)(2,1)} %collective-permute-done.5), channel_id=1, source_target_pairs={{12,14},{13,15},{14,12},{15,13},{28,30},{29,31},{30,28},{31,29}} | collective-permute-start | bytes 417800 | tf_op jit(solution)/shard_map/ppermute | solution.py:134
  41.5 7.2 %collective-permute-start.6 = (bf16[32,2176]{1,0:T(8,128)(2,1)}, bf16[32,2176]{1,0:T(8,128)(2,1)S(1)}, u32[]{:S(2)}, u32[]{:S(2)}) collective-permute-start(bf16[32,2176]{1,0:T(8,128)(2,1)} %collective-permute-done.2), channel_id=1, source_target_pairs={{0,2},{1,3},{2,0},{3,1},{16,18},{17,19},{18,16},{19,17}} | collective-permute-start | bytes 417800 | tf_op jit(solution)/shard_map/ppermute | solution.py:135
  45.6 8.1 %collective-permute-start.13 = (bf16[4,32,2176]{2,1,0:T(8,128)(2,1)S(1)}, bf16[4,32,2176]{2,1,0:T(8,128)(2,1)S(1)}, u32[]{:S(2)}, u32[]{:S(2)}) collective-permute-start(bf16[4,32,2176]{2,1,0:T(8,128)(2,1)S(1)} %select_select_fusion.1), channel_id=1, source_target_pairs={{0,1},{1,0},{2,3},{3,2},{4,5},{5,4},{6,7},{7,6},{8,9},{9,8},{10,11... | collective-permute-start | bytes 1671176 | tf_op jit(solution)/shard_map/ppermute | solution.py:139
  50.0 3.7 %collective-permute-start.14 = (bf16[4,32,2176]{2,1,0:T(8,128)(2,1)S(1)}, bf16[4,32,2176]{2,1,0:T(8,128)(2,1)S(1)}, u32[]{:S(2)}, u32[]{:S(2)}) collective-permute-start(bf16[4,32,2176]{2,1,0:T(8,128)(2,1)S(1)} %select_select_fusion), channel_id=1, source_target_pairs={{0,1},{1,0},{2,3},{3,2},{4,5},{5,4},{6,7},{7,6},{8,9},{9,8},{10,11... | collective-permute-start | bytes 1671176 | tf_op jit(solution)/shard_map/ppermute | solution.py:140
  77.7 4.4 %collective-permute-start.15 = (bf16[4,2,32,4096]{3,2,1,0:T(8,128)(2,1)S(1)}, bf16[4,2,32,4096]{3,2,1,0:T(8,128)(2,1)}, u32[]{:S(2)}, u32[]{:S(2)}) collective-permute-start(bf16[4,2,32,4096]{3,2,1,0:T(8,128)(2,1)S(1)} %select_bitcast_fusion), channel_id=1, source_target_pairs={{0,1},{1,0},{2,3},{3,2},{4,5},{5,4},{6,7},{7,6},{8,9},{9,8},{10,11... | collective-permute-start | bytes 6291464 | tf_op jit(solution)/shard_map/ppermute | solution.py:159
  86.5 11.0 %collective-permute-start.17 = (bf16[32,4096]{1,0:T(8,128)(2,1)S(1)}, bf16[32,4096]{1,0:T(8,128)(2,1)S(1)}, u32[]{:S(2)}, u32[]{:S(2)}) collective-permute-start(bf16[32,4096]{1,0:T(8,128)(2,1)S(1)} %get-tuple-element.21), channel_id=1, source_target_pairs={{0,2},{1,3},{2,0},{3,1},{16,18},{17,19},{18,16},{19,17}} | collective-permute-start | bytes 786440 | tf_op jit(solution)/shard_map/ppermute | solution.py:170
  89.2 8.4 %collective-permute-start.23 = (bf16[32,4096]{1,0:T(8,128)(2,1)S(1)}, bf16[32,4096]{1,0:T(8,128)(2,1)S(1)}, u32[]{:S(2)}, u32[]{:S(2)}) collective-permute-start(bf16[32,4096]{1,0:T(8,128)(2,1)S(1)} %get-tuple-element.18), channel_id=1, source_target_pairs={{12,14},{13,15},{14,12},{15,13},{28,30},{29,31},{30,28},{31,29}} | collective-permute-start | bytes 786440 | tf_op jit(solution)/shard_map/ppermute | solution.py:170
  90.1 12.5 %collective-permute-start.19 = (bf16[32,4096]{1,0:T(8,128)(2,1)S(1)}, bf16[32,4096]{1,0:T(8,128)(2,1)S(1)}, u32[]{:S(2)}, u32[]{:S(2)}) collective-permute-start(bf16[32,4096]{1,0:T(8,128)(2,1)S(1)} %get-tuple-element.20), channel_id=1, source_target_pairs={{0,2},{1,3},{2,0},{3,1},{4,6},{5,7},{6,4},{7,5},{16,18},{17,19},{1... | collective-permute-start | bytes 786440 | tf_op jit(solution)/shard_map/ppermute | solution.py:170
  93.4 9.9 %collective-permute-start.25 = (bf16[32,4096]{1,0:T(8,128)(2,1)S(1)}, bf16[32,4096]{1,0:T(8,128)(2,1)S(1)}, u32[]{:S(2)}, u32[]{:S(2)}) collective-permute-start(bf16[32,4096]{1,0:T(8,128)(2,1)S(1)} %get-tuple-element.17), channel_id=1, source_target_pairs={{8,10},{9,11},{10,8},{11,9},{12,14},{13,15},{14,12},{15,13},{24,26... | collective-permute-start | bytes 786440 | tf_op jit(solution)/shard_map/ppermute | solution.py:170
  97.7 6.3 %collective-permute-start.18 = (bf16[32,4096]{1,0:T(8,128)(2,1)S(1)}, bf16[32,4096]{1,0:T(8,128)(2,1)S(1)}, u32[]{:S(2)}, u32[]{:S(2)}) collective-permute-start(bf16[32,4096]{1,0:T(8,128)(2,1)S(1)} %get-tuple-element.11), channel_id=1, source_target_pairs={{0,4},{1,5},{2,6},{3,7},{16,20},{17,21},{18,22},{19,23}} | collective-permute-start | bytes 786440 | tf_op jit(solution)/shard_map/ppermute | solution.py:178
  99.0 5.0 %collective-permute-start.24 = (bf16[32,4096]{1,0:T(8,128)(2,1)S(1)}, bf16[32,4096]{1,0:T(8,128)(2,1)S(1)}, u32[]{:S(2)}, u32[]{:S(2)}) collective-permute-start(bf16[32,4096]{1,0:T(8,128)(2,1)S(1)} %get-tuple-element.12), channel_id=1, source_target_pairs={{12,8},{13,9},{14,10},{15,11},{28,24},{29,25},{30,26},{31,27}} | collective-permute-start | bytes 786440 | tf_op jit(solution)/shard_map/ppermute | solution.py:185
  99.7 10.4 %collective-permute-start.21 = (bf16[32,4096]{1,0:T(8,128)(2,1)S(1)}, bf16[32,4096]{1,0:T(8,128)(2,1)S(1)}, u32[]{:S(2)}, u32[]{:S(2)}) collective-permute-start(bf16[32,4096]{1,0:T(8,128)(2,1)S(1)} %get-tuple-element.19), channel_id=1, source_target_pairs={{0,2},{1,3},{2,0},{3,1},{4,6},{5,7},{6,4},{7,5},{8,10},{9,11},{10,... | collective-permute-start | bytes 786440 | tf_op jit(solution)/shard_map/ppermute | solution.py:170
  102.6 7.5 %collective-permute-start.27 = (bf16[32,4096]{1,0:T(8,128)(2,1)S(1)}, bf16[32,4096]{1,0:T(8,128)(2,1)S(1)}, u32[]{:S(2)}, u32[]{:S(2)}) collective-permute-start(bf16[32,4096]{1,0:T(8,128)(2,1)S(1)} %get-tuple-element.16), channel_id=1, source_target_pairs={{4,6},{5,7},{6,4},{7,5},{8,10},{9,11},{10,8},{11,9},{12,14},{13,15... | collective-permute-start | bytes 786440 | tf_op jit(solution)/shard_map/ppermute | solution.py:170
  104.1 8.5 %collective-permute-start.20 = (bf16[32,4096]{1,0:T(8,128)(2,1)S(1)}, bf16[32,4096]{1,0:T(8,128)(2,1)S(1)}, u32[]{:S(2)}, u32[]{:S(2)}) collective-permute-start(bf16[32,4096]{1,0:T(8,128)(2,1)S(1)} %get-tuple-element.9), channel_id=1, source_target_pairs={{0,4},{1,5},{2,6},{3,7},{4,8},{5,9},{6,10},{7,11},{16,20},{17,21},... | collective-permute-start | bytes 786440 | tf_op jit(solution)/shard_map/ppermute | solution.py:178
  108.5 4.1 %collective-permute-start.26 = (bf16[32,4096]{1,0:T(8,128)(2,1)S(1)}, bf16[32,4096]{1,0:T(8,128)(2,1)S(1)}, u32[]{:S(2)}, u32[]{:S(2)}) collective-permute-start(bf16[32,4096]{1,0:T(8,128)(2,1)S(1)} %get-tuple-element.10), channel_id=1, source_target_pairs={{8,4},{9,5},{10,6},{11,7},{12,8},{13,9},{14,10},{15,11},{24,20},{2... | collective-permute-start | bytes 786440 | tf_op jit(solution)/shard_map/ppermute | solution.py:185
  109.3 16.7 %copy-start.6 = (f32[32,2048]{1,0:T(8,128)S(1)}, f32[32,2048]{1,0:T(8,128)}, u32[]{:S(2)}) copy-start(f32[32,2048]{1,0:T(8,128)} %get-tuple-element.27) | copy-start | bytes 786436
  109.3 12.7 %collective-permute-start.16 = (bf16[32,4096]{1,0:T(8,128)(2,1)S(1)}, bf16[32,4096]{1,0:T(8,128)(2,1)S(1)}, u32[]{:S(2)}, u32[]{:S(2)}) collective-permute-start(bf16[32,4096]{1,0:T(8,128)(2,1)S(1)} %get-tuple-element.15), channel_id=1, source_target_pairs={{0,2},{1,3},{2,0},{3,1},{4,6},{5,7},{6,4},{7,5},{8,10},{9,11},{10,... | collective-permute-start | bytes 786440 | tf_op jit(solution)/shard_map/ppermute | solution.py:170
  112.8 11.6 %collective-permute-start.28 = (bf16[32,4096]{1,0:T(8,128)(2,1)S(1)}, bf16[32,4096]{1,0:T(8,128)(2,1)S(1)}, u32[]{:S(2)}, u32[]{:S(2)}) collective-permute-start(bf16[32,4096]{1,0:T(8,128)(2,1)S(1)} %get-tuple-element.8), channel_id=1, source_target_pairs={{4,0},{5,1},{6,2},{7,3},{8,4},{9,5},{10,6},{11,7},{12,8},{13,9},{1... | collective-permute-start | bytes 786440 | tf_op jit(solution)/shard_map/ppermute | solution.py:185
  114.1 11.8 %collective-permute-start.22 = (bf16[32,4096]{1,0:T(8,128)(2,1)S(1)}, bf16[32,4096]{1,0:T(8,128)(2,1)S(1)}, u32[]{:S(2)}, u32[]{:S(2)}) collective-permute-start(bf16[32,4096]{1,0:T(8,128)(2,1)S(1)} %get-tuple-element.7), channel_id=1, source_target_pairs={{0,4},{1,5},{2,6},{3,7},{4,8},{5,9},{6,10},{7,11},{8,12},{9,13},{1... | collective-permute-start | bytes 786440 | tf_op jit(solution)/shard_map/ppermute | solution.py:178
  (14 other events, 67.2 us)
Sparse Core Ops, SparseCore 0:
  20.9 43.5 all-gather.1

commit v8 on v5

--- a/solution.py
+++ b/solution.py
@@ -135,29 +135,16 @@
         there.append((lax.ppermute(behind, "expert", behind_row), line + step))
     column = place(here, lines, shard)
     across = place(there, lines, shard)
-    swap_core = [(j, j ^ 1) for j in range(experts)]
-    column_pair = lax.ppermute(column, "expert", swap_core)
-    across_pair = lax.ppermute(across, "expert", swap_core)
     in_row = (me // 2) % 2
-    on_chip = me % 2
     mine = jnp.stack([pick(in_row, [column, across]), pick(in_row, [across, column])], axis=1)
-    pair = jnp.stack(
-        [pick(in_row, [column_pair, across_pair]), pick(in_row, [across_pair, column_pair])], axis=1
-    )
-    full = jnp.stack([pick(on_chip, [mine, pair]), pick(on_chip, [pair, mine])], axis=2)
-    return full.reshape((experts * shard.shape[0],) + shard.shape[1:])
+    return mine.reshape((lines * 2 * shard.shape[0],) + shard.shape[1:])
 
 
 def topo_reduce_scatter(blocks, experts):
     lines = experts // 4
     me = lax.axis_index("expert")
-    rows = blocks.shape[0] // experts
-    cube = blocks.reshape((lines, 2, 2, rows) + blocks.shape[1:])
-    on_chip = me % 2
-    keep = pick(on_chip, [cube[:, :, 0], cube[:, :, 1]])
-    give = pick(on_chip, [cube[:, :, 1], cube[:, :, 0]])
-    got = lax.ppermute(give.astype(jnp.bfloat16), "expert", [(j, j ^ 1) for j in range(experts)])
-    plane = keep.astype(jnp.float32) + got.astype(jnp.float32)
+    rows = blocks.shape[0] // (2 * lines)
+    plane = blocks.reshape((lines, 2, rows) + blocks.shape[1:])
     in_row = (me // 2) % 2
     keep = pick(in_row, [plane[:, 0], plane[:, 1]])
     give = pick(in_row, [plane[:, 1], plane[:, 0]])
@@ -239,18 +226,23 @@
     grad_all = gathered[:, model_width : 2 * model_width]
     side_all = gathered[:, 2 * model_width : 2 * model_width + 2 * experts].astype(jnp.float32)
     column = jnp.arange(experts, dtype=jnp.int32)[None, :]
-    mine = jnp.sum(jnp.where(column == me, side_all[:, :experts] + side_all[:, experts:], 0.0), axis=1)
-    output, input_grad = expert_dense(
-        cent_all, grad_all, gate_weight[0], up_weight[0], down_weight[0]
-    )
-    parts = jnp.concatenate(
-        [
-            (mine[:, None] * output.astype(jnp.float32)).astype(jnp.bfloat16),
-            (mine[:, None] * input_grad.astype(jnp.float32)).astype(jnp.bfloat16),
-        ],
-        axis=1,
-    )
-    summed = topo_reduce_scatter(parts, experts)
+    summed_side = side_all[:, :experts] + side_all[:, experts:]
+    mine = jnp.sum(jnp.where(column == me, summed_side, 0.0), axis=1)
+    other = jnp.sum(jnp.where(column == (me ^ 1), summed_side, 0.0), axis=1)
+    swap_core = [(j, j ^ 1) for j in range(experts)]
+    gate_mat, up_mat, down_mat = gate_weight[0], up_weight[0], down_weight[0]
+    gate_pair = lax.ppermute(gate_mat, "expert", swap_core)
+    up_pair = lax.ppermute(up_mat, "expert", swap_core)
+    down_pair = lax.ppermute(down_mat, "expert", swap_core)
+    output, input_grad = expert_dense(cent_all, grad_all, gate_mat, up_mat, down_mat)
+    output_pair, input_grad_pair = expert_dense(cent_all, grad_all, gate_pair, up_pair, down_pair)
+    weighted_out = mine[:, None] * output.astype(jnp.float32) + other[:, None] * output_pair.astype(
+        jnp.float32
+    )
+    weighted_grad = mine[:, None] * input_grad.astype(jnp.float32) + other[
+        :, None
+    ] * input_grad_pair.astype(jnp.float32)
+    summed = topo_reduce_scatter(jnp.concatenate([weighted_out, weighted_grad], axis=1), experts)
     combined = summed[:, :model_width]
     centroid_grad = summed[:, model_width:] - grad_sum
     layer_out = tokens.astype(jnp.float32) + jnp.take(combined - centroid, cluster_ids, axis=0)

time: 145 us -> 122 us (0.84)
  other arithmetic: 21.1 us -> 9.35 us
  local copies, waits for them, and re-layouts: 9.53 us -> 5.69 us
  matrix products: 20.3 us -> 16.6 us
  waiting for transfers between devices: 31.6 us -> 28.1 us
    another operation x2 -> x1, other arithmetic: 5.2 us -> 0.22 us  [topo_all_gather(): jnp.stack([pick(in_row, [column, across]), pick(in_row, [across, column])...]
    add x1 -> x0, other arithmetic: 3.93 us -> none  [topo_reduce_scatter(): plane = keep.astype(jnp.float32) + got.astype(jnp.float32)]
    ppermute x3, waiting for transfers between devices: 3.92 us -> 0.01 us  [the longest x1 0.01 us: per_device_dense(): gate_pair = lax.ppermute(gate_mat, 'expert', swap_core)]
    select_n x2 -> x0, other arithmetic: 3.38 us -> none  [place(): stacked = jnp.where(slot == origin, piece[None], stacked)]
    select_n x4, other arithmetic: 1.44 us -> 4.46 us  [pick(): chosen = jnp.where(index == position, options[position], chosen)]
    dot_general x1 -> x2, matrix products: 4.48 us -> 2.04 us  [expert_dense(): lax.dot_general(grad_in, down_mat, against, preferred_element_type=jnp.fl...]
    ppermute x3, starting transfers between devices: 9.04 us -> 6.93 us  [topo_all_gather(): lax.ppermute(ahead, 'expert', [(j, j + 4) for j in range(experts) if step...]
    ppermute x3, starting transfers between devices: 20.1 us -> 22.2 us  [topo_reduce_scatter(): lax.ppermute(ahead.astype(jnp.bfloat16), 'expert', [(j, j + 4) for j in r...]
  transfers between devices with their start and end apart: 29 -> 29, of which waited for: 10 -> 10; matrix products, arithmetic and copies ran while one was open for 6% -> 11% of each run, Pallas kernels for 0% -> 0%
where the time goes in v8:
time: 122 us; the launch traced here: 121 us
  starting transfers between devices  60.3 us (49%)
  waiting for transfers between devices  28.1 us (23%)
  matrix products  16.6 us (14%)
  other arithmetic  9.35 us (8%)
  local copies, waits for them, and re-layouts  5.69 us (5%)
  between operations  1.28 us (1%)
    ppermute x3, starting transfers between devices, topo_reduce_scatter(): lax.ppermute(ahead.astype(jnp.bfloat16), 'expert', [(j, j + 4) for j in r...  22.2 us
    ppermute x7, starting transfers between devices, row_sum(): got = lax.ppermute(theirs.astype(jnp.bfloat16), 'expert', pairs)  11 us
    ppermute x3, waiting for transfers between devices, topo_all_gather(): lax.ppermute(behind, 'expert', [(j, j - 4) for j in range(experts) if 1 <...  9.77 us
    ppermute x3, starting transfers between devices, topo_all_gather(): there.append((lax.ppermute(behind, 'expert', behind_row), line + step))  8.48 us
    ppermute x3, waiting for transfers between devices, topo_reduce_scatter(): lax.ppermute(ahead.astype(jnp.bfloat16), 'expert', [(j, j + 4) for j in r...  7.11 us
    ppermute x3, starting transfers between devices, topo_all_gather(): lax.ppermute(ahead, 'expert', [(j, j + 4) for j in range(experts) if step...  6.93 us
    select_n x4, other arithmetic, pick(): chosen = jnp.where(index == position, options[position], chosen)  4.46 us
    ppermute x3, waiting for transfers between devices, topo_reduce_scatter(): lax.ppermute(behind.astype(jnp.bfloat16), 'expert', [(j, j - 4) for j in...  4.41 us
  transfers between devices with their start and end apart: 29, of which 10 were waited for; matrix products, arithmetic and copies ran while one was open for 11% of the time, Pallas kernels for 0%

profile of v8, /device:TPU:0, one launch (start us, length us, event | category | flops | bytes accessed | tf_op | source)
XLA Modules:
  0.0 121.3 jit_solution(403466935705138519)
XLA Ops:
  2.2 2.0 %fusion.70 = (bf16[32,2048]{1,0:T(8,128)(2,1)S(1)}, f32[32,2048]{1,0:T(8,128)}) fusion(bf16[128,2048]{1,0:T(8,128)(2,1)} %param.11, s32[128]{0:T(128)} %param.12), kind=kOutput, calls=%fused_computation.134 | convolution fusion | flops 16846848 | bytes 918016 | tf_op jit(solution)/shard_map/dot_general | solution.py:211
  4.2 2.0 %fusion.71 = (bf16[32,2048]{1,0:T(8,128)(2,1)S(1)}, f32[32,2048]{1,0:T(8,128)}) fusion(f32[32]{0:T(128)S(1)} %convert_reduce_fusion, bf16[128,2048]{1,0:T(8,128)(2,1)} %param.10, s32[128]{0:T(128)} %param.12), kind=kOutput, calls=%fused_computation.135 | convolution fusion | flops 16912384 | bytes 918144 | tf_op jit(solution)/shard_map/dot_general | solution.py:208
  6.2 1.3 %collective-permute-start = (bf16[32,4224]{1,0:T(8,128)(2,1)S(1)}, bf16[32,4224]{1,0:T(8,128)(2,1)S(1)}, u32[]{:S(2)}, u32[]{:S(2)}) collective-permute-start(bf16[32,4224]{1,0:T(8,128)(2,1)S(1)} %fusion.45), channel_id=1, source_target_pairs={{4,0},{5,1},{6,2},{7,3},{8,4},{9,5},{10,6},{11,7},{12,8},{13,9},{1... | collective-permute-start | bytes 811016 | tf_op jit(solution)/shard_map/ppermute | solution.py:125
  7.5 5.6 %collective-permute-start.3 = (bf16[32,4224]{1,0:T(8,128)(2,1)S(1)}, bf16[32,4224]{1,0:T(8,128)(2,1)S(1)}, u32[]{:S(2)}, u32[]{:S(2)}) collective-permute-start(bf16[32,4224]{1,0:T(8,128)(2,1)S(1)} %fusion.45), channel_id=1, source_target_pairs={{0,4},{1,5},{2,6},{3,7},{4,8},{5,9},{6,10},{7,11},{8,12},{9,13},{1... | collective-permute-start | bytes 811016 | tf_op jit(solution)/shard_map/ppermute | solution.py:120
  13.1 4.5 %collective-permute-done = bf16[32,4224]{1,0:T(8,128)(2,1)S(1)} collective-permute-done((bf16[32,4224]{1,0:T(8,128)(2,1)S(1)}, bf16[32,4224]{1,0:T(8,128)(2,1)S(1)}, u32[]{:S(2)}, u32[]{:S(2)}) %collective-permute-start) | collective-permute-done | bytes 270368 | tf_op jit(solution)/shard_map/ppermute | solution.py:125
  17.6 1.3 %collective-permute-start.1 = (bf16[32,4224]{1,0:T(8,128)(2,1)S(1)}, bf16[32,4224]{1,0:T(8,128)(2,1)S(1)}, u32[]{:S(2)}, u32[]{:S(2)}) collective-permute-start(bf16[32,4224]{1,0:T(8,128)(2,1)S(1)} %collective-permute-done), channel_id=1, source_target_pairs={{4,0},{5,1},{6,2},{7,3},{8,4},{9,5},{10,6},{11,7},{20,16},{21,17},... | collective-permute-start | bytes 811016 | tf_op jit(solution)/shard_map/ppermute | solution.py:125
  19.6 1.7 %collective-permute-start.12 = (bf16[32,4224]{1,0:T(8,128)(2,1)S(1)}, bf16[32,4224]{1,0:T(8,128)(2,1)S(1)}, u32[]{:S(2)}, u32[]{:S(2)}) collective-permute-start(bf16[32,4224]{1,0:T(8,128)(2,1)S(1)} %fusion.45), channel_id=1, source_target_pairs={{0,2},{1,3},{2,0},{3,1},{4,6},{5,7},{6,4},{7,5},{8,10},{9,11},{10,... | collective-permute-start | bytes 811016 | tf_op jit(solution)/shard_map/ppermute | solution.py:117
  21.3 2.2 %collective-permute-start.10 = (bf16[32,4224]{1,0:T(8,128)(2,1)S(1)}, bf16[32,4224]{1,0:T(8,128)(2,1)S(1)}, u32[]{:S(2)}, u32[]{:S(2)}) collective-permute-start(bf16[32,4224]{1,0:T(8,128)(2,1)S(1)} %collective-permute-done), channel_id=1, source_target_pairs={{0,2},{1,3},{2,0},{3,1},{4,6},{5,7},{6,4},{7,5},{8,10},{9,11},{10,... | collective-permute-start | bytes 811016 | tf_op jit(solution)/shard_map/ppermute | solution.py:135
  23.6 3.6 %collective-permute-done.1 = bf16[32,4224]{1,0:T(8,128)(2,1)S(1)} collective-permute-done((bf16[32,4224]{1,0:T(8,128)(2,1)S(1)}, bf16[32,4224]{1,0:T(8,128)(2,1)S(1)}, u32[]{:S(2)}, u32[]{:S(2)}) %collective-permute-start.1) | collective-permute-done | bytes 270368 | tf_op jit(solution)/shard_map/ppermute | solution.py:125
  27.1 1.3 %collective-permute-start.2 = (bf16[32,4224]{1,0:T(8,128)(2,1)S(1)}, bf16[32,4224]{1,0:T(8,128)(2,1)S(1)}, u32[]{:S(2)}, u32[]{:S(2)}) collective-permute-start(bf16[32,4224]{1,0:T(8,128)(2,1)S(1)} %collective-permute-done.1), channel_id=1, source_target_pairs={{4,0},{5,1},{6,2},{7,3},{20,16},{21,17},{22,18},{23,19}} | collective-permute-start | bytes 811016 | tf_op jit(solution)/shard_map/ppermute | solution.py:125
  29.9 3.3 %collective-permute-start.8 = (bf16[32,4224]{1,0:T(8,128)(2,1)S(1)}, bf16[32,4224]{1,0:T(8,128)(2,1)S(1)}, u32[]{:S(2)}, u32[]{:S(2)}) collective-permute-start(bf16[32,4224]{1,0:T(8,128)(2,1)S(1)} %collective-permute-done.1), channel_id=1, source_target_pairs={{0,2},{1,3},{2,0},{3,1},{4,6},{5,7},{6,4},{7,5},{16,18},{17,19},{1... | collective-permute-start | bytes 811016 | tf_op jit(solution)/shard_map/ppermute | solution.py:135
  34.1 1.7 %collective-permute-done.2 = bf16[32,4224]{1,0:T(8,128)(2,1)S(1)} collective-permute-done((bf16[32,4224]{1,0:T(8,128)(2,1)S(1)}, bf16[32,4224]{1,0:T(8,128)(2,1)S(1)}, u32[]{:S(2)}, u32[]{:S(2)}) %collective-permute-start.2) | collective-permute-done | bytes 270368 | tf_op jit(solution)/shard_map/ppermute | solution.py:125
  35.8 3.0 %collective-permute-start.6 = (bf16[32,4224]{1,0:T(8,128)(2,1)S(1)}, bf16[32,4224]{1,0:T(8,128)(2,1)S(1)}, u32[]{:S(2)}, u32[]{:S(2)}) collective-permute-start(bf16[32,4224]{1,0:T(8,128)(2,1)S(1)} %collective-permute-done.2), channel_id=1, source_target_pairs={{0,2},{1,3},{2,0},{3,1},{16,18},{17,19},{18,16},{19,17}} | collective-permute-start | bytes 811016 | tf_op jit(solution)/shard_map/ppermute | solution.py:135
  38.8 1.4 %collective-permute-start.7 = (bf16[32,4224]{1,0:T(8,128)(2,1)S(1)}, bf16[32,4224]{1,0:T(8,128)(2,1)}, u32[]{:S(2)}, u32[]{:S(2)}) collective-permute-start(bf16[32,4224]{1,0:T(8,128)(2,1)S(1)} %collective-permute-done.5), channel_id=1, source_target_pairs={{12,14},{13,15},{14,12},{15,13},{28,30},{29,31},{30,28},{31,29}} | collective-permute-start | bytes 811016 | tf_op jit(solution)/shard_map/ppermute | solution.py:134
  40.8 3.8 %collective-permute-done.6 = bf16[32,4224]{1,0:T(8,128)(2,1)S(1)} collective-permute-done((bf16[32,4224]{1,0:T(8,128)(2,1)S(1)}, bf16[32,4224]{1,0:T(8,128)(2,1)S(1)}, u32[]{:S(2)}, u32[]{:S(2)}) %collective-permute-start.6) | collective-permute-done | bytes 270368 | tf_op jit(solution)/shard_map/ppermute | solution.py:135
  44.7 2.0 %broadcast_select_fusion.1 = bf16[4,1,32,4224]{3,2,1,0:T(8,128)(2,1)S(1)} fusion(pred[]{:T(512)S(6)} %eq.148, bf16[32,4224]{1,0:T(8,128)(2,1)S(1)} %fusion.45, pred[4]{0:T(512)(128)(4,1)S(1)} %get-tuple-element.28, bf16[32,4224]{1,0:T(8,128)(2,1)S(1)} %collective-permute-done.3, pred[4]{0:T(512)(128)(4,1)S(1)} %get-tuple-element.29, ...), kind=kLoop, calls=%fused_computation.26 | loop fusion | flops 8110080 | bytes 4866077 | tf_op jit(solution)/shard_map/jit(_where)/select_n | solution.py:99
  46.7 2.0 %broadcast_select_fusion = bf16[4,1,32,4224]{3,2,1,0:T(8,128)(2,1)S(1)} fusion(pred[]{:T(512)S(6)} %eq.148, bf16[32,4224]{1,0:T(8,128)(2,1)S(1)} %fusion.45, pred[4]{0:T(512)(128)(4,1)S(1)} %get-tuple-element.28, bf16[32,4224]{1,0:T(8,128)(2,1)S(1)} %collective-permute-done.3, pred[4]{0:T(512)(128)(4,1)S(1)} %get-tuple-element.29, ...), kind=kLoop, calls=%fused_computation.25 | loop fusion | flops 8110080 | bytes 4866077 | tf_op jit(solution)/shard_map/jit(_where)/select_n | solution.py:99
  49.3 1.4 %copy-done = bf16[1,2048,768]{2,1,0:T(8,128)(2,1)S(1)} copy-done((bf16[1,2048,768]{2,1,0:T(8,128)(2,1)S(1)}, bf16[1,2048,768]{2,1,0:T(8,128)(2,1)}, u32[]{:S(2)}) %copy-start) | copy-done | bytes 3145752
  64.1 1.2 %fusion.4 = f32[256,2048]{1,0:T(8,128)S(1)} fusion(f32[256,2048]{1,0:T(8,128)S(1)} %fusion.6, f32[256,2048]{1,0:T(8,128)S(1)} %fusion.38, bf16[2048,768]{1,0:T(8,128)(2,1)S(1)} %collective-permute-done.13, f32[256]{0:T(256)S(1)} %get-tuple-element.3, f32[256,768]{1,0:T(8,128)S(1)} %fusion.18, f32[256,768]{1,0:T(8,128)S(1)} %fusion.12, f32[256,768]{1,0:T(8,128)S(1)} %fusion.16), kind=kOutput, calls=%fused_computation.9 | convolution fusion | flops 809893888 | bytes 11797504 | tf_op jit(solution)/shard_map/dot_general | solution.py:192
  66.2 3.3 %collective-permute-start.17 = (bf16[32,4096]{1,0:T(8,128)(2,1)S(1)}, bf16[32,4096]{1,0:T(8,128)(2,1)S(1)}, u32[]{:S(2)}, u32[]{:S(2)}) collective-permute-start(bf16[32,4096]{1,0:T(8,128)(2,1)S(1)} %get-tuple-element.19), channel_id=1, source_target_pairs={{0,2},{1,3},{2,0},{3,1},{16,18},{17,19},{18,16},{19,17}} | collective-permute-start | bytes 786440 | tf_op jit(solution)/shard_map/ppermute | solution.py:157
  70.4 2.6 %collective-permute-start.19 = (bf16[32,4096]{1,0:T(8,128)(2,1)S(1)}, bf16[32,4096]{1,0:T(8,128)(2,1)S(1)}, u32[]{:S(2)}, u32[]{:S(2)}) collective-permute-start(bf16[32,4096]{1,0:T(8,128)(2,1)S(1)} %get-tuple-element.18), channel_id=1, source_target_pairs={{0,2},{1,3},{2,0},{3,1},{4,6},{5,7},{6,4},{7,5},{16,18},{17,19},{1... | collective-permute-start | bytes 786440 | tf_op jit(solution)/shard_map/ppermute | solution.py:157
  73.7 2.6 %collective-permute-done.17 = bf16[32,4096]{1,0:T(8,128)(2,1)S(1)} collective-permute-done((bf16[32,4096]{1,0:T(8,128)(2,1)S(1)}, bf16[32,4096]{1,0:T(8,128)(2,1)S(1)}, u32[]{:S(2)}, u32[]{:S(2)}) %collective-permute-start.17) | collective-permute-done | bytes 262176 | tf_op jit(solution)/shard_map/ppermute | solution.py:157
  76.4 2.8 %collective-permute-start.18 = (bf16[32,4096]{1,0:T(8,128)(2,1)S(1)}, bf16[32,4096]{1,0:T(8,128)(2,1)S(1)}, u32[]{:S(2)}, u32[]{:S(2)}) collective-permute-start(bf16[32,4096]{1,0:T(8,128)(2,1)S(1)} %get-tuple-element.11), channel_id=1, source_target_pairs={{0,4},{1,5},{2,6},{3,7},{16,20},{17,21},{18,22},{19,23}} | collective-permute-start | bytes 786440 | tf_op jit(solution)/shard_map/ppermute | solution.py:165
  79.9 2.7 %collective-permute-start.21 = (bf16[32,4096]{1,0:T(8,128)(2,1)S(1)}, bf16[32,4096]{1,0:T(8,128)(2,1)S(1)}, u32[]{:S(2)}, u32[]{:S(2)}) collective-permute-start(bf16[32,4096]{1,0:T(8,128)(2,1)S(1)} %get-tuple-element.17), channel_id=1, source_target_pairs={{0,2},{1,3},{2,0},{3,1},{4,6},{5,7},{6,4},{7,5},{8,10},{9,11},{10,... | collective-permute-start | bytes 786440 | tf_op jit(solution)/shard_map/ppermute | solution.py:157
  83.3 1.4 %collective-permute-done.18 = bf16[32,4096]{1,0:T(8,128)(2,1)S(1)} collective-permute-done((bf16[32,4096]{1,0:T(8,128)(2,1)S(1)}, bf16[32,4096]{1,0:T(8,128)(2,1)S(1)}, u32[]{:S(2)}, u32[]{:S(2)}) %collective-permute-start.18) | collective-permute-done | bytes 262176 | tf_op jit(solution)/shard_map/ppermute | solution.py:165
  84.9 4.5 %collective-permute-start.20 = (bf16[32,4096]{1,0:T(8,128)(2,1)S(1)}, bf16[32,4096]{1,0:T(8,128)(2,1)S(1)}, u32[]{:S(2)}, u32[]{:S(2)}) collective-permute-start(bf16[32,4096]{1,0:T(8,128)(2,1)S(1)} %get-tuple-element.9), channel_id=1, source_target_pairs={{0,4},{1,5},{2,6},{3,7},{4,8},{5,9},{6,10},{7,11},{16,20},{17,21},... | collective-permute-start | bytes 786440 | tf_op jit(solution)/shard_map/ppermute | solution.py:165
  90.6 3.2 %collective-permute-done.20 = bf16[32,4096]{1,0:T(8,128)(2,1)S(1)} collective-permute-done((bf16[32,4096]{1,0:T(8,128)(2,1)S(1)}, bf16[32,4096]{1,0:T(8,128)(2,1)S(1)}, u32[]{:S(2)}, u32[]{:S(2)}) %collective-permute-start.20) | collective-permute-done | bytes 262176 | tf_op jit(solution)/shard_map/ppermute | solution.py:165
  94.0 14.9 %collective-permute-start.22 = (bf16[32,4096]{1,0:T(8,128)(2,1)S(1)}, bf16[32,4096]{1,0:T(8,128)(2,1)S(1)}, u32[]{:S(2)}, u32[]{:S(2)}) collective-permute-start(bf16[32,4096]{1,0:T(8,128)(2,1)S(1)} %get-tuple-element.7), channel_id=1, source_target_pairs={{0,4},{1,5},{2,6},{3,7},{4,8},{5,9},{6,10},{7,11},{8,12},{9,13},{1... | collective-permute-start | bytes 786440 | tf_op jit(solution)/shard_map/ppermute | solution.py:165
  108.9 1.3 %collective-permute-start.28 = (bf16[32,4096]{1,0:T(8,128)(2,1)S(1)}, bf16[32,4096]{1,0:T(8,128)(2,1)S(1)}, u32[]{:S(2)}, u32[]{:S(2)}) collective-permute-start(bf16[32,4096]{1,0:T(8,128)(2,1)S(1)} %get-tuple-element.8), channel_id=1, source_target_pairs={{4,0},{5,1},{6,2},{7,3},{8,4},{9,5},{10,6},{11,7},{12,8},{13,9},{1... | collective-permute-start | bytes 786440 | tf_op jit(solution)/shard_map/ppermute | solution.py:172
  110.3 2.5 %collective-permute-done.22 = bf16[32,4096]{1,0:T(8,128)(2,1)S(1)} collective-permute-done((bf16[32,4096]{1,0:T(8,128)(2,1)S(1)}, bf16[32,4096]{1,0:T(8,128)(2,1)S(1)}, u32[]{:S(2)}, u32[]{:S(2)}) %collective-permute-start.22) | collective-permute-done | bytes 262176 | tf_op jit(solution)/shard_map/ppermute | solution.py:165
  112.8 4.4 %collective-permute-done.28 = bf16[32,4096]{1,0:T(8,128)(2,1)S(1)} collective-permute-done((bf16[32,4096]{1,0:T(8,128)(2,1)S(1)}, bf16[32,4096]{1,0:T(8,128)(2,1)S(1)}, u32[]{:S(2)}, u32[]{:S(2)}) %collective-permute-start.28) | collective-permute-done | bytes 262176 | tf_op jit(solution)/shard_map/ppermute | solution.py:172
  119.7 1.7 %select_add_fusion = (f32[128,2048]{1,0:T(8,128)}, f32[128,2048]{1,0:T(8,128)}) fusion(f32[128,2048]{1,0:T(8,128)S(1)} %gather_fusion.1, bf16[128,2048]{1,0:T(8,128)(2,1)S(1)} %copy-done.1, pred[128]{0:T(512)(128)(4,1)S(1)} %compare_and_fusion, f32[128,2048]{1,0:T(8,128)S(1)} %gather_fusion, bf16[128,2048]{1,0:T(8,128)(2,1)S(1)} %copy-done.3), kind=kLoop, calls=%fused_computation.27 | loop fusion | flops 1572864 | bytes 5243008 | tf_op jit(solution)/shard_map/add | solution.py:249
  (87 shorter events, 26.9 us)
Async XLA Ops:
  6.2 11.4 %collective-permute-start = (bf16[32,4224]{1,0:T(8,128)(2,1)S(1)}, bf16[32,4224]{1,0:T(8,128)(2,1)S(1)}, u32[]{:S(2)}, u32[]{:S(2)}) collective-permute-start(bf16[32,4224]{1,0:T(8,128)(2,1)S(1)} %fusion.45), channel_id=1, source_target_pairs={{4,0},{5,1},{6,2},{7,3},{8,4},{9,5},{10,6},{11,7},{12,8},{13,9},{1... | collective-permute-start | bytes 811016 | tf_op jit(solution)/shard_map/ppermute | solution.py:125
  7.5 11.4 %collective-permute-start.3 = (bf16[32,4224]{1,0:T(8,128)(2,1)S(1)}, bf16[32,4224]{1,0:T(8,128)(2,1)S(1)}, u32[]{:S(2)}, u32[]{:S(2)}) collective-permute-start(bf16[32,4224]{1,0:T(8,128)(2,1)S(1)} %fusion.45), channel_id=1, source_target_pairs={{0,4},{1,5},{2,6},{3,7},{4,8},{5,9},{6,10},{7,11},{8,12},{9,13},{1... | collective-permute-start | bytes 811016 | tf_op jit(solution)/shard_map/ppermute | solution.py:120
  17.6 9.6 %collective-permute-start.1 = (bf16[32,4224]{1,0:T(8,128)(2,1)S(1)}, bf16[32,4224]{1,0:T(8,128)(2,1)S(1)}, u32[]{:S(2)}, u32[]{:S(2)}) collective-permute-start(bf16[32,4224]{1,0:T(8,128)(2,1)S(1)} %collective-permute-done), channel_id=1, source_target_pairs={{4,0},{5,1},{6,2},{7,3},{8,4},{9,5},{10,6},{11,7},{20,16},{21,17},... | collective-permute-start | bytes 811016 | tf_op jit(solution)/shard_map/ppermute | solution.py:125
  18.9 9.5 %collective-permute-start.4 = (bf16[32,4224]{1,0:T(8,128)(2,1)S(1)}, bf16[32,4224]{1,0:T(8,128)(2,1)S(1)}, u32[]{:S(2)}, u32[]{:S(2)}) collective-permute-start(bf16[32,4224]{1,0:T(8,128)(2,1)S(1)} %collective-permute-done.3), channel_id=1, source_target_pairs={{4,8},{5,9},{6,10},{7,11},{8,12},{9,13},{10,14},{11,15},{20,24},{2... | collective-permute-start | bytes 811016 | tf_op jit(solution)/shard_map/ppermute | solution.py:120
  19.6 10.3 %collective-permute-start.12 = (bf16[32,4224]{1,0:T(8,128)(2,1)S(1)}, bf16[32,4224]{1,0:T(8,128)(2,1)S(1)}, u32[]{:S(2)}, u32[]{:S(2)}) collective-permute-start(bf16[32,4224]{1,0:T(8,128)(2,1)S(1)} %fusion.45), channel_id=1, source_target_pairs={{0,2},{1,3},{2,0},{3,1},{4,6},{5,7},{6,4},{7,5},{8,10},{9,11},{10,... | collective-permute-start | bytes 811016 | tf_op jit(solution)/shard_map/ppermute | solution.py:117
  21.3 12.1 %collective-permute-start.10 = (bf16[32,4224]{1,0:T(8,128)(2,1)S(1)}, bf16[32,4224]{1,0:T(8,128)(2,1)S(1)}, u32[]{:S(2)}, u32[]{:S(2)}) collective-permute-start(bf16[32,4224]{1,0:T(8,128)(2,1)S(1)} %collective-permute-done), channel_id=1, source_target_pairs={{0,2},{1,3},{2,0},{3,1},{4,6},{5,7},{6,4},{7,5},{8,10},{9,11},{10,... | collective-permute-start | bytes 811016 | tf_op jit(solution)/shard_map/ppermute | solution.py:135
  27.1 8.6 %collective-permute-start.2 = (bf16[32,4224]{1,0:T(8,128)(2,1)S(1)}, bf16[32,4224]{1,0:T(8,128)(2,1)S(1)}, u32[]{:S(2)}, u32[]{:S(2)}) collective-permute-start(bf16[32,4224]{1,0:T(8,128)(2,1)S(1)} %collective-permute-done.1), channel_id=1, source_target_pairs={{4,0},{5,1},{6,2},{7,3},{20,16},{21,17},{22,18},{23,19}} | collective-permute-start | bytes 811016 | tf_op jit(solution)/shard_map/ppermute | solution.py:125
  28.4 10.3 %collective-permute-start.5 = (bf16[32,4224]{1,0:T(8,128)(2,1)S(1)}, bf16[32,4224]{1,0:T(8,128)(2,1)S(1)}, u32[]{:S(2)}, u32[]{:S(2)}) collective-permute-start(bf16[32,4224]{1,0:T(8,128)(2,1)S(1)} %collective-permute-done.4), channel_id=1, source_target_pairs={{8,12},{9,13},{10,14},{11,15},{24,28},{25,29},{26,30},{27,31}} | collective-permute-start | bytes 811016 | tf_op jit(solution)/shard_map/ppermute | solution.py:120
  29.2 11.0 %collective-permute-start.11 = (bf16[32,4224]{1,0:T(8,128)(2,1)S(1)}, bf16[32,4224]{1,0:T(8,128)(2,1)S(1)}, u32[]{:S(2)}, u32[]{:S(2)}) collective-permute-start(bf16[32,4224]{1,0:T(8,128)(2,1)S(1)} %collective-permute-done.3), channel_id=1, source_target_pairs={{4,6},{5,7},{6,4},{7,5},{8,10},{9,11},{10,8},{11,9},{12,14},{13,15... | collective-permute-start | bytes 811016 | tf_op jit(solution)/shard_map/ppermute | solution.py:134
  29.9 10.4 %collective-permute-start.8 = (bf16[32,4224]{1,0:T(8,128)(2,1)S(1)}, bf16[32,4224]{1,0:T(8,128)(2,1)S(1)}, u32[]{:S(2)}, u32[]{:S(2)}) collective-permute-start(bf16[32,4224]{1,0:T(8,128)(2,1)S(1)} %collective-permute-done.1), channel_id=1, source_target_pairs={{0,2},{1,3},{2,0},{3,1},{4,6},{5,7},{6,4},{7,5},{16,18},{17,19},{1... | collective-permute-start | bytes 811016 | tf_op jit(solution)/shard_map/ppermute | solution.py:135
  33.4 7.3 %collective-permute-start.9 = (bf16[32,4224]{1,0:T(8,128)(2,1)S(1)}, bf16[32,4224]{1,0:T(8,128)(2,1)S(1)}, u32[]{:S(2)}, u32[]{:S(2)}) collective-permute-start(bf16[32,4224]{1,0:T(8,128)(2,1)S(1)} %collective-permute-done.4), channel_id=1, source_target_pairs={{8,10},{9,11},{10,8},{11,9},{12,14},{13,15},{14,12},{15,13},{24,26... | collective-permute-start | bytes 811016 | tf_op jit(solution)/shard_map/ppermute | solution.py:134
  35.8 8.9 %collective-permute-start.6 = (bf16[32,4224]{1,0:T(8,128)(2,1)S(1)}, bf16[32,4224]{1,0:T(8,128)(2,1)S(1)}, u32[]{:S(2)}, u32[]{:S(2)}) collective-permute-start(bf16[32,4224]{1,0:T(8,128)(2,1)S(1)} %collective-permute-done.2), channel_id=1, source_target_pairs={{0,2},{1,3},{2,0},{3,1},{16,18},{17,19},{18,16},{19,17}} | collective-permute-start | bytes 811016 | tf_op jit(solution)/shard_map/ppermute | solution.py:135
  38.8 5.9 %collective-permute-start.7 = (bf16[32,4224]{1,0:T(8,128)(2,1)S(1)}, bf16[32,4224]{1,0:T(8,128)(2,1)}, u32[]{:S(2)}, u32[]{:S(2)}) collective-permute-start(bf16[32,4224]{1,0:T(8,128)(2,1)S(1)} %collective-permute-done.5), channel_id=1, source_target_pairs={{12,14},{13,15},{14,12},{15,13},{28,30},{29,31},{30,28},{31,29}} | collective-permute-start | bytes 811016 | tf_op jit(solution)/shard_map/ppermute | solution.py:134
  40.2 18.6 %collective-permute-start.14 = (bf16[2048,768]{1,0:T(8,128)(2,1)}, bf16[2048,768]{1,0:T(8,128)(2,1)S(1)}, u32[]{:S(2)}, u32[]{:S(2)}) collective-permute-start(bf16[2048,768]{1,0:T(8,128)(2,1)} %bitcast.79), channel_id=1, source_target_pairs={{0,1},{1,0},{2,3},{3,2},{4,5},{5,4},{6,7},{7,6},{8,9},{9,8},{10,11... | collective-permute-start | bytes 9437192 | tf_op jit(solution)/shard_map/ppermute | solution.py:235
  40.3 19.5 %collective-permute-start.13 = (bf16[2048,768]{1,0:T(8,128)(2,1)}, bf16[2048,768]{1,0:T(8,128)(2,1)S(1)}, u32[]{:S(2)}, u32[]{:S(2)}) collective-permute-start(bf16[2048,768]{1,0:T(8,128)(2,1)} %bitcast.87), channel_id=1, source_target_pairs={{0,1},{1,0},{2,3},{3,2},{4,5},{5,4},{6,7},{7,6},{8,9},{9,8},{10,11... | collective-permute-start | bytes 9437192 | tf_op jit(solution)/shard_map/ppermute | solution.py:234
  40.8 20.1 %collective-permute-start.15 = (bf16[768,2048]{1,0:T(8,128)(2,1)}, bf16[768,2048]{1,0:T(8,128)(2,1)S(1)}, u32[]{:S(2)}, u32[]{:S(2)}) collective-permute-start(bf16[768,2048]{1,0:T(8,128)(2,1)} %bitcast.88), channel_id=1, source_target_pairs={{0,1},{1,0},{2,3},{3,2},{4,5},{5,4},{6,7},{7,6},{8,9},{9,8},{10,11... | collective-permute-start | bytes 9437192 | tf_op jit(solution)/shard_map/ppermute | solution.py:236
  66.2 10.1 %collective-permute-start.17 = (bf16[32,4096]{1,0:T(8,128)(2,1)S(1)}, bf16[32,4096]{1,0:T(8,128)(2,1)S(1)}, u32[]{:S(2)}, u32[]{:S(2)}) collective-permute-start(bf16[32,4096]{1,0:T(8,128)(2,1)S(1)} %get-tuple-element.19), channel_id=1, source_target_pairs={{0,2},{1,3},{2,0},{3,1},{16,18},{17,19},{18,16},{19,17}} | collective-permute-start | bytes 786440 | tf_op jit(solution)/shard_map/ppermute | solution.py:157
  69.5 6.8 %collective-permute-start.23 = (bf16[32,4096]{1,0:T(8,128)(2,1)S(1)}, bf16[32,4096]{1,0:T(8,128)(2,1)S(1)}, u32[]{:S(2)}, u32[]{:S(2)}) collective-permute-start(bf16[32,4096]{1,0:T(8,128)(2,1)S(1)} %get-tuple-element.16), channel_id=1, source_target_pairs={{12,14},{13,15},{14,12},{15,13},{28,30},{29,31},{30,28},{31,29}} | collective-permute-start | bytes 786440 | tf_op jit(solution)/shard_map/ppermute | solution.py:157
  70.4 12.2 %collective-permute-start.19 = (bf16[32,4096]{1,0:T(8,128)(2,1)S(1)}, bf16[32,4096]{1,0:T(8,128)(2,1)S(1)}, u32[]{:S(2)}, u32[]{:S(2)}) collective-permute-start(bf16[32,4096]{1,0:T(8,128)(2,1)S(1)} %get-tuple-element.18), channel_id=1, source_target_pairs={{0,2},{1,3},{2,0},{3,1},{4,6},{5,7},{6,4},{7,5},{16,18},{17,19},{1... | collective-permute-start | bytes 786440 | tf_op jit(solution)/shard_map/ppermute | solution.py:157
  73.0 17.1 %copy-start.5 = (s32[128]{0:T(128)S(1)}, s32[128]{0:T(128)}, u32[]{:S(2)}) copy-start(s32[128]{0:T(128)} %param.12) | copy-start | bytes 1540
  73.0 10.3 %collective-permute-start.25 = (bf16[32,4096]{1,0:T(8,128)(2,1)S(1)}, bf16[32,4096]{1,0:T(8,128)(2,1)S(1)}, u32[]{:S(2)}, u32[]{:S(2)}) collective-permute-start(bf16[32,4096]{1,0:T(8,128)(2,1)S(1)} %get-tuple-element.15), channel_id=1, source_target_pairs={{8,10},{9,11},{10,8},{11,9},{12,14},{13,15},{14,12},{15,13},{24,26... | collective-permute-start | bytes 786440 | tf_op jit(solution)/shard_map/ppermute | solution.py:157
  76.4 8.3 %collective-permute-start.18 = (bf16[32,4096]{1,0:T(8,128)(2,1)S(1)}, bf16[32,4096]{1,0:T(8,128)(2,1)S(1)}, u32[]{:S(2)}, u32[]{:S(2)}) collective-permute-start(bf16[32,4096]{1,0:T(8,128)(2,1)S(1)} %get-tuple-element.11), channel_id=1, source_target_pairs={{0,4},{1,5},{2,6},{3,7},{16,20},{17,21},{18,22},{19,23}} | collective-permute-start | bytes 786440 | tf_op jit(solution)/shard_map/ppermute | solution.py:165
  79.2 5.4 %collective-permute-start.24 = (bf16[32,4096]{1,0:T(8,128)(2,1)S(1)}, bf16[32,4096]{1,0:T(8,128)(2,1)S(1)}, u32[]{:S(2)}, u32[]{:S(2)}) collective-permute-start(bf16[32,4096]{1,0:T(8,128)(2,1)S(1)} %get-tuple-element.12), channel_id=1, source_target_pairs={{12,8},{13,9},{14,10},{15,11},{28,24},{29,25},{30,26},{31,27}} | collective-permute-start | bytes 786440 | tf_op jit(solution)/shard_map/ppermute | solution.py:172
  79.9 10.7 %collective-permute-start.21 = (bf16[32,4096]{1,0:T(8,128)(2,1)S(1)}, bf16[32,4096]{1,0:T(8,128)(2,1)S(1)}, u32[]{:S(2)}, u32[]{:S(2)}) collective-permute-start(bf16[32,4096]{1,0:T(8,128)(2,1)S(1)} %get-tuple-element.17), channel_id=1, source_target_pairs={{0,2},{1,3},{2,0},{3,1},{4,6},{5,7},{6,4},{7,5},{8,10},{9,11},{10,... | collective-permute-start | bytes 786440 | tf_op jit(solution)/shard_map/ppermute | solution.py:157
  82.6 8.0 %collective-permute-start.27 = (bf16[32,4096]{1,0:T(8,128)(2,1)S(1)}, bf16[32,4096]{1,0:T(8,128)(2,1)S(1)}, u32[]{:S(2)}, u32[]{:S(2)}) collective-permute-start(bf16[32,4096]{1,0:T(8,128)(2,1)S(1)} %get-tuple-element.14), channel_id=1, source_target_pairs={{4,6},{5,7},{6,4},{7,5},{8,10},{9,11},{10,8},{11,9},{12,14},{13,15... | collective-permute-start | bytes 786440 | tf_op jit(solution)/shard_map/ppermute | solution.py:157
  84.9 8.9 %collective-permute-start.20 = (bf16[32,4096]{1,0:T(8,128)(2,1)S(1)}, bf16[32,4096]{1,0:T(8,128)(2,1)S(1)}, u32[]{:S(2)}, u32[]{:S(2)}) collective-permute-start(bf16[32,4096]{1,0:T(8,128)(2,1)S(1)} %get-tuple-element.9), channel_id=1, source_target_pairs={{0,4},{1,5},{2,6},{3,7},{4,8},{5,9},{6,10},{7,11},{16,20},{17,21},... | collective-permute-start | bytes 786440 | tf_op jit(solution)/shard_map/ppermute | solution.py:165
  89.4 4.5 %collective-permute-start.26 = (bf16[32,4096]{1,0:T(8,128)(2,1)S(1)}, bf16[32,4096]{1,0:T(8,128)(2,1)S(1)}, u32[]{:S(2)}, u32[]{:S(2)}) collective-permute-start(bf16[32,4096]{1,0:T(8,128)(2,1)S(1)} %get-tuple-element.10), channel_id=1, source_target_pairs={{8,4},{9,5},{10,6},{11,7},{12,8},{13,9},{14,10},{15,11},{24,20},{2... | collective-permute-start | bytes 786440 | tf_op jit(solution)/shard_map/ppermute | solution.py:172
  90.1 27.3 %copy-start.2 = (f32[32,2048]{1,0:T(8,128)S(1)}, f32[32,2048]{1,0:T(8,128)}, u32[]{:S(2)}) copy-start(f32[32,2048]{1,0:T(8,128)} %get-tuple-element.25) | copy-start | bytes 786436
  90.1 27.3 %copy-start.4 = (f32[32,2048]{1,0:T(8,128)S(1)}, f32[32,2048]{1,0:T(8,128)}, u32[]{:S(2)}) copy-start(f32[32,2048]{1,0:T(8,128)} %get-tuple-element.27) | copy-start | bytes 786436
  90.1 20.2 %collective-permute-start.16 = (bf16[32,4096]{1,0:T(8,128)(2,1)S(1)}, bf16[32,4096]{1,0:T(8,128)(2,1)S(1)}, u32[]{:S(2)}, u32[]{:S(2)}) collective-permute-start(bf16[32,4096]{1,0:T(8,128)(2,1)S(1)} %get-tuple-element.13), channel_id=1, source_target_pairs={{0,2},{1,3},{2,0},{3,1},{4,6},{5,7},{6,4},{7,5},{8,10},{9,11},{10,... | collective-permute-start | bytes 786440 | tf_op jit(solution)/shard_map/ppermute | solution.py:157
  94.0 18.8 %collective-permute-start.22 = (bf16[32,4096]{1,0:T(8,128)(2,1)S(1)}, bf16[32,4096]{1,0:T(8,128)(2,1)S(1)}, u32[]{:S(2)}, u32[]{:S(2)}) collective-permute-start(bf16[32,4096]{1,0:T(8,128)(2,1)S(1)} %get-tuple-element.7), channel_id=1, source_target_pairs={{0,4},{1,5},{2,6},{3,7},{4,8},{5,9},{6,10},{7,11},{8,12},{9,13},{1... | collective-permute-start | bytes 786440 | tf_op jit(solution)/shard_map/ppermute | solution.py:165
  108.9 8.3 %collective-permute-start.28 = (bf16[32,4096]{1,0:T(8,128)(2,1)S(1)}, bf16[32,4096]{1,0:T(8,128)(2,1)S(1)}, u32[]{:S(2)}, u32[]{:S(2)}) collective-permute-start(bf16[32,4096]{1,0:T(8,128)(2,1)S(1)} %get-tuple-element.8), channel_id=1, source_target_pairs={{4,0},{5,1},{6,2},{7,3},{8,4},{9,5},{10,6},{11,7},{12,8},{13,9},{1... | collective-permute-start | bytes 786440 | tf_op jit(solution)/shard_map/ppermute | solution.py:172
  (5 other events, 7.9 us)

commit v9 on v8

--- a/solution.py
+++ b/solution.py
@@ -129,10 +129,9 @@
         )
         here.append((ahead, line - step))
         here.append((behind, line + step))
-        ahead_row = [(j, j ^ 2) for j in range(experts) if j // 4 >= step]
-        behind_row = [(j, j ^ 2) for j in range(experts) if j // 4 <= lines - 1 - step]
-        there.append((lax.ppermute(ahead, "expert", ahead_row), line - step))
-        there.append((lax.ppermute(behind, "expert", behind_row), line + step))
+        both = lax.ppermute(jnp.stack([ahead, behind]), "expert", swap_row)
+        there.append((both[0], line - step))
+        there.append((both[1], line + step))
     column = place(here, lines, shard)
     across = place(there, lines, shard)
     in_row = (me // 2) % 2
@@ -150,31 +149,30 @@
     give = pick(in_row, [plane[:, 1], plane[:, 0]])
     line = me // 4
 
-    def row_sum(target, senders):
-        mine = lax.dynamic_index_in_dim(keep, target, 0, keepdims=False)
-        theirs = lax.dynamic_index_in_dim(give, target, 0, keepdims=False)
-        pairs = [(j, j ^ 2) for j in range(experts) if senders(j // 4)]
-        got = lax.ppermute(theirs.astype(jnp.bfloat16), "expert", pairs)
-        return mine + got.astype(jnp.float32)
+    def row_sums(targets):
+        mine = [lax.dynamic_index_in_dim(keep, t, 0, keepdims=False) for t in targets]
+        theirs = jnp.stack([lax.dynamic_index_in_dim(give, t, 0, keepdims=False) for t in targets])
+        pairs = [(j, j ^ 2) for j in range(experts)]
+        got = lax.ppermute(theirs.astype(jnp.bfloat16), "expert", pairs).astype(jnp.float32)
+        return [m + got[i] for i, m in enumerate(mine)]
 
     ahead = jnp.zeros(keep.shape[1:], jnp.float32)
     behind = jnp.zeros(keep.shape[1:], jnp.float32)
     for step in range(1, lines):
-        target = jnp.clip(line + lines - step, 0, lines - 1)
-        ahead = ahead + row_sum(target, lambda z, s=step: z <= s - 1)
+        ahead_target = jnp.clip(line + lines - step, 0, lines - 1)
+        behind_target = jnp.clip(line - lines + step, 0, lines - 1)
+        ahead_part, behind_part = row_sums([ahead_target, behind_target])
         ahead = lax.ppermute(
-            ahead.astype(jnp.bfloat16),
+            (ahead + ahead_part).astype(jnp.bfloat16),
             "expert",
             [(j, j + 4) for j in range(experts) if j // 4 <= step - 1],
         ).astype(jnp.float32)
-        target = jnp.clip(line - lines + step, 0, lines - 1)
-        behind = behind + row_sum(target, lambda z, s=step: z >= lines - s)
         behind = lax.ppermute(
-            behind.astype(jnp.bfloat16),
+            (behind + behind_part).astype(jnp.bfloat16),
             "expert",
             [(j, j - 4) for j in range(experts) if j // 4 >= lines - step],
         ).astype(jnp.float32)
-    return row_sum(line, lambda z: True) + ahead + behind
+    return row_sums([line])[0] + ahead + behind
 
 
 def expert_dense(cent_in, grad_in, gate_mat, up_mat, down_mat):

time: 122 us -> 149 us (1.22)
  waiting for transfers between devices: 28.1 us -> 72.3 us
  starting transfers between devices: 60.3 us -> 37.7 us
  matrix products: 16.6 us -> 20.4 us
  other arithmetic: 9.35 us -> 12.4 us
    ppermute x19 -> x13, waiting for transfers between devices: 18.3 us -> 53.9 us  [the longest x3 24.3 us: topo_all_gather(): both = lax.ppermute(jnp.stack([ahead, behind]), 'expert', swap_row)]
    ppermute x19 -> x13, starting transfers between devices: 47.1 us -> 24.7 us  [the longest x3 12.1 us: topo_reduce_scatter(): lax.ppermute((ahead + ahead_part).astype(jnp.bfloat16), 'expert', [(j, j...]
    ppermute x3, waiting for transfers between devices: 9.77 us -> 16.9 us  [topo_all_gather(): lax.ppermute(behind, 'expert', [(j, j - 4) for j in range(experts) if 1 <...]
    dot_general x2, matrix products: 1.95 us -> 3.9 us  [expert_dense(): up_act = jnp.dot(cent_in, up_mat, preferred_element_type=jnp.float32)]
    dot_general x2, matrix products: 2.15 us -> 3.98 us  [expert_dense(): lax.dot_general(up_grad, up_mat, against, preferred_element_type=jnp.floa...]
    ppermute x3, waiting for transfers between devices: 0.01 us -> 1.51 us  [topo_all_gather(): lax.ppermute(ahead, 'expert', [(j, j + 4) for j in range(experts) if step...]
    unnamed x17 -> x15, local copies, waits for them, and re-layouts: 3.54 us -> 2.44 us
  transfers between devices with their start and end apart: 29 -> 23, of which waited for: 10 -> 12; matrix products, arithmetic and copies ran while one was open for 11% -> 12% of each run, Pallas kernels for 0% -> 0%
where the time goes in v9:
time: 149 us
  waiting for transfers between devices  72.3 us (49%)
  starting transfers between devices  37.7 us (25%)
  matrix products  20.4 us (14%)
  other arithmetic  12.4 us (8%)
  local copies, waits for them, and re-layouts  4.68 us (3%)
    ppermute x3, waiting for transfers between devices, topo_all_gather(): both = lax.ppermute(jnp.stack([ahead, behind]), 'expert', swap_row)  24.3 us
    ppermute x4, waiting for transfers between devices, row_sums(): lax.ppermute(theirs.astype(jnp.bfloat16), 'expert', pairs)  22.7 us
    ppermute x3, waiting for transfers between devices, topo_all_gather(): lax.ppermute(behind, 'expert', [(j, j - 4) for j in range(experts) if 1 <...  16.9 us
    ppermute x3, starting transfers between devices, topo_reduce_scatter(): lax.ppermute((ahead + ahead_part).astype(jnp.bfloat16), 'expert', [(j, j...  12.1 us
    ppermute x3, starting transfers between devices, topo_all_gather(): lax.ppermute(ahead, 'expert', [(j, j + 4) for j in range(experts) if step...  6.97 us
    ppermute x4, starting transfers between devices, row_sums(): lax.ppermute(theirs.astype(jnp.bfloat16), 'expert', pairs)  5.32 us
    select_n x4, other arithmetic, pick(): chosen = jnp.where(index == position, options[position], chosen)  4.85 us
    ppermute x3, starting transfers between devices, topo_all_gather(): both = lax.ppermute(jnp.stack([ahead, behind]), 'expert', swap_row)  4.62 us
  transfers between devices with their start and end apart: 23, of which 12 were waited for; matrix products, arithmetic and copies ran while one was open for 12% of the time, Pallas kernels for 0%

profile of v9, /device:TPU:0, one launch (start us, length us, event | category | flops | bytes accessed | tf_op | source)
XLA Modules:
  0.0 148.8 jit_solution(6508782477684513779)
XLA Ops:
  2.2 2.0 %fusion.75 = (bf16[32,2048]{1,0:T(8,128)(2,1)S(1)}, f32[32,2048]{1,0:T(8,128)}) fusion(bf16[128,2048]{1,0:T(8,128)(2,1)} %param.11, s32[128]{0:T(128)} %param.12), kind=kOutput, calls=%fused_computation.152 | convolution fusion | flops 16846848 | bytes 918016 | tf_op jit(solution)/shard_map/dot_general | solution.py:209
  4.2 2.0 %fusion.76 = (bf16[32,2048]{1,0:T(8,128)(2,1)S(1)}, f32[32,2048]{1,0:T(8,128)}) fusion(f32[32]{0:T(128)S(1)} %convert_reduce_fusion, bf16[128,2048]{1,0:T(8,128)(2,1)} %param.10, s32[128]{0:T(128)} %param.12), kind=kOutput, calls=%fused_computation.153 | convolution fusion | flops 16912384 | bytes 918144 | tf_op jit(solution)/shard_map/dot_general | solution.py:206
  6.2 5.6 %collective-permute-start.3 = (bf16[32,4224]{1,0:T(8,128)(2,1)S(1)}, bf16[32,4224]{1,0:T(8,128)(2,1)}, u32[]{:S(2)}, u32[]{:S(2)}) collective-permute-start(bf16[32,4224]{1,0:T(8,128)(2,1)S(1)} %fusion.48), channel_id=1, source_target_pairs={{0,4},{1,5},{2,6},{3,7},{4,8},{5,9},{6,10},{7,11},{8,12},{9,13},{1... | collective-permute-start | bytes 811016 | tf_op jit(solution)/shard_map/ppermute | solution.py:120
  13.1 1.6 %collective-permute-start.9 = (bf16[32,4224]{1,0:T(8,128)(2,1)S(1)}, bf16[32,4224]{1,0:T(8,128)(2,1)}, u32[]{:S(2)}, u32[]{:S(2)}) collective-permute-start(bf16[32,4224]{1,0:T(8,128)(2,1)S(1)} %fusion.48), channel_id=1, source_target_pairs={{0,2},{1,3},{2,0},{3,1},{4,6},{5,7},{6,4},{7,5},{8,10},{9,11},{10,... | collective-permute-start | bytes 811016 | tf_op jit(solution)/shard_map/ppermute | solution.py:117
  15.3 1.5 %collective-permute-done.3 = bf16[32,4224]{1,0:T(8,128)(2,1)} collective-permute-done((bf16[32,4224]{1,0:T(8,128)(2,1)S(1)}, bf16[32,4224]{1,0:T(8,128)(2,1)}, u32[]{:S(2)}, u32[]{:S(2)}) %collective-permute-start.3) | collective-permute-done | bytes 270368 | tf_op jit(solution)/shard_map/ppermute | solution.py:120
  17.5 4.2 %collective-permute-done = bf16[32,4224]{1,0:T(8,128)(2,1)} collective-permute-done((bf16[32,4224]{1,0:T(8,128)(2,1)S(1)}, bf16[32,4224]{1,0:T(8,128)(2,1)}, u32[]{:S(2)}, u32[]{:S(2)}) %collective-permute-start) | collective-permute-done | bytes 270368 | tf_op jit(solution)/shard_map/ppermute | solution.py:125
  24.2 1.6 %collective-permute-start.8 = (bf16[2,32,4224]{2,1,0:T(8,128)(2,1)S(1)}, bf16[2,32,4224]{2,1,0:T(8,128)(2,1)S(1)}, u32[]{:S(2)}, u32[]{:S(2)}) collective-permute-start(bf16[2,32,4224]{2,1,0:T(8,128)(2,1)S(1)} %pad_maximum_fusion.4), channel_id=1, source_target_pairs={{0,2},{1,3},{2,0},{3,1},{4,6},{5,7},{6,4},{7,5},{8,10},{9,11},{10,... | collective-permute-start | bytes 1622024 | tf_op jit(solution)/shard_map/ppermute | solution.py:132
  25.7 5.1 %collective-permute-done.1 = bf16[32,4224]{1,0:T(8,128)(2,1)S(1)} collective-permute-done((bf16[32,4224]{1,0:T(8,128)(2,1)}, bf16[32,4224]{1,0:T(8,128)(2,1)S(1)}, u32[]{:S(2)}, u32[]{:S(2)}) %collective-permute-start.1) | collective-permute-done | bytes 270368 | tf_op jit(solution)/shard_map/ppermute | solution.py:125
  31.6 5.4 %collective-permute-done.8 = bf16[2,32,4224]{2,1,0:T(8,128)(2,1)S(1)} collective-permute-done((bf16[2,32,4224]{2,1,0:T(8,128)(2,1)S(1)}, bf16[2,32,4224]{2,1,0:T(8,128)(2,1)S(1)}, u32[]{:S(2)}, u32[]{:S(2)}) %collective-permute-start.8) | collective-permute-done | bytes 540704 | tf_op jit(solution)/shard_map/ppermute | solution.py:132
  38.5 7.5 %collective-permute-done.2 = bf16[32,4224]{1,0:T(8,128)(2,1)S(1)} collective-permute-done((bf16[32,4224]{1,0:T(8,128)(2,1)S(1)}, bf16[32,4224]{1,0:T(8,128)(2,1)S(1)}, u32[]{:S(2)}, u32[]{:S(2)}) %collective-permute-start.2) | collective-permute-done | bytes 270368 | tf_op jit(solution)/shard_map/ppermute | solution.py:125
  46.0 1.5 %collective-permute-start.7 = (bf16[2,32,4224]{2,1,0:T(8,128)(2,1)S(1)}, bf16[2,32,4224]{2,1,0:T(8,128)(2,1)S(1)}, u32[]{:S(2)}, u32[]{:S(2)}) collective-permute-start(bf16[2,32,4224]{2,1,0:T(8,128)(2,1)S(1)} %pad_maximum_fusion.3), channel_id=1, source_target_pairs={{0,2},{1,3},{2,0},{3,1},{4,6},{5,7},{6,4},{7,5},{8,10},{9,11},{10,... | collective-permute-start | bytes 1622024 | tf_op jit(solution)/shard_map/ppermute | solution.py:132
  47.6 10.9 %collective-permute-done.7 = bf16[2,32,4224]{2,1,0:T(8,128)(2,1)S(1)} collective-permute-done((bf16[2,32,4224]{2,1,0:T(8,128)(2,1)S(1)}, bf16[2,32,4224]{2,1,0:T(8,128)(2,1)S(1)}, u32[]{:S(2)}, u32[]{:S(2)}) %collective-permute-start.7) | collective-permute-done | bytes 540704 | tf_op jit(solution)/shard_map/ppermute | solution.py:132
  58.5 1.5 %collective-permute-start.6 = (bf16[2,32,4224]{2,1,0:T(8,128)(2,1)S(1)}, bf16[2,32,4224]{2,1,0:T(8,128)(2,1)S(1)}, u32[]{:S(2)}, u32[]{:S(2)}) collective-permute-start(bf16[2,32,4224]{2,1,0:T(8,128)(2,1)S(1)} %pad_maximum_fusion.2), channel_id=1, source_target_pairs={{0,2},{1,3},{2,0},{3,1},{4,6},{5,7},{6,4},{7,5},{8,10},{9,11},{10,... | collective-permute-start | bytes 1622024 | tf_op jit(solution)/shard_map/ppermute | solution.py:132
  60.0 8.0 %collective-permute-done.6 = bf16[2,32,4224]{2,1,0:T(8,128)(2,1)S(1)} collective-permute-done((bf16[2,32,4224]{2,1,0:T(8,128)(2,1)S(1)}, bf16[2,32,4224]{2,1,0:T(8,128)(2,1)S(1)}, u32[]{:S(2)}, u32[]{:S(2)}) %collective-permute-start.6) | collective-permute-done | bytes 540704 | tf_op jit(solution)/shard_map/ppermute | solution.py:132
  68.1 2.2 %broadcast_select_fusion.1 = bf16[4,1,32,4224]{3,2,1,0:T(8,128)(2,1)S(1)} fusion(pred[]{:T(512)S(6)} %eq.148, bf16[32,4224]{1,0:T(8,128)(2,1)S(1)} %fusion.48, pred[4]{0:T(512)(128)(4,1)S(1)} %get-tuple-element.34, bf16[32,4224]{1,0:T(8,128)(2,1)} %collective-permute-done.3, pred[4]{0:T(512)(128)(4,1)S(1)} %get-tuple-element.35, ...), kind=kLoop, calls=%fused_computation.26 | loop fusion | flops 8110080 | bytes 4866077 | tf_op jit(solution)/shard_map/jit(_where)/select_n | solution.py:99
  70.3 2.3 %broadcast_select_fusion = bf16[4,1,32,4224]{3,2,1,0:T(8,128)(2,1)S(1)} fusion(pred[]{:T(512)S(6)} %eq.148, bf16[32,4224]{1,0:T(8,128)(2,1)S(1)} %fusion.48, pred[4]{0:T(512)(128)(4,1)S(1)} %get-tuple-element.34, bf16[32,4224]{1,0:T(8,128)(2,1)} %collective-permute-done.3, pred[4]{0:T(512)(128)(4,1)S(1)} %get-tuple-element.35, ...), kind=kLoop, calls=%fused_computation.25 | loop fusion | flops 8110080 | bytes 4866077 | tf_op jit(solution)/shard_map/jit(_where)/select_n | solution.py:99
  73.0 1.4 copy-done
  81.6 2.9 %fusion.16 = f32[256,768]{1,0:T(8,128)S(1)} fusion(bf16[2048,768]{1,0:T(8,128)(2,1)} %collective-permute-done.11, bf16[256,4224]{1,0:T(8,128)(2,1)S(1)} %bitcast.120), kind=kOutput, calls=%fused_computation.41 | convolution fusion | flops 805306368 | bytes 4980736 | tf_op jit(solution)/shard_map/dot_general | solution.py:181
  86.6 2.9 %fusion.41 = f32[256,2048]{1,0:T(8,128)S(1)} fusion(bf16[2048,768]{1,0:T(8,128)(2,1)} %collective-permute-done.11, f32[256,768]{1,0:T(8,128)S(1)} %fusion.12, f32[256,768]{1,0:T(8,128)S(1)} %fusion.18), kind=kOutput, calls=%fused_computation.88 | convolution fusion | flops 806486016 | bytes 6815744 | tf_op jit(solution)/shard_map/dot_general | solution.py:191
  92.8 1.6 %collective-permute-start.14 = (bf16[2,32,4096]{2,1,0:T(8,128)(2,1)S(1)}, bf16[2,32,4096]{2,1,0:T(8,128)(2,1)S(1)}, u32[]{:S(2)}, u32[]{:S(2)}) collective-permute-start(bf16[2,32,4096]{2,1,0:T(8,128)(2,1)S(1)} %pad_maximum_fusion.5), channel_id=1, source_target_pairs={{0,2},{1,3},{2,0},{3,1},{4,6},{5,7},{6,4},{7,5},{8,10},{9,11},{10,... | collective-permute-start | bytes 1572872 | tf_op jit(solution)/shard_map/ppermute | solution.py:156
  95.2 12.5 %collective-permute-done.14 = bf16[2,32,4096]{2,1,0:T(8,128)(2,1)S(1)} collective-permute-done((bf16[2,32,4096]{2,1,0:T(8,128)(2,1)S(1)}, bf16[2,32,4096]{2,1,0:T(8,128)(2,1)S(1)}, u32[]{:S(2)}, u32[]{:S(2)}) %collective-permute-start.14) | collective-permute-done | bytes 524320 | tf_op jit(solution)/shard_map/ppermute | solution.py:156
  107.9 1.9 %collective-permute-start.15 = (bf16[32,4096]{1,0:T(8,128)(2,1)S(1)}, bf16[32,4096]{1,0:T(8,128)(2,1)S(1)}, u32[]{:S(2)}, u32[]{:S(2)}) collective-permute-start(bf16[32,4096]{1,0:T(8,128)(2,1)S(1)} %get-tuple-element.11), channel_id=1, source_target_pairs={{0,4},{1,5},{2,6},{3,7},{16,20},{17,21},{18,22},{19,23}} | collective-permute-start | bytes 786440 | tf_op jit(solution)/shard_map/ppermute | solution.py:165
  110.6 1.6 %collective-permute-start.18 = (bf16[2,32,4096]{2,1,0:T(8,128)(2,1)S(1)}, bf16[2,32,4096]{2,1,0:T(8,128)(2,1)S(1)}, u32[]{:S(2)}, u32[]{:S(2)}) collective-permute-start(bf16[2,32,4096]{2,1,0:T(8,128)(2,1)S(1)} %pad_maximum_fusion.7), channel_id=1, source_target_pairs={{0,2},{1,3},{2,0},{3,1},{4,6},{5,7},{6,4},{7,5},{8,10},{9,11},{10,... | collective-permute-start | bytes 1572872 | tf_op jit(solution)/shard_map/ppermute | solution.py:156
  112.2 6.7 %collective-permute-done.16 = bf16[2,32,4096]{2,1,0:T(8,128)(2,1)S(1)} collective-permute-done((bf16[2,32,4096]{2,1,0:T(8,128)(2,1)S(1)}, bf16[2,32,4096]{2,1,0:T(8,128)(2,1)S(1)}, u32[]{:S(2)}, u32[]{:S(2)}) %collective-permute-start.16) | collective-permute-done | bytes 524320 | tf_op jit(solution)/shard_map/ppermute | solution.py:156
  119.2 1.4 collective-permute-start.17
  121.4 1.6 %collective-permute-start.13 = (bf16[1,32,4096]{2,1,0:T(8,128)(2,1)S(1)}, bf16[1,32,4096]{2,1,0:T(8,128)(2,1)S(1)}, u32[]{:S(2)}, u32[]{:S(2)}) collective-permute-start(bf16[1,32,4096]{2,1,0:T(8,128)(2,1)S(1)} %get-tuple-element.13), channel_id=1, source_target_pairs={{0,2},{1,3},{2,0},{3,1},{4,6},{5,7},{6,4},{7,5},{8,10},{9,11},{10,... | collective-permute-start | bytes 786440 | tf_op jit(solution)/shard_map/ppermute | solution.py:156
  123.0 3.5 %collective-permute-done.18 = bf16[2,32,4096]{2,1,0:T(8,128)(2,1)S(1)} collective-permute-done((bf16[2,32,4096]{2,1,0:T(8,128)(2,1)S(1)}, bf16[2,32,4096]{2,1,0:T(8,128)(2,1)S(1)}, u32[]{:S(2)}, u32[]{:S(2)}) %collective-permute-start.18) | collective-permute-done | bytes 524320 | tf_op jit(solution)/shard_map/ppermute | solution.py:156
  126.7 8.8 %collective-permute-start.19 = (bf16[32,4096]{1,0:T(8,128)(2,1)S(1)}, bf16[32,4096]{1,0:T(8,128)(2,1)S(1)}, u32[]{:S(2)}, u32[]{:S(2)}) collective-permute-start(bf16[32,4096]{1,0:T(8,128)(2,1)S(1)} %get-tuple-element.7), channel_id=1, source_target_pairs={{0,4},{1,5},{2,6},{3,7},{4,8},{5,9},{6,10},{7,11},{8,12},{9,13},{1... | collective-permute-start | bytes 786440 | tf_op jit(solution)/shard_map/ppermute | solution.py:165
  135.5 1.3 collective-permute-start.22
  136.9 2.5 %collective-permute-done.19 = bf16[32,4096]{1,0:T(8,128)(2,1)S(1)} collective-permute-done((bf16[32,4096]{1,0:T(8,128)(2,1)S(1)}, bf16[32,4096]{1,0:T(8,128)(2,1)S(1)}, u32[]{:S(2)}, u32[]{:S(2)}) %collective-permute-start.19) | collective-permute-done | bytes 262176 | tf_op jit(solution)/shard_map/ppermute | solution.py:165
  139.4 4.4 %collective-permute-done.22 = bf16[32,4096]{1,0:T(8,128)(2,1)S(1)} collective-permute-done((bf16[32,4096]{1,0:T(8,128)(2,1)S(1)}, bf16[32,4096]{1,0:T(8,128)(2,1)S(1)}, u32[]{:S(2)}, u32[]{:S(2)}) %collective-permute-start.22) | collective-permute-done | bytes 262176 | tf_op jit(solution)/shard_map/ppermute | solution.py:170
  146.1 2.7 %select_add_fusion = (f32[128,2048]{1,0:T(8,128)}, f32[128,2048]{1,0:T(8,128)}) fusion(f32[128,2048]{1,0:T(8,128)S(1)} %gather_fusion.1, bf16[128,2048]{1,0:T(8,128)(2,1)S(1)} %copy-done.1, pred[128]{0:T(512)(128)(4,1)S(1)} %compare_and_fusion, f32[128,2048]{1,0:T(8,128)S(1)} %gather_fusion, bf16[128,2048]{1,0:T(8,128)(2,1)} %param.10), kind=kLoop, calls=%fused_computation.27 | loop fusion | flops 1572864 | bytes 5243008 | tf_op jit(solution)/shard_map/add | solution.py:247
  (85 shorter events, 26.9 us)
Async XLA Ops:
  6.2 10.7 %collective-permute-start.3 = (bf16[32,4224]{1,0:T(8,128)(2,1)S(1)}, bf16[32,4224]{1,0:T(8,128)(2,1)}, u32[]{:S(2)}, u32[]{:S(2)}) collective-permute-start(bf16[32,4224]{1,0:T(8,128)(2,1)S(1)} %fusion.48), channel_id=1, source_target_pairs={{0,4},{1,5},{2,6},{3,7},{4,8},{5,9},{6,10},{7,11},{8,12},{9,13},{1... | collective-permute-start | bytes 811016 | tf_op jit(solution)/shard_map/ppermute | solution.py:120
  11.8 9.9 %collective-permute-start = (bf16[32,4224]{1,0:T(8,128)(2,1)S(1)}, bf16[32,4224]{1,0:T(8,128)(2,1)}, u32[]{:S(2)}, u32[]{:S(2)}) collective-permute-start(bf16[32,4224]{1,0:T(8,128)(2,1)S(1)} %fusion.48), channel_id=1, source_target_pairs={{4,0},{5,1},{6,2},{7,3},{8,4},{9,5},{10,6},{11,7},{12,8},{13,9},{1... | collective-permute-start | bytes 811016 | tf_op jit(solution)/shard_map/ppermute | solution.py:125
  13.1 55.0 %collective-permute-start.9 = (bf16[32,4224]{1,0:T(8,128)(2,1)S(1)}, bf16[32,4224]{1,0:T(8,128)(2,1)}, u32[]{:S(2)}, u32[]{:S(2)}) collective-permute-start(bf16[32,4224]{1,0:T(8,128)(2,1)S(1)} %fusion.48), channel_id=1, source_target_pairs={{0,2},{1,3},{2,0},{3,1},{4,6},{5,7},{6,4},{7,5},{8,10},{9,11},{10,... | collective-permute-start | bytes 811016 | tf_op jit(solution)/shard_map/ppermute | solution.py:117
  14.7 66.9 %collective-permute-start.11 = (bf16[2048,768]{1,0:T(8,128)(2,1)}, bf16[2048,768]{1,0:T(8,128)(2,1)}, u32[]{:S(2)}, u32[]{:S(2)}) collective-permute-start(bf16[2048,768]{1,0:T(8,128)(2,1)} %bitcast.111), channel_id=1, source_target_pairs={{0,1},{1,0},{2,3},{3,2},{4,5},{5,4},{6,7},{7,6},{8,9},{9,8},{10,11... | collective-permute-start | bytes 9437192 | tf_op jit(solution)/shard_map/ppermute | solution.py:233
  14.7 69.8 %collective-permute-start.10 = (bf16[2048,768]{1,0:T(8,128)(2,1)}, bf16[2048,768]{1,0:T(8,128)(2,1)S(1)}, u32[]{:S(2)}, u32[]{:S(2)}) collective-permute-start(bf16[2048,768]{1,0:T(8,128)(2,1)} %bitcast.123), channel_id=1, source_target_pairs={{0,1},{1,0},{2,3},{3,2},{4,5},{5,4},{6,7},{7,6},{8,9},{9,8},{10,11... | collective-permute-start | bytes 9437192 | tf_op jit(solution)/shard_map/ppermute | solution.py:232
  15.3 23.1 %copy-start.6 = (bf16[1,768,2048]{2,1,0:T(8,128)(2,1)S(1)}, bf16[1,768,2048]{2,1,0:T(8,128)(2,1)}, u32[]{:S(2)}) copy-start(bf16[1,768,2048]{2,1,0:T(8,128)(2,1)} %param.17) | copy-start | bytes 9437188
  16.9 7.3 %collective-permute-start.4 = (bf16[32,4224]{1,0:T(8,128)(2,1)}, bf16[32,4224]{1,0:T(8,128)(2,1)S(1)}, u32[]{:S(2)}, u32[]{:S(2)}) collective-permute-start(bf16[32,4224]{1,0:T(8,128)(2,1)} %collective-permute-done.3), channel_id=1, source_target_pairs={{4,8},{5,9},{6,10},{7,11},{8,12},{9,13},{10,14},{11,15},{20,24},{2... | collective-permute-start | bytes 811016 | tf_op jit(solution)/shard_map/ppermute | solution.py:120
  21.8 9.1 %collective-permute-start.1 = (bf16[32,4224]{1,0:T(8,128)(2,1)}, bf16[32,4224]{1,0:T(8,128)(2,1)S(1)}, u32[]{:S(2)}, u32[]{:S(2)}) collective-permute-start(bf16[32,4224]{1,0:T(8,128)(2,1)} %collective-permute-done), channel_id=1, source_target_pairs={{4,0},{5,1},{6,2},{7,3},{8,4},{9,5},{10,6},{11,7},{20,16},{21,17},... | collective-permute-start | bytes 811016 | tf_op jit(solution)/shard_map/ppermute | solution.py:125
  24.2 12.9 %collective-permute-start.8 = (bf16[2,32,4224]{2,1,0:T(8,128)(2,1)S(1)}, bf16[2,32,4224]{2,1,0:T(8,128)(2,1)S(1)}, u32[]{:S(2)}, u32[]{:S(2)}) collective-permute-start(bf16[2,32,4224]{2,1,0:T(8,128)(2,1)S(1)} %pad_maximum_fusion.4), channel_id=1, source_target_pairs={{0,2},{1,3},{2,0},{3,1},{4,6},{5,7},{6,4},{7,5},{8,10},{9,11},{10,... | collective-permute-start | bytes 1622024 | tf_op jit(solution)/shard_map/ppermute | solution.py:132
  30.9 7.5 %collective-permute-start.5 = (bf16[32,4224]{1,0:T(8,128)(2,1)S(1)}, bf16[32,4224]{1,0:T(8,128)(2,1)S(1)}, u32[]{:S(2)}, u32[]{:S(2)}) collective-permute-start(bf16[32,4224]{1,0:T(8,128)(2,1)S(1)} %collective-permute-done.4), channel_id=1, source_target_pairs={{8,12},{9,13},{10,14},{11,15},{24,28},{25,29},{26,30},{27,31}} | collective-permute-start | bytes 811016 | tf_op jit(solution)/shard_map/ppermute | solution.py:120
  37.0 9.0 %collective-permute-start.2 = (bf16[32,4224]{1,0:T(8,128)(2,1)S(1)}, bf16[32,4224]{1,0:T(8,128)(2,1)S(1)}, u32[]{:S(2)}, u32[]{:S(2)}) collective-permute-start(bf16[32,4224]{1,0:T(8,128)(2,1)S(1)} %collective-permute-done.1), channel_id=1, source_target_pairs={{4,0},{5,1},{6,2},{7,3},{20,16},{21,17},{22,18},{23,19}} | collective-permute-start | bytes 811016 | tf_op jit(solution)/shard_map/ppermute | solution.py:125
  38.4 47.1 %collective-permute-start.12 = (bf16[768,2048]{1,0:T(8,128)(2,1)S(1)}, bf16[768,2048]{1,0:T(8,128)(2,1)S(1)}, u32[]{:S(2)}, u32[]{:S(2)}) collective-permute-start(bf16[768,2048]{1,0:T(8,128)(2,1)S(1)} %bitcast.124), channel_id=1, source_target_pairs={{0,1},{1,0},{2,3},{3,2},{4,5},{5,4},{6,7},{7,6},{8,9},{9,8},{10,11... | collective-permute-start | bytes 9437192 | tf_op jit(solution)/shard_map/ppermute | solution.py:234
  46.0 12.4 %collective-permute-start.7 = (bf16[2,32,4224]{2,1,0:T(8,128)(2,1)S(1)}, bf16[2,32,4224]{2,1,0:T(8,128)(2,1)S(1)}, u32[]{:S(2)}, u32[]{:S(2)}) collective-permute-start(bf16[2,32,4224]{2,1,0:T(8,128)(2,1)S(1)} %pad_maximum_fusion.3), channel_id=1, source_target_pairs={{0,2},{1,3},{2,0},{3,1},{4,6},{5,7},{6,4},{7,5},{8,10},{9,11},{10,... | collective-permute-start | bytes 1622024 | tf_op jit(solution)/shard_map/ppermute | solution.py:132
  58.5 9.6 %collective-permute-start.6 = (bf16[2,32,4224]{2,1,0:T(8,128)(2,1)S(1)}, bf16[2,32,4224]{2,1,0:T(8,128)(2,1)S(1)}, u32[]{:S(2)}, u32[]{:S(2)}) collective-permute-start(bf16[2,32,4224]{2,1,0:T(8,128)(2,1)S(1)} %pad_maximum_fusion.2), channel_id=1, source_target_pairs={{0,2},{1,3},{2,0},{3,1},{4,6},{5,7},{6,4},{7,5},{8,10},{9,11},{10,... | collective-permute-start | bytes 1622024 | tf_op jit(solution)/shard_map/ppermute | solution.py:132
  72.5 1.9 %copy-start = (bf16[1,2048,768]{2,1,0:T(8,128)(2,1)S(1)}, bf16[1,2048,768]{2,1,0:T(8,128)(2,1)}, u32[]{:S(2)}) copy-start(bf16[1,2048,768]{2,1,0:T(8,128)(2,1)} %param.16) | copy-start | bytes 9437188
  74.4 1.9 %copy-start.5 = (bf16[1,2048,768]{2,1,0:T(8,128)(2,1)S(1)}, bf16[1,2048,768]{2,1,0:T(8,128)(2,1)}, u32[]{:S(2)}) copy-start(bf16[1,2048,768]{2,1,0:T(8,128)(2,1)} %param.15) | copy-start | bytes 9437188
  92.8 14.9 %collective-permute-start.14 = (bf16[2,32,4096]{2,1,0:T(8,128)(2,1)S(1)}, bf16[2,32,4096]{2,1,0:T(8,128)(2,1)S(1)}, u32[]{:S(2)}, u32[]{:S(2)}) collective-permute-start(bf16[2,32,4096]{2,1,0:T(8,128)(2,1)S(1)} %pad_maximum_fusion.5), channel_id=1, source_target_pairs={{0,2},{1,3},{2,0},{3,1},{4,6},{5,7},{6,4},{7,5},{8,10},{9,11},{10,... | collective-permute-start | bytes 1572872 | tf_op jit(solution)/shard_map/ppermute | solution.py:156
  94.4 24.5 %collective-permute-start.16 = (bf16[2,32,4096]{2,1,0:T(8,128)(2,1)S(1)}, bf16[2,32,4096]{2,1,0:T(8,128)(2,1)S(1)}, u32[]{:S(2)}, u32[]{:S(2)}) collective-permute-start(bf16[2,32,4096]{2,1,0:T(8,128)(2,1)S(1)} %pad_maximum_fusion.6), channel_id=1, source_target_pairs={{0,2},{1,3},{2,0},{3,1},{4,6},{5,7},{6,4},{7,5},{8,10},{9,11},{10,... | collective-permute-start | bytes 1572872 | tf_op jit(solution)/shard_map/ppermute | solution.py:156
  107.9 11.1 %collective-permute-start.15 = (bf16[32,4096]{1,0:T(8,128)(2,1)S(1)}, bf16[32,4096]{1,0:T(8,128)(2,1)S(1)}, u32[]{:S(2)}, u32[]{:S(2)}) collective-permute-start(bf16[32,4096]{1,0:T(8,128)(2,1)S(1)} %get-tuple-element.11), channel_id=1, source_target_pairs={{0,4},{1,5},{2,6},{3,7},{16,20},{17,21},{18,22},{19,23}} | collective-permute-start | bytes 786440 | tf_op jit(solution)/shard_map/ppermute | solution.py:165
  109.9 9.2 %collective-permute-start.20 = (bf16[32,4096]{1,0:T(8,128)(2,1)S(1)}, bf16[32,4096]{1,0:T(8,128)(2,1)S(1)}, u32[]{:S(2)}, u32[]{:S(2)}) collective-permute-start(bf16[32,4096]{1,0:T(8,128)(2,1)S(1)} %get-tuple-element.12), channel_id=1, source_target_pairs={{12,8},{13,9},{14,10},{15,11},{28,24},{29,25},{30,26},{31,27}} | collective-permute-start | bytes 786440 | tf_op jit(solution)/shard_map/ppermute | solution.py:170
  110.6 10.8 %copy-start.4 = (s32[128]{0:T(128)S(1)}, s32[128]{0:T(128)}, u32[]{:S(2)}) copy-start(s32[128]{0:T(128)} %param.12) | copy-start | bytes 1540
  110.6 15.8 %collective-permute-start.18 = (bf16[2,32,4096]{2,1,0:T(8,128)(2,1)S(1)}, bf16[2,32,4096]{2,1,0:T(8,128)(2,1)S(1)}, u32[]{:S(2)}, u32[]{:S(2)}) collective-permute-start(bf16[2,32,4096]{2,1,0:T(8,128)(2,1)S(1)} %pad_maximum_fusion.7), channel_id=1, source_target_pairs={{0,2},{1,3},{2,0},{3,1},{4,6},{5,7},{6,4},{7,5},{8,10},{9,11},{10,... | collective-permute-start | bytes 1572872 | tf_op jit(solution)/shard_map/ppermute | solution.py:156
  119.2 7.3 %collective-permute-start.17 = (bf16[32,4096]{1,0:T(8,128)(2,1)S(1)}, bf16[32,4096]{1,0:T(8,128)(2,1)S(1)}, u32[]{:S(2)}, u32[]{:S(2)}) collective-permute-start(bf16[32,4096]{1,0:T(8,128)(2,1)S(1)} %get-tuple-element.9), channel_id=1, source_target_pairs={{0,4},{1,5},{2,6},{3,7},{4,8},{5,9},{6,10},{7,11},{16,20},{17,21},... | collective-permute-start | bytes 786440 | tf_op jit(solution)/shard_map/ppermute | solution.py:165
  120.7 5.9 %collective-permute-start.21 = (bf16[32,4096]{1,0:T(8,128)(2,1)S(1)}, bf16[32,4096]{1,0:T(8,128)(2,1)S(1)}, u32[]{:S(2)}, u32[]{:S(2)}) collective-permute-start(bf16[32,4096]{1,0:T(8,128)(2,1)S(1)} %get-tuple-element.10), channel_id=1, source_target_pairs={{8,4},{9,5},{10,6},{11,7},{12,8},{13,9},{14,10},{15,11},{24,20},{2... | collective-permute-start | bytes 786440 | tf_op jit(solution)/shard_map/ppermute | solution.py:170
  121.4 15.5 %collective-permute-start.13 = (bf16[1,32,4096]{2,1,0:T(8,128)(2,1)S(1)}, bf16[1,32,4096]{2,1,0:T(8,128)(2,1)S(1)}, u32[]{:S(2)}, u32[]{:S(2)}) collective-permute-start(bf16[1,32,4096]{2,1,0:T(8,128)(2,1)S(1)} %get-tuple-element.13), channel_id=1, source_target_pairs={{0,2},{1,3},{2,0},{3,1},{4,6},{5,7},{6,4},{7,5},{8,10},{9,11},{10,... | collective-permute-start | bytes 786440 | tf_op jit(solution)/shard_map/ppermute | solution.py:156
  126.5 17.4 %copy-start.2 = (f32[32,2048]{1,0:T(8,128)S(1)}, f32[32,2048]{1,0:T(8,128)}, u32[]{:S(2)}) copy-start(f32[32,2048]{1,0:T(8,128)} %get-tuple-element.31) | copy-start | bytes 786436
  126.5 17.4 %copy-start.3 = (f32[32,2048]{1,0:T(8,128)S(1)}, f32[32,2048]{1,0:T(8,128)}, u32[]{:S(2)}) copy-start(f32[32,2048]{1,0:T(8,128)} %get-tuple-element.33) | copy-start | bytes 786436
  126.7 12.6 %collective-permute-start.19 = (bf16[32,4096]{1,0:T(8,128)(2,1)S(1)}, bf16[32,4096]{1,0:T(8,128)(2,1)S(1)}, u32[]{:S(2)}, u32[]{:S(2)}) collective-permute-start(bf16[32,4096]{1,0:T(8,128)(2,1)S(1)} %get-tuple-element.7), channel_id=1, source_target_pairs={{0,4},{1,5},{2,6},{3,7},{4,8},{5,9},{6,10},{7,11},{8,12},{9,13},{1... | collective-permute-start | bytes 786440 | tf_op jit(solution)/shard_map/ppermute | solution.py:165
  135.5 8.3 %collective-permute-start.22 = (bf16[32,4096]{1,0:T(8,128)(2,1)S(1)}, bf16[32,4096]{1,0:T(8,128)(2,1)S(1)}, u32[]{:S(2)}, u32[]{:S(2)}) collective-permute-start(bf16[32,4096]{1,0:T(8,128)(2,1)S(1)} %get-tuple-element.8), channel_id=1, source_target_pairs={{4,0},{5,1},{6,2},{7,3},{8,4},{9,5},{10,6},{11,7},{12,8},{13,9},{1... | collective-permute-start | bytes 786440 | tf_op jit(solution)/shard_map/ppermute | solution.py:170
  145.0 1.0 copy-start.1

commit v10 on v8

--- a/solution.py
+++ b/solution.py
@@ -133,21 +133,16 @@
         behind_row = [(j, j ^ 2) for j in range(experts) if j // 4 <= lines - 1 - step]
         there.append((lax.ppermute(ahead, "expert", ahead_row), line - step))
         there.append((lax.ppermute(behind, "expert", behind_row), line + step))
-    column = place(here, lines, shard)
-    across = place(there, lines, shard)
-    in_row = (me // 2) % 2
-    mine = jnp.stack([pick(in_row, [column, across]), pick(in_row, [across, column])], axis=1)
-    return mine.reshape((lines * 2 * shard.shape[0],) + shard.shape[1:])
-
-
-def topo_reduce_scatter(blocks, experts):
+    flat = (lines * shard.shape[0],) + shard.shape[1:]
+    return place(here, lines, shard).reshape(flat), place(there, lines, shard).reshape(flat)
+
+
+def topo_reduce_scatter(own_row, other_row, experts):
     lines = experts // 4
     me = lax.axis_index("expert")
-    rows = blocks.shape[0] // (2 * lines)
-    plane = blocks.reshape((lines, 2, rows) + blocks.shape[1:])
-    in_row = (me // 2) % 2
-    keep = pick(in_row, [plane[:, 0], plane[:, 1]])
-    give = pick(in_row, [plane[:, 1], plane[:, 0]])
+    rows = own_row.shape[0] // lines
+    keep = own_row.reshape((lines, rows) + own_row.shape[1:])
+    give = other_row.reshape((lines, rows) + other_row.shape[1:])
     line = me // 4
 
     def row_sum(target, senders):
@@ -221,28 +216,35 @@
     payload = jnp.concatenate(
         [centroid.astype(jnp.bfloat16), grad_sum.astype(jnp.bfloat16), side], axis=1
     )
-    gathered = topo_all_gather(payload, experts)
-    cent_all = gathered[:, :model_width]
-    grad_all = gathered[:, model_width : 2 * model_width]
-    side_all = gathered[:, 2 * model_width : 2 * model_width + 2 * experts].astype(jnp.float32)
-    column = jnp.arange(experts, dtype=jnp.int32)[None, :]
-    summed_side = side_all[:, :experts] + side_all[:, experts:]
-    mine = jnp.sum(jnp.where(column == me, summed_side, 0.0), axis=1)
-    other = jnp.sum(jnp.where(column == (me ^ 1), summed_side, 0.0), axis=1)
+    column_rows, across_rows = topo_all_gather(payload, experts)
+    expert_ids = jnp.arange(experts, dtype=jnp.int32)[None, :]
     swap_core = [(j, j ^ 1) for j in range(experts)]
     gate_mat, up_mat, down_mat = gate_weight[0], up_weight[0], down_weight[0]
     gate_pair = lax.ppermute(gate_mat, "expert", swap_core)
     up_pair = lax.ppermute(up_mat, "expert", swap_core)
     down_pair = lax.ppermute(down_mat, "expert", swap_core)
-    output, input_grad = expert_dense(cent_all, grad_all, gate_mat, up_mat, down_mat)
-    output_pair, input_grad_pair = expert_dense(cent_all, grad_all, gate_pair, up_pair, down_pair)
-    weighted_out = mine[:, None] * output.astype(jnp.float32) + other[:, None] * output_pair.astype(
-        jnp.float32
-    )
-    weighted_grad = mine[:, None] * input_grad.astype(jnp.float32) + other[
-        :, None
-    ] * input_grad_pair.astype(jnp.float32)
-    summed = topo_reduce_scatter(jnp.concatenate([weighted_out, weighted_grad], axis=1), experts)
+
+    def contributions(gathered):
+        cent_rows_in = gathered[:, :model_width]
+        grad_rows_in = gathered[:, model_width : 2 * model_width]
+        side_rows = gathered[:, 2 * model_width : 2 * model_width + 2 * experts]
+        side_rows = side_rows.astype(jnp.float32)
+        summed_side = side_rows[:, :experts] + side_rows[:, experts:]
+        mine = jnp.sum(jnp.where(expert_ids == me, summed_side, 0.0), axis=1)[:, None]
+        other = jnp.sum(jnp.where(expert_ids == (me ^ 1), summed_side, 0.0), axis=1)[:, None]
+        output, input_grad = expert_dense(cent_rows_in, grad_rows_in, gate_mat, up_mat, down_mat)
+        output_pair, input_grad_pair = expert_dense(
+            cent_rows_in, grad_rows_in, gate_pair, up_pair, down_pair
+        )
+        weighted_out = mine * output.astype(jnp.float32) + other * output_pair.astype(jnp.float32)
+        weighted_grad = mine * input_grad.astype(jnp.float32) + other * input_grad_pair.astype(
+            jnp.float32
+        )
+        return jnp.concatenate([weighted_out, weighted_grad], axis=1)
+
+    own_row = contributions(column_rows)
+    other_row = contributions(across_rows)
+    summed = topo_reduce_scatter(own_row, other_row, experts)
     combined = summed[:, :model_width]
     centroid_grad = summed[:, model_width:] - grad_sum
     layer_out = tokens.astype(jnp.float32) + jnp.take(combined - centroid, cluster_ids, axis=0)

time: 122 us -> 124 us (1.016)
  matrix products: 16.6 us -> 25 us
  waiting for transfers between devices: 28.1 us -> 23.9 us
  local copies, waits for them, and re-layouts: 5.69 us -> 4.11 us
    ppermute x3, starting transfers between devices: 22.2 us -> 16.6 us  [topo_reduce_scatter(): lax.ppermute(ahead.astype(jnp.bfloat16), 'expert', [(j, j + 4) for j in r...]
    unnamed x17 -> x15, local copies, waits for them, and re-layouts: 3.54 us -> 0.83 us
    ppermute x7, waiting for transfers between devices: 2.66 us -> 0.02 us  [row_sum(): got = lax.ppermute(theirs.astype(jnp.bfloat16), 'expert', pairs)]
    dot_general x2 -> x4, matrix products: 2.04 us -> 4.65 us  [expert_dense(): lax.dot_general(grad_in, down_mat, against, preferred_element_type=jnp.fl...]
    dot_general x2 -> x4, matrix products: 2.15 us -> 4.62 us  [expert_dense(): lax.dot_general(up_grad, up_mat, against, preferred_element_type=jnp.floa...]
    dot_general x2 -> x4, matrix products: 2.39 us -> 4.65 us  [expert_dense(): lax.dot_general(gate_grad, gate_mat, against, preferred_element_type=jnp....]
    ppermute x3, starting transfers between devices: 6.93 us -> 9.04 us  [topo_all_gather(): lax.ppermute(ahead, 'expert', [(j, j + 4) for j in range(experts) if step...]
    ppermute x7, starting transfers between devices: 11 us -> 13 us  [row_sum(): got = lax.ppermute(theirs.astype(jnp.bfloat16), 'expert', pairs)]
  transfers between devices with their start and end apart: 29 -> 29, of which waited for: 10 -> 9; matrix products, arithmetic and copies ran while one was open for 11% -> 19% of each run, Pallas kernels for 0% -> 0%
where the time goes in v10:
time: 124 us; the launch traced here: 123 us
  starting transfers between devices  59.3 us (48%)
  matrix products  25 us (20%)
  waiting for transfers between devices  23.9 us (19%)
  other arithmetic  9.53 us (8%)
  local copies, waits for them, and re-layouts  4.11 us (3%)
  between operations  1.36 us (1%)
    ppermute x3, starting transfers between devices, topo_reduce_scatter(): lax.ppermute(ahead.astype(jnp.bfloat16), 'expert', [(j, j + 4) for j in r...  16.6 us
    ppermute x7, starting transfers between devices, row_sum(): got = lax.ppermute(theirs.astype(jnp.bfloat16), 'expert', pairs)  13 us
    ppermute x3, waiting for transfers between devices, topo_all_gather(): lax.ppermute(behind, 'expert', [(j, j - 4) for j in range(experts) if 1 <...  10 us
    ppermute x3, starting transfers between devices, topo_all_gather(): there.append((lax.ppermute(behind, 'expert', behind_row), line + step))  9.53 us
    ppermute x3, starting transfers between devices, topo_all_gather(): lax.ppermute(ahead, 'expert', [(j, j + 4) for j in range(experts) if step...  9.04 us
    ppermute x3, waiting for transfers between devices, topo_reduce_scatter(): lax.ppermute(ahead.astype(jnp.bfloat16), 'expert', [(j, j + 4) for j in r...  5.73 us
    dot_general x4, matrix products, expert_dense(): lax.dot_general(gate_grad, gate_mat, against, preferred_element_type=jnp....  4.65 us
    dot_general x4, matrix products, expert_dense(): lax.dot_general(grad_in, down_mat, against, preferred_element_type=jnp.fl...  4.65 us
  transfers between devices with their start and end apart: 29, of which 9 were waited for; matrix products, arithmetic and copies ran while one was open for 19% of the time, Pallas kernels for 0%

profile of v10, /device:TPU:0, one launch (start us, length us, event | category | flops | bytes accessed | tf_op | source)
XLA Modules:
  0.0 123.2 jit_solution(16530956637256616937)
XLA Ops:
  2.4 2.0 %fusion.126 = (bf16[32,2048]{1,0:T(8,128)(2,1)S(1)}, f32[32,2048]{1,0:T(8,128)}) fusion(bf16[128,2048]{1,0:T(8,128)(2,1)} %param.11, s32[128]{0:T(128)} %param.12), kind=kOutput, calls=%fused_computation.202 | convolution fusion | flops 16846848 | bytes 918016 | tf_op jit(solution)/shard_map/dot_general | solution.py:206
  4.4 2.0 %fusion.127 = (bf16[32,2048]{1,0:T(8,128)(2,1)S(1)}, f32[32,2048]{1,0:T(8,128)}) fusion(f32[32]{0:T(128)S(1)} %convert_reduce_fusion, bf16[128,2048]{1,0:T(8,128)(2,1)} %param.10, s32[128]{0:T(128)} %param.12), kind=kOutput, calls=%fused_computation.203 | convolution fusion | flops 16912384 | bytes 918144 | tf_op jit(solution)/shard_map/dot_general | solution.py:203
  6.4 1.3 %collective-permute-start = (bf16[32,4224]{1,0:T(8,128)(2,1)S(1)}, bf16[32,4224]{1,0:T(8,128)(2,1)}, u32[]{:S(2)}, u32[]{:S(2)}) collective-permute-start(bf16[32,4224]{1,0:T(8,128)(2,1)S(1)} %fusion.73), channel_id=1, source_target_pairs={{4,0},{5,1},{6,2},{7,3},{8,4},{9,5},{10,6},{11,7},{12,8},{13,9},{1... | collective-permute-start | bytes 811016 | tf_op jit(solution)/shard_map/ppermute | solution.py:125
  7.7 6.3 %collective-permute-start.3 = (bf16[32,4224]{1,0:T(8,128)(2,1)S(1)}, bf16[32,4224]{1,0:T(8,128)(2,1)}, u32[]{:S(2)}, u32[]{:S(2)}) collective-permute-start(bf16[32,4224]{1,0:T(8,128)(2,1)S(1)} %fusion.73), channel_id=1, source_target_pairs={{0,4},{1,5},{2,6},{3,7},{4,8},{5,9},{6,10},{7,11},{8,12},{9,13},{1... | collective-permute-start | bytes 811016 | tf_op jit(solution)/shard_map/ppermute | solution.py:120
  14.0 2.0 %collective-permute-start.15 = (bf16[32,4224]{1,0:T(8,128)(2,1)S(1)}, bf16[32,4224]{1,0:T(8,128)(2,1)}, u32[]{:S(2)}, u32[]{:S(2)}) collective-permute-start(bf16[32,4224]{1,0:T(8,128)(2,1)S(1)} %fusion.73), channel_id=1, source_target_pairs={{0,2},{1,3},{2,0},{3,1},{4,6},{5,7},{6,4},{7,5},{8,10},{9,11},{10,... | collective-permute-start | bytes 811016 | tf_op jit(solution)/shard_map/ppermute | solution.py:117
  15.9 2.0 %collective-permute-done = bf16[32,4224]{1,0:T(8,128)(2,1)} collective-permute-done((bf16[32,4224]{1,0:T(8,128)(2,1)S(1)}, bf16[32,4224]{1,0:T(8,128)(2,1)}, u32[]{:S(2)}, u32[]{:S(2)}) %collective-permute-start) | collective-permute-done | bytes 270368 | tf_op jit(solution)/shard_map/ppermute | solution.py:125
  17.9 1.3 %collective-permute-start.1 = (bf16[32,4224]{1,0:T(8,128)(2,1)}, bf16[32,4224]{1,0:T(8,128)(2,1)}, u32[]{:S(2)}, u32[]{:S(2)}) collective-permute-start(bf16[32,4224]{1,0:T(8,128)(2,1)} %collective-permute-done), channel_id=1, source_target_pairs={{4,0},{5,1},{6,2},{7,3},{8,4},{9,5},{10,6},{11,7},{20,16},{21,17},... | collective-permute-start | bytes 811016 | tf_op jit(solution)/shard_map/ppermute | solution.py:125
  19.2 1.4 %collective-permute-start.4 = (bf16[32,4224]{1,0:T(8,128)(2,1)}, bf16[32,4224]{1,0:T(8,128)(2,1)}, u32[]{:S(2)}, u32[]{:S(2)}) collective-permute-start(bf16[32,4224]{1,0:T(8,128)(2,1)} %collective-permute-done.3), channel_id=1, source_target_pairs={{4,8},{5,9},{6,10},{7,11},{8,12},{9,13},{10,14},{11,15},{20,24},{2... | collective-permute-start | bytes 811016 | tf_op jit(solution)/shard_map/ppermute | solution.py:120
  20.6 7.2 %collective-permute-done.1 = bf16[32,4224]{1,0:T(8,128)(2,1)} collective-permute-done((bf16[32,4224]{1,0:T(8,128)(2,1)}, bf16[32,4224]{1,0:T(8,128)(2,1)}, u32[]{:S(2)}, u32[]{:S(2)}) %collective-permute-start.1) | collective-permute-done | bytes 270368 | tf_op jit(solution)/shard_map/ppermute | solution.py:125
  27.8 1.3 %collective-permute-start.2 = (bf16[32,4224]{1,0:T(8,128)(2,1)}, bf16[32,4224]{1,0:T(8,128)(2,1)}, u32[]{:S(2)}, u32[]{:S(2)}) collective-permute-start(bf16[32,4224]{1,0:T(8,128)(2,1)} %collective-permute-done.1), channel_id=1, source_target_pairs={{4,0},{5,1},{6,2},{7,3},{20,16},{21,17},{22,18},{23,19}} | collective-permute-start | bytes 811016 | tf_op jit(solution)/shard_map/ppermute | solution.py:125
  29.1 1.4 %collective-permute-start.5 = (bf16[32,4224]{1,0:T(8,128)(2,1)}, bf16[32,4224]{1,0:T(8,128)(2,1)}, u32[]{:S(2)}, u32[]{:S(2)}) collective-permute-start(bf16[32,4224]{1,0:T(8,128)(2,1)} %collective-permute-done.4), channel_id=1, source_target_pairs={{8,12},{9,13},{10,14},{11,15},{24,28},{25,29},{26,30},{27,31}} | collective-permute-start | bytes 811016 | tf_op jit(solution)/shard_map/ppermute | solution.py:120
  31.6 3.5 %collective-permute-start.13 = (bf16[32,4224]{1,0:T(8,128)(2,1)}, bf16[32,4224]{1,0:T(8,128)(2,1)S(1)}, u32[]{:S(2)}, u32[]{:S(2)}) collective-permute-start(bf16[32,4224]{1,0:T(8,128)(2,1)} %collective-permute-done), channel_id=1, source_target_pairs={{0,2},{1,3},{2,0},{3,1},{4,6},{5,7},{6,4},{7,5},{8,10},{9,11},{10,... | collective-permute-start | bytes 811016 | tf_op jit(solution)/shard_map/ppermute | solution.py:135
  36.7 3.0 %collective-permute-start.11 = (bf16[32,4224]{1,0:T(8,128)(2,1)}, bf16[32,4224]{1,0:T(8,128)(2,1)S(1)}, u32[]{:S(2)}, u32[]{:S(2)}) collective-permute-start(bf16[32,4224]{1,0:T(8,128)(2,1)} %collective-permute-done.1), channel_id=1, source_target_pairs={{0,2},{1,3},{2,0},{3,1},{4,6},{5,7},{6,4},{7,5},{16,18},{17,19},{1... | collective-permute-start | bytes 811016 | tf_op jit(solution)/shard_map/ppermute | solution.py:135
  40.4 2.1 %fusion.35 = bf16[128,4224]{1,0:T(8,128)(2,1)S(1)} fusion(pred[128]{0:T(512)(128)(4,1)S(1)} %broadcast_in_dim.295, pred[128]{0:T(512)(128)(4,1)S(1)} %broadcast_in_dim.290, pred[128]{0:T(512)(128)(4,1)S(1)} %broadcast_in_dim.285, pred[128]{0:T(512)(128)(4,1)S(1)} %broadcast_in_dim.280, pred[128]{0:T(512)(128)(4,1)S(1)} %broadcast_in_dim.275, ...), kind=kLoop, calls=%fused_computation.50 | loop fusion | flops 3784704 | bytes 2974592 | tf_op jit(solution)/shard_map/jit(_where)/select_n | solution.py:107
  46.2 3.1 %collective-permute-start.9 = (bf16[32,4224]{1,0:T(8,128)(2,1)}, bf16[32,4224]{1,0:T(8,128)(2,1)S(1)}, u32[]{:S(2)}, u32[]{:S(2)}) collective-permute-start(bf16[32,4224]{1,0:T(8,128)(2,1)} %collective-permute-done.2), channel_id=1, source_target_pairs={{0,2},{1,3},{2,0},{3,1},{16,18},{17,19},{18,16},{19,17}} | collective-permute-start | bytes 811016 | tf_op jit(solution)/shard_map/ppermute | solution.py:135
  51.2 3.6 %collective-permute-done.9 = bf16[32,4224]{1,0:T(8,128)(2,1)S(1)} collective-permute-done((bf16[32,4224]{1,0:T(8,128)(2,1)}, bf16[32,4224]{1,0:T(8,128)(2,1)S(1)}, u32[]{:S(2)}, u32[]{:S(2)}) %collective-permute-start.9) | collective-permute-done | bytes 270368 | tf_op jit(solution)/shard_map/ppermute | solution.py:135
  54.8 1.7 %fusion.29 = bf16[128,4224]{1,0:T(8,128)(2,1)S(1)} fusion(pred[128]{0:T(512)(128)(4,1)S(1)} %broadcast_in_dim.295, pred[128]{0:T(512)(128)(4,1)S(1)} %broadcast_in_dim.290, pred[128]{0:T(512)(128)(4,1)S(1)} %broadcast_in_dim.285, pred[128]{0:T(512)(128)(4,1)S(1)} %broadcast_in_dim.280, pred[128]{0:T(512)(128)(4,1)S(1)} %broadcast_in_dim.275, ...), kind=kLoop, calls=%fused_computation.43 | loop fusion | flops 3784704 | bytes 2974592 | tf_op jit(solution)/shard_map/jit(_where)/select_n | solution.py:107
  62.7 1.2 fusion.9
  68.2 1.2 fusion.13
  69.7 3.0 %collective-permute-start.17 = (bf16[32,4096]{1,0:T(8,128)(2,1)S(1)}, bf16[32,4096]{1,0:T(8,128)(2,1)S(1)}, u32[]{:S(2)}, u32[]{:S(2)}) collective-permute-start(bf16[32,4096]{1,0:T(8,128)(2,1)S(1)} %get-tuple-element.23), channel_id=1, source_target_pairs={{0,2},{1,3},{2,0},{3,1},{16,18},{17,19},{18,16},{19,17}} | collective-permute-start | bytes 786440 | tf_op jit(solution)/shard_map/ppermute | solution.py:152
  73.3 2.9 %collective-permute-start.19 = (bf16[32,4096]{1,0:T(8,128)(2,1)S(1)}, bf16[32,4096]{1,0:T(8,128)(2,1)S(1)}, u32[]{:S(2)}, u32[]{:S(2)}) collective-permute-start(bf16[32,4096]{1,0:T(8,128)(2,1)S(1)} %get-tuple-element.22), channel_id=1, source_target_pairs={{0,2},{1,3},{2,0},{3,1},{4,6},{5,7},{6,4},{7,5},{16,18},{17,19},{1... | collective-permute-start | bytes 786440 | tf_op jit(solution)/shard_map/ppermute | solution.py:152
  81.2 1.2 fusion.6
  82.7 1.8 %collective-permute-start.18 = (bf16[32,4096]{1,0:T(8,128)(2,1)S(1)}, bf16[32,4096]{1,0:T(8,128)(2,1)S(1)}, u32[]{:S(2)}, u32[]{:S(2)}) collective-permute-start(bf16[32,4096]{1,0:T(8,128)(2,1)S(1)} %get-tuple-element.15), channel_id=1, source_target_pairs={{0,4},{1,5},{2,6},{3,7},{16,20},{17,21},{18,22},{19,23}} | collective-permute-start | bytes 786440 | tf_op jit(solution)/shard_map/ppermute | solution.py:160
  85.3 3.3 %collective-permute-start.21 = (bf16[32,4096]{1,0:T(8,128)(2,1)S(1)}, bf16[32,4096]{1,0:T(8,128)(2,1)S(1)}, u32[]{:S(2)}, u32[]{:S(2)}) collective-permute-start(bf16[32,4096]{1,0:T(8,128)(2,1)S(1)} %get-tuple-element.21), channel_id=1, source_target_pairs={{0,2},{1,3},{2,0},{3,1},{4,6},{5,7},{6,4},{7,5},{8,10},{9,11},{10,... | collective-permute-start | bytes 786440 | tf_op jit(solution)/shard_map/ppermute | solution.py:152
  90.3 4.4 %collective-permute-start.20 = (bf16[32,4096]{1,0:T(8,128)(2,1)S(1)}, bf16[32,4096]{1,0:T(8,128)(2,1)S(1)}, u32[]{:S(2)}, u32[]{:S(2)}) collective-permute-start(bf16[32,4096]{1,0:T(8,128)(2,1)S(1)} %get-tuple-element.13), channel_id=1, source_target_pairs={{0,4},{1,5},{2,6},{3,7},{4,8},{5,9},{6,10},{7,11},{16,20},{17,21},... | collective-permute-start | bytes 786440 | tf_op jit(solution)/shard_map/ppermute | solution.py:160
  95.4 1.4 %collective-permute-start.16 = (bf16[32,4096]{1,0:T(8,128)(2,1)S(1)}, bf16[32,4096]{1,0:T(8,128)(2,1)S(1)}, u32[]{:S(2)}, u32[]{:S(2)}) collective-permute-start(bf16[32,4096]{1,0:T(8,128)(2,1)S(1)} %get-tuple-element.17), channel_id=1, source_target_pairs={{0,2},{1,3},{2,0},{3,1},{4,6},{5,7},{6,4},{7,5},{8,10},{9,11},{10,... | collective-permute-start | bytes 786440 | tf_op jit(solution)/shard_map/ppermute | solution.py:152
  96.9 2.5 %collective-permute-done.20 = bf16[32,4096]{1,0:T(8,128)(2,1)S(1)} collective-permute-done((bf16[32,4096]{1,0:T(8,128)(2,1)S(1)}, bf16[32,4096]{1,0:T(8,128)(2,1)S(1)}, u32[]{:S(2)}, u32[]{:S(2)}) %collective-permute-start.20) | collective-permute-done | bytes 262176 | tf_op jit(solution)/shard_map/ppermute | solution.py:160
  99.6 10.3 %collective-permute-start.22 = (bf16[32,4096]{1,0:T(8,128)(2,1)S(1)}, bf16[32,4096]{1,0:T(8,128)(2,1)S(1)}, u32[]{:S(2)}, u32[]{:S(2)}) collective-permute-start(bf16[32,4096]{1,0:T(8,128)(2,1)S(1)} %get-tuple-element.11), channel_id=1, source_target_pairs={{0,4},{1,5},{2,6},{3,7},{4,8},{5,9},{6,10},{7,11},{8,12},{9,13},{1... | collective-permute-start | bytes 786440 | tf_op jit(solution)/shard_map/ppermute | solution.py:160
  109.9 1.3 %collective-permute-start.28 = (bf16[32,4096]{1,0:T(8,128)(2,1)S(1)}, bf16[32,4096]{1,0:T(8,128)(2,1)S(1)}, u32[]{:S(2)}, u32[]{:S(2)}) collective-permute-start(bf16[32,4096]{1,0:T(8,128)(2,1)S(1)} %get-tuple-element.12), channel_id=1, source_target_pairs={{4,0},{5,1},{6,2},{7,3},{8,4},{9,5},{10,6},{11,7},{12,8},{13,9},{1... | collective-permute-start | bytes 786440 | tf_op jit(solution)/shard_map/ppermute | solution.py:167
  111.2 2.5 %collective-permute-done.22 = bf16[32,4096]{1,0:T(8,128)(2,1)S(1)} collective-permute-done((bf16[32,4096]{1,0:T(8,128)(2,1)S(1)}, bf16[32,4096]{1,0:T(8,128)(2,1)S(1)}, u32[]{:S(2)}, u32[]{:S(2)}) %collective-permute-start.22) | collective-permute-done | bytes 262176 | tf_op jit(solution)/shard_map/ppermute | solution.py:160
  113.8 4.4 %collective-permute-done.28 = bf16[32,4096]{1,0:T(8,128)(2,1)S(1)} collective-permute-done((bf16[32,4096]{1,0:T(8,128)(2,1)S(1)}, bf16[32,4096]{1,0:T(8,128)(2,1)S(1)}, u32[]{:S(2)}, u32[]{:S(2)}) %collective-permute-start.28) | collective-permute-done | bytes 262176 | tf_op jit(solution)/shard_map/ppermute | solution.py:167
  120.4 2.8 %select_add_fusion = (f32[128,2048]{1,0:T(8,128)}, f32[128,2048]{1,0:T(8,128)}) fusion(f32[128,2048]{1,0:T(8,128)S(1)} %gather_fusion.1, bf16[128,2048]{1,0:T(8,128)(2,1)S(1)} %copy-done.3, pred[128]{0:T(512)(128)(4,1)S(1)} %compare_and_fusion, f32[128,2048]{1,0:T(8,128)S(1)} %gather_fusion, bf16[128,2048]{1,0:T(8,128)(2,1)} %param.10), kind=kLoop, calls=%fused_computation.51 | loop fusion | flops 1572864 | bytes 5243008 | tf_op jit(solution)/shard_map/add | solution.py:251
  (113 shorter events, 32.8 us)
Async XLA Ops:
  0.6 41.8 %copy-start = (bf16[1,2048,768]{2,1,0:T(8,128)(2,1)S(1)}, bf16[1,2048,768]{2,1,0:T(8,128)(2,1)}, u32[]{:S(2)}) copy-start(bf16[1,2048,768]{2,1,0:T(8,128)(2,1)} %param.16) | copy-start | bytes 9437188
  6.4 11.5 %collective-permute-start = (bf16[32,4224]{1,0:T(8,128)(2,1)S(1)}, bf16[32,4224]{1,0:T(8,128)(2,1)}, u32[]{:S(2)}, u32[]{:S(2)}) collective-permute-start(bf16[32,4224]{1,0:T(8,128)(2,1)S(1)} %fusion.73), channel_id=1, source_target_pairs={{4,0},{5,1},{6,2},{7,3},{8,4},{9,5},{10,6},{11,7},{12,8},{13,9},{1... | collective-permute-start | bytes 811016 | tf_op jit(solution)/shard_map/ppermute | solution.py:125
  7.7 11.5 %collective-permute-start.3 = (bf16[32,4224]{1,0:T(8,128)(2,1)S(1)}, bf16[32,4224]{1,0:T(8,128)(2,1)}, u32[]{:S(2)}, u32[]{:S(2)}) collective-permute-start(bf16[32,4224]{1,0:T(8,128)(2,1)S(1)} %fusion.73), channel_id=1, source_target_pairs={{0,4},{1,5},{2,6},{3,7},{4,8},{5,9},{6,10},{7,11},{8,12},{9,13},{1... | collective-permute-start | bytes 811016 | tf_op jit(solution)/shard_map/ppermute | solution.py:120
  14.0 31.6 %collective-permute-start.15 = (bf16[32,4224]{1,0:T(8,128)(2,1)S(1)}, bf16[32,4224]{1,0:T(8,128)(2,1)}, u32[]{:S(2)}, u32[]{:S(2)}) collective-permute-start(bf16[32,4224]{1,0:T(8,128)(2,1)S(1)} %fusion.73), channel_id=1, source_target_pairs={{0,2},{1,3},{2,0},{3,1},{4,6},{5,7},{6,4},{7,5},{8,10},{9,11},{10,... | collective-permute-start | bytes 811016 | tf_op jit(solution)/shard_map/ppermute | solution.py:117
  17.9 9.9 %collective-permute-start.1 = (bf16[32,4224]{1,0:T(8,128)(2,1)}, bf16[32,4224]{1,0:T(8,128)(2,1)}, u32[]{:S(2)}, u32[]{:S(2)}) collective-permute-start(bf16[32,4224]{1,0:T(8,128)(2,1)} %collective-permute-done), channel_id=1, source_target_pairs={{4,0},{5,1},{6,2},{7,3},{8,4},{9,5},{10,6},{11,7},{20,16},{21,17},... | collective-permute-start | bytes 811016 | tf_op jit(solution)/shard_map/ppermute | solution.py:125
  19.2 9.9 %collective-permute-start.4 = (bf16[32,4224]{1,0:T(8,128)(2,1)}, bf16[32,4224]{1,0:T(8,128)(2,1)}, u32[]{:S(2)}, u32[]{:S(2)}) collective-permute-start(bf16[32,4224]{1,0:T(8,128)(2,1)} %collective-permute-done.3), channel_id=1, source_target_pairs={{4,8},{5,9},{6,10},{7,11},{8,12},{9,13},{10,14},{11,15},{20,24},{2... | collective-permute-start | bytes 811016 | tf_op jit(solution)/shard_map/ppermute | solution.py:120
  27.8 8.9 %collective-permute-start.2 = (bf16[32,4224]{1,0:T(8,128)(2,1)}, bf16[32,4224]{1,0:T(8,128)(2,1)}, u32[]{:S(2)}, u32[]{:S(2)}) collective-permute-start(bf16[32,4224]{1,0:T(8,128)(2,1)} %collective-permute-done.1), channel_id=1, source_target_pairs={{4,0},{5,1},{6,2},{7,3},{20,16},{21,17},{22,18},{23,19}} | collective-permute-start | bytes 811016 | tf_op jit(solution)/shard_map/ppermute | solution.py:125
  29.1 10.6 %collective-permute-start.5 = (bf16[32,4224]{1,0:T(8,128)(2,1)}, bf16[32,4224]{1,0:T(8,128)(2,1)}, u32[]{:S(2)}, u32[]{:S(2)}) collective-permute-start(bf16[32,4224]{1,0:T(8,128)(2,1)} %collective-permute-done.4), channel_id=1, source_target_pairs={{8,12},{9,13},{10,14},{11,15},{24,28},{25,29},{26,30},{27,31}} | collective-permute-start | bytes 811016 | tf_op jit(solution)/shard_map/ppermute | solution.py:120
  31.6 14.6 %collective-permute-start.13 = (bf16[32,4224]{1,0:T(8,128)(2,1)}, bf16[32,4224]{1,0:T(8,128)(2,1)S(1)}, u32[]{:S(2)}, u32[]{:S(2)}) collective-permute-start(bf16[32,4224]{1,0:T(8,128)(2,1)} %collective-permute-done), channel_id=1, source_target_pairs={{0,2},{1,3},{2,0},{3,1},{4,6},{5,7},{6,4},{7,5},{8,10},{9,11},{10,... | collective-permute-start | bytes 811016 | tf_op jit(solution)/shard_map/ppermute | solution.py:135
  35.1 15.3 %collective-permute-start.14 = (bf16[32,4224]{1,0:T(8,128)(2,1)}, bf16[32,4224]{1,0:T(8,128)(2,1)S(1)}, u32[]{:S(2)}, u32[]{:S(2)}) collective-permute-start(bf16[32,4224]{1,0:T(8,128)(2,1)} %collective-permute-done.3), channel_id=1, source_target_pairs={{4,6},{5,7},{6,4},{7,5},{8,10},{9,11},{10,8},{11,9},{12,14},{13,15... | collective-permute-start | bytes 811016 | tf_op jit(solution)/shard_map/ppermute | solution.py:134
  36.7 13.9 %collective-permute-start.11 = (bf16[32,4224]{1,0:T(8,128)(2,1)}, bf16[32,4224]{1,0:T(8,128)(2,1)S(1)}, u32[]{:S(2)}, u32[]{:S(2)}) collective-permute-start(bf16[32,4224]{1,0:T(8,128)(2,1)} %collective-permute-done.1), channel_id=1, source_target_pairs={{0,2},{1,3},{2,0},{3,1},{4,6},{5,7},{6,4},{7,5},{16,18},{17,19},{1... | collective-permute-start | bytes 811016 | tf_op jit(solution)/shard_map/ppermute | solution.py:135
  39.7 11.4 %collective-permute-start.12 = (bf16[32,4224]{1,0:T(8,128)(2,1)}, bf16[32,4224]{1,0:T(8,128)(2,1)S(1)}, u32[]{:S(2)}, u32[]{:S(2)}) collective-permute-start(bf16[32,4224]{1,0:T(8,128)(2,1)} %collective-permute-done.4), channel_id=1, source_target_pairs={{8,10},{9,11},{10,8},{11,9},{12,14},{13,15},{14,12},{15,13},{24,26... | collective-permute-start | bytes 811016 | tf_op jit(solution)/shard_map/ppermute | solution.py:134
  45.5 5.7 %collective-permute-start.10 = (bf16[32,4224]{1,0:T(8,128)(2,1)}, bf16[32,4224]{1,0:T(8,128)(2,1)S(1)}, u32[]{:S(2)}, u32[]{:S(2)}) collective-permute-start(bf16[32,4224]{1,0:T(8,128)(2,1)} %collective-permute-done.5), channel_id=1, source_target_pairs={{12,14},{13,15},{14,12},{15,13},{28,30},{29,31},{30,28},{31,29}} | collective-permute-start | bytes 811016 | tf_op jit(solution)/shard_map/ppermute | solution.py:134
  46.2 8.6 %collective-permute-start.9 = (bf16[32,4224]{1,0:T(8,128)(2,1)}, bf16[32,4224]{1,0:T(8,128)(2,1)S(1)}, u32[]{:S(2)}, u32[]{:S(2)}) collective-permute-start(bf16[32,4224]{1,0:T(8,128)(2,1)} %collective-permute-done.2), channel_id=1, source_target_pairs={{0,2},{1,3},{2,0},{3,1},{16,18},{17,19},{18,16},{19,17}} | collective-permute-start | bytes 811016 | tf_op jit(solution)/shard_map/ppermute | solution.py:135
  50.5 13.4 %collective-permute-start.7 = (bf16[2048,768]{1,0:T(8,128)(2,1)S(1)}, bf16[2048,768]{1,0:T(8,128)(2,1)S(1)}, u32[]{:S(2)}, u32[]{:S(2)}) collective-permute-start(bf16[2048,768]{1,0:T(8,128)(2,1)S(1)} %bitcast.147), channel_id=1, source_target_pairs={{0,1},{1,0},{2,3},{3,2},{4,5},{5,4},{6,7},{7,6},{8,9},{9,8},{10,11... | collective-permute-start | bytes 9437192 | tf_op jit(solution)/shard_map/ppermute | solution.py:224
  50.6 13.9 %collective-permute-start.6 = (bf16[2048,768]{1,0:T(8,128)(2,1)S(1)}, bf16[2048,768]{1,0:T(8,128)(2,1)S(1)}, u32[]{:S(2)}, u32[]{:S(2)}) collective-permute-start(bf16[2048,768]{1,0:T(8,128)(2,1)S(1)} %bitcast.149), channel_id=1, source_target_pairs={{0,1},{1,0},{2,3},{3,2},{4,5},{5,4},{6,7},{7,6},{8,9},{9,8},{10,11... | collective-permute-start | bytes 9437192 | tf_op jit(solution)/shard_map/ppermute | solution.py:223
  51.1 14.1 %collective-permute-start.8 = (bf16[768,2048]{1,0:T(8,128)(2,1)S(1)}, bf16[768,2048]{1,0:T(8,128)(2,1)S(1)}, u32[]{:S(2)}, u32[]{:S(2)}) collective-permute-start(bf16[768,2048]{1,0:T(8,128)(2,1)S(1)} %bitcast.148), channel_id=1, source_target_pairs={{0,1},{1,0},{2,3},{3,2},{4,5},{5,4},{6,7},{7,6},{8,9},{9,8},{10,11... | collective-permute-start | bytes 9437192 | tf_op jit(solution)/shard_map/ppermute | solution.py:225
  69.7 12.9 %collective-permute-start.17 = (bf16[32,4096]{1,0:T(8,128)(2,1)S(1)}, bf16[32,4096]{1,0:T(8,128)(2,1)S(1)}, u32[]{:S(2)}, u32[]{:S(2)}) collective-permute-start(bf16[32,4096]{1,0:T(8,128)(2,1)S(1)} %get-tuple-element.23), channel_id=1, source_target_pairs={{0,2},{1,3},{2,0},{3,1},{16,18},{17,19},{18,16},{19,17}} | collective-permute-start | bytes 786440 | tf_op jit(solution)/shard_map/ppermute | solution.py:152
  72.6 10.0 %collective-permute-start.23 = (bf16[32,4096]{1,0:T(8,128)(2,1)S(1)}, bf16[32,4096]{1,0:T(8,128)(2,1)S(1)}, u32[]{:S(2)}, u32[]{:S(2)}) collective-permute-start(bf16[32,4096]{1,0:T(8,128)(2,1)S(1)} %get-tuple-element.20), channel_id=1, source_target_pairs={{12,14},{13,15},{14,12},{15,13},{28,30},{29,31},{30,28},{31,29}} | collective-permute-start | bytes 786440 | tf_op jit(solution)/shard_map/ppermute | solution.py:152
  73.3 15.2 %collective-permute-start.19 = (bf16[32,4096]{1,0:T(8,128)(2,1)S(1)}, bf16[32,4096]{1,0:T(8,128)(2,1)S(1)}, u32[]{:S(2)}, u32[]{:S(2)}) collective-permute-start(bf16[32,4096]{1,0:T(8,128)(2,1)S(1)} %get-tuple-element.22), channel_id=1, source_target_pairs={{0,2},{1,3},{2,0},{3,1},{4,6},{5,7},{6,4},{7,5},{16,18},{17,19},{1... | collective-permute-start | bytes 786440 | tf_op jit(solution)/shard_map/ppermute | solution.py:152
  76.2 13.2 %collective-permute-start.25 = (bf16[32,4096]{1,0:T(8,128)(2,1)S(1)}, bf16[32,4096]{1,0:T(8,128)(2,1)S(1)}, u32[]{:S(2)}, u32[]{:S(2)}) collective-permute-start(bf16[32,4096]{1,0:T(8,128)(2,1)S(1)} %get-tuple-element.19), channel_id=1, source_target_pairs={{8,10},{9,11},{10,8},{11,9},{12,14},{13,15},{14,12},{15,13},{24,26... | collective-permute-start | bytes 786440 | tf_op jit(solution)/shard_map/ppermute | solution.py:152
  82.7 7.4 %collective-permute-start.18 = (bf16[32,4096]{1,0:T(8,128)(2,1)S(1)}, bf16[32,4096]{1,0:T(8,128)(2,1)S(1)}, u32[]{:S(2)}, u32[]{:S(2)}) collective-permute-start(bf16[32,4096]{1,0:T(8,128)(2,1)S(1)} %get-tuple-element.15), channel_id=1, source_target_pairs={{0,4},{1,5},{2,6},{3,7},{16,20},{17,21},{18,22},{19,23}} | collective-permute-start | bytes 786440 | tf_op jit(solution)/shard_map/ppermute | solution.py:160
  84.6 5.6 %collective-permute-start.24 = (bf16[32,4096]{1,0:T(8,128)(2,1)S(1)}, bf16[32,4096]{1,0:T(8,128)(2,1)S(1)}, u32[]{:S(2)}, u32[]{:S(2)}) collective-permute-start(bf16[32,4096]{1,0:T(8,128)(2,1)S(1)} %get-tuple-element.16), channel_id=1, source_target_pairs={{12,8},{13,9},{14,10},{15,11},{28,24},{29,25},{30,26},{31,27}} | collective-permute-start | bytes 786440 | tf_op jit(solution)/shard_map/ppermute | solution.py:167
  85.3 11.6 %collective-permute-start.21 = (bf16[32,4096]{1,0:T(8,128)(2,1)S(1)}, bf16[32,4096]{1,0:T(8,128)(2,1)S(1)}, u32[]{:S(2)}, u32[]{:S(2)}) collective-permute-start(bf16[32,4096]{1,0:T(8,128)(2,1)S(1)} %get-tuple-element.21), channel_id=1, source_target_pairs={{0,2},{1,3},{2,0},{3,1},{4,6},{5,7},{6,4},{7,5},{8,10},{9,11},{10,... | collective-permute-start | bytes 786440 | tf_op jit(solution)/shard_map/ppermute | solution.py:152
  88.6 29.7 %copy-start.4 = (f32[32,2048]{1,0:T(8,128)S(1)}, f32[32,2048]{1,0:T(8,128)}, u32[]{:S(2)}) copy-start(f32[32,2048]{1,0:T(8,128)} %get-tuple-element.29) | copy-start | bytes 786436
  88.6 29.7 %copy-start.5 = (f32[32,2048]{1,0:T(8,128)S(1)}, f32[32,2048]{1,0:T(8,128)}, u32[]{:S(2)}) copy-start(f32[32,2048]{1,0:T(8,128)} %get-tuple-element.31) | copy-start | bytes 786436
  88.6 8.3 %collective-permute-start.27 = (bf16[32,4096]{1,0:T(8,128)(2,1)S(1)}, bf16[32,4096]{1,0:T(8,128)(2,1)S(1)}, u32[]{:S(2)}, u32[]{:S(2)}) collective-permute-start(bf16[32,4096]{1,0:T(8,128)(2,1)S(1)} %get-tuple-element.18), channel_id=1, source_target_pairs={{4,6},{5,7},{6,4},{7,5},{8,10},{9,11},{10,8},{11,9},{12,14},{13,15... | collective-permute-start | bytes 786440 | tf_op jit(solution)/shard_map/ppermute | solution.py:152
  90.3 9.1 %collective-permute-start.20 = (bf16[32,4096]{1,0:T(8,128)(2,1)S(1)}, bf16[32,4096]{1,0:T(8,128)(2,1)S(1)}, u32[]{:S(2)}, u32[]{:S(2)}) collective-permute-start(bf16[32,4096]{1,0:T(8,128)(2,1)S(1)} %get-tuple-element.13), channel_id=1, source_target_pairs={{0,4},{1,5},{2,6},{3,7},{4,8},{5,9},{6,10},{7,11},{16,20},{17,21},... | collective-permute-start | bytes 786440 | tf_op jit(solution)/shard_map/ppermute | solution.py:160
  94.7 4.7 %collective-permute-start.26 = (bf16[32,4096]{1,0:T(8,128)(2,1)S(1)}, bf16[32,4096]{1,0:T(8,128)(2,1)S(1)}, u32[]{:S(2)}, u32[]{:S(2)}) collective-permute-start(bf16[32,4096]{1,0:T(8,128)(2,1)S(1)} %get-tuple-element.14), channel_id=1, source_target_pairs={{8,4},{9,5},{10,6},{11,7},{12,8},{13,9},{14,10},{15,11},{24,20},{2... | collective-permute-start | bytes 786440 | tf_op jit(solution)/shard_map/ppermute | solution.py:167
  95.4 15.8 %collective-permute-start.16 = (bf16[32,4096]{1,0:T(8,128)(2,1)S(1)}, bf16[32,4096]{1,0:T(8,128)(2,1)S(1)}, u32[]{:S(2)}, u32[]{:S(2)}) collective-permute-start(bf16[32,4096]{1,0:T(8,128)(2,1)S(1)} %get-tuple-element.17), channel_id=1, source_target_pairs={{0,2},{1,3},{2,0},{3,1},{4,6},{5,7},{6,4},{7,5},{8,10},{9,11},{10,... | collective-permute-start | bytes 786440 | tf_op jit(solution)/shard_map/ppermute | solution.py:152
  99.6 14.2 %collective-permute-start.22 = (bf16[32,4096]{1,0:T(8,128)(2,1)S(1)}, bf16[32,4096]{1,0:T(8,128)(2,1)S(1)}, u32[]{:S(2)}, u32[]{:S(2)}) collective-permute-start(bf16[32,4096]{1,0:T(8,128)(2,1)S(1)} %get-tuple-element.11), channel_id=1, source_target_pairs={{0,4},{1,5},{2,6},{3,7},{4,8},{5,9},{6,10},{7,11},{8,12},{9,13},{1... | collective-permute-start | bytes 786440 | tf_op jit(solution)/shard_map/ppermute | solution.py:160
  109.9 8.3 %collective-permute-start.28 = (bf16[32,4096]{1,0:T(8,128)(2,1)S(1)}, bf16[32,4096]{1,0:T(8,128)(2,1)S(1)}, u32[]{:S(2)}, u32[]{:S(2)}) collective-permute-start(bf16[32,4096]{1,0:T(8,128)(2,1)S(1)} %get-tuple-element.12), channel_id=1, source_target_pairs={{4,0},{5,1},{6,2},{7,3},{8,4},{9,5},{10,6},{11,7},{12,8},{13,9},{1... | collective-permute-start | bytes 786440 | tf_op jit(solution)/shard_map/ppermute | solution.py:167
  (4 other events, 27.2 us)

commit v11 on v10

--- a/solution.py
+++ b/solution.py
@@ -112,27 +112,15 @@
     lines = experts // 4
     me = lax.axis_index("expert")
     line = me // 4
-    swap_row = [(j, j ^ 2) for j in range(experts)]
     here = [(shard, line)]
-    there = [(lax.ppermute(shard, "expert", swap_row), line)]
-    ahead, behind = shard, shard
-    for step in range(1, lines):
-        ahead = lax.ppermute(
-            ahead,
-            "expert",
-            [(j, j + 4) for j in range(experts) if step - 1 <= j // 4 < lines - 1],
-        )
-        behind = lax.ppermute(
-            behind,
-            "expert",
-            [(j, j - 4) for j in range(experts) if 1 <= j // 4 <= lines - step],
-        )
-        here.append((ahead, line - step))
-        here.append((behind, line + step))
-        ahead_row = [(j, j ^ 2) for j in range(experts) if j // 4 >= step]
-        behind_row = [(j, j ^ 2) for j in range(experts) if j // 4 <= lines - 1 - step]
-        there.append((lax.ppermute(ahead, "expert", ahead_row), line - step))
-        there.append((lax.ppermute(behind, "expert", behind_row), line + step))
+    there = [(lax.ppermute(shard, "expert", [(j, j ^ 2) for j in range(experts)]), line)]
+    for reach in range(1, lines):
+        for shift in (reach, -reach):
+            pairs = [(j, j + 4 * shift) for j in range(experts) if 0 <= j // 4 + shift < lines]
+            got = lax.ppermute(shard, "expert", pairs)
+            here.append((got, line - shift))
+            row = [(j, j ^ 2) for j in range(experts) if 0 <= j // 4 - shift < lines]
+            there.append((lax.ppermute(got, "expert", row), line - shift))
     flat = (lines * shard.shape[0],) + shard.shape[1:]
     return place(here, lines, shard).reshape(flat), place(there, lines, shard).reshape(flat)
 
@@ -152,24 +140,16 @@
         got = lax.ppermute(theirs.astype(jnp.bfloat16), "expert", pairs)
         return mine + got.astype(jnp.float32)
 
-    ahead = jnp.zeros(keep.shape[1:], jnp.float32)
-    behind = jnp.zeros(keep.shape[1:], jnp.float32)
-    for step in range(1, lines):
-        target = jnp.clip(line + lines - step, 0, lines - 1)
-        ahead = ahead + row_sum(target, lambda z, s=step: z <= s - 1)
-        ahead = lax.ppermute(
-            ahead.astype(jnp.bfloat16),
-            "expert",
-            [(j, j + 4) for j in range(experts) if j // 4 <= step - 1],
-        ).astype(jnp.float32)
-        target = jnp.clip(line - lines + step, 0, lines - 1)
-        behind = behind + row_sum(target, lambda z, s=step: z >= lines - s)
-        behind = lax.ppermute(
-            behind.astype(jnp.bfloat16),
-            "expert",
-            [(j, j - 4) for j in range(experts) if j // 4 >= lines - step],
-        ).astype(jnp.float32)
-    return row_sum(line, lambda z: True) + ahead + behind
+    total = row_sum(line, lambda z: True)
+    for reach in range(lines - 1, 0, -1):
+        for shift in (reach, -reach):
+            target = jnp.clip(line + shift, 0, lines - 1)
+            part = row_sum(target, lambda z, s=shift: 0 <= z + s < lines)
+            pairs = [(j, j + 4 * shift) for j in range(experts) if 0 <= j // 4 + shift < lines]
+            total = total + lax.ppermute(part.astype(jnp.bfloat16), "expert", pairs).astype(
+                jnp.float32
+            )
+    return total
 
 
 def expert_dense(cent_in, grad_in, gate_mat, up_mat, down_mat):

time: 124 us -> 136 us (1.097); the launches traced: 123 us -> 134 us
  starting transfers between devices: 59.3 us -> 69.1 us
  waiting for transfers between devices: 23.9 us -> 25.9 us
    ppermute x19, starting transfers between devices: 45.6 us -> 56.4 us  [the longest x6 24.3 us: topo_all_gather(): got = lax.ppermute(shard, 'expert', pairs)]
    ppermute x7, waiting for transfers between devices: 0.02 us -> 4.72 us  [row_sum(): got = lax.ppermute(theirs.astype(jnp.bfloat16), 'expert', pairs)]
    ppermute x19, waiting for transfers between devices: 23.8 us -> 21.1 us  [the longest x6 10.9 us: topo_reduce_scatter(): lax.ppermute(part.astype(jnp.bfloat16), 'expert', pairs).astype(jnp.float32)]
  transfers between devices with their start and end apart: 29 -> 29, of which waited for: 9 -> 6; matrix products, arithmetic and copies ran while one was open for 19% -> 16% of each run, Pallas kernels for 0% -> 0%
where the time goes in v11:
time: 136 us; the launch traced here: 134 us
  starting transfers between devices  69.1 us (51%)
  waiting for transfers between devices  25.9 us (19%)
  matrix products  25.1 us (18%)
  other arithmetic  8.69 us (6%)
  local copies, waits for them, and re-layouts  3.44 us (3%)
  between operations  1.4 us (1%)
    ppermute x6, starting transfers between devices, topo_all_gather(): got = lax.ppermute(shard, 'expert', pairs)  24.3 us
    ppermute x6, starting transfers between devices, topo_reduce_scatter(): lax.ppermute(part.astype(jnp.bfloat16), 'expert', pairs).astype(jnp.float32)  17.6 us
    ppermute x7, starting transfers between devices, row_sum(): got = lax.ppermute(theirs.astype(jnp.bfloat16), 'expert', pairs)  12.1 us
    ppermute x6, starting transfers between devices, topo_all_gather(): there.append((lax.ppermute(got, 'expert', row), line - shift))  12 us
    ppermute x6, waiting for transfers between devices, topo_reduce_scatter(): lax.ppermute(part.astype(jnp.bfloat16), 'expert', pairs).astype(jnp.float32)  10.9 us
    ppermute x6, waiting for transfers between devices, topo_all_gather(): there.append((lax.ppermute(got, 'expert', row), line - shift))  8.01 us
    ppermute x7, waiting for transfers between devices, row_sum(): got = lax.ppermute(theirs.astype(jnp.bfloat16), 'expert', pairs)  4.72 us
    dot_general x4, matrix products, expert_dense(): lax.dot_general(gate_grad, gate_mat, against, preferred_element_type=jnp....  4.67 us
  transfers between devices with their start and end apart: 29, of which 6 were waited for; matrix products, arithmetic and copies ran while one was open for 16% of the time, Pallas kernels for 0%

profile of v11, /device:TPU:0, one launch (start us, length us, event | category | flops | bytes accessed | tf_op | source)
XLA Modules:
  0.0 133.6 jit_solution(4020279510245180272)
XLA Ops:
  2.4 2.0 %fusion.126 = (bf16[32,2048]{1,0:T(8,128)(2,1)S(1)}, f32[32,2048]{1,0:T(8,128)}) fusion(bf16[128,2048]{1,0:T(8,128)(2,1)} %param.11, s32[128]{0:T(128)} %param.12), kind=kOutput, calls=%fused_computation.202 | convolution fusion | flops 16846848 | bytes 918016 | tf_op jit(solution)/shard_map/dot_general | solution.py:186
  4.4 2.0 %fusion.127 = (bf16[32,2048]{1,0:T(8,128)(2,1)S(1)}, f32[32,2048]{1,0:T(8,128)}) fusion(f32[32]{0:T(128)S(1)} %convert_reduce_fusion, bf16[128,2048]{1,0:T(8,128)(2,1)} %param.10, s32[128]{0:T(128)} %param.12), kind=kOutput, calls=%fused_computation.203 | convolution fusion | flops 16912384 | bytes 918144 | tf_op jit(solution)/shard_map/dot_general | solution.py:183
  6.4 1.3 collective-permute-start
  7.7 8.4 %collective-permute-start.1 = (bf16[32,4224]{1,0:T(8,128)(2,1)S(1)}, bf16[32,4224]{1,0:T(8,128)(2,1)}, u32[]{:S(2)}, u32[]{:S(2)}) collective-permute-start(bf16[32,4224]{1,0:T(8,128)(2,1)S(1)} %fusion.73), channel_id=1, source_target_pairs={{0,12},{1,13},{2,14},{3,15},{16,28},{17,29},{18,30},{19,31}} | collective-permute-start | bytes 811016 | tf_op jit(solution)/shard_map/ppermute | solution.py:120
  16.0 1.3 collective-permute-start.2
  17.3 6.9 %collective-permute-start.3 = (bf16[32,4224]{1,0:T(8,128)(2,1)S(1)}, bf16[32,4224]{1,0:T(8,128)(2,1)}, u32[]{:S(2)}, u32[]{:S(2)}) collective-permute-start(bf16[32,4224]{1,0:T(8,128)(2,1)S(1)} %fusion.73), channel_id=1, source_target_pairs={{0,8},{1,9},{2,10},{3,11},{4,12},{5,13},{6,14},{7,15},{16,24},{17,... | collective-permute-start | bytes 811016 | tf_op jit(solution)/shard_map/ppermute | solution.py:120
  24.2 1.3 collective-permute-start.4
  25.6 5.3 %collective-permute-start.5 = (bf16[32,4224]{1,0:T(8,128)(2,1)S(1)}, bf16[32,4224]{1,0:T(8,128)(2,1)}, u32[]{:S(2)}, u32[]{:S(2)}) collective-permute-start(bf16[32,4224]{1,0:T(8,128)(2,1)S(1)} %fusion.73), channel_id=1, source_target_pairs={{0,4},{1,5},{2,6},{3,7},{4,8},{5,9},{6,10},{7,11},{8,12},{9,13},{1... | collective-permute-start | bytes 811016 | tf_op jit(solution)/shard_map/ppermute | solution.py:120
  32.0 2.4 %collective-permute-start.15 = (bf16[32,4224]{1,0:T(8,128)(2,1)S(1)}, bf16[32,4224]{1,0:T(8,128)(2,1)S(1)}, u32[]{:S(2)}, u32[]{:S(2)}) collective-permute-start(bf16[32,4224]{1,0:T(8,128)(2,1)S(1)} %fusion.73), channel_id=1, source_target_pairs={{0,2},{1,3},{2,0},{3,1},{4,6},{5,7},{6,4},{7,5},{8,10},{9,11},{10,... | collective-permute-start | bytes 811016 | tf_op jit(solution)/shard_map/ppermute | solution.py:116
  34.4 2.2 %collective-permute-done.4 = bf16[32,4224]{1,0:T(8,128)(2,1)} collective-permute-done((bf16[32,4224]{1,0:T(8,128)(2,1)S(1)}, bf16[32,4224]{1,0:T(8,128)(2,1)}, u32[]{:S(2)}, u32[]{:S(2)}) %collective-permute-start.4) | collective-permute-done | bytes 270368 | tf_op jit(solution)/shard_map/ppermute | solution.py:120
  36.7 2.1 %fusion.35 = bf16[128,4224]{1,0:T(8,128)(2,1)S(1)} fusion(pred[128]{0:T(512)(128)(4,1)S(1)} %broadcast_in_dim.295, pred[128]{0:T(512)(128)(4,1)S(1)} %broadcast_in_dim.290, pred[128]{0:T(512)(128)(4,1)S(1)} %broadcast_in_dim.285, pred[128]{0:T(512)(128)(4,1)S(1)} %broadcast_in_dim.280, pred[128]{0:T(512)(128)(4,1)S(1)} %broadcast_in_dim.275, ...), kind=kLoop, calls=%fused_computation.50 | loop fusion | flops 3784704 | bytes 2974592 | tf_op jit(solution)/shard_map/jit(_where)/select_n | solution.py:107
  40.7 4.0 %collective-permute-start.11 = (bf16[32,4224]{1,0:T(8,128)(2,1)}, bf16[32,4224]{1,0:T(8,128)(2,1)S(1)}, u32[]{:S(2)}, u32[]{:S(2)}) collective-permute-start(bf16[32,4224]{1,0:T(8,128)(2,1)} %collective-permute-done.2), channel_id=1, source_target_pairs={{0,2},{1,3},{2,0},{3,1},{4,6},{5,7},{6,4},{7,5},{16,18},{17,19},{1... | collective-permute-start | bytes 811016 | tf_op jit(solution)/shard_map/ppermute | solution.py:123
  45.4 1.9 %collective-permute-start.13 = (bf16[32,4224]{1,0:T(8,128)(2,1)}, bf16[32,4224]{1,0:T(8,128)(2,1)S(1)}, u32[]{:S(2)}, u32[]{:S(2)}) collective-permute-start(bf16[32,4224]{1,0:T(8,128)(2,1)} %collective-permute-done.4), channel_id=1, source_target_pairs={{0,2},{1,3},{2,0},{3,1},{4,6},{5,7},{6,4},{7,5},{8,10},{9,11},{10,... | collective-permute-start | bytes 811016 | tf_op jit(solution)/shard_map/ppermute | solution.py:123
  49.2 4.1 %collective-permute-start.9 = (bf16[32,4224]{1,0:T(8,128)(2,1)}, bf16[32,4224]{1,0:T(8,128)(2,1)S(1)}, u32[]{:S(2)}, u32[]{:S(2)}) collective-permute-start(bf16[32,4224]{1,0:T(8,128)(2,1)} %collective-permute-done), channel_id=1, source_target_pairs={{0,2},{1,3},{2,0},{3,1},{16,18},{17,19},{18,16},{19,17}} | collective-permute-start | bytes 811016 | tf_op jit(solution)/shard_map/ppermute | solution.py:123
  55.1 2.8 %collective-permute-done.13 = bf16[32,4224]{1,0:T(8,128)(2,1)S(1)} collective-permute-done((bf16[32,4224]{1,0:T(8,128)(2,1)}, bf16[32,4224]{1,0:T(8,128)(2,1)S(1)}, u32[]{:S(2)}, u32[]{:S(2)}) %collective-permute-start.13) | collective-permute-done | bytes 270368 | tf_op jit(solution)/shard_map/ppermute | solution.py:123
  58.0 5.2 %collective-permute-done.9 = bf16[32,4224]{1,0:T(8,128)(2,1)S(1)} collective-permute-done((bf16[32,4224]{1,0:T(8,128)(2,1)}, bf16[32,4224]{1,0:T(8,128)(2,1)S(1)}, u32[]{:S(2)}, u32[]{:S(2)}) %collective-permute-start.9) | collective-permute-done | bytes 270368 | tf_op jit(solution)/shard_map/ppermute | solution.py:123
  70.1 1.2 fusion.9
  75.4 1.2 fusion.13
  76.9 3.6 %collective-permute-start.17 = (bf16[32,4096]{1,0:T(8,128)(2,1)S(1)}, bf16[32,4096]{1,0:T(8,128)(2,1)S(1)}, u32[]{:S(2)}, u32[]{:S(2)}) collective-permute-start(bf16[32,4096]{1,0:T(8,128)(2,1)S(1)} %get-tuple-element.23), channel_id=1, source_target_pairs={{0,2},{1,3},{2,0},{3,1},{16,18},{17,19},{18,16},{19,17}} | collective-permute-start | bytes 786440 | tf_op jit(solution)/shard_map/ppermute | solution.py:140
  81.3 2.2 %collective-permute-start.21 = (bf16[32,4096]{1,0:T(8,128)(2,1)S(1)}, bf16[32,4096]{1,0:T(8,128)(2,1)S(1)}, u32[]{:S(2)}, u32[]{:S(2)}) collective-permute-start(bf16[32,4096]{1,0:T(8,128)(2,1)S(1)} %get-tuple-element.21), channel_id=1, source_target_pairs={{0,2},{1,3},{2,0},{3,1},{4,6},{5,7},{6,4},{7,5},{16,18},{17,19},{1... | collective-permute-start | bytes 786440 | tf_op jit(solution)/shard_map/ppermute | solution.py:140
  84.2 3.9 %collective-permute-start.25 = (bf16[32,4096]{1,0:T(8,128)(2,1)S(1)}, bf16[32,4096]{1,0:T(8,128)(2,1)S(1)}, u32[]{:S(2)}, u32[]{:S(2)}) collective-permute-start(bf16[32,4096]{1,0:T(8,128)(2,1)S(1)} %get-tuple-element.19), channel_id=1, source_target_pairs={{0,2},{1,3},{2,0},{3,1},{4,6},{5,7},{6,4},{7,5},{8,10},{9,11},{10,... | collective-permute-start | bytes 786440 | tf_op jit(solution)/shard_map/ppermute | solution.py:140
  91.5 1.2 fusion.6
  94.6 4.7 %collective-permute-done.25 = bf16[32,4096]{1,0:T(8,128)(2,1)S(1)} collective-permute-done((bf16[32,4096]{1,0:T(8,128)(2,1)S(1)}, bf16[32,4096]{1,0:T(8,128)(2,1)S(1)}, u32[]{:S(2)}, u32[]{:S(2)}) %collective-permute-start.25) | collective-permute-done | bytes 262176 | tf_op jit(solution)/shard_map/ppermute | solution.py:140
  99.7 4.9 %collective-permute-start.18 = (bf16[32,4096]{1,0:T(8,128)(2,1)S(1)}, bf16[32,4096]{1,0:T(8,128)(2,1)S(1)}, u32[]{:S(2)}, u32[]{:S(2)}) collective-permute-start(bf16[32,4096]{1,0:T(8,128)(2,1)S(1)} %get-tuple-element.11), channel_id=1, source_target_pairs={{0,12},{1,13},{2,14},{3,15},{16,28},{17,29},{18,30},{19,31}} | collective-permute-start | bytes 786440 | tf_op jit(solution)/shard_map/ppermute | solution.py:149
  104.6 1.3 collective-permute-start.20
  105.9 5.3 %collective-permute-start.22 = (bf16[32,4096]{1,0:T(8,128)(2,1)S(1)}, bf16[32,4096]{1,0:T(8,128)(2,1)S(1)}, u32[]{:S(2)}, u32[]{:S(2)}) collective-permute-start(bf16[32,4096]{1,0:T(8,128)(2,1)S(1)} %get-tuple-element.15), channel_id=1, source_target_pairs={{0,8},{1,9},{2,10},{3,11},{4,12},{5,13},{6,14},{7,15},{16,24},{17,... | collective-permute-start | bytes 786440 | tf_op jit(solution)/shard_map/ppermute | solution.py:149
  111.2 1.3 collective-permute-start.24
  112.5 3.5 %collective-permute-start.26 = (bf16[32,4096]{1,0:T(8,128)(2,1)S(1)}, bf16[32,4096]{1,0:T(8,128)(2,1)S(1)}, u32[]{:S(2)}, u32[]{:S(2)}) collective-permute-start(bf16[32,4096]{1,0:T(8,128)(2,1)S(1)} %get-tuple-element.13), channel_id=1, source_target_pairs={{0,4},{1,5},{2,6},{3,7},{4,8},{5,9},{6,10},{7,11},{8,12},{9,13},{1... | collective-permute-start | bytes 786440 | tf_op jit(solution)/shard_map/ppermute | solution.py:149
  116.1 1.3 collective-permute-start.28
  117.5 8.6 %collective-permute-done.24 = bf16[32,4096]{1,0:T(8,128)(2,1)S(1)} collective-permute-done((bf16[32,4096]{1,0:T(8,128)(2,1)S(1)}, bf16[32,4096]{1,0:T(8,128)(2,1)S(1)}, u32[]{:S(2)}, u32[]{:S(2)}) %collective-permute-start.24) | collective-permute-done | bytes 262176 | tf_op jit(solution)/shard_map/ppermute | solution.py:149
  126.1 2.3 %collective-permute-done.28 = bf16[32,4096]{1,0:T(8,128)(2,1)S(1)} collective-permute-done((bf16[32,4096]{1,0:T(8,128)(2,1)S(1)}, bf16[32,4096]{1,0:T(8,128)(2,1)S(1)}, u32[]{:S(2)}, u32[]{:S(2)}) %collective-permute-start.28) | collective-permute-done | bytes 262176 | tf_op jit(solution)/shard_map/ppermute | solution.py:149
  130.8 2.8 %select_add_fusion = (f32[128,2048]{1,0:T(8,128)}, f32[128,2048]{1,0:T(8,128)}) fusion(f32[128,2048]{1,0:T(8,128)S(1)} %gather_fusion.1, bf16[128,2048]{1,0:T(8,128)(2,1)S(1)} %copy-done.3, pred[128]{0:T(512)(128)(4,1)S(1)} %compare_and_fusion, f32[128,2048]{1,0:T(8,128)S(1)} %gather_fusion, bf16[128,2048]{1,0:T(8,128)(2,1)} %param.10), kind=kLoop, calls=%fused_computation.51 | loop fusion | flops 1572864 | bytes 5243008 | tf_op jit(solution)/shard_map/add | solution.py:231
  (111 shorter events, 30.0 us)
Async XLA Ops:
  0.6 38.1 %copy-start = (bf16[1,2048,768]{2,1,0:T(8,128)(2,1)S(1)}, bf16[1,2048,768]{2,1,0:T(8,128)(2,1)}, u32[]{:S(2)}) copy-start(bf16[1,2048,768]{2,1,0:T(8,128)(2,1)} %param.16) | copy-start | bytes 9437188
  6.4 19.2 %collective-permute-start = (bf16[32,4224]{1,0:T(8,128)(2,1)S(1)}, bf16[32,4224]{1,0:T(8,128)(2,1)}, u32[]{:S(2)}, u32[]{:S(2)}) collective-permute-start(bf16[32,4224]{1,0:T(8,128)(2,1)S(1)} %fusion.73), channel_id=1, source_target_pairs={{12,0},{13,1},{14,2},{15,3},{28,16},{29,17},{30,18},{31,19}} | collective-permute-start | bytes 811016 | tf_op jit(solution)/shard_map/ppermute | solution.py:120
  7.7 24.3 %collective-permute-start.1 = (bf16[32,4224]{1,0:T(8,128)(2,1)S(1)}, bf16[32,4224]{1,0:T(8,128)(2,1)}, u32[]{:S(2)}, u32[]{:S(2)}) collective-permute-start(bf16[32,4224]{1,0:T(8,128)(2,1)S(1)} %fusion.73), channel_id=1, source_target_pairs={{0,12},{1,13},{2,14},{3,15},{16,28},{17,29},{18,30},{19,31}} | collective-permute-start | bytes 811016 | tf_op jit(solution)/shard_map/ppermute | solution.py:120
  16.0 18.4 %collective-permute-start.2 = (bf16[32,4224]{1,0:T(8,128)(2,1)S(1)}, bf16[32,4224]{1,0:T(8,128)(2,1)}, u32[]{:S(2)}, u32[]{:S(2)}) collective-permute-start(bf16[32,4224]{1,0:T(8,128)(2,1)S(1)} %fusion.73), channel_id=1, source_target_pairs={{8,0},{9,1},{10,2},{11,3},{12,4},{13,5},{14,6},{15,7},{24,16},{25,... | collective-permute-start | bytes 811016 | tf_op jit(solution)/shard_map/ppermute | solution.py:120
  17.3 17.1 %collective-permute-start.3 = (bf16[32,4224]{1,0:T(8,128)(2,1)S(1)}, bf16[32,4224]{1,0:T(8,128)(2,1)}, u32[]{:S(2)}, u32[]{:S(2)}) collective-permute-start(bf16[32,4224]{1,0:T(8,128)(2,1)S(1)} %fusion.73), channel_id=1, source_target_pairs={{0,8},{1,9},{2,10},{3,11},{4,12},{5,13},{6,14},{7,15},{16,24},{17,... | collective-permute-start | bytes 811016 | tf_op jit(solution)/shard_map/ppermute | solution.py:120
  24.2 12.5 %collective-permute-start.4 = (bf16[32,4224]{1,0:T(8,128)(2,1)S(1)}, bf16[32,4224]{1,0:T(8,128)(2,1)}, u32[]{:S(2)}, u32[]{:S(2)}) collective-permute-start(bf16[32,4224]{1,0:T(8,128)(2,1)S(1)} %fusion.73), channel_id=1, source_target_pairs={{4,0},{5,1},{6,2},{7,3},{8,4},{9,5},{10,6},{11,7},{12,8},{13,9},{1... | collective-permute-start | bytes 811016 | tf_op jit(solution)/shard_map/ppermute | solution.py:120
  25.6 11.1 %collective-permute-start.5 = (bf16[32,4224]{1,0:T(8,128)(2,1)S(1)}, bf16[32,4224]{1,0:T(8,128)(2,1)}, u32[]{:S(2)}, u32[]{:S(2)}) collective-permute-start(bf16[32,4224]{1,0:T(8,128)(2,1)S(1)} %fusion.73), channel_id=1, source_target_pairs={{0,4},{1,5},{2,6},{3,7},{4,8},{5,9},{6,10},{7,11},{8,12},{9,13},{1... | collective-permute-start | bytes 811016 | tf_op jit(solution)/shard_map/ppermute | solution.py:120
  32.0 16.5 %collective-permute-start.15 = (bf16[32,4224]{1,0:T(8,128)(2,1)S(1)}, bf16[32,4224]{1,0:T(8,128)(2,1)S(1)}, u32[]{:S(2)}, u32[]{:S(2)}) collective-permute-start(bf16[32,4224]{1,0:T(8,128)(2,1)S(1)} %fusion.73), channel_id=1, source_target_pairs={{0,2},{1,3},{2,0},{3,1},{4,6},{5,7},{6,4},{7,5},{8,10},{9,11},{10,... | collective-permute-start | bytes 811016 | tf_op jit(solution)/shard_map/ppermute | solution.py:116
  40.0 9.2 %collective-permute-start.10 = (bf16[32,4224]{1,0:T(8,128)(2,1)}, bf16[32,4224]{1,0:T(8,128)(2,1)S(1)}, u32[]{:S(2)}, u32[]{:S(2)}) collective-permute-start(bf16[32,4224]{1,0:T(8,128)(2,1)} %collective-permute-done.1), channel_id=1, source_target_pairs={{12,14},{13,15},{14,12},{15,13},{28,30},{29,31},{30,28},{31,29}} | collective-permute-start | bytes 811016 | tf_op jit(solution)/shard_map/ppermute | solution.py:123
  40.7 13.8 %collective-permute-start.11 = (bf16[32,4224]{1,0:T(8,128)(2,1)}, bf16[32,4224]{1,0:T(8,128)(2,1)S(1)}, u32[]{:S(2)}, u32[]{:S(2)}) collective-permute-start(bf16[32,4224]{1,0:T(8,128)(2,1)} %collective-permute-done.2), channel_id=1, source_target_pairs={{0,2},{1,3},{2,0},{3,1},{4,6},{5,7},{6,4},{7,5},{16,18},{17,19},{1... | collective-permute-start | bytes 811016 | tf_op jit(solution)/shard_map/ppermute | solution.py:123
  44.7 9.9 %collective-permute-start.12 = (bf16[32,4224]{1,0:T(8,128)(2,1)}, bf16[32,4224]{1,0:T(8,128)(2,1)S(1)}, u32[]{:S(2)}, u32[]{:S(2)}) collective-permute-start(bf16[32,4224]{1,0:T(8,128)(2,1)} %collective-permute-done.3), channel_id=1, source_target_pairs={{8,10},{9,11},{10,8},{11,9},{12,14},{13,15},{14,12},{15,13},{24,26... | collective-permute-start | bytes 811016 | tf_op jit(solution)/shard_map/ppermute | solution.py:123
  45.4 12.6 %collective-permute-start.13 = (bf16[32,4224]{1,0:T(8,128)(2,1)}, bf16[32,4224]{1,0:T(8,128)(2,1)S(1)}, u32[]{:S(2)}, u32[]{:S(2)}) collective-permute-start(bf16[32,4224]{1,0:T(8,128)(2,1)} %collective-permute-done.4), channel_id=1, source_target_pairs={{0,2},{1,3},{2,0},{3,1},{4,6},{5,7},{6,4},{7,5},{8,10},{9,11},{10,... | collective-permute-start | bytes 811016 | tf_op jit(solution)/shard_map/ppermute | solution.py:123
  48.5 9.5 %collective-permute-start.14 = (bf16[32,4224]{1,0:T(8,128)(2,1)}, bf16[32,4224]{1,0:T(8,128)(2,1)S(1)}, u32[]{:S(2)}, u32[]{:S(2)}) collective-permute-start(bf16[32,4224]{1,0:T(8,128)(2,1)} %collective-permute-done.5), channel_id=1, source_target_pairs={{4,6},{5,7},{6,4},{7,5},{8,10},{9,11},{10,8},{11,9},{12,14},{13,15... | collective-permute-start | bytes 811016 | tf_op jit(solution)/shard_map/ppermute | solution.py:123
  49.2 13.9 %collective-permute-start.9 = (bf16[32,4224]{1,0:T(8,128)(2,1)}, bf16[32,4224]{1,0:T(8,128)(2,1)S(1)}, u32[]{:S(2)}, u32[]{:S(2)}) collective-permute-start(bf16[32,4224]{1,0:T(8,128)(2,1)} %collective-permute-done), channel_id=1, source_target_pairs={{0,2},{1,3},{2,0},{3,1},{16,18},{17,19},{18,16},{19,17}} | collective-permute-start | bytes 811016 | tf_op jit(solution)/shard_map/ppermute | solution.py:123
  54.5 16.8 %collective-permute-start.7 = (bf16[2048,768]{1,0:T(8,128)(2,1)S(1)}, bf16[2048,768]{1,0:T(8,128)(2,1)S(1)}, u32[]{:S(2)}, u32[]{:S(2)}) collective-permute-start(bf16[2048,768]{1,0:T(8,128)(2,1)S(1)} %bitcast.147), channel_id=1, source_target_pairs={{0,1},{1,0},{2,3},{3,2},{4,5},{5,4},{6,7},{7,6},{8,9},{9,8},{10,11... | collective-permute-start | bytes 9437192 | tf_op jit(solution)/shard_map/ppermute | solution.py:204
  54.6 17.3 %collective-permute-start.6 = (bf16[2048,768]{1,0:T(8,128)(2,1)S(1)}, bf16[2048,768]{1,0:T(8,128)(2,1)S(1)}, u32[]{:S(2)}, u32[]{:S(2)}) collective-permute-start(bf16[2048,768]{1,0:T(8,128)(2,1)S(1)} %bitcast.149), channel_id=1, source_target_pairs={{0,1},{1,0},{2,3},{3,2},{4,5},{5,4},{6,7},{7,6},{8,9},{9,8},{10,11... | collective-permute-start | bytes 9437192 | tf_op jit(solution)/shard_map/ppermute | solution.py:203
  58.0 14.5 %collective-permute-start.8 = (bf16[768,2048]{1,0:T(8,128)(2,1)S(1)}, bf16[768,2048]{1,0:T(8,128)(2,1)S(1)}, u32[]{:S(2)}, u32[]{:S(2)}) collective-permute-start(bf16[768,2048]{1,0:T(8,128)(2,1)S(1)} %bitcast.148), channel_id=1, source_target_pairs={{0,1},{1,0},{2,3},{3,2},{4,5},{5,4},{6,7},{7,6},{8,9},{9,8},{10,11... | collective-permute-start | bytes 9437192 | tf_op jit(solution)/shard_map/ppermute | solution.py:205
  76.9 16.4 %collective-permute-start.17 = (bf16[32,4096]{1,0:T(8,128)(2,1)S(1)}, bf16[32,4096]{1,0:T(8,128)(2,1)S(1)}, u32[]{:S(2)}, u32[]{:S(2)}) collective-permute-start(bf16[32,4096]{1,0:T(8,128)(2,1)S(1)} %get-tuple-element.23), channel_id=1, source_target_pairs={{0,2},{1,3},{2,0},{3,1},{16,18},{17,19},{18,16},{19,17}} | collective-permute-start | bytes 786440 | tf_op jit(solution)/shard_map/ppermute | solution.py:140
  80.6 13.6 %collective-permute-start.19 = (bf16[32,4096]{1,0:T(8,128)(2,1)S(1)}, bf16[32,4096]{1,0:T(8,128)(2,1)S(1)}, u32[]{:S(2)}, u32[]{:S(2)}) collective-permute-start(bf16[32,4096]{1,0:T(8,128)(2,1)S(1)} %get-tuple-element.22), channel_id=1, source_target_pairs={{12,14},{13,15},{14,12},{15,13},{28,30},{29,31},{30,28},{31,29}} | collective-permute-start | bytes 786440 | tf_op jit(solution)/shard_map/ppermute | solution.py:140
  81.3 13.3 %collective-permute-start.21 = (bf16[32,4096]{1,0:T(8,128)(2,1)S(1)}, bf16[32,4096]{1,0:T(8,128)(2,1)S(1)}, u32[]{:S(2)}, u32[]{:S(2)}) collective-permute-start(bf16[32,4096]{1,0:T(8,128)(2,1)S(1)} %get-tuple-element.21), channel_id=1, source_target_pairs={{0,2},{1,3},{2,0},{3,1},{4,6},{5,7},{6,4},{7,5},{16,18},{17,19},{1... | collective-permute-start | bytes 786440 | tf_op jit(solution)/shard_map/ppermute | solution.py:140
  83.5 11.1 %collective-permute-start.23 = (bf16[32,4096]{1,0:T(8,128)(2,1)S(1)}, bf16[32,4096]{1,0:T(8,128)(2,1)S(1)}, u32[]{:S(2)}, u32[]{:S(2)}) collective-permute-start(bf16[32,4096]{1,0:T(8,128)(2,1)S(1)} %get-tuple-element.20), channel_id=1, source_target_pairs={{8,10},{9,11},{10,8},{11,9},{12,14},{13,15},{14,12},{15,13},{24,26... | collective-permute-start | bytes 786440 | tf_op jit(solution)/shard_map/ppermute | solution.py:140
  84.2 15.1 %collective-permute-start.25 = (bf16[32,4096]{1,0:T(8,128)(2,1)S(1)}, bf16[32,4096]{1,0:T(8,128)(2,1)S(1)}, u32[]{:S(2)}, u32[]{:S(2)}) collective-permute-start(bf16[32,4096]{1,0:T(8,128)(2,1)S(1)} %get-tuple-element.19), channel_id=1, source_target_pairs={{0,2},{1,3},{2,0},{3,1},{4,6},{5,7},{6,4},{7,5},{8,10},{9,11},{10,... | collective-permute-start | bytes 786440 | tf_op jit(solution)/shard_map/ppermute | solution.py:140
  93.4 5.9 %collective-permute-start.27 = (bf16[32,4096]{1,0:T(8,128)(2,1)S(1)}, bf16[32,4096]{1,0:T(8,128)(2,1)S(1)}, u32[]{:S(2)}, u32[]{:S(2)}) collective-permute-start(bf16[32,4096]{1,0:T(8,128)(2,1)S(1)} %get-tuple-element.18), channel_id=1, source_target_pairs={{4,6},{5,7},{6,4},{7,5},{8,10},{9,11},{10,8},{11,9},{12,14},{13,15... | collective-permute-start | bytes 786440 | tf_op jit(solution)/shard_map/ppermute | solution.py:140
  94.3 18.3 %collective-permute-start.16 = (bf16[32,4096]{1,0:T(8,128)(2,1)S(1)}, bf16[32,4096]{1,0:T(8,128)(2,1)S(1)}, u32[]{:S(2)}, u32[]{:S(2)}) collective-permute-start(bf16[32,4096]{1,0:T(8,128)(2,1)S(1)} %get-tuple-element.17), channel_id=1, source_target_pairs={{0,2},{1,3},{2,0},{3,1},{4,6},{5,7},{6,4},{7,5},{8,10},{9,11},{10,... | collective-permute-start | bytes 786440 | tf_op jit(solution)/shard_map/ppermute | solution.py:140
  99.3 29.3 %copy-start.4 = (f32[32,2048]{1,0:T(8,128)S(1)}, f32[32,2048]{1,0:T(8,128)}, u32[]{:S(2)}) copy-start(f32[32,2048]{1,0:T(8,128)} %get-tuple-element.29) | copy-start | bytes 786436
  99.3 29.3 %copy-start.5 = (f32[32,2048]{1,0:T(8,128)S(1)}, f32[32,2048]{1,0:T(8,128)}, u32[]{:S(2)}) copy-start(f32[32,2048]{1,0:T(8,128)} %get-tuple-element.31) | copy-start | bytes 786436
  99.7 16.4 %collective-permute-start.18 = (bf16[32,4096]{1,0:T(8,128)(2,1)S(1)}, bf16[32,4096]{1,0:T(8,128)(2,1)S(1)}, u32[]{:S(2)}, u32[]{:S(2)}) collective-permute-start(bf16[32,4096]{1,0:T(8,128)(2,1)S(1)} %get-tuple-element.11), channel_id=1, source_target_pairs={{0,12},{1,13},{2,14},{3,15},{16,28},{17,29},{18,30},{19,31}} | collective-permute-start | bytes 786440 | tf_op jit(solution)/shard_map/ppermute | solution.py:149
  104.6 12.8 %collective-permute-start.20 = (bf16[32,4096]{1,0:T(8,128)(2,1)S(1)}, bf16[32,4096]{1,0:T(8,128)(2,1)S(1)}, u32[]{:S(2)}, u32[]{:S(2)}) collective-permute-start(bf16[32,4096]{1,0:T(8,128)(2,1)S(1)} %get-tuple-element.16), channel_id=1, source_target_pairs={{12,0},{13,1},{14,2},{15,3},{28,16},{29,17},{30,18},{31,19}} | collective-permute-start | bytes 786440 | tf_op jit(solution)/shard_map/ppermute | solution.py:149
  105.9 11.5 %collective-permute-start.22 = (bf16[32,4096]{1,0:T(8,128)(2,1)S(1)}, bf16[32,4096]{1,0:T(8,128)(2,1)S(1)}, u32[]{:S(2)}, u32[]{:S(2)}) collective-permute-start(bf16[32,4096]{1,0:T(8,128)(2,1)S(1)} %get-tuple-element.15), channel_id=1, source_target_pairs={{0,8},{1,9},{2,10},{3,11},{4,12},{5,13},{6,14},{7,15},{16,24},{17,... | collective-permute-start | bytes 786440 | tf_op jit(solution)/shard_map/ppermute | solution.py:149
  111.2 14.8 %collective-permute-start.24 = (bf16[32,4096]{1,0:T(8,128)(2,1)S(1)}, bf16[32,4096]{1,0:T(8,128)(2,1)S(1)}, u32[]{:S(2)}, u32[]{:S(2)}) collective-permute-start(bf16[32,4096]{1,0:T(8,128)(2,1)S(1)} %get-tuple-element.14), channel_id=1, source_target_pairs={{8,0},{9,1},{10,2},{11,3},{12,4},{13,5},{14,6},{15,7},{24,16},{25,... | collective-permute-start | bytes 786440 | tf_op jit(solution)/shard_map/ppermute | solution.py:149
  112.5 13.5 %collective-permute-start.26 = (bf16[32,4096]{1,0:T(8,128)(2,1)S(1)}, bf16[32,4096]{1,0:T(8,128)(2,1)S(1)}, u32[]{:S(2)}, u32[]{:S(2)}) collective-permute-start(bf16[32,4096]{1,0:T(8,128)(2,1)S(1)} %get-tuple-element.13), channel_id=1, source_target_pairs={{0,4},{1,5},{2,6},{3,7},{4,8},{5,9},{6,10},{7,11},{8,12},{9,13},{1... | collective-permute-start | bytes 786440 | tf_op jit(solution)/shard_map/ppermute | solution.py:149
  116.1 12.2 %collective-permute-start.28 = (bf16[32,4096]{1,0:T(8,128)(2,1)S(1)}, bf16[32,4096]{1,0:T(8,128)(2,1)S(1)}, u32[]{:S(2)}, u32[]{:S(2)}) collective-permute-start(bf16[32,4096]{1,0:T(8,128)(2,1)S(1)} %get-tuple-element.12), channel_id=1, source_target_pairs={{4,0},{5,1},{6,2},{7,3},{8,4},{9,5},{10,6},{11,7},{12,8},{13,9},{1... | collective-permute-start | bytes 786440 | tf_op jit(solution)/shard_map/ppermute | solution.py:149
  (4 other events, 22.3 us)

commit v12 on v8

--- a/solution.py
+++ b/solution.py
@@ -204,11 +204,15 @@
     )
     counts = jnp.sum(member.astype(jnp.float32), axis=0)
     contract = (((0,), (0,)), ((), ()))
-    centroid = (
-        lax.dot_general(member, tokens, contract, preferred_element_type=jnp.float32)
-        / counts[:, None]
-    )
-    grad_sum = lax.dot_general(member, out_grad, contract, preferred_element_type=jnp.float32)
+    model_width = tokens.shape[1]
+    sums = lax.dot_general(
+        member,
+        jnp.concatenate([tokens, out_grad], axis=1),
+        contract,
+        preferred_element_type=jnp.float32,
+    )
+    centroid = sums[:, :model_width] / counts[:, None]
+    grad_sum = sums[:, model_width:]
     experts = lax.axis_size("expert")
     model_width = tokens.shape[1]
     picked = routes[:, :, None] == jnp.arange(experts, dtype=jnp.int32)[None, None, :]

time: 122 us -> 119 us (0.975)
  matrix products: 16.6 us -> 14.2 us
    dot_general x2 -> x1, matrix products: 3.93 us -> 1.49 us  [per_device_dense(): lax.dot_general(member, jnp.concatenate([tokens, out_grad], axis=1), cont...]
  transfers between devices with their start and end apart: 29 -> 29, of which waited for: 10 -> 10; matrix products, arithmetic and copies ran while one was open for 11% -> 12% of each run, Pallas kernels for 0% -> 0%
where the time goes in v12:
time: 119 us
  starting transfers between devices  60.9 us (51%)
  waiting for transfers between devices  27.4 us (23%)
  matrix products  14.2 us (12%)
  other arithmetic  9.09 us (8%)
  local copies, waits for them, and re-layouts  5.66 us (5%)
  between operations  1.3 us (1%)
    ppermute x3, starting transfers between devices, topo_reduce_scatter(): lax.ppermute(ahead.astype(jnp.bfloat16), 'expert', [(j, j + 4) for j in r...  22 us
    ppermute x7, starting transfers between devices, row_sum(): got = lax.ppermute(theirs.astype(jnp.bfloat16), 'expert', pairs)  11.2 us
    ppermute x3, waiting for transfers between devices, topo_all_gather(): lax.ppermute(behind, 'expert', [(j, j - 4) for j in range(experts) if 1 <...  9.06 us
    ppermute x3, starting transfers between devices, topo_all_gather(): there.append((lax.ppermute(behind, 'expert', behind_row), line + step))  8.5 us
    ppermute x3, waiting for transfers between devices, topo_reduce_scatter(): lax.ppermute(ahead.astype(jnp.bfloat16), 'expert', [(j, j + 4) for j in r...  7.04 us
    ppermute x3, starting transfers between devices, topo_all_gather(): lax.ppermute(ahead, 'expert', [(j, j + 4) for j in range(experts) if step...  6.93 us
    select_n x4, other arithmetic, pick(): chosen = jnp.where(index == position, options[position], chosen)  4.68 us
    ppermute x3, waiting for transfers between devices, topo_reduce_scatter(): lax.ppermute(behind.astype(jnp.bfloat16), 'expert', [(j, j - 4) for j in...  4.41 us
  transfers between devices with their start and end apart: 29, of which 10 were waited for; matrix products, arithmetic and copies ran while one was open for 12% of the time, Pallas kernels for 0%

profile of v12, /device:TPU:0, one launch (start us, length us, event | category | flops | bytes accessed | tf_op | source)
XLA Modules:
  0.0 118.6 jit_solution(10005144724676390623)
XLA Ops:
  1.4 1.5 %fusion.12 = f32[32,4096]{1,0:T(8,128)S(1)} fusion(bf16[128,2048]{1,0:T(8,128)(2,1)} %param.11, bf16[128,2048]{1,0:T(8,128)(2,1)} %param.10, s32[128]{0:T(128)} %param.12), kind=kOutput, calls=%fused_computation.26 | convolution fusion | flops 35655680 | bytes 1573376 | tf_op jit(solution)/shard_map/dot_general | solution.py:208
  3.2 1.3 %collective-permute-start = (bf16[32,4224]{1,0:T(8,128)(2,1)S(1)}, bf16[32,4224]{1,0:T(8,128)(2,1)S(1)}, u32[]{:S(2)}, u32[]{:S(2)}) collective-permute-start(bf16[32,4224]{1,0:T(8,128)(2,1)S(1)} %fusion.49), channel_id=1, source_target_pairs={{4,0},{5,1},{6,2},{7,3},{8,4},{9,5},{10,6},{11,7},{12,8},{13,9},{1... | collective-permute-start | bytes 811016 | tf_op jit(solution)/shard_map/ppermute | solution.py:125
  4.5 5.6 %collective-permute-start.3 = (bf16[32,4224]{1,0:T(8,128)(2,1)S(1)}, bf16[32,4224]{1,0:T(8,128)(2,1)S(1)}, u32[]{:S(2)}, u32[]{:S(2)}) collective-permute-start(bf16[32,4224]{1,0:T(8,128)(2,1)S(1)} %fusion.49), channel_id=1, source_target_pairs={{0,4},{1,5},{2,6},{3,7},{4,8},{5,9},{6,10},{7,11},{8,12},{9,13},{1... | collective-permute-start | bytes 811016 | tf_op jit(solution)/shard_map/ppermute | solution.py:120
  10.1 4.5 %collective-permute-done = bf16[32,4224]{1,0:T(8,128)(2,1)S(1)} collective-permute-done((bf16[32,4224]{1,0:T(8,128)(2,1)S(1)}, bf16[32,4224]{1,0:T(8,128)(2,1)S(1)}, u32[]{:S(2)}, u32[]{:S(2)}) %collective-permute-start) | collective-permute-done | bytes 270368 | tf_op jit(solution)/shard_map/ppermute | solution.py:125
  14.6 1.3 %collective-permute-start.1 = (bf16[32,4224]{1,0:T(8,128)(2,1)S(1)}, bf16[32,4224]{1,0:T(8,128)(2,1)S(1)}, u32[]{:S(2)}, u32[]{:S(2)}) collective-permute-start(bf16[32,4224]{1,0:T(8,128)(2,1)S(1)} %collective-permute-done), channel_id=1, source_target_pairs={{4,0},{5,1},{6,2},{7,3},{8,4},{9,5},{10,6},{11,7},{20,16},{21,17},... | collective-permute-start | bytes 811016 | tf_op jit(solution)/shard_map/ppermute | solution.py:125
  16.6 1.7 %collective-permute-start.12 = (bf16[32,4224]{1,0:T(8,128)(2,1)S(1)}, bf16[32,4224]{1,0:T(8,128)(2,1)S(1)}, u32[]{:S(2)}, u32[]{:S(2)}) collective-permute-start(bf16[32,4224]{1,0:T(8,128)(2,1)S(1)} %fusion.49), channel_id=1, source_target_pairs={{0,2},{1,3},{2,0},{3,1},{4,6},{5,7},{6,4},{7,5},{8,10},{9,11},{10,... | collective-permute-start | bytes 811016 | tf_op jit(solution)/shard_map/ppermute | solution.py:117
  18.4 2.2 %collective-permute-start.10 = (bf16[32,4224]{1,0:T(8,128)(2,1)S(1)}, bf16[32,4224]{1,0:T(8,128)(2,1)S(1)}, u32[]{:S(2)}, u32[]{:S(2)}) collective-permute-start(bf16[32,4224]{1,0:T(8,128)(2,1)S(1)} %collective-permute-done), channel_id=1, source_target_pairs={{0,2},{1,3},{2,0},{3,1},{4,6},{5,7},{6,4},{7,5},{8,10},{9,11},{10,... | collective-permute-start | bytes 811016 | tf_op jit(solution)/shard_map/ppermute | solution.py:135
  20.6 3.6 %collective-permute-done.1 = bf16[32,4224]{1,0:T(8,128)(2,1)S(1)} collective-permute-done((bf16[32,4224]{1,0:T(8,128)(2,1)S(1)}, bf16[32,4224]{1,0:T(8,128)(2,1)S(1)}, u32[]{:S(2)}, u32[]{:S(2)}) %collective-permute-start.1) | collective-permute-done | bytes 270368 | tf_op jit(solution)/shard_map/ppermute | solution.py:125
  24.2 1.3 %collective-permute-start.2 = (bf16[32,4224]{1,0:T(8,128)(2,1)S(1)}, bf16[32,4224]{1,0:T(8,128)(2,1)S(1)}, u32[]{:S(2)}, u32[]{:S(2)}) collective-permute-start(bf16[32,4224]{1,0:T(8,128)(2,1)S(1)} %collective-permute-done.1), channel_id=1, source_target_pairs={{4,0},{5,1},{6,2},{7,3},{20,16},{21,17},{22,18},{23,19}} | collective-permute-start | bytes 811016 | tf_op jit(solution)/shard_map/ppermute | solution.py:125
  26.9 3.3 %collective-permute-start.8 = (bf16[32,4224]{1,0:T(8,128)(2,1)S(1)}, bf16[32,4224]{1,0:T(8,128)(2,1)S(1)}, u32[]{:S(2)}, u32[]{:S(2)}) collective-permute-start(bf16[32,4224]{1,0:T(8,128)(2,1)S(1)} %collective-permute-done.1), channel_id=1, source_target_pairs={{0,2},{1,3},{2,0},{3,1},{4,6},{5,7},{6,4},{7,5},{16,18},{17,19},{1... | collective-permute-start | bytes 811016 | tf_op jit(solution)/shard_map/ppermute | solution.py:135
  30.5 1.4 %collective-permute-start.9 = (bf16[32,4224]{1,0:T(8,128)(2,1)S(1)}, bf16[32,4224]{1,0:T(8,128)(2,1)}, u32[]{:S(2)}, u32[]{:S(2)}) collective-permute-start(bf16[32,4224]{1,0:T(8,128)(2,1)S(1)} %collective-permute-done.4), channel_id=1, source_target_pairs={{8,10},{9,11},{10,8},{11,9},{12,14},{13,15},{14,12},{15,13},{24,26... | collective-permute-start | bytes 811016 | tf_op jit(solution)/shard_map/ppermute | solution.py:134
  32.8 3.0 %collective-permute-start.6 = (bf16[32,4224]{1,0:T(8,128)(2,1)S(1)}, bf16[32,4224]{1,0:T(8,128)(2,1)}, u32[]{:S(2)}, u32[]{:S(2)}) collective-permute-start(bf16[32,4224]{1,0:T(8,128)(2,1)S(1)} %collective-permute-done.2), channel_id=1, source_target_pairs={{0,2},{1,3},{2,0},{3,1},{16,18},{17,19},{18,16},{19,17}} | collective-permute-start | bytes 811016 | tf_op jit(solution)/shard_map/ppermute | solution.py:135
  35.8 1.4 %collective-permute-start.7 = (bf16[32,4224]{1,0:T(8,128)(2,1)S(1)}, bf16[32,4224]{1,0:T(8,128)(2,1)}, u32[]{:S(2)}, u32[]{:S(2)}) collective-permute-start(bf16[32,4224]{1,0:T(8,128)(2,1)S(1)} %collective-permute-done.5), channel_id=1, source_target_pairs={{12,14},{13,15},{14,12},{15,13},{28,30},{29,31},{30,28},{31,29}} | collective-permute-start | bytes 811016 | tf_op jit(solution)/shard_map/ppermute | solution.py:134
  37.9 3.9 %collective-permute-done.6 = bf16[32,4224]{1,0:T(8,128)(2,1)} collective-permute-done((bf16[32,4224]{1,0:T(8,128)(2,1)S(1)}, bf16[32,4224]{1,0:T(8,128)(2,1)}, u32[]{:S(2)}, u32[]{:S(2)}) %collective-permute-start.6) | collective-permute-done | bytes 270368 | tf_op jit(solution)/shard_map/ppermute | solution.py:135
  41.8 2.1 %broadcast_select_fusion.1 = bf16[4,1,32,4224]{3,2,1,0:T(8,128)(2,1)S(1)} fusion(pred[]{:T(512)S(6)} %eq.148, bf16[32,4224]{1,0:T(8,128)(2,1)S(1)} %fusion.49, pred[4]{0:T(512)(128)(4,1)S(1)} %get-tuple-element.24, bf16[32,4224]{1,0:T(8,128)(2,1)S(1)} %collective-permute-done.3, pred[4]{0:T(512)(128)(4,1)S(1)} %get-tuple-element.25, ...), kind=kLoop, calls=%fused_computation.25 | loop fusion | flops 8110080 | bytes 4866077 | tf_op jit(solution)/shard_map/jit(_where)/select_n | solution.py:99
  44.0 2.2 %broadcast_select_fusion = bf16[4,1,32,4224]{3,2,1,0:T(8,128)(2,1)S(1)} fusion(pred[]{:T(512)S(6)} %eq.148, bf16[32,4224]{1,0:T(8,128)(2,1)S(1)} %fusion.49, pred[4]{0:T(512)(128)(4,1)S(1)} %get-tuple-element.24, bf16[32,4224]{1,0:T(8,128)(2,1)S(1)} %collective-permute-done.3, pred[4]{0:T(512)(128)(4,1)S(1)} %get-tuple-element.25, ...), kind=kLoop, calls=%fused_computation.24 | loop fusion | flops 8110080 | bytes 4866077 | tf_op jit(solution)/shard_map/jit(_where)/select_n | solution.py:99
  46.6 1.4 %copy-done = bf16[1,2048,768]{2,1,0:T(8,128)(2,1)S(1)} copy-done((bf16[1,2048,768]{2,1,0:T(8,128)(2,1)S(1)}, bf16[1,2048,768]{2,1,0:T(8,128)(2,1)}, u32[]{:S(2)}) %copy-start) | copy-done | bytes 3145752
  53.9 1.1 fusion.41
  61.4 1.2 %fusion.4 = f32[256,2048]{1,0:T(8,128)S(1)} fusion(f32[256,2048]{1,0:T(8,128)S(1)} %fusion.6, f32[256,2048]{1,0:T(8,128)S(1)} %fusion.42, bf16[2048,768]{1,0:T(8,128)(2,1)S(1)} %collective-permute-done.13, f32[256]{0:T(256)S(1)} %get-tuple-element.3, f32[256,768]{1,0:T(8,128)S(1)} %fusion.22, f32[256,768]{1,0:T(8,128)S(1)} %fusion.16, f32[256,768]{1,0:T(8,128)S(1)} %fusion.20), kind=kOutput, calls=%fused_computation.9 | convolution fusion | flops 809893888 | bytes 11797504 | tf_op jit(solution)/shard_map/dot_general | solution.py:192
  63.6 3.3 %collective-permute-start.17 = (bf16[32,4096]{1,0:T(8,128)(2,1)S(1)}, bf16[32,4096]{1,0:T(8,128)(2,1)S(1)}, u32[]{:S(2)}, u32[]{:S(2)}) collective-permute-start(bf16[32,4096]{1,0:T(8,128)(2,1)S(1)} %get-tuple-element.21), channel_id=1, source_target_pairs={{0,2},{1,3},{2,0},{3,1},{16,18},{17,19},{18,16},{19,17}} | collective-permute-start | bytes 786440 | tf_op jit(solution)/shard_map/ppermute | solution.py:157
  67.8 2.6 %collective-permute-start.19 = (bf16[32,4096]{1,0:T(8,128)(2,1)S(1)}, bf16[32,4096]{1,0:T(8,128)(2,1)S(1)}, u32[]{:S(2)}, u32[]{:S(2)}) collective-permute-start(bf16[32,4096]{1,0:T(8,128)(2,1)S(1)} %get-tuple-element.20), channel_id=1, source_target_pairs={{0,2},{1,3},{2,0},{3,1},{4,6},{5,7},{6,4},{7,5},{16,18},{17,19},{1... | collective-permute-start | bytes 786440 | tf_op jit(solution)/shard_map/ppermute | solution.py:157
  71.1 2.6 %collective-permute-done.17 = bf16[32,4096]{1,0:T(8,128)(2,1)S(1)} collective-permute-done((bf16[32,4096]{1,0:T(8,128)(2,1)S(1)}, bf16[32,4096]{1,0:T(8,128)(2,1)S(1)}, u32[]{:S(2)}, u32[]{:S(2)}) %collective-permute-start.17) | collective-permute-done | bytes 262176 | tf_op jit(solution)/shard_map/ppermute | solution.py:157
  73.8 2.7 %collective-permute-start.18 = (bf16[32,4096]{1,0:T(8,128)(2,1)S(1)}, bf16[32,4096]{1,0:T(8,128)(2,1)S(1)}, u32[]{:S(2)}, u32[]{:S(2)}) collective-permute-start(bf16[32,4096]{1,0:T(8,128)(2,1)S(1)} %get-tuple-element.11), channel_id=1, source_target_pairs={{0,4},{1,5},{2,6},{3,7},{16,20},{17,21},{18,22},{19,23}} | collective-permute-start | bytes 786440 | tf_op jit(solution)/shard_map/ppermute | solution.py:165
  77.3 2.8 %collective-permute-start.21 = (bf16[32,4096]{1,0:T(8,128)(2,1)S(1)}, bf16[32,4096]{1,0:T(8,128)(2,1)S(1)}, u32[]{:S(2)}, u32[]{:S(2)}) collective-permute-start(bf16[32,4096]{1,0:T(8,128)(2,1)S(1)} %get-tuple-element.19), channel_id=1, source_target_pairs={{0,2},{1,3},{2,0},{3,1},{4,6},{5,7},{6,4},{7,5},{8,10},{9,11},{10,... | collective-permute-start | bytes 786440 | tf_op jit(solution)/shard_map/ppermute | solution.py:157
  80.8 1.3 %collective-permute-done.18 = bf16[32,4096]{1,0:T(8,128)(2,1)S(1)} collective-permute-done((bf16[32,4096]{1,0:T(8,128)(2,1)S(1)}, bf16[32,4096]{1,0:T(8,128)(2,1)S(1)}, u32[]{:S(2)}, u32[]{:S(2)}) %collective-permute-start.18) | collective-permute-done | bytes 262176 | tf_op jit(solution)/shard_map/ppermute | solution.py:165
  82.2 4.5 %collective-permute-start.20 = (bf16[32,4096]{1,0:T(8,128)(2,1)S(1)}, bf16[32,4096]{1,0:T(8,128)(2,1)S(1)}, u32[]{:S(2)}, u32[]{:S(2)}) collective-permute-start(bf16[32,4096]{1,0:T(8,128)(2,1)S(1)} %get-tuple-element.9), channel_id=1, source_target_pairs={{0,4},{1,5},{2,6},{3,7},{4,8},{5,9},{6,10},{7,11},{16,20},{17,21},... | collective-permute-start | bytes 786440 | tf_op jit(solution)/shard_map/ppermute | solution.py:165
  87.9 3.3 %collective-permute-done.20 = bf16[32,4096]{1,0:T(8,128)(2,1)S(1)} collective-permute-done((bf16[32,4096]{1,0:T(8,128)(2,1)S(1)}, bf16[32,4096]{1,0:T(8,128)(2,1)S(1)}, u32[]{:S(2)}, u32[]{:S(2)}) %collective-permute-start.20) | collective-permute-done | bytes 262176 | tf_op jit(solution)/shard_map/ppermute | solution.py:165
  91.4 14.8 %collective-permute-start.22 = (bf16[32,4096]{1,0:T(8,128)(2,1)S(1)}, bf16[32,4096]{1,0:T(8,128)(2,1)S(1)}, u32[]{:S(2)}, u32[]{:S(2)}) collective-permute-start(bf16[32,4096]{1,0:T(8,128)(2,1)S(1)} %get-tuple-element.7), channel_id=1, source_target_pairs={{0,4},{1,5},{2,6},{3,7},{4,8},{5,9},{6,10},{7,11},{8,12},{9,13},{1... | collective-permute-start | bytes 786440 | tf_op jit(solution)/shard_map/ppermute | solution.py:165
  106.2 1.3 %collective-permute-start.28 = (bf16[32,4096]{1,0:T(8,128)(2,1)S(1)}, bf16[32,4096]{1,0:T(8,128)(2,1)S(1)}, u32[]{:S(2)}, u32[]{:S(2)}) collective-permute-start(bf16[32,4096]{1,0:T(8,128)(2,1)S(1)} %get-tuple-element.8), channel_id=1, source_target_pairs={{4,0},{5,1},{6,2},{7,3},{8,4},{9,5},{10,6},{11,7},{12,8},{13,9},{1... | collective-permute-start | bytes 786440 | tf_op jit(solution)/shard_map/ppermute | solution.py:172
  107.6 2.5 %collective-permute-done.22 = bf16[32,4096]{1,0:T(8,128)(2,1)S(1)} collective-permute-done((bf16[32,4096]{1,0:T(8,128)(2,1)S(1)}, bf16[32,4096]{1,0:T(8,128)(2,1)S(1)}, u32[]{:S(2)}, u32[]{:S(2)}) %collective-permute-start.22) | collective-permute-done | bytes 262176 | tf_op jit(solution)/shard_map/ppermute | solution.py:165
  110.1 4.4 %collective-permute-done.28 = bf16[32,4096]{1,0:T(8,128)(2,1)S(1)} collective-permute-done((bf16[32,4096]{1,0:T(8,128)(2,1)S(1)}, bf16[32,4096]{1,0:T(8,128)(2,1)S(1)}, u32[]{:S(2)}, u32[]{:S(2)}) %collective-permute-start.28) | collective-permute-done | bytes 262176 | tf_op jit(solution)/shard_map/ppermute | solution.py:172
  116.9 1.7 %select_add_fusion = (f32[128,2048]{1,0:T(8,128)}, f32[128,2048]{1,0:T(8,128)}) fusion(f32[128,2048]{1,0:T(8,128)S(1)} %gather_fusion.1, bf16[128,2048]{1,0:T(8,128)(2,1)S(1)} %copy-done.1, pred[128]{0:T(512)(128)(4,1)S(1)} %compare_and_fusion, f32[128,2048]{1,0:T(8,128)S(1)} %gather_fusion, bf16[128,2048]{1,0:T(8,128)(2,1)S(1)} %copy-done.2), kind=kLoop, calls=%fused_computation.30 | loop fusion | flops 1572864 | bytes 5243008 | tf_op jit(solution)/shard_map/add | solution.py:253
  (88 shorter events, 25.6 us)
Async XLA Ops:
  0.6 2.4 %copy-start.4 = (s32[32,8]{0,1:T(8,128)S(1)}, s32[32,8]{0,1:T(8,128)}, u32[]{:S(2)}) copy-start(s32[32,8]{0,1:T(8,128)} %param.13) | copy-start | bytes 3076
  0.6 2.4 %copy-start.3 = (f32[32,8]{0,1:T(8,128)S(1)}, f32[32,8]{0,1:T(8,128)}, u32[]{:S(2)}) copy-start(f32[32,8]{0,1:T(8,128)} %param.14) | copy-start | bytes 3076
  3.2 11.4 %collective-permute-start = (bf16[32,4224]{1,0:T(8,128)(2,1)S(1)}, bf16[32,4224]{1,0:T(8,128)(2,1)S(1)}, u32[]{:S(2)}, u32[]{:S(2)}) collective-permute-start(bf16[32,4224]{1,0:T(8,128)(2,1)S(1)} %fusion.49), channel_id=1, source_target_pairs={{4,0},{5,1},{6,2},{7,3},{8,4},{9,5},{10,6},{11,7},{12,8},{13,9},{1... | collective-permute-start | bytes 811016 | tf_op jit(solution)/shard_map/ppermute | solution.py:125
  4.5 11.4 %collective-permute-start.3 = (bf16[32,4224]{1,0:T(8,128)(2,1)S(1)}, bf16[32,4224]{1,0:T(8,128)(2,1)S(1)}, u32[]{:S(2)}, u32[]{:S(2)}) collective-permute-start(bf16[32,4224]{1,0:T(8,128)(2,1)S(1)} %fusion.49), channel_id=1, source_target_pairs={{0,4},{1,5},{2,6},{3,7},{4,8},{5,9},{6,10},{7,11},{8,12},{9,13},{1... | collective-permute-start | bytes 811016 | tf_op jit(solution)/shard_map/ppermute | solution.py:120
  14.6 9.5 %collective-permute-start.1 = (bf16[32,4224]{1,0:T(8,128)(2,1)S(1)}, bf16[32,4224]{1,0:T(8,128)(2,1)S(1)}, u32[]{:S(2)}, u32[]{:S(2)}) collective-permute-start(bf16[32,4224]{1,0:T(8,128)(2,1)S(1)} %collective-permute-done), channel_id=1, source_target_pairs={{4,0},{5,1},{6,2},{7,3},{8,4},{9,5},{10,6},{11,7},{20,16},{21,17},... | collective-permute-start | bytes 811016 | tf_op jit(solution)/shard_map/ppermute | solution.py:125
  15.9 9.5 %collective-permute-start.4 = (bf16[32,4224]{1,0:T(8,128)(2,1)S(1)}, bf16[32,4224]{1,0:T(8,128)(2,1)S(1)}, u32[]{:S(2)}, u32[]{:S(2)}) collective-permute-start(bf16[32,4224]{1,0:T(8,128)(2,1)S(1)} %collective-permute-done.3), channel_id=1, source_target_pairs={{4,8},{5,9},{6,10},{7,11},{8,12},{9,13},{10,14},{11,15},{20,24},{2... | collective-permute-start | bytes 811016 | tf_op jit(solution)/shard_map/ppermute | solution.py:120
  16.6 10.3 %collective-permute-start.12 = (bf16[32,4224]{1,0:T(8,128)(2,1)S(1)}, bf16[32,4224]{1,0:T(8,128)(2,1)S(1)}, u32[]{:S(2)}, u32[]{:S(2)}) collective-permute-start(bf16[32,4224]{1,0:T(8,128)(2,1)S(1)} %fusion.49), channel_id=1, source_target_pairs={{0,2},{1,3},{2,0},{3,1},{4,6},{5,7},{6,4},{7,5},{8,10},{9,11},{10,... | collective-permute-start | bytes 811016 | tf_op jit(solution)/shard_map/ppermute | solution.py:117
  18.4 12.1 %collective-permute-start.10 = (bf16[32,4224]{1,0:T(8,128)(2,1)S(1)}, bf16[32,4224]{1,0:T(8,128)(2,1)S(1)}, u32[]{:S(2)}, u32[]{:S(2)}) collective-permute-start(bf16[32,4224]{1,0:T(8,128)(2,1)S(1)} %collective-permute-done), channel_id=1, source_target_pairs={{0,2},{1,3},{2,0},{3,1},{4,6},{5,7},{6,4},{7,5},{8,10},{9,11},{10,... | collective-permute-start | bytes 811016 | tf_op jit(solution)/shard_map/ppermute | solution.py:135
  24.2 8.6 %collective-permute-start.2 = (bf16[32,4224]{1,0:T(8,128)(2,1)S(1)}, bf16[32,4224]{1,0:T(8,128)(2,1)S(1)}, u32[]{:S(2)}, u32[]{:S(2)}) collective-permute-start(bf16[32,4224]{1,0:T(8,128)(2,1)S(1)} %collective-permute-done.1), channel_id=1, source_target_pairs={{4,0},{5,1},{6,2},{7,3},{20,16},{21,17},{22,18},{23,19}} | collective-permute-start | bytes 811016 | tf_op jit(solution)/shard_map/ppermute | solution.py:125
  25.5 10.3 %collective-permute-start.5 = (bf16[32,4224]{1,0:T(8,128)(2,1)S(1)}, bf16[32,4224]{1,0:T(8,128)(2,1)S(1)}, u32[]{:S(2)}, u32[]{:S(2)}) collective-permute-start(bf16[32,4224]{1,0:T(8,128)(2,1)S(1)} %collective-permute-done.4), channel_id=1, source_target_pairs={{8,12},{9,13},{10,14},{11,15},{24,28},{25,29},{26,30},{27,31}} | collective-permute-start | bytes 811016 | tf_op jit(solution)/shard_map/ppermute | solution.py:120
  26.2 11.0 %collective-permute-start.11 = (bf16[32,4224]{1,0:T(8,128)(2,1)S(1)}, bf16[32,4224]{1,0:T(8,128)(2,1)S(1)}, u32[]{:S(2)}, u32[]{:S(2)}) collective-permute-start(bf16[32,4224]{1,0:T(8,128)(2,1)S(1)} %collective-permute-done.3), channel_id=1, source_target_pairs={{4,6},{5,7},{6,4},{7,5},{8,10},{9,11},{10,8},{11,9},{12,14},{13,15... | collective-permute-start | bytes 811016 | tf_op jit(solution)/shard_map/ppermute | solution.py:134
  26.9 10.4 %collective-permute-start.8 = (bf16[32,4224]{1,0:T(8,128)(2,1)S(1)}, bf16[32,4224]{1,0:T(8,128)(2,1)S(1)}, u32[]{:S(2)}, u32[]{:S(2)}) collective-permute-start(bf16[32,4224]{1,0:T(8,128)(2,1)S(1)} %collective-permute-done.1), channel_id=1, source_target_pairs={{0,2},{1,3},{2,0},{3,1},{4,6},{5,7},{6,4},{7,5},{16,18},{17,19},{1... | collective-permute-start | bytes 811016 | tf_op jit(solution)/shard_map/ppermute | solution.py:135
  30.5 7.3 %collective-permute-start.9 = (bf16[32,4224]{1,0:T(8,128)(2,1)S(1)}, bf16[32,4224]{1,0:T(8,128)(2,1)}, u32[]{:S(2)}, u32[]{:S(2)}) collective-permute-start(bf16[32,4224]{1,0:T(8,128)(2,1)S(1)} %collective-permute-done.4), channel_id=1, source_target_pairs={{8,10},{9,11},{10,8},{11,9},{12,14},{13,15},{14,12},{15,13},{24,26... | collective-permute-start | bytes 811016 | tf_op jit(solution)/shard_map/ppermute | solution.py:134
  32.8 9.0 %collective-permute-start.6 = (bf16[32,4224]{1,0:T(8,128)(2,1)S(1)}, bf16[32,4224]{1,0:T(8,128)(2,1)}, u32[]{:S(2)}, u32[]{:S(2)}) collective-permute-start(bf16[32,4224]{1,0:T(8,128)(2,1)S(1)} %collective-permute-done.2), channel_id=1, source_target_pairs={{0,2},{1,3},{2,0},{3,1},{16,18},{17,19},{18,16},{19,17}} | collective-permute-start | bytes 811016 | tf_op jit(solution)/shard_map/ppermute | solution.py:135
  35.8 6.0 %collective-permute-start.7 = (bf16[32,4224]{1,0:T(8,128)(2,1)S(1)}, bf16[32,4224]{1,0:T(8,128)(2,1)}, u32[]{:S(2)}, u32[]{:S(2)}) collective-permute-start(bf16[32,4224]{1,0:T(8,128)(2,1)S(1)} %collective-permute-done.5), channel_id=1, source_target_pairs={{12,14},{13,15},{14,12},{15,13},{28,30},{29,31},{30,28},{31,29}} | collective-permute-start | bytes 811016 | tf_op jit(solution)/shard_map/ppermute | solution.py:134
  37.2 19.0 %collective-permute-start.14 = (bf16[2048,768]{1,0:T(8,128)(2,1)}, bf16[2048,768]{1,0:T(8,128)(2,1)S(1)}, u32[]{:S(2)}, u32[]{:S(2)}) collective-permute-start(bf16[2048,768]{1,0:T(8,128)(2,1)} %bitcast.77), channel_id=1, source_target_pairs={{0,1},{1,0},{2,3},{3,2},{4,5},{5,4},{6,7},{7,6},{8,9},{9,8},{10,11... | collective-permute-start | bytes 9437192 | tf_op jit(solution)/shard_map/ppermute | solution.py:239
  37.3 19.9 %collective-permute-start.13 = (bf16[2048,768]{1,0:T(8,128)(2,1)}, bf16[2048,768]{1,0:T(8,128)(2,1)S(1)}, u32[]{:S(2)}, u32[]{:S(2)}) collective-permute-start(bf16[2048,768]{1,0:T(8,128)(2,1)} %bitcast.85), channel_id=1, source_target_pairs={{0,1},{1,0},{2,3},{3,2},{4,5},{5,4},{6,7},{7,6},{8,9},{9,8},{10,11... | collective-permute-start | bytes 9437192 | tf_op jit(solution)/shard_map/ppermute | solution.py:238
  37.8 20.4 %collective-permute-start.15 = (bf16[768,2048]{1,0:T(8,128)(2,1)}, bf16[768,2048]{1,0:T(8,128)(2,1)S(1)}, u32[]{:S(2)}, u32[]{:S(2)}) collective-permute-start(bf16[768,2048]{1,0:T(8,128)(2,1)} %bitcast.86), channel_id=1, source_target_pairs={{0,1},{1,0},{2,3},{3,2},{4,5},{5,4},{6,7},{7,6},{8,9},{9,8},{10,11... | collective-permute-start | bytes 9437192 | tf_op jit(solution)/shard_map/ppermute | solution.py:240
  63.6 10.1 %collective-permute-start.17 = (bf16[32,4096]{1,0:T(8,128)(2,1)S(1)}, bf16[32,4096]{1,0:T(8,128)(2,1)S(1)}, u32[]{:S(2)}, u32[]{:S(2)}) collective-permute-start(bf16[32,4096]{1,0:T(8,128)(2,1)S(1)} %get-tuple-element.21), channel_id=1, source_target_pairs={{0,2},{1,3},{2,0},{3,1},{16,18},{17,19},{18,16},{19,17}} | collective-permute-start | bytes 786440 | tf_op jit(solution)/shard_map/ppermute | solution.py:157
  66.9 6.8 %collective-permute-start.23 = (bf16[32,4096]{1,0:T(8,128)(2,1)S(1)}, bf16[32,4096]{1,0:T(8,128)(2,1)S(1)}, u32[]{:S(2)}, u32[]{:S(2)}) collective-permute-start(bf16[32,4096]{1,0:T(8,128)(2,1)S(1)} %get-tuple-element.18), channel_id=1, source_target_pairs={{12,14},{13,15},{14,12},{15,13},{28,30},{29,31},{30,28},{31,29}} | collective-permute-start | bytes 786440 | tf_op jit(solution)/shard_map/ppermute | solution.py:157
  67.8 12.2 %collective-permute-start.19 = (bf16[32,4096]{1,0:T(8,128)(2,1)S(1)}, bf16[32,4096]{1,0:T(8,128)(2,1)S(1)}, u32[]{:S(2)}, u32[]{:S(2)}) collective-permute-start(bf16[32,4096]{1,0:T(8,128)(2,1)S(1)} %get-tuple-element.20), channel_id=1, source_target_pairs={{0,2},{1,3},{2,0},{3,1},{4,6},{5,7},{6,4},{7,5},{16,18},{17,19},{1... | collective-permute-start | bytes 786440 | tf_op jit(solution)/shard_map/ppermute | solution.py:157
  70.4 17.0 %copy-start.5 = (s32[128]{0:T(128)S(1)}, s32[128]{0:T(128)}, u32[]{:S(2)}) copy-start(s32[128]{0:T(128)} %param.12) | copy-start | bytes 1540
  70.4 10.3 %collective-permute-start.25 = (bf16[32,4096]{1,0:T(8,128)(2,1)S(1)}, bf16[32,4096]{1,0:T(8,128)(2,1)S(1)}, u32[]{:S(2)}, u32[]{:S(2)}) collective-permute-start(bf16[32,4096]{1,0:T(8,128)(2,1)S(1)} %get-tuple-element.17), channel_id=1, source_target_pairs={{8,10},{9,11},{10,8},{11,9},{12,14},{13,15},{14,12},{15,13},{24,26... | collective-permute-start | bytes 786440 | tf_op jit(solution)/shard_map/ppermute | solution.py:157
  73.8 8.2 %collective-permute-start.18 = (bf16[32,4096]{1,0:T(8,128)(2,1)S(1)}, bf16[32,4096]{1,0:T(8,128)(2,1)S(1)}, u32[]{:S(2)}, u32[]{:S(2)}) collective-permute-start(bf16[32,4096]{1,0:T(8,128)(2,1)S(1)} %get-tuple-element.11), channel_id=1, source_target_pairs={{0,4},{1,5},{2,6},{3,7},{16,20},{17,21},{18,22},{19,23}} | collective-permute-start | bytes 786440 | tf_op jit(solution)/shard_map/ppermute | solution.py:165
  76.6 5.4 %collective-permute-start.24 = (bf16[32,4096]{1,0:T(8,128)(2,1)S(1)}, bf16[32,4096]{1,0:T(8,128)(2,1)S(1)}, u32[]{:S(2)}, u32[]{:S(2)}) collective-permute-start(bf16[32,4096]{1,0:T(8,128)(2,1)S(1)} %get-tuple-element.12), channel_id=1, source_target_pairs={{12,8},{13,9},{14,10},{15,11},{28,24},{29,25},{30,26},{31,27}} | collective-permute-start | bytes 786440 | tf_op jit(solution)/shard_map/ppermute | solution.py:172
  77.3 10.6 %collective-permute-start.21 = (bf16[32,4096]{1,0:T(8,128)(2,1)S(1)}, bf16[32,4096]{1,0:T(8,128)(2,1)S(1)}, u32[]{:S(2)}, u32[]{:S(2)}) collective-permute-start(bf16[32,4096]{1,0:T(8,128)(2,1)S(1)} %get-tuple-element.19), channel_id=1, source_target_pairs={{0,2},{1,3},{2,0},{3,1},{4,6},{5,7},{6,4},{7,5},{8,10},{9,11},{10,... | collective-permute-start | bytes 786440 | tf_op jit(solution)/shard_map/ppermute | solution.py:157
  80.1 7.8 %collective-permute-start.27 = (bf16[32,4096]{1,0:T(8,128)(2,1)S(1)}, bf16[32,4096]{1,0:T(8,128)(2,1)S(1)}, u32[]{:S(2)}, u32[]{:S(2)}) collective-permute-start(bf16[32,4096]{1,0:T(8,128)(2,1)S(1)} %get-tuple-element.16), channel_id=1, source_target_pairs={{4,6},{5,7},{6,4},{7,5},{8,10},{9,11},{10,8},{11,9},{12,14},{13,15... | collective-permute-start | bytes 786440 | tf_op jit(solution)/shard_map/ppermute | solution.py:157
  82.2 9.0 %collective-permute-start.20 = (bf16[32,4096]{1,0:T(8,128)(2,1)S(1)}, bf16[32,4096]{1,0:T(8,128)(2,1)S(1)}, u32[]{:S(2)}, u32[]{:S(2)}) collective-permute-start(bf16[32,4096]{1,0:T(8,128)(2,1)S(1)} %get-tuple-element.9), channel_id=1, source_target_pairs={{0,4},{1,5},{2,6},{3,7},{4,8},{5,9},{6,10},{7,11},{16,20},{17,21},... | collective-permute-start | bytes 786440 | tf_op jit(solution)/shard_map/ppermute | solution.py:165
  86.7 4.5 %collective-permute-start.26 = (bf16[32,4096]{1,0:T(8,128)(2,1)S(1)}, bf16[32,4096]{1,0:T(8,128)(2,1)S(1)}, u32[]{:S(2)}, u32[]{:S(2)}) collective-permute-start(bf16[32,4096]{1,0:T(8,128)(2,1)S(1)} %get-tuple-element.10), channel_id=1, source_target_pairs={{8,4},{9,5},{10,6},{11,7},{12,8},{13,9},{14,10},{15,11},{24,20},{2... | collective-permute-start | bytes 786440 | tf_op jit(solution)/shard_map/ppermute | solution.py:172
  87.4 20.1 %collective-permute-start.16 = (bf16[32,4096]{1,0:T(8,128)(2,1)S(1)}, bf16[32,4096]{1,0:T(8,128)(2,1)S(1)}, u32[]{:S(2)}, u32[]{:S(2)}) collective-permute-start(bf16[32,4096]{1,0:T(8,128)(2,1)S(1)} %get-tuple-element.15), channel_id=1, source_target_pairs={{0,2},{1,3},{2,0},{3,1},{4,6},{5,7},{6,4},{7,5},{8,10},{9,11},{10,... | collective-permute-start | bytes 786440 | tf_op jit(solution)/shard_map/ppermute | solution.py:157
  91.4 18.7 %collective-permute-start.22 = (bf16[32,4096]{1,0:T(8,128)(2,1)S(1)}, bf16[32,4096]{1,0:T(8,128)(2,1)S(1)}, u32[]{:S(2)}, u32[]{:S(2)}) collective-permute-start(bf16[32,4096]{1,0:T(8,128)(2,1)S(1)} %get-tuple-element.7), channel_id=1, source_target_pairs={{0,4},{1,5},{2,6},{3,7},{4,8},{5,9},{6,10},{7,11},{8,12},{9,13},{1... | collective-permute-start | bytes 786440 | tf_op jit(solution)/shard_map/ppermute | solution.py:165
  106.2 8.3 %collective-permute-start.28 = (bf16[32,4096]{1,0:T(8,128)(2,1)S(1)}, bf16[32,4096]{1,0:T(8,128)(2,1)S(1)}, u32[]{:S(2)}, u32[]{:S(2)}) collective-permute-start(bf16[32,4096]{1,0:T(8,128)(2,1)S(1)} %get-tuple-element.8), channel_id=1, source_target_pairs={{4,0},{5,1},{6,2},{7,3},{8,4},{9,5},{10,6},{11,7},{12,8},{13,9},{1... | collective-permute-start | bytes 786440 | tf_op jit(solution)/shard_map/ppermute | solution.py:172
  (5 other events, 7.9 us)

commit v13 on v12

--- a/solution.py
+++ b/solution.py
@@ -131,8 +131,16 @@
         here.append((behind, line + step))
         ahead_row = [(j, j ^ 2) for j in range(experts) if j // 4 >= step]
         behind_row = [(j, j ^ 2) for j in range(experts) if j // 4 <= lines - 1 - step]
-        there.append((lax.ppermute(ahead, "expert", ahead_row), line - step))
-        there.append((lax.ppermute(behind, "expert", behind_row), line + step))
+        if 2 * step > lines - 1:
+            in_ahead = line >= step
+            got = lax.ppermute(
+                jnp.where(in_ahead, ahead, behind), "expert", sorted(ahead_row + behind_row)
+            )
+            origin = jnp.where(in_ahead, line - step, jnp.where(line <= lines - 1 - step, line + step, -1))
+            there.append((got, origin))
+        else:
+            there.append((lax.ppermute(ahead, "expert", ahead_row), line - step))
+            there.append((lax.ppermute(behind, "expert", behind_row), line + step))
     column = place(here, lines, shard)
     across = place(there, lines, shard)
     in_row = (me // 2) % 2
@@ -160,17 +168,23 @@
     ahead = jnp.zeros(keep.shape[1:], jnp.float32)
     behind = jnp.zeros(keep.shape[1:], jnp.float32)
     for step in range(1, lines):
-        target = jnp.clip(line + lines - step, 0, lines - 1)
-        ahead = ahead + row_sum(target, lambda z, s=step: z <= s - 1)
+        ahead_target = jnp.clip(line + lines - step, 0, lines - 1)
+        behind_target = jnp.clip(line - lines + step, 0, lines - 1)
+        if 2 * step <= lines:
+            in_ahead = line <= step - 1
+            target = jnp.where(in_ahead, ahead_target, behind_target)
+            ahead_part = row_sum(target, lambda z, s=step: z <= s - 1 or z >= lines - s)
+            behind_part = ahead_part
+        else:
+            ahead_part = row_sum(ahead_target, lambda z, s=step: z <= s - 1)
+            behind_part = row_sum(behind_target, lambda z, s=step: z >= lines - s)
         ahead = lax.ppermute(
-            ahead.astype(jnp.bfloat16),
+            (ahead + ahead_part).astype(jnp.bfloat16),
             "expert",
             [(j, j + 4) for j in range(experts) if j // 4 <= step - 1],
         ).astype(jnp.float32)
-        target = jnp.clip(line - lines + step, 0, lines - 1)
-        behind = behind + row_sum(target, lambda z, s=step: z >= lines - s)
         behind = lax.ppermute(
-            behind.astype(jnp.bfloat16),
+            (behind + behind_part).astype(jnp.bfloat16),
             "expert",
             [(j, j - 4) for j in range(experts) if j // 4 >= lines - step],
         ).astype(jnp.float32)

time: 119 us -> 115 us (0.966)
  starting transfers between devices: 60.9 us -> 43.6 us
  waiting for transfers between devices: 27.4 us -> 39.6 us
    ppermute x6 -> x8, waiting for transfers between devices: 11.5 us -> 21.3 us  [the longest x3 9.94 us: topo_reduce_scatter(): lax.ppermute((ahead + ahead_part).astype(jnp.bfloat16), 'expert', [(j, j...]
    ppermute x6 -> x8, starting transfers between devices: 24.7 us -> 18.6 us  [the longest x3 12 us: topo_reduce_scatter(): lax.ppermute((ahead + ahead_part).astype(jnp.bfloat16), 'expert', [(j, j...]
    ppermute x3 -> x1, starting transfers between devices: 8.5 us -> 3.59 us  [topo_all_gather(): there.append((lax.ppermute(behind, 'expert', behind_row), line + step))]
    ppermute x3 -> x1, waiting for transfers between devices: 4.22 us -> 0.01 us  [topo_all_gather(): there.append((lax.ppermute(behind, 'expert', behind_row), line + step))]
    ppermute x7 -> x5, starting transfers between devices: 11.2 us -> 7.23 us  [row_sum(): got = lax.ppermute(theirs.astype(jnp.bfloat16), 'expert', pairs)]
    ppermute x3, waiting for transfers between devices: 9.06 us -> 12.7 us  [topo_all_gather(): lax.ppermute(behind, 'expert', [(j, j - 4) for j in range(experts) if 1 <...]
    ppermute x7 -> x5, waiting for transfers between devices: 2.66 us -> 5.62 us  [row_sum(): got = lax.ppermute(theirs.astype(jnp.bfloat16), 'expert', pairs)]
    ppermute x3 -> x1, starting transfers between devices: 3.41 us -> 0.68 us  [topo_all_gather(): there.append((lax.ppermute(ahead, 'expert', ahead_row), line - step))]
  transfers between devices with their start and end apart: 29 -> 25, of which waited for: 10 -> 10; matrix products, arithmetic and copies ran while one was open for 12% -> 13% of each run, Pallas kernels for 0% -> 0%
where the time goes in v13:
time: 115 us; the launch traced here: 114 us
  starting transfers between devices  43.6 us (38%)
  waiting for transfers between devices  39.6 us (34%)
  matrix products  14.1 us (12%)
  other arithmetic  10 us (9%)
  local copies, waits for them, and re-layouts  5.63 us (5%)
  between operations  1.35 us (1%)
    ppermute x3, waiting for transfers between devices, topo_all_gather(): lax.ppermute(behind, 'expert', [(j, j - 4) for j in range(experts) if 1 <...  12.7 us
    ppermute x3, starting transfers between devices, topo_reduce_scatter(): lax.ppermute((ahead + ahead_part).astype(jnp.bfloat16), 'expert', [(j, j...  12 us
    ppermute x3, waiting for transfers between devices, topo_reduce_scatter(): lax.ppermute((ahead + ahead_part).astype(jnp.bfloat16), 'expert', [(j, j...  9.94 us
    ppermute x5, starting transfers between devices, row_sum(): got = lax.ppermute(theirs.astype(jnp.bfloat16), 'expert', pairs)  7.23 us
    ppermute x3, starting transfers between devices, topo_all_gather(): lax.ppermute(ahead, 'expert', [(j, j + 4) for j in range(experts) if step...  6.93 us
    ppermute x2, waiting for transfers between devices, topo_all_gather(): lax.ppermute(jnp.where(in_ahead, ahead, behind), 'expert', sorted(ahead_r...  6.89 us
    ppermute x5, waiting for transfers between devices, row_sum(): got = lax.ppermute(theirs.astype(jnp.bfloat16), 'expert', pairs)  5.62 us
    ppermute x3, waiting for transfers between devices, topo_reduce_scatter(): lax.ppermute((behind + behind_part).astype(jnp.bfloat16), 'expert', [(j,...  4.41 us
  transfers between devices with their start and end apart: 25, of which 10 were waited for; matrix products, arithmetic and copies ran while one was open for 13% of the time, Pallas kernels for 0%

profile of v13, /device:TPU:0, one launch (start us, length us, event | category | flops | bytes accessed | tf_op | source)
XLA Modules:
  0.0 114.2 jit_solution(6304870681406198111)
XLA Ops:
  1.4 1.5 %fusion.12 = f32[32,4096]{1,0:T(8,128)S(1)} fusion(bf16[128,2048]{1,0:T(8,128)(2,1)} %param.11, bf16[128,2048]{1,0:T(8,128)(2,1)} %param.10, s32[128]{0:T(128)} %param.12), kind=kOutput, calls=%fused_computation.26 | convolution fusion | flops 35655680 | bytes 1573376 | tf_op jit(solution)/shard_map/dot_general | solution.py:222
  3.2 1.3 %collective-permute-start = (bf16[32,4224]{1,0:T(8,128)(2,1)S(1)}, bf16[32,4224]{1,0:T(8,128)(2,1)S(1)}, u32[]{:S(2)}, u32[]{:S(2)}) collective-permute-start(bf16[32,4224]{1,0:T(8,128)(2,1)S(1)} %fusion.44), channel_id=1, source_target_pairs={{4,0},{5,1},{6,2},{7,3},{8,4},{9,5},{10,6},{11,7},{12,8},{13,9},{1... | collective-permute-start | bytes 811016 | tf_op jit(solution)/shard_map/ppermute | solution.py:125
  4.5 5.6 %collective-permute-start.3 = (bf16[32,4224]{1,0:T(8,128)(2,1)S(1)}, bf16[32,4224]{1,0:T(8,128)(2,1)S(1)}, u32[]{:S(2)}, u32[]{:S(2)}) collective-permute-start(bf16[32,4224]{1,0:T(8,128)(2,1)S(1)} %fusion.44), channel_id=1, source_target_pairs={{0,4},{1,5},{2,6},{3,7},{4,8},{5,9},{6,10},{7,11},{8,12},{9,13},{1... | collective-permute-start | bytes 811016 | tf_op jit(solution)/shard_map/ppermute | solution.py:120
  10.1 2.0 %collective-permute-start.10 = (bf16[32,4224]{1,0:T(8,128)(2,1)S(1)}, bf16[32,4224]{1,0:T(8,128)(2,1)S(1)}, u32[]{:S(2)}, u32[]{:S(2)}) collective-permute-start(bf16[32,4224]{1,0:T(8,128)(2,1)S(1)} %fusion.44), channel_id=1, source_target_pairs={{0,2},{1,3},{2,0},{3,1},{4,6},{5,7},{6,4},{7,5},{8,10},{9,11},{10,... | collective-permute-start | bytes 811016 | tf_op jit(solution)/shard_map/ppermute | solution.py:117
  12.1 2.5 %collective-permute-done = bf16[32,4224]{1,0:T(8,128)(2,1)S(1)} collective-permute-done((bf16[32,4224]{1,0:T(8,128)(2,1)S(1)}, bf16[32,4224]{1,0:T(8,128)(2,1)S(1)}, u32[]{:S(2)}, u32[]{:S(2)}) %collective-permute-start) | collective-permute-done | bytes 270368 | tf_op jit(solution)/shard_map/ppermute | solution.py:125
  14.6 1.3 %collective-permute-start.1 = (bf16[32,4224]{1,0:T(8,128)(2,1)S(1)}, bf16[32,4224]{1,0:T(8,128)(2,1)S(1)}, u32[]{:S(2)}, u32[]{:S(2)}) collective-permute-start(bf16[32,4224]{1,0:T(8,128)(2,1)S(1)} %collective-permute-done), channel_id=1, source_target_pairs={{4,0},{5,1},{6,2},{7,3},{8,4},{9,5},{10,6},{11,7},{20,16},{21,17},... | collective-permute-start | bytes 811016 | tf_op jit(solution)/shard_map/ppermute | solution.py:125
  16.7 3.6 %collective-permute-start.8 = (bf16[32,4224]{1,0:T(8,128)(2,1)S(1)}, bf16[32,4224]{1,0:T(8,128)(2,1)S(1)}, u32[]{:S(2)}, u32[]{:S(2)}) collective-permute-start(bf16[32,4224]{1,0:T(8,128)(2,1)S(1)} %collective-permute-done), channel_id=1, source_target_pairs={{0,2},{1,3},{2,0},{3,1},{4,6},{5,7},{6,4},{7,5},{8,10},{9,11},{10,... | collective-permute-start | bytes 811016 | tf_op jit(solution)/shard_map/ppermute | solution.py:143
  20.9 3.2 %collective-permute-done.1 = bf16[32,4224]{1,0:T(8,128)(2,1)S(1)} collective-permute-done((bf16[32,4224]{1,0:T(8,128)(2,1)S(1)}, bf16[32,4224]{1,0:T(8,128)(2,1)S(1)}, u32[]{:S(2)}, u32[]{:S(2)}) %collective-permute-start.1) | collective-permute-done | bytes 270368 | tf_op jit(solution)/shard_map/ppermute | solution.py:125
  24.2 1.3 %collective-permute-start.2 = (bf16[32,4224]{1,0:T(8,128)(2,1)S(1)}, bf16[32,4224]{1,0:T(8,128)(2,1)S(1)}, u32[]{:S(2)}, u32[]{:S(2)}) collective-permute-start(bf16[32,4224]{1,0:T(8,128)(2,1)S(1)} %collective-permute-done.1), channel_id=1, source_target_pairs={{4,0},{5,1},{6,2},{7,3},{20,16},{21,17},{22,18},{23,19}} | collective-permute-start | bytes 811016 | tf_op jit(solution)/shard_map/ppermute | solution.py:125
  26.9 7.0 %collective-permute-done.2 = bf16[32,4224]{1,0:T(8,128)(2,1)S(1)} collective-permute-done((bf16[32,4224]{1,0:T(8,128)(2,1)S(1)}, bf16[32,4224]{1,0:T(8,128)(2,1)S(1)}, u32[]{:S(2)}, u32[]{:S(2)}) %collective-permute-start.2) | collective-permute-done | bytes 270368 | tf_op jit(solution)/shard_map/ppermute | solution.py:125
  33.9 1.5 %collective-permute-start.7 = (bf16[32,4224]{1,0:T(8,128)(2,1)}, bf16[32,4224]{1,0:T(8,128)(2,1)S(1)}, u32[]{:S(2)}, u32[]{:S(2)}) collective-permute-start(bf16[32,4224]{1,0:T(8,128)(2,1)} %broadcast_select_fusion.2), channel_id=1, source_target_pairs={{0,2},{1,3},{2,0},{3,1},{4,6},{5,7},{6,4},{7,5},{8,10},{9,11},{10,... | collective-permute-start | bytes 811016 | tf_op jit(solution)/shard_map/ppermute | solution.py:136
  36.2 2.4 %collective-permute-start.6 = (bf16[32,4224]{1,0:T(8,128)(2,1)}, bf16[32,4224]{1,0:T(8,128)(2,1)}, u32[]{:S(2)}, u32[]{:S(2)}) collective-permute-start(bf16[32,4224]{1,0:T(8,128)(2,1)} %broadcast_select_fusion.3), channel_id=1, source_target_pairs={{0,2},{1,3},{2,0},{3,1},{12,14},{13,15},{14,12},{15,13},{16,18},{1... | collective-permute-start | bytes 811016 | tf_op jit(solution)/shard_map/ppermute | solution.py:136
  39.4 3.9 %collective-permute-done.7 = bf16[32,4224]{1,0:T(8,128)(2,1)S(1)} collective-permute-done((bf16[32,4224]{1,0:T(8,128)(2,1)}, bf16[32,4224]{1,0:T(8,128)(2,1)S(1)}, u32[]{:S(2)}, u32[]{:S(2)}) %collective-permute-start.7) | collective-permute-done | bytes 270368 | tf_op jit(solution)/shard_map/ppermute | solution.py:136
  43.3 3.0 %collective-permute-done.6 = bf16[32,4224]{1,0:T(8,128)(2,1)} collective-permute-done((bf16[32,4224]{1,0:T(8,128)(2,1)}, bf16[32,4224]{1,0:T(8,128)(2,1)}, u32[]{:S(2)}, u32[]{:S(2)}) %collective-permute-start.6) | collective-permute-done | bytes 270368 | tf_op jit(solution)/shard_map/ppermute | solution.py:136
  46.3 1.9 %broadcast_select_fusion.1 = bf16[4,1,32,4224]{3,2,1,0:T(8,128)(2,1)S(1)} fusion(pred[]{:T(512)S(6)} %eq.162, bf16[32,4224]{1,0:T(8,128)(2,1)S(1)} %collective-permute-done.10, pred[4]{0:T(512)(128)(4,1)S(1)} %get-tuple-element.22, bf16[32,4224]{1,0:T(8,128)(2,1)S(1)} %collective-permute-done.9, pred[4]{0:T(512)(128)(4,1)S(1)} %get-tuple-element.23, ...), kind=kLoop, calls=%fused_computation.25 | loop fusion | flops 7028736 | bytes 4325413 | tf_op jit(solution)/shard_map/jit(_where)/select_n | solution.py:99
  48.2 1.9 %broadcast_select_fusion = bf16[4,1,32,4224]{3,2,1,0:T(8,128)(2,1)S(1)} fusion(pred[]{:T(512)S(6)} %eq.162, bf16[32,4224]{1,0:T(8,128)(2,1)S(1)} %collective-permute-done.10, pred[4]{0:T(512)(128)(4,1)S(1)} %get-tuple-element.22, bf16[32,4224]{1,0:T(8,128)(2,1)S(1)} %collective-permute-done.9, pred[4]{0:T(512)(128)(4,1)S(1)} %get-tuple-element.23, ...), kind=kLoop, calls=%fused_computation.24 | loop fusion | flops 7028736 | bytes 4325413 | tf_op jit(solution)/shard_map/jit(_where)/select_n | solution.py:99
  50.6 1.4 %copy-done = bf16[1,2048,768]{2,1,0:T(8,128)(2,1)S(1)} copy-done((bf16[1,2048,768]{2,1,0:T(8,128)(2,1)S(1)}, bf16[1,2048,768]{2,1,0:T(8,128)(2,1)}, u32[]{:S(2)}) %copy-start) | copy-done | bytes 3145752
  57.9 1.1 fusion.36
  65.3 1.2 %fusion.4 = f32[256,2048]{1,0:T(8,128)S(1)} fusion(f32[256,2048]{1,0:T(8,128)S(1)} %fusion.6, f32[256,2048]{1,0:T(8,128)S(1)} %fusion.37, bf16[2048,768]{1,0:T(8,128)(2,1)S(1)} %collective-permute-done.11, f32[256]{0:T(256)S(1)} %get-tuple-element.3, f32[256,768]{1,0:T(8,128)S(1)} %fusion.22, f32[256,768]{1,0:T(8,128)S(1)} %fusion.16, f32[256,768]{1,0:T(8,128)S(1)} %fusion.20), kind=kOutput, calls=%fused_computation.9 | convolution fusion | flops 809893888 | bytes 11797504 | tf_op jit(solution)/shard_map/dot_general | solution.py:206
  67.5 2.5 %collective-permute-start.15 = (bf16[32,4096]{1,0:T(8,128)(2,1)S(1)}, bf16[32,4096]{1,0:T(8,128)(2,1)S(1)}, u32[]{:S(2)}, u32[]{:S(2)}) collective-permute-start(bf16[32,4096]{1,0:T(8,128)(2,1)S(1)} %get-tuple-element.17), channel_id=1, source_target_pairs={{0,2},{1,3},{2,0},{3,1},{12,14},{13,15},{14,12},{15,13},{16,18},{1... | collective-permute-start | bytes 786440 | tf_op jit(solution)/shard_map/ppermute | solution.py:165
  70.2 1.5 %collective-permute-start.17 = (bf16[32,4096]{1,0:T(8,128)(2,1)S(1)}, bf16[32,4096]{1,0:T(8,128)(2,1)S(1)}, u32[]{:S(2)}, u32[]{:S(2)}) collective-permute-start(bf16[32,4096]{1,0:T(8,128)(2,1)S(1)} %get-tuple-element.16), channel_id=1, source_target_pairs={{0,2},{1,3},{2,0},{3,1},{4,6},{5,7},{6,4},{7,5},{8,10},{9,11},{10,... | collective-permute-start | bytes 786440 | tf_op jit(solution)/shard_map/ppermute | solution.py:165
  71.7 5.6 %collective-permute-done.15 = bf16[32,4096]{1,0:T(8,128)(2,1)S(1)} collective-permute-done((bf16[32,4096]{1,0:T(8,128)(2,1)S(1)}, bf16[32,4096]{1,0:T(8,128)(2,1)S(1)}, u32[]{:S(2)}, u32[]{:S(2)}) %collective-permute-start.15) | collective-permute-done | bytes 262176 | tf_op jit(solution)/shard_map/ppermute | solution.py:165
  77.4 1.3 %collective-permute-start.16 = (bf16[32,4096]{1,0:T(8,128)(2,1)S(1)}, bf16[32,4096]{1,0:T(8,128)(2,1)S(1)}, u32[]{:S(2)}, u32[]{:S(2)}) collective-permute-start(bf16[32,4096]{1,0:T(8,128)(2,1)S(1)} %fusion.33), channel_id=1, source_target_pairs={{0,4},{1,5},{2,6},{3,7},{16,20},{17,21},{18,22},{19,23}} | collective-permute-start | bytes 786440 | tf_op jit(solution)/shard_map/ppermute | solution.py:181
  79.4 2.2 %collective-permute-start.19 = (bf16[32,4096]{1,0:T(8,128)(2,1)S(1)}, bf16[32,4096]{1,0:T(8,128)(2,1)S(1)}, u32[]{:S(2)}, u32[]{:S(2)}) collective-permute-start(bf16[32,4096]{1,0:T(8,128)(2,1)S(1)} %get-tuple-element.15), channel_id=1, source_target_pairs={{0,2},{1,3},{2,0},{3,1},{4,6},{5,7},{6,4},{7,5},{8,10},{9,11},{10,... | collective-permute-start | bytes 786440 | tf_op jit(solution)/shard_map/ppermute | solution.py:165
  82.3 2.0 %collective-permute-done.16 = bf16[32,4096]{1,0:T(8,128)(2,1)S(1)} collective-permute-done((bf16[32,4096]{1,0:T(8,128)(2,1)S(1)}, bf16[32,4096]{1,0:T(8,128)(2,1)S(1)}, u32[]{:S(2)}, u32[]{:S(2)}) %collective-permute-start.16) | collective-permute-done | bytes 262176 | tf_op jit(solution)/shard_map/ppermute | solution.py:181
  84.5 4.4 %collective-permute-start.18 = (bf16[32,4096]{1,0:T(8,128)(2,1)S(1)}, bf16[32,4096]{1,0:T(8,128)(2,1)S(1)}, u32[]{:S(2)}, u32[]{:S(2)}) collective-permute-start(bf16[32,4096]{1,0:T(8,128)(2,1)S(1)} %get-tuple-element.7), channel_id=1, source_target_pairs={{0,4},{1,5},{2,6},{3,7},{4,8},{5,9},{6,10},{7,11},{16,20},{17,21},... | collective-permute-start | bytes 786440 | tf_op jit(solution)/shard_map/ppermute | solution.py:181
  89.9 5.4 %collective-permute-done.18 = bf16[32,4096]{1,0:T(8,128)(2,1)S(1)} collective-permute-done((bf16[32,4096]{1,0:T(8,128)(2,1)S(1)}, bf16[32,4096]{1,0:T(8,128)(2,1)S(1)}, u32[]{:S(2)}, u32[]{:S(2)}) %collective-permute-start.18) | collective-permute-done | bytes 262176 | tf_op jit(solution)/shard_map/ppermute | solution.py:181
  95.6 6.3 %collective-permute-start.20 = (bf16[32,4096]{1,0:T(8,128)(2,1)S(1)}, bf16[32,4096]{1,0:T(8,128)(2,1)S(1)}, u32[]{:S(2)}, u32[]{:S(2)}) collective-permute-start(bf16[32,4096]{1,0:T(8,128)(2,1)S(1)} %get-tuple-element.9), channel_id=1, source_target_pairs={{0,4},{1,5},{2,6},{3,7},{4,8},{5,9},{6,10},{7,11},{8,12},{9,13},{1... | collective-permute-start | bytes 786440 | tf_op jit(solution)/shard_map/ppermute | solution.py:181
  101.9 1.3 %collective-permute-start.24 = (bf16[32,4096]{1,0:T(8,128)(2,1)S(1)}, bf16[32,4096]{1,0:T(8,128)(2,1)S(1)}, u32[]{:S(2)}, u32[]{:S(2)}) collective-permute-start(bf16[32,4096]{1,0:T(8,128)(2,1)S(1)} %get-tuple-element.10), channel_id=1, source_target_pairs={{4,0},{5,1},{6,2},{7,3},{8,4},{9,5},{10,6},{11,7},{12,8},{13,9},{1... | collective-permute-start | bytes 786440 | tf_op jit(solution)/shard_map/ppermute | solution.py:186
  103.2 2.5 %collective-permute-done.20 = bf16[32,4096]{1,0:T(8,128)(2,1)S(1)} collective-permute-done((bf16[32,4096]{1,0:T(8,128)(2,1)S(1)}, bf16[32,4096]{1,0:T(8,128)(2,1)S(1)}, u32[]{:S(2)}, u32[]{:S(2)}) %collective-permute-start.20) | collective-permute-done | bytes 262176 | tf_op jit(solution)/shard_map/ppermute | solution.py:181
  105.7 4.4 %collective-permute-done.24 = bf16[32,4096]{1,0:T(8,128)(2,1)S(1)} collective-permute-done((bf16[32,4096]{1,0:T(8,128)(2,1)S(1)}, bf16[32,4096]{1,0:T(8,128)(2,1)S(1)}, u32[]{:S(2)}, u32[]{:S(2)}) %collective-permute-start.24) | collective-permute-done | bytes 262176 | tf_op jit(solution)/shard_map/ppermute | solution.py:186
  112.6 1.7 %select_add_fusion = (f32[128,2048]{1,0:T(8,128)}, f32[128,2048]{1,0:T(8,128)}) fusion(f32[128,2048]{1,0:T(8,128)S(1)} %gather_fusion.1, bf16[128,2048]{1,0:T(8,128)(2,1)S(1)} %copy-done.1, pred[128]{0:T(512)(128)(4,1)S(1)} %compare_and_fusion, f32[128,2048]{1,0:T(8,128)S(1)} %gather_fusion, bf16[128,2048]{1,0:T(8,128)(2,1)S(1)} %copy-done.2), kind=kLoop, calls=%fused_computation.30 | loop fusion | flops 1572864 | bytes 5243008 | tf_op jit(solution)/shard_map/add | solution.py:267
  (83 shorter events, 24.2 us)
Async XLA Ops:
  0.6 2.4 %copy-start.4 = (s32[32,8]{0,1:T(8,128)S(1)}, s32[32,8]{0,1:T(8,128)}, u32[]{:S(2)}) copy-start(s32[32,8]{0,1:T(8,128)} %param.13) | copy-start | bytes 3076
  0.6 2.4 %copy-start.3 = (f32[32,8]{0,1:T(8,128)S(1)}, f32[32,8]{0,1:T(8,128)}, u32[]{:S(2)}) copy-start(f32[32,8]{0,1:T(8,128)} %param.14) | copy-start | bytes 3076
  3.2 11.4 %collective-permute-start = (bf16[32,4224]{1,0:T(8,128)(2,1)S(1)}, bf16[32,4224]{1,0:T(8,128)(2,1)S(1)}, u32[]{:S(2)}, u32[]{:S(2)}) collective-permute-start(bf16[32,4224]{1,0:T(8,128)(2,1)S(1)} %fusion.44), channel_id=1, source_target_pairs={{4,0},{5,1},{6,2},{7,3},{8,4},{9,5},{10,6},{11,7},{12,8},{13,9},{1... | collective-permute-start | bytes 811016 | tf_op jit(solution)/shard_map/ppermute | solution.py:125
  4.5 11.4 %collective-permute-start.3 = (bf16[32,4224]{1,0:T(8,128)(2,1)S(1)}, bf16[32,4224]{1,0:T(8,128)(2,1)S(1)}, u32[]{:S(2)}, u32[]{:S(2)}) collective-permute-start(bf16[32,4224]{1,0:T(8,128)(2,1)S(1)} %fusion.44), channel_id=1, source_target_pairs={{0,4},{1,5},{2,6},{3,7},{4,8},{5,9},{6,10},{7,11},{8,12},{9,13},{1... | collective-permute-start | bytes 811016 | tf_op jit(solution)/shard_map/ppermute | solution.py:120
  10.1 28.6 %collective-permute-start.10 = (bf16[32,4224]{1,0:T(8,128)(2,1)S(1)}, bf16[32,4224]{1,0:T(8,128)(2,1)S(1)}, u32[]{:S(2)}, u32[]{:S(2)}) collective-permute-start(bf16[32,4224]{1,0:T(8,128)(2,1)S(1)} %fusion.44), channel_id=1, source_target_pairs={{0,2},{1,3},{2,0},{3,1},{4,6},{5,7},{6,4},{7,5},{8,10},{9,11},{10,... | collective-permute-start | bytes 811016 | tf_op jit(solution)/shard_map/ppermute | solution.py:117
  14.6 9.5 %collective-permute-start.1 = (bf16[32,4224]{1,0:T(8,128)(2,1)S(1)}, bf16[32,4224]{1,0:T(8,128)(2,1)S(1)}, u32[]{:S(2)}, u32[]{:S(2)}) collective-permute-start(bf16[32,4224]{1,0:T(8,128)(2,1)S(1)} %collective-permute-done), channel_id=1, source_target_pairs={{4,0},{5,1},{6,2},{7,3},{8,4},{9,5},{10,6},{11,7},{20,16},{21,17},... | collective-permute-start | bytes 811016 | tf_op jit(solution)/shard_map/ppermute | solution.py:125
  15.9 9.5 %collective-permute-start.4 = (bf16[32,4224]{1,0:T(8,128)(2,1)S(1)}, bf16[32,4224]{1,0:T(8,128)(2,1)S(1)}, u32[]{:S(2)}, u32[]{:S(2)}) collective-permute-start(bf16[32,4224]{1,0:T(8,128)(2,1)S(1)} %collective-permute-done.3), channel_id=1, source_target_pairs={{4,8},{5,9},{6,10},{7,11},{8,12},{9,13},{10,14},{11,15},{20,24},{2... | collective-permute-start | bytes 811016 | tf_op jit(solution)/shard_map/ppermute | solution.py:120
  16.7 22.2 %collective-permute-start.8 = (bf16[32,4224]{1,0:T(8,128)(2,1)S(1)}, bf16[32,4224]{1,0:T(8,128)(2,1)S(1)}, u32[]{:S(2)}, u32[]{:S(2)}) collective-permute-start(bf16[32,4224]{1,0:T(8,128)(2,1)S(1)} %collective-permute-done), channel_id=1, source_target_pairs={{0,2},{1,3},{2,0},{3,1},{4,6},{5,7},{6,4},{7,5},{8,10},{9,11},{10,... | collective-permute-start | bytes 811016 | tf_op jit(solution)/shard_map/ppermute | solution.py:143
  20.3 19.1 %collective-permute-start.9 = (bf16[32,4224]{1,0:T(8,128)(2,1)S(1)}, bf16[32,4224]{1,0:T(8,128)(2,1)S(1)}, u32[]{:S(2)}, u32[]{:S(2)}) collective-permute-start(bf16[32,4224]{1,0:T(8,128)(2,1)S(1)} %collective-permute-done.3), channel_id=1, source_target_pairs={{4,6},{5,7},{6,4},{7,5},{8,10},{9,11},{10,8},{11,9},{12,14},{13,15... | collective-permute-start | bytes 811016 | tf_op jit(solution)/shard_map/ppermute | solution.py:142
  24.2 9.7 %collective-permute-start.2 = (bf16[32,4224]{1,0:T(8,128)(2,1)S(1)}, bf16[32,4224]{1,0:T(8,128)(2,1)S(1)}, u32[]{:S(2)}, u32[]{:S(2)}) collective-permute-start(bf16[32,4224]{1,0:T(8,128)(2,1)S(1)} %collective-permute-done.1), channel_id=1, source_target_pairs={{4,0},{5,1},{6,2},{7,3},{20,16},{21,17},{22,18},{23,19}} | collective-permute-start | bytes 811016 | tf_op jit(solution)/shard_map/ppermute | solution.py:125
  25.5 10.0 %collective-permute-start.5 = (bf16[32,4224]{1,0:T(8,128)(2,1)S(1)}, bf16[32,4224]{1,0:T(8,128)(2,1)S(1)}, u32[]{:S(2)}, u32[]{:S(2)}) collective-permute-start(bf16[32,4224]{1,0:T(8,128)(2,1)S(1)} %collective-permute-done.4), channel_id=1, source_target_pairs={{8,12},{9,13},{10,14},{11,15},{24,28},{25,29},{26,30},{27,31}} | collective-permute-start | bytes 811016 | tf_op jit(solution)/shard_map/ppermute | solution.py:120
  33.9 9.4 %collective-permute-start.7 = (bf16[32,4224]{1,0:T(8,128)(2,1)}, bf16[32,4224]{1,0:T(8,128)(2,1)S(1)}, u32[]{:S(2)}, u32[]{:S(2)}) collective-permute-start(bf16[32,4224]{1,0:T(8,128)(2,1)} %broadcast_select_fusion.2), channel_id=1, source_target_pairs={{0,2},{1,3},{2,0},{3,1},{4,6},{5,7},{6,4},{7,5},{8,10},{9,11},{10,... | collective-permute-start | bytes 811016 | tf_op jit(solution)/shard_map/ppermute | solution.py:136
  36.2 10.1 %collective-permute-start.6 = (bf16[32,4224]{1,0:T(8,128)(2,1)}, bf16[32,4224]{1,0:T(8,128)(2,1)}, u32[]{:S(2)}, u32[]{:S(2)}) collective-permute-start(bf16[32,4224]{1,0:T(8,128)(2,1)} %broadcast_select_fusion.3), channel_id=1, source_target_pairs={{0,2},{1,3},{2,0},{3,1},{12,14},{13,15},{14,12},{15,13},{16,18},{1... | collective-permute-start | bytes 811016 | tf_op jit(solution)/shard_map/ppermute | solution.py:136
  38.8 21.3 %collective-permute-start.12 = (bf16[2048,768]{1,0:T(8,128)(2,1)}, bf16[2048,768]{1,0:T(8,128)(2,1)S(1)}, u32[]{:S(2)}, u32[]{:S(2)}) collective-permute-start(bf16[2048,768]{1,0:T(8,128)(2,1)} %bitcast.63), channel_id=1, source_target_pairs={{0,1},{1,0},{2,3},{3,2},{4,5},{5,4},{6,7},{7,6},{8,9},{9,8},{10,11... | collective-permute-start | bytes 9437192 | tf_op jit(solution)/shard_map/ppermute | solution.py:253
  38.8 22.2 %collective-permute-start.11 = (bf16[2048,768]{1,0:T(8,128)(2,1)}, bf16[2048,768]{1,0:T(8,128)(2,1)S(1)}, u32[]{:S(2)}, u32[]{:S(2)}) collective-permute-start(bf16[2048,768]{1,0:T(8,128)(2,1)} %bitcast.71), channel_id=1, source_target_pairs={{0,1},{1,0},{2,3},{3,2},{4,5},{5,4},{6,7},{7,6},{8,9},{9,8},{10,11... | collective-permute-start | bytes 9437192 | tf_op jit(solution)/shard_map/ppermute | solution.py:252
  39.3 22.8 %collective-permute-start.13 = (bf16[768,2048]{1,0:T(8,128)(2,1)}, bf16[768,2048]{1,0:T(8,128)(2,1)S(1)}, u32[]{:S(2)}, u32[]{:S(2)}) collective-permute-start(bf16[768,2048]{1,0:T(8,128)(2,1)} %bitcast.72), channel_id=1, source_target_pairs={{0,1},{1,0},{2,3},{3,2},{4,5},{5,4},{6,7},{7,6},{8,9},{9,8},{10,11... | collective-permute-start | bytes 9437192 | tf_op jit(solution)/shard_map/ppermute | solution.py:254
  50.1 1.9 %copy-start = (bf16[1,2048,768]{2,1,0:T(8,128)(2,1)S(1)}, bf16[1,2048,768]{2,1,0:T(8,128)(2,1)}, u32[]{:S(2)}) copy-start(bf16[1,2048,768]{2,1,0:T(8,128)(2,1)} %param.16) | copy-start | bytes 9437188
  52.0 1.9 %copy-start.6 = (bf16[1,2048,768]{2,1,0:T(8,128)(2,1)S(1)}, bf16[1,2048,768]{2,1,0:T(8,128)(2,1)}, u32[]{:S(2)}) copy-start(bf16[1,2048,768]{2,1,0:T(8,128)(2,1)} %param.15) | copy-start | bytes 9437188
  53.9 1.9 %copy-start.7 = (bf16[1,768,2048]{2,1,0:T(8,128)(2,1)S(1)}, bf16[1,768,2048]{2,1,0:T(8,128)(2,1)}, u32[]{:S(2)}) copy-start(bf16[1,768,2048]{2,1,0:T(8,128)(2,1)} %param.17) | copy-start | bytes 9437188
  67.5 9.9 %collective-permute-start.15 = (bf16[32,4096]{1,0:T(8,128)(2,1)S(1)}, bf16[32,4096]{1,0:T(8,128)(2,1)S(1)}, u32[]{:S(2)}, u32[]{:S(2)}) collective-permute-start(bf16[32,4096]{1,0:T(8,128)(2,1)S(1)} %get-tuple-element.17), channel_id=1, source_target_pairs={{0,2},{1,3},{2,0},{3,1},{12,14},{13,15},{14,12},{15,13},{16,18},{1... | collective-permute-start | bytes 786440 | tf_op jit(solution)/shard_map/ppermute | solution.py:165
  70.2 19.4 %copy-start.5 = (s32[128]{0:T(128)S(1)}, s32[128]{0:T(128)}, u32[]{:S(2)}) copy-start(s32[128]{0:T(128)} %param.12) | copy-start | bytes 1540
  70.2 12.1 %collective-permute-start.17 = (bf16[32,4096]{1,0:T(8,128)(2,1)S(1)}, bf16[32,4096]{1,0:T(8,128)(2,1)S(1)}, u32[]{:S(2)}, u32[]{:S(2)}) collective-permute-start(bf16[32,4096]{1,0:T(8,128)(2,1)S(1)} %get-tuple-element.16), channel_id=1, source_target_pairs={{0,2},{1,3},{2,0},{3,1},{4,6},{5,7},{6,4},{7,5},{8,10},{9,11},{10,... | collective-permute-start | bytes 786440 | tf_op jit(solution)/shard_map/ppermute | solution.py:165
  77.4 6.9 %collective-permute-start.16 = (bf16[32,4096]{1,0:T(8,128)(2,1)S(1)}, bf16[32,4096]{1,0:T(8,128)(2,1)S(1)}, u32[]{:S(2)}, u32[]{:S(2)}) collective-permute-start(bf16[32,4096]{1,0:T(8,128)(2,1)S(1)} %fusion.33), channel_id=1, source_target_pairs={{0,4},{1,5},{2,6},{3,7},{16,20},{17,21},{18,22},{19,23}} | collective-permute-start | bytes 786440 | tf_op jit(solution)/shard_map/ppermute | solution.py:181
  78.7 5.6 %collective-permute-start.21 = (bf16[32,4096]{1,0:T(8,128)(2,1)S(1)}, bf16[32,4096]{1,0:T(8,128)(2,1)S(1)}, u32[]{:S(2)}, u32[]{:S(2)}) collective-permute-start(bf16[32,4096]{1,0:T(8,128)(2,1)S(1)} %fusion.33), channel_id=1, source_target_pairs={{12,8},{13,9},{14,10},{15,11},{28,24},{29,25},{30,26},{31,27}} | collective-permute-start | bytes 786440 | tf_op jit(solution)/shard_map/ppermute | solution.py:186
  79.4 10.5 %collective-permute-start.19 = (bf16[32,4096]{1,0:T(8,128)(2,1)S(1)}, bf16[32,4096]{1,0:T(8,128)(2,1)S(1)}, u32[]{:S(2)}, u32[]{:S(2)}) collective-permute-start(bf16[32,4096]{1,0:T(8,128)(2,1)S(1)} %get-tuple-element.15), channel_id=1, source_target_pairs={{0,2},{1,3},{2,0},{3,1},{4,6},{5,7},{6,4},{7,5},{8,10},{9,11},{10,... | collective-permute-start | bytes 786440 | tf_op jit(solution)/shard_map/ppermute | solution.py:165
  81.6 8.3 %collective-permute-start.23 = (bf16[32,4096]{1,0:T(8,128)(2,1)S(1)}, bf16[32,4096]{1,0:T(8,128)(2,1)S(1)}, u32[]{:S(2)}, u32[]{:S(2)}) collective-permute-start(bf16[32,4096]{1,0:T(8,128)(2,1)S(1)} %get-tuple-element.14), channel_id=1, source_target_pairs={{4,6},{5,7},{6,4},{7,5},{8,10},{9,11},{10,8},{11,9},{12,14},{13,15... | collective-permute-start | bytes 786440 | tf_op jit(solution)/shard_map/ppermute | solution.py:165
  84.5 10.9 %collective-permute-start.18 = (bf16[32,4096]{1,0:T(8,128)(2,1)S(1)}, bf16[32,4096]{1,0:T(8,128)(2,1)S(1)}, u32[]{:S(2)}, u32[]{:S(2)}) collective-permute-start(bf16[32,4096]{1,0:T(8,128)(2,1)S(1)} %get-tuple-element.7), channel_id=1, source_target_pairs={{0,4},{1,5},{2,6},{3,7},{4,8},{5,9},{6,10},{7,11},{16,20},{17,21},... | collective-permute-start | bytes 786440 | tf_op jit(solution)/shard_map/ppermute | solution.py:181
  88.9 6.5 %collective-permute-start.22 = (bf16[32,4096]{1,0:T(8,128)(2,1)S(1)}, bf16[32,4096]{1,0:T(8,128)(2,1)S(1)}, u32[]{:S(2)}, u32[]{:S(2)}) collective-permute-start(bf16[32,4096]{1,0:T(8,128)(2,1)S(1)} %get-tuple-element.8), channel_id=1, source_target_pairs={{8,4},{9,5},{10,6},{11,7},{12,8},{13,9},{14,10},{15,11},{24,20},{2... | collective-permute-start | bytes 786440 | tf_op jit(solution)/shard_map/ppermute | solution.py:186
  89.6 13.7 %collective-permute-start.14 = (bf16[32,4096]{1,0:T(8,128)(2,1)S(1)}, bf16[32,4096]{1,0:T(8,128)(2,1)S(1)}, u32[]{:S(2)}, u32[]{:S(2)}) collective-permute-start(bf16[32,4096]{1,0:T(8,128)(2,1)S(1)} %get-tuple-element.13), channel_id=1, source_target_pairs={{0,2},{1,3},{2,0},{3,1},{4,6},{5,7},{6,4},{7,5},{8,10},{9,11},{10,... | collective-permute-start | bytes 786440 | tf_op jit(solution)/shard_map/ppermute | solution.py:165
  95.6 10.2 %collective-permute-start.20 = (bf16[32,4096]{1,0:T(8,128)(2,1)S(1)}, bf16[32,4096]{1,0:T(8,128)(2,1)S(1)}, u32[]{:S(2)}, u32[]{:S(2)}) collective-permute-start(bf16[32,4096]{1,0:T(8,128)(2,1)S(1)} %get-tuple-element.9), channel_id=1, source_target_pairs={{0,4},{1,5},{2,6},{3,7},{4,8},{5,9},{6,10},{7,11},{8,12},{9,13},{1... | collective-permute-start | bytes 786440 | tf_op jit(solution)/shard_map/ppermute | solution.py:181
  101.9 8.3 %collective-permute-start.24 = (bf16[32,4096]{1,0:T(8,128)(2,1)S(1)}, bf16[32,4096]{1,0:T(8,128)(2,1)S(1)}, u32[]{:S(2)}, u32[]{:S(2)}) collective-permute-start(bf16[32,4096]{1,0:T(8,128)(2,1)S(1)} %get-tuple-element.10), channel_id=1, source_target_pairs={{4,0},{5,1},{6,2},{7,3},{8,4},{9,5},{10,6},{11,7},{12,8},{13,9},{1... | collective-permute-start | bytes 786440 | tf_op jit(solution)/shard_map/ppermute | solution.py:186
  111.4 1.2 %copy-start.2 = (bf16[128,2048]{1,0:T(8,128)(2,1)S(1)}, bf16[128,2048]{1,0:T(8,128)(2,1)}, u32[]{:S(2)}) copy-start(bf16[128,2048]{1,0:T(8,128)(2,1)} %param.10) | copy-start | bytes 1572868
  (1 other events, 1.0 us)

commit v14 on v12

--- a/solution.py
+++ b/solution.py
@@ -108,6 +108,10 @@
     return stacked
 
 
+def by_line(line, values):
+    return pick(line, [jnp.asarray(v, jnp.int32) for v in values])
+
+
 def topo_all_gather(shard, experts):
     lines = experts // 4
     me = lax.axis_index("expert")
@@ -115,7 +119,17 @@
     swap_row = [(j, j ^ 2) for j in range(experts)]
     here = [(shard, line)]
     there = [(lax.ppermute(shard, "expert", swap_row), line)]
+    pieces = []
+    queues = [[] for _ in range(lines)]
     ahead, behind = shard, shard
+
+    def send_row(queue_heads):
+        senders = [z for z in range(lines) if queue_heads[z] is not None]
+        data = pick(line, [pieces[queue_heads[z] if queue_heads[z] is not None else 0][0] for z in range(lines)])
+        origin = by_line(line, [pieces[h][1][z] if h is not None else -1 for z, h in enumerate(queue_heads)])
+        pairs = [(j, j ^ 2) for j in range(experts) if j // 4 in senders]
+        there.append((lax.ppermute(data, "expert", pairs), origin))
+
     for step in range(1, lines):
         ahead = lax.ppermute(
             ahead,
@@ -129,10 +143,16 @@
         )
         here.append((ahead, line - step))
         here.append((behind, line + step))
-        ahead_row = [(j, j ^ 2) for j in range(experts) if j // 4 >= step]
-        behind_row = [(j, j ^ 2) for j in range(experts) if j // 4 <= lines - 1 - step]
-        there.append((lax.ppermute(ahead, "expert", ahead_row), line - step))
-        there.append((lax.ppermute(behind, "expert", behind_row), line + step))
+        pieces.append((ahead, [z - step for z in range(lines)]))
+        pieces.append((behind, [z + step for z in range(lines)]))
+        for z in range(lines):
+            if z >= step:
+                queues[z].append(len(pieces) - 2)
+            if z <= lines - 1 - step:
+                queues[z].append(len(pieces) - 1)
+        send_row([queues[z].pop(0) if queues[z] else None for z in range(lines)])
+    while any(queues):
+        send_row([queues[z].pop(0) if queues[z] else None for z in range(lines)])
     column = place(here, lines, shard)
     across = place(there, lines, shard)
     in_row = (me // 2) % 2
@@ -149,32 +169,42 @@
     keep = pick(in_row, [plane[:, 0], plane[:, 1]])
     give = pick(in_row, [plane[:, 1], plane[:, 0]])
     line = me // 4
-
-    def row_sum(target, senders):
+    plans = []
+    for z in range(lines):
+        needs = [(step, 0, z + lines - step) for step in range(z + 1, lines)]
+        needs += [(step, 1, z - lines + step) for step in range(lines - z, lines)]
+        needs = sorted(needs) + [(lines, 2, z)]
+        assert all(need[0] >= slot + 1 for slot, need in enumerate(needs))
+        plans.append(needs)
+    summed = []
+    for slot in range(lines):
+        target = by_line(line, [plans[z][slot][2] for z in range(lines)])
         mine = lax.dynamic_index_in_dim(keep, target, 0, keepdims=False)
         theirs = lax.dynamic_index_in_dim(give, target, 0, keepdims=False)
-        pairs = [(j, j ^ 2) for j in range(experts) if senders(j // 4)]
-        got = lax.ppermute(theirs.astype(jnp.bfloat16), "expert", pairs)
-        return mine + got.astype(jnp.float32)
+        got = lax.ppermute(theirs.astype(jnp.bfloat16), "expert", [(j, j ^ 2) for j in range(experts)])
+        summed.append(mine + got.astype(jnp.float32))
+
+    def ready(step, role):
+        slots = []
+        for z in range(lines):
+            found = [k for k, need in enumerate(plans[z]) if need[:2] == (step, role)]
+            slots.append(found[0] if found else 0)
+        return pick(line, [summed[k] for k in slots])
 
     ahead = jnp.zeros(keep.shape[1:], jnp.float32)
     behind = jnp.zeros(keep.shape[1:], jnp.float32)
     for step in range(1, lines):
-        target = jnp.clip(line + lines - step, 0, lines - 1)
-        ahead = ahead + row_sum(target, lambda z, s=step: z <= s - 1)
         ahead = lax.ppermute(
-            ahead.astype(jnp.bfloat16),
+            (ahead + ready(step, 0)).astype(jnp.bfloat16),
             "expert",
             [(j, j + 4) for j in range(experts) if j // 4 <= step - 1],
         ).astype(jnp.float32)
-        target = jnp.clip(line - lines + step, 0, lines - 1)
-        behind = behind + row_sum(target, lambda z, s=step: z >= lines - s)
         behind = lax.ppermute(
-            behind.astype(jnp.bfloat16),
+            (behind + ready(step, 1)).astype(jnp.bfloat16),
             "expert",
             [(j, j - 4) for j in range(experts) if j // 4 >= lines - step],
         ).astype(jnp.float32)
-    return row_sum(line, lambda z: True) + ahead + behind
+    return ready(lines, 2) + ahead + behind
 
 
 def expert_dense(cent_in, grad_in, gate_mat, up_mat, down_mat):

time: 119 us -> 124 us (1.042)
  waiting for transfers between devices: 27.4 us -> 59.2 us
  starting transfers between devices: 60.9 us -> 32.1 us
  matrix products: 14.2 us -> 17.9 us
  other arithmetic: 9.09 us -> 7.65 us
    ppermute x19 -> x13, starting transfers between devices: 47.8 us -> 19.5 us  [the longest x3 10.9 us: topo_reduce_scatter(): lax.ppermute((ahead + ready(step, 0)).astype(jnp.bfloat16), 'expert', [(j...]
    ppermute x19 -> x13, waiting for transfers between devices: 18.3 us -> 42.3 us  [the longest x3 14.4 us: send_row(): there.append((lax.ppermute(data, 'expert', pairs), origin))]
    ppermute x3, waiting for transfers between devices: 9.06 us -> 16.9 us  [topo_all_gather(): lax.ppermute(behind, 'expert', [(j, j - 4) for j in range(experts) if 1 <...]
    dot_general x2, matrix products: 1.99 us -> 3.84 us  [expert_dense(): up_act = jnp.dot(cent_in, up_mat, preferred_element_type=jnp.float32)]
    dot_general x2, matrix products: 2.17 us -> 4 us  [expert_dense(): lax.dot_general(up_grad, up_mat, against, preferred_element_type=jnp.floa...]
    select_n x4 -> x5, other arithmetic: 4.68 us -> 3.11 us  [pick(): chosen = jnp.where(index == position, options[position], chosen)]
  transfers between devices with their start and end apart: 29 -> 23, of which waited for: 10 -> 12; matrix products, arithmetic and copies ran while one was open for 12% -> 11% of each run, Pallas kernels for 0% -> 0%
where the time goes in v14:
time: 124 us
  waiting for transfers between devices  59.2 us (48%)
  starting transfers between devices  32.1 us (26%)
  matrix products  17.9 us (14%)
  other arithmetic  7.65 us (6%)
  local copies, waits for them, and re-layouts  5.6 us (5%)
    ppermute x3, waiting for transfers between devices, topo_all_gather(): lax.ppermute(behind, 'expert', [(j, j - 4) for j in range(experts) if 1 <...  16.9 us
    ppermute x3, waiting for transfers between devices, send_row(): there.append((lax.ppermute(data, 'expert', pairs), origin))  14.4 us
    ppermute x3, waiting for transfers between devices, topo_reduce_scatter(): lax.ppermute((ahead + ready(step, 0)).astype(jnp.bfloat16), 'expert', [(j...  12.5 us
    ppermute x3, starting transfers between devices, topo_reduce_scatter(): lax.ppermute((ahead + ready(step, 0)).astype(jnp.bfloat16), 'expert', [(j...  10.9 us
    ppermute x4, waiting for transfers between devices, topo_reduce_scatter(): lax.ppermute(theirs.astype(jnp.bfloat16), 'expert', [(j, j ^ 2) for j in...  7.97 us
    ppermute x3, waiting for transfers between devices, topo_reduce_scatter(): lax.ppermute((behind + ready(step, 1)).astype(jnp.bfloat16), 'expert', [(...  7.46 us
    ppermute x3, starting transfers between devices, topo_all_gather(): lax.ppermute(ahead, 'expert', [(j, j + 4) for j in range(experts) if step...  6.93 us
    dot_general x2, matrix products, expert_dense(): lax.dot_general(up_grad, up_mat, against, preferred_element_type=jnp.floa...  4 us
  transfers between devices with their start and end apart: 23, of which 12 were waited for; matrix products, arithmetic and copies ran while one was open for 11% of the time, Pallas kernels for 0%

profile of v14, /device:TPU:0, one launch (start us, length us, event | category | flops | bytes accessed | tf_op | source)
XLA Modules:
  0.0 123.6 jit_solution(16922579087719884970)
XLA Ops:
  1.4 1.5 %fusion.14 = f32[32,4096]{1,0:T(8,128)S(1)} fusion(bf16[128,2048]{1,0:T(8,128)(2,1)} %param.11, bf16[128,2048]{1,0:T(8,128)(2,1)} %param.10, s32[128]{0:T(128)} %param.12), kind=kOutput, calls=%fused_computation.26 | convolution fusion | flops 35655680 | bytes 1573376 | tf_op jit(solution)/shard_map/dot_general | solution.py:238
  3.2 1.3 %collective-permute-start = (bf16[32,4224]{1,0:T(8,128)(2,1)S(1)}, bf16[32,4224]{1,0:T(8,128)(2,1)S(1)}, u32[]{:S(2)}, u32[]{:S(2)}) collective-permute-start(bf16[32,4224]{1,0:T(8,128)(2,1)S(1)} %fusion.47), channel_id=1, source_target_pairs={{4,0},{5,1},{6,2},{7,3},{8,4},{9,5},{10,6},{11,7},{12,8},{13,9},{1... | collective-permute-start | bytes 811016 | tf_op jit(solution)/shard_map/ppermute | solution.py:139
  4.5 5.6 %collective-permute-start.3 = (bf16[32,4224]{1,0:T(8,128)(2,1)S(1)}, bf16[32,4224]{1,0:T(8,128)(2,1)S(1)}, u32[]{:S(2)}, u32[]{:S(2)}) collective-permute-start(bf16[32,4224]{1,0:T(8,128)(2,1)S(1)} %fusion.47), channel_id=1, source_target_pairs={{0,4},{1,5},{2,6},{3,7},{4,8},{5,9},{6,10},{7,11},{8,12},{9,13},{1... | collective-permute-start | bytes 811016 | tf_op jit(solution)/shard_map/ppermute | solution.py:134
  10.1 4.5 %collective-permute-done = bf16[32,4224]{1,0:T(8,128)(2,1)S(1)} collective-permute-done((bf16[32,4224]{1,0:T(8,128)(2,1)S(1)}, bf16[32,4224]{1,0:T(8,128)(2,1)S(1)}, u32[]{:S(2)}, u32[]{:S(2)}) %collective-permute-start) | collective-permute-done | bytes 270368 | tf_op jit(solution)/shard_map/ppermute | solution.py:139
  14.6 1.3 %collective-permute-start.1 = (bf16[32,4224]{1,0:T(8,128)(2,1)S(1)}, bf16[32,4224]{1,0:T(8,128)(2,1)S(1)}, u32[]{:S(2)}, u32[]{:S(2)}) collective-permute-start(bf16[32,4224]{1,0:T(8,128)(2,1)S(1)} %collective-permute-done), channel_id=1, source_target_pairs={{4,0},{5,1},{6,2},{7,3},{8,4},{9,5},{10,6},{11,7},{20,16},{21,17},... | collective-permute-start | bytes 811016 | tf_op jit(solution)/shard_map/ppermute | solution.py:139
  16.6 1.7 %collective-permute-start.9 = (bf16[32,4224]{1,0:T(8,128)(2,1)S(1)}, bf16[32,4224]{1,0:T(8,128)(2,1)S(1)}, u32[]{:S(2)}, u32[]{:S(2)}) collective-permute-start(bf16[32,4224]{1,0:T(8,128)(2,1)S(1)} %fusion.47), channel_id=1, source_target_pairs={{0,2},{1,3},{2,0},{3,1},{4,6},{5,7},{6,4},{7,5},{8,10},{9,11},{10,... | collective-permute-start | bytes 811016 | tf_op jit(solution)/shard_map/ppermute | solution.py:121
  18.4 5.8 %collective-permute-done.1 = bf16[32,4224]{1,0:T(8,128)(2,1)S(1)} collective-permute-done((bf16[32,4224]{1,0:T(8,128)(2,1)S(1)}, bf16[32,4224]{1,0:T(8,128)(2,1)S(1)}, u32[]{:S(2)}, u32[]{:S(2)}) %collective-permute-start.1) | collective-permute-done | bytes 270368 | tf_op jit(solution)/shard_map/ppermute | solution.py:139
  24.2 1.3 %collective-permute-start.2 = (bf16[32,4224]{1,0:T(8,128)(2,1)S(1)}, bf16[32,4224]{1,0:T(8,128)(2,1)S(1)}, u32[]{:S(2)}, u32[]{:S(2)}) collective-permute-start(bf16[32,4224]{1,0:T(8,128)(2,1)S(1)} %collective-permute-done.1), channel_id=1, source_target_pairs={{4,0},{5,1},{6,2},{7,3},{20,16},{21,17},{22,18},{23,19}} | collective-permute-start | bytes 811016 | tf_op jit(solution)/shard_map/ppermute | solution.py:139
  26.2 6.6 %collective-permute-done.2 = bf16[32,4224]{1,0:T(8,128)(2,1)S(1)} collective-permute-done((bf16[32,4224]{1,0:T(8,128)(2,1)S(1)}, bf16[32,4224]{1,0:T(8,128)(2,1)S(1)}, u32[]{:S(2)}, u32[]{:S(2)}) %collective-permute-start.2) | collective-permute-done | bytes 270368 | tf_op jit(solution)/shard_map/ppermute | solution.py:139
  33.8 1.1 collective-permute-start.6
  35.8 1.1 collective-permute-start.8
  37.0 6.4 %collective-permute-done.6 = bf16[32,4224]{1,0:T(8,128)(2,1)S(1)} collective-permute-done((bf16[32,4224]{1,0:T(8,128)(2,1)}, bf16[32,4224]{1,0:T(8,128)(2,1)S(1)}, u32[]{:S(2)}, u32[]{:S(2)}) %collective-permute-start.6) | collective-permute-done | bytes 270368 | tf_op jit(solution)/shard_map/ppermute | solution.py:131
  43.4 5.1 %collective-permute-done.7 = bf16[32,4224]{1,0:T(8,128)(2,1)S(1)} collective-permute-done((bf16[32,4224]{1,0:T(8,128)(2,1)}, bf16[32,4224]{1,0:T(8,128)(2,1)S(1)}, u32[]{:S(2)}, u32[]{:S(2)}) %collective-permute-start.7) | collective-permute-done | bytes 270368 | tf_op jit(solution)/shard_map/ppermute | solution.py:131
  48.5 2.9 %collective-permute-done.8 = bf16[32,4224]{1,0:T(8,128)(2,1)S(1)} collective-permute-done((bf16[32,4224]{1,0:T(8,128)(2,1)}, bf16[32,4224]{1,0:T(8,128)(2,1)S(1)}, u32[]{:S(2)}, u32[]{:S(2)}) %collective-permute-start.8) | collective-permute-done | bytes 270368 | tf_op jit(solution)/shard_map/ppermute | solution.py:131
  53.6 1.4 %copy-done = bf16[1,2048,768]{2,1,0:T(8,128)(2,1)S(1)} copy-done((bf16[1,2048,768]{2,1,0:T(8,128)(2,1)S(1)}, bf16[1,2048,768]{2,1,0:T(8,128)(2,1)}, u32[]{:S(2)}) %copy-start) | copy-done | bytes 3145752
  60.9 1.1 fusion.38
  62.0 1.1 fusion.6
  63.1 2.9 %fusion.22 = f32[256,768]{1,0:T(8,128)S(1)} fusion(bf16[2048,768]{1,0:T(8,128)(2,1)} %collective-permute-done.11, bf16[256,4224]{1,0:T(8,128)(2,1)S(1)} %bitcast.61), kind=kOutput, calls=%fused_computation.46 | convolution fusion | flops 805306368 | bytes 4980736 | tf_op jit(solution)/shard_map/dot_general | solution.py:213
  68.1 2.9 %fusion.39 = f32[256,2048]{1,0:T(8,128)S(1)} fusion(bf16[2048,768]{1,0:T(8,128)(2,1)} %collective-permute-done.11, f32[256,768]{1,0:T(8,128)S(1)} %fusion.18, f32[256,768]{1,0:T(8,128)S(1)} %fusion.24), kind=kOutput, calls=%fused_computation.75 | convolution fusion | flops 806486016 | bytes 6815744 | tf_op jit(solution)/shard_map/dot_general | solution.py:223
  71.0 1.1 fusion.9
  72.1 1.2 fusion.4
  75.1 1.5 %collective-permute-start.16 = (bf16[32,4096]{1,0:T(8,128)(2,1)S(1)}, bf16[32,4096]{1,0:T(8,128)(2,1)S(1)}, u32[]{:S(2)}, u32[]{:S(2)}) collective-permute-start(bf16[32,4096]{1,0:T(8,128)(2,1)S(1)} %get-tuple-element.15), channel_id=1, source_target_pairs={{0,2},{1,3},{2,0},{3,1},{4,6},{5,7},{6,4},{7,5},{8,10},{9,11},{10,... | collective-permute-start | bytes 786440 | tf_op jit(solution)/shard_map/ppermute | solution.py:184
  76.7 6.9 %collective-permute-done.14 = bf16[32,4096]{1,0:T(8,128)(2,1)S(1)} collective-permute-done((bf16[32,4096]{1,0:T(8,128)(2,1)S(1)}, bf16[32,4096]{1,0:T(8,128)(2,1)S(1)}, u32[]{:S(2)}, u32[]{:S(2)}) %collective-permute-start.14) | collective-permute-done | bytes 262176 | tf_op jit(solution)/shard_map/ppermute | solution.py:184
  83.6 1.5 %collective-permute-start.15 = (bf16[32,4096]{1,0:T(8,128)(2,1)S(1)}, bf16[32,4096]{1,0:T(8,128)(2,1)S(1)}, u32[]{:S(2)}, u32[]{:S(2)}) collective-permute-start(bf16[32,4096]{1,0:T(8,128)(2,1)S(1)} %get-tuple-element.5), channel_id=1, source_target_pairs={{0,4},{1,5},{2,6},{3,7},{16,20},{17,21},{18,22},{19,23}} | collective-permute-start | bytes 786440 | tf_op jit(solution)/shard_map/ppermute | solution.py:197
  87.5 3.5 %collective-permute-done.15 = bf16[32,4096]{1,0:T(8,128)(2,1)S(1)} collective-permute-done((bf16[32,4096]{1,0:T(8,128)(2,1)S(1)}, bf16[32,4096]{1,0:T(8,128)(2,1)S(1)}, u32[]{:S(2)}, u32[]{:S(2)}) %collective-permute-start.15) | collective-permute-done | bytes 262176 | tf_op jit(solution)/shard_map/ppermute | solution.py:197
  91.1 4.4 %collective-permute-start.17 = (bf16[32,4096]{1,0:T(8,128)(2,1)S(1)}, bf16[32,4096]{1,0:T(8,128)(2,1)S(1)}, u32[]{:S(2)}, u32[]{:S(2)}) collective-permute-start(bf16[32,4096]{1,0:T(8,128)(2,1)S(1)} %add_convert_fusion.1), channel_id=1, source_target_pairs={{0,4},{1,5},{2,6},{3,7},{4,8},{5,9},{6,10},{7,11},{16,20},{17,21},... | collective-permute-start | bytes 786440 | tf_op jit(solution)/shard_map/ppermute | solution.py:197
  95.5 6.6 %collective-permute-done.17 = bf16[32,4096]{1,0:T(8,128)(2,1)S(1)} collective-permute-done((bf16[32,4096]{1,0:T(8,128)(2,1)S(1)}, bf16[32,4096]{1,0:T(8,128)(2,1)S(1)}, u32[]{:S(2)}, u32[]{:S(2)}) %collective-permute-start.17) | collective-permute-done | bytes 262176 | tf_op jit(solution)/shard_map/ppermute | solution.py:197
  103.2 5.0 %collective-permute-start.19 = (bf16[32,4096]{1,0:T(8,128)(2,1)S(1)}, bf16[32,4096]{1,0:T(8,128)(2,1)S(1)}, u32[]{:S(2)}, u32[]{:S(2)}) collective-permute-start(bf16[32,4096]{1,0:T(8,128)(2,1)S(1)} %get-tuple-element.9), channel_id=1, source_target_pairs={{0,4},{1,5},{2,6},{3,7},{4,8},{5,9},{6,10},{7,11},{8,12},{9,13},{1... | collective-permute-start | bytes 786440 | tf_op jit(solution)/shard_map/ppermute | solution.py:197
  108.4 1.3 %collective-permute-start.22 = (bf16[32,4096]{1,0:T(8,128)(2,1)S(1)}, bf16[32,4096]{1,0:T(8,128)(2,1)S(1)}, u32[]{:S(2)}, u32[]{:S(2)}) collective-permute-start(bf16[32,4096]{1,0:T(8,128)(2,1)S(1)} %add_convert_fusion), channel_id=1, source_target_pairs={{4,0},{5,1},{6,2},{7,3},{8,4},{9,5},{10,6},{11,7},{12,8},{13,9},{1... | collective-permute-start | bytes 786440 | tf_op jit(solution)/shard_map/ppermute | solution.py:202
  109.7 2.4 %collective-permute-done.19 = bf16[32,4096]{1,0:T(8,128)(2,1)S(1)} collective-permute-done((bf16[32,4096]{1,0:T(8,128)(2,1)S(1)}, bf16[32,4096]{1,0:T(8,128)(2,1)S(1)}, u32[]{:S(2)}, u32[]{:S(2)}) %collective-permute-start.19) | collective-permute-done | bytes 262176 | tf_op jit(solution)/shard_map/ppermute | solution.py:197
  112.1 7.5 %collective-permute-done.22 = bf16[32,4096]{1,0:T(8,128)(2,1)S(1)} collective-permute-done((bf16[32,4096]{1,0:T(8,128)(2,1)S(1)}, bf16[32,4096]{1,0:T(8,128)(2,1)S(1)}, u32[]{:S(2)}, u32[]{:S(2)}) %collective-permute-start.22) | collective-permute-done | bytes 262176 | tf_op jit(solution)/shard_map/ppermute | solution.py:202
  122.0 1.7 %select_add_fusion = (f32[128,2048]{1,0:T(8,128)}, f32[128,2048]{1,0:T(8,128)}) fusion(f32[128,2048]{1,0:T(8,128)S(1)} %gather_fusion.1, bf16[128,2048]{1,0:T(8,128)(2,1)S(1)} %copy-done.1, pred[128]{0:T(512)(128)(4,1)S(1)} %compare_and_fusion, f32[128,2048]{1,0:T(8,128)S(1)} %gather_fusion, bf16[128,2048]{1,0:T(8,128)(2,1)S(1)} %copy-done.2), kind=kLoop, calls=%fused_computation.30 | loop fusion | flops 1572864 | bytes 5243008 | tf_op jit(solution)/shard_map/add | solution.py:283
  (79 shorter events, 22.4 us)
Async XLA Ops:
  0.6 2.4 %copy-start.4 = (s32[32,8]{0,1:T(8,128)S(1)}, s32[32,8]{0,1:T(8,128)}, u32[]{:S(2)}) copy-start(s32[32,8]{0,1:T(8,128)} %param.13) | copy-start | bytes 3076
  0.6 2.4 %copy-start.3 = (f32[32,8]{0,1:T(8,128)S(1)}, f32[32,8]{0,1:T(8,128)}, u32[]{:S(2)}) copy-start(f32[32,8]{0,1:T(8,128)} %param.14) | copy-start | bytes 3076
  3.2 11.4 %collective-permute-start = (bf16[32,4224]{1,0:T(8,128)(2,1)S(1)}, bf16[32,4224]{1,0:T(8,128)(2,1)S(1)}, u32[]{:S(2)}, u32[]{:S(2)}) collective-permute-start(bf16[32,4224]{1,0:T(8,128)(2,1)S(1)} %fusion.47), channel_id=1, source_target_pairs={{4,0},{5,1},{6,2},{7,3},{8,4},{9,5},{10,6},{11,7},{12,8},{13,9},{1... | collective-permute-start | bytes 811016 | tf_op jit(solution)/shard_map/ppermute | solution.py:139
  4.5 11.4 %collective-permute-start.3 = (bf16[32,4224]{1,0:T(8,128)(2,1)S(1)}, bf16[32,4224]{1,0:T(8,128)(2,1)S(1)}, u32[]{:S(2)}, u32[]{:S(2)}) collective-permute-start(bf16[32,4224]{1,0:T(8,128)(2,1)S(1)} %fusion.47), channel_id=1, source_target_pairs={{0,4},{1,5},{2,6},{3,7},{4,8},{5,9},{6,10},{7,11},{8,12},{9,13},{1... | collective-permute-start | bytes 811016 | tf_op jit(solution)/shard_map/ppermute | solution.py:134
  14.6 9.5 %collective-permute-start.1 = (bf16[32,4224]{1,0:T(8,128)(2,1)S(1)}, bf16[32,4224]{1,0:T(8,128)(2,1)S(1)}, u32[]{:S(2)}, u32[]{:S(2)}) collective-permute-start(bf16[32,4224]{1,0:T(8,128)(2,1)S(1)} %collective-permute-done), channel_id=1, source_target_pairs={{4,0},{5,1},{6,2},{7,3},{8,4},{9,5},{10,6},{11,7},{20,16},{21,17},... | collective-permute-start | bytes 811016 | tf_op jit(solution)/shard_map/ppermute | solution.py:139
  15.9 9.5 %collective-permute-start.4 = (bf16[32,4224]{1,0:T(8,128)(2,1)S(1)}, bf16[32,4224]{1,0:T(8,128)(2,1)S(1)}, u32[]{:S(2)}, u32[]{:S(2)}) collective-permute-start(bf16[32,4224]{1,0:T(8,128)(2,1)S(1)} %collective-permute-done.3), channel_id=1, source_target_pairs={{4,8},{5,9},{6,10},{7,11},{8,12},{9,13},{10,14},{11,15},{20,24},{2... | collective-permute-start | bytes 811016 | tf_op jit(solution)/shard_map/ppermute | solution.py:134
  16.6 20.3 %collective-permute-start.9 = (bf16[32,4224]{1,0:T(8,128)(2,1)S(1)}, bf16[32,4224]{1,0:T(8,128)(2,1)S(1)}, u32[]{:S(2)}, u32[]{:S(2)}) collective-permute-start(bf16[32,4224]{1,0:T(8,128)(2,1)S(1)} %fusion.47), channel_id=1, source_target_pairs={{0,2},{1,3},{2,0},{3,1},{4,6},{5,7},{6,4},{7,5},{8,10},{9,11},{10,... | collective-permute-start | bytes 811016 | tf_op jit(solution)/shard_map/ppermute | solution.py:121
  18.4 44.8 %collective-permute-start.11 = (bf16[2048,768]{1,0:T(8,128)(2,1)}, bf16[2048,768]{1,0:T(8,128)(2,1)}, u32[]{:S(2)}, u32[]{:S(2)}) collective-permute-start(bf16[2048,768]{1,0:T(8,128)(2,1)} %bitcast.56), channel_id=1, source_target_pairs={{0,1},{1,0},{2,3},{3,2},{4,5},{5,4},{6,7},{7,6},{8,9},{9,8},{10,11... | collective-permute-start | bytes 9437192 | tf_op jit(solution)/shard_map/ppermute | solution.py:269
  24.2 8.6 %collective-permute-start.2 = (bf16[32,4224]{1,0:T(8,128)(2,1)S(1)}, bf16[32,4224]{1,0:T(8,128)(2,1)S(1)}, u32[]{:S(2)}, u32[]{:S(2)}) collective-permute-start(bf16[32,4224]{1,0:T(8,128)(2,1)S(1)} %collective-permute-done.1), channel_id=1, source_target_pairs={{4,0},{5,1},{6,2},{7,3},{20,16},{21,17},{22,18},{23,19}} | collective-permute-start | bytes 811016 | tf_op jit(solution)/shard_map/ppermute | solution.py:139
  25.5 7.3 %collective-permute-start.5 = (bf16[32,4224]{1,0:T(8,128)(2,1)S(1)}, bf16[32,4224]{1,0:T(8,128)(2,1)S(1)}, u32[]{:S(2)}, u32[]{:S(2)}) collective-permute-start(bf16[32,4224]{1,0:T(8,128)(2,1)S(1)} %collective-permute-done.4), channel_id=1, source_target_pairs={{8,12},{9,13},{10,14},{11,15},{24,28},{25,29},{26,30},{27,31}} | collective-permute-start | bytes 811016 | tf_op jit(solution)/shard_map/ppermute | solution.py:134
  33.8 9.6 %collective-permute-start.6 = (bf16[32,4224]{1,0:T(8,128)(2,1)}, bf16[32,4224]{1,0:T(8,128)(2,1)S(1)}, u32[]{:S(2)}, u32[]{:S(2)}) collective-permute-start(bf16[32,4224]{1,0:T(8,128)(2,1)} %get-tuple-element.17), channel_id=1, source_target_pairs={{0,2},{1,3},{2,0},{3,1},{4,6},{5,7},{6,4},{7,5},{8,10},{9,11},{10,... | collective-permute-start | bytes 811016 | tf_op jit(solution)/shard_map/ppermute | solution.py:131
  34.9 13.6 %collective-permute-start.7 = (bf16[32,4224]{1,0:T(8,128)(2,1)}, bf16[32,4224]{1,0:T(8,128)(2,1)S(1)}, u32[]{:S(2)}, u32[]{:S(2)}) collective-permute-start(bf16[32,4224]{1,0:T(8,128)(2,1)} %get-tuple-element.18), channel_id=1, source_target_pairs={{0,2},{1,3},{2,0},{3,1},{4,6},{5,7},{6,4},{7,5},{8,10},{9,11},{10,... | collective-permute-start | bytes 811016 | tf_op jit(solution)/shard_map/ppermute | solution.py:131
  35.8 15.6 %collective-permute-start.8 = (bf16[32,4224]{1,0:T(8,128)(2,1)}, bf16[32,4224]{1,0:T(8,128)(2,1)S(1)}, u32[]{:S(2)}, u32[]{:S(2)}) collective-permute-start(bf16[32,4224]{1,0:T(8,128)(2,1)} %get-tuple-element.19), channel_id=1, source_target_pairs={{0,2},{1,3},{2,0},{3,1},{4,6},{5,7},{6,4},{7,5},{8,10},{9,11},{10,... | collective-permute-start | bytes 811016 | tf_op jit(solution)/shard_map/ppermute | solution.py:131
  36.9 29.1 %collective-permute-start.10 = (bf16[2048,768]{1,0:T(8,128)(2,1)}, bf16[2048,768]{1,0:T(8,128)(2,1)S(1)}, u32[]{:S(2)}, u32[]{:S(2)}) collective-permute-start(bf16[2048,768]{1,0:T(8,128)(2,1)} %bitcast.64), channel_id=1, source_target_pairs={{0,1},{1,0},{2,3},{3,2},{4,5},{5,4},{6,7},{7,6},{8,9},{9,8},{10,11... | collective-permute-start | bytes 9437192 | tf_op jit(solution)/shard_map/ppermute | solution.py:268
  43.4 23.6 %collective-permute-start.12 = (bf16[768,2048]{1,0:T(8,128)(2,1)}, bf16[768,2048]{1,0:T(8,128)(2,1)S(1)}, u32[]{:S(2)}, u32[]{:S(2)}) collective-permute-start(bf16[768,2048]{1,0:T(8,128)(2,1)} %bitcast.65), channel_id=1, source_target_pairs={{0,1},{1,0},{2,3},{3,2},{4,5},{5,4},{6,7},{7,6},{8,9},{9,8},{10,11... | collective-permute-start | bytes 9437192 | tf_op jit(solution)/shard_map/ppermute | solution.py:270
  53.1 1.9 %copy-start = (bf16[1,2048,768]{2,1,0:T(8,128)(2,1)S(1)}, bf16[1,2048,768]{2,1,0:T(8,128)(2,1)}, u32[]{:S(2)}) copy-start(bf16[1,2048,768]{2,1,0:T(8,128)(2,1)} %param.16) | copy-start | bytes 9437188
  55.0 1.9 %copy-start.6 = (bf16[1,2048,768]{2,1,0:T(8,128)(2,1)S(1)}, bf16[1,2048,768]{2,1,0:T(8,128)(2,1)}, u32[]{:S(2)}) copy-start(bf16[1,2048,768]{2,1,0:T(8,128)(2,1)} %param.15) | copy-start | bytes 9437188
  56.9 1.9 %copy-start.7 = (bf16[1,768,2048]{2,1,0:T(8,128)(2,1)S(1)}, bf16[1,768,2048]{2,1,0:T(8,128)(2,1)}, u32[]{:S(2)}) copy-start(bf16[1,768,2048]{2,1,0:T(8,128)(2,1)} %param.17) | copy-start | bytes 9437188
  74.3 9.3 %collective-permute-start.14 = (bf16[32,4096]{1,0:T(8,128)(2,1)S(1)}, bf16[32,4096]{1,0:T(8,128)(2,1)S(1)}, u32[]{:S(2)}, u32[]{:S(2)}) collective-permute-start(bf16[32,4096]{1,0:T(8,128)(2,1)S(1)} %get-tuple-element.16), channel_id=1, source_target_pairs={{0,2},{1,3},{2,0},{3,1},{4,6},{5,7},{6,4},{7,5},{8,10},{9,11},{10,... | collective-permute-start | bytes 786440 | tf_op jit(solution)/shard_map/ppermute | solution.py:184
  75.1 12.4 %collective-permute-start.16 = (bf16[32,4096]{1,0:T(8,128)(2,1)S(1)}, bf16[32,4096]{1,0:T(8,128)(2,1)S(1)}, u32[]{:S(2)}, u32[]{:S(2)}) collective-permute-start(bf16[32,4096]{1,0:T(8,128)(2,1)S(1)} %get-tuple-element.15), channel_id=1, source_target_pairs={{0,2},{1,3},{2,0},{3,1},{4,6},{5,7},{6,4},{7,5},{8,10},{9,11},{10,... | collective-permute-start | bytes 786440 | tf_op jit(solution)/shard_map/ppermute | solution.py:184
  83.6 7.3 %collective-permute-start.15 = (bf16[32,4096]{1,0:T(8,128)(2,1)S(1)}, bf16[32,4096]{1,0:T(8,128)(2,1)S(1)}, u32[]{:S(2)}, u32[]{:S(2)}) collective-permute-start(bf16[32,4096]{1,0:T(8,128)(2,1)S(1)} %get-tuple-element.5), channel_id=1, source_target_pairs={{0,4},{1,5},{2,6},{3,7},{16,20},{17,21},{18,22},{19,23}} | collective-permute-start | bytes 786440 | tf_op jit(solution)/shard_map/ppermute | solution.py:197
  85.1 10.4 %collective-permute-start.18 = (bf16[32,4096]{1,0:T(8,128)(2,1)S(1)}, bf16[32,4096]{1,0:T(8,128)(2,1)S(1)}, u32[]{:S(2)}, u32[]{:S(2)}) collective-permute-start(bf16[32,4096]{1,0:T(8,128)(2,1)S(1)} %get-tuple-element.14), channel_id=1, source_target_pairs={{0,2},{1,3},{2,0},{3,1},{4,6},{5,7},{6,4},{7,5},{8,10},{9,11},{10,... | collective-permute-start | bytes 786440 | tf_op jit(solution)/shard_map/ppermute | solution.py:184
  85.8 9.8 %collective-permute-start.20 = (bf16[32,4096]{1,0:T(8,128)(2,1)S(1)}, bf16[32,4096]{1,0:T(8,128)(2,1)S(1)}, u32[]{:S(2)}, u32[]{:S(2)}) collective-permute-start(bf16[32,4096]{1,0:T(8,128)(2,1)S(1)} %get-tuple-element.5), channel_id=1, source_target_pairs={{12,8},{13,9},{14,10},{15,11},{28,24},{29,25},{30,26},{31,27}} | collective-permute-start | bytes 786440 | tf_op jit(solution)/shard_map/ppermute | solution.py:202
  91.0 12.2 %copy-start.5 = (s32[128]{0:T(128)S(1)}, s32[128]{0:T(128)}, u32[]{:S(2)}) copy-start(s32[128]{0:T(128)} %param.12) | copy-start | bytes 1540
  91.1 11.0 %collective-permute-start.17 = (bf16[32,4096]{1,0:T(8,128)(2,1)S(1)}, bf16[32,4096]{1,0:T(8,128)(2,1)S(1)}, u32[]{:S(2)}, u32[]{:S(2)}) collective-permute-start(bf16[32,4096]{1,0:T(8,128)(2,1)S(1)} %add_convert_fusion.1), channel_id=1, source_target_pairs={{0,4},{1,5},{2,6},{3,7},{4,8},{5,9},{6,10},{7,11},{16,20},{17,21},... | collective-permute-start | bytes 786440 | tf_op jit(solution)/shard_map/ppermute | solution.py:197
  102.4 5.8 %collective-permute-start.21 = (bf16[32,4096]{1,0:T(8,128)(2,1)S(1)}, bf16[32,4096]{1,0:T(8,128)(2,1)S(1)}, u32[]{:S(2)}, u32[]{:S(2)}) collective-permute-start(bf16[32,4096]{1,0:T(8,128)(2,1)S(1)} %get-tuple-element.10), channel_id=1, source_target_pairs={{8,4},{9,5},{10,6},{11,7},{12,8},{13,9},{14,10},{15,11},{24,20},{2... | collective-permute-start | bytes 786440 | tf_op jit(solution)/shard_map/ppermute | solution.py:202
  103.1 6.6 %collective-permute-start.13 = (bf16[32,4096]{1,0:T(8,128)(2,1)S(1)}, bf16[32,4096]{1,0:T(8,128)(2,1)S(1)}, u32[]{:S(2)}, u32[]{:S(2)}) collective-permute-start(bf16[32,4096]{1,0:T(8,128)(2,1)S(1)} %get-tuple-element.13), channel_id=1, source_target_pairs={{0,2},{1,3},{2,0},{3,1},{4,6},{5,7},{6,4},{7,5},{8,10},{9,11},{10,... | collective-permute-start | bytes 786440 | tf_op jit(solution)/shard_map/ppermute | solution.py:184
  103.2 8.9 %collective-permute-start.19 = (bf16[32,4096]{1,0:T(8,128)(2,1)S(1)}, bf16[32,4096]{1,0:T(8,128)(2,1)S(1)}, u32[]{:S(2)}, u32[]{:S(2)}) collective-permute-start(bf16[32,4096]{1,0:T(8,128)(2,1)S(1)} %get-tuple-element.9), channel_id=1, source_target_pairs={{0,4},{1,5},{2,6},{3,7},{4,8},{5,9},{6,10},{7,11},{8,12},{9,13},{1... | collective-permute-start | bytes 786440 | tf_op jit(solution)/shard_map/ppermute | solution.py:197
  108.4 11.2 %collective-permute-start.22 = (bf16[32,4096]{1,0:T(8,128)(2,1)S(1)}, bf16[32,4096]{1,0:T(8,128)(2,1)S(1)}, u32[]{:S(2)}, u32[]{:S(2)}) collective-permute-start(bf16[32,4096]{1,0:T(8,128)(2,1)S(1)} %add_convert_fusion), channel_id=1, source_target_pairs={{4,0},{5,1},{6,2},{7,3},{8,4},{9,5},{10,6},{11,7},{12,8},{13,9},{1... | collective-permute-start | bytes 786440 | tf_op jit(solution)/shard_map/ppermute | solution.py:202
  120.8 1.0 copy-start.1
  120.8 1.2 copy-start.2

commit v15 on v13

--- a/solution.py
+++ b/solution.py
@@ -108,6 +108,10 @@
     return stacked
 
 
+def by_line(line, values):
+    return pick(line, [jnp.asarray(v, jnp.int32) for v in values])
+
+
 def topo_all_gather(shard, experts):
     lines = experts // 4
     me = lax.axis_index("expert")
@@ -115,7 +119,17 @@
     swap_row = [(j, j ^ 2) for j in range(experts)]
     here = [(shard, line)]
     there = [(lax.ppermute(shard, "expert", swap_row), line)]
+    pieces = []
+    queues = [[] for _ in range(lines)]
     ahead, behind = shard, shard
+
+    def send_row(queue_heads):
+        senders = [z for z in range(lines) if queue_heads[z] is not None]
+        data = pick(line, [pieces[queue_heads[z] if queue_heads[z] is not None else 0][0] for z in range(lines)])
+        origin = by_line(line, [pieces[h][1][z] if h is not None else -1 for z, h in enumerate(queue_heads)])
+        pairs = [(j, j ^ 2) for j in range(experts) if j // 4 in senders]
+        there.append((lax.ppermute(data, "expert", pairs), origin))
+
     for step in range(1, lines):
         ahead = lax.ppermute(
             ahead,
@@ -129,18 +143,16 @@
         )
         here.append((ahead, line - step))
         here.append((behind, line + step))
-        ahead_row = [(j, j ^ 2) for j in range(experts) if j // 4 >= step]
-        behind_row = [(j, j ^ 2) for j in range(experts) if j // 4 <= lines - 1 - step]
-        if 2 * step > lines - 1:
-            in_ahead = line >= step
-            got = lax.ppermute(
-                jnp.where(in_ahead, ahead, behind), "expert", sorted(ahead_row + behind_row)
-            )
-            origin = jnp.where(in_ahead, line - step, jnp.where(line <= lines - 1 - step, line + step, -1))
-            there.append((got, origin))
-        else:
-            there.append((lax.ppermute(ahead, "expert", ahead_row), line - step))
-            there.append((lax.ppermute(behind, "expert", behind_row), line + step))
+        pieces.append((ahead, [z - step for z in range(lines)]))
+        pieces.append((behind, [z + step for z in range(lines)]))
+        for z in range(lines):
+            if z >= step:
+                queues[z].append(len(pieces) - 2)
+            if z <= lines - 1 - step:
+                queues[z].append(len(pieces) - 1)
+        send_row([queues[z].pop(0) if queues[z] else None for z in range(lines)])
+    while any(queues):
+        send_row([queues[z].pop(0) if queues[z] else None for z in range(lines)])
     column = place(here, lines, shard)
     across = place(there, lines, shard)
     in_row = (me // 2) % 2

time: 115 us -> 122 us (1.061)
  waiting for transfers between devices: 39.6 us -> 48.2 us
  matrix products: 14.1 us -> 17.9 us
  starting transfers between devices: 43.6 us -> 40.8 us
  other arithmetic: 10 us -> 7.43 us
    ppermute x4 -> x3, waiting for transfers between devices: 6.9 us -> 14.4 us  [send_row(): there.append((lax.ppermute(data, 'expert', pairs), origin))]
    ppermute x4 -> x3, starting transfers between devices: 8.19 us -> 3.11 us  [send_row(): there.append((lax.ppermute(data, 'expert', pairs), origin))]
    ppermute x3, waiting for transfers between devices: 12.7 us -> 16.9 us  [topo_all_gather(): lax.ppermute(behind, 'expert', [(j, j - 4) for j in range(experts) if 1 <...]
    ppermute x3, starting transfers between devices: 12 us -> 15.2 us  [topo_reduce_scatter(): lax.ppermute((ahead + ahead_part).astype(jnp.bfloat16), 'expert', [(j, j...]
    ppermute x3, waiting for transfers between devices: 9.94 us -> 7.31 us  [topo_reduce_scatter(): lax.ppermute((ahead + ahead_part).astype(jnp.bfloat16), 'expert', [(j, j...]
    dot_general x2, matrix products: 1.95 us -> 3.84 us  [expert_dense(): up_act = jnp.dot(cent_in, up_mat, preferred_element_type=jnp.float32)]
    dot_general x2, matrix products: 2.12 us -> 4 us  [expert_dense(): lax.dot_general(up_grad, up_mat, against, preferred_element_type=jnp.floa...]
    select_n x2 -> x0, other arithmetic: 1.5 us -> none  [topo_all_gather(): jnp.where(in_ahead, ahead, behind)]
  transfers between devices with their start and end apart: 25 -> 24, of which waited for: 10 -> 11; matrix products, arithmetic and copies ran while one was open for 13% -> 11% of each run, Pallas kernels for 0% -> 0%
where the time goes in v15:
time: 122 us; the launch traced here: 121 us
  waiting for transfers between devices  48.2 us (40%)
  starting transfers between devices  40.8 us (33%)
  matrix products  17.9 us (15%)
  other arithmetic  7.43 us (6%)
  local copies, waits for them, and re-layouts  5.63 us (5%)
    ppermute x3, waiting for transfers between devices, topo_all_gather(): lax.ppermute(behind, 'expert', [(j, j - 4) for j in range(experts) if 1 <...  16.9 us
    ppermute x3, starting transfers between devices, topo_reduce_scatter(): lax.ppermute((ahead + ahead_part).astype(jnp.bfloat16), 'expert', [(j, j...  15.2 us
    ppermute x3, waiting for transfers between devices, send_row(): there.append((lax.ppermute(data, 'expert', pairs), origin))  14.4 us
    ppermute x3, waiting for transfers between devices, topo_reduce_scatter(): lax.ppermute((ahead + ahead_part).astype(jnp.bfloat16), 'expert', [(j, j...  7.31 us
    ppermute x5, starting transfers between devices, row_sum(): got = lax.ppermute(theirs.astype(jnp.bfloat16), 'expert', pairs)  7.23 us
    ppermute x3, starting transfers between devices, topo_all_gather(): lax.ppermute(ahead, 'expert', [(j, j + 4) for j in range(experts) if step...  6.93 us
    ppermute x5, waiting for transfers between devices, row_sum(): got = lax.ppermute(theirs.astype(jnp.bfloat16), 'expert', pairs)  5.18 us
    ppermute x3, waiting for transfers between devices, topo_reduce_scatter(): lax.ppermute((behind + behind_part).astype(jnp.bfloat16), 'expert', [(j,...  4.41 us
  transfers between devices with their start and end apart: 24, of which 11 were waited for; matrix products, arithmetic and copies ran while one was open for 11% of the time, Pallas kernels for 0%

profile of v15, /device:TPU:0, one launch (start us, length us, event | category | flops | bytes accessed | tf_op | source)
XLA Modules:
  0.0 121.1 jit_solution(2568164515082935579)
XLA Ops:
  1.4 1.5 %fusion.14 = f32[32,4096]{1,0:T(8,128)S(1)} fusion(bf16[128,2048]{1,0:T(8,128)(2,1)} %param.11, bf16[128,2048]{1,0:T(8,128)(2,1)} %param.10, s32[128]{0:T(128)} %param.12), kind=kOutput, calls=%fused_computation.26 | convolution fusion | flops 35655680 | bytes 1573376 | tf_op jit(solution)/shard_map/dot_general | solution.py:234
  3.2 1.3 %collective-permute-start = (bf16[32,4224]{1,0:T(8,128)(2,1)S(1)}, bf16[32,4224]{1,0:T(8,128)(2,1)S(1)}, u32[]{:S(2)}, u32[]{:S(2)}) collective-permute-start(bf16[32,4224]{1,0:T(8,128)(2,1)S(1)} %fusion.47), channel_id=1, source_target_pairs={{4,0},{5,1},{6,2},{7,3},{8,4},{9,5},{10,6},{11,7},{12,8},{13,9},{1... | collective-permute-start | bytes 811016 | tf_op jit(solution)/shard_map/ppermute | solution.py:139
  4.5 5.6 %collective-permute-start.3 = (bf16[32,4224]{1,0:T(8,128)(2,1)S(1)}, bf16[32,4224]{1,0:T(8,128)(2,1)S(1)}, u32[]{:S(2)}, u32[]{:S(2)}) collective-permute-start(bf16[32,4224]{1,0:T(8,128)(2,1)S(1)} %fusion.47), channel_id=1, source_target_pairs={{0,4},{1,5},{2,6},{3,7},{4,8},{5,9},{6,10},{7,11},{8,12},{9,13},{1... | collective-permute-start | bytes 811016 | tf_op jit(solution)/shard_map/ppermute | solution.py:134
  10.1 4.5 %collective-permute-done = bf16[32,4224]{1,0:T(8,128)(2,1)S(1)} collective-permute-done((bf16[32,4224]{1,0:T(8,128)(2,1)S(1)}, bf16[32,4224]{1,0:T(8,128)(2,1)S(1)}, u32[]{:S(2)}, u32[]{:S(2)}) %collective-permute-start) | collective-permute-done | bytes 270368 | tf_op jit(solution)/shard_map/ppermute | solution.py:139
  14.6 1.3 %collective-permute-start.1 = (bf16[32,4224]{1,0:T(8,128)(2,1)S(1)}, bf16[32,4224]{1,0:T(8,128)(2,1)S(1)}, u32[]{:S(2)}, u32[]{:S(2)}) collective-permute-start(bf16[32,4224]{1,0:T(8,128)(2,1)S(1)} %collective-permute-done), channel_id=1, source_target_pairs={{4,0},{5,1},{6,2},{7,3},{8,4},{9,5},{10,6},{11,7},{20,16},{21,17},... | collective-permute-start | bytes 811016 | tf_op jit(solution)/shard_map/ppermute | solution.py:139
  16.6 1.7 %collective-permute-start.9 = (bf16[32,4224]{1,0:T(8,128)(2,1)S(1)}, bf16[32,4224]{1,0:T(8,128)(2,1)S(1)}, u32[]{:S(2)}, u32[]{:S(2)}) collective-permute-start(bf16[32,4224]{1,0:T(8,128)(2,1)S(1)} %fusion.47), channel_id=1, source_target_pairs={{0,2},{1,3},{2,0},{3,1},{4,6},{5,7},{6,4},{7,5},{8,10},{9,11},{10,... | collective-permute-start | bytes 811016 | tf_op jit(solution)/shard_map/ppermute | solution.py:121
  18.4 5.8 %collective-permute-done.1 = bf16[32,4224]{1,0:T(8,128)(2,1)S(1)} collective-permute-done((bf16[32,4224]{1,0:T(8,128)(2,1)S(1)}, bf16[32,4224]{1,0:T(8,128)(2,1)S(1)}, u32[]{:S(2)}, u32[]{:S(2)}) %collective-permute-start.1) | collective-permute-done | bytes 270368 | tf_op jit(solution)/shard_map/ppermute | solution.py:139
  24.2 1.3 %collective-permute-start.2 = (bf16[32,4224]{1,0:T(8,128)(2,1)S(1)}, bf16[32,4224]{1,0:T(8,128)(2,1)S(1)}, u32[]{:S(2)}, u32[]{:S(2)}) collective-permute-start(bf16[32,4224]{1,0:T(8,128)(2,1)S(1)} %collective-permute-done.1), channel_id=1, source_target_pairs={{4,0},{5,1},{6,2},{7,3},{20,16},{21,17},{22,18},{23,19}} | collective-permute-start | bytes 811016 | tf_op jit(solution)/shard_map/ppermute | solution.py:139
  26.2 6.6 %collective-permute-done.2 = bf16[32,4224]{1,0:T(8,128)(2,1)S(1)} collective-permute-done((bf16[32,4224]{1,0:T(8,128)(2,1)S(1)}, bf16[32,4224]{1,0:T(8,128)(2,1)S(1)}, u32[]{:S(2)}, u32[]{:S(2)}) %collective-permute-start.2) | collective-permute-done | bytes 270368 | tf_op jit(solution)/shard_map/ppermute | solution.py:139
  37.0 6.4 %collective-permute-done.6 = bf16[32,4224]{1,0:T(8,128)(2,1)S(1)} collective-permute-done((bf16[32,4224]{1,0:T(8,128)(2,1)}, bf16[32,4224]{1,0:T(8,128)(2,1)S(1)}, u32[]{:S(2)}, u32[]{:S(2)}) %collective-permute-start.6) | collective-permute-done | bytes 270368 | tf_op jit(solution)/shard_map/ppermute | solution.py:131
  43.4 5.1 %collective-permute-done.7 = bf16[32,4224]{1,0:T(8,128)(2,1)S(1)} collective-permute-done((bf16[32,4224]{1,0:T(8,128)(2,1)}, bf16[32,4224]{1,0:T(8,128)(2,1)S(1)}, u32[]{:S(2)}, u32[]{:S(2)}) %collective-permute-start.7) | collective-permute-done | bytes 270368 | tf_op jit(solution)/shard_map/ppermute | solution.py:131
  48.5 2.9 %collective-permute-done.8 = bf16[32,4224]{1,0:T(8,128)(2,1)S(1)} collective-permute-done((bf16[32,4224]{1,0:T(8,128)(2,1)}, bf16[32,4224]{1,0:T(8,128)(2,1)S(1)}, u32[]{:S(2)}, u32[]{:S(2)}) %collective-permute-start.8) | collective-permute-done | bytes 270368 | tf_op jit(solution)/shard_map/ppermute | solution.py:131
  53.6 1.4 %copy-done = bf16[1,2048,768]{2,1,0:T(8,128)(2,1)S(1)} copy-done((bf16[1,2048,768]{2,1,0:T(8,128)(2,1)S(1)}, bf16[1,2048,768]{2,1,0:T(8,128)(2,1)}, u32[]{:S(2)}) %copy-start) | copy-done | bytes 3145752
  60.9 1.1 fusion.38
  62.0 1.1 fusion.6
  63.1 2.9 %fusion.22 = f32[256,768]{1,0:T(8,128)S(1)} fusion(bf16[2048,768]{1,0:T(8,128)(2,1)} %collective-permute-done.11, bf16[256,4224]{1,0:T(8,128)(2,1)S(1)} %bitcast.68), kind=kOutput, calls=%fused_computation.44 | convolution fusion | flops 805306368 | bytes 4980736 | tf_op jit(solution)/shard_map/dot_general | solution.py:209
  68.1 2.9 %fusion.39 = f32[256,2048]{1,0:T(8,128)S(1)} fusion(bf16[2048,768]{1,0:T(8,128)(2,1)} %collective-permute-done.11, f32[256,768]{1,0:T(8,128)S(1)} %fusion.18, f32[256,768]{1,0:T(8,128)S(1)} %fusion.24), kind=kOutput, calls=%fused_computation.75 | convolution fusion | flops 806486016 | bytes 6815744 | tf_op jit(solution)/shard_map/dot_general | solution.py:219
  71.0 1.1 fusion.9
  72.1 1.2 %fusion.4 = f32[256,2048]{1,0:T(8,128)S(1)} fusion(f32[256,2048]{1,0:T(8,128)S(1)} %fusion.6, f32[256,2048]{1,0:T(8,128)S(1)} %fusion.39, bf16[2048,768]{1,0:T(8,128)(2,1)S(1)} %collective-permute-done.10, f32[256]{0:T(256)S(1)} %get-tuple-element.3, f32[256,768]{1,0:T(8,128)S(1)} %fusion.24, f32[256,768]{1,0:T(8,128)S(1)} %fusion.18, f32[256,768]{1,0:T(8,128)S(1)} %fusion.22), kind=kOutput, calls=%fused_computation.9 | convolution fusion | flops 809893888 | bytes 11797504 | tf_op jit(solution)/shard_map/dot_general | solution.py:218
  74.3 2.5 %collective-permute-start.14 = (bf16[32,4096]{1,0:T(8,128)(2,1)S(1)}, bf16[32,4096]{1,0:T(8,128)(2,1)S(1)}, u32[]{:S(2)}, u32[]{:S(2)}) collective-permute-start(bf16[32,4096]{1,0:T(8,128)(2,1)S(1)} %get-tuple-element.17), channel_id=1, source_target_pairs={{0,2},{1,3},{2,0},{3,1},{12,14},{13,15},{14,12},{15,13},{16,18},{1... | collective-permute-start | bytes 786440 | tf_op jit(solution)/shard_map/ppermute | solution.py:177
  77.0 1.5 %collective-permute-start.16 = (bf16[32,4096]{1,0:T(8,128)(2,1)S(1)}, bf16[32,4096]{1,0:T(8,128)(2,1)S(1)}, u32[]{:S(2)}, u32[]{:S(2)}) collective-permute-start(bf16[32,4096]{1,0:T(8,128)(2,1)S(1)} %get-tuple-element.16), channel_id=1, source_target_pairs={{0,2},{1,3},{2,0},{3,1},{4,6},{5,7},{6,4},{7,5},{8,10},{9,11},{10,... | collective-permute-start | bytes 786440 | tf_op jit(solution)/shard_map/ppermute | solution.py:177
  78.5 5.2 %collective-permute-done.14 = bf16[32,4096]{1,0:T(8,128)(2,1)S(1)} collective-permute-done((bf16[32,4096]{1,0:T(8,128)(2,1)S(1)}, bf16[32,4096]{1,0:T(8,128)(2,1)S(1)}, u32[]{:S(2)}, u32[]{:S(2)}) %collective-permute-start.14) | collective-permute-done | bytes 262176 | tf_op jit(solution)/shard_map/ppermute | solution.py:177
  83.8 1.3 %collective-permute-start.15 = (bf16[32,4096]{1,0:T(8,128)(2,1)S(1)}, bf16[32,4096]{1,0:T(8,128)(2,1)S(1)}, u32[]{:S(2)}, u32[]{:S(2)}) collective-permute-start(bf16[32,4096]{1,0:T(8,128)(2,1)S(1)} %fusion.35), channel_id=1, source_target_pairs={{0,4},{1,5},{2,6},{3,7},{16,20},{17,21},{18,22},{19,23}} | collective-permute-start | bytes 786440 | tf_op jit(solution)/shard_map/ppermute | solution.py:193
  85.8 2.2 %collective-permute-start.18 = (bf16[32,4096]{1,0:T(8,128)(2,1)S(1)}, bf16[32,4096]{1,0:T(8,128)(2,1)S(1)}, u32[]{:S(2)}, u32[]{:S(2)}) collective-permute-start(bf16[32,4096]{1,0:T(8,128)(2,1)S(1)} %get-tuple-element.15), channel_id=1, source_target_pairs={{0,2},{1,3},{2,0},{3,1},{4,6},{5,7},{6,4},{7,5},{8,10},{9,11},{10,... | collective-permute-start | bytes 786440 | tf_op jit(solution)/shard_map/ppermute | solution.py:177
  88.7 2.0 %collective-permute-done.15 = bf16[32,4096]{1,0:T(8,128)(2,1)S(1)} collective-permute-done((bf16[32,4096]{1,0:T(8,128)(2,1)S(1)}, bf16[32,4096]{1,0:T(8,128)(2,1)S(1)}, u32[]{:S(2)}, u32[]{:S(2)}) %collective-permute-start.15) | collective-permute-done | bytes 262176 | tf_op jit(solution)/shard_map/ppermute | solution.py:193
  90.8 4.4 %collective-permute-start.17 = (bf16[32,4096]{1,0:T(8,128)(2,1)S(1)}, bf16[32,4096]{1,0:T(8,128)(2,1)S(1)}, u32[]{:S(2)}, u32[]{:S(2)}) collective-permute-start(bf16[32,4096]{1,0:T(8,128)(2,1)S(1)} %get-tuple-element.7), channel_id=1, source_target_pairs={{0,4},{1,5},{2,6},{3,7},{4,8},{5,9},{6,10},{7,11},{16,20},{17,21},... | collective-permute-start | bytes 786440 | tf_op jit(solution)/shard_map/ppermute | solution.py:193
  96.3 2.8 %collective-permute-done.17 = bf16[32,4096]{1,0:T(8,128)(2,1)S(1)} collective-permute-done((bf16[32,4096]{1,0:T(8,128)(2,1)S(1)}, bf16[32,4096]{1,0:T(8,128)(2,1)S(1)}, u32[]{:S(2)}, u32[]{:S(2)}) %collective-permute-start.17) | collective-permute-done | bytes 262176 | tf_op jit(solution)/shard_map/ppermute | solution.py:193
  99.3 9.5 %collective-permute-start.19 = (bf16[32,4096]{1,0:T(8,128)(2,1)S(1)}, bf16[32,4096]{1,0:T(8,128)(2,1)S(1)}, u32[]{:S(2)}, u32[]{:S(2)}) collective-permute-start(bf16[32,4096]{1,0:T(8,128)(2,1)S(1)} %get-tuple-element.9), channel_id=1, source_target_pairs={{0,4},{1,5},{2,6},{3,7},{4,8},{5,9},{6,10},{7,11},{8,12},{9,13},{1... | collective-permute-start | bytes 786440 | tf_op jit(solution)/shard_map/ppermute | solution.py:193
  108.8 1.3 %collective-permute-start.23 = (bf16[32,4096]{1,0:T(8,128)(2,1)S(1)}, bf16[32,4096]{1,0:T(8,128)(2,1)S(1)}, u32[]{:S(2)}, u32[]{:S(2)}) collective-permute-start(bf16[32,4096]{1,0:T(8,128)(2,1)S(1)} %get-tuple-element.10), channel_id=1, source_target_pairs={{4,0},{5,1},{6,2},{7,3},{8,4},{9,5},{10,6},{11,7},{12,8},{13,9},{1... | collective-permute-start | bytes 786440 | tf_op jit(solution)/shard_map/ppermute | solution.py:198
  110.1 2.5 %collective-permute-done.19 = bf16[32,4096]{1,0:T(8,128)(2,1)S(1)} collective-permute-done((bf16[32,4096]{1,0:T(8,128)(2,1)S(1)}, bf16[32,4096]{1,0:T(8,128)(2,1)S(1)}, u32[]{:S(2)}, u32[]{:S(2)}) %collective-permute-start.19) | collective-permute-done | bytes 262176 | tf_op jit(solution)/shard_map/ppermute | solution.py:193
  112.6 4.4 %collective-permute-done.23 = bf16[32,4096]{1,0:T(8,128)(2,1)S(1)} collective-permute-done((bf16[32,4096]{1,0:T(8,128)(2,1)S(1)}, bf16[32,4096]{1,0:T(8,128)(2,1)S(1)}, u32[]{:S(2)}, u32[]{:S(2)}) %collective-permute-start.23) | collective-permute-done | bytes 262176 | tf_op jit(solution)/shard_map/ppermute | solution.py:198
  119.5 1.7 %select_add_fusion = (f32[128,2048]{1,0:T(8,128)}, f32[128,2048]{1,0:T(8,128)}) fusion(f32[128,2048]{1,0:T(8,128)S(1)} %gather_fusion.1, bf16[128,2048]{1,0:T(8,128)(2,1)S(1)} %copy-done.1, pred[128]{0:T(512)(128)(4,1)S(1)} %compare_and_fusion, f32[128,2048]{1,0:T(8,128)S(1)} %gather_fusion, bf16[128,2048]{1,0:T(8,128)(2,1)S(1)} %copy-done.2), kind=kLoop, calls=%fused_computation.30 | loop fusion | flops 1572864 | bytes 5243008 | tf_op jit(solution)/shard_map/add | solution.py:279
  (80 shorter events, 23.0 us)
Async XLA Ops:
  0.6 2.4 %copy-start.4 = (s32[32,8]{0,1:T(8,128)S(1)}, s32[32,8]{0,1:T(8,128)}, u32[]{:S(2)}) copy-start(s32[32,8]{0,1:T(8,128)} %param.13) | copy-start | bytes 3076
  0.6 2.4 %copy-start.3 = (f32[32,8]{0,1:T(8,128)S(1)}, f32[32,8]{0,1:T(8,128)}, u32[]{:S(2)}) copy-start(f32[32,8]{0,1:T(8,128)} %param.14) | copy-start | bytes 3076
  3.2 11.4 %collective-permute-start = (bf16[32,4224]{1,0:T(8,128)(2,1)S(1)}, bf16[32,4224]{1,0:T(8,128)(2,1)S(1)}, u32[]{:S(2)}, u32[]{:S(2)}) collective-permute-start(bf16[32,4224]{1,0:T(8,128)(2,1)S(1)} %fusion.47), channel_id=1, source_target_pairs={{4,0},{5,1},{6,2},{7,3},{8,4},{9,5},{10,6},{11,7},{12,8},{13,9},{1... | collective-permute-start | bytes 811016 | tf_op jit(solution)/shard_map/ppermute | solution.py:139
  4.5 11.4 %collective-permute-start.3 = (bf16[32,4224]{1,0:T(8,128)(2,1)S(1)}, bf16[32,4224]{1,0:T(8,128)(2,1)S(1)}, u32[]{:S(2)}, u32[]{:S(2)}) collective-permute-start(bf16[32,4224]{1,0:T(8,128)(2,1)S(1)} %fusion.47), channel_id=1, source_target_pairs={{0,4},{1,5},{2,6},{3,7},{4,8},{5,9},{6,10},{7,11},{8,12},{9,13},{1... | collective-permute-start | bytes 811016 | tf_op jit(solution)/shard_map/ppermute | solution.py:134
  14.6 9.5 %collective-permute-start.1 = (bf16[32,4224]{1,0:T(8,128)(2,1)S(1)}, bf16[32,4224]{1,0:T(8,128)(2,1)S(1)}, u32[]{:S(2)}, u32[]{:S(2)}) collective-permute-start(bf16[32,4224]{1,0:T(8,128)(2,1)S(1)} %collective-permute-done), channel_id=1, source_target_pairs={{4,0},{5,1},{6,2},{7,3},{8,4},{9,5},{10,6},{11,7},{20,16},{21,17},... | collective-permute-start | bytes 811016 | tf_op jit(solution)/shard_map/ppermute | solution.py:139
  15.9 9.5 %collective-permute-start.4 = (bf16[32,4224]{1,0:T(8,128)(2,1)S(1)}, bf16[32,4224]{1,0:T(8,128)(2,1)S(1)}, u32[]{:S(2)}, u32[]{:S(2)}) collective-permute-start(bf16[32,4224]{1,0:T(8,128)(2,1)S(1)} %collective-permute-done.3), channel_id=1, source_target_pairs={{4,8},{5,9},{6,10},{7,11},{8,12},{9,13},{10,14},{11,15},{20,24},{2... | collective-permute-start | bytes 811016 | tf_op jit(solution)/shard_map/ppermute | solution.py:134
  16.6 20.3 %collective-permute-start.9 = (bf16[32,4224]{1,0:T(8,128)(2,1)S(1)}, bf16[32,4224]{1,0:T(8,128)(2,1)S(1)}, u32[]{:S(2)}, u32[]{:S(2)}) collective-permute-start(bf16[32,4224]{1,0:T(8,128)(2,1)S(1)} %fusion.47), channel_id=1, source_target_pairs={{0,2},{1,3},{2,0},{3,1},{4,6},{5,7},{6,4},{7,5},{8,10},{9,11},{10,... | collective-permute-start | bytes 811016 | tf_op jit(solution)/shard_map/ppermute | solution.py:121
  18.4 44.8 %collective-permute-start.11 = (bf16[2048,768]{1,0:T(8,128)(2,1)}, bf16[2048,768]{1,0:T(8,128)(2,1)}, u32[]{:S(2)}, u32[]{:S(2)}) collective-permute-start(bf16[2048,768]{1,0:T(8,128)(2,1)} %bitcast.63), channel_id=1, source_target_pairs={{0,1},{1,0},{2,3},{3,2},{4,5},{5,4},{6,7},{7,6},{8,9},{9,8},{10,11... | collective-permute-start | bytes 9437192 | tf_op jit(solution)/shard_map/ppermute | solution.py:265
  24.2 8.6 %collective-permute-start.2 = (bf16[32,4224]{1,0:T(8,128)(2,1)S(1)}, bf16[32,4224]{1,0:T(8,128)(2,1)S(1)}, u32[]{:S(2)}, u32[]{:S(2)}) collective-permute-start(bf16[32,4224]{1,0:T(8,128)(2,1)S(1)} %collective-permute-done.1), channel_id=1, source_target_pairs={{4,0},{5,1},{6,2},{7,3},{20,16},{21,17},{22,18},{23,19}} | collective-permute-start | bytes 811016 | tf_op jit(solution)/shard_map/ppermute | solution.py:139
  25.5 7.3 %collective-permute-start.5 = (bf16[32,4224]{1,0:T(8,128)(2,1)S(1)}, bf16[32,4224]{1,0:T(8,128)(2,1)S(1)}, u32[]{:S(2)}, u32[]{:S(2)}) collective-permute-start(bf16[32,4224]{1,0:T(8,128)(2,1)S(1)} %collective-permute-done.4), channel_id=1, source_target_pairs={{8,12},{9,13},{10,14},{11,15},{24,28},{25,29},{26,30},{27,31}} | collective-permute-start | bytes 811016 | tf_op jit(solution)/shard_map/ppermute | solution.py:134
  33.8 9.6 %collective-permute-start.6 = (bf16[32,4224]{1,0:T(8,128)(2,1)}, bf16[32,4224]{1,0:T(8,128)(2,1)S(1)}, u32[]{:S(2)}, u32[]{:S(2)}) collective-permute-start(bf16[32,4224]{1,0:T(8,128)(2,1)} %get-tuple-element.18), channel_id=1, source_target_pairs={{0,2},{1,3},{2,0},{3,1},{4,6},{5,7},{6,4},{7,5},{8,10},{9,11},{10,... | collective-permute-start | bytes 811016 | tf_op jit(solution)/shard_map/ppermute | solution.py:131
  34.9 13.6 %collective-permute-start.7 = (bf16[32,4224]{1,0:T(8,128)(2,1)}, bf16[32,4224]{1,0:T(8,128)(2,1)S(1)}, u32[]{:S(2)}, u32[]{:S(2)}) collective-permute-start(bf16[32,4224]{1,0:T(8,128)(2,1)} %get-tuple-element.19), channel_id=1, source_target_pairs={{0,2},{1,3},{2,0},{3,1},{4,6},{5,7},{6,4},{7,5},{8,10},{9,11},{10,... | collective-permute-start | bytes 811016 | tf_op jit(solution)/shard_map/ppermute | solution.py:131
  35.8 15.6 %collective-permute-start.8 = (bf16[32,4224]{1,0:T(8,128)(2,1)}, bf16[32,4224]{1,0:T(8,128)(2,1)S(1)}, u32[]{:S(2)}, u32[]{:S(2)}) collective-permute-start(bf16[32,4224]{1,0:T(8,128)(2,1)} %get-tuple-element.20), channel_id=1, source_target_pairs={{0,2},{1,3},{2,0},{3,1},{4,6},{5,7},{6,4},{7,5},{8,10},{9,11},{10,... | collective-permute-start | bytes 811016 | tf_op jit(solution)/shard_map/ppermute | solution.py:131
  36.9 29.1 %collective-permute-start.10 = (bf16[2048,768]{1,0:T(8,128)(2,1)}, bf16[2048,768]{1,0:T(8,128)(2,1)S(1)}, u32[]{:S(2)}, u32[]{:S(2)}) collective-permute-start(bf16[2048,768]{1,0:T(8,128)(2,1)} %bitcast.71), channel_id=1, source_target_pairs={{0,1},{1,0},{2,3},{3,2},{4,5},{5,4},{6,7},{7,6},{8,9},{9,8},{10,11... | collective-permute-start | bytes 9437192 | tf_op jit(solution)/shard_map/ppermute | solution.py:264
  43.4 23.6 %collective-permute-start.12 = (bf16[768,2048]{1,0:T(8,128)(2,1)}, bf16[768,2048]{1,0:T(8,128)(2,1)S(1)}, u32[]{:S(2)}, u32[]{:S(2)}) collective-permute-start(bf16[768,2048]{1,0:T(8,128)(2,1)} %bitcast.72), channel_id=1, source_target_pairs={{0,1},{1,0},{2,3},{3,2},{4,5},{5,4},{6,7},{7,6},{8,9},{9,8},{10,11... | collective-permute-start | bytes 9437192 | tf_op jit(solution)/shard_map/ppermute | solution.py:266
  53.1 1.9 %copy-start = (bf16[1,2048,768]{2,1,0:T(8,128)(2,1)S(1)}, bf16[1,2048,768]{2,1,0:T(8,128)(2,1)}, u32[]{:S(2)}) copy-start(bf16[1,2048,768]{2,1,0:T(8,128)(2,1)} %param.16) | copy-start | bytes 9437188
  55.0 1.9 %copy-start.6 = (bf16[1,2048,768]{2,1,0:T(8,128)(2,1)S(1)}, bf16[1,2048,768]{2,1,0:T(8,128)(2,1)}, u32[]{:S(2)}) copy-start(bf16[1,2048,768]{2,1,0:T(8,128)(2,1)} %param.15) | copy-start | bytes 9437188
  56.9 1.9 %copy-start.7 = (bf16[1,768,2048]{2,1,0:T(8,128)(2,1)S(1)}, bf16[1,768,2048]{2,1,0:T(8,128)(2,1)}, u32[]{:S(2)}) copy-start(bf16[1,768,2048]{2,1,0:T(8,128)(2,1)} %param.17) | copy-start | bytes 9437188
  74.3 9.4 %collective-permute-start.14 = (bf16[32,4096]{1,0:T(8,128)(2,1)S(1)}, bf16[32,4096]{1,0:T(8,128)(2,1)S(1)}, u32[]{:S(2)}, u32[]{:S(2)}) collective-permute-start(bf16[32,4096]{1,0:T(8,128)(2,1)S(1)} %get-tuple-element.17), channel_id=1, source_target_pairs={{0,2},{1,3},{2,0},{3,1},{12,14},{13,15},{14,12},{15,13},{16,18},{1... | collective-permute-start | bytes 786440 | tf_op jit(solution)/shard_map/ppermute | solution.py:177
  77.0 18.9 %copy-start.5 = (s32[128]{0:T(128)S(1)}, s32[128]{0:T(128)}, u32[]{:S(2)}) copy-start(s32[128]{0:T(128)} %param.12) | copy-start | bytes 1540
  77.0 11.7 %collective-permute-start.16 = (bf16[32,4096]{1,0:T(8,128)(2,1)S(1)}, bf16[32,4096]{1,0:T(8,128)(2,1)S(1)}, u32[]{:S(2)}, u32[]{:S(2)}) collective-permute-start(bf16[32,4096]{1,0:T(8,128)(2,1)S(1)} %get-tuple-element.16), channel_id=1, source_target_pairs={{0,2},{1,3},{2,0},{3,1},{4,6},{5,7},{6,4},{7,5},{8,10},{9,11},{10,... | collective-permute-start | bytes 786440 | tf_op jit(solution)/shard_map/ppermute | solution.py:177
  83.8 6.9 %collective-permute-start.15 = (bf16[32,4096]{1,0:T(8,128)(2,1)S(1)}, bf16[32,4096]{1,0:T(8,128)(2,1)S(1)}, u32[]{:S(2)}, u32[]{:S(2)}) collective-permute-start(bf16[32,4096]{1,0:T(8,128)(2,1)S(1)} %fusion.35), channel_id=1, source_target_pairs={{0,4},{1,5},{2,6},{3,7},{16,20},{17,21},{18,22},{19,23}} | collective-permute-start | bytes 786440 | tf_op jit(solution)/shard_map/ppermute | solution.py:193
  85.1 5.6 %collective-permute-start.20 = (bf16[32,4096]{1,0:T(8,128)(2,1)S(1)}, bf16[32,4096]{1,0:T(8,128)(2,1)S(1)}, u32[]{:S(2)}, u32[]{:S(2)}) collective-permute-start(bf16[32,4096]{1,0:T(8,128)(2,1)S(1)} %fusion.35), channel_id=1, source_target_pairs={{12,8},{13,9},{14,10},{15,11},{28,24},{29,25},{30,26},{31,27}} | collective-permute-start | bytes 786440 | tf_op jit(solution)/shard_map/ppermute | solution.py:198
  85.8 10.5 %collective-permute-start.18 = (bf16[32,4096]{1,0:T(8,128)(2,1)S(1)}, bf16[32,4096]{1,0:T(8,128)(2,1)S(1)}, u32[]{:S(2)}, u32[]{:S(2)}) collective-permute-start(bf16[32,4096]{1,0:T(8,128)(2,1)S(1)} %get-tuple-element.15), channel_id=1, source_target_pairs={{0,2},{1,3},{2,0},{3,1},{4,6},{5,7},{6,4},{7,5},{8,10},{9,11},{10,... | collective-permute-start | bytes 786440 | tf_op jit(solution)/shard_map/ppermute | solution.py:177
  88.0 8.3 %collective-permute-start.22 = (bf16[32,4096]{1,0:T(8,128)(2,1)S(1)}, bf16[32,4096]{1,0:T(8,128)(2,1)S(1)}, u32[]{:S(2)}, u32[]{:S(2)}) collective-permute-start(bf16[32,4096]{1,0:T(8,128)(2,1)S(1)} %get-tuple-element.14), channel_id=1, source_target_pairs={{4,6},{5,7},{6,4},{7,5},{8,10},{9,11},{10,8},{11,9},{12,14},{13,15... | collective-permute-start | bytes 786440 | tf_op jit(solution)/shard_map/ppermute | solution.py:177
  90.8 8.3 %collective-permute-start.17 = (bf16[32,4096]{1,0:T(8,128)(2,1)S(1)}, bf16[32,4096]{1,0:T(8,128)(2,1)S(1)}, u32[]{:S(2)}, u32[]{:S(2)}) collective-permute-start(bf16[32,4096]{1,0:T(8,128)(2,1)S(1)} %get-tuple-element.7), channel_id=1, source_target_pairs={{0,4},{1,5},{2,6},{3,7},{4,8},{5,9},{6,10},{7,11},{16,20},{17,21},... | collective-permute-start | bytes 786440 | tf_op jit(solution)/shard_map/ppermute | solution.py:193
  95.2 3.9 %collective-permute-start.21 = (bf16[32,4096]{1,0:T(8,128)(2,1)S(1)}, bf16[32,4096]{1,0:T(8,128)(2,1)S(1)}, u32[]{:S(2)}, u32[]{:S(2)}) collective-permute-start(bf16[32,4096]{1,0:T(8,128)(2,1)S(1)} %get-tuple-element.8), channel_id=1, source_target_pairs={{8,4},{9,5},{10,6},{11,7},{12,8},{13,9},{14,10},{15,11},{24,20},{2... | collective-permute-start | bytes 786440 | tf_op jit(solution)/shard_map/ppermute | solution.py:198
  95.9 14.2 %collective-permute-start.13 = (bf16[32,4096]{1,0:T(8,128)(2,1)S(1)}, bf16[32,4096]{1,0:T(8,128)(2,1)S(1)}, u32[]{:S(2)}, u32[]{:S(2)}) collective-permute-start(bf16[32,4096]{1,0:T(8,128)(2,1)S(1)} %get-tuple-element.13), channel_id=1, source_target_pairs={{0,2},{1,3},{2,0},{3,1},{4,6},{5,7},{6,4},{7,5},{8,10},{9,11},{10,... | collective-permute-start | bytes 786440 | tf_op jit(solution)/shard_map/ppermute | solution.py:177
  99.3 13.3 %collective-permute-start.19 = (bf16[32,4096]{1,0:T(8,128)(2,1)S(1)}, bf16[32,4096]{1,0:T(8,128)(2,1)S(1)}, u32[]{:S(2)}, u32[]{:S(2)}) collective-permute-start(bf16[32,4096]{1,0:T(8,128)(2,1)S(1)} %get-tuple-element.9), channel_id=1, source_target_pairs={{0,4},{1,5},{2,6},{3,7},{4,8},{5,9},{6,10},{7,11},{8,12},{9,13},{1... | collective-permute-start | bytes 786440 | tf_op jit(solution)/shard_map/ppermute | solution.py:193
  108.8 8.3 %collective-permute-start.23 = (bf16[32,4096]{1,0:T(8,128)(2,1)S(1)}, bf16[32,4096]{1,0:T(8,128)(2,1)S(1)}, u32[]{:S(2)}, u32[]{:S(2)}) collective-permute-start(bf16[32,4096]{1,0:T(8,128)(2,1)S(1)} %get-tuple-element.10), channel_id=1, source_target_pairs={{4,0},{5,1},{6,2},{7,3},{8,4},{9,5},{10,6},{11,7},{12,8},{13,9},{1... | collective-permute-start | bytes 786440 | tf_op jit(solution)/shard_map/ppermute | solution.py:198
  118.3 1.0 copy-start.1
  118.3 1.2 copy-start.2

commit v16 on v13

--- a/solution.py
+++ b/solution.py
@@ -165,6 +165,8 @@
         got = lax.ppermute(theirs.astype(jnp.bfloat16), "expert", pairs)
         return mine + got.astype(jnp.float32)
 
+    if lines == 4:
+        return four_line_sum(keep, give, line, row_sum)
     ahead = jnp.zeros(keep.shape[1:], jnp.float32)
     behind = jnp.zeros(keep.shape[1:], jnp.float32)
     for step in range(1, lines):
@@ -191,6 +193,32 @@
     return row_sum(line, lambda z: True) + ahead + behind
 
 
+def four_line_sum(keep, give, line, row_sum):
+    experts = 16
+    end = (line == 0) | (line == 3)
+    first = row_sum(jnp.where(end, 3 - line, line), lambda z: True)
+    ahead = lax.ppermute(first.astype(jnp.bfloat16), "expert", [(j, j + 4) for j in range(4)])
+    behind = lax.ppermute(first.astype(jnp.bfloat16), "expert", [(j, j - 4) for j in range(12, 16)])
+    ahead, behind = ahead.astype(jnp.float32), behind.astype(jnp.float32)
+    second = row_sum(jnp.where(line <= 1, line + 2, line - 2), lambda z: True)
+    ahead = lax.ppermute(
+        (ahead + second).astype(jnp.bfloat16), "expert", [(j, j + 4) for j in range(8)]
+    ).astype(jnp.float32)
+    behind = lax.ppermute(
+        (behind + second).astype(jnp.bfloat16), "expert", [(j, j - 4) for j in range(8, 16)]
+    ).astype(jnp.float32)
+    third = row_sum(jnp.where(line <= 2, line + 1, line - 1), lambda z: True)
+    fourth = row_sum(jnp.where(end, line, line - 1), lambda z: True)
+    behind_part = jnp.where(line == 3, third, fourth)
+    ahead = lax.ppermute(
+        (ahead + third).astype(jnp.bfloat16), "expert", [(j, j + 4) for j in range(12)]
+    ).astype(jnp.float32)
+    behind = lax.ppermute(
+        (behind + behind_part).astype(jnp.bfloat16), "expert", [(j, j - 4) for j in range(4, 16)]
+    ).astype(jnp.float32)
+    return jnp.where(end, fourth, first) + ahead + behind
+
+
 def expert_dense(cent_in, grad_in, gate_mat, up_mat, down_mat):
     against = (((1,), (1,)), ((), ()))
     gate_act = jnp.dot(cent_in, gate_mat, preferred_element_type=jnp.float32)

time: 115 us -> 115 us (level)
  starting transfers between devices: 43.6 us -> 40.6 us
  waiting for transfers between devices: 39.6 us -> 42.2 us
    ppermute x5 -> x4, starting transfers between devices: 7.23 us -> 4.25 us  [row_sum(): got = lax.ppermute(theirs.astype(jnp.bfloat16), 'expert', pairs)]
    ppermute x5 -> x4, waiting for transfers between devices: 5.62 us -> 8.12 us  [row_sum(): got = lax.ppermute(theirs.astype(jnp.bfloat16), 'expert', pairs)]
  transfers between devices with their start and end apart: 25 -> 24, of which waited for: 10 -> 11; matrix products, arithmetic and copies ran while one was open for 13% -> 13% of each run, Pallas kernels for 0% -> 0%
where the time goes in v16:
time: 115 us; the launch traced here: 114 us
  waiting for transfers between devices  42.2 us (37%)
  starting transfers between devices  40.6 us (35%)
  matrix products  14.1 us (12%)
  other arithmetic  10.1 us (9%)
  local copies, waits for them, and re-layouts  5.6 us (5%)
  between operations  1.31 us (1%)
    ppermute x3, waiting for transfers between devices, topo_all_gather(): lax.ppermute(behind, 'expert', [(j, j - 4) for j in range(experts) if 1 <...  12.7 us
    ppermute x4, waiting for transfers between devices, row_sum(): got = lax.ppermute(theirs.astype(jnp.bfloat16), 'expert', pairs)  8.12 us
    ppermute x3, starting transfers between devices, topo_all_gather(): lax.ppermute(ahead, 'expert', [(j, j + 4) for j in range(experts) if step...  6.93 us
    ppermute x2, waiting for transfers between devices, topo_all_gather(): lax.ppermute(jnp.where(in_ahead, ahead, behind), 'expert', sorted(ahead_r...  6.9 us
    ppermute x1, starting transfers between devices, four_line_sum(): lax.ppermute((ahead + third).astype(jnp.bfloat16), 'expert', [(j, j + 4)...  6.33 us
    ppermute x1, waiting for transfers between devices, four_line_sum(): lax.ppermute((ahead + second).astype(jnp.bfloat16), 'expert', [(j, j + 4)...  5.15 us
    ppermute x1, waiting for transfers between devices, four_line_sum(): lax.ppermute((behind + behind_part).astype(jnp.bfloat16), 'expert', [(j,...  4.41 us
    ppermute x1, starting transfers between devices, four_line_sum(): lax.ppermute((ahead + second).astype(jnp.bfloat16), 'expert', [(j, j + 4)...  4.4 us
  transfers between devices with their start and end apart: 24, of which 11 were waited for; matrix products, arithmetic and copies ran while one was open for 13% of the time, Pallas kernels for 0%

profile of v16, /device:TPU:0, one launch (start us, length us, event | category | flops | bytes accessed | tf_op | source)
XLA Modules:
  0.0 113.9 jit_solution(4954853460605595661)
XLA Ops:
  1.4 1.5 %fusion.12 = f32[32,4096]{1,0:T(8,128)S(1)} fusion(bf16[128,2048]{1,0:T(8,128)(2,1)} %param.11, bf16[128,2048]{1,0:T(8,128)(2,1)} %param.10, s32[128]{0:T(128)} %param.12), kind=kOutput, calls=%fused_computation.26 | convolution fusion | flops 35655680 | bytes 1573376 | tf_op jit(solution)/shard_map/dot_general | solution.py:250
  3.2 1.3 %collective-permute-start = (bf16[32,4224]{1,0:T(8,128)(2,1)S(1)}, bf16[32,4224]{1,0:T(8,128)(2,1)S(1)}, u32[]{:S(2)}, u32[]{:S(2)}) collective-permute-start(bf16[32,4224]{1,0:T(8,128)(2,1)S(1)} %fusion.38), channel_id=1, source_target_pairs={{4,0},{5,1},{6,2},{7,3},{8,4},{9,5},{10,6},{11,7},{12,8},{13,9},{1... | collective-permute-start | bytes 811016 | tf_op jit(solution)/shard_map/ppermute | solution.py:125
  4.5 5.6 %collective-permute-start.3 = (bf16[32,4224]{1,0:T(8,128)(2,1)S(1)}, bf16[32,4224]{1,0:T(8,128)(2,1)S(1)}, u32[]{:S(2)}, u32[]{:S(2)}) collective-permute-start(bf16[32,4224]{1,0:T(8,128)(2,1)S(1)} %fusion.38), channel_id=1, source_target_pairs={{0,4},{1,5},{2,6},{3,7},{4,8},{5,9},{6,10},{7,11},{8,12},{9,13},{1... | collective-permute-start | bytes 811016 | tf_op jit(solution)/shard_map/ppermute | solution.py:120
  10.1 2.0 %collective-permute-start.10 = (bf16[32,4224]{1,0:T(8,128)(2,1)S(1)}, bf16[32,4224]{1,0:T(8,128)(2,1)S(1)}, u32[]{:S(2)}, u32[]{:S(2)}) collective-permute-start(bf16[32,4224]{1,0:T(8,128)(2,1)S(1)} %fusion.38), channel_id=1, source_target_pairs={{0,2},{1,3},{2,0},{3,1},{4,6},{5,7},{6,4},{7,5},{8,10},{9,11},{10,... | collective-permute-start | bytes 811016 | tf_op jit(solution)/shard_map/ppermute | solution.py:117
  12.1 2.5 %collective-permute-done = bf16[32,4224]{1,0:T(8,128)(2,1)S(1)} collective-permute-done((bf16[32,4224]{1,0:T(8,128)(2,1)S(1)}, bf16[32,4224]{1,0:T(8,128)(2,1)S(1)}, u32[]{:S(2)}, u32[]{:S(2)}) %collective-permute-start) | collective-permute-done | bytes 270368 | tf_op jit(solution)/shard_map/ppermute | solution.py:125
  14.6 1.3 %collective-permute-start.1 = (bf16[32,4224]{1,0:T(8,128)(2,1)S(1)}, bf16[32,4224]{1,0:T(8,128)(2,1)S(1)}, u32[]{:S(2)}, u32[]{:S(2)}) collective-permute-start(bf16[32,4224]{1,0:T(8,128)(2,1)S(1)} %collective-permute-done), channel_id=1, source_target_pairs={{4,0},{5,1},{6,2},{7,3},{8,4},{9,5},{10,6},{11,7},{20,16},{21,17},... | collective-permute-start | bytes 811016 | tf_op jit(solution)/shard_map/ppermute | solution.py:125
  16.7 3.6 %collective-permute-start.8 = (bf16[32,4224]{1,0:T(8,128)(2,1)S(1)}, bf16[32,4224]{1,0:T(8,128)(2,1)S(1)}, u32[]{:S(2)}, u32[]{:S(2)}) collective-permute-start(bf16[32,4224]{1,0:T(8,128)(2,1)S(1)} %collective-permute-done), channel_id=1, source_target_pairs={{0,2},{1,3},{2,0},{3,1},{4,6},{5,7},{6,4},{7,5},{8,10},{9,11},{10,... | collective-permute-start | bytes 811016 | tf_op jit(solution)/shard_map/ppermute | solution.py:143
  20.9 3.2 %collective-permute-done.1 = bf16[32,4224]{1,0:T(8,128)(2,1)S(1)} collective-permute-done((bf16[32,4224]{1,0:T(8,128)(2,1)S(1)}, bf16[32,4224]{1,0:T(8,128)(2,1)S(1)}, u32[]{:S(2)}, u32[]{:S(2)}) %collective-permute-start.1) | collective-permute-done | bytes 270368 | tf_op jit(solution)/shard_map/ppermute | solution.py:125
  24.2 1.3 %collective-permute-start.2 = (bf16[32,4224]{1,0:T(8,128)(2,1)S(1)}, bf16[32,4224]{1,0:T(8,128)(2,1)S(1)}, u32[]{:S(2)}, u32[]{:S(2)}) collective-permute-start(bf16[32,4224]{1,0:T(8,128)(2,1)S(1)} %collective-permute-done.1), channel_id=1, source_target_pairs={{4,0},{5,1},{6,2},{7,3},{20,16},{21,17},{22,18},{23,19}} | collective-permute-start | bytes 811016 | tf_op jit(solution)/shard_map/ppermute | solution.py:125
  26.9 7.0 %collective-permute-done.2 = bf16[32,4224]{1,0:T(8,128)(2,1)S(1)} collective-permute-done((bf16[32,4224]{1,0:T(8,128)(2,1)S(1)}, bf16[32,4224]{1,0:T(8,128)(2,1)S(1)}, u32[]{:S(2)}, u32[]{:S(2)}) %collective-permute-start.2) | collective-permute-done | bytes 270368 | tf_op jit(solution)/shard_map/ppermute | solution.py:125
  33.9 1.5 %collective-permute-start.7 = (bf16[32,4224]{1,0:T(8,128)(2,1)}, bf16[32,4224]{1,0:T(8,128)(2,1)S(1)}, u32[]{:S(2)}, u32[]{:S(2)}) collective-permute-start(bf16[32,4224]{1,0:T(8,128)(2,1)} %broadcast_select_fusion.2), channel_id=1, source_target_pairs={{0,2},{1,3},{2,0},{3,1},{4,6},{5,7},{6,4},{7,5},{8,10},{9,11},{10,... | collective-permute-start | bytes 811016 | tf_op jit(solution)/shard_map/ppermute | solution.py:136
  36.2 2.4 %collective-permute-start.6 = (bf16[32,4224]{1,0:T(8,128)(2,1)}, bf16[32,4224]{1,0:T(8,128)(2,1)}, u32[]{:S(2)}, u32[]{:S(2)}) collective-permute-start(bf16[32,4224]{1,0:T(8,128)(2,1)} %broadcast_select_fusion.3), channel_id=1, source_target_pairs={{0,2},{1,3},{2,0},{3,1},{12,14},{13,15},{14,12},{15,13},{16,18},{1... | collective-permute-start | bytes 811016 | tf_op jit(solution)/shard_map/ppermute | solution.py:136
  39.4 3.9 %collective-permute-done.7 = bf16[32,4224]{1,0:T(8,128)(2,1)S(1)} collective-permute-done((bf16[32,4224]{1,0:T(8,128)(2,1)}, bf16[32,4224]{1,0:T(8,128)(2,1)S(1)}, u32[]{:S(2)}, u32[]{:S(2)}) %collective-permute-start.7) | collective-permute-done | bytes 270368 | tf_op jit(solution)/shard_map/ppermute | solution.py:136
  43.3 3.0 %collective-permute-done.6 = bf16[32,4224]{1,0:T(8,128)(2,1)} collective-permute-done((bf16[32,4224]{1,0:T(8,128)(2,1)}, bf16[32,4224]{1,0:T(8,128)(2,1)}, u32[]{:S(2)}, u32[]{:S(2)}) %collective-permute-start.6) | collective-permute-done | bytes 270368 | tf_op jit(solution)/shard_map/ppermute | solution.py:136
  46.3 1.9 %broadcast_select_fusion.1 = bf16[4,1,32,4224]{3,2,1,0:T(8,128)(2,1)S(1)} fusion(pred[]{:T(512)S(6)} %eq.171, bf16[32,4224]{1,0:T(8,128)(2,1)S(1)} %collective-permute-done.10, pred[4]{0:T(512)(128)(4,1)S(1)} %get-tuple-element.21, bf16[32,4224]{1,0:T(8,128)(2,1)S(1)} %collective-permute-done.9, pred[4]{0:T(512)(128)(4,1)S(1)} %get-tuple-element.22, ...), kind=kLoop, calls=%fused_computation.25 | loop fusion | flops 7028736 | bytes 4325413 | tf_op jit(solution)/shard_map/jit(_where)/select_n | solution.py:99
  48.2 1.9 %broadcast_select_fusion = bf16[4,1,32,4224]{3,2,1,0:T(8,128)(2,1)S(1)} fusion(pred[]{:T(512)S(6)} %eq.171, bf16[32,4224]{1,0:T(8,128)(2,1)S(1)} %collective-permute-done.10, pred[4]{0:T(512)(128)(4,1)S(1)} %get-tuple-element.21, bf16[32,4224]{1,0:T(8,128)(2,1)S(1)} %collective-permute-done.9, pred[4]{0:T(512)(128)(4,1)S(1)} %get-tuple-element.22, ...), kind=kLoop, calls=%fused_computation.24 | loop fusion | flops 7028736 | bytes 4325413 | tf_op jit(solution)/shard_map/jit(_where)/select_n | solution.py:99
  50.6 1.4 %copy-done = bf16[1,2048,768]{2,1,0:T(8,128)(2,1)S(1)} copy-done((bf16[1,2048,768]{2,1,0:T(8,128)(2,1)S(1)}, bf16[1,2048,768]{2,1,0:T(8,128)(2,1)}, u32[]{:S(2)}) %copy-start) | copy-done | bytes 3145752
  57.9 1.1 fusion.29
  65.3 1.2 %fusion.4 = f32[256,2048]{1,0:T(8,128)S(1)} fusion(f32[256,2048]{1,0:T(8,128)S(1)} %fusion.6, f32[256,2048]{1,0:T(8,128)S(1)} %fusion.30, bf16[2048,768]{1,0:T(8,128)(2,1)S(1)} %collective-permute-done.11, f32[256]{0:T(256)S(1)} %get-tuple-element.3, f32[256,768]{1,0:T(8,128)S(1)} %fusion.22, f32[256,768]{1,0:T(8,128)S(1)} %fusion.16, f32[256,768]{1,0:T(8,128)S(1)} %fusion.20), kind=kOutput, calls=%fused_computation.9 | convolution fusion | flops 809893888 | bytes 11797504 | tf_op jit(solution)/shard_map/dot_general | solution.py:234
  68.3 1.6 %collective-permute-start.17 = (bf16[32,4096]{1,0:T(8,128)(2,1)S(1)}, bf16[32,4096]{1,0:T(8,128)(2,1)S(1)}, u32[]{:S(2)}, u32[]{:S(2)}) collective-permute-start(bf16[32,4096]{1,0:T(8,128)(2,1)S(1)} %get-tuple-element.14), channel_id=1, source_target_pairs={{0,2},{1,3},{2,0},{3,1},{4,6},{5,7},{6,4},{7,5},{8,10},{9,11},{10,... | collective-permute-start | bytes 786440 | tf_op jit(solution)/shard_map/ppermute | solution.py:165
  69.9 6.6 %collective-permute-done.15 = bf16[32,4096]{1,0:T(8,128)(2,1)S(1)} collective-permute-done((bf16[32,4096]{1,0:T(8,128)(2,1)S(1)}, bf16[32,4096]{1,0:T(8,128)(2,1)S(1)}, u32[]{:S(2)}, u32[]{:S(2)}) %collective-permute-start.15) | collective-permute-done | bytes 262176 | tf_op jit(solution)/shard_map/ppermute | solution.py:165
  76.6 1.3 %collective-permute-start.16 = (bf16[32,4096]{1,0:T(8,128)(2,1)S(1)}, bf16[32,4096]{1,0:T(8,128)(2,1)S(1)}, u32[]{:S(2)}, u32[]{:S(2)}) collective-permute-start(bf16[32,4096]{1,0:T(8,128)(2,1)S(1)} %fusion.37), channel_id=1, source_target_pairs={{0,4},{1,5},{2,6},{3,7},{16,20},{17,21},{18,22},{19,23}} | collective-permute-start | bytes 786440 | tf_op jit(solution)/shard_map/ppermute | solution.py:200
  78.9 1.7 %collective-permute-start.19 = (bf16[32,4096]{1,0:T(8,128)(2,1)S(1)}, bf16[32,4096]{1,0:T(8,128)(2,1)S(1)}, u32[]{:S(2)}, u32[]{:S(2)}) collective-permute-start(bf16[32,4096]{1,0:T(8,128)(2,1)S(1)} %get-tuple-element.13), channel_id=1, source_target_pairs={{0,2},{1,3},{2,0},{3,1},{4,6},{5,7},{6,4},{7,5},{8,10},{9,11},{10,... | collective-permute-start | bytes 786440 | tf_op jit(solution)/shard_map/ppermute | solution.py:165
  80.7 1.5 %collective-permute-done.17 = bf16[32,4096]{1,0:T(8,128)(2,1)S(1)} collective-permute-done((bf16[32,4096]{1,0:T(8,128)(2,1)S(1)}, bf16[32,4096]{1,0:T(8,128)(2,1)S(1)}, u32[]{:S(2)}, u32[]{:S(2)}) %collective-permute-start.17) | collective-permute-done | bytes 262176 | tf_op jit(solution)/shard_map/ppermute | solution.py:165
  82.1 2.4 %collective-permute-done.16 = bf16[32,4096]{1,0:T(8,128)(2,1)S(1)} collective-permute-done((bf16[32,4096]{1,0:T(8,128)(2,1)S(1)}, bf16[32,4096]{1,0:T(8,128)(2,1)S(1)}, u32[]{:S(2)}, u32[]{:S(2)}) %collective-permute-start.16) | collective-permute-done | bytes 262176 | tf_op jit(solution)/shard_map/ppermute | solution.py:200
  84.6 4.4 %collective-permute-start.18 = (bf16[32,4096]{1,0:T(8,128)(2,1)S(1)}, bf16[32,4096]{1,0:T(8,128)(2,1)S(1)}, u32[]{:S(2)}, u32[]{:S(2)}) collective-permute-start(bf16[32,4096]{1,0:T(8,128)(2,1)S(1)} %get-tuple-element.9), channel_id=1, source_target_pairs={{0,4},{1,5},{2,6},{3,7},{4,8},{5,9},{6,10},{7,11},{16,20},{17,21},... | collective-permute-start | bytes 786440 | tf_op jit(solution)/shard_map/ppermute | solution.py:204
  89.8 5.2 %collective-permute-done.18 = bf16[32,4096]{1,0:T(8,128)(2,1)S(1)} collective-permute-done((bf16[32,4096]{1,0:T(8,128)(2,1)S(1)}, bf16[32,4096]{1,0:T(8,128)(2,1)S(1)}, u32[]{:S(2)}, u32[]{:S(2)}) %collective-permute-start.18) | collective-permute-done | bytes 262176 | tf_op jit(solution)/shard_map/ppermute | solution.py:204
  95.1 6.3 %collective-permute-start.20 = (bf16[32,4096]{1,0:T(8,128)(2,1)S(1)}, bf16[32,4096]{1,0:T(8,128)(2,1)S(1)}, u32[]{:S(2)}, u32[]{:S(2)}) collective-permute-start(bf16[32,4096]{1,0:T(8,128)(2,1)S(1)} %get-tuple-element.7), channel_id=1, source_target_pairs={{0,4},{1,5},{2,6},{3,7},{4,8},{5,9},{6,10},{7,11},{8,12},{9,13},{1... | collective-permute-start | bytes 786440 | tf_op jit(solution)/shard_map/ppermute | solution.py:213
  101.5 1.3 %collective-permute-start.23 = (bf16[32,4096]{1,0:T(8,128)(2,1)S(1)}, bf16[32,4096]{1,0:T(8,128)(2,1)S(1)}, u32[]{:S(2)}, u32[]{:S(2)}) collective-permute-start(bf16[32,4096]{1,0:T(8,128)(2,1)S(1)} %get-tuple-element.8), channel_id=1, source_target_pairs={{4,0},{5,1},{6,2},{7,3},{8,4},{9,5},{10,6},{11,7},{12,8},{13,9},{1... | collective-permute-start | bytes 786440 | tf_op jit(solution)/shard_map/ppermute | solution.py:216
  102.8 2.5 %collective-permute-done.20 = bf16[32,4096]{1,0:T(8,128)(2,1)S(1)} collective-permute-done((bf16[32,4096]{1,0:T(8,128)(2,1)S(1)}, bf16[32,4096]{1,0:T(8,128)(2,1)S(1)}, u32[]{:S(2)}, u32[]{:S(2)}) %collective-permute-start.20) | collective-permute-done | bytes 262176 | tf_op jit(solution)/shard_map/ppermute | solution.py:213
  105.3 4.4 %collective-permute-done.23 = bf16[32,4096]{1,0:T(8,128)(2,1)S(1)} collective-permute-done((bf16[32,4096]{1,0:T(8,128)(2,1)S(1)}, bf16[32,4096]{1,0:T(8,128)(2,1)S(1)}, u32[]{:S(2)}, u32[]{:S(2)}) %collective-permute-start.23) | collective-permute-done | bytes 262176 | tf_op jit(solution)/shard_map/ppermute | solution.py:216
  112.3 1.7 %select_add_fusion = (f32[128,2048]{1,0:T(8,128)}, f32[128,2048]{1,0:T(8,128)}) fusion(f32[128,2048]{1,0:T(8,128)S(1)} %gather_fusion.1, bf16[128,2048]{1,0:T(8,128)(2,1)S(1)} %copy-done.1, pred[128]{0:T(512)(128)(4,1)S(1)} %compare_and_fusion, f32[128,2048]{1,0:T(8,128)S(1)} %gather_fusion, bf16[128,2048]{1,0:T(8,128)(2,1)S(1)} %copy-done.2), kind=kLoop, calls=%fused_computation.30 | loop fusion | flops 1572864 | bytes 5243008 | tf_op jit(solution)/shard_map/add | solution.py:295
  (81 shorter events, 24.1 us)
Async XLA Ops:
  0.6 2.4 %copy-start.4 = (s32[32,8]{0,1:T(8,128)S(1)}, s32[32,8]{0,1:T(8,128)}, u32[]{:S(2)}) copy-start(s32[32,8]{0,1:T(8,128)} %param.13) | copy-start | bytes 3076
  0.6 2.4 %copy-start.3 = (f32[32,8]{0,1:T(8,128)S(1)}, f32[32,8]{0,1:T(8,128)}, u32[]{:S(2)}) copy-start(f32[32,8]{0,1:T(8,128)} %param.14) | copy-start | bytes 3076
  3.2 11.4 %collective-permute-start = (bf16[32,4224]{1,0:T(8,128)(2,1)S(1)}, bf16[32,4224]{1,0:T(8,128)(2,1)S(1)}, u32[]{:S(2)}, u32[]{:S(2)}) collective-permute-start(bf16[32,4224]{1,0:T(8,128)(2,1)S(1)} %fusion.38), channel_id=1, source_target_pairs={{4,0},{5,1},{6,2},{7,3},{8,4},{9,5},{10,6},{11,7},{12,8},{13,9},{1... | collective-permute-start | bytes 811016 | tf_op jit(solution)/shard_map/ppermute | solution.py:125
  4.5 11.4 %collective-permute-start.3 = (bf16[32,4224]{1,0:T(8,128)(2,1)S(1)}, bf16[32,4224]{1,0:T(8,128)(2,1)S(1)}, u32[]{:S(2)}, u32[]{:S(2)}) collective-permute-start(bf16[32,4224]{1,0:T(8,128)(2,1)S(1)} %fusion.38), channel_id=1, source_target_pairs={{0,4},{1,5},{2,6},{3,7},{4,8},{5,9},{6,10},{7,11},{8,12},{9,13},{1... | collective-permute-start | bytes 811016 | tf_op jit(solution)/shard_map/ppermute | solution.py:120
  10.1 28.6 %collective-permute-start.10 = (bf16[32,4224]{1,0:T(8,128)(2,1)S(1)}, bf16[32,4224]{1,0:T(8,128)(2,1)S(1)}, u32[]{:S(2)}, u32[]{:S(2)}) collective-permute-start(bf16[32,4224]{1,0:T(8,128)(2,1)S(1)} %fusion.38), channel_id=1, source_target_pairs={{0,2},{1,3},{2,0},{3,1},{4,6},{5,7},{6,4},{7,5},{8,10},{9,11},{10,... | collective-permute-start | bytes 811016 | tf_op jit(solution)/shard_map/ppermute | solution.py:117
  14.6 9.5 %collective-permute-start.1 = (bf16[32,4224]{1,0:T(8,128)(2,1)S(1)}, bf16[32,4224]{1,0:T(8,128)(2,1)S(1)}, u32[]{:S(2)}, u32[]{:S(2)}) collective-permute-start(bf16[32,4224]{1,0:T(8,128)(2,1)S(1)} %collective-permute-done), channel_id=1, source_target_pairs={{4,0},{5,1},{6,2},{7,3},{8,4},{9,5},{10,6},{11,7},{20,16},{21,17},... | collective-permute-start | bytes 811016 | tf_op jit(solution)/shard_map/ppermute | solution.py:125
  15.9 9.5 %collective-permute-start.4 = (bf16[32,4224]{1,0:T(8,128)(2,1)S(1)}, bf16[32,4224]{1,0:T(8,128)(2,1)S(1)}, u32[]{:S(2)}, u32[]{:S(2)}) collective-permute-start(bf16[32,4224]{1,0:T(8,128)(2,1)S(1)} %collective-permute-done.3), channel_id=1, source_target_pairs={{4,8},{5,9},{6,10},{7,11},{8,12},{9,13},{10,14},{11,15},{20,24},{2... | collective-permute-start | bytes 811016 | tf_op jit(solution)/shard_map/ppermute | solution.py:120
  16.7 22.2 %collective-permute-start.8 = (bf16[32,4224]{1,0:T(8,128)(2,1)S(1)}, bf16[32,4224]{1,0:T(8,128)(2,1)S(1)}, u32[]{:S(2)}, u32[]{:S(2)}) collective-permute-start(bf16[32,4224]{1,0:T(8,128)(2,1)S(1)} %collective-permute-done), channel_id=1, source_target_pairs={{0,2},{1,3},{2,0},{3,1},{4,6},{5,7},{6,4},{7,5},{8,10},{9,11},{10,... | collective-permute-start | bytes 811016 | tf_op jit(solution)/shard_map/ppermute | solution.py:143
  20.3 19.1 %collective-permute-start.9 = (bf16[32,4224]{1,0:T(8,128)(2,1)S(1)}, bf16[32,4224]{1,0:T(8,128)(2,1)S(1)}, u32[]{:S(2)}, u32[]{:S(2)}) collective-permute-start(bf16[32,4224]{1,0:T(8,128)(2,1)S(1)} %collective-permute-done.3), channel_id=1, source_target_pairs={{4,6},{5,7},{6,4},{7,5},{8,10},{9,11},{10,8},{11,9},{12,14},{13,15... | collective-permute-start | bytes 811016 | tf_op jit(solution)/shard_map/ppermute | solution.py:142
  24.2 9.8 %collective-permute-start.2 = (bf16[32,4224]{1,0:T(8,128)(2,1)S(1)}, bf16[32,4224]{1,0:T(8,128)(2,1)S(1)}, u32[]{:S(2)}, u32[]{:S(2)}) collective-permute-start(bf16[32,4224]{1,0:T(8,128)(2,1)S(1)} %collective-permute-done.1), channel_id=1, source_target_pairs={{4,0},{5,1},{6,2},{7,3},{20,16},{21,17},{22,18},{23,19}} | collective-permute-start | bytes 811016 | tf_op jit(solution)/shard_map/ppermute | solution.py:125
  25.5 10.0 %collective-permute-start.5 = (bf16[32,4224]{1,0:T(8,128)(2,1)S(1)}, bf16[32,4224]{1,0:T(8,128)(2,1)S(1)}, u32[]{:S(2)}, u32[]{:S(2)}) collective-permute-start(bf16[32,4224]{1,0:T(8,128)(2,1)S(1)} %collective-permute-done.4), channel_id=1, source_target_pairs={{8,12},{9,13},{10,14},{11,15},{24,28},{25,29},{26,30},{27,31}} | collective-permute-start | bytes 811016 | tf_op jit(solution)/shard_map/ppermute | solution.py:120
  33.9 9.4 %collective-permute-start.7 = (bf16[32,4224]{1,0:T(8,128)(2,1)}, bf16[32,4224]{1,0:T(8,128)(2,1)S(1)}, u32[]{:S(2)}, u32[]{:S(2)}) collective-permute-start(bf16[32,4224]{1,0:T(8,128)(2,1)} %broadcast_select_fusion.2), channel_id=1, source_target_pairs={{0,2},{1,3},{2,0},{3,1},{4,6},{5,7},{6,4},{7,5},{8,10},{9,11},{10,... | collective-permute-start | bytes 811016 | tf_op jit(solution)/shard_map/ppermute | solution.py:136
  36.2 10.1 %collective-permute-start.6 = (bf16[32,4224]{1,0:T(8,128)(2,1)}, bf16[32,4224]{1,0:T(8,128)(2,1)}, u32[]{:S(2)}, u32[]{:S(2)}) collective-permute-start(bf16[32,4224]{1,0:T(8,128)(2,1)} %broadcast_select_fusion.3), channel_id=1, source_target_pairs={{0,2},{1,3},{2,0},{3,1},{12,14},{13,15},{14,12},{15,13},{16,18},{1... | collective-permute-start | bytes 811016 | tf_op jit(solution)/shard_map/ppermute | solution.py:136
  38.8 21.3 %collective-permute-start.12 = (bf16[2048,768]{1,0:T(8,128)(2,1)}, bf16[2048,768]{1,0:T(8,128)(2,1)S(1)}, u32[]{:S(2)}, u32[]{:S(2)}) collective-permute-start(bf16[2048,768]{1,0:T(8,128)(2,1)} %bitcast.57), channel_id=1, source_target_pairs={{0,1},{1,0},{2,3},{3,2},{4,5},{5,4},{6,7},{7,6},{8,9},{9,8},{10,11... | collective-permute-start | bytes 9437192 | tf_op jit(solution)/shard_map/ppermute | solution.py:281
  38.8 22.2 %collective-permute-start.11 = (bf16[2048,768]{1,0:T(8,128)(2,1)}, bf16[2048,768]{1,0:T(8,128)(2,1)S(1)}, u32[]{:S(2)}, u32[]{:S(2)}) collective-permute-start(bf16[2048,768]{1,0:T(8,128)(2,1)} %bitcast.65), channel_id=1, source_target_pairs={{0,1},{1,0},{2,3},{3,2},{4,5},{5,4},{6,7},{7,6},{8,9},{9,8},{10,11... | collective-permute-start | bytes 9437192 | tf_op jit(solution)/shard_map/ppermute | solution.py:280
  39.3 22.8 %collective-permute-start.13 = (bf16[768,2048]{1,0:T(8,128)(2,1)}, bf16[768,2048]{1,0:T(8,128)(2,1)S(1)}, u32[]{:S(2)}, u32[]{:S(2)}) collective-permute-start(bf16[768,2048]{1,0:T(8,128)(2,1)} %bitcast.66), channel_id=1, source_target_pairs={{0,1},{1,0},{2,3},{3,2},{4,5},{5,4},{6,7},{7,6},{8,9},{9,8},{10,11... | collective-permute-start | bytes 9437192 | tf_op jit(solution)/shard_map/ppermute | solution.py:282
  50.1 1.9 %copy-start = (bf16[1,2048,768]{2,1,0:T(8,128)(2,1)S(1)}, bf16[1,2048,768]{2,1,0:T(8,128)(2,1)}, u32[]{:S(2)}) copy-start(bf16[1,2048,768]{2,1,0:T(8,128)(2,1)} %param.16) | copy-start | bytes 9437188
  52.0 1.9 %copy-start.6 = (bf16[1,2048,768]{2,1,0:T(8,128)(2,1)S(1)}, bf16[1,2048,768]{2,1,0:T(8,128)(2,1)}, u32[]{:S(2)}) copy-start(bf16[1,2048,768]{2,1,0:T(8,128)(2,1)} %param.15) | copy-start | bytes 9437188
  53.9 1.9 %copy-start.7 = (bf16[1,768,2048]{2,1,0:T(8,128)(2,1)S(1)}, bf16[1,768,2048]{2,1,0:T(8,128)(2,1)}, u32[]{:S(2)}) copy-start(bf16[1,768,2048]{2,1,0:T(8,128)(2,1)} %param.17) | copy-start | bytes 9437188
  67.5 9.0 %collective-permute-start.15 = (bf16[32,4096]{1,0:T(8,128)(2,1)S(1)}, bf16[32,4096]{1,0:T(8,128)(2,1)S(1)}, u32[]{:S(2)}, u32[]{:S(2)}) collective-permute-start(bf16[32,4096]{1,0:T(8,128)(2,1)S(1)} %get-tuple-element.15), channel_id=1, source_target_pairs={{0,2},{1,3},{2,0},{3,1},{4,6},{5,7},{6,4},{7,5},{8,10},{9,11},{10,... | collective-permute-start | bytes 786440 | tf_op jit(solution)/shard_map/ppermute | solution.py:165
  68.3 21.4 %copy-start.5 = (s32[128]{0:T(128)S(1)}, s32[128]{0:T(128)}, u32[]{:S(2)}) copy-start(s32[128]{0:T(128)} %param.12) | copy-start | bytes 1540
  68.3 13.8 %collective-permute-start.17 = (bf16[32,4096]{1,0:T(8,128)(2,1)S(1)}, bf16[32,4096]{1,0:T(8,128)(2,1)S(1)}, u32[]{:S(2)}, u32[]{:S(2)}) collective-permute-start(bf16[32,4096]{1,0:T(8,128)(2,1)S(1)} %get-tuple-element.14), channel_id=1, source_target_pairs={{0,2},{1,3},{2,0},{3,1},{4,6},{5,7},{6,4},{7,5},{8,10},{9,11},{10,... | collective-permute-start | bytes 786440 | tf_op jit(solution)/shard_map/ppermute | solution.py:165
  76.6 7.9 %collective-permute-start.16 = (bf16[32,4096]{1,0:T(8,128)(2,1)S(1)}, bf16[32,4096]{1,0:T(8,128)(2,1)S(1)}, u32[]{:S(2)}, u32[]{:S(2)}) collective-permute-start(bf16[32,4096]{1,0:T(8,128)(2,1)S(1)} %fusion.37), channel_id=1, source_target_pairs={{0,4},{1,5},{2,6},{3,7},{16,20},{17,21},{18,22},{19,23}} | collective-permute-start | bytes 786440 | tf_op jit(solution)/shard_map/ppermute | solution.py:200
  77.9 6.6 %collective-permute-start.21 = (bf16[32,4096]{1,0:T(8,128)(2,1)S(1)}, bf16[32,4096]{1,0:T(8,128)(2,1)S(1)}, u32[]{:S(2)}, u32[]{:S(2)}) collective-permute-start(bf16[32,4096]{1,0:T(8,128)(2,1)S(1)} %fusion.37), channel_id=1, source_target_pairs={{12,8},{13,9},{14,10},{15,11},{28,24},{29,25},{30,26},{31,27}} | collective-permute-start | bytes 786440 | tf_op jit(solution)/shard_map/ppermute | solution.py:201
  78.6 11.2 %collective-permute-start.14 = (bf16[32,4096]{1,0:T(8,128)(2,1)S(1)}, bf16[32,4096]{1,0:T(8,128)(2,1)S(1)}, u32[]{:S(2)}, u32[]{:S(2)}) collective-permute-start(bf16[32,4096]{1,0:T(8,128)(2,1)S(1)} %get-tuple-element.16), channel_id=1, source_target_pairs={{0,2},{1,3},{2,0},{3,1},{4,6},{5,7},{6,4},{7,5},{8,10},{9,11},{10,... | collective-permute-start | bytes 786440 | tf_op jit(solution)/shard_map/ppermute | solution.py:165
  78.9 10.9 %collective-permute-start.19 = (bf16[32,4096]{1,0:T(8,128)(2,1)S(1)}, bf16[32,4096]{1,0:T(8,128)(2,1)S(1)}, u32[]{:S(2)}, u32[]{:S(2)}) collective-permute-start(bf16[32,4096]{1,0:T(8,128)(2,1)S(1)} %get-tuple-element.13), channel_id=1, source_target_pairs={{0,2},{1,3},{2,0},{3,1},{4,6},{5,7},{6,4},{7,5},{8,10},{9,11},{10,... | collective-permute-start | bytes 786440 | tf_op jit(solution)/shard_map/ppermute | solution.py:165
  84.6 10.3 %collective-permute-start.18 = (bf16[32,4096]{1,0:T(8,128)(2,1)S(1)}, bf16[32,4096]{1,0:T(8,128)(2,1)S(1)}, u32[]{:S(2)}, u32[]{:S(2)}) collective-permute-start(bf16[32,4096]{1,0:T(8,128)(2,1)S(1)} %get-tuple-element.9), channel_id=1, source_target_pairs={{0,4},{1,5},{2,6},{3,7},{4,8},{5,9},{6,10},{7,11},{16,20},{17,21},... | collective-permute-start | bytes 786440 | tf_op jit(solution)/shard_map/ppermute | solution.py:204
  89.1 5.9 %collective-permute-start.22 = (bf16[32,4096]{1,0:T(8,128)(2,1)S(1)}, bf16[32,4096]{1,0:T(8,128)(2,1)S(1)}, u32[]{:S(2)}, u32[]{:S(2)}) collective-permute-start(bf16[32,4096]{1,0:T(8,128)(2,1)S(1)} %get-tuple-element.10), channel_id=1, source_target_pairs={{8,4},{9,5},{10,6},{11,7},{12,8},{13,9},{14,10},{15,11},{24,20},{2... | collective-permute-start | bytes 786440 | tf_op jit(solution)/shard_map/ppermute | solution.py:207
  95.1 10.2 %collective-permute-start.20 = (bf16[32,4096]{1,0:T(8,128)(2,1)S(1)}, bf16[32,4096]{1,0:T(8,128)(2,1)S(1)}, u32[]{:S(2)}, u32[]{:S(2)}) collective-permute-start(bf16[32,4096]{1,0:T(8,128)(2,1)S(1)} %get-tuple-element.7), channel_id=1, source_target_pairs={{0,4},{1,5},{2,6},{3,7},{4,8},{5,9},{6,10},{7,11},{8,12},{9,13},{1... | collective-permute-start | bytes 786440 | tf_op jit(solution)/shard_map/ppermute | solution.py:213
  101.5 8.3 %collective-permute-start.23 = (bf16[32,4096]{1,0:T(8,128)(2,1)S(1)}, bf16[32,4096]{1,0:T(8,128)(2,1)S(1)}, u32[]{:S(2)}, u32[]{:S(2)}) collective-permute-start(bf16[32,4096]{1,0:T(8,128)(2,1)S(1)} %get-tuple-element.8), channel_id=1, source_target_pairs={{4,0},{5,1},{6,2},{7,3},{8,4},{9,5},{10,6},{11,7},{12,8},{13,9},{1... | collective-permute-start | bytes 786440 | tf_op jit(solution)/shard_map/ppermute | solution.py:216
  111.0 1.0 copy-start.1
  111.1 1.2 %copy-start.2 = (bf16[128,2048]{1,0:T(8,128)(2,1)S(1)}, bf16[128,2048]{1,0:T(8,128)(2,1)}, u32[]{:S(2)}) copy-start(bf16[128,2048]{1,0:T(8,128)(2,1)} %param.10) | copy-start | bytes 1572868

commit v17 on v16

--- a/solution.py
+++ b/solution.py
@@ -114,6 +114,13 @@
     line = me // 4
     swap_row = [(j, j ^ 2) for j in range(experts)]
     here = [(shard, line)]
+    if lines == 4:
+        here, there = four_line_gather(shard, line, here, swap_row)
+        column = place(here, lines, shard)
+        across = place(there, lines, shard)
+        in_row = (me // 2) % 2
+        mine = jnp.stack([pick(in_row, [column, across]), pick(in_row, [across, column])], axis=1)
+        return mine.reshape((lines * 2 * shard.shape[0],) + shard.shape[1:])
     there = [(lax.ppermute(shard, "expert", swap_row), line)]
     ahead, behind = shard, shard
     for step in range(1, lines):
@@ -193,6 +200,28 @@
     return row_sum(line, lambda z: True) + ahead + behind
 
 
+def four_line_gather(shard, line, here, swap_row):
+    there = [(lax.ppermute(shard, "expert", swap_row), line)]
+    ahead = lax.ppermute(shard, "expert", [(j, j + 4) for j in range(12)])
+    behind = lax.ppermute(shard, "expert", [(j, j - 4) for j in range(4, 16)])
+    here = here + [(ahead, line - 1), (behind, line + 1)]
+    first_behind = behind
+    got = lax.ppermute(jnp.where(line == 0, behind, ahead), "expert", swap_row)
+    there.append((got, jnp.where(line == 0, line + 1, line - 1)))
+    ahead = lax.ppermute(ahead, "expert", [(j, j + 4) for j in range(4, 12)])
+    behind = lax.ppermute(behind, "expert", [(j, j - 4) for j in range(4, 12)])
+    here = here + [(ahead, line - 2), (behind, line + 2)]
+    got = lax.ppermute(jnp.where(line >= 2, ahead, behind), "expert", swap_row)
+    there.append((got, jnp.where(line >= 2, line - 2, line + 2)))
+    ahead = lax.ppermute(ahead, "expert", [(j, j + 4) for j in range(8, 12)])
+    behind = lax.ppermute(behind, "expert", [(j, j - 4) for j in range(4, 8)])
+    here = here + [(ahead, line - 3), (behind, line + 3)]
+    last = jnp.where(line == 3, ahead, jnp.where(line == 0, behind, first_behind))
+    got = lax.ppermute(last, "expert", swap_row)
+    there.append((got, jnp.where(line == 3, 0, jnp.where(line == 0, 3, line + 1))))
+    return here, there
+
+
 def four_line_sum(keep, give, line, row_sum):
     experts = 16
     end = (line == 0) | (line == 3)

time: 115 us -> 123 us (1.070)
  starting transfers between devices: 40.6 us -> 45.6 us
  matrix products: 14.1 us -> 17.9 us
  other arithmetic: 10.1 us -> 8.16 us
  waiting for transfers between devices: 42.2 us -> 43.6 us
    ppermute x1, starting transfers between devices: 6.33 us -> 11.6 us  [four_line_sum(): lax.ppermute((ahead + third).astype(jnp.bfloat16), 'expert', [(j, j + 4)...]
    ppermute x11 -> x10, starting transfers between devices: 21 us -> 16.2 us  [the longest x1 5.57 us: four_line_gather(): ahead = lax.ppermute(shard, 'expert', [(j, j + 4) for j in range(12)])]
    ppermute x1, starting transfers between devices: 1.31 us -> 5.94 us  [four_line_sum(): lax.ppermute(first.astype(jnp.bfloat16), 'expert', [(j, j + 4) for j in r...]
    ppermute x11 -> x10, waiting for transfers between devices: 19.7 us -> 23.7 us  [the longest x1 7.5 us: four_line_gather(): behind = lax.ppermute(behind, 'expert', [(j, j - 4) for j in range(4, 12)])]
    ppermute x4, waiting for transfers between devices: 8.12 us -> 5.2 us  [row_sum(): got = lax.ppermute(theirs.astype(jnp.bfloat16), 'expert', pairs)]
    select_n x4, other arithmetic: 4.35 us -> 2.13 us  [pick(): chosen = jnp.where(index == position, options[position], chosen)]
    dot_general x2, matrix products: 1.95 us -> 3.84 us  [expert_dense(): up_act = jnp.dot(cent_in, up_mat, preferred_element_type=jnp.float32)]
    dot_general x2, matrix products: 2.12 us -> 4 us  [expert_dense(): lax.dot_general(up_grad, up_mat, against, preferred_element_type=jnp.floa...]
  transfers between devices with their start and end apart: 24 -> 23, of which waited for: 11 -> 10; matrix products, arithmetic and copies ran while one was open for 13% -> 12% of each run, Pallas kernels for 0% -> 0%
where the time goes in v17:
time: 123 us; the launch traced here: 122 us
  starting transfers between devices  45.6 us (37%)
  waiting for transfers between devices  43.6 us (35%)
  matrix products  17.9 us (15%)
  other arithmetic  8.16 us (7%)
  local copies, waits for them, and re-layouts  5.6 us (5%)
    ppermute x1, starting transfers between devices, four_line_sum(): lax.ppermute((ahead + third).astype(jnp.bfloat16), 'expert', [(j, j + 4)...  11.6 us
    ppermute x1, waiting for transfers between devices, four_line_gather(): behind = lax.ppermute(behind, 'expert', [(j, j - 4) for j in range(4, 12)])  7.5 us
    ppermute x1, waiting for transfers between devices, four_line_gather(): got = lax.ppermute(last, 'expert', swap_row)  6.28 us
    ppermute x1, starting transfers between devices, four_line_sum(): lax.ppermute(first.astype(jnp.bfloat16), 'expert', [(j, j + 4) for j in r...  5.94 us
    ppermute x1, starting transfers between devices, four_line_gather(): ahead = lax.ppermute(shard, 'expert', [(j, j + 4) for j in range(12)])  5.57 us
    ppermute x4, waiting for transfers between devices, row_sum(): got = lax.ppermute(theirs.astype(jnp.bfloat16), 'expert', pairs)  5.2 us
    ppermute x1, waiting for transfers between devices, four_line_gather(): behind = lax.ppermute(behind, 'expert', [(j, j - 4) for j in range(4, 8)])  4.53 us
    ppermute x1, waiting for transfers between devices, four_line_sum(): lax.ppermute((behind + behind_part).astype(jnp.bfloat16), 'expert', [(j,...  4.41 us
  transfers between devices with their start and end apart: 23, of which 10 were waited for; matrix products, arithmetic and copies ran while one was open for 12% of the time, Pallas kernels for 0%

profile of v17, /device:TPU:0, one launch (start us, length us, event | category | flops | bytes accessed | tf_op | source)
XLA Modules:
  0.0 122.0 jit_solution(15212661848978445874)
XLA Ops:
  1.4 1.5 %fusion.14 = f32[32,4096]{1,0:T(8,128)S(1)} fusion(bf16[128,2048]{1,0:T(8,128)(2,1)} %param.11, bf16[128,2048]{1,0:T(8,128)(2,1)} %param.10, s32[128]{0:T(128)} %param.12), kind=kOutput, calls=%fused_computation.26 | convolution fusion | flops 35655680 | bytes 1573376 | tf_op jit(solution)/shard_map/dot_general | solution.py:279
  3.2 1.3 %collective-permute-start = (bf16[32,4224]{1,0:T(8,128)(2,1)S(1)}, bf16[32,4224]{1,0:T(8,128)(2,1)S(1)}, u32[]{:S(2)}, u32[]{:S(2)}) collective-permute-start(bf16[32,4224]{1,0:T(8,128)(2,1)S(1)} %fusion.40), channel_id=1, source_target_pairs={{4,0},{5,1},{6,2},{7,3},{8,4},{9,5},{10,6},{11,7},{12,8},{13,9},{1... | collective-permute-start | bytes 811016 | tf_op jit(solution)/shard_map/ppermute | solution.py:206
  4.5 5.6 %collective-permute-start.3 = (bf16[32,4224]{1,0:T(8,128)(2,1)S(1)}, bf16[32,4224]{1,0:T(8,128)(2,1)S(1)}, u32[]{:S(2)}, u32[]{:S(2)}) collective-permute-start(bf16[32,4224]{1,0:T(8,128)(2,1)S(1)} %fusion.40), channel_id=1, source_target_pairs={{0,4},{1,5},{2,6},{3,7},{4,8},{5,9},{6,10},{7,11},{8,12},{9,13},{1... | collective-permute-start | bytes 811016 | tf_op jit(solution)/shard_map/ppermute | solution.py:205
  10.1 2.0 %collective-permute-start.9 = (bf16[32,4224]{1,0:T(8,128)(2,1)S(1)}, bf16[32,4224]{1,0:T(8,128)(2,1)S(1)}, u32[]{:S(2)}, u32[]{:S(2)}) collective-permute-start(bf16[32,4224]{1,0:T(8,128)(2,1)S(1)} %fusion.40), channel_id=1, source_target_pairs={{0,2},{1,3},{2,0},{3,1},{4,6},{5,7},{6,4},{7,5},{8,10},{9,11},{10,... | collective-permute-start | bytes 811016 | tf_op jit(solution)/shard_map/ppermute | solution.py:204
  12.1 2.5 %collective-permute-done = bf16[32,4224]{1,0:T(8,128)(2,1)S(1)} collective-permute-done((bf16[32,4224]{1,0:T(8,128)(2,1)S(1)}, bf16[32,4224]{1,0:T(8,128)(2,1)S(1)}, u32[]{:S(2)}, u32[]{:S(2)}) %collective-permute-start) | collective-permute-done | bytes 270368 | tf_op jit(solution)/shard_map/ppermute | solution.py:206
  14.6 1.3 %collective-permute-start.1 = (bf16[32,4224]{1,0:T(8,128)(2,1)S(1)}, bf16[32,4224]{1,0:T(8,128)(2,1)S(1)}, u32[]{:S(2)}, u32[]{:S(2)}) collective-permute-start(bf16[32,4224]{1,0:T(8,128)(2,1)S(1)} %collective-permute-done), channel_id=1, source_target_pairs={{4,0},{5,1},{6,2},{7,3},{8,4},{9,5},{10,6},{11,7},{20,16},{21,17},... | collective-permute-start | bytes 811016 | tf_op jit(solution)/shard_map/ppermute | solution.py:212
  16.7 7.5 %collective-permute-done.1 = bf16[32,4224]{1,0:T(8,128)(2,1)S(1)} collective-permute-done((bf16[32,4224]{1,0:T(8,128)(2,1)S(1)}, bf16[32,4224]{1,0:T(8,128)(2,1)S(1)}, u32[]{:S(2)}, u32[]{:S(2)}) %collective-permute-start.1) | collective-permute-done | bytes 270368 | tf_op jit(solution)/shard_map/ppermute | solution.py:212
  24.2 1.3 %collective-permute-start.2 = (bf16[32,4224]{1,0:T(8,128)(2,1)S(1)}, bf16[32,4224]{1,0:T(8,128)(2,1)S(1)}, u32[]{:S(2)}, u32[]{:S(2)}) collective-permute-start(bf16[32,4224]{1,0:T(8,128)(2,1)S(1)} %collective-permute-done.1), channel_id=1, source_target_pairs={{4,0},{5,1},{6,2},{7,3},{20,16},{21,17},{22,18},{23,19}} | collective-permute-start | bytes 811016 | tf_op jit(solution)/shard_map/ppermute | solution.py:217
  26.9 1.4 %collective-permute-start.7 = (bf16[32,4224]{1,0:T(8,128)(2,1)}, bf16[32,4224]{1,0:T(8,128)(2,1)S(1)}, u32[]{:S(2)}, u32[]{:S(2)}) collective-permute-start(bf16[32,4224]{1,0:T(8,128)(2,1)} %broadcast_select_fusion), channel_id=1, source_target_pairs={{0,2},{1,3},{2,0},{3,1},{4,6},{5,7},{6,4},{7,5},{8,10},{9,11},{10,... | collective-permute-start | bytes 811016 | tf_op jit(solution)/shard_map/ppermute | solution.py:214
  28.3 4.5 %collective-permute-done.2 = bf16[32,4224]{1,0:T(8,128)(2,1)S(1)} collective-permute-done((bf16[32,4224]{1,0:T(8,128)(2,1)S(1)}, bf16[32,4224]{1,0:T(8,128)(2,1)S(1)}, u32[]{:S(2)}, u32[]{:S(2)}) %collective-permute-start.2) | collective-permute-done | bytes 270368 | tf_op jit(solution)/shard_map/ppermute | solution.py:217
  33.7 1.1 collective-permute-start.6
  36.3 6.3 %collective-permute-done.6 = bf16[32,4224]{1,0:T(8,128)(2,1)S(1)} collective-permute-done((bf16[32,4224]{1,0:T(8,128)(2,1)}, bf16[32,4224]{1,0:T(8,128)(2,1)S(1)}, u32[]{:S(2)}, u32[]{:S(2)}) %collective-permute-start.6) | collective-permute-done | bytes 270368 | tf_op jit(solution)/shard_map/ppermute | solution.py:220
  42.6 2.9 %collective-permute-done.8 = bf16[32,4224]{1,0:T(8,128)(2,1)S(1)} collective-permute-done((bf16[32,4224]{1,0:T(8,128)(2,1)}, bf16[32,4224]{1,0:T(8,128)(2,1)S(1)}, u32[]{:S(2)}, u32[]{:S(2)}) %collective-permute-start.8) | collective-permute-done | bytes 270368 | tf_op jit(solution)/shard_map/ppermute | solution.py:209
  47.7 1.4 %copy-done = bf16[1,2048,768]{2,1,0:T(8,128)(2,1)S(1)} copy-done((bf16[1,2048,768]{2,1,0:T(8,128)(2,1)S(1)}, bf16[1,2048,768]{2,1,0:T(8,128)(2,1)}, u32[]{:S(2)}) %copy-start) | copy-done | bytes 3145752
  55.0 1.1 fusion.31
  56.1 1.1 fusion.6
  57.3 2.9 %fusion.22 = f32[256,768]{1,0:T(8,128)S(1)} fusion(bf16[2048,768]{1,0:T(8,128)(2,1)} %collective-permute-done.11, bf16[256,4224]{1,0:T(8,128)(2,1)S(1)} %bitcast.62), kind=kOutput, calls=%fused_computation.44 | convolution fusion | flops 805306368 | bytes 4980736 | tf_op jit(solution)/shard_map/dot_general | solution.py:254
  62.2 2.9 %fusion.32 = f32[256,2048]{1,0:T(8,128)S(1)} fusion(bf16[2048,768]{1,0:T(8,128)(2,1)} %collective-permute-done.11, f32[256,768]{1,0:T(8,128)S(1)} %fusion.18, f32[256,768]{1,0:T(8,128)S(1)} %fusion.24), kind=kOutput, calls=%fused_computation.68 | convolution fusion | flops 806486016 | bytes 6815744 | tf_op jit(solution)/shard_map/dot_general | solution.py:264
  65.1 1.1 fusion.9
  66.2 1.2 %fusion.4 = f32[256,2048]{1,0:T(8,128)S(1)} fusion(f32[256,2048]{1,0:T(8,128)S(1)} %fusion.6, f32[256,2048]{1,0:T(8,128)S(1)} %fusion.32, bf16[2048,768]{1,0:T(8,128)(2,1)S(1)} %collective-permute-done.10, f32[256]{0:T(256)S(1)} %get-tuple-element.3, f32[256,768]{1,0:T(8,128)S(1)} %fusion.24, f32[256,768]{1,0:T(8,128)S(1)} %fusion.18, f32[256,768]{1,0:T(8,128)S(1)} %fusion.22), kind=kOutput, calls=%fused_computation.9 | convolution fusion | flops 809893888 | bytes 11797504 | tf_op jit(solution)/shard_map/dot_general | solution.py:263
  68.4 1.1 collective-permute-start.14
  70.8 5.2 %collective-permute-done.14 = bf16[32,4096]{1,0:T(8,128)(2,1)S(1)} collective-permute-done((bf16[32,4096]{1,0:T(8,128)(2,1)S(1)}, bf16[32,4096]{1,0:T(8,128)(2,1)S(1)}, u32[]{:S(2)}, u32[]{:S(2)}) %collective-permute-start.14) | collective-permute-done | bytes 262176 | tf_op jit(solution)/shard_map/ppermute | solution.py:172
  76.0 5.9 %collective-permute-start.15 = (bf16[32,4096]{1,0:T(8,128)(2,1)S(1)}, bf16[32,4096]{1,0:T(8,128)(2,1)S(1)}, u32[]{:S(2)}, u32[]{:S(2)}) collective-permute-start(bf16[32,4096]{1,0:T(8,128)(2,1)S(1)} %fusion.39), channel_id=1, source_target_pairs={{0,4},{1,5},{2,6},{3,7},{16,20},{17,21},{18,22},{19,23}} | collective-permute-start | bytes 786440 | tf_op jit(solution)/shard_map/ppermute | solution.py:229
  83.4 1.3 %collective-permute-start.18 = (bf16[32,4096]{1,0:T(8,128)(2,1)S(1)}, bf16[32,4096]{1,0:T(8,128)(2,1)S(1)}, u32[]{:S(2)}, u32[]{:S(2)}) collective-permute-start(bf16[32,4096]{1,0:T(8,128)(2,1)S(1)} %get-tuple-element.13), channel_id=1, source_target_pairs={{0,2},{1,3},{2,0},{3,1},{4,6},{5,7},{6,4},{7,5},{8,10},{9,11},{10,... | collective-permute-start | bytes 786440 | tf_op jit(solution)/shard_map/ppermute | solution.py:172
  84.7 3.8 %collective-permute-done.15 = bf16[32,4096]{1,0:T(8,128)(2,1)S(1)} collective-permute-done((bf16[32,4096]{1,0:T(8,128)(2,1)S(1)}, bf16[32,4096]{1,0:T(8,128)(2,1)S(1)}, u32[]{:S(2)}, u32[]{:S(2)}) %collective-permute-start.15) | collective-permute-done | bytes 262176 | tf_op jit(solution)/shard_map/ppermute | solution.py:229
  88.7 4.4 %collective-permute-start.17 = (bf16[32,4096]{1,0:T(8,128)(2,1)S(1)}, bf16[32,4096]{1,0:T(8,128)(2,1)S(1)}, u32[]{:S(2)}, u32[]{:S(2)}) collective-permute-start(bf16[32,4096]{1,0:T(8,128)(2,1)S(1)} %get-tuple-element.9), channel_id=1, source_target_pairs={{0,4},{1,5},{2,6},{3,7},{4,8},{5,9},{6,10},{7,11},{16,20},{17,21},... | collective-permute-start | bytes 786440 | tf_op jit(solution)/shard_map/ppermute | solution.py:233
  93.8 4.0 %collective-permute-done.17 = bf16[32,4096]{1,0:T(8,128)(2,1)S(1)} collective-permute-done((bf16[32,4096]{1,0:T(8,128)(2,1)S(1)}, bf16[32,4096]{1,0:T(8,128)(2,1)S(1)}, u32[]{:S(2)}, u32[]{:S(2)}) %collective-permute-start.17) | collective-permute-done | bytes 262176 | tf_op jit(solution)/shard_map/ppermute | solution.py:233
  98.0 11.6 %collective-permute-start.19 = (bf16[32,4096]{1,0:T(8,128)(2,1)S(1)}, bf16[32,4096]{1,0:T(8,128)(2,1)S(1)}, u32[]{:S(2)}, u32[]{:S(2)}) collective-permute-start(bf16[32,4096]{1,0:T(8,128)(2,1)S(1)} %get-tuple-element.7), channel_id=1, source_target_pairs={{0,4},{1,5},{2,6},{3,7},{4,8},{5,9},{6,10},{7,11},{8,12},{9,13},{1... | collective-permute-start | bytes 786440 | tf_op jit(solution)/shard_map/ppermute | solution.py:242
  109.6 1.3 %collective-permute-start.22 = (bf16[32,4096]{1,0:T(8,128)(2,1)S(1)}, bf16[32,4096]{1,0:T(8,128)(2,1)S(1)}, u32[]{:S(2)}, u32[]{:S(2)}) collective-permute-start(bf16[32,4096]{1,0:T(8,128)(2,1)S(1)} %get-tuple-element.8), channel_id=1, source_target_pairs={{4,0},{5,1},{6,2},{7,3},{8,4},{9,5},{10,6},{11,7},{12,8},{13,9},{1... | collective-permute-start | bytes 786440 | tf_op jit(solution)/shard_map/ppermute | solution.py:245
  110.9 2.5 %collective-permute-done.19 = bf16[32,4096]{1,0:T(8,128)(2,1)S(1)} collective-permute-done((bf16[32,4096]{1,0:T(8,128)(2,1)S(1)}, bf16[32,4096]{1,0:T(8,128)(2,1)S(1)}, u32[]{:S(2)}, u32[]{:S(2)}) %collective-permute-start.19) | collective-permute-done | bytes 262176 | tf_op jit(solution)/shard_map/ppermute | solution.py:242
  113.5 4.4 %collective-permute-done.22 = bf16[32,4096]{1,0:T(8,128)(2,1)S(1)} collective-permute-done((bf16[32,4096]{1,0:T(8,128)(2,1)S(1)}, bf16[32,4096]{1,0:T(8,128)(2,1)S(1)}, u32[]{:S(2)}, u32[]{:S(2)}) %collective-permute-start.22) | collective-permute-done | bytes 262176 | tf_op jit(solution)/shard_map/ppermute | solution.py:245
  120.4 1.7 %select_add_fusion = (f32[128,2048]{1,0:T(8,128)}, f32[128,2048]{1,0:T(8,128)}) fusion(f32[128,2048]{1,0:T(8,128)S(1)} %gather_fusion.1, bf16[128,2048]{1,0:T(8,128)(2,1)S(1)} %copy-done.1, pred[128]{0:T(512)(128)(4,1)S(1)} %compare_and_fusion, f32[128,2048]{1,0:T(8,128)S(1)} %gather_fusion, bf16[128,2048]{1,0:T(8,128)(2,1)S(1)} %copy-done.2), kind=kLoop, calls=%fused_computation.30 | loop fusion | flops 1572864 | bytes 5243008 | tf_op jit(solution)/shard_map/add | solution.py:324
  (79 shorter events, 22.8 us)
Async XLA Ops:
  0.6 2.4 %copy-start.4 = (s32[32,8]{0,1:T(8,128)S(1)}, s32[32,8]{0,1:T(8,128)}, u32[]{:S(2)}) copy-start(s32[32,8]{0,1:T(8,128)} %param.13) | copy-start | bytes 3076
  0.6 2.4 %copy-start.3 = (f32[32,8]{0,1:T(8,128)S(1)}, f32[32,8]{0,1:T(8,128)}, u32[]{:S(2)}) copy-start(f32[32,8]{0,1:T(8,128)} %param.14) | copy-start | bytes 3076
  3.2 11.4 %collective-permute-start = (bf16[32,4224]{1,0:T(8,128)(2,1)S(1)}, bf16[32,4224]{1,0:T(8,128)(2,1)S(1)}, u32[]{:S(2)}, u32[]{:S(2)}) collective-permute-start(bf16[32,4224]{1,0:T(8,128)(2,1)S(1)} %fusion.40), channel_id=1, source_target_pairs={{4,0},{5,1},{6,2},{7,3},{8,4},{9,5},{10,6},{11,7},{12,8},{13,9},{1... | collective-permute-start | bytes 811016 | tf_op jit(solution)/shard_map/ppermute | solution.py:206
  4.5 11.4 %collective-permute-start.3 = (bf16[32,4224]{1,0:T(8,128)(2,1)S(1)}, bf16[32,4224]{1,0:T(8,128)(2,1)S(1)}, u32[]{:S(2)}, u32[]{:S(2)}) collective-permute-start(bf16[32,4224]{1,0:T(8,128)(2,1)S(1)} %fusion.40), channel_id=1, source_target_pairs={{0,4},{1,5},{2,6},{3,7},{4,8},{5,9},{6,10},{7,11},{8,12},{9,13},{1... | collective-permute-start | bytes 811016 | tf_op jit(solution)/shard_map/ppermute | solution.py:205
  10.1 25.6 %collective-permute-start.9 = (bf16[32,4224]{1,0:T(8,128)(2,1)S(1)}, bf16[32,4224]{1,0:T(8,128)(2,1)S(1)}, u32[]{:S(2)}, u32[]{:S(2)}) collective-permute-start(bf16[32,4224]{1,0:T(8,128)(2,1)S(1)} %fusion.40), channel_id=1, source_target_pairs={{0,2},{1,3},{2,0},{3,1},{4,6},{5,7},{6,4},{7,5},{8,10},{9,11},{10,... | collective-permute-start | bytes 811016 | tf_op jit(solution)/shard_map/ppermute | solution.py:204
  12.1 45.1 %collective-permute-start.11 = (bf16[2048,768]{1,0:T(8,128)(2,1)}, bf16[2048,768]{1,0:T(8,128)(2,1)}, u32[]{:S(2)}, u32[]{:S(2)}) collective-permute-start(bf16[2048,768]{1,0:T(8,128)(2,1)} %bitcast.57), channel_id=1, source_target_pairs={{0,1},{1,0},{2,3},{3,2},{4,5},{5,4},{6,7},{7,6},{8,9},{9,8},{10,11... | collective-permute-start | bytes 9437192 | tf_op jit(solution)/shard_map/ppermute | solution.py:310
  14.6 9.5 %collective-permute-start.1 = (bf16[32,4224]{1,0:T(8,128)(2,1)S(1)}, bf16[32,4224]{1,0:T(8,128)(2,1)S(1)}, u32[]{:S(2)}, u32[]{:S(2)}) collective-permute-start(bf16[32,4224]{1,0:T(8,128)(2,1)S(1)} %collective-permute-done), channel_id=1, source_target_pairs={{4,0},{5,1},{6,2},{7,3},{8,4},{9,5},{10,6},{11,7},{20,16},{21,17},... | collective-permute-start | bytes 811016 | tf_op jit(solution)/shard_map/ppermute | solution.py:212
  15.9 9.5 %collective-permute-start.4 = (bf16[32,4224]{1,0:T(8,128)(2,1)S(1)}, bf16[32,4224]{1,0:T(8,128)(2,1)S(1)}, u32[]{:S(2)}, u32[]{:S(2)}) collective-permute-start(bf16[32,4224]{1,0:T(8,128)(2,1)S(1)} %collective-permute-done.3), channel_id=1, source_target_pairs={{4,8},{5,9},{6,10},{7,11},{8,12},{9,13},{10,14},{11,15},{20,24},{2... | collective-permute-start | bytes 811016 | tf_op jit(solution)/shard_map/ppermute | solution.py:211
  24.2 8.6 %collective-permute-start.2 = (bf16[32,4224]{1,0:T(8,128)(2,1)S(1)}, bf16[32,4224]{1,0:T(8,128)(2,1)S(1)}, u32[]{:S(2)}, u32[]{:S(2)}) collective-permute-start(bf16[32,4224]{1,0:T(8,128)(2,1)S(1)} %collective-permute-done.1), channel_id=1, source_target_pairs={{4,0},{5,1},{6,2},{7,3},{20,16},{21,17},{22,18},{23,19}} | collective-permute-start | bytes 811016 | tf_op jit(solution)/shard_map/ppermute | solution.py:217
  25.5 7.3 %collective-permute-start.5 = (bf16[32,4224]{1,0:T(8,128)(2,1)S(1)}, bf16[32,4224]{1,0:T(8,128)(2,1)S(1)}, u32[]{:S(2)}, u32[]{:S(2)}) collective-permute-start(bf16[32,4224]{1,0:T(8,128)(2,1)S(1)} %collective-permute-done.4), channel_id=1, source_target_pairs={{8,12},{9,13},{10,14},{11,15},{24,28},{25,29},{26,30},{27,31}} | collective-permute-start | bytes 811016 | tf_op jit(solution)/shard_map/ppermute | solution.py:216
  26.9 8.9 %collective-permute-start.7 = (bf16[32,4224]{1,0:T(8,128)(2,1)}, bf16[32,4224]{1,0:T(8,128)(2,1)S(1)}, u32[]{:S(2)}, u32[]{:S(2)}) collective-permute-start(bf16[32,4224]{1,0:T(8,128)(2,1)} %broadcast_select_fusion), channel_id=1, source_target_pairs={{0,2},{1,3},{2,0},{3,1},{4,6},{5,7},{6,4},{7,5},{8,10},{9,11},{10,... | collective-permute-start | bytes 811016 | tf_op jit(solution)/shard_map/ppermute | solution.py:214
  33.7 8.9 %collective-permute-start.6 = (bf16[32,4224]{1,0:T(8,128)(2,1)}, bf16[32,4224]{1,0:T(8,128)(2,1)S(1)}, u32[]{:S(2)}, u32[]{:S(2)}) collective-permute-start(bf16[32,4224]{1,0:T(8,128)(2,1)} %get-tuple-element.17), channel_id=1, source_target_pairs={{0,2},{1,3},{2,0},{3,1},{4,6},{5,7},{6,4},{7,5},{8,10},{9,11},{10,... | collective-permute-start | bytes 811016 | tf_op jit(solution)/shard_map/ppermute | solution.py:220
  34.8 10.7 %collective-permute-start.8 = (bf16[32,4224]{1,0:T(8,128)(2,1)}, bf16[32,4224]{1,0:T(8,128)(2,1)S(1)}, u32[]{:S(2)}, u32[]{:S(2)}) collective-permute-start(bf16[32,4224]{1,0:T(8,128)(2,1)} %get-tuple-element.18), channel_id=1, source_target_pairs={{0,2},{1,3},{2,0},{3,1},{4,6},{5,7},{6,4},{7,5},{8,10},{9,11},{10,... | collective-permute-start | bytes 811016 | tf_op jit(solution)/shard_map/ppermute | solution.py:209
  35.8 24.4 %collective-permute-start.10 = (bf16[2048,768]{1,0:T(8,128)(2,1)}, bf16[2048,768]{1,0:T(8,128)(2,1)S(1)}, u32[]{:S(2)}, u32[]{:S(2)}) collective-permute-start(bf16[2048,768]{1,0:T(8,128)(2,1)} %bitcast.65), channel_id=1, source_target_pairs={{0,1},{1,0},{2,3},{3,2},{4,5},{5,4},{6,7},{7,6},{8,9},{9,8},{10,11... | collective-permute-start | bytes 9437192 | tf_op jit(solution)/shard_map/ppermute | solution.py:309
  35.8 25.3 %collective-permute-start.12 = (bf16[768,2048]{1,0:T(8,128)(2,1)}, bf16[768,2048]{1,0:T(8,128)(2,1)S(1)}, u32[]{:S(2)}, u32[]{:S(2)}) collective-permute-start(bf16[768,2048]{1,0:T(8,128)(2,1)} %bitcast.66), channel_id=1, source_target_pairs={{0,1},{1,0},{2,3},{3,2},{4,5},{5,4},{6,7},{7,6},{8,9},{9,8},{10,11... | collective-permute-start | bytes 9437192 | tf_op jit(solution)/shard_map/ppermute | solution.py:311
  47.2 1.9 %copy-start = (bf16[1,2048,768]{2,1,0:T(8,128)(2,1)S(1)}, bf16[1,2048,768]{2,1,0:T(8,128)(2,1)}, u32[]{:S(2)}) copy-start(bf16[1,2048,768]{2,1,0:T(8,128)(2,1)} %param.16) | copy-start | bytes 9437188
  49.1 1.9 %copy-start.6 = (bf16[1,2048,768]{2,1,0:T(8,128)(2,1)S(1)}, bf16[1,2048,768]{2,1,0:T(8,128)(2,1)}, u32[]{:S(2)}) copy-start(bf16[1,2048,768]{2,1,0:T(8,128)(2,1)} %param.15) | copy-start | bytes 9437188
  51.0 1.9 %copy-start.7 = (bf16[1,768,2048]{2,1,0:T(8,128)(2,1)S(1)}, bf16[1,768,2048]{2,1,0:T(8,128)(2,1)}, u32[]{:S(2)}) copy-start(bf16[1,768,2048]{2,1,0:T(8,128)(2,1)} %param.17) | copy-start | bytes 9437188
  68.4 7.6 %collective-permute-start.14 = (bf16[32,4096]{1,0:T(8,128)(2,1)S(1)}, bf16[32,4096]{1,0:T(8,128)(2,1)S(1)}, u32[]{:S(2)}, u32[]{:S(2)}) collective-permute-start(bf16[32,4096]{1,0:T(8,128)(2,1)S(1)} %get-tuple-element.15), channel_id=1, source_target_pairs={{0,2},{1,3},{2,0},{3,1},{4,6},{5,7},{6,4},{7,5},{8,10},{9,11},{10,... | collective-permute-start | bytes 786440 | tf_op jit(solution)/shard_map/ppermute | solution.py:172
  69.7 24.1 %copy-start.5 = (s32[128]{0:T(128)S(1)}, s32[128]{0:T(128)}, u32[]{:S(2)}) copy-start(s32[128]{0:T(128)} %param.12) | copy-start | bytes 1540
  69.7 15.0 %collective-permute-start.16 = (bf16[32,4096]{1,0:T(8,128)(2,1)S(1)}, bf16[32,4096]{1,0:T(8,128)(2,1)S(1)}, u32[]{:S(2)}, u32[]{:S(2)}) collective-permute-start(bf16[32,4096]{1,0:T(8,128)(2,1)S(1)} %get-tuple-element.14), channel_id=1, source_target_pairs={{0,2},{1,3},{2,0},{3,1},{4,6},{5,7},{6,4},{7,5},{8,10},{9,11},{10,... | collective-permute-start | bytes 786440 | tf_op jit(solution)/shard_map/ppermute | solution.py:172
  76.0 12.5 %collective-permute-start.15 = (bf16[32,4096]{1,0:T(8,128)(2,1)S(1)}, bf16[32,4096]{1,0:T(8,128)(2,1)S(1)}, u32[]{:S(2)}, u32[]{:S(2)}) collective-permute-start(bf16[32,4096]{1,0:T(8,128)(2,1)S(1)} %fusion.39), channel_id=1, source_target_pairs={{0,4},{1,5},{2,6},{3,7},{16,20},{17,21},{18,22},{19,23}} | collective-permute-start | bytes 786440 | tf_op jit(solution)/shard_map/ppermute | solution.py:229
  82.0 6.6 %collective-permute-start.20 = (bf16[32,4096]{1,0:T(8,128)(2,1)S(1)}, bf16[32,4096]{1,0:T(8,128)(2,1)S(1)}, u32[]{:S(2)}, u32[]{:S(2)}) collective-permute-start(bf16[32,4096]{1,0:T(8,128)(2,1)S(1)} %fusion.39), channel_id=1, source_target_pairs={{12,8},{13,9},{14,10},{15,11},{28,24},{29,25},{30,26},{31,27}} | collective-permute-start | bytes 786440 | tf_op jit(solution)/shard_map/ppermute | solution.py:230
  82.7 11.2 %collective-permute-start.13 = (bf16[32,4096]{1,0:T(8,128)(2,1)S(1)}, bf16[32,4096]{1,0:T(8,128)(2,1)S(1)}, u32[]{:S(2)}, u32[]{:S(2)}) collective-permute-start(bf16[32,4096]{1,0:T(8,128)(2,1)S(1)} %get-tuple-element.16), channel_id=1, source_target_pairs={{0,2},{1,3},{2,0},{3,1},{4,6},{5,7},{6,4},{7,5},{8,10},{9,11},{10,... | collective-permute-start | bytes 786440 | tf_op jit(solution)/shard_map/ppermute | solution.py:172
  83.4 10.4 %collective-permute-start.18 = (bf16[32,4096]{1,0:T(8,128)(2,1)S(1)}, bf16[32,4096]{1,0:T(8,128)(2,1)S(1)}, u32[]{:S(2)}, u32[]{:S(2)}) collective-permute-start(bf16[32,4096]{1,0:T(8,128)(2,1)S(1)} %get-tuple-element.13), channel_id=1, source_target_pairs={{0,2},{1,3},{2,0},{3,1},{4,6},{5,7},{6,4},{7,5},{8,10},{9,11},{10,... | collective-permute-start | bytes 786440 | tf_op jit(solution)/shard_map/ppermute | solution.py:172
  88.7 9.1 %collective-permute-start.17 = (bf16[32,4096]{1,0:T(8,128)(2,1)S(1)}, bf16[32,4096]{1,0:T(8,128)(2,1)S(1)}, u32[]{:S(2)}, u32[]{:S(2)}) collective-permute-start(bf16[32,4096]{1,0:T(8,128)(2,1)S(1)} %get-tuple-element.9), channel_id=1, source_target_pairs={{0,4},{1,5},{2,6},{3,7},{4,8},{5,9},{6,10},{7,11},{16,20},{17,21},... | collective-permute-start | bytes 786440 | tf_op jit(solution)/shard_map/ppermute | solution.py:233
  93.1 4.7 %collective-permute-start.21 = (bf16[32,4096]{1,0:T(8,128)(2,1)S(1)}, bf16[32,4096]{1,0:T(8,128)(2,1)S(1)}, u32[]{:S(2)}, u32[]{:S(2)}) collective-permute-start(bf16[32,4096]{1,0:T(8,128)(2,1)S(1)} %get-tuple-element.10), channel_id=1, source_target_pairs={{8,4},{9,5},{10,6},{11,7},{12,8},{13,9},{14,10},{15,11},{24,20},{2... | collective-permute-start | bytes 786440 | tf_op jit(solution)/shard_map/ppermute | solution.py:236
  98.0 15.4 %collective-permute-start.19 = (bf16[32,4096]{1,0:T(8,128)(2,1)S(1)}, bf16[32,4096]{1,0:T(8,128)(2,1)S(1)}, u32[]{:S(2)}, u32[]{:S(2)}) collective-permute-start(bf16[32,4096]{1,0:T(8,128)(2,1)S(1)} %get-tuple-element.7), channel_id=1, source_target_pairs={{0,4},{1,5},{2,6},{3,7},{4,8},{5,9},{6,10},{7,11},{8,12},{9,13},{1... | collective-permute-start | bytes 786440 | tf_op jit(solution)/shard_map/ppermute | solution.py:242
  109.6 8.3 %collective-permute-start.22 = (bf16[32,4096]{1,0:T(8,128)(2,1)S(1)}, bf16[32,4096]{1,0:T(8,128)(2,1)S(1)}, u32[]{:S(2)}, u32[]{:S(2)}) collective-permute-start(bf16[32,4096]{1,0:T(8,128)(2,1)S(1)} %get-tuple-element.8), channel_id=1, source_target_pairs={{4,0},{5,1},{6,2},{7,3},{8,4},{9,5},{10,6},{11,7},{12,8},{13,9},{1... | collective-permute-start | bytes 786440 | tf_op jit(solution)/shard_map/ppermute | solution.py:245
  119.2 1.0 copy-start.1
  119.2 1.2 copy-start.2

commit v18 on v16

--- a/solution.py
+++ b/solution.py
@@ -219,6 +219,25 @@
     return jnp.where(end, fourth, first) + ahead + behind
 
 
+def expert_joined(cent_in, grad_in, joined_mat, down_mat):
+    hidden_width = down_mat.shape[0]
+    against = (((1,), (1,)), ((), ()))
+    both_act = jnp.dot(cent_in, joined_mat, preferred_element_type=jnp.float32)
+    gate_act = both_act[:, :hidden_width]
+    up_act = both_act[:, hidden_width:]
+    sigmoid_gate = jax.nn.sigmoid(gate_act)
+    hidden = (gate_act * sigmoid_gate * up_act).astype(jnp.bfloat16)
+    output = jnp.dot(hidden, down_mat, preferred_element_type=jnp.float32).astype(jnp.bfloat16)
+    hidden_grad = lax.dot_general(grad_in, down_mat, against, preferred_element_type=jnp.float32)
+    gate_grad = (
+        hidden_grad * up_act * sigmoid_gate * (1.0 + gate_act * (1.0 - sigmoid_gate))
+    ).astype(jnp.bfloat16)
+    up_grad = (hidden_grad * gate_act * sigmoid_gate).astype(jnp.bfloat16)
+    joined_grad = jnp.concatenate([gate_grad, up_grad], axis=1)
+    summed = lax.dot_general(joined_grad, joined_mat, against, preferred_element_type=jnp.float32)
+    return output, summed.astype(jnp.bfloat16)
+
+
 def expert_dense(cent_in, grad_in, gate_mat, up_mat, down_mat):
     against = (((1,), (1,)), ((), ()))
     gate_act = jnp.dot(cent_in, gate_mat, preferred_element_type=jnp.float32)
@@ -277,11 +296,11 @@
     other = jnp.sum(jnp.where(column == (me ^ 1), summed_side, 0.0), axis=1)
     swap_core = [(j, j ^ 1) for j in range(experts)]
     gate_mat, up_mat, down_mat = gate_weight[0], up_weight[0], down_weight[0]
-    gate_pair = lax.ppermute(gate_mat, "expert", swap_core)
-    up_pair = lax.ppermute(up_mat, "expert", swap_core)
+    joined_mat = jnp.concatenate([gate_mat, up_mat], axis=1)
+    joined_pair = lax.ppermute(joined_mat, "expert", swap_core)
     down_pair = lax.ppermute(down_mat, "expert", swap_core)
-    output, input_grad = expert_dense(cent_all, grad_all, gate_mat, up_mat, down_mat)
-    output_pair, input_grad_pair = expert_dense(cent_all, grad_all, gate_pair, up_pair, down_pair)
+    output, input_grad = expert_joined(cent_all, grad_all, joined_mat, down_mat)
+    output_pair, input_grad_pair = expert_joined(cent_all, grad_all, joined_pair, down_pair)
     weighted_out = mine[:, None] * output.astype(jnp.float32) + other[:, None] * output_pair.astype(
         jnp.float32
     )

time: 115 us -> 125 us (1.087)
  other arithmetic: 10.1 us -> 15.9 us
  matrix products: 14.1 us -> 19 us
  local copies, waits for them, and re-layouts: 5.6 us -> 3.88 us
    concatenate x0 -> x1, other arithmetic: none -> 5.93 us  [per_device_dense(): joined_mat = jnp.concatenate([gate_mat, up_mat], axis=1)]
    dot_general x12 -> x8, matrix products: 12.6 us -> 17.5 us  [the longest x2 6.45 us: expert_joined(): lax.dot_general(joined_grad, joined_mat, against, preferred_element_type=...]
    unnamed x17, local copies, waits for them, and re-layouts: 3.53 us -> 1.81 us
    ppermute x1, starting transfers between devices: 3.59 us -> 1.98 us  [topo_all_gather(): there.append((lax.ppermute(behind, 'expert', behind_row), line + step))]
    ppermute x1, waiting for transfers between devices: 5.15 us -> 3.6 us  [four_line_sum(): lax.ppermute((ahead + second).astype(jnp.bfloat16), 'expert', [(j, j + 4)...]
    ppermute x2, waiting for transfers between devices: 6.9 us -> 8.41 us  [topo_all_gather(): lax.ppermute(jnp.where(in_ahead, ahead, behind), 'expert', sorted(ahead_r...]
    ppermute x3, waiting for transfers between devices: 12.7 us -> 14 us  [topo_all_gather(): lax.ppermute(behind, 'expert', [(j, j - 4) for j in range(experts) if 1 <...]
  transfers between devices with their start and end apart: 24 -> 23, of which waited for: 11 -> 10; matrix products, arithmetic and copies ran while one was open for 13% -> 18% of each run, Pallas kernels for 0% -> 0%
where the time goes in v18:
time: 125 us; the launch traced here: 124 us
  waiting for transfers between devices  43 us (34%)
  starting transfers between devices  40.9 us (33%)
  matrix products  19 us (15%)
  other arithmetic  15.9 us (13%)
  local copies, waits for them, and re-layouts  3.88 us (3%)
  between operations  1.29 us (1%)
    ppermute x3, waiting for transfers between devices, topo_all_gather(): lax.ppermute(behind, 'expert', [(j, j - 4) for j in range(experts) if 1 <...  14 us
    ppermute x2, waiting for transfers between devices, topo_all_gather(): lax.ppermute(jnp.where(in_ahead, ahead, behind), 'expert', sorted(ahead_r...  8.41 us
    ppermute x1, starting transfers between devices, four_line_sum(): lax.ppermute((ahead + third).astype(jnp.bfloat16), 'expert', [(j, j + 4)...  7.44 us
    ppermute x3, starting transfers between devices, topo_all_gather(): lax.ppermute(ahead, 'expert', [(j, j + 4) for j in range(experts) if step...  6.93 us
    ppermute x4, waiting for transfers between devices, row_sum(): got = lax.ppermute(theirs.astype(jnp.bfloat16), 'expert', pairs)  6.89 us
    dot_general x2, matrix products, expert_joined(): lax.dot_general(joined_grad, joined_mat, against, preferred_element_type=...  6.45 us
    dot_general x2, matrix products, expert_joined(): both_act = jnp.dot(cent_in, joined_mat, preferred_element_type=jnp.float32)  6.38 us
    concatenate x1, other arithmetic, per_device_dense(): joined_mat = jnp.concatenate([gate_mat, up_mat], axis=1)  5.93 us
  transfers between devices with their start and end apart: 23, of which 10 were waited for; matrix products, arithmetic and copies ran while one was open for 18% of the time, Pallas kernels for 0%

profile of v18, /device:TPU:0, one launch (start us, length us, event | category | flops | bytes accessed | tf_op | source)
XLA Modules:
  0.0 124.0 jit_solution(6244237368795118827)
XLA Ops:
  1.4 1.5 %fusion.10 = f32[32,4096]{1,0:T(8,128)S(1)} fusion(bf16[128,2048]{1,0:T(8,128)(2,1)} %param.11, bf16[128,2048]{1,0:T(8,128)(2,1)} %param.10, s32[128]{0:T(128)} %param.12), kind=kOutput, calls=%fused_computation.25 | convolution fusion | flops 35655680 | bytes 1573376 | tf_op jit(solution)/shard_map/dot_general | solution.py:269
  3.2 1.3 %collective-permute-start = (bf16[32,4224]{1,0:T(8,128)(2,1)S(1)}, bf16[32,4224]{1,0:T(8,128)(2,1)S(1)}, u32[]{:S(2)}, u32[]{:S(2)}) collective-permute-start(bf16[32,4224]{1,0:T(8,128)(2,1)S(1)} %fusion.32), channel_id=1, source_target_pairs={{4,0},{5,1},{6,2},{7,3},{8,4},{9,5},{10,6},{11,7},{12,8},{13,9},{1... | collective-permute-start | bytes 811016 | tf_op jit(solution)/shard_map/ppermute | solution.py:125
  4.5 5.6 %collective-permute-start.3 = (bf16[32,4224]{1,0:T(8,128)(2,1)S(1)}, bf16[32,4224]{1,0:T(8,128)(2,1)S(1)}, u32[]{:S(2)}, u32[]{:S(2)}) collective-permute-start(bf16[32,4224]{1,0:T(8,128)(2,1)S(1)} %fusion.32), channel_id=1, source_target_pairs={{0,4},{1,5},{2,6},{3,7},{4,8},{5,9},{6,10},{7,11},{8,12},{9,13},{1... | collective-permute-start | bytes 811016 | tf_op jit(solution)/shard_map/ppermute | solution.py:120
  10.1 2.0 %collective-permute-start.10 = (bf16[32,4224]{1,0:T(8,128)(2,1)S(1)}, bf16[32,4224]{1,0:T(8,128)(2,1)S(1)}, u32[]{:S(2)}, u32[]{:S(2)}) collective-permute-start(bf16[32,4224]{1,0:T(8,128)(2,1)S(1)} %fusion.32), channel_id=1, source_target_pairs={{0,2},{1,3},{2,0},{3,1},{4,6},{5,7},{6,4},{7,5},{8,10},{9,11},{10,... | collective-permute-start | bytes 811016 | tf_op jit(solution)/shard_map/ppermute | solution.py:117
  12.1 5.9 %pad_maximum_fusion = bf16[2048,1536]{1,0:T(8,128)(2,1)} fusion(bf16[2048,768]{1,0:T(8,128)(2,1)} %bitcast.49, bf16[2048,768]{1,0:T(8,128)(2,1)} %bitcast.52), kind=kLoop, calls=%fused_computation.2 | loop fusion | flops 12582912 | bytes 12582912 | tf_op jit(solution)/shard_map/concatenate | solution.py:299
  18.1 1.3 %collective-permute-start.1 = (bf16[32,4224]{1,0:T(8,128)(2,1)S(1)}, bf16[32,4224]{1,0:T(8,128)(2,1)S(1)}, u32[]{:S(2)}, u32[]{:S(2)}) collective-permute-start(bf16[32,4224]{1,0:T(8,128)(2,1)S(1)} %collective-permute-done), channel_id=1, source_target_pairs={{4,0},{5,1},{6,2},{7,3},{8,4},{9,5},{10,6},{11,7},{20,16},{21,17},... | collective-permute-start | bytes 811016 | tf_op jit(solution)/shard_map/ppermute | solution.py:125
  20.1 2.0 %collective-permute-start.8 = (bf16[32,4224]{1,0:T(8,128)(2,1)S(1)}, bf16[32,4224]{1,0:T(8,128)(2,1)S(1)}, u32[]{:S(2)}, u32[]{:S(2)}) collective-permute-start(bf16[32,4224]{1,0:T(8,128)(2,1)S(1)} %collective-permute-done), channel_id=1, source_target_pairs={{0,2},{1,3},{2,0},{3,1},{4,6},{5,7},{6,4},{7,5},{8,10},{9,11},{10,... | collective-permute-start | bytes 811016 | tf_op jit(solution)/shard_map/ppermute | solution.py:143
  22.1 6.8 %collective-permute-done.1 = bf16[32,4224]{1,0:T(8,128)(2,1)S(1)} collective-permute-done((bf16[32,4224]{1,0:T(8,128)(2,1)S(1)}, bf16[32,4224]{1,0:T(8,128)(2,1)S(1)}, u32[]{:S(2)}, u32[]{:S(2)}) %collective-permute-start.1) | collective-permute-done | bytes 270368 | tf_op jit(solution)/shard_map/ppermute | solution.py:125
  28.8 1.3 %collective-permute-start.2 = (bf16[32,4224]{1,0:T(8,128)(2,1)S(1)}, bf16[32,4224]{1,0:T(8,128)(2,1)S(1)}, u32[]{:S(2)}, u32[]{:S(2)}) collective-permute-start(bf16[32,4224]{1,0:T(8,128)(2,1)S(1)} %collective-permute-done.1), channel_id=1, source_target_pairs={{4,0},{5,1},{6,2},{7,3},{20,16},{21,17},{22,18},{23,19}} | collective-permute-start | bytes 811016 | tf_op jit(solution)/shard_map/ppermute | solution.py:125
  31.6 7.3 %collective-permute-done.2 = bf16[32,4224]{1,0:T(8,128)(2,1)S(1)} collective-permute-done((bf16[32,4224]{1,0:T(8,128)(2,1)S(1)}, bf16[32,4224]{1,0:T(8,128)(2,1)S(1)}, u32[]{:S(2)}, u32[]{:S(2)}) %collective-permute-start.2) | collective-permute-done | bytes 270368 | tf_op jit(solution)/shard_map/ppermute | solution.py:125
  40.9 3.4 %collective-permute-start.6 = (bf16[32,4224]{1,0:T(8,128)(2,1)}, bf16[32,4224]{1,0:T(8,128)(2,1)}, u32[]{:S(2)}, u32[]{:S(2)}) collective-permute-start(bf16[32,4224]{1,0:T(8,128)(2,1)} %broadcast_select_fusion.3), channel_id=1, source_target_pairs={{0,2},{1,3},{2,0},{3,1},{12,14},{13,15},{14,12},{15,13},{16,18},{1... | collective-permute-start | bytes 811016 | tf_op jit(solution)/shard_map/ppermute | solution.py:136
  44.5 4.7 %collective-permute-done.7 = bf16[32,4224]{1,0:T(8,128)(2,1)S(1)} collective-permute-done((bf16[32,4224]{1,0:T(8,128)(2,1)}, bf16[32,4224]{1,0:T(8,128)(2,1)S(1)}, u32[]{:S(2)}, u32[]{:S(2)}) %collective-permute-start.7) | collective-permute-done | bytes 270368 | tf_op jit(solution)/shard_map/ppermute | solution.py:136
  49.2 3.7 %collective-permute-done.6 = bf16[32,4224]{1,0:T(8,128)(2,1)} collective-permute-done((bf16[32,4224]{1,0:T(8,128)(2,1)}, bf16[32,4224]{1,0:T(8,128)(2,1)}, u32[]{:S(2)}, u32[]{:S(2)}) %collective-permute-start.6) | collective-permute-done | bytes 270368 | tf_op jit(solution)/shard_map/ppermute | solution.py:136
  52.9 1.9 %broadcast_select_fusion.1 = bf16[4,1,32,4224]{3,2,1,0:T(8,128)(2,1)S(1)} fusion(pred[]{:T(512)S(6)} %eq.171, bf16[32,4224]{1,0:T(8,128)(2,1)S(1)} %collective-permute-done.10, pred[4]{0:T(512)(128)(4,1)S(1)} %get-tuple-element.25, bf16[32,4224]{1,0:T(8,128)(2,1)S(1)} %collective-permute-done.9, pred[4]{0:T(512)(128)(4,1)S(1)} %get-tuple-element.26, ...), kind=kLoop, calls=%fused_computation.24 | loop fusion | flops 7028736 | bytes 4325413 | tf_op jit(solution)/shard_map/jit(_where)/select_n | solution.py:99
  54.8 2.0 %broadcast_select_fusion = bf16[4,1,32,4224]{3,2,1,0:T(8,128)(2,1)S(1)} fusion(pred[]{:T(512)S(6)} %eq.171, bf16[32,4224]{1,0:T(8,128)(2,1)S(1)} %collective-permute-done.10, pred[4]{0:T(512)(128)(4,1)S(1)} %get-tuple-element.25, bf16[32,4224]{1,0:T(8,128)(2,1)S(1)} %collective-permute-done.9, pred[4]{0:T(512)(128)(4,1)S(1)} %get-tuple-element.26, ...), kind=kLoop, calls=%fused_computation.23 | loop fusion | flops 7028736 | bytes 4325413 | tf_op jit(solution)/shard_map/jit(_where)/select_n | solution.py:99
  57.3 1.4 %copy-done = bf16[1,2048,768]{2,1,0:T(8,128)(2,1)S(1)} copy-done((bf16[1,2048,768]{2,1,0:T(8,128)(2,1)S(1)}, bf16[1,2048,768]{2,1,0:T(8,128)(2,1)}, u32[]{:S(2)}) %copy-start) | copy-done | bytes 3145752
  58.7 1.8 %fusion.20 = f32[256,1536]{1,0:T(8,128)S(1)} fusion(bf16[256,4224]{1,0:T(8,128)(2,1)S(1)} %bitcast.56, bf16[2048,768]{1,0:T(8,128)(2,1)S(1)} %bitcast.50, bf16[2048,768]{1,0:T(8,128)(2,1)S(1)} %bitcast.53), kind=kOutput, calls=%fused_computation.37 | convolution fusion | flops 1623195648 | bytes 8912896 | tf_op jit(solution)/shard_map/dot_general | solution.py:225
  62.9 1.8 %fusion.4 = f32[256,2048]{1,0:T(8,128)S(1)} fusion(f32[256]{0:T(256)S(1)} %get-tuple-element.4, bf16[256,768]{1,0:T(8,128)(2,1)S(1)} %get-tuple-element.14, bf16[256,768]{1,0:T(8,128)(2,1)S(1)} %get-tuple-element.13, bf16[2048,768]{1,0:T(8,128)(2,1)S(1)} %bitcast.51, bf16[2048,768]{1,0:T(8,128)(2,1)S(1)} %bitcast.54), kind=kOutput, calls=%fused_computation.10 | convolution fusion | flops 1626341376 | bytes 9176064 | tf_op jit(solution)/shard_map/dot_general | solution.py:237
  64.7 4.6 %fusion.18 = f32[256,1536]{1,0:T(8,128)S(1)} fusion(bf16[2048,1536]{1,0:T(8,128)(2,1)} %collective-permute-done.11, bf16[256,4224]{1,0:T(8,128)(2,1)S(1)} %bitcast.58), kind=kOutput, calls=%fused_computation.35 | convolution fusion | flops 1610612736 | bytes 8912896 | tf_op jit(solution)/shard_map/dot_general | solution.py:225
  71.7 4.6 %fusion.2 = f32[256,2048]{1,0:T(8,128)S(1)} fusion(f32[256,2048]{1,0:T(8,128)S(1)} %fusion.4, bf16[2048,1536]{1,0:T(8,128)(2,1)} %collective-permute-done.11, f32[256]{0:T(256)S(1)} %get-tuple-element.3, bf16[256,768]{1,0:T(8,128)(2,1)S(1)} %get-tuple-element.12, bf16[256,768]{1,0:T(8,128)(2,1)S(1)} %get-tuple-element.11), kind=kOutput, calls=%fused_computation.7 | convolution fusion | flops 1614282752 | bytes 11273216 | tf_op jit(solution)/shard_map/dot_general | solution.py:237
  78.1 1.3 %collective-permute-start.16 = (bf16[32,4096]{1,0:T(8,128)(2,1)S(1)}, bf16[32,4096]{1,0:T(8,128)(2,1)S(1)}, u32[]{:S(2)}, u32[]{:S(2)}) collective-permute-start(bf16[32,4096]{1,0:T(8,128)(2,1)S(1)} %get-tuple-element.18), channel_id=1, source_target_pairs={{0,2},{1,3},{2,0},{3,1},{4,6},{5,7},{6,4},{7,5},{8,10},{9,11},{10,... | collective-permute-start | bytes 786440 | tf_op jit(solution)/shard_map/ppermute | solution.py:165
  79.5 6.7 %collective-permute-done.14 = bf16[32,4096]{1,0:T(8,128)(2,1)S(1)} collective-permute-done((bf16[32,4096]{1,0:T(8,128)(2,1)S(1)}, bf16[32,4096]{1,0:T(8,128)(2,1)S(1)}, u32[]{:S(2)}, u32[]{:S(2)}) %collective-permute-start.14) | collective-permute-done | bytes 262176 | tf_op jit(solution)/shard_map/ppermute | solution.py:165
  86.3 2.5 %collective-permute-start.15 = (bf16[32,4096]{1,0:T(8,128)(2,1)S(1)}, bf16[32,4096]{1,0:T(8,128)(2,1)S(1)}, u32[]{:S(2)}, u32[]{:S(2)}) collective-permute-start(bf16[32,4096]{1,0:T(8,128)(2,1)S(1)} %fusion.31), channel_id=1, source_target_pairs={{0,4},{1,5},{2,6},{3,7},{16,20},{17,21},{18,22},{19,23}} | collective-permute-start | bytes 786440 | tf_op jit(solution)/shard_map/ppermute | solution.py:200
  90.4 1.3 %collective-permute-start.18 = (bf16[32,4096]{1,0:T(8,128)(2,1)S(1)}, bf16[32,4096]{1,0:T(8,128)(2,1)S(1)}, u32[]{:S(2)}, u32[]{:S(2)}) collective-permute-start(bf16[32,4096]{1,0:T(8,128)(2,1)S(1)} %get-tuple-element.17), channel_id=1, source_target_pairs={{0,2},{1,3},{2,0},{3,1},{4,6},{5,7},{6,4},{7,5},{8,10},{9,11},{10,... | collective-permute-start | bytes 786440 | tf_op jit(solution)/shard_map/ppermute | solution.py:165
  91.8 3.2 %collective-permute-done.15 = bf16[32,4096]{1,0:T(8,128)(2,1)S(1)} collective-permute-done((bf16[32,4096]{1,0:T(8,128)(2,1)S(1)}, bf16[32,4096]{1,0:T(8,128)(2,1)S(1)}, u32[]{:S(2)}, u32[]{:S(2)}) %collective-permute-start.15) | collective-permute-done | bytes 262176 | tf_op jit(solution)/shard_map/ppermute | solution.py:200
  95.2 4.4 %collective-permute-start.17 = (bf16[32,4096]{1,0:T(8,128)(2,1)S(1)}, bf16[32,4096]{1,0:T(8,128)(2,1)S(1)}, u32[]{:S(2)}, u32[]{:S(2)}) collective-permute-start(bf16[32,4096]{1,0:T(8,128)(2,1)S(1)} %get-tuple-element.9), channel_id=1, source_target_pairs={{0,4},{1,5},{2,6},{3,7},{4,8},{5,9},{6,10},{7,11},{16,20},{17,21},... | collective-permute-start | bytes 786440 | tf_op jit(solution)/shard_map/ppermute | solution.py:204
  100.3 3.6 %collective-permute-done.17 = bf16[32,4096]{1,0:T(8,128)(2,1)S(1)} collective-permute-done((bf16[32,4096]{1,0:T(8,128)(2,1)S(1)}, bf16[32,4096]{1,0:T(8,128)(2,1)S(1)}, u32[]{:S(2)}, u32[]{:S(2)}) %collective-permute-start.17) | collective-permute-done | bytes 262176 | tf_op jit(solution)/shard_map/ppermute | solution.py:204
  104.1 7.4 %collective-permute-start.19 = (bf16[32,4096]{1,0:T(8,128)(2,1)S(1)}, bf16[32,4096]{1,0:T(8,128)(2,1)S(1)}, u32[]{:S(2)}, u32[]{:S(2)}) collective-permute-start(bf16[32,4096]{1,0:T(8,128)(2,1)S(1)} %get-tuple-element.7), channel_id=1, source_target_pairs={{0,4},{1,5},{2,6},{3,7},{4,8},{5,9},{6,10},{7,11},{8,12},{9,13},{1... | collective-permute-start | bytes 786440 | tf_op jit(solution)/shard_map/ppermute | solution.py:213
  111.6 1.3 %collective-permute-start.22 = (bf16[32,4096]{1,0:T(8,128)(2,1)S(1)}, bf16[32,4096]{1,0:T(8,128)(2,1)S(1)}, u32[]{:S(2)}, u32[]{:S(2)}) collective-permute-start(bf16[32,4096]{1,0:T(8,128)(2,1)S(1)} %get-tuple-element.8), channel_id=1, source_target_pairs={{4,0},{5,1},{6,2},{7,3},{8,4},{9,5},{10,6},{11,7},{12,8},{13,9},{1... | collective-permute-start | bytes 786440 | tf_op jit(solution)/shard_map/ppermute | solution.py:216
  112.9 2.5 %collective-permute-done.19 = bf16[32,4096]{1,0:T(8,128)(2,1)S(1)} collective-permute-done((bf16[32,4096]{1,0:T(8,128)(2,1)S(1)}, bf16[32,4096]{1,0:T(8,128)(2,1)S(1)}, u32[]{:S(2)}, u32[]{:S(2)}) %collective-permute-start.19) | collective-permute-done | bytes 262176 | tf_op jit(solution)/shard_map/ppermute | solution.py:213
  115.4 4.4 %collective-permute-done.22 = bf16[32,4096]{1,0:T(8,128)(2,1)S(1)} collective-permute-done((bf16[32,4096]{1,0:T(8,128)(2,1)S(1)}, bf16[32,4096]{1,0:T(8,128)(2,1)S(1)}, u32[]{:S(2)}, u32[]{:S(2)}) %collective-permute-start.22) | collective-permute-done | bytes 262176 | tf_op jit(solution)/shard_map/ppermute | solution.py:216
  122.3 1.7 %select_add_fusion = (f32[128,2048]{1,0:T(8,128)}, f32[128,2048]{1,0:T(8,128)}) fusion(f32[128,2048]{1,0:T(8,128)S(1)} %gather_fusion.1, bf16[128,2048]{1,0:T(8,128)(2,1)S(1)} %copy-done.2, pred[128]{0:T(512)(128)(4,1)S(1)} %compare_and_fusion, f32[128,2048]{1,0:T(8,128)S(1)} %gather_fusion, bf16[128,2048]{1,0:T(8,128)(2,1)S(1)} %copy-done.3), kind=kLoop, calls=%fused_computation.29 | loop fusion | flops 1572864 | bytes 5243008 | tf_op jit(solution)/shard_map/add | solution.py:314
  (76 shorter events, 17.7 us)
Async XLA Ops:
  0.6 2.4 %copy-start.5 = (s32[32,8]{0,1:T(8,128)S(1)}, s32[32,8]{0,1:T(8,128)}, u32[]{:S(2)}) copy-start(s32[32,8]{0,1:T(8,128)} %param.13) | copy-start | bytes 3076
  0.6 2.4 %copy-start.4 = (f32[32,8]{0,1:T(8,128)S(1)}, f32[32,8]{0,1:T(8,128)}, u32[]{:S(2)}) copy-start(f32[32,8]{0,1:T(8,128)} %param.14) | copy-start | bytes 3076
  3.2 14.8 %collective-permute-start = (bf16[32,4224]{1,0:T(8,128)(2,1)S(1)}, bf16[32,4224]{1,0:T(8,128)(2,1)S(1)}, u32[]{:S(2)}, u32[]{:S(2)}) collective-permute-start(bf16[32,4224]{1,0:T(8,128)(2,1)S(1)} %fusion.32), channel_id=1, source_target_pairs={{4,0},{5,1},{6,2},{7,3},{8,4},{9,5},{10,6},{11,7},{12,8},{13,9},{1... | collective-permute-start | bytes 811016 | tf_op jit(solution)/shard_map/ppermute | solution.py:125
  4.5 14.8 %collective-permute-start.3 = (bf16[32,4224]{1,0:T(8,128)(2,1)S(1)}, bf16[32,4224]{1,0:T(8,128)(2,1)S(1)}, u32[]{:S(2)}, u32[]{:S(2)}) collective-permute-start(bf16[32,4224]{1,0:T(8,128)(2,1)S(1)} %fusion.32), channel_id=1, source_target_pairs={{0,4},{1,5},{2,6},{3,7},{4,8},{5,9},{6,10},{7,11},{8,12},{9,13},{1... | collective-permute-start | bytes 811016 | tf_op jit(solution)/shard_map/ppermute | solution.py:120
  10.1 30.8 %collective-permute-start.10 = (bf16[32,4224]{1,0:T(8,128)(2,1)S(1)}, bf16[32,4224]{1,0:T(8,128)(2,1)S(1)}, u32[]{:S(2)}, u32[]{:S(2)}) collective-permute-start(bf16[32,4224]{1,0:T(8,128)(2,1)S(1)} %fusion.32), channel_id=1, source_target_pairs={{0,2},{1,3},{2,0},{3,1},{4,6},{5,7},{6,4},{7,5},{8,10},{9,11},{10,... | collective-permute-start | bytes 811016 | tf_op jit(solution)/shard_map/ppermute | solution.py:117
  18.1 46.7 %collective-permute-start.11 = (bf16[2048,1536]{1,0:T(8,128)(2,1)}, bf16[2048,1536]{1,0:T(8,128)(2,1)}, u32[]{:S(2)}, u32[]{:S(2)}) collective-permute-start(bf16[2048,1536]{1,0:T(8,128)(2,1)} %pad_maximum_fusion), channel_id=1, source_target_pairs={{0,1},{1,0},{2,3},{3,2},{4,5},{5,4},{6,7},{7,6},{8,9},{9,8},{10,11... | collective-permute-start | bytes 18874376 | tf_op jit(solution)/shard_map/ppermute | solution.py:300
  18.1 10.8 %collective-permute-start.1 = (bf16[32,4224]{1,0:T(8,128)(2,1)S(1)}, bf16[32,4224]{1,0:T(8,128)(2,1)S(1)}, u32[]{:S(2)}, u32[]{:S(2)}) collective-permute-start(bf16[32,4224]{1,0:T(8,128)(2,1)S(1)} %collective-permute-done), channel_id=1, source_target_pairs={{4,0},{5,1},{6,2},{7,3},{8,4},{9,5},{10,6},{11,7},{20,16},{21,17},... | collective-permute-start | bytes 811016 | tf_op jit(solution)/shard_map/ppermute | solution.py:125
  19.4 10.8 %collective-permute-start.4 = (bf16[32,4224]{1,0:T(8,128)(2,1)S(1)}, bf16[32,4224]{1,0:T(8,128)(2,1)S(1)}, u32[]{:S(2)}, u32[]{:S(2)}) collective-permute-start(bf16[32,4224]{1,0:T(8,128)(2,1)S(1)} %collective-permute-done.3), channel_id=1, source_target_pairs={{4,8},{5,9},{6,10},{7,11},{8,12},{9,13},{10,14},{11,15},{20,24},{2... | collective-permute-start | bytes 811016 | tf_op jit(solution)/shard_map/ppermute | solution.py:120
  20.1 24.3 %collective-permute-start.8 = (bf16[32,4224]{1,0:T(8,128)(2,1)S(1)}, bf16[32,4224]{1,0:T(8,128)(2,1)S(1)}, u32[]{:S(2)}, u32[]{:S(2)}) collective-permute-start(bf16[32,4224]{1,0:T(8,128)(2,1)S(1)} %collective-permute-done), channel_id=1, source_target_pairs={{0,2},{1,3},{2,0},{3,1},{4,6},{5,7},{6,4},{7,5},{8,10},{9,11},{10,... | collective-permute-start | bytes 811016 | tf_op jit(solution)/shard_map/ppermute | solution.py:143
  28.8 10.0 %collective-permute-start.2 = (bf16[32,4224]{1,0:T(8,128)(2,1)S(1)}, bf16[32,4224]{1,0:T(8,128)(2,1)S(1)}, u32[]{:S(2)}, u32[]{:S(2)}) collective-permute-start(bf16[32,4224]{1,0:T(8,128)(2,1)S(1)} %collective-permute-done.1), channel_id=1, source_target_pairs={{4,0},{5,1},{6,2},{7,3},{20,16},{21,17},{22,18},{23,19}} | collective-permute-start | bytes 811016 | tf_op jit(solution)/shard_map/ppermute | solution.py:125
  30.1 9.4 %collective-permute-start.5 = (bf16[32,4224]{1,0:T(8,128)(2,1)S(1)}, bf16[32,4224]{1,0:T(8,128)(2,1)S(1)}, u32[]{:S(2)}, u32[]{:S(2)}) collective-permute-start(bf16[32,4224]{1,0:T(8,128)(2,1)S(1)} %collective-permute-done.4), channel_id=1, source_target_pairs={{8,12},{9,13},{10,14},{11,15},{24,28},{25,29},{26,30},{27,31}} | collective-permute-start | bytes 811016 | tf_op jit(solution)/shard_map/ppermute | solution.py:120
  38.8 5.7 %collective-permute-start.9 = (bf16[32,4224]{1,0:T(8,128)(2,1)S(1)}, bf16[32,4224]{1,0:T(8,128)(2,1)S(1)}, u32[]{:S(2)}, u32[]{:S(2)}) collective-permute-start(bf16[32,4224]{1,0:T(8,128)(2,1)S(1)} %collective-permute-done.3), channel_id=1, source_target_pairs={{4,6},{5,7},{6,4},{7,5},{8,10},{9,11},{10,8},{11,9},{12,14},{13,15... | collective-permute-start | bytes 811016 | tf_op jit(solution)/shard_map/ppermute | solution.py:142
  39.5 9.7 %collective-permute-start.7 = (bf16[32,4224]{1,0:T(8,128)(2,1)}, bf16[32,4224]{1,0:T(8,128)(2,1)S(1)}, u32[]{:S(2)}, u32[]{:S(2)}) collective-permute-start(bf16[32,4224]{1,0:T(8,128)(2,1)} %broadcast_select_fusion.2), channel_id=1, source_target_pairs={{0,2},{1,3},{2,0},{3,1},{4,6},{5,7},{6,4},{7,5},{8,10},{9,11},{10,... | collective-permute-start | bytes 811016 | tf_op jit(solution)/shard_map/ppermute | solution.py:136
  40.9 12.0 %collective-permute-start.6 = (bf16[32,4224]{1,0:T(8,128)(2,1)}, bf16[32,4224]{1,0:T(8,128)(2,1)}, u32[]{:S(2)}, u32[]{:S(2)}) collective-permute-start(bf16[32,4224]{1,0:T(8,128)(2,1)} %broadcast_select_fusion.3), channel_id=1, source_target_pairs={{0,2},{1,3},{2,0},{3,1},{12,14},{13,15},{14,12},{15,13},{16,18},{1... | collective-permute-start | bytes 811016 | tf_op jit(solution)/shard_map/ppermute | solution.py:136
  44.4 24.9 %collective-permute-start.12 = (bf16[768,2048]{1,0:T(8,128)(2,1)}, bf16[768,2048]{1,0:T(8,128)(2,1)S(1)}, u32[]{:S(2)}, u32[]{:S(2)}) collective-permute-start(bf16[768,2048]{1,0:T(8,128)(2,1)} %bitcast.60), channel_id=1, source_target_pairs={{0,1},{1,0},{2,3},{3,2},{4,5},{5,4},{6,7},{7,6},{8,9},{9,8},{10,11... | collective-permute-start | bytes 9437192 | tf_op jit(solution)/shard_map/ppermute | solution.py:301
  54.8 2.5 %copy-start.1 = (bf16[1,2048,768]{2,1,0:T(8,128)(2,1)S(1)}, bf16[1,2048,768]{2,1,0:T(8,128)(2,1)}, u32[]{:S(2)}) copy-start(bf16[1,2048,768]{2,1,0:T(8,128)(2,1)} %param.15) | copy-start | bytes 9437188
  56.8 1.9 %copy-start = (bf16[1,2048,768]{2,1,0:T(8,128)(2,1)S(1)}, bf16[1,2048,768]{2,1,0:T(8,128)(2,1)}, u32[]{:S(2)}) copy-start(bf16[1,2048,768]{2,1,0:T(8,128)(2,1)} %param.16) | copy-start | bytes 9437188
  58.7 1.9 %copy-start.7 = (bf16[1,768,2048]{2,1,0:T(8,128)(2,1)S(1)}, bf16[1,768,2048]{2,1,0:T(8,128)(2,1)}, u32[]{:S(2)}) copy-start(bf16[1,768,2048]{2,1,0:T(8,128)(2,1)} %param.17) | copy-start | bytes 9437188
  77.1 9.1 %collective-permute-start.14 = (bf16[32,4096]{1,0:T(8,128)(2,1)S(1)}, bf16[32,4096]{1,0:T(8,128)(2,1)S(1)}, u32[]{:S(2)}, u32[]{:S(2)}) collective-permute-start(bf16[32,4096]{1,0:T(8,128)(2,1)S(1)} %get-tuple-element.19), channel_id=1, source_target_pairs={{0,2},{1,3},{2,0},{3,1},{4,6},{5,7},{6,4},{7,5},{8,10},{9,11},{10,... | collective-permute-start | bytes 786440 | tf_op jit(solution)/shard_map/ppermute | solution.py:165
  78.1 22.1 %copy-start.6 = (s32[128]{0:T(128)S(1)}, s32[128]{0:T(128)}, u32[]{:S(2)}) copy-start(s32[128]{0:T(128)} %param.12) | copy-start | bytes 1540
  78.1 13.7 %collective-permute-start.16 = (bf16[32,4096]{1,0:T(8,128)(2,1)S(1)}, bf16[32,4096]{1,0:T(8,128)(2,1)S(1)}, u32[]{:S(2)}, u32[]{:S(2)}) collective-permute-start(bf16[32,4096]{1,0:T(8,128)(2,1)S(1)} %get-tuple-element.18), channel_id=1, source_target_pairs={{0,2},{1,3},{2,0},{3,1},{4,6},{5,7},{6,4},{7,5},{8,10},{9,11},{10,... | collective-permute-start | bytes 786440 | tf_op jit(solution)/shard_map/ppermute | solution.py:165
  86.3 8.7 %collective-permute-start.15 = (bf16[32,4096]{1,0:T(8,128)(2,1)S(1)}, bf16[32,4096]{1,0:T(8,128)(2,1)S(1)}, u32[]{:S(2)}, u32[]{:S(2)}) collective-permute-start(bf16[32,4096]{1,0:T(8,128)(2,1)S(1)} %fusion.31), channel_id=1, source_target_pairs={{0,4},{1,5},{2,6},{3,7},{16,20},{17,21},{18,22},{19,23}} | collective-permute-start | bytes 786440 | tf_op jit(solution)/shard_map/ppermute | solution.py:200
  88.7 6.3 %collective-permute-start.20 = (bf16[32,4096]{1,0:T(8,128)(2,1)S(1)}, bf16[32,4096]{1,0:T(8,128)(2,1)S(1)}, u32[]{:S(2)}, u32[]{:S(2)}) collective-permute-start(bf16[32,4096]{1,0:T(8,128)(2,1)S(1)} %fusion.31), channel_id=1, source_target_pairs={{12,8},{13,9},{14,10},{15,11},{28,24},{29,25},{30,26},{31,27}} | collective-permute-start | bytes 786440 | tf_op jit(solution)/shard_map/ppermute | solution.py:201
  89.6 10.7 %collective-permute-start.13 = (bf16[32,4096]{1,0:T(8,128)(2,1)S(1)}, bf16[32,4096]{1,0:T(8,128)(2,1)S(1)}, u32[]{:S(2)}, u32[]{:S(2)}) collective-permute-start(bf16[32,4096]{1,0:T(8,128)(2,1)S(1)} %get-tuple-element.20), channel_id=1, source_target_pairs={{0,2},{1,3},{2,0},{3,1},{4,6},{5,7},{6,4},{7,5},{8,10},{9,11},{10,... | collective-permute-start | bytes 786440 | tf_op jit(solution)/shard_map/ppermute | solution.py:165
  90.4 9.9 %collective-permute-start.18 = (bf16[32,4096]{1,0:T(8,128)(2,1)S(1)}, bf16[32,4096]{1,0:T(8,128)(2,1)S(1)}, u32[]{:S(2)}, u32[]{:S(2)}) collective-permute-start(bf16[32,4096]{1,0:T(8,128)(2,1)S(1)} %get-tuple-element.17), channel_id=1, source_target_pairs={{0,2},{1,3},{2,0},{3,1},{4,6},{5,7},{6,4},{7,5},{8,10},{9,11},{10,... | collective-permute-start | bytes 786440 | tf_op jit(solution)/shard_map/ppermute | solution.py:165
  95.2 8.7 %collective-permute-start.17 = (bf16[32,4096]{1,0:T(8,128)(2,1)S(1)}, bf16[32,4096]{1,0:T(8,128)(2,1)S(1)}, u32[]{:S(2)}, u32[]{:S(2)}) collective-permute-start(bf16[32,4096]{1,0:T(8,128)(2,1)S(1)} %get-tuple-element.9), channel_id=1, source_target_pairs={{0,4},{1,5},{2,6},{3,7},{4,8},{5,9},{6,10},{7,11},{16,20},{17,21},... | collective-permute-start | bytes 786440 | tf_op jit(solution)/shard_map/ppermute | solution.py:204
  99.6 4.3 %collective-permute-start.21 = (bf16[32,4096]{1,0:T(8,128)(2,1)S(1)}, bf16[32,4096]{1,0:T(8,128)(2,1)S(1)}, u32[]{:S(2)}, u32[]{:S(2)}) collective-permute-start(bf16[32,4096]{1,0:T(8,128)(2,1)S(1)} %get-tuple-element.10), channel_id=1, source_target_pairs={{8,4},{9,5},{10,6},{11,7},{12,8},{13,9},{14,10},{15,11},{24,20},{2... | collective-permute-start | bytes 786440 | tf_op jit(solution)/shard_map/ppermute | solution.py:207
  104.1 11.3 %collective-permute-start.19 = (bf16[32,4096]{1,0:T(8,128)(2,1)S(1)}, bf16[32,4096]{1,0:T(8,128)(2,1)S(1)}, u32[]{:S(2)}, u32[]{:S(2)}) collective-permute-start(bf16[32,4096]{1,0:T(8,128)(2,1)S(1)} %get-tuple-element.7), channel_id=1, source_target_pairs={{0,4},{1,5},{2,6},{3,7},{4,8},{5,9},{6,10},{7,11},{8,12},{9,13},{1... | collective-permute-start | bytes 786440 | tf_op jit(solution)/shard_map/ppermute | solution.py:213
  111.6 8.3 %collective-permute-start.22 = (bf16[32,4096]{1,0:T(8,128)(2,1)S(1)}, bf16[32,4096]{1,0:T(8,128)(2,1)S(1)}, u32[]{:S(2)}, u32[]{:S(2)}) collective-permute-start(bf16[32,4096]{1,0:T(8,128)(2,1)S(1)} %get-tuple-element.8), channel_id=1, source_target_pairs={{4,0},{5,1},{6,2},{7,3},{8,4},{9,5},{10,6},{11,7},{12,8},{13,9},{1... | collective-permute-start | bytes 786440 | tf_op jit(solution)/shard_map/ppermute | solution.py:216
  121.1 1.0 copy-start.2
  121.1 1.2 copy-start.3

commit v19 on v16

--- a/solution.py
+++ b/solution.py
@@ -141,21 +141,17 @@
         else:
             there.append((lax.ppermute(ahead, "expert", ahead_row), line - step))
             there.append((lax.ppermute(behind, "expert", behind_row), line + step))
-    column = place(here, lines, shard)
-    across = place(there, lines, shard)
-    in_row = (me // 2) % 2
-    mine = jnp.stack([pick(in_row, [column, across]), pick(in_row, [across, column])], axis=1)
-    return mine.reshape((lines * 2 * shard.shape[0],) + shard.shape[1:])
+    both = jnp.stack([place(here, lines, shard), place(there, lines, shard)])
+    return both.reshape((lines * 2 * shard.shape[0],) + shard.shape[1:])
 
 
 def topo_reduce_scatter(blocks, experts):
     lines = experts // 4
     me = lax.axis_index("expert")
     rows = blocks.shape[0] // (2 * lines)
-    plane = blocks.reshape((lines, 2, rows) + blocks.shape[1:])
-    in_row = (me // 2) % 2
-    keep = pick(in_row, [plane[:, 0], plane[:, 1]])
-    give = pick(in_row, [plane[:, 1], plane[:, 0]])
+    plane = blocks.reshape((2, lines, rows) + blocks.shape[1:])
+    keep = plane[0]
+    give = plane[1]
     line = me // 4
 
     def row_sum(target, senders):

time: 115 us -> 106 us (0.922)
  other arithmetic: 10.1 us -> 5.12 us
  waiting for transfers between devices: 42.2 us -> 40.6 us
  local copies, waits for them, and re-layouts: 5.6 us -> 4.14 us
    select_n x4 -> x2, other arithmetic: 4.35 us -> 1 us  [place(): stacked = jnp.where(slot == origin, piece[None], stacked)]
    ppermute x1, waiting for transfers between devices: 5.15 us -> 3.23 us  [four_line_sum(): lax.ppermute((ahead + second).astype(jnp.bfloat16), 'expert', [(j, j + 4)...]
    unnamed x17, local copies, waits for them, and re-layouts: 3.53 us -> 2.07 us
    select_n x2, other arithmetic: 1.5 us -> 0.08 us  [topo_all_gather(): jnp.where(in_ahead, ahead, behind)]
  transfers between devices with their start and end apart: 24 -> 24, of which waited for: 11 -> 11; matrix products, arithmetic and copies ran while one was open for 13% -> 10% of each run, Pallas kernels for 0% -> 0%
where the time goes in v19:
time: 106 us
  waiting for transfers between devices  40.6 us (38%)
  starting transfers between devices  40.5 us (38%)
  matrix products  14 us (13%)
  other arithmetic  5.12 us (5%)
  local copies, waits for them, and re-layouts  4.14 us (4%)
  between operations  1.28 us (1%)
    ppermute x3, waiting for transfers between devices, topo_all_gather(): lax.ppermute(behind, 'expert', [(j, j - 4) for j in range(experts) if 1 <...  13.4 us
    ppermute x4, waiting for transfers between devices, row_sum(): got = lax.ppermute(theirs.astype(jnp.bfloat16), 'expert', pairs)  8.54 us
    ppermute x3, starting transfers between devices, topo_all_gather(): lax.ppermute(ahead, 'expert', [(j, j + 4) for j in range(experts) if step...  6.93 us
    ppermute x1, starting transfers between devices, four_line_sum(): lax.ppermute((ahead + third).astype(jnp.bfloat16), 'expert', [(j, j + 4)...  6.28 us
    ppermute x2, waiting for transfers between devices, topo_all_gather(): lax.ppermute(jnp.where(in_ahead, ahead, behind), 'expert', sorted(ahead_r...  6.13 us
    ppermute x1, waiting for transfers between devices, four_line_sum(): lax.ppermute((behind + behind_part).astype(jnp.bfloat16), 'expert', [(j,...  4.41 us
    ppermute x1, starting transfers between devices, four_line_sum(): lax.ppermute((ahead + second).astype(jnp.bfloat16), 'expert', [(j, j + 4)...  4.4 us
    ppermute x4, starting transfers between devices, row_sum(): got = lax.ppermute(theirs.astype(jnp.bfloat16), 'expert', pairs)  4.18 us
  transfers between devices with their start and end apart: 24, of which 11 were waited for; matrix products, arithmetic and copies ran while one was open for 10% of the time, Pallas kernels for 0%

profile of v19, /device:TPU:0, one launch (start us, length us, event | category | flops | bytes accessed | tf_op | source)
XLA Modules:
  0.0 105.6 jit_solution(11332692062966056804)
XLA Ops:
  1.4 1.5 %fusion.13 = f32[32,4096]{1,0:T(8,128)S(1)} fusion(bf16[128,2048]{1,0:T(8,128)(2,1)} %param.11, bf16[128,2048]{1,0:T(8,128)(2,1)} %param.10, s32[128]{0:T(128)} %param.12), kind=kOutput, calls=%fused_computation.25 | convolution fusion | flops 35655680 | bytes 1573376 | tf_op jit(solution)/shard_map/dot_general | solution.py:246
  3.2 1.3 %collective-permute-start = (bf16[32,4224]{1,0:T(8,128)(2,1)S(1)}, bf16[32,4224]{1,0:T(8,128)(2,1)S(1)}, u32[]{:S(2)}, u32[]{:S(2)}) collective-permute-start(bf16[32,4224]{1,0:T(8,128)(2,1)S(1)} %fusion.39), channel_id=1, source_target_pairs={{4,0},{5,1},{6,2},{7,3},{8,4},{9,5},{10,6},{11,7},{12,8},{13,9},{1... | collective-permute-start | bytes 811016 | tf_op jit(solution)/shard_map/ppermute | solution.py:125
  4.5 5.6 %collective-permute-start.3 = (bf16[32,4224]{1,0:T(8,128)(2,1)S(1)}, bf16[32,4224]{1,0:T(8,128)(2,1)S(1)}, u32[]{:S(2)}, u32[]{:S(2)}) collective-permute-start(bf16[32,4224]{1,0:T(8,128)(2,1)S(1)} %fusion.39), channel_id=1, source_target_pairs={{0,4},{1,5},{2,6},{3,7},{4,8},{5,9},{6,10},{7,11},{8,12},{9,13},{1... | collective-permute-start | bytes 811016 | tf_op jit(solution)/shard_map/ppermute | solution.py:120
  10.1 2.0 %collective-permute-start.10 = (bf16[32,4224]{1,0:T(8,128)(2,1)S(1)}, bf16[32,4224]{1,0:T(8,128)(2,1)S(1)}, u32[]{:S(2)}, u32[]{:S(2)}) collective-permute-start(bf16[32,4224]{1,0:T(8,128)(2,1)S(1)} %fusion.39), channel_id=1, source_target_pairs={{0,2},{1,3},{2,0},{3,1},{4,6},{5,7},{6,4},{7,5},{8,10},{9,11},{10,... | collective-permute-start | bytes 811016 | tf_op jit(solution)/shard_map/ppermute | solution.py:117
  12.2 2.5 %collective-permute-done = bf16[32,4224]{1,0:T(8,128)(2,1)S(1)} collective-permute-done((bf16[32,4224]{1,0:T(8,128)(2,1)S(1)}, bf16[32,4224]{1,0:T(8,128)(2,1)S(1)}, u32[]{:S(2)}, u32[]{:S(2)}) %collective-permute-start) | collective-permute-done | bytes 270368 | tf_op jit(solution)/shard_map/ppermute | solution.py:125
  14.6 1.3 %collective-permute-start.1 = (bf16[32,4224]{1,0:T(8,128)(2,1)S(1)}, bf16[32,4224]{1,0:T(8,128)(2,1)S(1)}, u32[]{:S(2)}, u32[]{:S(2)}) collective-permute-start(bf16[32,4224]{1,0:T(8,128)(2,1)S(1)} %collective-permute-done), channel_id=1, source_target_pairs={{4,0},{5,1},{6,2},{7,3},{8,4},{9,5},{10,6},{11,7},{20,16},{21,17},... | collective-permute-start | bytes 811016 | tf_op jit(solution)/shard_map/ppermute | solution.py:125
  16.7 3.6 %collective-permute-start.8 = (bf16[32,4224]{1,0:T(8,128)(2,1)S(1)}, bf16[32,4224]{1,0:T(8,128)(2,1)S(1)}, u32[]{:S(2)}, u32[]{:S(2)}) collective-permute-start(bf16[32,4224]{1,0:T(8,128)(2,1)S(1)} %collective-permute-done), channel_id=1, source_target_pairs={{0,2},{1,3},{2,0},{3,1},{4,6},{5,7},{6,4},{7,5},{8,10},{9,11},{10,... | collective-permute-start | bytes 811016 | tf_op jit(solution)/shard_map/ppermute | solution.py:143
  21.0 3.2 %collective-permute-done.1 = bf16[32,4224]{1,0:T(8,128)(2,1)S(1)} collective-permute-done((bf16[32,4224]{1,0:T(8,128)(2,1)S(1)}, bf16[32,4224]{1,0:T(8,128)(2,1)S(1)}, u32[]{:S(2)}, u32[]{:S(2)}) %collective-permute-start.1) | collective-permute-done | bytes 270368 | tf_op jit(solution)/shard_map/ppermute | solution.py:125
  24.2 1.3 %collective-permute-start.2 = (bf16[32,4224]{1,0:T(8,128)(2,1)S(1)}, bf16[32,4224]{1,0:T(8,128)(2,1)S(1)}, u32[]{:S(2)}, u32[]{:S(2)}) collective-permute-start(bf16[32,4224]{1,0:T(8,128)(2,1)S(1)} %collective-permute-done.1), channel_id=1, source_target_pairs={{4,0},{5,1},{6,2},{7,3},{20,16},{21,17},{22,18},{23,19}} | collective-permute-start | bytes 811016 | tf_op jit(solution)/shard_map/ppermute | solution.py:125
  26.2 7.8 %collective-permute-done.2 = bf16[32,4224]{1,0:T(8,128)(2,1)S(1)} collective-permute-done((bf16[32,4224]{1,0:T(8,128)(2,1)S(1)}, bf16[32,4224]{1,0:T(8,128)(2,1)S(1)}, u32[]{:S(2)}, u32[]{:S(2)}) %collective-permute-start.2) | collective-permute-done | bytes 270368 | tf_op jit(solution)/shard_map/ppermute | solution.py:125
  34.0 1.5 %collective-permute-start.7 = (bf16[32,4224]{1,0:T(8,128)(2,1)S(1)}, bf16[32,4224]{1,0:T(8,128)(2,1)S(1)}, u32[]{:S(2)}, u32[]{:S(2)}) collective-permute-start(bf16[32,4224]{1,0:T(8,128)(2,1)S(1)} %broadcast_select_fusion), channel_id=1, source_target_pairs={{0,2},{1,3},{2,0},{3,1},{4,6},{5,7},{6,4},{7,5},{8,10},{9,11},{10,... | collective-permute-start | bytes 811016 | tf_op jit(solution)/shard_map/ppermute | solution.py:136
  35.5 2.4 %collective-permute-start.6 = (bf16[32,4224]{1,0:T(8,128)(2,1)S(1)}, bf16[32,4224]{1,0:T(8,128)(2,1)S(1)}, u32[]{:S(2)}, u32[]{:S(2)}) collective-permute-start(bf16[32,4224]{1,0:T(8,128)(2,1)S(1)} %broadcast_select_fusion.1), channel_id=1, source_target_pairs={{0,2},{1,3},{2,0},{3,1},{12,14},{13,15},{14,12},{15,13},{16,18},{1... | collective-permute-start | bytes 811016 | tf_op jit(solution)/shard_map/ppermute | solution.py:136
  39.2 3.2 %collective-permute-done.7 = bf16[32,4224]{1,0:T(8,128)(2,1)S(1)} collective-permute-done((bf16[32,4224]{1,0:T(8,128)(2,1)S(1)}, bf16[32,4224]{1,0:T(8,128)(2,1)S(1)}, u32[]{:S(2)}, u32[]{:S(2)}) %collective-permute-start.7) | collective-permute-done | bytes 270368 | tf_op jit(solution)/shard_map/ppermute | solution.py:136
  42.5 2.9 %collective-permute-done.6 = bf16[32,4224]{1,0:T(8,128)(2,1)S(1)} collective-permute-done((bf16[32,4224]{1,0:T(8,128)(2,1)S(1)}, bf16[32,4224]{1,0:T(8,128)(2,1)S(1)}, u32[]{:S(2)}, u32[]{:S(2)}) %collective-permute-start.6) | collective-permute-done | bytes 270368 | tf_op jit(solution)/shard_map/ppermute | solution.py:136
  50.1 1.0 fusion.19
  51.1 1.1 %fusion.11 = f32[256,2048]{1,0:T(8,128)S(1)} fusion(f32[256]{0:T(256)S(1)} %get-tuple-element.4, f32[256,768]{1,0:T(8,128)S(1)} %fusion.25, f32[256,768]{1,0:T(8,128)S(1)} %fusion.27, bf16[1,768,2048]{2,1,0:T(8,128)(2,1)S(1)} %copy-done.7), kind=kOutput, calls=%fused_computation.19 | convolution fusion | flops 808058880 | bytes 6816768 | tf_op jit(solution)/shard_map/dot_general | solution.py:224
  52.2 1.1 %fusion.30 = f32[256,2048]{1,0:T(8,128)S(1)} fusion(f32[256,768]{1,0:T(8,128)S(1)} %fusion.27, f32[256,768]{1,0:T(8,128)S(1)} %fusion.19, f32[256,768]{1,0:T(8,128)S(1)} %fusion.25, bf16[1,2048,768]{2,1,0:T(8,128)(2,1)S(1)} %copy-done.6), kind=kOutput, calls=%fused_computation.66 | convolution fusion | flops 807272448 | bytes 7602176 | tf_op jit(solution)/shard_map/dot_general | solution.py:230
  53.3 1.1 %fusion.6 = f32[256,2048]{1,0:T(8,128)S(1)} fusion(f32[256,2048]{1,0:T(8,128)S(1)} %fusion.30, f32[256]{0:T(256)S(1)} %get-tuple-element.4, f32[256,768]{1,0:T(8,128)S(1)} %fusion.19, f32[256,768]{1,0:T(8,128)S(1)} %fusion.27, bf16[1,2048,768]{2,1,0:T(8,128)(2,1)S(1)} %copy-done), kind=kOutput, calls=%fused_computation.12 | convolution fusion | flops 808583168 | bytes 8913920 | tf_op jit(solution)/shard_map/dot_general | solution.py:231
  59.5 1.1 %fusion.4 = f32[256,2048]{1,0:T(8,128)S(1)} fusion(f32[256,2048]{1,0:T(8,128)S(1)} %fusion.6, f32[256,2048]{1,0:T(8,128)S(1)} %fusion.31, bf16[2048,768]{1,0:T(8,128)(2,1)S(1)} %collective-permute-done.11, f32[256]{0:T(256)S(1)} %get-tuple-element.3, f32[256,768]{1,0:T(8,128)S(1)} %fusion.23, f32[256,768]{1,0:T(8,128)S(1)} %fusion.17, ...), kind=kOutput, calls=%fused_computation.10 | convolution fusion | flops 809893888 | bytes 11797504 | tf_op jit(solution)/shard_map/dot_general | solution.py:230
  60.9 1.3 %collective-permute-start.15 = (bf16[32,4096]{1,0:T(8,128)(2,1)S(1)}, bf16[32,4096]{1,0:T(8,128)(2,1)S(1)}, u32[]{:S(2)}, u32[]{:S(2)}) collective-permute-start(bf16[32,4096]{1,0:T(8,128)(2,1)S(1)} %get-tuple-element.15), channel_id=1, source_target_pairs={{0,2},{1,3},{2,0},{3,1},{4,6},{5,7},{6,4},{7,5},{8,10},{9,11},{10,... | collective-permute-start | bytes 786440 | tf_op jit(solution)/shard_map/ppermute | solution.py:161
  63.1 7.1 %collective-permute-done.15 = bf16[32,4096]{1,0:T(8,128)(2,1)S(1)} collective-permute-done((bf16[32,4096]{1,0:T(8,128)(2,1)S(1)}, bf16[32,4096]{1,0:T(8,128)(2,1)S(1)}, u32[]{:S(2)}, u32[]{:S(2)}) %collective-permute-start.15) | collective-permute-done | bytes 262176 | tf_op jit(solution)/shard_map/ppermute | solution.py:161
  70.2 1.3 %collective-permute-start.16 = (bf16[32,4096]{1,0:T(8,128)(2,1)S(1)}, bf16[32,4096]{1,0:T(8,128)(2,1)S(1)}, u32[]{:S(2)}, u32[]{:S(2)}) collective-permute-start(bf16[32,4096]{1,0:T(8,128)(2,1)S(1)} %fusion.38), channel_id=1, source_target_pairs={{0,4},{1,5},{2,6},{3,7},{16,20},{17,21},{18,22},{19,23}} | collective-permute-start | bytes 786440 | tf_op jit(solution)/shard_map/ppermute | solution.py:196
  72.2 1.3 %collective-permute-start.14 = (bf16[32,4096]{1,0:T(8,128)(2,1)S(1)}, bf16[32,4096]{1,0:T(8,128)(2,1)S(1)}, u32[]{:S(2)}, u32[]{:S(2)}) collective-permute-start(bf16[32,4096]{1,0:T(8,128)(2,1)S(1)} %get-tuple-element.16), channel_id=1, source_target_pairs={{0,2},{1,3},{2,0},{3,1},{4,6},{5,7},{6,4},{7,5},{8,10},{9,11},{10,... | collective-permute-start | bytes 786440 | tf_op jit(solution)/shard_map/ppermute | solution.py:161
  74.3 1.5 %collective-permute-done.17 = bf16[32,4096]{1,0:T(8,128)(2,1)S(1)} collective-permute-done((bf16[32,4096]{1,0:T(8,128)(2,1)S(1)}, bf16[32,4096]{1,0:T(8,128)(2,1)S(1)}, u32[]{:S(2)}, u32[]{:S(2)}) %collective-permute-start.17) | collective-permute-done | bytes 262176 | tf_op jit(solution)/shard_map/ppermute | solution.py:161
  75.8 2.4 %collective-permute-done.16 = bf16[32,4096]{1,0:T(8,128)(2,1)S(1)} collective-permute-done((bf16[32,4096]{1,0:T(8,128)(2,1)S(1)}, bf16[32,4096]{1,0:T(8,128)(2,1)S(1)}, u32[]{:S(2)}, u32[]{:S(2)}) %collective-permute-start.16) | collective-permute-done | bytes 262176 | tf_op jit(solution)/shard_map/ppermute | solution.py:196
  78.3 4.4 %collective-permute-start.18 = (bf16[32,4096]{1,0:T(8,128)(2,1)S(1)}, bf16[32,4096]{1,0:T(8,128)(2,1)S(1)}, u32[]{:S(2)}, u32[]{:S(2)}) collective-permute-start(bf16[32,4096]{1,0:T(8,128)(2,1)S(1)} %get-tuple-element.9), channel_id=1, source_target_pairs={{0,4},{1,5},{2,6},{3,7},{4,8},{5,9},{6,10},{7,11},{16,20},{17,21},... | collective-permute-start | bytes 786440 | tf_op jit(solution)/shard_map/ppermute | solution.py:200
  83.5 3.2 %collective-permute-done.18 = bf16[32,4096]{1,0:T(8,128)(2,1)S(1)} collective-permute-done((bf16[32,4096]{1,0:T(8,128)(2,1)S(1)}, bf16[32,4096]{1,0:T(8,128)(2,1)S(1)}, u32[]{:S(2)}, u32[]{:S(2)}) %collective-permute-start.18) | collective-permute-done | bytes 262176 | tf_op jit(solution)/shard_map/ppermute | solution.py:200
  86.9 6.3 %collective-permute-start.20 = (bf16[32,4096]{1,0:T(8,128)(2,1)S(1)}, bf16[32,4096]{1,0:T(8,128)(2,1)S(1)}, u32[]{:S(2)}, u32[]{:S(2)}) collective-permute-start(bf16[32,4096]{1,0:T(8,128)(2,1)S(1)} %get-tuple-element.7), channel_id=1, source_target_pairs={{0,4},{1,5},{2,6},{3,7},{4,8},{5,9},{6,10},{7,11},{8,12},{9,13},{1... | collective-permute-start | bytes 786440 | tf_op jit(solution)/shard_map/ppermute | solution.py:209
  93.2 1.3 %collective-permute-start.23 = (bf16[32,4096]{1,0:T(8,128)(2,1)S(1)}, bf16[32,4096]{1,0:T(8,128)(2,1)S(1)}, u32[]{:S(2)}, u32[]{:S(2)}) collective-permute-start(bf16[32,4096]{1,0:T(8,128)(2,1)S(1)} %get-tuple-element.8), channel_id=1, source_target_pairs={{4,0},{5,1},{6,2},{7,3},{8,4},{9,5},{10,6},{11,7},{12,8},{13,9},{1... | collective-permute-start | bytes 786440 | tf_op jit(solution)/shard_map/ppermute | solution.py:212
  94.5 2.5 %collective-permute-done.20 = bf16[32,4096]{1,0:T(8,128)(2,1)S(1)} collective-permute-done((bf16[32,4096]{1,0:T(8,128)(2,1)S(1)}, bf16[32,4096]{1,0:T(8,128)(2,1)S(1)}, u32[]{:S(2)}, u32[]{:S(2)}) %collective-permute-start.20) | collective-permute-done | bytes 262176 | tf_op jit(solution)/shard_map/ppermute | solution.py:209
  97.0 4.4 %collective-permute-done.23 = bf16[32,4096]{1,0:T(8,128)(2,1)S(1)} collective-permute-done((bf16[32,4096]{1,0:T(8,128)(2,1)S(1)}, bf16[32,4096]{1,0:T(8,128)(2,1)S(1)}, u32[]{:S(2)}, u32[]{:S(2)}) %collective-permute-start.23) | collective-permute-done | bytes 262176 | tf_op jit(solution)/shard_map/ppermute | solution.py:212
  104.0 1.7 %select_add_fusion = (f32[128,2048]{1,0:T(8,128)}, f32[128,2048]{1,0:T(8,128)}) fusion(f32[128,2048]{1,0:T(8,128)S(1)} %gather_fusion.1, bf16[128,2048]{1,0:T(8,128)(2,1)S(1)} %copy-done.1, pred[128]{0:T(512)(128)(4,1)S(1)} %compare_and_fusion, f32[128,2048]{1,0:T(8,128)S(1)} %gather_fusion, bf16[128,2048]{1,0:T(8,128)(2,1)S(1)} %copy-done.2), kind=kLoop, calls=%fused_computation.29 | loop fusion | flops 1572864 | bytes 5243008 | tf_op jit(solution)/shard_map/add | solution.py:291
  (80 shorter events, 20.3 us)
Async XLA Ops:
  0.6 2.4 %copy-start.4 = (s32[32,8]{0,1:T(8,128)S(1)}, s32[32,8]{0,1:T(8,128)}, u32[]{:S(2)}) copy-start(s32[32,8]{0,1:T(8,128)} %param.13) | copy-start | bytes 3076
  0.6 2.4 %copy-start.3 = (f32[32,8]{0,1:T(8,128)S(1)}, f32[32,8]{0,1:T(8,128)}, u32[]{:S(2)}) copy-start(f32[32,8]{0,1:T(8,128)} %param.14) | copy-start | bytes 3076
  3.2 11.4 %collective-permute-start = (bf16[32,4224]{1,0:T(8,128)(2,1)S(1)}, bf16[32,4224]{1,0:T(8,128)(2,1)S(1)}, u32[]{:S(2)}, u32[]{:S(2)}) collective-permute-start(bf16[32,4224]{1,0:T(8,128)(2,1)S(1)} %fusion.39), channel_id=1, source_target_pairs={{4,0},{5,1},{6,2},{7,3},{8,4},{9,5},{10,6},{11,7},{12,8},{13,9},{1... | collective-permute-start | bytes 811016 | tf_op jit(solution)/shard_map/ppermute | solution.py:125
  4.5 11.4 %collective-permute-start.3 = (bf16[32,4224]{1,0:T(8,128)(2,1)S(1)}, bf16[32,4224]{1,0:T(8,128)(2,1)S(1)}, u32[]{:S(2)}, u32[]{:S(2)}) collective-permute-start(bf16[32,4224]{1,0:T(8,128)(2,1)S(1)} %fusion.39), channel_id=1, source_target_pairs={{0,4},{1,5},{2,6},{3,7},{4,8},{5,9},{6,10},{7,11},{8,12},{9,13},{1... | collective-permute-start | bytes 811016 | tf_op jit(solution)/shard_map/ppermute | solution.py:120
  10.1 28.5 %collective-permute-start.10 = (bf16[32,4224]{1,0:T(8,128)(2,1)S(1)}, bf16[32,4224]{1,0:T(8,128)(2,1)S(1)}, u32[]{:S(2)}, u32[]{:S(2)}) collective-permute-start(bf16[32,4224]{1,0:T(8,128)(2,1)S(1)} %fusion.39), channel_id=1, source_target_pairs={{0,2},{1,3},{2,0},{3,1},{4,6},{5,7},{6,4},{7,5},{8,10},{9,11},{10,... | collective-permute-start | bytes 811016 | tf_op jit(solution)/shard_map/ppermute | solution.py:117
  14.6 9.6 %collective-permute-start.1 = (bf16[32,4224]{1,0:T(8,128)(2,1)S(1)}, bf16[32,4224]{1,0:T(8,128)(2,1)S(1)}, u32[]{:S(2)}, u32[]{:S(2)}) collective-permute-start(bf16[32,4224]{1,0:T(8,128)(2,1)S(1)} %collective-permute-done), channel_id=1, source_target_pairs={{4,0},{5,1},{6,2},{7,3},{8,4},{9,5},{10,6},{11,7},{20,16},{21,17},... | collective-permute-start | bytes 811016 | tf_op jit(solution)/shard_map/ppermute | solution.py:125
  15.9 9.5 %collective-permute-start.4 = (bf16[32,4224]{1,0:T(8,128)(2,1)S(1)}, bf16[32,4224]{1,0:T(8,128)(2,1)S(1)}, u32[]{:S(2)}, u32[]{:S(2)}) collective-permute-start(bf16[32,4224]{1,0:T(8,128)(2,1)S(1)} %collective-permute-done.3), channel_id=1, source_target_pairs={{4,8},{5,9},{6,10},{7,11},{8,12},{9,13},{10,14},{11,15},{20,24},{2... | collective-permute-start | bytes 811016 | tf_op jit(solution)/shard_map/ppermute | solution.py:120
  16.7 21.9 %collective-permute-start.8 = (bf16[32,4224]{1,0:T(8,128)(2,1)S(1)}, bf16[32,4224]{1,0:T(8,128)(2,1)S(1)}, u32[]{:S(2)}, u32[]{:S(2)}) collective-permute-start(bf16[32,4224]{1,0:T(8,128)(2,1)S(1)} %collective-permute-done), channel_id=1, source_target_pairs={{0,2},{1,3},{2,0},{3,1},{4,6},{5,7},{6,4},{7,5},{8,10},{9,11},{10,... | collective-permute-start | bytes 811016 | tf_op jit(solution)/shard_map/ppermute | solution.py:143
  20.3 18.8 %collective-permute-start.9 = (bf16[32,4224]{1,0:T(8,128)(2,1)S(1)}, bf16[32,4224]{1,0:T(8,128)(2,1)S(1)}, u32[]{:S(2)}, u32[]{:S(2)}) collective-permute-start(bf16[32,4224]{1,0:T(8,128)(2,1)S(1)} %collective-permute-done.3), channel_id=1, source_target_pairs={{4,6},{5,7},{6,4},{7,5},{8,10},{9,11},{10,8},{11,9},{12,14},{13,15... | collective-permute-start | bytes 811016 | tf_op jit(solution)/shard_map/ppermute | solution.py:142
  24.2 9.8 %collective-permute-start.2 = (bf16[32,4224]{1,0:T(8,128)(2,1)S(1)}, bf16[32,4224]{1,0:T(8,128)(2,1)S(1)}, u32[]{:S(2)}, u32[]{:S(2)}) collective-permute-start(bf16[32,4224]{1,0:T(8,128)(2,1)S(1)} %collective-permute-done.1), channel_id=1, source_target_pairs={{4,0},{5,1},{6,2},{7,3},{20,16},{21,17},{22,18},{23,19}} | collective-permute-start | bytes 811016 | tf_op jit(solution)/shard_map/ppermute | solution.py:125
  25.5 10.0 %collective-permute-start.5 = (bf16[32,4224]{1,0:T(8,128)(2,1)S(1)}, bf16[32,4224]{1,0:T(8,128)(2,1)S(1)}, u32[]{:S(2)}, u32[]{:S(2)}) collective-permute-start(bf16[32,4224]{1,0:T(8,128)(2,1)S(1)} %collective-permute-done.4), channel_id=1, source_target_pairs={{8,12},{9,13},{10,14},{11,15},{24,28},{25,29},{26,30},{27,31}} | collective-permute-start | bytes 811016 | tf_op jit(solution)/shard_map/ppermute | solution.py:120
  26.2 12.4 %copy-start = (bf16[1,2048,768]{2,1,0:T(8,128)(2,1)S(1)}, bf16[1,2048,768]{2,1,0:T(8,128)(2,1)}, u32[]{:S(2)}) copy-start(bf16[1,2048,768]{2,1,0:T(8,128)(2,1)} %param.16) | copy-start | bytes 9437188
  34.0 8.5 %collective-permute-start.7 = (bf16[32,4224]{1,0:T(8,128)(2,1)S(1)}, bf16[32,4224]{1,0:T(8,128)(2,1)S(1)}, u32[]{:S(2)}, u32[]{:S(2)}) collective-permute-start(bf16[32,4224]{1,0:T(8,128)(2,1)S(1)} %broadcast_select_fusion), channel_id=1, source_target_pairs={{0,2},{1,3},{2,0},{3,1},{4,6},{5,7},{6,4},{7,5},{8,10},{9,11},{10,... | collective-permute-start | bytes 811016 | tf_op jit(solution)/shard_map/ppermute | solution.py:136
  35.5 9.8 %collective-permute-start.6 = (bf16[32,4224]{1,0:T(8,128)(2,1)S(1)}, bf16[32,4224]{1,0:T(8,128)(2,1)S(1)}, u32[]{:S(2)}, u32[]{:S(2)}) collective-permute-start(bf16[32,4224]{1,0:T(8,128)(2,1)S(1)} %broadcast_select_fusion.1), channel_id=1, source_target_pairs={{0,2},{1,3},{2,0},{3,1},{12,14},{13,15},{14,12},{15,13},{16,18},{1... | collective-permute-start | bytes 811016 | tf_op jit(solution)/shard_map/ppermute | solution.py:136
  38.6 15.8 %collective-permute-start.12 = (bf16[2048,768]{1,0:T(8,128)(2,1)S(1)}, bf16[2048,768]{1,0:T(8,128)(2,1)S(1)}, u32[]{:S(2)}, u32[]{:S(2)}) collective-permute-start(bf16[2048,768]{1,0:T(8,128)(2,1)S(1)} %bitcast.61), channel_id=1, source_target_pairs={{0,1},{1,0},{2,3},{3,2},{4,5},{5,4},{6,7},{7,6},{8,9},{9,8},{10,11... | collective-permute-start | bytes 9437192 | tf_op jit(solution)/shard_map/ppermute | solution.py:277
  38.7 16.8 %collective-permute-start.11 = (bf16[2048,768]{1,0:T(8,128)(2,1)}, bf16[2048,768]{1,0:T(8,128)(2,1)S(1)}, u32[]{:S(2)}, u32[]{:S(2)}) collective-permute-start(bf16[2048,768]{1,0:T(8,128)(2,1)} %bitcast.69), channel_id=1, source_target_pairs={{0,1},{1,0},{2,3},{3,2},{4,5},{5,4},{6,7},{7,6},{8,9},{9,8},{10,11... | collective-permute-start | bytes 9437192 | tf_op jit(solution)/shard_map/ppermute | solution.py:276
  39.2 17.3 %collective-permute-start.13 = (bf16[768,2048]{1,0:T(8,128)(2,1)}, bf16[768,2048]{1,0:T(8,128)(2,1)S(1)}, u32[]{:S(2)}, u32[]{:S(2)}) collective-permute-start(bf16[768,2048]{1,0:T(8,128)(2,1)} %bitcast.70), channel_id=1, source_target_pairs={{0,1},{1,0},{2,3},{3,2},{4,5},{5,4},{6,7},{7,6},{8,9},{9,8},{10,11... | collective-permute-start | bytes 9437192 | tf_op jit(solution)/shard_map/ppermute | solution.py:278
  46.3 1.9 %copy-start.6 = (bf16[1,2048,768]{2,1,0:T(8,128)(2,1)S(1)}, bf16[1,2048,768]{2,1,0:T(8,128)(2,1)}, u32[]{:S(2)}) copy-start(bf16[1,2048,768]{2,1,0:T(8,128)(2,1)} %param.15) | copy-start | bytes 9437188
  48.2 1.9 %copy-start.7 = (bf16[1,768,2048]{2,1,0:T(8,128)(2,1)S(1)}, bf16[1,768,2048]{2,1,0:T(8,128)(2,1)}, u32[]{:S(2)}) copy-start(bf16[1,768,2048]{2,1,0:T(8,128)(2,1)} %param.17) | copy-start | bytes 9437188
  60.9 9.3 %collective-permute-start.15 = (bf16[32,4096]{1,0:T(8,128)(2,1)S(1)}, bf16[32,4096]{1,0:T(8,128)(2,1)S(1)}, u32[]{:S(2)}, u32[]{:S(2)}) collective-permute-start(bf16[32,4096]{1,0:T(8,128)(2,1)S(1)} %get-tuple-element.15), channel_id=1, source_target_pairs={{0,2},{1,3},{2,0},{3,1},{4,6},{5,7},{6,4},{7,5},{8,10},{9,11},{10,... | collective-permute-start | bytes 786440 | tf_op jit(solution)/shard_map/ppermute | solution.py:161
  62.2 13.6 %collective-permute-start.17 = (bf16[32,4096]{1,0:T(8,128)(2,1)S(1)}, bf16[32,4096]{1,0:T(8,128)(2,1)S(1)}, u32[]{:S(2)}, u32[]{:S(2)}) collective-permute-start(bf16[32,4096]{1,0:T(8,128)(2,1)S(1)} %get-tuple-element.14), channel_id=1, source_target_pairs={{0,2},{1,3},{2,0},{3,1},{4,6},{5,7},{6,4},{7,5},{8,10},{9,11},{10,... | collective-permute-start | bytes 786440 | tf_op jit(solution)/shard_map/ppermute | solution.py:161
  63.1 20.3 %copy-start.5 = (s32[128]{0:T(128)S(1)}, s32[128]{0:T(128)}, u32[]{:S(2)}) copy-start(s32[128]{0:T(128)} %param.12) | copy-start | bytes 1540
  70.2 7.9 %collective-permute-start.16 = (bf16[32,4096]{1,0:T(8,128)(2,1)S(1)}, bf16[32,4096]{1,0:T(8,128)(2,1)S(1)}, u32[]{:S(2)}, u32[]{:S(2)}) collective-permute-start(bf16[32,4096]{1,0:T(8,128)(2,1)S(1)} %fusion.38), channel_id=1, source_target_pairs={{0,4},{1,5},{2,6},{3,7},{16,20},{17,21},{18,22},{19,23}} | collective-permute-start | bytes 786440 | tf_op jit(solution)/shard_map/ppermute | solution.py:196
  71.6 6.6 %collective-permute-start.21 = (bf16[32,4096]{1,0:T(8,128)(2,1)S(1)}, bf16[32,4096]{1,0:T(8,128)(2,1)S(1)}, u32[]{:S(2)}, u32[]{:S(2)}) collective-permute-start(bf16[32,4096]{1,0:T(8,128)(2,1)S(1)} %fusion.38), channel_id=1, source_target_pairs={{12,8},{13,9},{14,10},{15,11},{28,24},{29,25},{30,26},{31,27}} | collective-permute-start | bytes 786440 | tf_op jit(solution)/shard_map/ppermute | solution.py:197
  72.2 11.2 %collective-permute-start.14 = (bf16[32,4096]{1,0:T(8,128)(2,1)S(1)}, bf16[32,4096]{1,0:T(8,128)(2,1)S(1)}, u32[]{:S(2)}, u32[]{:S(2)}) collective-permute-start(bf16[32,4096]{1,0:T(8,128)(2,1)S(1)} %get-tuple-element.16), channel_id=1, source_target_pairs={{0,2},{1,3},{2,0},{3,1},{4,6},{5,7},{6,4},{7,5},{8,10},{9,11},{10,... | collective-permute-start | bytes 786440 | tf_op jit(solution)/shard_map/ppermute | solution.py:161
  73.6 9.9 %collective-permute-start.19 = (bf16[32,4096]{1,0:T(8,128)(2,1)S(1)}, bf16[32,4096]{1,0:T(8,128)(2,1)S(1)}, u32[]{:S(2)}, u32[]{:S(2)}) collective-permute-start(bf16[32,4096]{1,0:T(8,128)(2,1)S(1)} %get-tuple-element.13), channel_id=1, source_target_pairs={{0,2},{1,3},{2,0},{3,1},{4,6},{5,7},{6,4},{7,5},{8,10},{9,11},{10,... | collective-permute-start | bytes 786440 | tf_op jit(solution)/shard_map/ppermute | solution.py:161
  78.3 8.4 %collective-permute-start.18 = (bf16[32,4096]{1,0:T(8,128)(2,1)S(1)}, bf16[32,4096]{1,0:T(8,128)(2,1)S(1)}, u32[]{:S(2)}, u32[]{:S(2)}) collective-permute-start(bf16[32,4096]{1,0:T(8,128)(2,1)S(1)} %get-tuple-element.9), channel_id=1, source_target_pairs={{0,4},{1,5},{2,6},{3,7},{4,8},{5,9},{6,10},{7,11},{16,20},{17,21},... | collective-permute-start | bytes 786440 | tf_op jit(solution)/shard_map/ppermute | solution.py:200
  82.7 4.0 %collective-permute-start.22 = (bf16[32,4096]{1,0:T(8,128)(2,1)S(1)}, bf16[32,4096]{1,0:T(8,128)(2,1)S(1)}, u32[]{:S(2)}, u32[]{:S(2)}) collective-permute-start(bf16[32,4096]{1,0:T(8,128)(2,1)S(1)} %get-tuple-element.10), channel_id=1, source_target_pairs={{8,4},{9,5},{10,6},{11,7},{12,8},{13,9},{14,10},{15,11},{24,20},{2... | collective-permute-start | bytes 786440 | tf_op jit(solution)/shard_map/ppermute | solution.py:203
  86.9 10.1 %collective-permute-start.20 = (bf16[32,4096]{1,0:T(8,128)(2,1)S(1)}, bf16[32,4096]{1,0:T(8,128)(2,1)S(1)}, u32[]{:S(2)}, u32[]{:S(2)}) collective-permute-start(bf16[32,4096]{1,0:T(8,128)(2,1)S(1)} %get-tuple-element.7), channel_id=1, source_target_pairs={{0,4},{1,5},{2,6},{3,7},{4,8},{5,9},{6,10},{7,11},{8,12},{9,13},{1... | collective-permute-start | bytes 786440 | tf_op jit(solution)/shard_map/ppermute | solution.py:209
  93.2 8.3 %collective-permute-start.23 = (bf16[32,4096]{1,0:T(8,128)(2,1)S(1)}, bf16[32,4096]{1,0:T(8,128)(2,1)S(1)}, u32[]{:S(2)}, u32[]{:S(2)}) collective-permute-start(bf16[32,4096]{1,0:T(8,128)(2,1)S(1)} %get-tuple-element.8), channel_id=1, source_target_pairs={{4,0},{5,1},{6,2},{7,3},{8,4},{9,5},{10,6},{11,7},{12,8},{13,9},{1... | collective-permute-start | bytes 786440 | tf_op jit(solution)/shard_map/ppermute | solution.py:212
  102.8 1.0 copy-start.1
  102.8 1.2 %copy-start.2 = (bf16[128,2048]{1,0:T(8,128)(2,1)S(1)}, bf16[128,2048]{1,0:T(8,128)(2,1)}, u32[]{:S(2)}) copy-start(bf16[128,2048]{1,0:T(8,128)(2,1)} %param.10) | copy-start | bytes 1572868

commit v20 on v19

--- a/solution.py
+++ b/solution.py
@@ -287,10 +287,10 @@
     summed = topo_reduce_scatter(jnp.concatenate([weighted_out, weighted_grad], axis=1), experts)
     combined = summed[:, :model_width]
     centroid_grad = summed[:, model_width:] - grad_sum
-    layer_out = tokens.astype(jnp.float32) + jnp.take(combined - centroid, cluster_ids, axis=0)
-    token_grad = out_grad.astype(jnp.float32) + jnp.take(
-        centroid_grad / counts[:, None], cluster_ids, axis=0
-    )
+    table = jnp.concatenate([combined - centroid, centroid_grad / counts[:, None]], axis=1)
+    spread = jnp.dot(member.astype(jnp.float32), table, precision=lax.Precision.HIGHEST)
+    layer_out = tokens.astype(jnp.float32) + spread[:, :model_width]
+    token_grad = out_grad.astype(jnp.float32) + spread[:, model_width:]
     return (layer_out, token_grad)
 
 

time: 106 us -> 105 us (level)
  local copies, waits for them, and re-layouts: 4.14 us -> 2.05 us
    gather x2 -> x0, local copies, waits for them, and re-layouts: 1.95 us -> none  [the longest x1 0.98 us: per_device_dense(): jnp.take(combined - centroid, cluster_ids, axis=0)]
where the time goes in v20:
time: 105 us; the launch traced here: 104 us
  waiting for transfers between devices  40.6 us (39%)
  starting transfers between devices  40.5 us (39%)
  matrix products  14.9 us (14%)
  other arithmetic  5.01 us (5%)
  local copies, waits for them, and re-layouts  2.05 us (2%)
  between operations  1.26 us (1%)
    ppermute x3, waiting for transfers between devices, topo_all_gather(): lax.ppermute(behind, 'expert', [(j, j - 4) for j in range(experts) if 1 <...  13.4 us
    ppermute x4, waiting for transfers between devices, row_sum(): got = lax.ppermute(theirs.astype(jnp.bfloat16), 'expert', pairs)  8.55 us
    ppermute x3, starting transfers between devices, topo_all_gather(): lax.ppermute(ahead, 'expert', [(j, j + 4) for j in range(experts) if step...  6.93 us
    ppermute x1, starting transfers between devices, four_line_sum(): lax.ppermute((ahead + third).astype(jnp.bfloat16), 'expert', [(j, j + 4)...  6.33 us
    ppermute x2, waiting for transfers between devices, topo_all_gather(): lax.ppermute(jnp.where(in_ahead, ahead, behind), 'expert', sorted(ahead_r...  6.15 us
    ppermute x1, waiting for transfers between devices, four_line_sum(): lax.ppermute((behind + behind_part).astype(jnp.bfloat16), 'expert', [(j,...  4.42 us
    ppermute x1, starting transfers between devices, four_line_sum(): lax.ppermute((ahead + second).astype(jnp.bfloat16), 'expert', [(j, j + 4)...  4.4 us
    ppermute x4, starting transfers between devices, row_sum(): got = lax.ppermute(theirs.astype(jnp.bfloat16), 'expert', pairs)  4.18 us
  transfers between devices with their start and end apart: 24, of which 11 were waited for; matrix products, arithmetic and copies ran while one was open for 10% of the time, Pallas kernels for 0%

profile of v20, /device:TPU:0, one launch (start us, length us, event | category | flops | bytes accessed | tf_op | source)
XLA Modules:
  0.0 104.4 jit_solution(11400006283872980629)
XLA Ops:
  1.4 1.5 %fusion.13 = f32[32,4096]{1,0:T(8,128)S(1)} fusion(bf16[128,2048]{1,0:T(8,128)(2,1)} %param.9, bf16[128,2048]{1,0:T(8,128)(2,1)} %param.8, s32[128]{0:T(128)} %param.10), kind=kOutput, calls=%fused_computation.25 | convolution fusion | flops 35655680 | bytes 1573376 | tf_op jit(solution)/shard_map/dot_general | solution.py:246
  3.2 1.3 %collective-permute-start = (bf16[32,4224]{1,0:T(8,128)(2,1)S(1)}, bf16[32,4224]{1,0:T(8,128)(2,1)S(1)}, u32[]{:S(2)}, u32[]{:S(2)}) collective-permute-start(bf16[32,4224]{1,0:T(8,128)(2,1)S(1)} %fusion.43), channel_id=1, source_target_pairs={{4,0},{5,1},{6,2},{7,3},{8,4},{9,5},{10,6},{11,7},{12,8},{13,9},{1... | collective-permute-start | bytes 811016 | tf_op jit(solution)/shard_map/ppermute | solution.py:125
  4.5 5.6 %collective-permute-start.3 = (bf16[32,4224]{1,0:T(8,128)(2,1)S(1)}, bf16[32,4224]{1,0:T(8,128)(2,1)S(1)}, u32[]{:S(2)}, u32[]{:S(2)}) collective-permute-start(bf16[32,4224]{1,0:T(8,128)(2,1)S(1)} %fusion.43), channel_id=1, source_target_pairs={{0,4},{1,5},{2,6},{3,7},{4,8},{5,9},{6,10},{7,11},{8,12},{9,13},{1... | collective-permute-start | bytes 811016 | tf_op jit(solution)/shard_map/ppermute | solution.py:120
  10.1 2.0 %collective-permute-start.10 = (bf16[32,4224]{1,0:T(8,128)(2,1)S(1)}, bf16[32,4224]{1,0:T(8,128)(2,1)S(1)}, u32[]{:S(2)}, u32[]{:S(2)}) collective-permute-start(bf16[32,4224]{1,0:T(8,128)(2,1)S(1)} %fusion.43), channel_id=1, source_target_pairs={{0,2},{1,3},{2,0},{3,1},{4,6},{5,7},{6,4},{7,5},{8,10},{9,11},{10,... | collective-permute-start | bytes 811016 | tf_op jit(solution)/shard_map/ppermute | solution.py:117
  12.2 2.5 %collective-permute-done = bf16[32,4224]{1,0:T(8,128)(2,1)S(1)} collective-permute-done((bf16[32,4224]{1,0:T(8,128)(2,1)S(1)}, bf16[32,4224]{1,0:T(8,128)(2,1)S(1)}, u32[]{:S(2)}, u32[]{:S(2)}) %collective-permute-start) | collective-permute-done | bytes 270368 | tf_op jit(solution)/shard_map/ppermute | solution.py:125
  14.6 1.3 %collective-permute-start.1 = (bf16[32,4224]{1,0:T(8,128)(2,1)S(1)}, bf16[32,4224]{1,0:T(8,128)(2,1)S(1)}, u32[]{:S(2)}, u32[]{:S(2)}) collective-permute-start(bf16[32,4224]{1,0:T(8,128)(2,1)S(1)} %collective-permute-done), channel_id=1, source_target_pairs={{4,0},{5,1},{6,2},{7,3},{8,4},{9,5},{10,6},{11,7},{20,16},{21,17},... | collective-permute-start | bytes 811016 | tf_op jit(solution)/shard_map/ppermute | solution.py:125
  16.7 3.6 %collective-permute-start.8 = (bf16[32,4224]{1,0:T(8,128)(2,1)S(1)}, bf16[32,4224]{1,0:T(8,128)(2,1)S(1)}, u32[]{:S(2)}, u32[]{:S(2)}) collective-permute-start(bf16[32,4224]{1,0:T(8,128)(2,1)S(1)} %collective-permute-done), channel_id=1, source_target_pairs={{0,2},{1,3},{2,0},{3,1},{4,6},{5,7},{6,4},{7,5},{8,10},{9,11},{10,... | collective-permute-start | bytes 811016 | tf_op jit(solution)/shard_map/ppermute | solution.py:143
  21.0 3.2 %collective-permute-done.1 = bf16[32,4224]{1,0:T(8,128)(2,1)S(1)} collective-permute-done((bf16[32,4224]{1,0:T(8,128)(2,1)S(1)}, bf16[32,4224]{1,0:T(8,128)(2,1)S(1)}, u32[]{:S(2)}, u32[]{:S(2)}) %collective-permute-start.1) | collective-permute-done | bytes 270368 | tf_op jit(solution)/shard_map/ppermute | solution.py:125
  24.2 1.3 %collective-permute-start.2 = (bf16[32,4224]{1,0:T(8,128)(2,1)S(1)}, bf16[32,4224]{1,0:T(8,128)(2,1)S(1)}, u32[]{:S(2)}, u32[]{:S(2)}) collective-permute-start(bf16[32,4224]{1,0:T(8,128)(2,1)S(1)} %collective-permute-done.1), channel_id=1, source_target_pairs={{4,0},{5,1},{6,2},{7,3},{20,16},{21,17},{22,18},{23,19}} | collective-permute-start | bytes 811016 | tf_op jit(solution)/shard_map/ppermute | solution.py:125
  26.2 7.8 %collective-permute-done.2 = bf16[32,4224]{1,0:T(8,128)(2,1)S(1)} collective-permute-done((bf16[32,4224]{1,0:T(8,128)(2,1)S(1)}, bf16[32,4224]{1,0:T(8,128)(2,1)S(1)}, u32[]{:S(2)}, u32[]{:S(2)}) %collective-permute-start.2) | collective-permute-done | bytes 270368 | tf_op jit(solution)/shard_map/ppermute | solution.py:125
  34.0 1.5 %collective-permute-start.7 = (bf16[32,4224]{1,0:T(8,128)(2,1)S(1)}, bf16[32,4224]{1,0:T(8,128)(2,1)S(1)}, u32[]{:S(2)}, u32[]{:S(2)}) collective-permute-start(bf16[32,4224]{1,0:T(8,128)(2,1)S(1)} %broadcast_select_fusion), channel_id=1, source_target_pairs={{0,2},{1,3},{2,0},{3,1},{4,6},{5,7},{6,4},{7,5},{8,10},{9,11},{10,... | collective-permute-start | bytes 811016 | tf_op jit(solution)/shard_map/ppermute | solution.py:136
  35.6 2.4 %collective-permute-start.6 = (bf16[32,4224]{1,0:T(8,128)(2,1)S(1)}, bf16[32,4224]{1,0:T(8,128)(2,1)S(1)}, u32[]{:S(2)}, u32[]{:S(2)}) collective-permute-start(bf16[32,4224]{1,0:T(8,128)(2,1)S(1)} %broadcast_select_fusion.1), channel_id=1, source_target_pairs={{0,2},{1,3},{2,0},{3,1},{12,14},{13,15},{14,12},{15,13},{16,18},{1... | collective-permute-start | bytes 811016 | tf_op jit(solution)/shard_map/ppermute | solution.py:136
  39.2 3.3 %collective-permute-done.7 = bf16[32,4224]{1,0:T(8,128)(2,1)S(1)} collective-permute-done((bf16[32,4224]{1,0:T(8,128)(2,1)S(1)}, bf16[32,4224]{1,0:T(8,128)(2,1)S(1)}, u32[]{:S(2)}, u32[]{:S(2)}) %collective-permute-start.7) | collective-permute-done | bytes 270368 | tf_op jit(solution)/shard_map/ppermute | solution.py:136
  42.5 2.9 %collective-permute-done.6 = bf16[32,4224]{1,0:T(8,128)(2,1)S(1)} collective-permute-done((bf16[32,4224]{1,0:T(8,128)(2,1)S(1)}, bf16[32,4224]{1,0:T(8,128)(2,1)S(1)}, u32[]{:S(2)}, u32[]{:S(2)}) %collective-permute-start.6) | collective-permute-done | bytes 270368 | tf_op jit(solution)/shard_map/ppermute | solution.py:136
  51.1 1.1 %fusion.11 = f32[256,2048]{1,0:T(8,128)S(1)} fusion(f32[256]{0:T(256)S(1)} %get-tuple-element.3, f32[256,768]{1,0:T(8,128)S(1)} %fusion.25, f32[256,768]{1,0:T(8,128)S(1)} %fusion.27, bf16[1,768,2048]{2,1,0:T(8,128)(2,1)S(1)} %copy-done.7), kind=kOutput, calls=%fused_computation.17 | convolution fusion | flops 808058880 | bytes 6816768 | tf_op jit(solution)/shard_map/dot_general | solution.py:224
  52.2 1.1 %fusion.34 = f32[256,2048]{1,0:T(8,128)S(1)} fusion(f32[256,768]{1,0:T(8,128)S(1)} %fusion.27, f32[256,768]{1,0:T(8,128)S(1)} %fusion.19, f32[256,768]{1,0:T(8,128)S(1)} %fusion.25, bf16[1,2048,768]{2,1,0:T(8,128)(2,1)S(1)} %copy-done.6), kind=kOutput, calls=%fused_computation.68 | convolution fusion | flops 807272448 | bytes 7602176 | tf_op jit(solution)/shard_map/dot_general | solution.py:230
  53.3 1.1 %fusion.6 = f32[256,2048]{1,0:T(8,128)S(1)} fusion(f32[256,2048]{1,0:T(8,128)S(1)} %fusion.34, f32[256]{0:T(256)S(1)} %get-tuple-element.3, f32[256,768]{1,0:T(8,128)S(1)} %fusion.19, f32[256,768]{1,0:T(8,128)S(1)} %fusion.27, bf16[1,2048,768]{2,1,0:T(8,128)(2,1)S(1)} %copy-done), kind=kOutput, calls=%fused_computation.10 | convolution fusion | flops 808583168 | bytes 8913920 | tf_op jit(solution)/shard_map/dot_general | solution.py:231
  58.5 1.0 fusion.9
  59.5 1.1 %fusion.4 = f32[256,2048]{1,0:T(8,128)S(1)} fusion(f32[256,2048]{1,0:T(8,128)S(1)} %fusion.6, f32[256,2048]{1,0:T(8,128)S(1)} %fusion.35, bf16[2048,768]{1,0:T(8,128)(2,1)S(1)} %collective-permute-done.11, f32[256]{0:T(256)S(1)} %get-tuple-element.2, f32[256,768]{1,0:T(8,128)S(1)} %fusion.23, f32[256,768]{1,0:T(8,128)S(1)} %fusion.17, f32[256,768]{1,0:T(8,128)S(1)} %fusion.21), kind=kOutput, calls=%fused_computation.8 | convolution fusion | flops 809893888 | bytes 11797504 | tf_op jit(solution)/shard_map/dot_general | solution.py:230
  60.9 1.3 %collective-permute-start.15 = (bf16[32,4096]{1,0:T(8,128)(2,1)S(1)}, bf16[32,4096]{1,0:T(8,128)(2,1)S(1)}, u32[]{:S(2)}, u32[]{:S(2)}) collective-permute-start(bf16[32,4096]{1,0:T(8,128)(2,1)S(1)} %get-tuple-element.16), channel_id=1, source_target_pairs={{0,2},{1,3},{2,0},{3,1},{4,6},{5,7},{6,4},{7,5},{8,10},{9,11},{10,... | collective-permute-start | bytes 786440 | tf_op jit(solution)/shard_map/ppermute | solution.py:161
  63.1 7.1 %collective-permute-done.15 = bf16[32,4096]{1,0:T(8,128)(2,1)S(1)} collective-permute-done((bf16[32,4096]{1,0:T(8,128)(2,1)S(1)}, bf16[32,4096]{1,0:T(8,128)(2,1)S(1)}, u32[]{:S(2)}, u32[]{:S(2)}) %collective-permute-start.15) | collective-permute-done | bytes 262176 | tf_op jit(solution)/shard_map/ppermute | solution.py:161
  70.2 1.3 %collective-permute-start.16 = (bf16[32,4096]{1,0:T(8,128)(2,1)S(1)}, bf16[32,4096]{1,0:T(8,128)(2,1)S(1)}, u32[]{:S(2)}, u32[]{:S(2)}) collective-permute-start(bf16[32,4096]{1,0:T(8,128)(2,1)S(1)} %fusion.42), channel_id=1, source_target_pairs={{0,4},{1,5},{2,6},{3,7},{16,20},{17,21},{18,22},{19,23}} | collective-permute-start | bytes 786440 | tf_op jit(solution)/shard_map/ppermute | solution.py:196
  72.2 1.3 %collective-permute-start.14 = (bf16[32,4096]{1,0:T(8,128)(2,1)S(1)}, bf16[32,4096]{1,0:T(8,128)(2,1)S(1)}, u32[]{:S(2)}, u32[]{:S(2)}) collective-permute-start(bf16[32,4096]{1,0:T(8,128)(2,1)S(1)} %get-tuple-element.17), channel_id=1, source_target_pairs={{0,2},{1,3},{2,0},{3,1},{4,6},{5,7},{6,4},{7,5},{8,10},{9,11},{10,... | collective-permute-start | bytes 786440 | tf_op jit(solution)/shard_map/ppermute | solution.py:161
  74.3 1.5 %collective-permute-done.17 = bf16[32,4096]{1,0:T(8,128)(2,1)S(1)} collective-permute-done((bf16[32,4096]{1,0:T(8,128)(2,1)S(1)}, bf16[32,4096]{1,0:T(8,128)(2,1)S(1)}, u32[]{:S(2)}, u32[]{:S(2)}) %collective-permute-start.17) | collective-permute-done | bytes 262176 | tf_op jit(solution)/shard_map/ppermute | solution.py:161
  75.8 2.4 %collective-permute-done.16 = bf16[32,4096]{1,0:T(8,128)(2,1)S(1)} collective-permute-done((bf16[32,4096]{1,0:T(8,128)(2,1)S(1)}, bf16[32,4096]{1,0:T(8,128)(2,1)S(1)}, u32[]{:S(2)}, u32[]{:S(2)}) %collective-permute-start.16) | collective-permute-done | bytes 262176 | tf_op jit(solution)/shard_map/ppermute | solution.py:196
  78.3 4.4 %collective-permute-start.18 = (bf16[32,4096]{1,0:T(8,128)(2,1)S(1)}, bf16[32,4096]{1,0:T(8,128)(2,1)S(1)}, u32[]{:S(2)}, u32[]{:S(2)}) collective-permute-start(bf16[32,4096]{1,0:T(8,128)(2,1)S(1)} %get-tuple-element.8), channel_id=1, source_target_pairs={{0,4},{1,5},{2,6},{3,7},{4,8},{5,9},{6,10},{7,11},{16,20},{17,21},... | collective-permute-start | bytes 786440 | tf_op jit(solution)/shard_map/ppermute | solution.py:200
  83.4 3.2 %collective-permute-done.18 = bf16[32,4096]{1,0:T(8,128)(2,1)S(1)} collective-permute-done((bf16[32,4096]{1,0:T(8,128)(2,1)S(1)}, bf16[32,4096]{1,0:T(8,128)(2,1)S(1)}, u32[]{:S(2)}, u32[]{:S(2)}) %collective-permute-start.18) | collective-permute-done | bytes 262176 | tf_op jit(solution)/shard_map/ppermute | solution.py:200
  86.8 6.3 %collective-permute-start.20 = (bf16[32,4096]{1,0:T(8,128)(2,1)S(1)}, bf16[32,4096]{1,0:T(8,128)(2,1)S(1)}, u32[]{:S(2)}, u32[]{:S(2)}) collective-permute-start(bf16[32,4096]{1,0:T(8,128)(2,1)S(1)} %get-tuple-element.6), channel_id=1, source_target_pairs={{0,4},{1,5},{2,6},{3,7},{4,8},{5,9},{6,10},{7,11},{8,12},{9,13},{1... | collective-permute-start | bytes 786440 | tf_op jit(solution)/shard_map/ppermute | solution.py:209
  93.1 1.3 %collective-permute-start.23 = (bf16[32,4096]{1,0:T(8,128)(2,1)S(1)}, bf16[32,4096]{1,0:T(8,128)(2,1)S(1)}, u32[]{:S(2)}, u32[]{:S(2)}) collective-permute-start(bf16[32,4096]{1,0:T(8,128)(2,1)S(1)} %get-tuple-element.7), channel_id=1, source_target_pairs={{4,0},{5,1},{6,2},{7,3},{8,4},{9,5},{10,6},{11,7},{12,8},{13,9},{1... | collective-permute-start | bytes 786440 | tf_op jit(solution)/shard_map/ppermute | solution.py:212
  94.4 2.5 %collective-permute-done.20 = bf16[32,4096]{1,0:T(8,128)(2,1)S(1)} collective-permute-done((bf16[32,4096]{1,0:T(8,128)(2,1)S(1)}, bf16[32,4096]{1,0:T(8,128)(2,1)S(1)}, u32[]{:S(2)}, u32[]{:S(2)}) %collective-permute-start.20) | collective-permute-done | bytes 262176 | tf_op jit(solution)/shard_map/ppermute | solution.py:209
  97.0 4.4 %collective-permute-done.23 = bf16[32,4096]{1,0:T(8,128)(2,1)S(1)} collective-permute-done((bf16[32,4096]{1,0:T(8,128)(2,1)S(1)}, bf16[32,4096]{1,0:T(8,128)(2,1)S(1)}, u32[]{:S(2)}, u32[]{:S(2)}) %collective-permute-start.23) | collective-permute-done | bytes 262176 | tf_op jit(solution)/shard_map/ppermute | solution.py:212
  102.8 1.6 %slice_add_fusion = (f32[128,2048]{1,0:T(8,128)}, f32[128,2048]{1,0:T(8,128)}) fusion(f32[128,4096]{1,0:T(8,128)S(1)} %fusion.30, bf16[128,2048]{1,0:T(8,128)(2,1)S(1)} %copy-done.1, bf16[128,2048]{1,0:T(8,128)(2,1)S(1)} %copy-done.2), kind=kLoop, calls=%fused_computation.23 | loop fusion | flops 1048576 | bytes 5242880 | tf_op jit(solution)/shard_map/add | solution.py:293
  (76 shorter events, 19.1 us)
Async XLA Ops:
  0.6 2.4 %copy-start.4 = (s32[32,8]{0,1:T(8,128)S(1)}, s32[32,8]{0,1:T(8,128)}, u32[]{:S(2)}) copy-start(s32[32,8]{0,1:T(8,128)} %param.11) | copy-start | bytes 3076
  0.6 2.4 %copy-start.3 = (f32[32,8]{0,1:T(8,128)S(1)}, f32[32,8]{0,1:T(8,128)}, u32[]{:S(2)}) copy-start(f32[32,8]{0,1:T(8,128)} %param.12) | copy-start | bytes 3076
  3.2 11.4 %collective-permute-start = (bf16[32,4224]{1,0:T(8,128)(2,1)S(1)}, bf16[32,4224]{1,0:T(8,128)(2,1)S(1)}, u32[]{:S(2)}, u32[]{:S(2)}) collective-permute-start(bf16[32,4224]{1,0:T(8,128)(2,1)S(1)} %fusion.43), channel_id=1, source_target_pairs={{4,0},{5,1},{6,2},{7,3},{8,4},{9,5},{10,6},{11,7},{12,8},{13,9},{1... | collective-permute-start | bytes 811016 | tf_op jit(solution)/shard_map/ppermute | solution.py:125
  4.5 11.4 %collective-permute-start.3 = (bf16[32,4224]{1,0:T(8,128)(2,1)S(1)}, bf16[32,4224]{1,0:T(8,128)(2,1)S(1)}, u32[]{:S(2)}, u32[]{:S(2)}) collective-permute-start(bf16[32,4224]{1,0:T(8,128)(2,1)S(1)} %fusion.43), channel_id=1, source_target_pairs={{0,4},{1,5},{2,6},{3,7},{4,8},{5,9},{6,10},{7,11},{8,12},{9,13},{1... | collective-permute-start | bytes 811016 | tf_op jit(solution)/shard_map/ppermute | solution.py:120
  10.1 28.4 %collective-permute-start.10 = (bf16[32,4224]{1,0:T(8,128)(2,1)S(1)}, bf16[32,4224]{1,0:T(8,128)(2,1)S(1)}, u32[]{:S(2)}, u32[]{:S(2)}) collective-permute-start(bf16[32,4224]{1,0:T(8,128)(2,1)S(1)} %fusion.43), channel_id=1, source_target_pairs={{0,2},{1,3},{2,0},{3,1},{4,6},{5,7},{6,4},{7,5},{8,10},{9,11},{10,... | collective-permute-start | bytes 811016 | tf_op jit(solution)/shard_map/ppermute | solution.py:117
  14.6 9.6 %collective-permute-start.1 = (bf16[32,4224]{1,0:T(8,128)(2,1)S(1)}, bf16[32,4224]{1,0:T(8,128)(2,1)S(1)}, u32[]{:S(2)}, u32[]{:S(2)}) collective-permute-start(bf16[32,4224]{1,0:T(8,128)(2,1)S(1)} %collective-permute-done), channel_id=1, source_target_pairs={{4,0},{5,1},{6,2},{7,3},{8,4},{9,5},{10,6},{11,7},{20,16},{21,17},... | collective-permute-start | bytes 811016 | tf_op jit(solution)/shard_map/ppermute | solution.py:125
  15.9 9.5 %collective-permute-start.4 = (bf16[32,4224]{1,0:T(8,128)(2,1)S(1)}, bf16[32,4224]{1,0:T(8,128)(2,1)S(1)}, u32[]{:S(2)}, u32[]{:S(2)}) collective-permute-start(bf16[32,4224]{1,0:T(8,128)(2,1)S(1)} %collective-permute-done.3), channel_id=1, source_target_pairs={{4,8},{5,9},{6,10},{7,11},{8,12},{9,13},{10,14},{11,15},{20,24},{2... | collective-permute-start | bytes 811016 | tf_op jit(solution)/shard_map/ppermute | solution.py:120
  16.7 21.9 %collective-permute-start.8 = (bf16[32,4224]{1,0:T(8,128)(2,1)S(1)}, bf16[32,4224]{1,0:T(8,128)(2,1)S(1)}, u32[]{:S(2)}, u32[]{:S(2)}) collective-permute-start(bf16[32,4224]{1,0:T(8,128)(2,1)S(1)} %collective-permute-done), channel_id=1, source_target_pairs={{0,2},{1,3},{2,0},{3,1},{4,6},{5,7},{6,4},{7,5},{8,10},{9,11},{10,... | collective-permute-start | bytes 811016 | tf_op jit(solution)/shard_map/ppermute | solution.py:143
  20.3 18.8 %collective-permute-start.9 = (bf16[32,4224]{1,0:T(8,128)(2,1)S(1)}, bf16[32,4224]{1,0:T(8,128)(2,1)S(1)}, u32[]{:S(2)}, u32[]{:S(2)}) collective-permute-start(bf16[32,4224]{1,0:T(8,128)(2,1)S(1)} %collective-permute-done.3), channel_id=1, source_target_pairs={{4,6},{5,7},{6,4},{7,5},{8,10},{9,11},{10,8},{11,9},{12,14},{13,15... | collective-permute-start | bytes 811016 | tf_op jit(solution)/shard_map/ppermute | solution.py:142
  24.2 9.8 %collective-permute-start.2 = (bf16[32,4224]{1,0:T(8,128)(2,1)S(1)}, bf16[32,4224]{1,0:T(8,128)(2,1)S(1)}, u32[]{:S(2)}, u32[]{:S(2)}) collective-permute-start(bf16[32,4224]{1,0:T(8,128)(2,1)S(1)} %collective-permute-done.1), channel_id=1, source_target_pairs={{4,0},{5,1},{6,2},{7,3},{20,16},{21,17},{22,18},{23,19}} | collective-permute-start | bytes 811016 | tf_op jit(solution)/shard_map/ppermute | solution.py:125
  25.5 10.0 %collective-permute-start.5 = (bf16[32,4224]{1,0:T(8,128)(2,1)S(1)}, bf16[32,4224]{1,0:T(8,128)(2,1)S(1)}, u32[]{:S(2)}, u32[]{:S(2)}) collective-permute-start(bf16[32,4224]{1,0:T(8,128)(2,1)S(1)} %collective-permute-done.4), channel_id=1, source_target_pairs={{8,12},{9,13},{10,14},{11,15},{24,28},{25,29},{26,30},{27,31}} | collective-permute-start | bytes 811016 | tf_op jit(solution)/shard_map/ppermute | solution.py:120
  26.2 12.3 %copy-start = (bf16[1,2048,768]{2,1,0:T(8,128)(2,1)S(1)}, bf16[1,2048,768]{2,1,0:T(8,128)(2,1)}, u32[]{:S(2)}) copy-start(bf16[1,2048,768]{2,1,0:T(8,128)(2,1)} %param.14) | copy-start | bytes 9437188
  34.0 8.5 %collective-permute-start.7 = (bf16[32,4224]{1,0:T(8,128)(2,1)S(1)}, bf16[32,4224]{1,0:T(8,128)(2,1)S(1)}, u32[]{:S(2)}, u32[]{:S(2)}) collective-permute-start(bf16[32,4224]{1,0:T(8,128)(2,1)S(1)} %broadcast_select_fusion), channel_id=1, source_target_pairs={{0,2},{1,3},{2,0},{3,1},{4,6},{5,7},{6,4},{7,5},{8,10},{9,11},{10,... | collective-permute-start | bytes 811016 | tf_op jit(solution)/shard_map/ppermute | solution.py:136
  35.6 9.8 %collective-permute-start.6 = (bf16[32,4224]{1,0:T(8,128)(2,1)S(1)}, bf16[32,4224]{1,0:T(8,128)(2,1)S(1)}, u32[]{:S(2)}, u32[]{:S(2)}) collective-permute-start(bf16[32,4224]{1,0:T(8,128)(2,1)S(1)} %broadcast_select_fusion.1), channel_id=1, source_target_pairs={{0,2},{1,3},{2,0},{3,1},{12,14},{13,15},{14,12},{15,13},{16,18},{1... | collective-permute-start | bytes 811016 | tf_op jit(solution)/shard_map/ppermute | solution.py:136
  38.6 15.8 %collective-permute-start.12 = (bf16[2048,768]{1,0:T(8,128)(2,1)S(1)}, bf16[2048,768]{1,0:T(8,128)(2,1)S(1)}, u32[]{:S(2)}, u32[]{:S(2)}) collective-permute-start(bf16[2048,768]{1,0:T(8,128)(2,1)S(1)} %bitcast.61), channel_id=1, source_target_pairs={{0,1},{1,0},{2,3},{3,2},{4,5},{5,4},{6,7},{7,6},{8,9},{9,8},{10,11... | collective-permute-start | bytes 9437192 | tf_op jit(solution)/shard_map/ppermute | solution.py:277
  38.6 16.7 %collective-permute-start.11 = (bf16[2048,768]{1,0:T(8,128)(2,1)}, bf16[2048,768]{1,0:T(8,128)(2,1)S(1)}, u32[]{:S(2)}, u32[]{:S(2)}) collective-permute-start(bf16[2048,768]{1,0:T(8,128)(2,1)} %bitcast.69), channel_id=1, source_target_pairs={{0,1},{1,0},{2,3},{3,2},{4,5},{5,4},{6,7},{7,6},{8,9},{9,8},{10,11... | collective-permute-start | bytes 9437192 | tf_op jit(solution)/shard_map/ppermute | solution.py:276
  39.1 17.2 %collective-permute-start.13 = (bf16[768,2048]{1,0:T(8,128)(2,1)}, bf16[768,2048]{1,0:T(8,128)(2,1)S(1)}, u32[]{:S(2)}, u32[]{:S(2)}) collective-permute-start(bf16[768,2048]{1,0:T(8,128)(2,1)} %bitcast.70), channel_id=1, source_target_pairs={{0,1},{1,0},{2,3},{3,2},{4,5},{5,4},{6,7},{7,6},{8,9},{9,8},{10,11... | collective-permute-start | bytes 9437192 | tf_op jit(solution)/shard_map/ppermute | solution.py:278
  46.3 1.9 %copy-start.6 = (bf16[1,2048,768]{2,1,0:T(8,128)(2,1)S(1)}, bf16[1,2048,768]{2,1,0:T(8,128)(2,1)}, u32[]{:S(2)}) copy-start(bf16[1,2048,768]{2,1,0:T(8,128)(2,1)} %param.13) | copy-start | bytes 9437188
  48.2 1.9 %copy-start.7 = (bf16[1,768,2048]{2,1,0:T(8,128)(2,1)S(1)}, bf16[1,768,2048]{2,1,0:T(8,128)(2,1)}, u32[]{:S(2)}) copy-start(bf16[1,768,2048]{2,1,0:T(8,128)(2,1)} %param.15) | copy-start | bytes 9437188
  60.9 9.3 %collective-permute-start.15 = (bf16[32,4096]{1,0:T(8,128)(2,1)S(1)}, bf16[32,4096]{1,0:T(8,128)(2,1)S(1)}, u32[]{:S(2)}, u32[]{:S(2)}) collective-permute-start(bf16[32,4096]{1,0:T(8,128)(2,1)S(1)} %get-tuple-element.16), channel_id=1, source_target_pairs={{0,2},{1,3},{2,0},{3,1},{4,6},{5,7},{6,4},{7,5},{8,10},{9,11},{10,... | collective-permute-start | bytes 786440 | tf_op jit(solution)/shard_map/ppermute | solution.py:161
  62.2 13.6 %collective-permute-start.17 = (bf16[32,4096]{1,0:T(8,128)(2,1)S(1)}, bf16[32,4096]{1,0:T(8,128)(2,1)S(1)}, u32[]{:S(2)}, u32[]{:S(2)}) collective-permute-start(bf16[32,4096]{1,0:T(8,128)(2,1)S(1)} %get-tuple-element.15), channel_id=1, source_target_pairs={{0,2},{1,3},{2,0},{3,1},{4,6},{5,7},{6,4},{7,5},{8,10},{9,11},{10,... | collective-permute-start | bytes 786440 | tf_op jit(solution)/shard_map/ppermute | solution.py:161
  70.2 7.9 %collective-permute-start.16 = (bf16[32,4096]{1,0:T(8,128)(2,1)S(1)}, bf16[32,4096]{1,0:T(8,128)(2,1)S(1)}, u32[]{:S(2)}, u32[]{:S(2)}) collective-permute-start(bf16[32,4096]{1,0:T(8,128)(2,1)S(1)} %fusion.42), channel_id=1, source_target_pairs={{0,4},{1,5},{2,6},{3,7},{16,20},{17,21},{18,22},{19,23}} | collective-permute-start | bytes 786440 | tf_op jit(solution)/shard_map/ppermute | solution.py:196
  71.6 6.6 %collective-permute-start.21 = (bf16[32,4096]{1,0:T(8,128)(2,1)S(1)}, bf16[32,4096]{1,0:T(8,128)(2,1)S(1)}, u32[]{:S(2)}, u32[]{:S(2)}) collective-permute-start(bf16[32,4096]{1,0:T(8,128)(2,1)S(1)} %fusion.42), channel_id=1, source_target_pairs={{12,8},{13,9},{14,10},{15,11},{28,24},{29,25},{30,26},{31,27}} | collective-permute-start | bytes 786440 | tf_op jit(solution)/shard_map/ppermute | solution.py:197
  72.2 11.2 %collective-permute-start.14 = (bf16[32,4096]{1,0:T(8,128)(2,1)S(1)}, bf16[32,4096]{1,0:T(8,128)(2,1)S(1)}, u32[]{:S(2)}, u32[]{:S(2)}) collective-permute-start(bf16[32,4096]{1,0:T(8,128)(2,1)S(1)} %get-tuple-element.17), channel_id=1, source_target_pairs={{0,2},{1,3},{2,0},{3,1},{4,6},{5,7},{6,4},{7,5},{8,10},{9,11},{10,... | collective-permute-start | bytes 786440 | tf_op jit(solution)/shard_map/ppermute | solution.py:161
  73.5 9.9 %collective-permute-start.19 = (bf16[32,4096]{1,0:T(8,128)(2,1)S(1)}, bf16[32,4096]{1,0:T(8,128)(2,1)S(1)}, u32[]{:S(2)}, u32[]{:S(2)}) collective-permute-start(bf16[32,4096]{1,0:T(8,128)(2,1)S(1)} %get-tuple-element.14), channel_id=1, source_target_pairs={{0,2},{1,3},{2,0},{3,1},{4,6},{5,7},{6,4},{7,5},{8,10},{9,11},{10,... | collective-permute-start | bytes 786440 | tf_op jit(solution)/shard_map/ppermute | solution.py:161
  78.3 8.3 %collective-permute-start.18 = (bf16[32,4096]{1,0:T(8,128)(2,1)S(1)}, bf16[32,4096]{1,0:T(8,128)(2,1)S(1)}, u32[]{:S(2)}, u32[]{:S(2)}) collective-permute-start(bf16[32,4096]{1,0:T(8,128)(2,1)S(1)} %get-tuple-element.8), channel_id=1, source_target_pairs={{0,4},{1,5},{2,6},{3,7},{4,8},{5,9},{6,10},{7,11},{16,20},{17,21},... | collective-permute-start | bytes 786440 | tf_op jit(solution)/shard_map/ppermute | solution.py:200
  82.7 3.9 %collective-permute-start.22 = (bf16[32,4096]{1,0:T(8,128)(2,1)S(1)}, bf16[32,4096]{1,0:T(8,128)(2,1)S(1)}, u32[]{:S(2)}, u32[]{:S(2)}) collective-permute-start(bf16[32,4096]{1,0:T(8,128)(2,1)S(1)} %get-tuple-element.9), channel_id=1, source_target_pairs={{8,4},{9,5},{10,6},{11,7},{12,8},{13,9},{14,10},{15,11},{24,20},{2... | collective-permute-start | bytes 786440 | tf_op jit(solution)/shard_map/ppermute | solution.py:203
  86.8 10.2 %collective-permute-start.20 = (bf16[32,4096]{1,0:T(8,128)(2,1)S(1)}, bf16[32,4096]{1,0:T(8,128)(2,1)S(1)}, u32[]{:S(2)}, u32[]{:S(2)}) collective-permute-start(bf16[32,4096]{1,0:T(8,128)(2,1)S(1)} %get-tuple-element.6), channel_id=1, source_target_pairs={{0,4},{1,5},{2,6},{3,7},{4,8},{5,9},{6,10},{7,11},{8,12},{9,13},{1... | collective-permute-start | bytes 786440 | tf_op jit(solution)/shard_map/ppermute | solution.py:209
  93.1 8.6 %copy-start.5 = (s32[128]{0:T(128)S(1)}, s32[128]{0:T(128)}, u32[]{:S(2)}) copy-start(s32[128]{0:T(128)} %param.10) | copy-start | bytes 1540
  93.1 8.3 %collective-permute-start.23 = (bf16[32,4096]{1,0:T(8,128)(2,1)S(1)}, bf16[32,4096]{1,0:T(8,128)(2,1)S(1)}, u32[]{:S(2)}, u32[]{:S(2)}) collective-permute-start(bf16[32,4096]{1,0:T(8,128)(2,1)S(1)} %get-tuple-element.7), channel_id=1, source_target_pairs={{4,0},{5,1},{6,2},{7,3},{8,4},{9,5},{10,6},{11,7},{12,8},{13,9},{1... | collective-permute-start | bytes 786440 | tf_op jit(solution)/shard_map/ppermute | solution.py:212
  101.6 1.2 %copy-start.1 = (bf16[128,2048]{1,0:T(8,128)(2,1)S(1)}, bf16[128,2048]{1,0:T(8,128)(2,1)}, u32[]{:S(2)}) copy-start(bf16[128,2048]{1,0:T(8,128)(2,1)} %param.9) | copy-start | bytes 1572868
  101.6 1.2 %copy-start.2 = (bf16[128,2048]{1,0:T(8,128)(2,1)S(1)}, bf16[128,2048]{1,0:T(8,128)(2,1)}, u32[]{:S(2)}) copy-start(bf16[128,2048]{1,0:T(8,128)(2,1)} %param.8) | copy-start | bytes 1572868

commit v21 on v20

--- a/solution.py
+++ b/solution.py
@@ -114,6 +114,10 @@
     line = me // 4
     swap_row = [(j, j ^ 2) for j in range(experts)]
     here = [(shard, line)]
+    if lines == 4:
+        here, there = four_line_gather(shard, line, swap_row)
+        both = jnp.stack([place(here, lines, shard), place(there, lines, shard)])
+        return both.reshape((lines * 2 * shard.shape[0],) + shard.shape[1:])
     there = [(lax.ppermute(shard, "expert", swap_row), line)]
     ahead, behind = shard, shard
     for step in range(1, lines):
@@ -189,6 +193,41 @@
     return row_sum(line, lambda z: True) + ahead + behind
 
 
+def four_line_gather(shard, line, swap_row):
+    own_row = lax.ppermute(shard, "expert", swap_row)
+    ahead = lax.ppermute(shard, "expert", [(j, j + 4) for j in range(12)])
+    behind = lax.ppermute(shard, "expert", [(j, j - 4) for j in range(4, 16)])
+    ahead_row = lax.ppermute(ahead, "expert", [(j, j ^ 2) for j in range(4, 16)])
+    behind_row = lax.ppermute(behind, "expert", [(j, j ^ 2) for j in range(12)])
+    ahead_two = lax.ppermute(ahead, "expert", [(j, j + 4) for j in range(4, 12)])
+    behind_two = lax.ppermute(behind, "expert", [(j, j - 4) for j in range(4, 12)])
+    second_row = lax.ppermute(jnp.where(line >= 2, ahead_two, behind_two), "expert", swap_row)
+    last_ahead = lax.ppermute(
+        jnp.stack([ahead_two, second_row]), "expert", [(j, j + 4) for j in range(8, 12)]
+    )
+    last_behind = lax.ppermute(
+        jnp.stack([behind_two, second_row]), "expert", [(j, j - 4) for j in range(4, 8)]
+    )
+    here = [
+        (shard, line),
+        (ahead, line - 1),
+        (behind, line + 1),
+        (ahead_two, line - 2),
+        (behind_two, line + 2),
+        (last_ahead[0], line - 3),
+        (last_behind[0], line + 3),
+    ]
+    there = [
+        (own_row, line),
+        (ahead_row, line - 1),
+        (behind_row, line + 1),
+        (second_row, jnp.where(line >= 2, line - 2, line + 2)),
+        (last_ahead[1], line - 3),
+        (last_behind[1], line + 3),
+    ]
+    return here, there
+
+
 def four_line_sum(keep, give, line, row_sum):
     experts = 16
     end = (line == 0) | (line == 3)

time: 105 us -> 129 us (1.23)
  starting transfers between devices: 40.5 us -> 49.9 us
  matrix products: 14.9 us -> 22.7 us
  waiting for transfers between devices: 40.6 us -> 46.3 us
    ppermute x1, starting transfers between devices: 6.33 us -> 14.1 us  [four_line_sum(): lax.ppermute((ahead + third).astype(jnp.bfloat16), 'expert', [(j, j + 4)...]
    ppermute x11 -> x10, waiting for transfers between devices: 19.6 us -> 25.7 us  [the longest x1 7.55 us: four_line_gather(): lax.ppermute(behind, 'expert', [(j, j - 4) for j in range(4, 12)])]
    ppermute x1, starting transfers between devices: 1.31 us -> 7.18 us  [four_line_sum(): lax.ppermute(first.astype(jnp.bfloat16), 'expert', [(j, j + 4) for j in r...]
    ppermute x11 -> x10, starting transfers between devices: 21 us -> 16.9 us  [the longest x1 5.57 us: four_line_gather(): ahead = lax.ppermute(shard, 'expert', [(j, j + 4) for j in range(12)])]
    dot_general x2, matrix products: 2.25 us -> 4.28 us  [expert_dense(): lax.dot_general(gate_grad, gate_mat, against, preferred_element_type=jnp....]
    dot_general x2, matrix products: 1.95 us -> 3.88 us  [expert_dense(): up_act = jnp.dot(cent_in, up_mat, preferred_element_type=jnp.float32)]
    dot_general x2, matrix products: 1.97 us -> 3.88 us  [expert_dense(): gate_act = jnp.dot(cent_in, gate_mat, preferred_element_type=jnp.float32)]
    dot_general x2, matrix products: 2.11 us -> 4.01 us  [expert_dense(): lax.dot_general(up_grad, up_mat, against, preferred_element_type=jnp.floa...]
  transfers between devices with their start and end apart: 24 -> 23, of which waited for: 11 -> 9; matrix products, arithmetic and copies ran while one was open for 10% -> 11% of each run, Pallas kernels for 0% -> 0%
where the time goes in v21:
time: 129 us; the launch traced here: 128 us
  starting transfers between devices  49.9 us (39%)
  waiting for transfers between devices  46.3 us (36%)
  matrix products  22.7 us (18%)
  other arithmetic  5.18 us (4%)
  local copies, waits for them, and re-layouts  3.04 us (2%)
    ppermute x1, starting transfers between devices, four_line_sum(): lax.ppermute((ahead + third).astype(jnp.bfloat16), 'expert', [(j, j + 4)...  14.1 us
    ppermute x1, waiting for transfers between devices, four_line_gather(): lax.ppermute(behind, 'expert', [(j, j - 4) for j in range(4, 12)])  7.55 us
    ppermute x1, starting transfers between devices, four_line_sum(): lax.ppermute(first.astype(jnp.bfloat16), 'expert', [(j, j + 4) for j in r...  7.18 us
    ppermute x4, waiting for transfers between devices, row_sum(): got = lax.ppermute(theirs.astype(jnp.bfloat16), 'expert', pairs)  6.94 us
    ppermute x1, waiting for transfers between devices, four_line_gather(): lax.ppermute(jnp.where(line >= 2, ahead_two, behind_two), 'expert', swap_...  6.88 us
    ppermute x1, waiting for transfers between devices, four_line_gather(): lax.ppermute(jnp.stack([behind_two, second_row]), 'expert', [(j, j - 4) f...  6.69 us
    ppermute x1, starting transfers between devices, four_line_gather(): ahead = lax.ppermute(shard, 'expert', [(j, j + 4) for j in range(12)])  5.57 us
    ppermute x1, waiting for transfers between devices, four_line_gather(): behind = lax.ppermute(shard, 'expert', [(j, j - 4) for j in range(4, 16)])  4.53 us
  transfers between devices with their start and end apart: 23, of which 9 were waited for; matrix products, arithmetic and copies ran while one was open for 11% of the time, Pallas kernels for 0%

profile of v21, /device:TPU:0, one launch (start us, length us, event | category | flops | bytes accessed | tf_op | source)
XLA Modules:
  0.0 128.3 jit_solution(1194286139062594864)
XLA Ops:
  1.4 1.5 %fusion.13 = f32[32,4096]{1,0:T(8,128)S(1)} fusion(bf16[128,2048]{1,0:T(8,128)(2,1)} %param.9, bf16[128,2048]{1,0:T(8,128)(2,1)} %param.8, s32[128]{0:T(128)} %param.10), kind=kOutput, calls=%fused_computation.25 | convolution fusion | flops 35655680 | bytes 1573376 | tf_op jit(solution)/shard_map/dot_general | solution.py:285
  3.2 1.3 %collective-permute-start = (bf16[32,4224]{1,0:T(8,128)(2,1)S(1)}, bf16[32,4224]{1,0:T(8,128)(2,1)S(1)}, u32[]{:S(2)}, u32[]{:S(2)}) collective-permute-start(bf16[32,4224]{1,0:T(8,128)(2,1)S(1)} %fusion.43), channel_id=1, source_target_pairs={{4,0},{5,1},{6,2},{7,3},{8,4},{9,5},{10,6},{11,7},{12,8},{13,9},{1... | collective-permute-start | bytes 811016 | tf_op jit(solution)/shard_map/ppermute | solution.py:199
  4.5 5.6 %collective-permute-start.2 = (bf16[32,4224]{1,0:T(8,128)(2,1)S(1)}, bf16[32,4224]{1,0:T(8,128)(2,1)S(1)}, u32[]{:S(2)}, u32[]{:S(2)}) collective-permute-start(bf16[32,4224]{1,0:T(8,128)(2,1)S(1)} %fusion.43), channel_id=1, source_target_pairs={{0,4},{1,5},{2,6},{3,7},{4,8},{5,9},{6,10},{7,11},{8,12},{9,13},{1... | collective-permute-start | bytes 811016 | tf_op jit(solution)/shard_map/ppermute | solution.py:198
  10.1 4.5 %collective-permute-done = bf16[32,4224]{1,0:T(8,128)(2,1)S(1)} collective-permute-done((bf16[32,4224]{1,0:T(8,128)(2,1)S(1)}, bf16[32,4224]{1,0:T(8,128)(2,1)S(1)}, u32[]{:S(2)}, u32[]{:S(2)}) %collective-permute-start) | collective-permute-done | bytes 270368 | tf_op jit(solution)/shard_map/ppermute | solution.py:199
  14.6 1.3 collective-permute-start.1
  16.6 7.5 %collective-permute-done.1 = bf16[32,4224]{1,0:T(8,128)(2,1)S(1)} collective-permute-done((bf16[32,4224]{1,0:T(8,128)(2,1)S(1)}, bf16[32,4224]{1,0:T(8,128)(2,1)S(1)}, u32[]{:S(2)}, u32[]{:S(2)}) %collective-permute-start.1) | collective-permute-done | bytes 270368 | tf_op jit(solution)/shard_map/ppermute | solution.py:203
  24.2 1.4 %collective-permute-start.4 = (bf16[32,4224]{1,0:T(8,128)(2,1)S(1)}, bf16[32,4224]{1,0:T(8,128)(2,1)S(1)}, u32[]{:S(2)}, u32[]{:S(2)}) collective-permute-start(bf16[32,4224]{1,0:T(8,128)(2,1)S(1)} %broadcast_select_fusion), channel_id=1, source_target_pairs={{0,2},{1,3},{2,0},{3,1},{4,6},{5,7},{6,4},{7,5},{8,10},{9,11},{10,... | collective-permute-start | bytes 811016 | tf_op jit(solution)/shard_map/ppermute | solution.py:204
  26.8 6.9 %collective-permute-done.4 = bf16[32,4224]{1,0:T(8,128)(2,1)S(1)} collective-permute-done((bf16[32,4224]{1,0:T(8,128)(2,1)S(1)}, bf16[32,4224]{1,0:T(8,128)(2,1)S(1)}, u32[]{:S(2)}, u32[]{:S(2)}) %collective-permute-start.4) | collective-permute-done | bytes 270368 | tf_op jit(solution)/shard_map/ppermute | solution.py:204
  33.8 1.3 %collective-permute-start.5 = (bf16[2,32,4224]{2,1,0:T(8,128)(2,1)S(1)}, bf16[2,32,4224]{2,1,0:T(8,128)(2,1)S(1)}, u32[]{:S(2)}, u32[]{:S(2)}) collective-permute-start(bf16[2,32,4224]{2,1,0:T(8,128)(2,1)S(1)} %get-tuple-element.22), channel_id=1, source_target_pairs={{4,0},{5,1},{6,2},{7,3},{20,16},{21,17},{22,18},{23,19}} | collective-permute-start | bytes 1622024 | tf_op jit(solution)/shard_map/ppermute | solution.py:208
  35.2 3.2 %collective-permute-start.7 = (bf16[32,4224]{1,0:T(8,128)(2,1)S(1)}, bf16[32,4224]{1,0:T(8,128)(2,1)S(1)}, u32[]{:S(2)}, u32[]{:S(2)}) collective-permute-start(bf16[32,4224]{1,0:T(8,128)(2,1)S(1)} %collective-permute-done), channel_id=1, source_target_pairs={{0,2},{1,3},{2,0},{3,1},{4,6},{5,7},{6,4},{7,5},{8,10},{9,11},{10,... | collective-permute-start | bytes 811016 | tf_op jit(solution)/shard_map/ppermute | solution.py:201
  38.4 6.7 %collective-permute-done.5 = bf16[2,32,4224]{2,1,0:T(8,128)(2,1)S(1)} collective-permute-done((bf16[2,32,4224]{2,1,0:T(8,128)(2,1)S(1)}, bf16[2,32,4224]{2,1,0:T(8,128)(2,1)S(1)}, u32[]{:S(2)}, u32[]{:S(2)}) %collective-permute-start.5) | collective-permute-done | bytes 540704 | tf_op jit(solution)/shard_map/ppermute | solution.py:208
  48.7 1.4 %copy-done = bf16[1,2048,768]{2,1,0:T(8,128)(2,1)S(1)} copy-done((bf16[1,2048,768]{2,1,0:T(8,128)(2,1)S(1)}, bf16[1,2048,768]{2,1,0:T(8,128)(2,1)}, u32[]{:S(2)}) %copy-start) | copy-done | bytes 3145752
  54.0 1.1 fusion.11
  55.0 1.1 fusion.34
  56.2 1.1 fusion.6
  57.3 2.9 %fusion.21 = f32[256,768]{1,0:T(8,128)S(1)} fusion(bf16[2048,768]{1,0:T(8,128)(2,1)} %collective-permute-done.11, bf16[256,4224]{1,0:T(8,128)(2,1)S(1)} %bitcast.79), kind=kOutput, calls=%fused_computation.41 | convolution fusion | flops 805306368 | bytes 4980736 | tf_op jit(solution)/shard_map/dot_general | solution.py:260
  60.2 2.9 %fusion.23 = f32[256,768]{1,0:T(8,128)S(1)} fusion(bf16[2048,768]{1,0:T(8,128)(2,1)} %collective-permute-done.10, bf16[256,4224]{1,0:T(8,128)(2,1)S(1)} %bitcast.80), kind=kOutput, calls=%fused_computation.43 | convolution fusion | flops 805306368 | bytes 4980736 | tf_op jit(solution)/shard_map/dot_general | solution.py:259
  64.1 2.9 %fusion.35 = f32[256,2048]{1,0:T(8,128)S(1)} fusion(bf16[2048,768]{1,0:T(8,128)(2,1)} %collective-permute-done.11, f32[256,768]{1,0:T(8,128)S(1)} %fusion.17, f32[256,768]{1,0:T(8,128)S(1)} %fusion.23), kind=kOutput, calls=%fused_computation.71 | convolution fusion | flops 806486016 | bytes 6815744 | tf_op jit(solution)/shard_map/dot_general | solution.py:270
  67.1 1.1 fusion.9
  68.2 3.2 %fusion.4 = f32[256,2048]{1,0:T(8,128)S(1)} fusion(f32[256,2048]{1,0:T(8,128)S(1)} %fusion.6, f32[256,2048]{1,0:T(8,128)S(1)} %fusion.35, bf16[2048,768]{1,0:T(8,128)(2,1)} %collective-permute-done.10, f32[256]{0:T(256)S(1)} %get-tuple-element.2, f32[256,768]{1,0:T(8,128)S(1)} %fusion.23, f32[256,768]{1,0:T(8,128)S(1)} %fusion.17, f32[256,768]{1,0:T(8,128)S(1)} %fusion.21), kind=kOutput, calls=%fused_computation.8 | convolution fusion | flops 809893888 | bytes 11797504 | tf_op jit(solution)/shard_map/dot_general | solution.py:269
  71.6 1.3 %collective-permute-start.14 = (bf16[32,4096]{1,0:T(8,128)(2,1)S(1)}, bf16[32,4096]{1,0:T(8,128)(2,1)S(1)}, u32[]{:S(2)}, u32[]{:S(2)}) collective-permute-start(bf16[32,4096]{1,0:T(8,128)(2,1)S(1)} %get-tuple-element.16), channel_id=1, source_target_pairs={{0,2},{1,3},{2,0},{3,1},{4,6},{5,7},{6,4},{7,5},{8,10},{9,11},{10,... | collective-permute-start | bytes 786440 | tf_op jit(solution)/shard_map/ppermute | solution.py:165
  73.8 6.9 %collective-permute-done.14 = bf16[32,4096]{1,0:T(8,128)(2,1)S(1)} collective-permute-done((bf16[32,4096]{1,0:T(8,128)(2,1)S(1)}, bf16[32,4096]{1,0:T(8,128)(2,1)S(1)}, u32[]{:S(2)}, u32[]{:S(2)}) %collective-permute-start.14) | collective-permute-done | bytes 262176 | tf_op jit(solution)/shard_map/ppermute | solution.py:165
  80.8 7.2 %collective-permute-start.15 = (bf16[32,4096]{1,0:T(8,128)(2,1)S(1)}, bf16[32,4096]{1,0:T(8,128)(2,1)S(1)}, u32[]{:S(2)}, u32[]{:S(2)}) collective-permute-start(bf16[32,4096]{1,0:T(8,128)(2,1)S(1)} %fusion.42), channel_id=1, source_target_pairs={{0,4},{1,5},{2,6},{3,7},{16,20},{17,21},{18,22},{19,23}} | collective-permute-start | bytes 786440 | tf_op jit(solution)/shard_map/ppermute | solution.py:235
  89.5 1.3 collective-permute-start.18
  90.8 3.6 %collective-permute-done.15 = bf16[32,4096]{1,0:T(8,128)(2,1)S(1)} collective-permute-done((bf16[32,4096]{1,0:T(8,128)(2,1)S(1)}, bf16[32,4096]{1,0:T(8,128)(2,1)S(1)}, u32[]{:S(2)}, u32[]{:S(2)}) %collective-permute-start.15) | collective-permute-done | bytes 262176 | tf_op jit(solution)/shard_map/ppermute | solution.py:235
  94.5 4.4 %collective-permute-start.17 = (bf16[32,4096]{1,0:T(8,128)(2,1)S(1)}, bf16[32,4096]{1,0:T(8,128)(2,1)S(1)}, u32[]{:S(2)}, u32[]{:S(2)}) collective-permute-start(bf16[32,4096]{1,0:T(8,128)(2,1)S(1)} %get-tuple-element.8), channel_id=1, source_target_pairs={{0,4},{1,5},{2,6},{3,7},{4,8},{5,9},{6,10},{7,11},{16,20},{17,21},... | collective-permute-start | bytes 786440 | tf_op jit(solution)/shard_map/ppermute | solution.py:239
  99.6 3.2 %collective-permute-done.17 = bf16[32,4096]{1,0:T(8,128)(2,1)S(1)} collective-permute-done((bf16[32,4096]{1,0:T(8,128)(2,1)S(1)}, bf16[32,4096]{1,0:T(8,128)(2,1)S(1)}, u32[]{:S(2)}, u32[]{:S(2)}) %collective-permute-start.17) | collective-permute-done | bytes 262176 | tf_op jit(solution)/shard_map/ppermute | solution.py:239
  102.9 14.1 %collective-permute-start.19 = (bf16[32,4096]{1,0:T(8,128)(2,1)S(1)}, bf16[32,4096]{1,0:T(8,128)(2,1)S(1)}, u32[]{:S(2)}, u32[]{:S(2)}) collective-permute-start(bf16[32,4096]{1,0:T(8,128)(2,1)S(1)} %get-tuple-element.6), channel_id=1, source_target_pairs={{0,4},{1,5},{2,6},{3,7},{4,8},{5,9},{6,10},{7,11},{8,12},{9,13},{1... | collective-permute-start | bytes 786440 | tf_op jit(solution)/shard_map/ppermute | solution.py:248
  117.1 1.3 %collective-permute-start.22 = (bf16[32,4096]{1,0:T(8,128)(2,1)S(1)}, bf16[32,4096]{1,0:T(8,128)(2,1)S(1)}, u32[]{:S(2)}, u32[]{:S(2)}) collective-permute-start(bf16[32,4096]{1,0:T(8,128)(2,1)S(1)} %get-tuple-element.7), channel_id=1, source_target_pairs={{4,0},{5,1},{6,2},{7,3},{8,4},{9,5},{10,6},{11,7},{12,8},{13,9},{1... | collective-permute-start | bytes 786440 | tf_op jit(solution)/shard_map/ppermute | solution.py:251
  118.4 2.5 %collective-permute-done.19 = bf16[32,4096]{1,0:T(8,128)(2,1)S(1)} collective-permute-done((bf16[32,4096]{1,0:T(8,128)(2,1)S(1)}, bf16[32,4096]{1,0:T(8,128)(2,1)S(1)}, u32[]{:S(2)}, u32[]{:S(2)}) %collective-permute-start.19) | collective-permute-done | bytes 262176 | tf_op jit(solution)/shard_map/ppermute | solution.py:248
  120.9 4.4 %collective-permute-done.22 = bf16[32,4096]{1,0:T(8,128)(2,1)S(1)} collective-permute-done((bf16[32,4096]{1,0:T(8,128)(2,1)S(1)}, bf16[32,4096]{1,0:T(8,128)(2,1)S(1)}, u32[]{:S(2)}, u32[]{:S(2)}) %collective-permute-start.22) | collective-permute-done | bytes 262176 | tf_op jit(solution)/shard_map/ppermute | solution.py:251
  126.7 1.6 %slice_add_fusion = (f32[128,2048]{1,0:T(8,128)}, f32[128,2048]{1,0:T(8,128)}) fusion(f32[128,4096]{1,0:T(8,128)S(1)} %fusion.30, bf16[128,2048]{1,0:T(8,128)(2,1)S(1)} %copy-done.1, bf16[128,2048]{1,0:T(8,128)(2,1)S(1)} %copy-done.2), kind=kLoop, calls=%fused_computation.23 | loop fusion | flops 1048576 | bytes 5242880 | tf_op jit(solution)/shard_map/add | solution.py:332
  (75 shorter events, 16.6 us)
Async XLA Ops:
  0.6 2.4 %copy-start.4 = (s32[32,8]{0,1:T(8,128)S(1)}, s32[32,8]{0,1:T(8,128)}, u32[]{:S(2)}) copy-start(s32[32,8]{0,1:T(8,128)} %param.11) | copy-start | bytes 3076
  0.6 2.4 %copy-start.3 = (f32[32,8]{0,1:T(8,128)S(1)}, f32[32,8]{0,1:T(8,128)}, u32[]{:S(2)}) copy-start(f32[32,8]{0,1:T(8,128)} %param.12) | copy-start | bytes 3076
  3.2 11.4 %collective-permute-start = (bf16[32,4224]{1,0:T(8,128)(2,1)S(1)}, bf16[32,4224]{1,0:T(8,128)(2,1)S(1)}, u32[]{:S(2)}, u32[]{:S(2)}) collective-permute-start(bf16[32,4224]{1,0:T(8,128)(2,1)S(1)} %fusion.43), channel_id=1, source_target_pairs={{4,0},{5,1},{6,2},{7,3},{8,4},{9,5},{10,6},{11,7},{12,8},{13,9},{1... | collective-permute-start | bytes 811016 | tf_op jit(solution)/shard_map/ppermute | solution.py:199
  4.5 11.4 %collective-permute-start.2 = (bf16[32,4224]{1,0:T(8,128)(2,1)S(1)}, bf16[32,4224]{1,0:T(8,128)(2,1)S(1)}, u32[]{:S(2)}, u32[]{:S(2)}) collective-permute-start(bf16[32,4224]{1,0:T(8,128)(2,1)S(1)} %fusion.43), channel_id=1, source_target_pairs={{0,4},{1,5},{2,6},{3,7},{4,8},{5,9},{6,10},{7,11},{8,12},{9,13},{1... | collective-permute-start | bytes 811016 | tf_op jit(solution)/shard_map/ppermute | solution.py:198
  14.6 9.6 %collective-permute-start.1 = (bf16[32,4224]{1,0:T(8,128)(2,1)S(1)}, bf16[32,4224]{1,0:T(8,128)(2,1)S(1)}, u32[]{:S(2)}, u32[]{:S(2)}) collective-permute-start(bf16[32,4224]{1,0:T(8,128)(2,1)S(1)} %collective-permute-done), channel_id=1, source_target_pairs={{4,0},{5,1},{6,2},{7,3},{8,4},{9,5},{10,6},{11,7},{20,16},{21,17},... | collective-permute-start | bytes 811016 | tf_op jit(solution)/shard_map/ppermute | solution.py:203
  15.9 8.3 %collective-permute-start.3 = (bf16[32,4224]{1,0:T(8,128)(2,1)S(1)}, bf16[32,4224]{1,0:T(8,128)(2,1)S(1)}, u32[]{:S(2)}, u32[]{:S(2)}) collective-permute-start(bf16[32,4224]{1,0:T(8,128)(2,1)S(1)} %collective-permute-done.2), channel_id=1, source_target_pairs={{4,8},{5,9},{6,10},{7,11},{8,12},{9,13},{10,14},{11,15},{20,24},{2... | collective-permute-start | bytes 811016 | tf_op jit(solution)/shard_map/ppermute | solution.py:202
  24.2 9.5 %collective-permute-start.4 = (bf16[32,4224]{1,0:T(8,128)(2,1)S(1)}, bf16[32,4224]{1,0:T(8,128)(2,1)S(1)}, u32[]{:S(2)}, u32[]{:S(2)}) collective-permute-start(bf16[32,4224]{1,0:T(8,128)(2,1)S(1)} %broadcast_select_fusion), channel_id=1, source_target_pairs={{0,2},{1,3},{2,0},{3,1},{4,6},{5,7},{6,4},{7,5},{8,10},{9,11},{10,... | collective-permute-start | bytes 811016 | tf_op jit(solution)/shard_map/ppermute | solution.py:204
  25.7 21.6 %collective-permute-start.9 = (bf16[32,4224]{1,0:T(8,128)(2,1)S(1)}, bf16[32,4224]{1,0:T(8,128)(2,1)S(1)}, u32[]{:S(2)}, u32[]{:S(2)}) collective-permute-start(bf16[32,4224]{1,0:T(8,128)(2,1)S(1)} %fusion.43), channel_id=1, source_target_pairs={{0,2},{1,3},{2,0},{3,1},{4,6},{5,7},{6,4},{7,5},{8,10},{9,11},{10,... | collective-permute-start | bytes 811016 | tf_op jit(solution)/shard_map/ppermute | solution.py:197
  26.3 30.9 %collective-permute-start.11 = (bf16[2048,768]{1,0:T(8,128)(2,1)}, bf16[2048,768]{1,0:T(8,128)(2,1)}, u32[]{:S(2)}, u32[]{:S(2)}) collective-permute-start(bf16[2048,768]{1,0:T(8,128)(2,1)} %bitcast.72), channel_id=1, source_target_pairs={{0,1},{1,0},{2,3},{3,2},{4,5},{5,4},{6,7},{7,6},{8,9},{9,8},{10,11... | collective-permute-start | bytes 9437192 | tf_op jit(solution)/shard_map/ppermute | solution.py:316
  26.3 33.9 %collective-permute-start.10 = (bf16[2048,768]{1,0:T(8,128)(2,1)}, bf16[2048,768]{1,0:T(8,128)(2,1)}, u32[]{:S(2)}, u32[]{:S(2)}) collective-permute-start(bf16[2048,768]{1,0:T(8,128)(2,1)} %bitcast.83), channel_id=1, source_target_pairs={{0,1},{1,0},{2,3},{3,2},{4,5},{5,4},{6,7},{7,6},{8,9},{9,8},{10,11... | collective-permute-start | bytes 9437192 | tf_op jit(solution)/shard_map/ppermute | solution.py:315
  33.8 11.3 %collective-permute-start.5 = (bf16[2,32,4224]{2,1,0:T(8,128)(2,1)S(1)}, bf16[2,32,4224]{2,1,0:T(8,128)(2,1)S(1)}, u32[]{:S(2)}, u32[]{:S(2)}) collective-permute-start(bf16[2,32,4224]{2,1,0:T(8,128)(2,1)S(1)} %get-tuple-element.22), channel_id=1, source_target_pairs={{4,0},{5,1},{6,2},{7,3},{20,16},{21,17},{22,18},{23,19}} | collective-permute-start | bytes 1622024 | tf_op jit(solution)/shard_map/ppermute | solution.py:208
  35.2 12.5 %collective-permute-start.7 = (bf16[32,4224]{1,0:T(8,128)(2,1)S(1)}, bf16[32,4224]{1,0:T(8,128)(2,1)S(1)}, u32[]{:S(2)}, u32[]{:S(2)}) collective-permute-start(bf16[32,4224]{1,0:T(8,128)(2,1)S(1)} %collective-permute-done), channel_id=1, source_target_pairs={{0,2},{1,3},{2,0},{3,1},{4,6},{5,7},{6,4},{7,5},{8,10},{9,11},{10,... | collective-permute-start | bytes 811016 | tf_op jit(solution)/shard_map/ppermute | solution.py:201
  45.1 0.8 collective-permute-start.6
  45.8 1.9 %copy-start.7 = (bf16[1,768,2048]{2,1,0:T(8,128)(2,1)S(1)}, bf16[1,768,2048]{2,1,0:T(8,128)(2,1)}, u32[]{:S(2)}) copy-start(bf16[1,768,2048]{2,1,0:T(8,128)(2,1)} %param.15) | copy-start | bytes 9437188
  45.8 1.9 %collective-permute-start.8 = (bf16[32,4224]{1,0:T(8,128)(2,1)S(1)}, bf16[32,4224]{1,0:T(8,128)(2,1)S(1)}, u32[]{:S(2)}, u32[]{:S(2)}) collective-permute-start(bf16[32,4224]{1,0:T(8,128)(2,1)S(1)} %collective-permute-done.2), channel_id=1, source_target_pairs={{4,6},{5,7},{6,4},{7,5},{8,10},{9,11},{10,8},{11,9},{12,14},{13,15... | collective-permute-start | bytes 811016 | tf_op jit(solution)/shard_map/ppermute | solution.py:200
  47.7 15.4 %collective-permute-start.12 = (bf16[768,2048]{1,0:T(8,128)(2,1)S(1)}, bf16[768,2048]{1,0:T(8,128)(2,1)S(1)}, u32[]{:S(2)}, u32[]{:S(2)}) collective-permute-start(bf16[768,2048]{1,0:T(8,128)(2,1)S(1)} %bitcast.84), channel_id=1, source_target_pairs={{0,1},{1,0},{2,3},{3,2},{4,5},{5,4},{6,7},{7,6},{8,9},{9,8},{10,11... | collective-permute-start | bytes 9437192 | tf_op jit(solution)/shard_map/ppermute | solution.py:317
  48.2 1.9 %copy-start = (bf16[1,2048,768]{2,1,0:T(8,128)(2,1)S(1)}, bf16[1,2048,768]{2,1,0:T(8,128)(2,1)}, u32[]{:S(2)}) copy-start(bf16[1,2048,768]{2,1,0:T(8,128)(2,1)} %param.14) | copy-start | bytes 9437188
  50.1 1.9 %copy-start.6 = (bf16[1,2048,768]{2,1,0:T(8,128)(2,1)S(1)}, bf16[1,2048,768]{2,1,0:T(8,128)(2,1)}, u32[]{:S(2)}) copy-start(bf16[1,2048,768]{2,1,0:T(8,128)(2,1)} %param.13) | copy-start | bytes 9437188
  71.6 9.2 %collective-permute-start.14 = (bf16[32,4096]{1,0:T(8,128)(2,1)S(1)}, bf16[32,4096]{1,0:T(8,128)(2,1)S(1)}, u32[]{:S(2)}, u32[]{:S(2)}) collective-permute-start(bf16[32,4096]{1,0:T(8,128)(2,1)S(1)} %get-tuple-element.16), channel_id=1, source_target_pairs={{0,2},{1,3},{2,0},{3,1},{4,6},{5,7},{6,4},{7,5},{8,10},{9,11},{10,... | collective-permute-start | bytes 786440 | tf_op jit(solution)/shard_map/ppermute | solution.py:165
  72.9 17.9 %collective-permute-start.16 = (bf16[32,4096]{1,0:T(8,128)(2,1)S(1)}, bf16[32,4096]{1,0:T(8,128)(2,1)S(1)}, u32[]{:S(2)}, u32[]{:S(2)}) collective-permute-start(bf16[32,4096]{1,0:T(8,128)(2,1)S(1)} %get-tuple-element.15), channel_id=1, source_target_pairs={{0,2},{1,3},{2,0},{3,1},{4,6},{5,7},{6,4},{7,5},{8,10},{9,11},{10,... | collective-permute-start | bytes 786440 | tf_op jit(solution)/shard_map/ppermute | solution.py:165
  80.8 13.5 %collective-permute-start.15 = (bf16[32,4096]{1,0:T(8,128)(2,1)S(1)}, bf16[32,4096]{1,0:T(8,128)(2,1)S(1)}, u32[]{:S(2)}, u32[]{:S(2)}) collective-permute-start(bf16[32,4096]{1,0:T(8,128)(2,1)S(1)} %fusion.42), channel_id=1, source_target_pairs={{0,4},{1,5},{2,6},{3,7},{16,20},{17,21},{18,22},{19,23}} | collective-permute-start | bytes 786440 | tf_op jit(solution)/shard_map/ppermute | solution.py:235
  88.0 6.3 %collective-permute-start.20 = (bf16[32,4096]{1,0:T(8,128)(2,1)S(1)}, bf16[32,4096]{1,0:T(8,128)(2,1)S(1)}, u32[]{:S(2)}, u32[]{:S(2)}) collective-permute-start(bf16[32,4096]{1,0:T(8,128)(2,1)S(1)} %fusion.42), channel_id=1, source_target_pairs={{12,8},{13,9},{14,10},{15,11},{28,24},{29,25},{30,26},{31,27}} | collective-permute-start | bytes 786440 | tf_op jit(solution)/shard_map/ppermute | solution.py:236
  88.7 10.9 %collective-permute-start.13 = (bf16[32,4096]{1,0:T(8,128)(2,1)S(1)}, bf16[32,4096]{1,0:T(8,128)(2,1)S(1)}, u32[]{:S(2)}, u32[]{:S(2)}) collective-permute-start(bf16[32,4096]{1,0:T(8,128)(2,1)S(1)} %get-tuple-element.17), channel_id=1, source_target_pairs={{0,2},{1,3},{2,0},{3,1},{4,6},{5,7},{6,4},{7,5},{8,10},{9,11},{10,... | collective-permute-start | bytes 786440 | tf_op jit(solution)/shard_map/ppermute | solution.py:165
  89.5 10.1 %collective-permute-start.18 = (bf16[32,4096]{1,0:T(8,128)(2,1)S(1)}, bf16[32,4096]{1,0:T(8,128)(2,1)S(1)}, u32[]{:S(2)}, u32[]{:S(2)}) collective-permute-start(bf16[32,4096]{1,0:T(8,128)(2,1)S(1)} %get-tuple-element.14), channel_id=1, source_target_pairs={{0,2},{1,3},{2,0},{3,1},{4,6},{5,7},{6,4},{7,5},{8,10},{9,11},{10,... | collective-permute-start | bytes 786440 | tf_op jit(solution)/shard_map/ppermute | solution.py:165
  94.5 8.3 %collective-permute-start.17 = (bf16[32,4096]{1,0:T(8,128)(2,1)S(1)}, bf16[32,4096]{1,0:T(8,128)(2,1)S(1)}, u32[]{:S(2)}, u32[]{:S(2)}) collective-permute-start(bf16[32,4096]{1,0:T(8,128)(2,1)S(1)} %get-tuple-element.8), channel_id=1, source_target_pairs={{0,4},{1,5},{2,6},{3,7},{4,8},{5,9},{6,10},{7,11},{16,20},{17,21},... | collective-permute-start | bytes 786440 | tf_op jit(solution)/shard_map/ppermute | solution.py:239
  98.9 3.9 %collective-permute-start.21 = (bf16[32,4096]{1,0:T(8,128)(2,1)S(1)}, bf16[32,4096]{1,0:T(8,128)(2,1)S(1)}, u32[]{:S(2)}, u32[]{:S(2)}) collective-permute-start(bf16[32,4096]{1,0:T(8,128)(2,1)S(1)} %get-tuple-element.9), channel_id=1, source_target_pairs={{8,4},{9,5},{10,6},{11,7},{12,8},{13,9},{14,10},{15,11},{24,20},{2... | collective-permute-start | bytes 786440 | tf_op jit(solution)/shard_map/ppermute | solution.py:242
  102.9 18.0 %collective-permute-start.19 = (bf16[32,4096]{1,0:T(8,128)(2,1)S(1)}, bf16[32,4096]{1,0:T(8,128)(2,1)S(1)}, u32[]{:S(2)}, u32[]{:S(2)}) collective-permute-start(bf16[32,4096]{1,0:T(8,128)(2,1)S(1)} %get-tuple-element.6), channel_id=1, source_target_pairs={{0,4},{1,5},{2,6},{3,7},{4,8},{5,9},{6,10},{7,11},{8,12},{9,13},{1... | collective-permute-start | bytes 786440 | tf_op jit(solution)/shard_map/ppermute | solution.py:248
  117.0 8.6 %copy-start.5 = (s32[128]{0:T(128)S(1)}, s32[128]{0:T(128)}, u32[]{:S(2)}) copy-start(s32[128]{0:T(128)} %param.10) | copy-start | bytes 1540
  117.1 8.3 %collective-permute-start.22 = (bf16[32,4096]{1,0:T(8,128)(2,1)S(1)}, bf16[32,4096]{1,0:T(8,128)(2,1)S(1)}, u32[]{:S(2)}, u32[]{:S(2)}) collective-permute-start(bf16[32,4096]{1,0:T(8,128)(2,1)S(1)} %get-tuple-element.7), channel_id=1, source_target_pairs={{4,0},{5,1},{6,2},{7,3},{8,4},{9,5},{10,6},{11,7},{12,8},{13,9},{1... | collective-permute-start | bytes 786440 | tf_op jit(solution)/shard_map/ppermute | solution.py:251
  125.5 1.2 copy-start.1
  125.5 1.2 copy-start.2

commit v22 on v20

--- a/solution.py
+++ b/solution.py
@@ -240,17 +240,18 @@
     member = (cluster_ids[:, None] == jnp.arange(cent_rows, dtype=jnp.int32)[None, :]).astype(
         jnp.bfloat16
     )
-    counts = jnp.sum(member.astype(jnp.float32), axis=0)
     contract = (((0,), (0,)), ((), ()))
     model_width = tokens.shape[1]
+    ones = jnp.ones((tokens.shape[0], 128), jnp.bfloat16)
     sums = lax.dot_general(
         member,
-        jnp.concatenate([tokens, out_grad], axis=1),
+        jnp.concatenate([tokens, out_grad, ones], axis=1),
         contract,
         preferred_element_type=jnp.float32,
     )
+    counts = sums[:, 2 * model_width]
     centroid = sums[:, :model_width] / counts[:, None]
-    grad_sum = sums[:, model_width:]
+    grad_sum = sums[:, model_width : 2 * model_width]
     experts = lax.axis_size("expert")
     model_width = tokens.shape[1]
     picked = routes[:, :, None] == jnp.arange(experts, dtype=jnp.int32)[None, None, :]

time: 105 us -> 104 us (level)
  no operation moved by 1% of the time
where the time goes in v22:
time: 104 us
  waiting for transfers between devices  40.6 us (39%)
  starting transfers between devices  40.5 us (39%)
  matrix products  15.1 us (15%)
  other arithmetic  4.23 us (4%)
  local copies, waits for them, and re-layouts  2.18 us (2%)
  between operations  1.28 us (1%)
    ppermute x3, waiting for transfers between devices, topo_all_gather(): lax.ppermute(behind, 'expert', [(j, j - 4) for j in range(experts) if 1 <...  13.4 us
    ppermute x4, waiting for transfers between devices, row_sum(): got = lax.ppermute(theirs.astype(jnp.bfloat16), 'expert', pairs)  8.55 us
    ppermute x3, starting transfers between devices, topo_all_gather(): lax.ppermute(ahead, 'expert', [(j, j + 4) for j in range(experts) if step...  6.93 us
    ppermute x1, starting transfers between devices, four_line_sum(): lax.ppermute((ahead + third).astype(jnp.bfloat16), 'expert', [(j, j + 4)...  6.33 us
    ppermute x2, waiting for transfers between devices, topo_all_gather(): lax.ppermute(jnp.where(in_ahead, ahead, behind), 'expert', sorted(ahead_r...  6.14 us
    ppermute x1, waiting for transfers between devices, four_line_sum(): lax.ppermute((behind + behind_part).astype(jnp.bfloat16), 'expert', [(j,...  4.42 us
    ppermute x1, starting transfers between devices, four_line_sum(): lax.ppermute((ahead + second).astype(jnp.bfloat16), 'expert', [(j, j + 4)...  4.4 us
    ppermute x4, starting transfers between devices, row_sum(): got = lax.ppermute(theirs.astype(jnp.bfloat16), 'expert', pairs)  4.18 us
  transfers between devices with their start and end apart: 24, of which 11 were waited for; matrix products, arithmetic and copies ran while one was open for 10% of the time, Pallas kernels for 0%

profile of v22, /device:TPU:0, one launch (start us, length us, event | category | flops | bytes accessed | tf_op | source)
XLA Modules:
  0.0 103.8 jit_solution(498592824121925037)
XLA Ops:
  0.7 1.6 %fusion.13 = f32[32,4224]{1,0:T(8,128)S(1)} fusion(bf16[128,2048]{1,0:T(8,128)(2,1)} %param.9, bf16[128,2048]{1,0:T(8,128)(2,1)} %param.8, bf16[4224]{0:T(1024)(128)(2,1)S(1)} %pad.18.clone, s32[128]{0:T(128)} %param.10), kind=kOutput, calls=%fused_computation.21 | convolution fusion | flops 37851136 | bytes 1598208 | tf_op jit(solution)/shard_map/dot_general | solution.py:246
  2.7 1.3 %collective-permute-start = (bf16[32,4224]{1,0:T(8,128)(2,1)S(1)}, bf16[32,4224]{1,0:T(8,128)(2,1)S(1)}, u32[]{:S(2)}, u32[]{:S(2)}) collective-permute-start(bf16[32,4224]{1,0:T(8,128)(2,1)S(1)} %fusion.45), channel_id=1, source_target_pairs={{4,0},{5,1},{6,2},{7,3},{8,4},{9,5},{10,6},{11,7},{12,8},{13,9},{1... | collective-permute-start | bytes 811016 | tf_op jit(solution)/shard_map/ppermute | solution.py:125
  4.0 5.6 %collective-permute-start.3 = (bf16[32,4224]{1,0:T(8,128)(2,1)S(1)}, bf16[32,4224]{1,0:T(8,128)(2,1)S(1)}, u32[]{:S(2)}, u32[]{:S(2)}) collective-permute-start(bf16[32,4224]{1,0:T(8,128)(2,1)S(1)} %fusion.45), channel_id=1, source_target_pairs={{0,4},{1,5},{2,6},{3,7},{4,8},{5,9},{6,10},{7,11},{8,12},{9,13},{1... | collective-permute-start | bytes 811016 | tf_op jit(solution)/shard_map/ppermute | solution.py:120
  9.6 2.0 %collective-permute-start.10 = (bf16[32,4224]{1,0:T(8,128)(2,1)S(1)}, bf16[32,4224]{1,0:T(8,128)(2,1)S(1)}, u32[]{:S(2)}, u32[]{:S(2)}) collective-permute-start(bf16[32,4224]{1,0:T(8,128)(2,1)S(1)} %fusion.45), channel_id=1, source_target_pairs={{0,2},{1,3},{2,0},{3,1},{4,6},{5,7},{6,4},{7,5},{8,10},{9,11},{10,... | collective-permute-start | bytes 811016 | tf_op jit(solution)/shard_map/ppermute | solution.py:117
  11.7 2.5 %collective-permute-done = bf16[32,4224]{1,0:T(8,128)(2,1)S(1)} collective-permute-done((bf16[32,4224]{1,0:T(8,128)(2,1)S(1)}, bf16[32,4224]{1,0:T(8,128)(2,1)S(1)}, u32[]{:S(2)}, u32[]{:S(2)}) %collective-permute-start) | collective-permute-done | bytes 270368 | tf_op jit(solution)/shard_map/ppermute | solution.py:125
  14.1 1.3 %collective-permute-start.1 = (bf16[32,4224]{1,0:T(8,128)(2,1)S(1)}, bf16[32,4224]{1,0:T(8,128)(2,1)S(1)}, u32[]{:S(2)}, u32[]{:S(2)}) collective-permute-start(bf16[32,4224]{1,0:T(8,128)(2,1)S(1)} %collective-permute-done), channel_id=1, source_target_pairs={{4,0},{5,1},{6,2},{7,3},{8,4},{9,5},{10,6},{11,7},{20,16},{21,17},... | collective-permute-start | bytes 811016 | tf_op jit(solution)/shard_map/ppermute | solution.py:125
  16.2 3.6 %collective-permute-start.8 = (bf16[32,4224]{1,0:T(8,128)(2,1)S(1)}, bf16[32,4224]{1,0:T(8,128)(2,1)S(1)}, u32[]{:S(2)}, u32[]{:S(2)}) collective-permute-start(bf16[32,4224]{1,0:T(8,128)(2,1)S(1)} %collective-permute-done), channel_id=1, source_target_pairs={{0,2},{1,3},{2,0},{3,1},{4,6},{5,7},{6,4},{7,5},{8,10},{9,11},{10,... | collective-permute-start | bytes 811016 | tf_op jit(solution)/shard_map/ppermute | solution.py:143
  20.5 3.2 %collective-permute-done.1 = bf16[32,4224]{1,0:T(8,128)(2,1)S(1)} collective-permute-done((bf16[32,4224]{1,0:T(8,128)(2,1)S(1)}, bf16[32,4224]{1,0:T(8,128)(2,1)S(1)}, u32[]{:S(2)}, u32[]{:S(2)}) %collective-permute-start.1) | collective-permute-done | bytes 270368 | tf_op jit(solution)/shard_map/ppermute | solution.py:125
  23.7 1.3 %collective-permute-start.2 = (bf16[32,4224]{1,0:T(8,128)(2,1)S(1)}, bf16[32,4224]{1,0:T(8,128)(2,1)S(1)}, u32[]{:S(2)}, u32[]{:S(2)}) collective-permute-start(bf16[32,4224]{1,0:T(8,128)(2,1)S(1)} %collective-permute-done.1), channel_id=1, source_target_pairs={{4,0},{5,1},{6,2},{7,3},{20,16},{21,17},{22,18},{23,19}} | collective-permute-start | bytes 811016 | tf_op jit(solution)/shard_map/ppermute | solution.py:125
  25.7 7.8 %collective-permute-done.2 = bf16[32,4224]{1,0:T(8,128)(2,1)S(1)} collective-permute-done((bf16[32,4224]{1,0:T(8,128)(2,1)S(1)}, bf16[32,4224]{1,0:T(8,128)(2,1)S(1)}, u32[]{:S(2)}, u32[]{:S(2)}) %collective-permute-start.2) | collective-permute-done | bytes 270368 | tf_op jit(solution)/shard_map/ppermute | solution.py:125
  33.5 1.5 %collective-permute-start.7 = (bf16[32,4224]{1,0:T(8,128)(2,1)S(1)}, bf16[32,4224]{1,0:T(8,128)(2,1)S(1)}, u32[]{:S(2)}, u32[]{:S(2)}) collective-permute-start(bf16[32,4224]{1,0:T(8,128)(2,1)S(1)} %broadcast_select_fusion), channel_id=1, source_target_pairs={{0,2},{1,3},{2,0},{3,1},{4,6},{5,7},{6,4},{7,5},{8,10},{9,11},{10,... | collective-permute-start | bytes 811016 | tf_op jit(solution)/shard_map/ppermute | solution.py:136
  35.1 2.4 %collective-permute-start.6 = (bf16[32,4224]{1,0:T(8,128)(2,1)S(1)}, bf16[32,4224]{1,0:T(8,128)(2,1)S(1)}, u32[]{:S(2)}, u32[]{:S(2)}) collective-permute-start(bf16[32,4224]{1,0:T(8,128)(2,1)S(1)} %broadcast_select_fusion.1), channel_id=1, source_target_pairs={{0,2},{1,3},{2,0},{3,1},{12,14},{13,15},{14,12},{15,13},{16,18},{1... | collective-permute-start | bytes 811016 | tf_op jit(solution)/shard_map/ppermute | solution.py:136
  38.7 3.2 %collective-permute-done.7 = bf16[32,4224]{1,0:T(8,128)(2,1)S(1)} collective-permute-done((bf16[32,4224]{1,0:T(8,128)(2,1)S(1)}, bf16[32,4224]{1,0:T(8,128)(2,1)S(1)}, u32[]{:S(2)}, u32[]{:S(2)}) %collective-permute-start.7) | collective-permute-done | bytes 270368 | tf_op jit(solution)/shard_map/ppermute | solution.py:136
  42.0 2.9 %collective-permute-done.6 = bf16[32,4224]{1,0:T(8,128)(2,1)S(1)} collective-permute-done((bf16[32,4224]{1,0:T(8,128)(2,1)S(1)}, bf16[32,4224]{1,0:T(8,128)(2,1)S(1)}, u32[]{:S(2)}, u32[]{:S(2)}) %collective-permute-start.6) | collective-permute-done | bytes 270368 | tf_op jit(solution)/shard_map/ppermute | solution.py:136
  50.6 1.1 %fusion.11 = f32[256,2048]{1,0:T(8,128)S(1)} fusion(f32[256]{0:T(256)S(1)} %get-tuple-element.3, f32[256,768]{1,0:T(8,128)S(1)} %fusion.26, f32[256,768]{1,0:T(8,128)S(1)} %fusion.28, bf16[1,768,2048]{2,1,0:T(8,128)(2,1)S(1)} %copy-done.7), kind=kOutput, calls=%fused_computation.17 | convolution fusion | flops 808058880 | bytes 6816768 | tf_op jit(solution)/shard_map/dot_general | solution.py:224
  51.7 1.1 %fusion.36 = f32[256,2048]{1,0:T(8,128)S(1)} fusion(f32[256,768]{1,0:T(8,128)S(1)} %fusion.28, f32[256,768]{1,0:T(8,128)S(1)} %fusion.20, f32[256,768]{1,0:T(8,128)S(1)} %fusion.26, bf16[1,2048,768]{2,1,0:T(8,128)(2,1)S(1)} %copy-done.6), kind=kOutput, calls=%fused_computation.70 | convolution fusion | flops 807272448 | bytes 7602176 | tf_op jit(solution)/shard_map/dot_general | solution.py:230
  52.8 1.1 %fusion.6 = f32[256,2048]{1,0:T(8,128)S(1)} fusion(f32[256,2048]{1,0:T(8,128)S(1)} %fusion.36, f32[256]{0:T(256)S(1)} %get-tuple-element.3, f32[256,768]{1,0:T(8,128)S(1)} %fusion.20, f32[256,768]{1,0:T(8,128)S(1)} %fusion.28, bf16[1,2048,768]{2,1,0:T(8,128)(2,1)S(1)} %copy-done), kind=kOutput, calls=%fused_computation.10 | convolution fusion | flops 808583168 | bytes 8913920 | tf_op jit(solution)/shard_map/dot_general | solution.py:231
  58.0 1.0 fusion.9
  59.0 1.1 %fusion.4 = f32[256,2048]{1,0:T(8,128)S(1)} fusion(f32[256,2048]{1,0:T(8,128)S(1)} %fusion.6, f32[256,2048]{1,0:T(8,128)S(1)} %fusion.37, bf16[2048,768]{1,0:T(8,128)(2,1)S(1)} %collective-permute-done.11, f32[256]{0:T(256)S(1)} %get-tuple-element.2, f32[256,768]{1,0:T(8,128)S(1)} %fusion.24, f32[256,768]{1,0:T(8,128)S(1)} %fusion.18, f32[256,768]{1,0:T(8,128)S(1)} %fusion.22), kind=kOutput, calls=%fused_computation.8 | convolution fusion | flops 809893888 | bytes 11797504 | tf_op jit(solution)/shard_map/dot_general | solution.py:230
  60.4 1.3 %collective-permute-start.15 = (bf16[32,4096]{1,0:T(8,128)(2,1)S(1)}, bf16[32,4096]{1,0:T(8,128)(2,1)S(1)}, u32[]{:S(2)}, u32[]{:S(2)}) collective-permute-start(bf16[32,4096]{1,0:T(8,128)(2,1)S(1)} %get-tuple-element.16), channel_id=1, source_target_pairs={{0,2},{1,3},{2,0},{3,1},{4,6},{5,7},{6,4},{7,5},{8,10},{9,11},{10,... | collective-permute-start | bytes 786440 | tf_op jit(solution)/shard_map/ppermute | solution.py:161
  62.6 7.1 %collective-permute-done.15 = bf16[32,4096]{1,0:T(8,128)(2,1)S(1)} collective-permute-done((bf16[32,4096]{1,0:T(8,128)(2,1)S(1)}, bf16[32,4096]{1,0:T(8,128)(2,1)S(1)}, u32[]{:S(2)}, u32[]{:S(2)}) %collective-permute-start.15) | collective-permute-done | bytes 262176 | tf_op jit(solution)/shard_map/ppermute | solution.py:161
  69.7 1.3 %collective-permute-start.16 = (bf16[32,4096]{1,0:T(8,128)(2,1)S(1)}, bf16[32,4096]{1,0:T(8,128)(2,1)S(1)}, u32[]{:S(2)}, u32[]{:S(2)}) collective-permute-start(bf16[32,4096]{1,0:T(8,128)(2,1)S(1)} %fusion.44), channel_id=1, source_target_pairs={{0,4},{1,5},{2,6},{3,7},{16,20},{17,21},{18,22},{19,23}} | collective-permute-start | bytes 786440 | tf_op jit(solution)/shard_map/ppermute | solution.py:196
  71.7 1.3 %collective-permute-start.14 = (bf16[32,4096]{1,0:T(8,128)(2,1)S(1)}, bf16[32,4096]{1,0:T(8,128)(2,1)S(1)}, u32[]{:S(2)}, u32[]{:S(2)}) collective-permute-start(bf16[32,4096]{1,0:T(8,128)(2,1)S(1)} %get-tuple-element.17), channel_id=1, source_target_pairs={{0,2},{1,3},{2,0},{3,1},{4,6},{5,7},{6,4},{7,5},{8,10},{9,11},{10,... | collective-permute-start | bytes 786440 | tf_op jit(solution)/shard_map/ppermute | solution.py:161
  73.8 1.5 %collective-permute-done.17 = bf16[32,4096]{1,0:T(8,128)(2,1)S(1)} collective-permute-done((bf16[32,4096]{1,0:T(8,128)(2,1)S(1)}, bf16[32,4096]{1,0:T(8,128)(2,1)S(1)}, u32[]{:S(2)}, u32[]{:S(2)}) %collective-permute-start.17) | collective-permute-done | bytes 262176 | tf_op jit(solution)/shard_map/ppermute | solution.py:161
  75.3 2.3 %collective-permute-done.16 = bf16[32,4096]{1,0:T(8,128)(2,1)S(1)} collective-permute-done((bf16[32,4096]{1,0:T(8,128)(2,1)S(1)}, bf16[32,4096]{1,0:T(8,128)(2,1)S(1)}, u32[]{:S(2)}, u32[]{:S(2)}) %collective-permute-start.16) | collective-permute-done | bytes 262176 | tf_op jit(solution)/shard_map/ppermute | solution.py:196
  77.8 4.4 %collective-permute-start.18 = (bf16[32,4096]{1,0:T(8,128)(2,1)S(1)}, bf16[32,4096]{1,0:T(8,128)(2,1)S(1)}, u32[]{:S(2)}, u32[]{:S(2)}) collective-permute-start(bf16[32,4096]{1,0:T(8,128)(2,1)S(1)} %get-tuple-element.8), channel_id=1, source_target_pairs={{0,4},{1,5},{2,6},{3,7},{4,8},{5,9},{6,10},{7,11},{16,20},{17,21},... | collective-permute-start | bytes 786440 | tf_op jit(solution)/shard_map/ppermute | solution.py:200
  82.9 3.2 %collective-permute-done.18 = bf16[32,4096]{1,0:T(8,128)(2,1)S(1)} collective-permute-done((bf16[32,4096]{1,0:T(8,128)(2,1)S(1)}, bf16[32,4096]{1,0:T(8,128)(2,1)S(1)}, u32[]{:S(2)}, u32[]{:S(2)}) %collective-permute-start.18) | collective-permute-done | bytes 262176 | tf_op jit(solution)/shard_map/ppermute | solution.py:200
  86.2 6.3 %collective-permute-start.20 = (bf16[32,4096]{1,0:T(8,128)(2,1)S(1)}, bf16[32,4096]{1,0:T(8,128)(2,1)S(1)}, u32[]{:S(2)}, u32[]{:S(2)}) collective-permute-start(bf16[32,4096]{1,0:T(8,128)(2,1)S(1)} %get-tuple-element.6), channel_id=1, source_target_pairs={{0,4},{1,5},{2,6},{3,7},{4,8},{5,9},{6,10},{7,11},{8,12},{9,13},{1... | collective-permute-start | bytes 786440 | tf_op jit(solution)/shard_map/ppermute | solution.py:209
  92.6 1.3 %collective-permute-start.23 = (bf16[32,4096]{1,0:T(8,128)(2,1)S(1)}, bf16[32,4096]{1,0:T(8,128)(2,1)S(1)}, u32[]{:S(2)}, u32[]{:S(2)}) collective-permute-start(bf16[32,4096]{1,0:T(8,128)(2,1)S(1)} %get-tuple-element.7), channel_id=1, source_target_pairs={{4,0},{5,1},{6,2},{7,3},{8,4},{9,5},{10,6},{11,7},{12,8},{13,9},{1... | collective-permute-start | bytes 786440 | tf_op jit(solution)/shard_map/ppermute | solution.py:212
  93.9 2.5 %collective-permute-done.20 = bf16[32,4096]{1,0:T(8,128)(2,1)S(1)} collective-permute-done((bf16[32,4096]{1,0:T(8,128)(2,1)S(1)}, bf16[32,4096]{1,0:T(8,128)(2,1)S(1)}, u32[]{:S(2)}, u32[]{:S(2)}) %collective-permute-start.20) | collective-permute-done | bytes 262176 | tf_op jit(solution)/shard_map/ppermute | solution.py:209
  96.4 4.4 %collective-permute-done.23 = bf16[32,4096]{1,0:T(8,128)(2,1)S(1)} collective-permute-done((bf16[32,4096]{1,0:T(8,128)(2,1)S(1)}, bf16[32,4096]{1,0:T(8,128)(2,1)S(1)}, u32[]{:S(2)}, u32[]{:S(2)}) %collective-permute-start.23) | collective-permute-done | bytes 262176 | tf_op jit(solution)/shard_map/ppermute | solution.py:212
  102.3 1.6 %slice_add_fusion = (f32[128,2048]{1,0:T(8,128)}, f32[128,2048]{1,0:T(8,128)}) fusion(f32[128,4096]{1,0:T(8,128)S(1)} %fusion.32, bf16[128,2048]{1,0:T(8,128)(2,1)S(1)} %copy-done.1, bf16[128,2048]{1,0:T(8,128)(2,1)S(1)} %copy-done.2), kind=kLoop, calls=%fused_computation.28 | loop fusion | flops 1048576 | bytes 5242880 | tf_op jit(solution)/shard_map/add | solution.py:294
  (78 shorter events, 18.5 us)
Async XLA Ops:
  0.6 1.9 %copy-start.4 = (s32[32,8]{0,1:T(8,128)S(1)}, s32[32,8]{0,1:T(8,128)}, u32[]{:S(2)}) copy-start(s32[32,8]{0,1:T(8,128)} %param.11) | copy-start | bytes 3076
  0.6 1.9 %copy-start.3 = (f32[32,8]{0,1:T(8,128)S(1)}, f32[32,8]{0,1:T(8,128)}, u32[]{:S(2)}) copy-start(f32[32,8]{0,1:T(8,128)} %param.12) | copy-start | bytes 3076
  2.7 11.4 %collective-permute-start = (bf16[32,4224]{1,0:T(8,128)(2,1)S(1)}, bf16[32,4224]{1,0:T(8,128)(2,1)S(1)}, u32[]{:S(2)}, u32[]{:S(2)}) collective-permute-start(bf16[32,4224]{1,0:T(8,128)(2,1)S(1)} %fusion.45), channel_id=1, source_target_pairs={{4,0},{5,1},{6,2},{7,3},{8,4},{9,5},{10,6},{11,7},{12,8},{13,9},{1... | collective-permute-start | bytes 811016 | tf_op jit(solution)/shard_map/ppermute | solution.py:125
  4.0 11.4 %collective-permute-start.3 = (bf16[32,4224]{1,0:T(8,128)(2,1)S(1)}, bf16[32,4224]{1,0:T(8,128)(2,1)S(1)}, u32[]{:S(2)}, u32[]{:S(2)}) collective-permute-start(bf16[32,4224]{1,0:T(8,128)(2,1)S(1)} %fusion.45), channel_id=1, source_target_pairs={{0,4},{1,5},{2,6},{3,7},{4,8},{5,9},{6,10},{7,11},{8,12},{9,13},{1... | collective-permute-start | bytes 811016 | tf_op jit(solution)/shard_map/ppermute | solution.py:120
  9.6 28.4 %collective-permute-start.10 = (bf16[32,4224]{1,0:T(8,128)(2,1)S(1)}, bf16[32,4224]{1,0:T(8,128)(2,1)S(1)}, u32[]{:S(2)}, u32[]{:S(2)}) collective-permute-start(bf16[32,4224]{1,0:T(8,128)(2,1)S(1)} %fusion.45), channel_id=1, source_target_pairs={{0,2},{1,3},{2,0},{3,1},{4,6},{5,7},{6,4},{7,5},{8,10},{9,11},{10,... | collective-permute-start | bytes 811016 | tf_op jit(solution)/shard_map/ppermute | solution.py:117
  14.1 9.6 %collective-permute-start.1 = (bf16[32,4224]{1,0:T(8,128)(2,1)S(1)}, bf16[32,4224]{1,0:T(8,128)(2,1)S(1)}, u32[]{:S(2)}, u32[]{:S(2)}) collective-permute-start(bf16[32,4224]{1,0:T(8,128)(2,1)S(1)} %collective-permute-done), channel_id=1, source_target_pairs={{4,0},{5,1},{6,2},{7,3},{8,4},{9,5},{10,6},{11,7},{20,16},{21,17},... | collective-permute-start | bytes 811016 | tf_op jit(solution)/shard_map/ppermute | solution.py:125
  15.4 9.5 %collective-permute-start.4 = (bf16[32,4224]{1,0:T(8,128)(2,1)S(1)}, bf16[32,4224]{1,0:T(8,128)(2,1)S(1)}, u32[]{:S(2)}, u32[]{:S(2)}) collective-permute-start(bf16[32,4224]{1,0:T(8,128)(2,1)S(1)} %collective-permute-done.3), channel_id=1, source_target_pairs={{4,8},{5,9},{6,10},{7,11},{8,12},{9,13},{10,14},{11,15},{20,24},{2... | collective-permute-start | bytes 811016 | tf_op jit(solution)/shard_map/ppermute | solution.py:120
  16.2 21.9 %collective-permute-start.8 = (bf16[32,4224]{1,0:T(8,128)(2,1)S(1)}, bf16[32,4224]{1,0:T(8,128)(2,1)S(1)}, u32[]{:S(2)}, u32[]{:S(2)}) collective-permute-start(bf16[32,4224]{1,0:T(8,128)(2,1)S(1)} %collective-permute-done), channel_id=1, source_target_pairs={{0,2},{1,3},{2,0},{3,1},{4,6},{5,7},{6,4},{7,5},{8,10},{9,11},{10,... | collective-permute-start | bytes 811016 | tf_op jit(solution)/shard_map/ppermute | solution.py:143
  19.8 18.8 %collective-permute-start.9 = (bf16[32,4224]{1,0:T(8,128)(2,1)S(1)}, bf16[32,4224]{1,0:T(8,128)(2,1)S(1)}, u32[]{:S(2)}, u32[]{:S(2)}) collective-permute-start(bf16[32,4224]{1,0:T(8,128)(2,1)S(1)} %collective-permute-done.3), channel_id=1, source_target_pairs={{4,6},{5,7},{6,4},{7,5},{8,10},{9,11},{10,8},{11,9},{12,14},{13,15... | collective-permute-start | bytes 811016 | tf_op jit(solution)/shard_map/ppermute | solution.py:142
  23.7 9.8 %collective-permute-start.2 = (bf16[32,4224]{1,0:T(8,128)(2,1)S(1)}, bf16[32,4224]{1,0:T(8,128)(2,1)S(1)}, u32[]{:S(2)}, u32[]{:S(2)}) collective-permute-start(bf16[32,4224]{1,0:T(8,128)(2,1)S(1)} %collective-permute-done.1), channel_id=1, source_target_pairs={{4,0},{5,1},{6,2},{7,3},{20,16},{21,17},{22,18},{23,19}} | collective-permute-start | bytes 811016 | tf_op jit(solution)/shard_map/ppermute | solution.py:125
  25.0 10.0 %collective-permute-start.5 = (bf16[32,4224]{1,0:T(8,128)(2,1)S(1)}, bf16[32,4224]{1,0:T(8,128)(2,1)S(1)}, u32[]{:S(2)}, u32[]{:S(2)}) collective-permute-start(bf16[32,4224]{1,0:T(8,128)(2,1)S(1)} %collective-permute-done.4), channel_id=1, source_target_pairs={{8,12},{9,13},{10,14},{11,15},{24,28},{25,29},{26,30},{27,31}} | collective-permute-start | bytes 811016 | tf_op jit(solution)/shard_map/ppermute | solution.py:120
  25.7 12.3 %copy-start = (bf16[1,2048,768]{2,1,0:T(8,128)(2,1)S(1)}, bf16[1,2048,768]{2,1,0:T(8,128)(2,1)}, u32[]{:S(2)}) copy-start(bf16[1,2048,768]{2,1,0:T(8,128)(2,1)} %param.14) | copy-start | bytes 9437188
  33.5 8.5 %collective-permute-start.7 = (bf16[32,4224]{1,0:T(8,128)(2,1)S(1)}, bf16[32,4224]{1,0:T(8,128)(2,1)S(1)}, u32[]{:S(2)}, u32[]{:S(2)}) collective-permute-start(bf16[32,4224]{1,0:T(8,128)(2,1)S(1)} %broadcast_select_fusion), channel_id=1, source_target_pairs={{0,2},{1,3},{2,0},{3,1},{4,6},{5,7},{6,4},{7,5},{8,10},{9,11},{10,... | collective-permute-start | bytes 811016 | tf_op jit(solution)/shard_map/ppermute | solution.py:136
  35.1 9.8 %collective-permute-start.6 = (bf16[32,4224]{1,0:T(8,128)(2,1)S(1)}, bf16[32,4224]{1,0:T(8,128)(2,1)S(1)}, u32[]{:S(2)}, u32[]{:S(2)}) collective-permute-start(bf16[32,4224]{1,0:T(8,128)(2,1)S(1)} %broadcast_select_fusion.1), channel_id=1, source_target_pairs={{0,2},{1,3},{2,0},{3,1},{12,14},{13,15},{14,12},{15,13},{16,18},{1... | collective-permute-start | bytes 811016 | tf_op jit(solution)/shard_map/ppermute | solution.py:136
  38.1 15.8 %collective-permute-start.12 = (bf16[2048,768]{1,0:T(8,128)(2,1)S(1)}, bf16[2048,768]{1,0:T(8,128)(2,1)S(1)}, u32[]{:S(2)}, u32[]{:S(2)}) collective-permute-start(bf16[2048,768]{1,0:T(8,128)(2,1)S(1)} %bitcast.61), channel_id=1, source_target_pairs={{0,1},{1,0},{2,3},{3,2},{4,5},{5,4},{6,7},{7,6},{8,9},{9,8},{10,11... | collective-permute-start | bytes 9437192 | tf_op jit(solution)/shard_map/ppermute | solution.py:278
  38.1 16.7 %collective-permute-start.11 = (bf16[2048,768]{1,0:T(8,128)(2,1)}, bf16[2048,768]{1,0:T(8,128)(2,1)S(1)}, u32[]{:S(2)}, u32[]{:S(2)}) collective-permute-start(bf16[2048,768]{1,0:T(8,128)(2,1)} %bitcast.69), channel_id=1, source_target_pairs={{0,1},{1,0},{2,3},{3,2},{4,5},{5,4},{6,7},{7,6},{8,9},{9,8},{10,11... | collective-permute-start | bytes 9437192 | tf_op jit(solution)/shard_map/ppermute | solution.py:277
  38.6 17.2 %collective-permute-start.13 = (bf16[768,2048]{1,0:T(8,128)(2,1)}, bf16[768,2048]{1,0:T(8,128)(2,1)S(1)}, u32[]{:S(2)}, u32[]{:S(2)}) collective-permute-start(bf16[768,2048]{1,0:T(8,128)(2,1)} %bitcast.70), channel_id=1, source_target_pairs={{0,1},{1,0},{2,3},{3,2},{4,5},{5,4},{6,7},{7,6},{8,9},{9,8},{10,11... | collective-permute-start | bytes 9437192 | tf_op jit(solution)/shard_map/ppermute | solution.py:279
  45.8 1.9 %copy-start.6 = (bf16[1,2048,768]{2,1,0:T(8,128)(2,1)S(1)}, bf16[1,2048,768]{2,1,0:T(8,128)(2,1)}, u32[]{:S(2)}) copy-start(bf16[1,2048,768]{2,1,0:T(8,128)(2,1)} %param.13) | copy-start | bytes 9437188
  47.7 1.9 %copy-start.7 = (bf16[1,768,2048]{2,1,0:T(8,128)(2,1)S(1)}, bf16[1,768,2048]{2,1,0:T(8,128)(2,1)}, u32[]{:S(2)}) copy-start(bf16[1,768,2048]{2,1,0:T(8,128)(2,1)} %param.15) | copy-start | bytes 9437188
  60.4 9.3 %collective-permute-start.15 = (bf16[32,4096]{1,0:T(8,128)(2,1)S(1)}, bf16[32,4096]{1,0:T(8,128)(2,1)S(1)}, u32[]{:S(2)}, u32[]{:S(2)}) collective-permute-start(bf16[32,4096]{1,0:T(8,128)(2,1)S(1)} %get-tuple-element.16), channel_id=1, source_target_pairs={{0,2},{1,3},{2,0},{3,1},{4,6},{5,7},{6,4},{7,5},{8,10},{9,11},{10,... | collective-permute-start | bytes 786440 | tf_op jit(solution)/shard_map/ppermute | solution.py:161
  61.7 13.6 %collective-permute-start.17 = (bf16[32,4096]{1,0:T(8,128)(2,1)S(1)}, bf16[32,4096]{1,0:T(8,128)(2,1)S(1)}, u32[]{:S(2)}, u32[]{:S(2)}) collective-permute-start(bf16[32,4096]{1,0:T(8,128)(2,1)S(1)} %get-tuple-element.15), channel_id=1, source_target_pairs={{0,2},{1,3},{2,0},{3,1},{4,6},{5,7},{6,4},{7,5},{8,10},{9,11},{10,... | collective-permute-start | bytes 786440 | tf_op jit(solution)/shard_map/ppermute | solution.py:161
  69.7 7.9 %collective-permute-start.16 = (bf16[32,4096]{1,0:T(8,128)(2,1)S(1)}, bf16[32,4096]{1,0:T(8,128)(2,1)S(1)}, u32[]{:S(2)}, u32[]{:S(2)}) collective-permute-start(bf16[32,4096]{1,0:T(8,128)(2,1)S(1)} %fusion.44), channel_id=1, source_target_pairs={{0,4},{1,5},{2,6},{3,7},{16,20},{17,21},{18,22},{19,23}} | collective-permute-start | bytes 786440 | tf_op jit(solution)/shard_map/ppermute | solution.py:196
  71.0 6.6 %collective-permute-start.21 = (bf16[32,4096]{1,0:T(8,128)(2,1)S(1)}, bf16[32,4096]{1,0:T(8,128)(2,1)S(1)}, u32[]{:S(2)}, u32[]{:S(2)}) collective-permute-start(bf16[32,4096]{1,0:T(8,128)(2,1)S(1)} %fusion.44), channel_id=1, source_target_pairs={{12,8},{13,9},{14,10},{15,11},{28,24},{29,25},{30,26},{31,27}} | collective-permute-start | bytes 786440 | tf_op jit(solution)/shard_map/ppermute | solution.py:197
  71.7 11.1 %collective-permute-start.14 = (bf16[32,4096]{1,0:T(8,128)(2,1)S(1)}, bf16[32,4096]{1,0:T(8,128)(2,1)S(1)}, u32[]{:S(2)}, u32[]{:S(2)}) collective-permute-start(bf16[32,4096]{1,0:T(8,128)(2,1)S(1)} %get-tuple-element.17), channel_id=1, source_target_pairs={{0,2},{1,3},{2,0},{3,1},{4,6},{5,7},{6,4},{7,5},{8,10},{9,11},{10,... | collective-permute-start | bytes 786440 | tf_op jit(solution)/shard_map/ppermute | solution.py:161
  73.0 9.8 %collective-permute-start.19 = (bf16[32,4096]{1,0:T(8,128)(2,1)S(1)}, bf16[32,4096]{1,0:T(8,128)(2,1)S(1)}, u32[]{:S(2)}, u32[]{:S(2)}) collective-permute-start(bf16[32,4096]{1,0:T(8,128)(2,1)S(1)} %get-tuple-element.14), channel_id=1, source_target_pairs={{0,2},{1,3},{2,0},{3,1},{4,6},{5,7},{6,4},{7,5},{8,10},{9,11},{10,... | collective-permute-start | bytes 786440 | tf_op jit(solution)/shard_map/ppermute | solution.py:161
  77.8 8.3 %collective-permute-start.18 = (bf16[32,4096]{1,0:T(8,128)(2,1)S(1)}, bf16[32,4096]{1,0:T(8,128)(2,1)S(1)}, u32[]{:S(2)}, u32[]{:S(2)}) collective-permute-start(bf16[32,4096]{1,0:T(8,128)(2,1)S(1)} %get-tuple-element.8), channel_id=1, source_target_pairs={{0,4},{1,5},{2,6},{3,7},{4,8},{5,9},{6,10},{7,11},{16,20},{17,21},... | collective-permute-start | bytes 786440 | tf_op jit(solution)/shard_map/ppermute | solution.py:200
  82.2 3.9 %collective-permute-start.22 = (bf16[32,4096]{1,0:T(8,128)(2,1)S(1)}, bf16[32,4096]{1,0:T(8,128)(2,1)S(1)}, u32[]{:S(2)}, u32[]{:S(2)}) collective-permute-start(bf16[32,4096]{1,0:T(8,128)(2,1)S(1)} %get-tuple-element.9), channel_id=1, source_target_pairs={{8,4},{9,5},{10,6},{11,7},{12,8},{13,9},{14,10},{15,11},{24,20},{2... | collective-permute-start | bytes 786440 | tf_op jit(solution)/shard_map/ppermute | solution.py:203
  86.2 10.2 %collective-permute-start.20 = (bf16[32,4096]{1,0:T(8,128)(2,1)S(1)}, bf16[32,4096]{1,0:T(8,128)(2,1)S(1)}, u32[]{:S(2)}, u32[]{:S(2)}) collective-permute-start(bf16[32,4096]{1,0:T(8,128)(2,1)S(1)} %get-tuple-element.6), channel_id=1, source_target_pairs={{0,4},{1,5},{2,6},{3,7},{4,8},{5,9},{6,10},{7,11},{8,12},{9,13},{1... | collective-permute-start | bytes 786440 | tf_op jit(solution)/shard_map/ppermute | solution.py:209
  92.6 8.6 %copy-start.5 = (s32[128]{0:T(128)S(1)}, s32[128]{0:T(128)}, u32[]{:S(2)}) copy-start(s32[128]{0:T(128)} %param.10) | copy-start | bytes 1540
  92.6 8.3 %collective-permute-start.23 = (bf16[32,4096]{1,0:T(8,128)(2,1)S(1)}, bf16[32,4096]{1,0:T(8,128)(2,1)S(1)}, u32[]{:S(2)}, u32[]{:S(2)}) collective-permute-start(bf16[32,4096]{1,0:T(8,128)(2,1)S(1)} %get-tuple-element.7), channel_id=1, source_target_pairs={{4,0},{5,1},{6,2},{7,3},{8,4},{9,5},{10,6},{11,7},{12,8},{13,9},{1... | collective-permute-start | bytes 786440 | tf_op jit(solution)/shard_map/ppermute | solution.py:212
  101.0 1.2 %copy-start.1 = (bf16[128,2048]{1,0:T(8,128)(2,1)S(1)}, bf16[128,2048]{1,0:T(8,128)(2,1)}, u32[]{:S(2)}) copy-start(bf16[128,2048]{1,0:T(8,128)(2,1)} %param.9) | copy-start | bytes 1572868
  101.1 1.2 %copy-start.2 = (bf16[128,2048]{1,0:T(8,128)(2,1)S(1)}, bf16[128,2048]{1,0:T(8,128)(2,1)}, u32[]{:S(2)}) copy-start(bf16[128,2048]{1,0:T(8,128)(2,1)} %param.8) | copy-start | bytes 1572868

commit v23 on v22

--- a/solution.py
+++ b/solution.py
@@ -161,8 +161,6 @@
         got = lax.ppermute(theirs.astype(jnp.bfloat16), "expert", pairs)
         return mine + got.astype(jnp.float32)
 
-    if lines == 4:
-        return four_line_sum(keep, give, line, row_sum)
     ahead = jnp.zeros(keep.shape[1:], jnp.float32)
     behind = jnp.zeros(keep.shape[1:], jnp.float32)
     for step in range(1, lines):

time: 104 us -> 104 us (level)
  waiting for transfers between devices: 40.6 us -> 34.9 us
  starting transfers between devices: 40.5 us -> 46 us
    ppermute x4 -> x5, starting transfers between devices: 4.18 us -> 9.68 us  [row_sum(): got = lax.ppermute(theirs.astype(jnp.bfloat16), 'expert', pairs)]
    ppermute x6, waiting for transfers between devices: 12.5 us -> 9.33 us  [the longest x3 4.92 us: topo_reduce_scatter(): lax.ppermute((ahead + ahead_part).astype(jnp.bfloat16), 'expert', [(j, j...]
    ppermute x4 -> x5, waiting for transfers between devices: 8.55 us -> 6.01 us  [row_sum(): got = lax.ppermute(theirs.astype(jnp.bfloat16), 'expert', pairs)]
  transfers between devices with their start and end apart: 24 -> 25, of which waited for: 11 -> 10; matrix products, arithmetic and copies ran while one was open for 10% -> 10% of each run, Pallas kernels for 0% -> 0%
where the time goes in v23:
time: 104 us
  starting transfers between devices  46 us (44%)
  waiting for transfers between devices  34.9 us (34%)
  matrix products  15.1 us (15%)
  other arithmetic  4.14 us (4%)
  local copies, waits for them, and re-layouts  2.2 us (2%)
  between operations  1.31 us (1%)
    ppermute x3, waiting for transfers between devices, topo_all_gather(): lax.ppermute(behind, 'expert', [(j, j - 4) for j in range(experts) if 1 <...  13.4 us
    ppermute x3, starting transfers between devices, topo_reduce_scatter(): lax.ppermute((ahead + ahead_part).astype(jnp.bfloat16), 'expert', [(j, j...  12 us
    ppermute x5, starting transfers between devices, row_sum(): got = lax.ppermute(theirs.astype(jnp.bfloat16), 'expert', pairs)  9.68 us
    ppermute x3, starting transfers between devices, topo_all_gather(): lax.ppermute(ahead, 'expert', [(j, j + 4) for j in range(experts) if step...  6.93 us
    ppermute x2, waiting for transfers between devices, topo_all_gather(): lax.ppermute(jnp.where(in_ahead, ahead, behind), 'expert', sorted(ahead_r...  6.14 us
    ppermute x5, waiting for transfers between devices, row_sum(): got = lax.ppermute(theirs.astype(jnp.bfloat16), 'expert', pairs)  6.01 us
    ppermute x3, waiting for transfers between devices, topo_reduce_scatter(): lax.ppermute((ahead + ahead_part).astype(jnp.bfloat16), 'expert', [(j, j...  4.92 us
    ppermute x3, waiting for transfers between devices, topo_reduce_scatter(): lax.ppermute((behind + behind_part).astype(jnp.bfloat16), 'expert', [(j,...  4.41 us
  transfers between devices with their start and end apart: 25, of which 10 were waited for; matrix products, arithmetic and copies ran while one was open for 10% of the time, Pallas kernels for 0%

profile of v23, /device:TPU:0, one launch (start us, length us, event | category | flops | bytes accessed | tf_op | source)
XLA Modules:
  0.0 103.7 jit_solution(6975675390589250950)
XLA Ops:
  0.7 1.6 %fusion.13 = f32[32,4224]{1,0:T(8,128)S(1)} fusion(bf16[128,2048]{1,0:T(8,128)(2,1)} %param.9, bf16[128,2048]{1,0:T(8,128)(2,1)} %param.8, bf16[4224]{0:T(1024)(128)(2,1)S(1)} %pad.18.clone, s32[128]{0:T(128)} %param.10), kind=kOutput, calls=%fused_computation.21 | convolution fusion | flops 37851136 | bytes 1598208 | tf_op jit(solution)/shard_map/dot_general | solution.py:244
  2.7 1.3 %collective-permute-start = (bf16[32,4224]{1,0:T(8,128)(2,1)S(1)}, bf16[32,4224]{1,0:T(8,128)(2,1)S(1)}, u32[]{:S(2)}, u32[]{:S(2)}) collective-permute-start(bf16[32,4224]{1,0:T(8,128)(2,1)S(1)} %fusion.51), channel_id=1, source_target_pairs={{4,0},{5,1},{6,2},{7,3},{8,4},{9,5},{10,6},{11,7},{12,8},{13,9},{1... | collective-permute-start | bytes 811016 | tf_op jit(solution)/shard_map/ppermute | solution.py:125
  4.0 5.6 %collective-permute-start.3 = (bf16[32,4224]{1,0:T(8,128)(2,1)S(1)}, bf16[32,4224]{1,0:T(8,128)(2,1)S(1)}, u32[]{:S(2)}, u32[]{:S(2)}) collective-permute-start(bf16[32,4224]{1,0:T(8,128)(2,1)S(1)} %fusion.51), channel_id=1, source_target_pairs={{0,4},{1,5},{2,6},{3,7},{4,8},{5,9},{6,10},{7,11},{8,12},{9,13},{1... | collective-permute-start | bytes 811016 | tf_op jit(solution)/shard_map/ppermute | solution.py:120
  9.6 2.0 %collective-permute-start.10 = (bf16[32,4224]{1,0:T(8,128)(2,1)S(1)}, bf16[32,4224]{1,0:T(8,128)(2,1)S(1)}, u32[]{:S(2)}, u32[]{:S(2)}) collective-permute-start(bf16[32,4224]{1,0:T(8,128)(2,1)S(1)} %fusion.51), channel_id=1, source_target_pairs={{0,2},{1,3},{2,0},{3,1},{4,6},{5,7},{6,4},{7,5},{8,10},{9,11},{10,... | collective-permute-start | bytes 811016 | tf_op jit(solution)/shard_map/ppermute | solution.py:117
  11.7 2.5 %collective-permute-done = bf16[32,4224]{1,0:T(8,128)(2,1)S(1)} collective-permute-done((bf16[32,4224]{1,0:T(8,128)(2,1)S(1)}, bf16[32,4224]{1,0:T(8,128)(2,1)S(1)}, u32[]{:S(2)}, u32[]{:S(2)}) %collective-permute-start) | collective-permute-done | bytes 270368 | tf_op jit(solution)/shard_map/ppermute | solution.py:125
  14.1 1.3 %collective-permute-start.1 = (bf16[32,4224]{1,0:T(8,128)(2,1)S(1)}, bf16[32,4224]{1,0:T(8,128)(2,1)S(1)}, u32[]{:S(2)}, u32[]{:S(2)}) collective-permute-start(bf16[32,4224]{1,0:T(8,128)(2,1)S(1)} %collective-permute-done), channel_id=1, source_target_pairs={{4,0},{5,1},{6,2},{7,3},{8,4},{9,5},{10,6},{11,7},{20,16},{21,17},... | collective-permute-start | bytes 811016 | tf_op jit(solution)/shard_map/ppermute | solution.py:125
  16.2 3.6 %collective-permute-start.8 = (bf16[32,4224]{1,0:T(8,128)(2,1)S(1)}, bf16[32,4224]{1,0:T(8,128)(2,1)S(1)}, u32[]{:S(2)}, u32[]{:S(2)}) collective-permute-start(bf16[32,4224]{1,0:T(8,128)(2,1)S(1)} %collective-permute-done), channel_id=1, source_target_pairs={{0,2},{1,3},{2,0},{3,1},{4,6},{5,7},{6,4},{7,5},{8,10},{9,11},{10,... | collective-permute-start | bytes 811016 | tf_op jit(solution)/shard_map/ppermute | solution.py:143
  20.5 3.2 %collective-permute-done.1 = bf16[32,4224]{1,0:T(8,128)(2,1)S(1)} collective-permute-done((bf16[32,4224]{1,0:T(8,128)(2,1)S(1)}, bf16[32,4224]{1,0:T(8,128)(2,1)S(1)}, u32[]{:S(2)}, u32[]{:S(2)}) %collective-permute-start.1) | collective-permute-done | bytes 270368 | tf_op jit(solution)/shard_map/ppermute | solution.py:125
  23.7 1.3 %collective-permute-start.2 = (bf16[32,4224]{1,0:T(8,128)(2,1)S(1)}, bf16[32,4224]{1,0:T(8,128)(2,1)S(1)}, u32[]{:S(2)}, u32[]{:S(2)}) collective-permute-start(bf16[32,4224]{1,0:T(8,128)(2,1)S(1)} %collective-permute-done.1), channel_id=1, source_target_pairs={{4,0},{5,1},{6,2},{7,3},{20,16},{21,17},{22,18},{23,19}} | collective-permute-start | bytes 811016 | tf_op jit(solution)/shard_map/ppermute | solution.py:125
  25.7 7.8 %collective-permute-done.2 = bf16[32,4224]{1,0:T(8,128)(2,1)S(1)} collective-permute-done((bf16[32,4224]{1,0:T(8,128)(2,1)S(1)}, bf16[32,4224]{1,0:T(8,128)(2,1)S(1)}, u32[]{:S(2)}, u32[]{:S(2)}) %collective-permute-start.2) | collective-permute-done | bytes 270368 | tf_op jit(solution)/shard_map/ppermute | solution.py:125
  33.5 1.5 %collective-permute-start.7 = (bf16[32,4224]{1,0:T(8,128)(2,1)S(1)}, bf16[32,4224]{1,0:T(8,128)(2,1)S(1)}, u32[]{:S(2)}, u32[]{:S(2)}) collective-permute-start(bf16[32,4224]{1,0:T(8,128)(2,1)S(1)} %broadcast_select_fusion), channel_id=1, source_target_pairs={{0,2},{1,3},{2,0},{3,1},{4,6},{5,7},{6,4},{7,5},{8,10},{9,11},{10,... | collective-permute-start | bytes 811016 | tf_op jit(solution)/shard_map/ppermute | solution.py:136
  35.1 2.4 %collective-permute-start.6 = (bf16[32,4224]{1,0:T(8,128)(2,1)S(1)}, bf16[32,4224]{1,0:T(8,128)(2,1)S(1)}, u32[]{:S(2)}, u32[]{:S(2)}) collective-permute-start(bf16[32,4224]{1,0:T(8,128)(2,1)S(1)} %broadcast_select_fusion.1), channel_id=1, source_target_pairs={{0,2},{1,3},{2,0},{3,1},{12,14},{13,15},{14,12},{15,13},{16,18},{1... | collective-permute-start | bytes 811016 | tf_op jit(solution)/shard_map/ppermute | solution.py:136
  38.7 3.2 %collective-permute-done.7 = bf16[32,4224]{1,0:T(8,128)(2,1)S(1)} collective-permute-done((bf16[32,4224]{1,0:T(8,128)(2,1)S(1)}, bf16[32,4224]{1,0:T(8,128)(2,1)S(1)}, u32[]{:S(2)}, u32[]{:S(2)}) %collective-permute-start.7) | collective-permute-done | bytes 270368 | tf_op jit(solution)/shard_map/ppermute | solution.py:136
  42.0 2.9 %collective-permute-done.6 = bf16[32,4224]{1,0:T(8,128)(2,1)S(1)} collective-permute-done((bf16[32,4224]{1,0:T(8,128)(2,1)S(1)}, bf16[32,4224]{1,0:T(8,128)(2,1)S(1)}, u32[]{:S(2)}, u32[]{:S(2)}) %collective-permute-start.6) | collective-permute-done | bytes 270368 | tf_op jit(solution)/shard_map/ppermute | solution.py:136
  50.6 1.1 %fusion.11 = f32[256,2048]{1,0:T(8,128)S(1)} fusion(f32[256]{0:T(256)S(1)} %get-tuple-element.3, f32[256,768]{1,0:T(8,128)S(1)} %fusion.26, f32[256,768]{1,0:T(8,128)S(1)} %fusion.28, bf16[1,768,2048]{2,1,0:T(8,128)(2,1)S(1)} %copy-done.7), kind=kOutput, calls=%fused_computation.17 | convolution fusion | flops 808058880 | bytes 6816768 | tf_op jit(solution)/shard_map/dot_general | solution.py:222
  51.7 1.1 %fusion.43 = f32[256,2048]{1,0:T(8,128)S(1)} fusion(f32[256,768]{1,0:T(8,128)S(1)} %fusion.28, f32[256,768]{1,0:T(8,128)S(1)} %fusion.20, f32[256,768]{1,0:T(8,128)S(1)} %fusion.26, bf16[1,2048,768]{2,1,0:T(8,128)(2,1)S(1)} %copy-done.6), kind=kOutput, calls=%fused_computation.76 | convolution fusion | flops 807272448 | bytes 7602176 | tf_op jit(solution)/shard_map/dot_general | solution.py:228
  52.8 1.1 %fusion.6 = f32[256,2048]{1,0:T(8,128)S(1)} fusion(f32[256,2048]{1,0:T(8,128)S(1)} %fusion.43, f32[256]{0:T(256)S(1)} %get-tuple-element.3, f32[256,768]{1,0:T(8,128)S(1)} %fusion.20, f32[256,768]{1,0:T(8,128)S(1)} %fusion.28, bf16[1,2048,768]{2,1,0:T(8,128)(2,1)S(1)} %copy-done), kind=kOutput, calls=%fused_computation.10 | convolution fusion | flops 808583168 | bytes 8913920 | tf_op jit(solution)/shard_map/dot_general | solution.py:229
  56.9 1.0 fusion.44
  58.0 1.0 %fusion.9 = f32[256,2048]{1,0:T(8,128)S(1)} fusion(f32[256,2048]{1,0:T(8,128)S(1)} %fusion.11, bf16[768,2048]{1,0:T(8,128)(2,1)S(1)} %collective-permute-done.13, f32[256]{0:T(256)S(1)} %get-tuple-element.2, f32[256,768]{1,0:T(8,128)S(1)} %fusion.22, f32[256,768]{1,0:T(8,128)S(1)} %fusion.24), kind=kOutput, calls=%fused_computation.14 | convolution fusion | flops 808583168 | bytes 8913920 | tf_op jit(solution)/shard_map/dot_general | solution.py:222
  59.0 1.1 %fusion.4 = f32[256,2048]{1,0:T(8,128)S(1)} fusion(f32[256,2048]{1,0:T(8,128)S(1)} %fusion.6, f32[256,2048]{1,0:T(8,128)S(1)} %fusion.44, bf16[2048,768]{1,0:T(8,128)(2,1)S(1)} %collective-permute-done.11, f32[256]{0:T(256)S(1)} %get-tuple-element.2, f32[256,768]{1,0:T(8,128)S(1)} %fusion.24, f32[256,768]{1,0:T(8,128)S(1)} %fusion.18, f32[256,768]{1,0:T(8,128)S(1)} %fusion.22), kind=kOutput, calls=%fused_computation.8 | convolution fusion | flops 809893888 | bytes 11797504 | tf_op jit(solution)/shard_map/dot_general | solution.py:228
  60.4 3.1 %collective-permute-start.15 = (bf16[32,4096]{1,0:T(8,128)(2,1)S(1)}, bf16[32,4096]{1,0:T(8,128)(2,1)S(1)}, u32[]{:S(2)}, u32[]{:S(2)}) collective-permute-start(bf16[32,4096]{1,0:T(8,128)(2,1)S(1)} %get-tuple-element.18), channel_id=1, source_target_pairs={{0,2},{1,3},{2,0},{3,1},{12,14},{13,15},{14,12},{15,13},{16,18},{1... | collective-permute-start | bytes 786440 | tf_op jit(solution)/shard_map/ppermute | solution.py:161
  64.6 6.0 %collective-permute-done.15 = bf16[32,4096]{1,0:T(8,128)(2,1)S(1)} collective-permute-done((bf16[32,4096]{1,0:T(8,128)(2,1)S(1)}, bf16[32,4096]{1,0:T(8,128)(2,1)S(1)}, u32[]{:S(2)}, u32[]{:S(2)}) %collective-permute-start.15) | collective-permute-done | bytes 262176 | tf_op jit(solution)/shard_map/ppermute | solution.py:161
  70.6 1.3 %collective-permute-start.16 = (bf16[32,4096]{1,0:T(8,128)(2,1)S(1)}, bf16[32,4096]{1,0:T(8,128)(2,1)S(1)}, u32[]{:S(2)}, u32[]{:S(2)}) collective-permute-start(bf16[32,4096]{1,0:T(8,128)(2,1)S(1)} %fusion.40), channel_id=1, source_target_pairs={{0,4},{1,5},{2,6},{3,7},{16,20},{17,21},{18,22},{19,23}} | collective-permute-start | bytes 786440 | tf_op jit(solution)/shard_map/ppermute | solution.py:177
  72.6 3.4 %collective-permute-start.19 = (bf16[32,4096]{1,0:T(8,128)(2,1)S(1)}, bf16[32,4096]{1,0:T(8,128)(2,1)S(1)}, u32[]{:S(2)}, u32[]{:S(2)}) collective-permute-start(bf16[32,4096]{1,0:T(8,128)(2,1)S(1)} %get-tuple-element.16), channel_id=1, source_target_pairs={{0,2},{1,3},{2,0},{3,1},{4,6},{5,7},{6,4},{7,5},{8,10},{9,11},{10,... | collective-permute-start | bytes 786440 | tf_op jit(solution)/shard_map/ppermute | solution.py:161
  77.7 4.4 %collective-permute-start.18 = (bf16[32,4096]{1,0:T(8,128)(2,1)S(1)}, bf16[32,4096]{1,0:T(8,128)(2,1)S(1)}, u32[]{:S(2)}, u32[]{:S(2)}) collective-permute-start(bf16[32,4096]{1,0:T(8,128)(2,1)S(1)} %get-tuple-element.6), channel_id=1, source_target_pairs={{0,4},{1,5},{2,6},{3,7},{4,8},{5,9},{6,10},{7,11},{16,20},{17,21},... | collective-permute-start | bytes 786440 | tf_op jit(solution)/shard_map/ppermute | solution.py:177
  82.8 1.6 %collective-permute-start.14 = (bf16[32,4096]{1,0:T(8,128)(2,1)S(1)}, bf16[32,4096]{1,0:T(8,128)(2,1)S(1)}, u32[]{:S(2)}, u32[]{:S(2)}) collective-permute-start(bf16[32,4096]{1,0:T(8,128)(2,1)S(1)} %get-tuple-element.14), channel_id=1, source_target_pairs={{0,2},{1,3},{2,0},{3,1},{4,6},{5,7},{6,4},{7,5},{8,10},{9,11},{10,... | collective-permute-start | bytes 786440 | tf_op jit(solution)/shard_map/ppermute | solution.py:161
  84.3 1.6 %collective-permute-done.18 = bf16[32,4096]{1,0:T(8,128)(2,1)S(1)} collective-permute-done((bf16[32,4096]{1,0:T(8,128)(2,1)S(1)}, bf16[32,4096]{1,0:T(8,128)(2,1)S(1)}, u32[]{:S(2)}, u32[]{:S(2)}) %collective-permute-start.18) | collective-permute-done | bytes 262176 | tf_op jit(solution)/shard_map/ppermute | solution.py:177
  86.1 6.3 %collective-permute-start.20 = (bf16[32,4096]{1,0:T(8,128)(2,1)S(1)}, bf16[32,4096]{1,0:T(8,128)(2,1)S(1)}, u32[]{:S(2)}, u32[]{:S(2)}) collective-permute-start(bf16[32,4096]{1,0:T(8,128)(2,1)S(1)} %get-tuple-element.10), channel_id=1, source_target_pairs={{0,4},{1,5},{2,6},{3,7},{4,8},{5,9},{6,10},{7,11},{8,12},{9,13},{1... | collective-permute-start | bytes 786440 | tf_op jit(solution)/shard_map/ppermute | solution.py:177
  92.5 1.3 %collective-permute-start.24 = (bf16[32,4096]{1,0:T(8,128)(2,1)S(1)}, bf16[32,4096]{1,0:T(8,128)(2,1)S(1)}, u32[]{:S(2)}, u32[]{:S(2)}) collective-permute-start(bf16[32,4096]{1,0:T(8,128)(2,1)S(1)} %get-tuple-element.11), channel_id=1, source_target_pairs={{4,0},{5,1},{6,2},{7,3},{8,4},{9,5},{10,6},{11,7},{12,8},{13,9},{1... | collective-permute-start | bytes 786440 | tf_op jit(solution)/shard_map/ppermute | solution.py:182
  93.8 2.5 %collective-permute-done.20 = bf16[32,4096]{1,0:T(8,128)(2,1)S(1)} collective-permute-done((bf16[32,4096]{1,0:T(8,128)(2,1)S(1)}, bf16[32,4096]{1,0:T(8,128)(2,1)S(1)}, u32[]{:S(2)}, u32[]{:S(2)}) %collective-permute-start.20) | collective-permute-done | bytes 262176 | tf_op jit(solution)/shard_map/ppermute | solution.py:177
  96.3 4.4 %collective-permute-done.24 = bf16[32,4096]{1,0:T(8,128)(2,1)S(1)} collective-permute-done((bf16[32,4096]{1,0:T(8,128)(2,1)S(1)}, bf16[32,4096]{1,0:T(8,128)(2,1)S(1)}, u32[]{:S(2)}, u32[]{:S(2)}) %collective-permute-start.24) | collective-permute-done | bytes 262176 | tf_op jit(solution)/shard_map/ppermute | solution.py:182
  102.1 1.6 %slice_add_fusion = (f32[128,2048]{1,0:T(8,128)}, f32[128,2048]{1,0:T(8,128)}) fusion(f32[128,4096]{1,0:T(8,128)S(1)} %fusion.32, bf16[128,2048]{1,0:T(8,128)(2,1)S(1)} %copy-done.1, bf16[128,2048]{1,0:T(8,128)(2,1)S(1)} %copy-done.2), kind=kLoop, calls=%fused_computation.28 | loop fusion | flops 1048576 | bytes 5242880 | tf_op jit(solution)/shard_map/add | solution.py:292
  (80 shorter events, 18.1 us)
Async XLA Ops:
  0.6 1.9 %copy-start.4 = (s32[32,8]{0,1:T(8,128)S(1)}, s32[32,8]{0,1:T(8,128)}, u32[]{:S(2)}) copy-start(s32[32,8]{0,1:T(8,128)} %param.11) | copy-start | bytes 3076
  0.6 1.9 %copy-start.3 = (f32[32,8]{0,1:T(8,128)S(1)}, f32[32,8]{0,1:T(8,128)}, u32[]{:S(2)}) copy-start(f32[32,8]{0,1:T(8,128)} %param.12) | copy-start | bytes 3076
  2.7 11.4 %collective-permute-start = (bf16[32,4224]{1,0:T(8,128)(2,1)S(1)}, bf16[32,4224]{1,0:T(8,128)(2,1)S(1)}, u32[]{:S(2)}, u32[]{:S(2)}) collective-permute-start(bf16[32,4224]{1,0:T(8,128)(2,1)S(1)} %fusion.51), channel_id=1, source_target_pairs={{4,0},{5,1},{6,2},{7,3},{8,4},{9,5},{10,6},{11,7},{12,8},{13,9},{1... | collective-permute-start | bytes 811016 | tf_op jit(solution)/shard_map/ppermute | solution.py:125
  4.0 11.4 %collective-permute-start.3 = (bf16[32,4224]{1,0:T(8,128)(2,1)S(1)}, bf16[32,4224]{1,0:T(8,128)(2,1)S(1)}, u32[]{:S(2)}, u32[]{:S(2)}) collective-permute-start(bf16[32,4224]{1,0:T(8,128)(2,1)S(1)} %fusion.51), channel_id=1, source_target_pairs={{0,4},{1,5},{2,6},{3,7},{4,8},{5,9},{6,10},{7,11},{8,12},{9,13},{1... | collective-permute-start | bytes 811016 | tf_op jit(solution)/shard_map/ppermute | solution.py:120
  9.6 28.4 %collective-permute-start.10 = (bf16[32,4224]{1,0:T(8,128)(2,1)S(1)}, bf16[32,4224]{1,0:T(8,128)(2,1)S(1)}, u32[]{:S(2)}, u32[]{:S(2)}) collective-permute-start(bf16[32,4224]{1,0:T(8,128)(2,1)S(1)} %fusion.51), channel_id=1, source_target_pairs={{0,2},{1,3},{2,0},{3,1},{4,6},{5,7},{6,4},{7,5},{8,10},{9,11},{10,... | collective-permute-start | bytes 811016 | tf_op jit(solution)/shard_map/ppermute | solution.py:117
  14.1 9.6 %collective-permute-start.1 = (bf16[32,4224]{1,0:T(8,128)(2,1)S(1)}, bf16[32,4224]{1,0:T(8,128)(2,1)S(1)}, u32[]{:S(2)}, u32[]{:S(2)}) collective-permute-start(bf16[32,4224]{1,0:T(8,128)(2,1)S(1)} %collective-permute-done), channel_id=1, source_target_pairs={{4,0},{5,1},{6,2},{7,3},{8,4},{9,5},{10,6},{11,7},{20,16},{21,17},... | collective-permute-start | bytes 811016 | tf_op jit(solution)/shard_map/ppermute | solution.py:125
  15.4 9.5 %collective-permute-start.4 = (bf16[32,4224]{1,0:T(8,128)(2,1)S(1)}, bf16[32,4224]{1,0:T(8,128)(2,1)S(1)}, u32[]{:S(2)}, u32[]{:S(2)}) collective-permute-start(bf16[32,4224]{1,0:T(8,128)(2,1)S(1)} %collective-permute-done.3), channel_id=1, source_target_pairs={{4,8},{5,9},{6,10},{7,11},{8,12},{9,13},{10,14},{11,15},{20,24},{2... | collective-permute-start | bytes 811016 | tf_op jit(solution)/shard_map/ppermute | solution.py:120
  16.2 21.9 %collective-permute-start.8 = (bf16[32,4224]{1,0:T(8,128)(2,1)S(1)}, bf16[32,4224]{1,0:T(8,128)(2,1)S(1)}, u32[]{:S(2)}, u32[]{:S(2)}) collective-permute-start(bf16[32,4224]{1,0:T(8,128)(2,1)S(1)} %collective-permute-done), channel_id=1, source_target_pairs={{0,2},{1,3},{2,0},{3,1},{4,6},{5,7},{6,4},{7,5},{8,10},{9,11},{10,... | collective-permute-start | bytes 811016 | tf_op jit(solution)/shard_map/ppermute | solution.py:143
  19.8 18.8 %collective-permute-start.9 = (bf16[32,4224]{1,0:T(8,128)(2,1)S(1)}, bf16[32,4224]{1,0:T(8,128)(2,1)S(1)}, u32[]{:S(2)}, u32[]{:S(2)}) collective-permute-start(bf16[32,4224]{1,0:T(8,128)(2,1)S(1)} %collective-permute-done.3), channel_id=1, source_target_pairs={{4,6},{5,7},{6,4},{7,5},{8,10},{9,11},{10,8},{11,9},{12,14},{13,15... | collective-permute-start | bytes 811016 | tf_op jit(solution)/shard_map/ppermute | solution.py:142
  23.7 9.8 %collective-permute-start.2 = (bf16[32,4224]{1,0:T(8,128)(2,1)S(1)}, bf16[32,4224]{1,0:T(8,128)(2,1)S(1)}, u32[]{:S(2)}, u32[]{:S(2)}) collective-permute-start(bf16[32,4224]{1,0:T(8,128)(2,1)S(1)} %collective-permute-done.1), channel_id=1, source_target_pairs={{4,0},{5,1},{6,2},{7,3},{20,16},{21,17},{22,18},{23,19}} | collective-permute-start | bytes 811016 | tf_op jit(solution)/shard_map/ppermute | solution.py:125
  25.0 10.0 %collective-permute-start.5 = (bf16[32,4224]{1,0:T(8,128)(2,1)S(1)}, bf16[32,4224]{1,0:T(8,128)(2,1)S(1)}, u32[]{:S(2)}, u32[]{:S(2)}) collective-permute-start(bf16[32,4224]{1,0:T(8,128)(2,1)S(1)} %collective-permute-done.4), channel_id=1, source_target_pairs={{8,12},{9,13},{10,14},{11,15},{24,28},{25,29},{26,30},{27,31}} | collective-permute-start | bytes 811016 | tf_op jit(solution)/shard_map/ppermute | solution.py:120
  25.7 12.3 %copy-start = (bf16[1,2048,768]{2,1,0:T(8,128)(2,1)S(1)}, bf16[1,2048,768]{2,1,0:T(8,128)(2,1)}, u32[]{:S(2)}) copy-start(bf16[1,2048,768]{2,1,0:T(8,128)(2,1)} %param.14) | copy-start | bytes 9437188
  33.5 8.5 %collective-permute-start.7 = (bf16[32,4224]{1,0:T(8,128)(2,1)S(1)}, bf16[32,4224]{1,0:T(8,128)(2,1)S(1)}, u32[]{:S(2)}, u32[]{:S(2)}) collective-permute-start(bf16[32,4224]{1,0:T(8,128)(2,1)S(1)} %broadcast_select_fusion), channel_id=1, source_target_pairs={{0,2},{1,3},{2,0},{3,1},{4,6},{5,7},{6,4},{7,5},{8,10},{9,11},{10,... | collective-permute-start | bytes 811016 | tf_op jit(solution)/shard_map/ppermute | solution.py:136
  35.1 9.8 %collective-permute-start.6 = (bf16[32,4224]{1,0:T(8,128)(2,1)S(1)}, bf16[32,4224]{1,0:T(8,128)(2,1)S(1)}, u32[]{:S(2)}, u32[]{:S(2)}) collective-permute-start(bf16[32,4224]{1,0:T(8,128)(2,1)S(1)} %broadcast_select_fusion.1), channel_id=1, source_target_pairs={{0,2},{1,3},{2,0},{3,1},{12,14},{13,15},{14,12},{15,13},{16,18},{1... | collective-permute-start | bytes 811016 | tf_op jit(solution)/shard_map/ppermute | solution.py:136
  38.1 15.8 %collective-permute-start.12 = (bf16[2048,768]{1,0:T(8,128)(2,1)S(1)}, bf16[2048,768]{1,0:T(8,128)(2,1)S(1)}, u32[]{:S(2)}, u32[]{:S(2)}) collective-permute-start(bf16[2048,768]{1,0:T(8,128)(2,1)S(1)} %bitcast.67), channel_id=1, source_target_pairs={{0,1},{1,0},{2,3},{3,2},{4,5},{5,4},{6,7},{7,6},{8,9},{9,8},{10,11... | collective-permute-start | bytes 9437192 | tf_op jit(solution)/shard_map/ppermute | solution.py:276
  38.2 16.7 %collective-permute-start.11 = (bf16[2048,768]{1,0:T(8,128)(2,1)}, bf16[2048,768]{1,0:T(8,128)(2,1)S(1)}, u32[]{:S(2)}, u32[]{:S(2)}) collective-permute-start(bf16[2048,768]{1,0:T(8,128)(2,1)} %bitcast.75), channel_id=1, source_target_pairs={{0,1},{1,0},{2,3},{3,2},{4,5},{5,4},{6,7},{7,6},{8,9},{9,8},{10,11... | collective-permute-start | bytes 9437192 | tf_op jit(solution)/shard_map/ppermute | solution.py:275
  38.6 17.2 %collective-permute-start.13 = (bf16[768,2048]{1,0:T(8,128)(2,1)}, bf16[768,2048]{1,0:T(8,128)(2,1)S(1)}, u32[]{:S(2)}, u32[]{:S(2)}) collective-permute-start(bf16[768,2048]{1,0:T(8,128)(2,1)} %bitcast.76), channel_id=1, source_target_pairs={{0,1},{1,0},{2,3},{3,2},{4,5},{5,4},{6,7},{7,6},{8,9},{9,8},{10,11... | collective-permute-start | bytes 9437192 | tf_op jit(solution)/shard_map/ppermute | solution.py:277
  45.8 1.9 %copy-start.6 = (bf16[1,2048,768]{2,1,0:T(8,128)(2,1)S(1)}, bf16[1,2048,768]{2,1,0:T(8,128)(2,1)}, u32[]{:S(2)}) copy-start(bf16[1,2048,768]{2,1,0:T(8,128)(2,1)} %param.13) | copy-start | bytes 9437188
  47.7 1.9 %copy-start.7 = (bf16[1,768,2048]{2,1,0:T(8,128)(2,1)S(1)}, bf16[1,768,2048]{2,1,0:T(8,128)(2,1)}, u32[]{:S(2)}) copy-start(bf16[1,768,2048]{2,1,0:T(8,128)(2,1)} %param.15) | copy-start | bytes 9437188
  60.4 10.2 %collective-permute-start.15 = (bf16[32,4096]{1,0:T(8,128)(2,1)S(1)}, bf16[32,4096]{1,0:T(8,128)(2,1)S(1)}, u32[]{:S(2)}, u32[]{:S(2)}) collective-permute-start(bf16[32,4096]{1,0:T(8,128)(2,1)S(1)} %get-tuple-element.18), channel_id=1, source_target_pairs={{0,2},{1,3},{2,0},{3,1},{12,14},{13,15},{14,12},{15,13},{16,18},{1... | collective-permute-start | bytes 786440 | tf_op jit(solution)/shard_map/ppermute | solution.py:161
  63.5 13.2 %collective-permute-start.17 = (bf16[32,4096]{1,0:T(8,128)(2,1)S(1)}, bf16[32,4096]{1,0:T(8,128)(2,1)S(1)}, u32[]{:S(2)}, u32[]{:S(2)}) collective-permute-start(bf16[32,4096]{1,0:T(8,128)(2,1)S(1)} %get-tuple-element.17), channel_id=1, source_target_pairs={{0,2},{1,3},{2,0},{3,1},{4,6},{5,7},{6,4},{7,5},{8,10},{9,11},{10,... | collective-permute-start | bytes 786440 | tf_op jit(solution)/shard_map/ppermute | solution.py:161
  70.6 6.9 %collective-permute-start.16 = (bf16[32,4096]{1,0:T(8,128)(2,1)S(1)}, bf16[32,4096]{1,0:T(8,128)(2,1)S(1)}, u32[]{:S(2)}, u32[]{:S(2)}) collective-permute-start(bf16[32,4096]{1,0:T(8,128)(2,1)S(1)} %fusion.40), channel_id=1, source_target_pairs={{0,4},{1,5},{2,6},{3,7},{16,20},{17,21},{18,22},{19,23}} | collective-permute-start | bytes 786440 | tf_op jit(solution)/shard_map/ppermute | solution.py:177
  71.9 5.6 %collective-permute-start.21 = (bf16[32,4096]{1,0:T(8,128)(2,1)S(1)}, bf16[32,4096]{1,0:T(8,128)(2,1)S(1)}, u32[]{:S(2)}, u32[]{:S(2)}) collective-permute-start(bf16[32,4096]{1,0:T(8,128)(2,1)S(1)} %fusion.40), channel_id=1, source_target_pairs={{12,8},{13,9},{14,10},{15,11},{28,24},{29,25},{30,26},{31,27}} | collective-permute-start | bytes 786440 | tf_op jit(solution)/shard_map/ppermute | solution.py:182
  72.6 11.7 %collective-permute-start.19 = (bf16[32,4096]{1,0:T(8,128)(2,1)S(1)}, bf16[32,4096]{1,0:T(8,128)(2,1)S(1)}, u32[]{:S(2)}, u32[]{:S(2)}) collective-permute-start(bf16[32,4096]{1,0:T(8,128)(2,1)S(1)} %get-tuple-element.16), channel_id=1, source_target_pairs={{0,2},{1,3},{2,0},{3,1},{4,6},{5,7},{6,4},{7,5},{8,10},{9,11},{10,... | collective-permute-start | bytes 786440 | tf_op jit(solution)/shard_map/ppermute | solution.py:161
  76.0 8.3 %collective-permute-start.23 = (bf16[32,4096]{1,0:T(8,128)(2,1)S(1)}, bf16[32,4096]{1,0:T(8,128)(2,1)S(1)}, u32[]{:S(2)}, u32[]{:S(2)}) collective-permute-start(bf16[32,4096]{1,0:T(8,128)(2,1)S(1)} %get-tuple-element.15), channel_id=1, source_target_pairs={{4,6},{5,7},{6,4},{7,5},{8,10},{9,11},{10,8},{11,9},{12,14},{13,15... | collective-permute-start | bytes 786440 | tf_op jit(solution)/shard_map/ppermute | solution.py:161
  77.7 8.3 %collective-permute-start.18 = (bf16[32,4096]{1,0:T(8,128)(2,1)S(1)}, bf16[32,4096]{1,0:T(8,128)(2,1)S(1)}, u32[]{:S(2)}, u32[]{:S(2)}) collective-permute-start(bf16[32,4096]{1,0:T(8,128)(2,1)S(1)} %get-tuple-element.6), channel_id=1, source_target_pairs={{0,4},{1,5},{2,6},{3,7},{4,8},{5,9},{6,10},{7,11},{16,20},{17,21},... | collective-permute-start | bytes 786440 | tf_op jit(solution)/shard_map/ppermute | solution.py:177
  82.1 3.9 %collective-permute-start.22 = (bf16[32,4096]{1,0:T(8,128)(2,1)S(1)}, bf16[32,4096]{1,0:T(8,128)(2,1)S(1)}, u32[]{:S(2)}, u32[]{:S(2)}) collective-permute-start(bf16[32,4096]{1,0:T(8,128)(2,1)S(1)} %get-tuple-element.7), channel_id=1, source_target_pairs={{8,4},{9,5},{10,6},{11,7},{12,8},{13,9},{14,10},{15,11},{24,20},{2... | collective-permute-start | bytes 786440 | tf_op jit(solution)/shard_map/ppermute | solution.py:182
  82.8 11.0 %collective-permute-start.14 = (bf16[32,4096]{1,0:T(8,128)(2,1)S(1)}, bf16[32,4096]{1,0:T(8,128)(2,1)S(1)}, u32[]{:S(2)}, u32[]{:S(2)}) collective-permute-start(bf16[32,4096]{1,0:T(8,128)(2,1)S(1)} %get-tuple-element.14), channel_id=1, source_target_pairs={{0,2},{1,3},{2,0},{3,1},{4,6},{5,7},{6,4},{7,5},{8,10},{9,11},{10,... | collective-permute-start | bytes 786440 | tf_op jit(solution)/shard_map/ppermute | solution.py:161
  86.1 14.9 %copy-start.5 = (s32[128]{0:T(128)S(1)}, s32[128]{0:T(128)}, u32[]{:S(2)}) copy-start(s32[128]{0:T(128)} %param.10) | copy-start | bytes 1540
  86.1 10.2 %collective-permute-start.20 = (bf16[32,4096]{1,0:T(8,128)(2,1)S(1)}, bf16[32,4096]{1,0:T(8,128)(2,1)S(1)}, u32[]{:S(2)}, u32[]{:S(2)}) collective-permute-start(bf16[32,4096]{1,0:T(8,128)(2,1)S(1)} %get-tuple-element.10), channel_id=1, source_target_pairs={{0,4},{1,5},{2,6},{3,7},{4,8},{5,9},{6,10},{7,11},{8,12},{9,13},{1... | collective-permute-start | bytes 786440 | tf_op jit(solution)/shard_map/ppermute | solution.py:177
  92.5 8.3 %collective-permute-start.24 = (bf16[32,4096]{1,0:T(8,128)(2,1)S(1)}, bf16[32,4096]{1,0:T(8,128)(2,1)S(1)}, u32[]{:S(2)}, u32[]{:S(2)}) collective-permute-start(bf16[32,4096]{1,0:T(8,128)(2,1)S(1)} %get-tuple-element.11), channel_id=1, source_target_pairs={{4,0},{5,1},{6,2},{7,3},{8,4},{9,5},{10,6},{11,7},{12,8},{13,9},{1... | collective-permute-start | bytes 786440 | tf_op jit(solution)/shard_map/ppermute | solution.py:182
  100.9 1.2 %copy-start.1 = (bf16[128,2048]{1,0:T(8,128)(2,1)S(1)}, bf16[128,2048]{1,0:T(8,128)(2,1)}, u32[]{:S(2)}) copy-start(bf16[128,2048]{1,0:T(8,128)(2,1)} %param.9) | copy-start | bytes 1572868
  (1 other events, 1.2 us)

commit v24 on v22

--- a/solution.py
+++ b/solution.py
@@ -289,7 +289,17 @@
     combined = summed[:, :model_width]
     centroid_grad = summed[:, model_width:] - grad_sum
     table = jnp.concatenate([combined - centroid, centroid_grad / counts[:, None]], axis=1)
-    spread = jnp.dot(member.astype(jnp.float32), table, precision=lax.Precision.HIGHEST)
+    table_hi = table.astype(jnp.bfloat16)
+    rest = table - table_hi.astype(jnp.float32)
+    table_mid = rest.astype(jnp.bfloat16)
+    table_lo = (rest - table_mid.astype(jnp.float32)).astype(jnp.bfloat16)
+    parts = jnp.dot(
+        member,
+        jnp.concatenate([table_hi, table_mid, table_lo], axis=1),
+        preferred_element_type=jnp.float32,
+    )
+    width = table.shape[1]
+    spread = (parts[:, :width] + parts[:, width : 2 * width]) + parts[:, 2 * width :]
     layer_out = tokens.astype(jnp.float32) + spread[:, :model_width]
     token_grad = out_grad.astype(jnp.float32) + spread[:, model_width:]
     return (layer_out, token_grad)

time: 104 us -> 106 us (1.019)
  local copies, waits for them, and re-layouts: 2.18 us -> 3.4 us
    unnamed x17, local copies, waits for them, and re-layouts: 1.93 us -> 3.16 us
where the time goes in v24:
time: 106 us; the launch traced here: 105 us
  waiting for transfers between devices  40.6 us (38%)
  starting transfers between devices  40.5 us (38%)
  matrix products  15 us (14%)
  other arithmetic  4.66 us (4%)
  local copies, waits for them, and re-layouts  3.4 us (3%)
  between operations  1.28 us (1%)
    ppermute x3, waiting for transfers between devices, topo_all_gather(): lax.ppermute(behind, 'expert', [(j, j - 4) for j in range(experts) if 1 <...  13.4 us
    ppermute x4, waiting for transfers between devices, row_sum(): got = lax.ppermute(theirs.astype(jnp.bfloat16), 'expert', pairs)  8.55 us
    ppermute x3, starting transfers between devices, topo_all_gather(): lax.ppermute(ahead, 'expert', [(j, j + 4) for j in range(experts) if step...  6.93 us
    ppermute x1, starting transfers between devices, four_line_sum(): lax.ppermute((ahead + third).astype(jnp.bfloat16), 'expert', [(j, j + 4)...  6.33 us
    ppermute x2, waiting for transfers between devices, topo_all_gather(): lax.ppermute(jnp.where(in_ahead, ahead, behind), 'expert', sorted(ahead_r...  6.14 us
    ppermute x1, waiting for transfers between devices, four_line_sum(): lax.ppermute((behind + behind_part).astype(jnp.bfloat16), 'expert', [(j,...  4.41 us
    ppermute x1, starting transfers between devices, four_line_sum(): lax.ppermute((ahead + second).astype(jnp.bfloat16), 'expert', [(j, j + 4)...  4.4 us
    ppermute x4, starting transfers between devices, row_sum(): got = lax.ppermute(theirs.astype(jnp.bfloat16), 'expert', pairs)  4.18 us
  transfers between devices with their start and end apart: 24, of which 11 were waited for; matrix products, arithmetic and copies ran while one was open for 10% of the time, Pallas kernels for 0%

profile of v24, /device:TPU:0, one launch (start us, length us, event | category | flops | bytes accessed | tf_op | source)
XLA Modules:
  0.0 105.5 jit_solution(2551526982634173536)
XLA Ops:
  0.7 1.6 %fusion.13 = f32[32,4224]{1,0:T(8,128)S(1)} fusion(bf16[128,2048]{1,0:T(8,128)(2,1)} %param.9, bf16[128,2048]{1,0:T(8,128)(2,1)} %param.8, bf16[4224]{0:T(1024)(128)(2,1)S(1)} %pad.21.clone, s32[128]{0:T(128)} %param.10), kind=kOutput, calls=%fused_computation.23 | convolution fusion | flops 37851136 | bytes 1598208 | tf_op jit(solution)/shard_map/dot_general | solution.py:246
  2.7 1.3 %collective-permute-start = (bf16[32,4224]{1,0:T(8,128)(2,1)S(1)}, bf16[32,4224]{1,0:T(8,128)(2,1)S(1)}, u32[]{:S(2)}, u32[]{:S(2)}) collective-permute-start(bf16[32,4224]{1,0:T(8,128)(2,1)S(1)} %fusion.48), channel_id=1, source_target_pairs={{4,0},{5,1},{6,2},{7,3},{8,4},{9,5},{10,6},{11,7},{12,8},{13,9},{1... | collective-permute-start | bytes 811016 | tf_op jit(solution)/shard_map/ppermute | solution.py:125
  4.0 5.6 %collective-permute-start.3 = (bf16[32,4224]{1,0:T(8,128)(2,1)S(1)}, bf16[32,4224]{1,0:T(8,128)(2,1)S(1)}, u32[]{:S(2)}, u32[]{:S(2)}) collective-permute-start(bf16[32,4224]{1,0:T(8,128)(2,1)S(1)} %fusion.48), channel_id=1, source_target_pairs={{0,4},{1,5},{2,6},{3,7},{4,8},{5,9},{6,10},{7,11},{8,12},{9,13},{1... | collective-permute-start | bytes 811016 | tf_op jit(solution)/shard_map/ppermute | solution.py:120
  9.6 2.0 %collective-permute-start.10 = (bf16[32,4224]{1,0:T(8,128)(2,1)S(1)}, bf16[32,4224]{1,0:T(8,128)(2,1)S(1)}, u32[]{:S(2)}, u32[]{:S(2)}) collective-permute-start(bf16[32,4224]{1,0:T(8,128)(2,1)S(1)} %fusion.48), channel_id=1, source_target_pairs={{0,2},{1,3},{2,0},{3,1},{4,6},{5,7},{6,4},{7,5},{8,10},{9,11},{10,... | collective-permute-start | bytes 811016 | tf_op jit(solution)/shard_map/ppermute | solution.py:117
  11.7 2.5 %collective-permute-done = bf16[32,4224]{1,0:T(8,128)(2,1)S(1)} collective-permute-done((bf16[32,4224]{1,0:T(8,128)(2,1)S(1)}, bf16[32,4224]{1,0:T(8,128)(2,1)S(1)}, u32[]{:S(2)}, u32[]{:S(2)}) %collective-permute-start) | collective-permute-done | bytes 270368 | tf_op jit(solution)/shard_map/ppermute | solution.py:125
  14.1 1.3 %collective-permute-start.1 = (bf16[32,4224]{1,0:T(8,128)(2,1)S(1)}, bf16[32,4224]{1,0:T(8,128)(2,1)S(1)}, u32[]{:S(2)}, u32[]{:S(2)}) collective-permute-start(bf16[32,4224]{1,0:T(8,128)(2,1)S(1)} %collective-permute-done), channel_id=1, source_target_pairs={{4,0},{5,1},{6,2},{7,3},{8,4},{9,5},{10,6},{11,7},{20,16},{21,17},... | collective-permute-start | bytes 811016 | tf_op jit(solution)/shard_map/ppermute | solution.py:125
  16.2 3.6 %collective-permute-start.8 = (bf16[32,4224]{1,0:T(8,128)(2,1)S(1)}, bf16[32,4224]{1,0:T(8,128)(2,1)S(1)}, u32[]{:S(2)}, u32[]{:S(2)}) collective-permute-start(bf16[32,4224]{1,0:T(8,128)(2,1)S(1)} %collective-permute-done), channel_id=1, source_target_pairs={{0,2},{1,3},{2,0},{3,1},{4,6},{5,7},{6,4},{7,5},{8,10},{9,11},{10,... | collective-permute-start | bytes 811016 | tf_op jit(solution)/shard_map/ppermute | solution.py:143
  20.5 3.2 %collective-permute-done.1 = bf16[32,4224]{1,0:T(8,128)(2,1)S(1)} collective-permute-done((bf16[32,4224]{1,0:T(8,128)(2,1)S(1)}, bf16[32,4224]{1,0:T(8,128)(2,1)S(1)}, u32[]{:S(2)}, u32[]{:S(2)}) %collective-permute-start.1) | collective-permute-done | bytes 270368 | tf_op jit(solution)/shard_map/ppermute | solution.py:125
  23.7 1.3 %collective-permute-start.2 = (bf16[32,4224]{1,0:T(8,128)(2,1)S(1)}, bf16[32,4224]{1,0:T(8,128)(2,1)S(1)}, u32[]{:S(2)}, u32[]{:S(2)}) collective-permute-start(bf16[32,4224]{1,0:T(8,128)(2,1)S(1)} %collective-permute-done.1), channel_id=1, source_target_pairs={{4,0},{5,1},{6,2},{7,3},{20,16},{21,17},{22,18},{23,19}} | collective-permute-start | bytes 811016 | tf_op jit(solution)/shard_map/ppermute | solution.py:125
  25.7 7.8 %collective-permute-done.2 = bf16[32,4224]{1,0:T(8,128)(2,1)S(1)} collective-permute-done((bf16[32,4224]{1,0:T(8,128)(2,1)S(1)}, bf16[32,4224]{1,0:T(8,128)(2,1)S(1)}, u32[]{:S(2)}, u32[]{:S(2)}) %collective-permute-start.2) | collective-permute-done | bytes 270368 | tf_op jit(solution)/shard_map/ppermute | solution.py:125
  33.5 1.5 %collective-permute-start.7 = (bf16[32,4224]{1,0:T(8,128)(2,1)S(1)}, bf16[32,4224]{1,0:T(8,128)(2,1)S(1)}, u32[]{:S(2)}, u32[]{:S(2)}) collective-permute-start(bf16[32,4224]{1,0:T(8,128)(2,1)S(1)} %broadcast_select_fusion), channel_id=1, source_target_pairs={{0,2},{1,3},{2,0},{3,1},{4,6},{5,7},{6,4},{7,5},{8,10},{9,11},{10,... | collective-permute-start | bytes 811016 | tf_op jit(solution)/shard_map/ppermute | solution.py:136
  35.1 2.4 %collective-permute-start.6 = (bf16[32,4224]{1,0:T(8,128)(2,1)S(1)}, bf16[32,4224]{1,0:T(8,128)(2,1)S(1)}, u32[]{:S(2)}, u32[]{:S(2)}) collective-permute-start(bf16[32,4224]{1,0:T(8,128)(2,1)S(1)} %broadcast_select_fusion.1), channel_id=1, source_target_pairs={{0,2},{1,3},{2,0},{3,1},{12,14},{13,15},{14,12},{15,13},{16,18},{1... | collective-permute-start | bytes 811016 | tf_op jit(solution)/shard_map/ppermute | solution.py:136
  38.7 3.2 %collective-permute-done.7 = bf16[32,4224]{1,0:T(8,128)(2,1)S(1)} collective-permute-done((bf16[32,4224]{1,0:T(8,128)(2,1)S(1)}, bf16[32,4224]{1,0:T(8,128)(2,1)S(1)}, u32[]{:S(2)}, u32[]{:S(2)}) %collective-permute-start.7) | collective-permute-done | bytes 270368 | tf_op jit(solution)/shard_map/ppermute | solution.py:136
  42.0 2.9 %collective-permute-done.6 = bf16[32,4224]{1,0:T(8,128)(2,1)S(1)} collective-permute-done((bf16[32,4224]{1,0:T(8,128)(2,1)S(1)}, bf16[32,4224]{1,0:T(8,128)(2,1)S(1)}, u32[]{:S(2)}, u32[]{:S(2)}) %collective-permute-start.6) | collective-permute-done | bytes 270368 | tf_op jit(solution)/shard_map/ppermute | solution.py:136
  50.6 1.1 %fusion.11 = f32[256,2048]{1,0:T(8,128)S(1)} fusion(f32[256]{0:T(256)S(1)} %get-tuple-element.3, f32[256,768]{1,0:T(8,128)S(1)} %fusion.32, f32[256,768]{1,0:T(8,128)S(1)} %fusion.34, bf16[1,768,2048]{2,1,0:T(8,128)(2,1)S(1)} %copy-done.7), kind=kOutput, calls=%fused_computation.17 | convolution fusion | flops 808058880 | bytes 6816768 | tf_op jit(solution)/shard_map/dot_general | solution.py:224
  51.7 1.1 %fusion.39 = f32[256,2048]{1,0:T(8,128)S(1)} fusion(f32[256,768]{1,0:T(8,128)S(1)} %fusion.34, f32[256,768]{1,0:T(8,128)S(1)} %fusion.20, f32[256,768]{1,0:T(8,128)S(1)} %fusion.32, bf16[1,2048,768]{2,1,0:T(8,128)(2,1)S(1)} %copy-done.6), kind=kOutput, calls=%fused_computation.78 | convolution fusion | flops 807272448 | bytes 7602176 | tf_op jit(solution)/shard_map/dot_general | solution.py:230
  52.8 1.1 %fusion.6 = f32[256,2048]{1,0:T(8,128)S(1)} fusion(f32[256,2048]{1,0:T(8,128)S(1)} %fusion.39, f32[256]{0:T(256)S(1)} %get-tuple-element.3, f32[256,768]{1,0:T(8,128)S(1)} %fusion.20, f32[256,768]{1,0:T(8,128)S(1)} %fusion.34, bf16[1,2048,768]{2,1,0:T(8,128)(2,1)S(1)} %copy-done), kind=kOutput, calls=%fused_computation.10 | convolution fusion | flops 808583168 | bytes 8913920 | tf_op jit(solution)/shard_map/dot_general | solution.py:231
  58.0 1.0 fusion.9
  59.0 1.1 %fusion.4 = f32[256,2048]{1,0:T(8,128)S(1)} fusion(f32[256,2048]{1,0:T(8,128)S(1)} %fusion.6, f32[256,2048]{1,0:T(8,128)S(1)} %fusion.40, bf16[2048,768]{1,0:T(8,128)(2,1)S(1)} %collective-permute-done.11, f32[256]{0:T(256)S(1)} %get-tuple-element.2, f32[256,768]{1,0:T(8,128)S(1)} %fusion.30, f32[256,768]{1,0:T(8,128)S(1)} %fusion.18, f32[256,768]{1,0:T(8,128)S(1)} %fusion.28), kind=kOutput, calls=%fused_computation.8 | convolution fusion | flops 809893888 | bytes 11797504 | tf_op jit(solution)/shard_map/dot_general | solution.py:230
  60.4 1.3 %collective-permute-start.15 = (bf16[32,4096]{1,0:T(8,128)(2,1)S(1)}, bf16[32,4096]{1,0:T(8,128)(2,1)S(1)}, u32[]{:S(2)}, u32[]{:S(2)}) collective-permute-start(bf16[32,4096]{1,0:T(8,128)(2,1)S(1)} %get-tuple-element.16), channel_id=1, source_target_pairs={{0,2},{1,3},{2,0},{3,1},{4,6},{5,7},{6,4},{7,5},{8,10},{9,11},{10,... | collective-permute-start | bytes 786440 | tf_op jit(solution)/shard_map/ppermute | solution.py:161
  62.6 7.1 %collective-permute-done.15 = bf16[32,4096]{1,0:T(8,128)(2,1)S(1)} collective-permute-done((bf16[32,4096]{1,0:T(8,128)(2,1)S(1)}, bf16[32,4096]{1,0:T(8,128)(2,1)S(1)}, u32[]{:S(2)}, u32[]{:S(2)}) %collective-permute-start.15) | collective-permute-done | bytes 262176 | tf_op jit(solution)/shard_map/ppermute | solution.py:161
  69.7 1.3 %collective-permute-start.16 = (bf16[32,4096]{1,0:T(8,128)(2,1)S(1)}, bf16[32,4096]{1,0:T(8,128)(2,1)S(1)}, u32[]{:S(2)}, u32[]{:S(2)}) collective-permute-start(bf16[32,4096]{1,0:T(8,128)(2,1)S(1)} %fusion.47), channel_id=1, source_target_pairs={{0,4},{1,5},{2,6},{3,7},{16,20},{17,21},{18,22},{19,23}} | collective-permute-start | bytes 786440 | tf_op jit(solution)/shard_map/ppermute | solution.py:196
  71.7 1.3 %collective-permute-start.14 = (bf16[32,4096]{1,0:T(8,128)(2,1)S(1)}, bf16[32,4096]{1,0:T(8,128)(2,1)S(1)}, u32[]{:S(2)}, u32[]{:S(2)}) collective-permute-start(bf16[32,4096]{1,0:T(8,128)(2,1)S(1)} %get-tuple-element.17), channel_id=1, source_target_pairs={{0,2},{1,3},{2,0},{3,1},{4,6},{5,7},{6,4},{7,5},{8,10},{9,11},{10,... | collective-permute-start | bytes 786440 | tf_op jit(solution)/shard_map/ppermute | solution.py:161
  73.8 1.5 %collective-permute-done.17 = bf16[32,4096]{1,0:T(8,128)(2,1)S(1)} collective-permute-done((bf16[32,4096]{1,0:T(8,128)(2,1)S(1)}, bf16[32,4096]{1,0:T(8,128)(2,1)S(1)}, u32[]{:S(2)}, u32[]{:S(2)}) %collective-permute-start.17) | collective-permute-done | bytes 262176 | tf_op jit(solution)/shard_map/ppermute | solution.py:161
  75.3 2.3 %collective-permute-done.16 = bf16[32,4096]{1,0:T(8,128)(2,1)S(1)} collective-permute-done((bf16[32,4096]{1,0:T(8,128)(2,1)S(1)}, bf16[32,4096]{1,0:T(8,128)(2,1)S(1)}, u32[]{:S(2)}, u32[]{:S(2)}) %collective-permute-start.16) | collective-permute-done | bytes 262176 | tf_op jit(solution)/shard_map/ppermute | solution.py:196
  77.8 4.4 %collective-permute-start.18 = (bf16[32,4096]{1,0:T(8,128)(2,1)S(1)}, bf16[32,4096]{1,0:T(8,128)(2,1)S(1)}, u32[]{:S(2)}, u32[]{:S(2)}) collective-permute-start(bf16[32,4096]{1,0:T(8,128)(2,1)S(1)} %get-tuple-element.8), channel_id=1, source_target_pairs={{0,4},{1,5},{2,6},{3,7},{4,8},{5,9},{6,10},{7,11},{16,20},{17,21},... | collective-permute-start | bytes 786440 | tf_op jit(solution)/shard_map/ppermute | solution.py:200
  82.9 3.2 %collective-permute-done.18 = bf16[32,4096]{1,0:T(8,128)(2,1)S(1)} collective-permute-done((bf16[32,4096]{1,0:T(8,128)(2,1)S(1)}, bf16[32,4096]{1,0:T(8,128)(2,1)S(1)}, u32[]{:S(2)}, u32[]{:S(2)}) %collective-permute-start.18) | collective-permute-done | bytes 262176 | tf_op jit(solution)/shard_map/ppermute | solution.py:200
  86.2 6.3 %collective-permute-start.20 = (bf16[32,4096]{1,0:T(8,128)(2,1)S(1)}, bf16[32,4096]{1,0:T(8,128)(2,1)S(1)}, u32[]{:S(2)}, u32[]{:S(2)}) collective-permute-start(bf16[32,4096]{1,0:T(8,128)(2,1)S(1)} %get-tuple-element.6), channel_id=1, source_target_pairs={{0,4},{1,5},{2,6},{3,7},{4,8},{5,9},{6,10},{7,11},{8,12},{9,13},{1... | collective-permute-start | bytes 786440 | tf_op jit(solution)/shard_map/ppermute | solution.py:209
  92.6 1.3 %collective-permute-start.23 = (bf16[32,4096]{1,0:T(8,128)(2,1)S(1)}, bf16[32,4096]{1,0:T(8,128)(2,1)S(1)}, u32[]{:S(2)}, u32[]{:S(2)}) collective-permute-start(bf16[32,4096]{1,0:T(8,128)(2,1)S(1)} %get-tuple-element.7), channel_id=1, source_target_pairs={{4,0},{5,1},{6,2},{7,3},{8,4},{9,5},{10,6},{11,7},{12,8},{13,9},{1... | collective-permute-start | bytes 786440 | tf_op jit(solution)/shard_map/ppermute | solution.py:212
  93.9 2.6 %collective-permute-done.20 = bf16[32,4096]{1,0:T(8,128)(2,1)S(1)} collective-permute-done((bf16[32,4096]{1,0:T(8,128)(2,1)S(1)}, bf16[32,4096]{1,0:T(8,128)(2,1)S(1)}, u32[]{:S(2)}, u32[]{:S(2)}) %collective-permute-start.20) | collective-permute-done | bytes 262176 | tf_op jit(solution)/shard_map/ppermute | solution.py:209
  96.4 4.4 %collective-permute-done.23 = bf16[32,4096]{1,0:T(8,128)(2,1)S(1)} collective-permute-done((bf16[32,4096]{1,0:T(8,128)(2,1)S(1)}, bf16[32,4096]{1,0:T(8,128)(2,1)S(1)}, u32[]{:S(2)}, u32[]{:S(2)}) %collective-permute-start.23) | collective-permute-done | bytes 262176 | tf_op jit(solution)/shard_map/ppermute | solution.py:212
  103.9 1.6 %slice_add_fusion.2 = (f32[128,2048]{1,0:T(8,128)}, f32[128,2048]{1,0:T(8,128)}) fusion(f32[128,4096]{1,0:T(8,128)S(1)} %slice_add_fusion, bf16[128,2048]{1,0:T(8,128)(2,1)S(1)} %copy-done.1, bf16[128,2048]{1,0:T(8,128)(2,1)S(1)} %copy-done.2), kind=kLoop, calls=%fused_computation.30 | loop fusion | flops 1048576 | bytes 5242880 | tf_op jit(solution)/shard_map/add | solution.py:304
  (81 shorter events, 20.1 us)
Async XLA Ops:
  0.6 1.9 %copy-start.4 = (s32[32,8]{0,1:T(8,128)S(1)}, s32[32,8]{0,1:T(8,128)}, u32[]{:S(2)}) copy-start(s32[32,8]{0,1:T(8,128)} %param.11) | copy-start | bytes 3076
  0.6 1.9 %copy-start.3 = (f32[32,8]{0,1:T(8,128)S(1)}, f32[32,8]{0,1:T(8,128)}, u32[]{:S(2)}) copy-start(f32[32,8]{0,1:T(8,128)} %param.12) | copy-start | bytes 3076
  2.7 11.4 %collective-permute-start = (bf16[32,4224]{1,0:T(8,128)(2,1)S(1)}, bf16[32,4224]{1,0:T(8,128)(2,1)S(1)}, u32[]{:S(2)}, u32[]{:S(2)}) collective-permute-start(bf16[32,4224]{1,0:T(8,128)(2,1)S(1)} %fusion.48), channel_id=1, source_target_pairs={{4,0},{5,1},{6,2},{7,3},{8,4},{9,5},{10,6},{11,7},{12,8},{13,9},{1... | collective-permute-start | bytes 811016 | tf_op jit(solution)/shard_map/ppermute | solution.py:125
  4.0 11.4 %collective-permute-start.3 = (bf16[32,4224]{1,0:T(8,128)(2,1)S(1)}, bf16[32,4224]{1,0:T(8,128)(2,1)S(1)}, u32[]{:S(2)}, u32[]{:S(2)}) collective-permute-start(bf16[32,4224]{1,0:T(8,128)(2,1)S(1)} %fusion.48), channel_id=1, source_target_pairs={{0,4},{1,5},{2,6},{3,7},{4,8},{5,9},{6,10},{7,11},{8,12},{9,13},{1... | collective-permute-start | bytes 811016 | tf_op jit(solution)/shard_map/ppermute | solution.py:120
  9.6 28.4 %collective-permute-start.10 = (bf16[32,4224]{1,0:T(8,128)(2,1)S(1)}, bf16[32,4224]{1,0:T(8,128)(2,1)S(1)}, u32[]{:S(2)}, u32[]{:S(2)}) collective-permute-start(bf16[32,4224]{1,0:T(8,128)(2,1)S(1)} %fusion.48), channel_id=1, source_target_pairs={{0,2},{1,3},{2,0},{3,1},{4,6},{5,7},{6,4},{7,5},{8,10},{9,11},{10,... | collective-permute-start | bytes 811016 | tf_op jit(solution)/shard_map/ppermute | solution.py:117
  14.1 9.6 %collective-permute-start.1 = (bf16[32,4224]{1,0:T(8,128)(2,1)S(1)}, bf16[32,4224]{1,0:T(8,128)(2,1)S(1)}, u32[]{:S(2)}, u32[]{:S(2)}) collective-permute-start(bf16[32,4224]{1,0:T(8,128)(2,1)S(1)} %collective-permute-done), channel_id=1, source_target_pairs={{4,0},{5,1},{6,2},{7,3},{8,4},{9,5},{10,6},{11,7},{20,16},{21,17},... | collective-permute-start | bytes 811016 | tf_op jit(solution)/shard_map/ppermute | solution.py:125
  15.4 9.5 %collective-permute-start.4 = (bf16[32,4224]{1,0:T(8,128)(2,1)S(1)}, bf16[32,4224]{1,0:T(8,128)(2,1)S(1)}, u32[]{:S(2)}, u32[]{:S(2)}) collective-permute-start(bf16[32,4224]{1,0:T(8,128)(2,1)S(1)} %collective-permute-done.3), channel_id=1, source_target_pairs={{4,8},{5,9},{6,10},{7,11},{8,12},{9,13},{10,14},{11,15},{20,24},{2... | collective-permute-start | bytes 811016 | tf_op jit(solution)/shard_map/ppermute | solution.py:120
  16.2 21.9 %collective-permute-start.8 = (bf16[32,4224]{1,0:T(8,128)(2,1)S(1)}, bf16[32,4224]{1,0:T(8,128)(2,1)S(1)}, u32[]{:S(2)}, u32[]{:S(2)}) collective-permute-start(bf16[32,4224]{1,0:T(8,128)(2,1)S(1)} %collective-permute-done), channel_id=1, source_target_pairs={{0,2},{1,3},{2,0},{3,1},{4,6},{5,7},{6,4},{7,5},{8,10},{9,11},{10,... | collective-permute-start | bytes 811016 | tf_op jit(solution)/shard_map/ppermute | solution.py:143
  19.8 18.8 %collective-permute-start.9 = (bf16[32,4224]{1,0:T(8,128)(2,1)S(1)}, bf16[32,4224]{1,0:T(8,128)(2,1)S(1)}, u32[]{:S(2)}, u32[]{:S(2)}) collective-permute-start(bf16[32,4224]{1,0:T(8,128)(2,1)S(1)} %collective-permute-done.3), channel_id=1, source_target_pairs={{4,6},{5,7},{6,4},{7,5},{8,10},{9,11},{10,8},{11,9},{12,14},{13,15... | collective-permute-start | bytes 811016 | tf_op jit(solution)/shard_map/ppermute | solution.py:142
  23.7 9.8 %collective-permute-start.2 = (bf16[32,4224]{1,0:T(8,128)(2,1)S(1)}, bf16[32,4224]{1,0:T(8,128)(2,1)S(1)}, u32[]{:S(2)}, u32[]{:S(2)}) collective-permute-start(bf16[32,4224]{1,0:T(8,128)(2,1)S(1)} %collective-permute-done.1), channel_id=1, source_target_pairs={{4,0},{5,1},{6,2},{7,3},{20,16},{21,17},{22,18},{23,19}} | collective-permute-start | bytes 811016 | tf_op jit(solution)/shard_map/ppermute | solution.py:125
  25.0 10.0 %collective-permute-start.5 = (bf16[32,4224]{1,0:T(8,128)(2,1)S(1)}, bf16[32,4224]{1,0:T(8,128)(2,1)S(1)}, u32[]{:S(2)}, u32[]{:S(2)}) collective-permute-start(bf16[32,4224]{1,0:T(8,128)(2,1)S(1)} %collective-permute-done.4), channel_id=1, source_target_pairs={{8,12},{9,13},{10,14},{11,15},{24,28},{25,29},{26,30},{27,31}} | collective-permute-start | bytes 811016 | tf_op jit(solution)/shard_map/ppermute | solution.py:120
  25.7 12.3 %copy-start = (bf16[1,2048,768]{2,1,0:T(8,128)(2,1)S(1)}, bf16[1,2048,768]{2,1,0:T(8,128)(2,1)}, u32[]{:S(2)}) copy-start(bf16[1,2048,768]{2,1,0:T(8,128)(2,1)} %param.14) | copy-start | bytes 9437188
  33.5 8.5 %collective-permute-start.7 = (bf16[32,4224]{1,0:T(8,128)(2,1)S(1)}, bf16[32,4224]{1,0:T(8,128)(2,1)S(1)}, u32[]{:S(2)}, u32[]{:S(2)}) collective-permute-start(bf16[32,4224]{1,0:T(8,128)(2,1)S(1)} %broadcast_select_fusion), channel_id=1, source_target_pairs={{0,2},{1,3},{2,0},{3,1},{4,6},{5,7},{6,4},{7,5},{8,10},{9,11},{10,... | collective-permute-start | bytes 811016 | tf_op jit(solution)/shard_map/ppermute | solution.py:136
  35.1 9.8 %collective-permute-start.6 = (bf16[32,4224]{1,0:T(8,128)(2,1)S(1)}, bf16[32,4224]{1,0:T(8,128)(2,1)S(1)}, u32[]{:S(2)}, u32[]{:S(2)}) collective-permute-start(bf16[32,4224]{1,0:T(8,128)(2,1)S(1)} %broadcast_select_fusion.1), channel_id=1, source_target_pairs={{0,2},{1,3},{2,0},{3,1},{12,14},{13,15},{14,12},{15,13},{16,18},{1... | collective-permute-start | bytes 811016 | tf_op jit(solution)/shard_map/ppermute | solution.py:136
  38.1 15.8 %collective-permute-start.12 = (bf16[2048,768]{1,0:T(8,128)(2,1)S(1)}, bf16[2048,768]{1,0:T(8,128)(2,1)S(1)}, u32[]{:S(2)}, u32[]{:S(2)}) collective-permute-start(bf16[2048,768]{1,0:T(8,128)(2,1)S(1)} %bitcast.61), channel_id=1, source_target_pairs={{0,1},{1,0},{2,3},{3,2},{4,5},{5,4},{6,7},{7,6},{8,9},{9,8},{10,11... | collective-permute-start | bytes 9437192 | tf_op jit(solution)/shard_map/ppermute | solution.py:278
  38.1 16.7 %collective-permute-start.11 = (bf16[2048,768]{1,0:T(8,128)(2,1)}, bf16[2048,768]{1,0:T(8,128)(2,1)S(1)}, u32[]{:S(2)}, u32[]{:S(2)}) collective-permute-start(bf16[2048,768]{1,0:T(8,128)(2,1)} %bitcast.69), channel_id=1, source_target_pairs={{0,1},{1,0},{2,3},{3,2},{4,5},{5,4},{6,7},{7,6},{8,9},{9,8},{10,11... | collective-permute-start | bytes 9437192 | tf_op jit(solution)/shard_map/ppermute | solution.py:277
  38.6 17.2 %collective-permute-start.13 = (bf16[768,2048]{1,0:T(8,128)(2,1)}, bf16[768,2048]{1,0:T(8,128)(2,1)S(1)}, u32[]{:S(2)}, u32[]{:S(2)}) collective-permute-start(bf16[768,2048]{1,0:T(8,128)(2,1)} %bitcast.70), channel_id=1, source_target_pairs={{0,1},{1,0},{2,3},{3,2},{4,5},{5,4},{6,7},{7,6},{8,9},{9,8},{10,11... | collective-permute-start | bytes 9437192 | tf_op jit(solution)/shard_map/ppermute | solution.py:279
  45.8 1.9 %copy-start.6 = (bf16[1,2048,768]{2,1,0:T(8,128)(2,1)S(1)}, bf16[1,2048,768]{2,1,0:T(8,128)(2,1)}, u32[]{:S(2)}) copy-start(bf16[1,2048,768]{2,1,0:T(8,128)(2,1)} %param.13) | copy-start | bytes 9437188
  47.7 1.9 %copy-start.7 = (bf16[1,768,2048]{2,1,0:T(8,128)(2,1)S(1)}, bf16[1,768,2048]{2,1,0:T(8,128)(2,1)}, u32[]{:S(2)}) copy-start(bf16[1,768,2048]{2,1,0:T(8,128)(2,1)} %param.15) | copy-start | bytes 9437188
  60.4 9.3 %collective-permute-start.15 = (bf16[32,4096]{1,0:T(8,128)(2,1)S(1)}, bf16[32,4096]{1,0:T(8,128)(2,1)S(1)}, u32[]{:S(2)}, u32[]{:S(2)}) collective-permute-start(bf16[32,4096]{1,0:T(8,128)(2,1)S(1)} %get-tuple-element.16), channel_id=1, source_target_pairs={{0,2},{1,3},{2,0},{3,1},{4,6},{5,7},{6,4},{7,5},{8,10},{9,11},{10,... | collective-permute-start | bytes 786440 | tf_op jit(solution)/shard_map/ppermute | solution.py:161
  61.7 13.6 %collective-permute-start.17 = (bf16[32,4096]{1,0:T(8,128)(2,1)S(1)}, bf16[32,4096]{1,0:T(8,128)(2,1)S(1)}, u32[]{:S(2)}, u32[]{:S(2)}) collective-permute-start(bf16[32,4096]{1,0:T(8,128)(2,1)S(1)} %get-tuple-element.15), channel_id=1, source_target_pairs={{0,2},{1,3},{2,0},{3,1},{4,6},{5,7},{6,4},{7,5},{8,10},{9,11},{10,... | collective-permute-start | bytes 786440 | tf_op jit(solution)/shard_map/ppermute | solution.py:161
  69.7 7.9 %collective-permute-start.16 = (bf16[32,4096]{1,0:T(8,128)(2,1)S(1)}, bf16[32,4096]{1,0:T(8,128)(2,1)S(1)}, u32[]{:S(2)}, u32[]{:S(2)}) collective-permute-start(bf16[32,4096]{1,0:T(8,128)(2,1)S(1)} %fusion.47), channel_id=1, source_target_pairs={{0,4},{1,5},{2,6},{3,7},{16,20},{17,21},{18,22},{19,23}} | collective-permute-start | bytes 786440 | tf_op jit(solution)/shard_map/ppermute | solution.py:196
  71.0 6.6 %collective-permute-start.21 = (bf16[32,4096]{1,0:T(8,128)(2,1)S(1)}, bf16[32,4096]{1,0:T(8,128)(2,1)S(1)}, u32[]{:S(2)}, u32[]{:S(2)}) collective-permute-start(bf16[32,4096]{1,0:T(8,128)(2,1)S(1)} %fusion.47), channel_id=1, source_target_pairs={{12,8},{13,9},{14,10},{15,11},{28,24},{29,25},{30,26},{31,27}} | collective-permute-start | bytes 786440 | tf_op jit(solution)/shard_map/ppermute | solution.py:197
  71.7 11.1 %collective-permute-start.14 = (bf16[32,4096]{1,0:T(8,128)(2,1)S(1)}, bf16[32,4096]{1,0:T(8,128)(2,1)S(1)}, u32[]{:S(2)}, u32[]{:S(2)}) collective-permute-start(bf16[32,4096]{1,0:T(8,128)(2,1)S(1)} %get-tuple-element.17), channel_id=1, source_target_pairs={{0,2},{1,3},{2,0},{3,1},{4,6},{5,7},{6,4},{7,5},{8,10},{9,11},{10,... | collective-permute-start | bytes 786440 | tf_op jit(solution)/shard_map/ppermute | solution.py:161
  73.0 9.8 %collective-permute-start.19 = (bf16[32,4096]{1,0:T(8,128)(2,1)S(1)}, bf16[32,4096]{1,0:T(8,128)(2,1)S(1)}, u32[]{:S(2)}, u32[]{:S(2)}) collective-permute-start(bf16[32,4096]{1,0:T(8,128)(2,1)S(1)} %get-tuple-element.14), channel_id=1, source_target_pairs={{0,2},{1,3},{2,0},{3,1},{4,6},{5,7},{6,4},{7,5},{8,10},{9,11},{10,... | collective-permute-start | bytes 786440 | tf_op jit(solution)/shard_map/ppermute | solution.py:161
  77.8 8.3 %collective-permute-start.18 = (bf16[32,4096]{1,0:T(8,128)(2,1)S(1)}, bf16[32,4096]{1,0:T(8,128)(2,1)S(1)}, u32[]{:S(2)}, u32[]{:S(2)}) collective-permute-start(bf16[32,4096]{1,0:T(8,128)(2,1)S(1)} %get-tuple-element.8), channel_id=1, source_target_pairs={{0,4},{1,5},{2,6},{3,7},{4,8},{5,9},{6,10},{7,11},{16,20},{17,21},... | collective-permute-start | bytes 786440 | tf_op jit(solution)/shard_map/ppermute | solution.py:200
  82.2 3.9 %collective-permute-start.22 = (bf16[32,4096]{1,0:T(8,128)(2,1)S(1)}, bf16[32,4096]{1,0:T(8,128)(2,1)S(1)}, u32[]{:S(2)}, u32[]{:S(2)}) collective-permute-start(bf16[32,4096]{1,0:T(8,128)(2,1)S(1)} %get-tuple-element.9), channel_id=1, source_target_pairs={{8,4},{9,5},{10,6},{11,7},{12,8},{13,9},{14,10},{15,11},{24,20},{2... | collective-permute-start | bytes 786440 | tf_op jit(solution)/shard_map/ppermute | solution.py:203
  86.2 10.2 %collective-permute-start.20 = (bf16[32,4096]{1,0:T(8,128)(2,1)S(1)}, bf16[32,4096]{1,0:T(8,128)(2,1)S(1)}, u32[]{:S(2)}, u32[]{:S(2)}) collective-permute-start(bf16[32,4096]{1,0:T(8,128)(2,1)S(1)} %get-tuple-element.6), channel_id=1, source_target_pairs={{0,4},{1,5},{2,6},{3,7},{4,8},{5,9},{6,10},{7,11},{8,12},{9,13},{1... | collective-permute-start | bytes 786440 | tf_op jit(solution)/shard_map/ppermute | solution.py:209
  92.6 8.3 %collective-permute-start.23 = (bf16[32,4096]{1,0:T(8,128)(2,1)S(1)}, bf16[32,4096]{1,0:T(8,128)(2,1)S(1)}, u32[]{:S(2)}, u32[]{:S(2)}) collective-permute-start(bf16[32,4096]{1,0:T(8,128)(2,1)S(1)} %get-tuple-element.7), channel_id=1, source_target_pairs={{4,0},{5,1},{6,2},{7,3},{8,4},{9,5},{10,6},{11,7},{12,8},{13,9},{1... | collective-permute-start | bytes 786440 | tf_op jit(solution)/shard_map/ppermute | solution.py:212
  101.0 0.7 copy-start.5
  102.7 1.0 copy-start.1
  102.7 1.2 %copy-start.2 = (bf16[128,2048]{1,0:T(8,128)(2,1)S(1)}, bf16[128,2048]{1,0:T(8,128)(2,1)}, u32[]{:S(2)}) copy-start(bf16[128,2048]{1,0:T(8,128)(2,1)} %param.8) | copy-start | bytes 1572868
